TPU v7x, 32 devices: a whole 2x2x4 slice. The times are simulated.
32 devices in a mesh: groups: 2 (over x), seq: 4 (over y, core), pair: 4 (over z).
Axes of the slice: x: 2, y: 2, z: 4, core: 2. Of those that a mesh axis runs over, the one named last changes fastest.
Arguments:
- sequence: bfloat16 [4096, 1536], P(('groups', 'seq', 'pair')), parts along dimension 0, may hold values from -12 to 12
- gain_conv: float32 [1536], replicated, may hold values from 0.25 to 1.75
- conv_weight: bfloat16 [5, 1536, 1536], P(None, 'pair'), may hold values from -0.0625 to 0.0625
- gain_attn: float32 [1536], replicated, may hold values from 0.25 to 1.75
- w_qkv: bfloat16 [1536, 3072], P(None, 'pair'), may hold values from -1 to 1
- w_out: bfloat16 [1024, 1536], P('pair'), may hold values from -0.75 to 0.75
- gain_pool: float32 [1536], replicated, may hold values from 0.25 to 1.75
- w_pair: bfloat16 [1536, 256], replicated, may hold values from -0.15625 to 0.15625
- w_up: bfloat16 [128, 256], replicated, may hold values from -0.5 to 0.5
- w_down: bfloat16 [256, 128], replicated, may hold values from -0.375 to 0.375
Outputs:
- seq_out: bfloat16 [4096, 1536], P(('groups', 'seq', 'pair')), parts along dimension 0
- pair_map: bfloat16 [256, 128, 128], P(('groups', 'seq'), 'pair'), parts along dimension 0
There are 2 independent parts, one for each index of `groups`. A program takes and returns all parts, laid end to end along the dimension named above; an argument that names none is the same for every part. Nothing has to cross between parts.
All inputs are finite; a program needn't handle non-finite values.
Results may differ from a plain program's by a relative error of at most 0.024.
Values may be sent and summed in bfloat16 or wider, within the bound.
No kernel may reach another device: no remote copies, remote signals or barrier semaphores. Data moves between devices by JAX's collectives and lax.ppermute only.
A program may use at most 64 MiB of HBM per device.

v0:
```python
import math

import jax
import jax.numpy as jnp
from jax import lax
from jax.sharding import PartitionSpec as P

KEY_SIZE = 128
VALUE_SIZE = 128
DILATION = 4
POOL = 16
PAIR_CH = 128


EPS = 1e-06


def padded_2(value, sides, width):
    for axis, dim in sides:
        peers, length = (lax.axis_size(axis), value.shape[dim])
        up = [(i, (i + 1) % peers) for i in range(peers - 1)]
        down = [(j, i) for i, j in up]
        last = lax.slice_in_dim(value, length - width, length, axis=dim)
        first = lax.slice_in_dim(value, 0, width, axis=dim)
        before = lax.ppermute(last, axis, up)
        after = lax.ppermute(first, axis, down)
        value = jnp.concatenate([before, value, after], axis=dim)
    return value


def norm_rows(values, gain):
    return values * lax.rsqrt(jnp.mean(values * values, axis=-1, keepdims=True) + EPS) * gain


def conv_rows(padded, conv_weight, row_total):
    summed = jnp.zeros((row_total, conv_weight.shape[2]), jnp.float32)
    for offset in range(conv_weight.shape[0]):
        shifted = lax.dynamic_slice_in_dim(padded, offset * DILATION, row_total, 0)
        summed = summed + jnp.dot(shifted, conv_weight[offset], preferred_element_type=jnp.float32)
    return summed


def shards(
    sequence, gain_conv, conv_weight, gain_attn, w_qkv, w_out, gain_pool, w_pair, w_up, w_down
):
    pair_count = lax.axis_size("pair")
    seq_count = lax.axis_size("seq")
    row_count = sequence.shape[0]
    channels = sequence.shape[1]
    local_rows = row_count * pair_count
    inputs = sequence.astype(jnp.float32)
    normed = norm_rows(inputs, gain_conv).astype(jnp.bfloat16)
    swapped = lax.all_to_all(normed, "pair", split_axis=1, concat_axis=0, tiled=True)
    padded = padded_2(swapped, (("seq", 0),), DILATION * (conv_weight.shape[0] - 1) // 2)
    summed = lax.psum_scatter(
        conv_rows(padded, conv_weight, row_count * lax.axis_size("pair")),
        "pair",
        scatter_dimension=0,
        tiled=True,
    )
    first_out = (inputs + summed).astype(jnp.bfloat16)
    attn_in = norm_rows(first_out.astype(jnp.float32), gain_attn).astype(jnp.bfloat16)
    projected = jnp.dot(
        lax.all_gather(attn_in, "pair", axis=0, tiled=True),
        w_qkv,
        preferred_element_type=jnp.float32,
    ).astype(jnp.bfloat16)
    head_count = projected.shape[1] // (2 * KEY_SIZE + VALUE_SIZE)
    grouped = projected.reshape(local_rows, head_count, 2 * KEY_SIZE + VALUE_SIZE)
    queries = grouped[:, :, :KEY_SIZE]
    key_rows = grouped[:, :, KEY_SIZE : 2 * KEY_SIZE].reshape(local_rows, head_count * KEY_SIZE)
    value_rows = grouped[:, :, 2 * KEY_SIZE :].reshape(local_rows, head_count * VALUE_SIZE)
    scale = 1.0 / math.sqrt(KEY_SIZE)
    start_state = (
        jnp.full((head_count, local_rows), -1e30, jnp.float32),
        jnp.zeros((head_count, local_rows), jnp.float32),
        jnp.zeros((head_count, local_rows, VALUE_SIZE), jnp.float32),
    )
    carried = start_state
    key_piece = lax.all_gather(key_rows, "seq", axis=0, tiled=True)
    value_piece = lax.all_gather(value_rows, "seq", axis=0, tiled=True)
    piece_rows = key_piece.shape[0]
    block_rows = math.gcd(piece_rows, 512)
    block_count = piece_rows // block_rows
    key_blocks = key_piece.reshape(block_count, block_rows, head_count, KEY_SIZE)
    value_blocks = value_piece.reshape(block_count, block_rows, head_count, VALUE_SIZE)

    def one_block(state, blocks):
        running_max, running_sum, weighted = state
        key_block, value_block = blocks
        scores = (
            jnp.einsum("qhd,khd->hqk", queries, key_block, preferred_element_type=jnp.float32)
            * scale
        )
        new_max = jnp.maximum(running_max, jnp.max(scores, axis=-1))
        shrink = jnp.exp(running_max - new_max)
        weights = jnp.exp(scores - new_max[:, :, None])
        running_sum = running_sum * shrink + jnp.sum(weights, axis=-1)
        update = jnp.einsum(
            "hqk,khd->hqd",
            weights.astype(jnp.bfloat16),
            value_block,
            preferred_element_type=jnp.float32,
        )
        weighted = weighted * shrink[:, :, None] + update
        return ((new_max, running_sum, weighted), None)

    carried, unused = lax.scan(one_block, carried, (key_blocks, value_blocks))
    running_max, running_sum, weighted = carried
    attended = (weighted / running_sum[:, :, None]).astype(jnp.bfloat16)
    attended = attended.transpose(1, 0, 2).reshape(local_rows, head_count * VALUE_SIZE)
    mixed = lax.psum_scatter(
        jnp.dot(attended, w_out, preferred_element_type=jnp.float32).astype(jnp.bfloat16),
        "pair",
        scatter_dimension=0,
        tiled=True,
    ).astype(jnp.float32)
    seq_out = (first_out.astype(jnp.float32) + mixed).astype(jnp.bfloat16)
    bin_count = row_count // POOL
    pooled = jnp.mean(seq_out.astype(jnp.float32).reshape(bin_count, POOL, channels), axis=1)
    bin_norm = norm_rows(pooled, gain_pool).astype(jnp.bfloat16)
    sides = jnp.dot(bin_norm, w_pair, preferred_element_type=jnp.float32).astype(jnp.bfloat16)
    left_side = sides[:, :PAIR_CH]
    right_side = sides[:, PAIR_CH:]
    tile_rows = bin_count * pair_count
    tile_cols = bin_count * seq_count
    row_side = lax.all_gather(left_side, "pair", axis=0, tiled=True)
    all_right = lax.all_gather(right_side, ("seq", "pair"), axis=0, tiled=True)
    column_side = lax.dynamic_slice_in_dim(
        all_right, lax.axis_index("pair") * tile_cols, tile_cols, 0
    )
    pair_tile = (
        row_side.astype(jnp.float32)[:, None, :] * column_side.astype(jnp.float32)[None, :, :]
    ).astype(jnp.bfloat16)
    flat_rows = pair_tile.reshape(tile_rows * tile_cols, PAIR_CH)
    hidden = jax.nn.relu(jnp.dot(flat_rows, w_up, preferred_element_type=jnp.float32)).astype(
        jnp.bfloat16
    )
    pair_out = flat_rows.astype(jnp.float32) + jnp.dot(
        hidden, w_down, preferred_element_type=jnp.float32
    )
    pair_map = pair_out.astype(jnp.bfloat16).reshape(tile_rows, tile_cols, PAIR_CH)
    return (seq_out, pair_map)


def solution(mesh):
    return jax.shard_map(
        shards,
        mesh=mesh,
        in_specs=(
            P(("groups", "seq", "pair"), None),
            P(),
            P(None, "pair", None),
            P(),
            P(None, "pair"),
            P("pair", None),
            P(),
            P(),
            P(),
            P(),
        ),
        out_specs=(P(("groups", "seq", "pair"), None), P(("groups", "seq"), "pair", None)),
        check_vma=False,
    )
```

profile of v0, /device:TPU:0, one launch (start us, length us, event | category | flops | bytes accessed | tf_op | source)
XLA Modules:
  0.0 302.2 jit_solution(12201782446949053224)
XLA Ops:
  9.8 17.8 %all_to_all.19 = bf16[128,4,384]{2,0,1:T(8,128)(2,1)S(1)} all-to-all(bf16[128,4,384]{2,0,1:T(8,128)(2,1)S(1)} %bitcast.84), channel_id=1, replica_groups=mesh['groups'=2,'seq'=4,'pair'=4] {'pair'}, dimensions={1} | all-to-all | bytes 786432 | tf_op jit(solution)/shard_map/all_to_all | solution.py:53
  27.6 1.5 collective-permute-start
  29.1 2.4 fusion.19
  33.8 2.4 collective-permute-done.1
  38.1 2.6 fusion.10
  40.8 60.6 %reduce-scatter.3.cloned.1.call-done = f32[128,1536]{1,0:T(8,128)} async-done(((f32[512,1536]{1,0:T(8,128)}), f32[128,1536]{1,0:T(8,128)}) %reduce-scatter.3.cloned.1.call-update) | async-done | bytes 786448 | tf_op jit(solution)/shard_map/reduce_scatter | solution.py:55
  104.5 37.2 %all-gather.4.cloned.1.call-done = bf16[512,1536]{1,0:T(8,128)(2,1)} async-done(((bf16[128,1536]{1,0:T(8,128)(2,1)}), bf16[512,1536]{1,0:T(8,128)(2,1)}) %all-gather.4.cloned.1.call-update) | async-done | bytes 1572880 | tf_op jit(solution)/shard_map/all_gather | solution.py:64
  141.7 3.7 %convolution_convert_fusion.1 = bf16[512,768]{1,0:T(8,128)(2,1)} fusion(bf16[512,1536]{1,0:T(8,128)(2,1)} %all-gather.4.cloned.1.call-done, bf16[1536,768]{1,0:T(8,128)(2,1)S(1)} %copy-done), kind=kOutput, calls=%fused_computation.25 | convolution fusion | flops 1208352768 | bytes 4718592 | tf_op jit(solution)/shard_map/dot_general | solution.py:63
  145.4 2.1 reshape.71
  149.5 1.7 copy.43
  151.3 13.8 %all-gather.6.cloned.1.call-done = bf16[2048,256]{1,0:T(8,128)(2,1)} async-done(((bf16[512,256]{1,0:T(8,128)(2,1)}), bf16[2048,256]{1,0:T(8,128)(2,1)}) %all-gather.6.cloned.1.call-update) | async-done | bytes 1048592 | tf_op jit(solution)/shard_map/all_gather | solution.py:80
  165.2 2.2 reshape.73
  167.3 16.0 %all-gather.8.cloned.1.call-done = bf16[2048,256]{1,0:T(8,128)(2,1)} async-done(((bf16[512,256]{1,0:T(8,128)(2,1)}), bf16[2048,256]{1,0:T(8,128)(2,1)}) %all-gather.8.cloned.1.call-update) | async-done | bytes 1048592 | tf_op jit(solution)/shard_map/all_gather | solution.py:81
  183.3 2.2 reshape.75
  185.5 24.8 %while.15 = (s32[]{:T(128)}, f32[2,512]{1,0:T(2,128)S(1)}, f32[2,512]{1,0:T(2,128)S(1)}, f32[2,512,128]{2,1,0:T(8,128)S(1)}, bf16[4,512,2,128]{3,2,1,0:T(2,128)(...) while((s32[]{:T(128)}, f32[2,512]{1,0:T(2,128)S(1)}, ...), condition=%wide.region_6.7_spmd.clone, body=%wide.region_3.6_spmd.clone.sunk | while | flops 273028096 | bytes 17629320 | solution.py:108
  186.9 1.8 bitcast_reduce_fusion.2
  188.7 2.1 fusion.74
  191.7 1.4 constant_dynamic-slice_fusion.3
  193.1 1.8 bitcast_reduce_fusion.2
  194.9 2.1 fusion.74
  197.9 1.4 constant_dynamic-slice_fusion.3
  199.3 1.8 bitcast_reduce_fusion.2
  201.1 2.1 fusion.74
  204.1 1.4 constant_dynamic-slice_fusion.3
  205.5 1.8 bitcast_reduce_fusion.2
  207.3 2.1 fusion.74
  210.6 3.0 convolution_convert_fusion
  213.6 35.4 %reduce-scatter.5.cloned.1.call-done = bf16[128,1536]{1,0:T(8,128)(2,1)} async-done(((bf16[512,1536]{1,0:T(8,128)(2,1)}), bf16[128,1536]{1,0:T(8,128)(2,1)}) %reduce-scatter.5.cloned.1.call-update) | async-done | bytes 393232 | tf_op jit(solution)/shard_map/reduce_scatter | solution.py:112
  249.1 1.8 convert_reduce_fusion
  251.3 30.4 %all_gather.19 = bf16[128,128]{1,0:T(8,128)(2,1)S(1)} all-gather(bf16[8,128]{1,0:T(8,128)(2,1)S(1)} %get-tuple-element.110), channel_id=1, replica_groups=mesh['groups'=2,'seq'=4,'pair'=4] {'seq','pair'}, dimensions={0}, use_global_device_ids=true | all-gather | bytes 34816 | tf_op jit(solution)/shard_map/all_gather | solution.py:128
  281.7 11.9 %all_gather.18 = bf16[32,128]{1,0:T(8,128)(2,1)S(1)} all-gather(bf16[8,128]{1,0:T(8,128)(2,1)S(1)} %get-tuple-element.109), channel_id=1, replica_groups=mesh['groups'=2,'seq'=4,'pair'=4] {'pair'}, dimensions={0}, use_global_device_ids=true | all-gather | bytes 10240 | tf_op jit(solution)/shard_map/all_gather | solution.py:127
  293.6 2.1 fusion.15
  (79 shorter events, 17.8 us)
Async XLA Ops:
  7.2 134.5 %copy-start = (bf16[1536,768]{1,0:T(8,128)(2,1)S(1)}, bf16[1536,768]{1,0:T(8,128)(2,1)}, u32[]{:S(2)}) copy-start(bf16[1536,768]{1,0:T(8,128)(2,1)} %param.16) | copy-start | bytes 7077892
  7.2 94.2 %reduce-scatter.3.cloned.1.call-start = ((), (), s32[]{:S(2)}) async-start(), calls=%async_computation.3 | async-start | bytes 3932160 | tf_op jit(solution)/shard_map/reduce_scatter | solution.py:55
  27.6 5.3 %copy-start.2 = (bf16[5,384,1536]{2,1,0:T(8,128)(2,1)S(1)}, bf16[5,384,1536]{2,1,0:T(8,128)(2,1)}, u32[]{:S(2)}) copy-start(bf16[5,384,1536]{2,1,0:T(8,128)(2,1)} %param.14) | copy-start | bytes 17694724
  27.6 5.3 %collective-permute-start = (bf16[8,384]{1,0:T(8,128)(2,1)S(1)}, bf16[8,384]{1,0:T(8,128)(2,1)S(1)}, u32[]{:S(2)}, u32[]{:S(2)}) collective-permute-start(bf16[8,384]{1,0:T(8,128)(2,1)S(1)} %get-tuple-element.107), channel_id=1, source_target_pairs={{0,4},{4,8},{8,12},{1,5},{5,9},{9,13},{2,6},{6,10},{10,14},{3,7},{... | collective-permute-start | bytes 18440 | tf_op jit(solution)/shard_map/ppermute | solution.py:25
  31.5 4.7 %collective-permute-start.1 = (bf16[8,384]{1,0:T(8,128)(2,1)S(1)}, bf16[8,384]{1,0:T(8,128)(2,1)S(1)}, u32[]{:S(2)}, u32[]{:S(2)}) collective-permute-start(bf16[8,384]{1,0:T(8,128)(2,1)S(1)} %get-tuple-element.108), channel_id=1, source_target_pairs={{4,0},{8,4},{12,8},{5,1},{9,5},{13,9},{6,2},{10,6},{14,10},{7,3},{... | collective-permute-start | bytes 18440 | tf_op jit(solution)/shard_map/ppermute | solution.py:26
  40.8 60.6 %copy-start.3 = (bf16[128,1536]{1,0:T(8,128)(2,1)S(1)}, bf16[128,1536]{1,0:T(8,128)(2,1)}, u32[]{:S(2)}) copy-start(bf16[128,1536]{1,0:T(8,128)(2,1)} %param.12) | copy-start | bytes 1179652
  40.8 62.7 %copy-start.7 = (f32[1536]{0:T(1024)S(1)}, f32[1536]{0:T(1024)}, u32[]{:S(2)}) copy-start(f32[1536]{0:T(1024)} %param.15) | copy-start | bytes 18436
  40.8 100.9 %all-gather.4.cloned.1.call-start = ((), (), s32[]{:S(2)}) async-start(), calls=%async_computation.4 | async-start | bytes 1966080 | tf_op jit(solution)/shard_map/all_gather | solution.py:64
  102.7 0.8 copy-start.4
  104.4 60.7 %all-gather.6.cloned.1.call-start = ((), (), s32[]{:S(2)}) async-start(), calls=%async_computation.5 | async-start | bytes 1310720 | tf_op jit(solution)/shard_map/all_gather | solution.py:80
  149.4 33.9 %all-gather.8.cloned.1.call-start = ((), (), s32[]{:S(2)}) async-start(), calls=%async_computation.6 | async-start | bytes 1310720 | tf_op jit(solution)/shard_map/all_gather | solution.py:81
  151.2 97.9 %reduce-scatter.5.cloned.1.call-start = ((), (), s32[]{:S(2)}) async-start(), calls=%async_computation.7 | async-start | bytes 1966080 | tf_op jit(solution)/shard_map/reduce_scatter | solution.py:112
  188.7 2.2 copy-start.1
  194.9 2.2 copy-start.1
  201.1 2.2 copy-start.1
  207.3 2.2 copy-start.1
  210.5 38.5 %copy-start.5 = (bf16[128,1536]{1,0:T(8,128)(2,1)S(1)}, bf16[128,1536]{1,0:T(8,128)(2,1)}, u32[]{:S(2)}) copy-start(bf16[128,1536]{1,0:T(8,128)(2,1)} %copy-done.4) | copy-start | bytes 1179652
  210.6 40.4 %copy-start.6 = (bf16[1536,256]{1,0:T(8,128)(2,1)S(1)}, bf16[1536,256]{1,0:T(8,128)(2,1)}, u32[]{:S(2)}) copy-start(bf16[1536,256]{1,0:T(8,128)(2,1)} %param.19) | copy-start | bytes 2359300
  210.6 40.4 %copy-start.8 = (f32[1536]{0:T(1024)S(1)}, f32[1536]{0:T(1024)}, u32[]{:S(2)}) copy-start(f32[1536]{0:T(1024)} %param.18) | copy-start | bytes 18436
Sparse Core Ops, SparseCore 0:
  40.9 60.4 reduce-scatter.2
  104.5 37.0 all-gather.3
  149.5 15.5 all-gather.5
  166.6 16.7 all-gather.7
  213.7 35.2 reduce-scatter.4
where the time goes:
time: 303 us; the launch traced here: 302 us
  waiting for transfers between devices  166 us (55%)
  blocking collectives  60 us (20%)
  matrix products  27.2 us (9%)
  local copies, waits for them, and re-layouts  17.1 us (6%)
  other arithmetic  15.3 us (5%)
  between operations  14 us (5%)
  starting transfers between devices  3.04 us (1%)
    reduce_scatter x1, waiting for transfers between devices, shards(): lax.psum_scatter(conv_rows(padded, conv_weight, row_count * lax.axis_size...  60.6 us
    all_gather x1, waiting for transfers between devices, shards(): lax.all_gather(attn_in, 'pair', axis=0, tiled=True)  37.2 us
    reduce_scatter x1, waiting for transfers between devices, shards(): lax.psum_scatter(jnp.dot(attended, w_out, preferred_element_type=jnp.floa...  35.4 us
    all_gather x1, blocking collectives, shards(): all_right = lax.all_gather(right_side, ('seq', 'pair'), axis=0, tiled=True)  30.4 us
    all_to_all x1, blocking collectives, shards(): lax.all_to_all(normed, 'pair', split_axis=1, concat_axis=0, tiled=True)  17.8 us
    all_gather x1, waiting for transfers between devices, shards(): value_piece = lax.all_gather(value_rows, 'seq', axis=0, tiled=True)  16 us
    all_gather x1, waiting for transfers between devices, shards(): key_piece = lax.all_gather(key_rows, 'seq', axis=0, tiled=True)  13.8 us
    all_gather x1, blocking collectives, shards(): row_side = lax.all_gather(left_side, 'pair', axis=0, tiled=True)  11.9 us
  transfers between devices with their start and end apart: 7, of which 6 were waited for; matrix products, arithmetic and copies ran while one was open for 2% of the time, Pallas kernels for 0%

commit v1 on v0

v1 whole, which is shorter than its diff:
```python
import math

import jax
import jax.numpy as jnp
from jax import lax
from jax.sharding import PartitionSpec as P

KEY_SIZE = 128
VALUE_SIZE = 128
DILATION = 4
POOL = 16
PAIR_CH = 128


EPS = 1e-06


def padded_2(value, sides, width):
    for axis, dim in sides:
        peers, length = (lax.axis_size(axis), value.shape[dim])
        up = [(i, (i + 1) % peers) for i in range(peers - 1)]
        down = [(j, i) for i, j in up]
        last = lax.slice_in_dim(value, length - width, length, axis=dim)
        first = lax.slice_in_dim(value, 0, width, axis=dim)
        before = lax.ppermute(last, axis, up)
        after = lax.ppermute(first, axis, down)
        value = jnp.concatenate([before, value, after], axis=dim)
    return value


def norm_rows(values, gain):
    return values * lax.rsqrt(jnp.mean(values * values, axis=-1, keepdims=True) + EPS) * gain


def conv_rows(padded, conv_weight, row_total):
    summed = jnp.zeros((row_total, conv_weight.shape[2]), jnp.float32)
    for offset in range(conv_weight.shape[0]):
        shifted = lax.dynamic_slice_in_dim(padded, offset * DILATION, row_total, 0)
        summed = summed + jnp.dot(shifted, conv_weight[offset], preferred_element_type=jnp.float32)
    return summed


def line_reduce_scatter(partial, axis):
    n = lax.axis_size(axis)
    me = lax.axis_index(axis)
    rows = partial.shape[0] // n
    blocks = partial.reshape(n, rows, partial.shape[1])
    right = [(i, i + 1) for i in range(n - 1)]
    left = [(i + 1, i) for i in range(n - 1)]
    got_r = jnp.zeros((rows, partial.shape[1]), jnp.bfloat16)
    got_l = jnp.zeros((rows, partial.shape[1]), jnp.bfloat16)
    for step in range(1, n):
        idx_r = jnp.clip(me + n - step, 0, n - 1)
        idx_l = jnp.clip(me - (n - step), 0, n - 1)
        send_r = (blocks[idx_r] + got_r.astype(jnp.float32)).astype(jnp.bfloat16)
        send_l = (blocks[idx_l] + got_l.astype(jnp.float32)).astype(jnp.bfloat16)
        got_r = lax.ppermute(send_r, axis, right)
        got_l = lax.ppermute(send_l, axis, left)
    own = blocks[me]
    return own + got_r.astype(jnp.float32) + got_l.astype(jnp.float32)


def line_all_gather(value, axis):
    n = lax.axis_size(axis)
    me = lax.axis_index(axis)
    rows = value.shape[0]
    right = [(i, i + 1) for i in range(n - 1)]
    left = [(i + 1, i) for i in range(n - 1)]
    slots = jnp.zeros((n + 1, rows) + value.shape[1:], value.dtype)
    slots = lax.dynamic_update_index_in_dim(slots, value, me, 0)
    flow_r, flow_l = value, value
    for step in range(1, n):
        flow_r = lax.ppermute(flow_r, axis, right)
        flow_l = lax.ppermute(flow_l, axis, left)
        at_r = jnp.where(me - step >= 0, me - step, n)
        at_l = jnp.where(me + step < n, me + step, n)
        slots = lax.dynamic_update_index_in_dim(slots, flow_r, at_r, 0)
        slots = lax.dynamic_update_index_in_dim(slots, flow_l, at_l, 0)
    return slots[:n].reshape((n * rows,) + value.shape[1:])


def doubling_all_gather(value, axis):
    n = lax.axis_size(axis)
    assert n & (n - 1) == 0
    me = lax.axis_index(axis)
    out = value
    k = 1
    while k < n:
        other = lax.ppermute(out, axis, [(i, i ^ k) for i in range(n)])
        low = (me & k) == 0
        out = jnp.where(low, jnp.concatenate([out, other], 0), jnp.concatenate([other, out], 0))
        k *= 2
    return out


def shards(
    sequence, gain_conv, conv_weight, gain_attn, w_qkv, w_out, gain_pool, w_pair, w_up, w_down
):
    pair_count = lax.axis_size("pair")
    seq_count = lax.axis_size("seq")
    row_count = sequence.shape[0]
    channels = sequence.shape[1]
    local_rows = row_count * pair_count
    inputs = sequence.astype(jnp.float32)
    normed = norm_rows(inputs, gain_conv).astype(jnp.bfloat16)
    swapped = lax.all_to_all(normed, "pair", split_axis=1, concat_axis=0, tiled=True)
    padded = padded_2(swapped, (("seq", 0),), DILATION * (conv_weight.shape[0] - 1) // 2)
    with jax.named_scope("conv_reduce"):
        summed = line_reduce_scatter(conv_rows(padded, conv_weight, local_rows), "pair")
    first_out = (inputs + summed).astype(jnp.bfloat16)
    attn_in = norm_rows(first_out.astype(jnp.float32), gain_attn).astype(jnp.bfloat16)
    with jax.named_scope("attn_in_gather"):
        block_in = line_all_gather(attn_in, "pair")
    projected = jnp.dot(block_in, w_qkv, preferred_element_type=jnp.float32).astype(jnp.bfloat16)
    head_count = projected.shape[1] // (2 * KEY_SIZE + VALUE_SIZE)
    grouped = projected.reshape(local_rows, head_count, 2 * KEY_SIZE + VALUE_SIZE).transpose(1, 0, 2)
    queries = grouped[:, :, :KEY_SIZE]
    kv = grouped[:, :, KEY_SIZE:]
    scale = 1.0 / math.sqrt(KEY_SIZE)
    ring = [(i, (i + 1) % seq_count) for i in range(seq_count)]

    def attend(state, kv_block):
        running_max, running_sum, weighted = state
        key_block = kv_block[:, :, :KEY_SIZE]
        value_block = kv_block[:, :, KEY_SIZE:]
        scores = (
            jnp.einsum("hqd,hkd->hqk", queries, key_block, preferred_element_type=jnp.float32)
            * scale
        )
        new_max = jnp.maximum(running_max, jnp.max(scores, axis=-1))
        shrink = jnp.exp(running_max - new_max)
        weights = jnp.exp(scores - new_max[:, :, None])
        running_sum = running_sum * shrink + jnp.sum(weights, axis=-1)
        update = jnp.einsum(
            "hqk,hkd->hqd",
            weights.astype(jnp.bfloat16),
            value_block,
            preferred_element_type=jnp.float32,
        )
        weighted = weighted * shrink[:, :, None] + update
        return (new_max, running_sum, weighted)

    state = (
        jnp.full((head_count, local_rows), -1e30, jnp.float32),
        jnp.zeros((head_count, local_rows), jnp.float32),
        jnp.zeros((head_count, local_rows, VALUE_SIZE), jnp.float32),
    )
    with jax.named_scope("kv_ring"):
        current = kv
        for step in range(seq_count):
            if step + 1 < seq_count:
                arriving = lax.ppermute(current, "seq", ring)
            state = attend(state, current)
            if step + 1 < seq_count:
                current = arriving
    running_max, running_sum, weighted = state
    attended = (weighted / running_sum[:, :, None]).astype(jnp.bfloat16)
    attended = attended.transpose(1, 0, 2).reshape(local_rows, head_count * VALUE_SIZE)
    with jax.named_scope("out_reduce"):
        mixed = line_reduce_scatter(
            jnp.dot(attended, w_out, preferred_element_type=jnp.float32), "pair"
        )
    seq_out = (first_out.astype(jnp.float32) + mixed).astype(jnp.bfloat16)
    bin_count = row_count // POOL
    pooled = jnp.mean(seq_out.astype(jnp.float32).reshape(bin_count, POOL, channels), axis=1)
    bin_norm = norm_rows(pooled, gain_pool).astype(jnp.bfloat16)
    sides = jnp.dot(bin_norm, w_pair, preferred_element_type=jnp.float32).astype(jnp.bfloat16)
    with jax.named_scope("sides_gather"):
        all_sides = doubling_all_gather(doubling_all_gather(sides, "pair"), "seq")
    tile_rows = bin_count * pair_count
    tile_cols = bin_count * seq_count
    row_side = lax.dynamic_slice_in_dim(
        all_sides, lax.axis_index("seq") * tile_rows, tile_rows, 0
    )[:, :PAIR_CH]
    column_side = lax.dynamic_slice_in_dim(
        all_sides, lax.axis_index("pair") * tile_cols, tile_cols, 0
    )[:, PAIR_CH:]
    pair_tile = (
        row_side.astype(jnp.float32)[:, None, :] * column_side.astype(jnp.float32)[None, :, :]
    ).astype(jnp.bfloat16)
    flat_rows = pair_tile.reshape(tile_rows * tile_cols, PAIR_CH)
    hidden = jax.nn.relu(jnp.dot(flat_rows, w_up, preferred_element_type=jnp.float32)).astype(
        jnp.bfloat16
    )
    pair_out = flat_rows.astype(jnp.float32) + jnp.dot(
        hidden, w_down, preferred_element_type=jnp.float32
    )
    pair_map = pair_out.astype(jnp.bfloat16).reshape(tile_rows, tile_cols, PAIR_CH)
    return (seq_out, pair_map)


def solution(mesh):
    return jax.shard_map(
        shards,
        mesh=mesh,
        in_specs=(
            P(("groups", "seq", "pair"), None),
            P(),
            P(None, "pair", None),
            P(),
            P(None, "pair"),
            P("pair", None),
            P(),
            P(),
            P(),
            P(),
        ),
        out_specs=(P(("groups", "seq", "pair"), None), P(("groups", "seq"), "pair", None)),
        check_vma=False,
    )
```

time: 303 us -> 229 us (0.76)
  blocking collectives: 60 us -> 0 us
  starting transfers between devices: 3.04 us -> 62.1 us
  waiting for transfers between devices: 166 us -> 125 us
  between operations: 14 us -> 1.2 us
  matrix products: 27.2 us -> 15.6 us
  local copies, waits for them, and re-layouts: 17.1 us -> 10.8 us
    ppermute x0 -> x25, waiting for transfers between devices: none -> 111 us  [the longest x6 32.6 us: line_reduce_scatter(): got_l = lax.ppermute(send_l, axis, left)]
    reduce_scatter x2 -> x0, waiting for transfers between devices: 96 us -> none  [the longest x1 60.6 us: shards(): lax.psum_scatter(conv_rows(padded, conv_weight, row_count * lax.axis_size...]
    all_gather x3 -> x0, waiting for transfers between devices: 67.1 us -> none  [the longest x1 37.2 us: shards(): lax.all_gather(attn_in, 'pair', axis=0, tiled=True)]
    ppermute x0 -> x25, starting transfers between devices: none -> 53 us  [the longest x6 25 us: line_reduce_scatter(): got_r = lax.ppermute(send_r, axis, right)]
    all_gather x2 -> x0, blocking collectives: 42.2 us -> none  [the longest x1 30.4 us: shards(): all_right = lax.all_gather(right_side, ('seq', 'pair'), axis=0, tiled=True)]
    all_to_all x1 -> x0, blocking collectives: 17.8 us -> none  [shards(): lax.all_to_all(normed, 'pair', split_axis=1, concat_axis=0, tiled=True)]
    all_to_all x0 -> x1, waiting for transfers between devices: none -> 11.7 us  [shards(): lax.all_to_all(normed, 'pair', split_axis=1, concat_axis=0, tiled=True)]
    dot_general x9, matrix products: 13.9 us -> 6.07 us  [the longest x4 2.91 us: attend(): jnp.einsum('hqk,hkd->hqd', weights.astype(jnp.bfloat16), value_block, pre...]
  transfers between devices with their start and end apart: 7 -> 28, of which waited for: 6 -> 21; matrix products, arithmetic and copies ran while one was open for 2% -> 5% of each run, Pallas kernels for 0% -> 0%
where the time goes in v1:
time: 229 us; the launch traced here: 228 us
  waiting for transfers between devices  125 us (55%)
  starting transfers between devices  62.1 us (27%)
  matrix products  15.6 us (7%)
  other arithmetic  13.1 us (6%)
  local copies, waits for them, and re-layouts  10.8 us (5%)
    ppermute x6, waiting for transfers between devices, line_reduce_scatter(): got_l = lax.ppermute(send_l, axis, left)  32.6 us
    ppermute x6, waiting for transfers between devices, line_reduce_scatter(): got_r = lax.ppermute(send_r, axis, right)  28.1 us
    ppermute x6, starting transfers between devices, line_reduce_scatter(): got_r = lax.ppermute(send_r, axis, right)  25 us
    ppermute x3, waiting for transfers between devices, shards(): arriving = lax.ppermute(current, 'seq', ring)  24.4 us
    ppermute x3, waiting for transfers between devices, line_all_gather(): flow_r = lax.ppermute(flow_r, axis, right)  13.1 us
    ppermute x3, starting transfers between devices, line_all_gather(): flow_r = lax.ppermute(flow_r, axis, right)  12.2 us
    all_to_all x1, waiting for transfers between devices, shards(): lax.all_to_all(normed, 'pair', split_axis=1, concat_axis=0, tiled=True)  11.7 us
    ppermute x4, waiting for transfers between devices, doubling_all_gather(): other = lax.ppermute(out, axis, [(i, i ^ k) for i in range(n)])  9.48 us
  transfers between devices with their start and end apart: 28, of which 21 were waited for; matrix products, arithmetic and copies ran while one was open for 5% of the time, Pallas kernels for 0%

profile of v1, /device:TPU:0, one launch (start us, length us, event | category | flops | bytes accessed | tf_op | source)
XLA Modules:
  0.0 228.1 jit_solution(8391843378703551363)
XLA Ops:
  3.9 6.3 %all-to-all-start = ((bf16[128,4,384]{2,0,1:T(8,128)(2,1)}), bf16[128,4,384]{2,0,1:T(8,128)(2,1)S(1)}, u32[]{:S(2)}, u32[]{:S(2)}) async-start(bf16[128,4,384]{2,0,1:T(8,128)(2,1)} %bitcast.205), calls=%async_computation | async-start | bytes 786432 | tf_op jit(solution)/shard_map/all_to_all | solution.py:106
  10.2 11.7 %all-to-all-done = bf16[128,4,384]{2,0,1:T(8,128)(2,1)S(1)} async-done(((bf16[128,4,384]{2,0,1:T(8,128)(2,1)}), bf16[128,4,384]{2,0,1:T(8,128)(2,1)S(1)}, u32[]{:S(2)}, u32[]{:S(2)}) %all-to-all-start) | async-done | bytes 393248 | tf_op jit(solution)/shard_map/all_to_all | solution.py:106
  23.5 2.4 %fusion.26 = f32[512,1536]{1,0:T(8,128)S(1)} fusion(bf16[512,384]{1,0:T(8,128)(2,1)S(1)} %bitcast.212, bf16[5,384,1536]{2,1,0:T(8,128)(2,1)} %param.12), kind=kOutput, calls=%fused_computation.48 | convolution fusion | flops 603979776 | bytes 4718592 | tf_op jit(solution)/shard_map/conv_reduce/dot_general | solution.py:39
  28.2 2.3 %collective-permute-done.1 = bf16[8,384]{1,0:T(8,128)(2,1)S(1)} collective-permute-done((bf16[8,384]{1,0:T(8,128)(2,1)S(1)}, bf16[8,384]{1,0:T(8,128)(2,1)S(1)}, u32[]{:S(2)}, u32[]{:S(2)}) %collective-permute-start.1) | collective-permute-done | bytes 6176 | tf_op jit(solution)/shard_map/ppermute | solution.py:26
  35.2 2.2 collective-permute-start.2
  38.7 5.8 %collective-permute-done.2 = bf16[128,1536]{1,0:T(8,128)(2,1)} collective-permute-done((bf16[128,1536]{1,0:T(8,128)(2,1)S(1)}, bf16[128,1536]{1,0:T(8,128)(2,1)}, u32[]{:S(2)}, u32[]{:S(2)}) %collective-permute-start.2) | collective-permute-done | bytes 393248 | tf_op jit(solution)/shard_map/conv_reduce/ppermute | solution.py:57
  45.8 5.2 %collective-permute-start.3 = (bf16[128,1536]{1,0:T(8,128)(2,1)S(1)}, bf16[128,1536]{1,0:T(8,128)(2,1)}, u32[]{:S(2)}, u32[]{:S(2)}) collective-permute-start(bf16[128,1536]{1,0:T(8,128)(2,1)S(1)} %fusion.65), channel_id=1, source_target_pairs={{0,1},{1,2},{2,3},{4,5},{5,6},{6,7},{8,9},{9,10},{10,11},{12,13},{... | collective-permute-start | bytes 1179656 | tf_op jit(solution)/shard_map/conv_reduce/ppermute | solution.py:57
  51.1 8.0 %collective-permute-done.3 = bf16[128,1536]{1,0:T(8,128)(2,1)} collective-permute-done((bf16[128,1536]{1,0:T(8,128)(2,1)S(1)}, bf16[128,1536]{1,0:T(8,128)(2,1)}, u32[]{:S(2)}, u32[]{:S(2)}) %collective-permute-start.3) | collective-permute-done | bytes 393248 | tf_op jit(solution)/shard_map/conv_reduce/ppermute | solution.py:57
  59.1 2.5 %fusion.66 = (bf16[128,1536]{1,0:T(8,128)(2,1)}, bf16[128,1536]{1,0:T(8,128)(2,1)S(1)}) fusion(bf16[128,1536]{1,0:T(8,128)(2,1)} %collective-permute-done.3, f32[4,128,1536]{2,1,0:T(8,128)} %bitcast.208, s32[]{:T(128)S(6)} %min.25, bf16[128,1536]{1,0:T(8,128)(2,1)} %collective-permute-done.5, s32[]{:T(128)S(6)} %min.29), kind=kLoop, calls=%fused_computation.96 | loop fusion | flops 1179648 | bytes 3145736 | tf_op jit(solution)/shard_map/conv_reduce/convert_element_type | solution.py:55
  62.9 5.9 %collective-permute-start.4 = (bf16[128,1536]{1,0:T(8,128)(2,1)}, bf16[128,1536]{1,0:T(8,128)(2,1)}, u32[]{:S(2)}, u32[]{:S(2)}) collective-permute-start(bf16[128,1536]{1,0:T(8,128)(2,1)} %get-tuple-element.18), channel_id=1, source_target_pairs={{0,1},{1,2},{2,3},{4,5},{5,6},{6,7},{8,9},{9,10},{10,11},{12,13},{... | collective-permute-start | bytes 1179656 | tf_op jit(solution)/shard_map/conv_reduce/ppermute | solution.py:57
  68.8 7.1 %collective-permute-done.6 = bf16[128,1536]{1,0:T(8,128)(2,1)S(1)} collective-permute-done((bf16[128,1536]{1,0:T(8,128)(2,1)S(1)}, bf16[128,1536]{1,0:T(8,128)(2,1)S(1)}, u32[]{:S(2)}, u32[]{:S(2)}) %collective-permute-start.6) | collective-permute-done | bytes 393248 | tf_op jit(solution)/shard_map/conv_reduce/ppermute | solution.py:58
  78.4 11.6 %collective-permute-done.7 = bf16[128,1536]{1,0:T(8,128)(2,1)S(1)} collective-permute-done((bf16[128,1536]{1,0:T(8,128)(2,1)S(1)}, bf16[128,1536]{1,0:T(8,128)(2,1)S(1)}, u32[]{:S(2)}, u32[]{:S(2)}) %collective-permute-start.7) | collective-permute-done | bytes 393248 | tf_op jit(solution)/shard_map/conv_reduce/ppermute | solution.py:58
  94.1 3.6 %collective-permute-start.8 = (bf16[128,1536]{1,0:T(8,128)(2,1)}, bf16[128,1536]{1,0:T(8,128)(2,1)S(1)}, u32[]{:S(2)}, u32[]{:S(2)}) collective-permute-start(bf16[128,1536]{1,0:T(8,128)(2,1)} %get-tuple-element.11), channel_id=1, source_target_pairs={{0,1},{1,2},{2,3},{4,5},{5,6},{6,7},{8,9},{9,10},{10,11},{12,13},{... | collective-permute-start | bytes 1179656 | tf_op jit(solution)/shard_map/attn_in_gather/ppermute | solution.py:73
  99.0 6.5 %collective-permute-done.8 = bf16[128,1536]{1,0:T(8,128)(2,1)S(1)} collective-permute-done((bf16[128,1536]{1,0:T(8,128)(2,1)}, bf16[128,1536]{1,0:T(8,128)(2,1)S(1)}, u32[]{:S(2)}, u32[]{:S(2)}) %collective-permute-start.8) | collective-permute-done | bytes 393248 | tf_op jit(solution)/shard_map/attn_in_gather/ppermute | solution.py:73
  105.5 4.3 %collective-permute-start.10 = (bf16[128,1536]{1,0:T(8,128)(2,1)S(1)}, bf16[128,1536]{1,0:T(8,128)(2,1)S(1)}, u32[]{:S(2)}, u32[]{:S(2)}) collective-permute-start(bf16[128,1536]{1,0:T(8,128)(2,1)S(1)} %collective-permute-done.8), channel_id=1, source_target_pairs={{0,1},{1,2},{2,3},{4,5},{5,6},{6,7},{8,9},{9,10},{10,11},{12,13},{... | collective-permute-start | bytes 1179656 | tf_op jit(solution)/shard_map/attn_in_gather/ppermute | solution.py:73
  112.7 3.8 %collective-permute-done.10 = bf16[128,1536]{1,0:T(8,128)(2,1)S(1)} collective-permute-done((bf16[128,1536]{1,0:T(8,128)(2,1)S(1)}, bf16[128,1536]{1,0:T(8,128)(2,1)S(1)}, u32[]{:S(2)}, u32[]{:S(2)}) %collective-permute-start.10) | collective-permute-done | bytes 393248 | tf_op jit(solution)/shard_map/attn_in_gather/ppermute | solution.py:73
  116.5 4.4 %collective-permute-start.12 = (bf16[128,1536]{1,0:T(8,128)(2,1)S(1)}, bf16[128,1536]{1,0:T(8,128)(2,1)S(1)}, u32[]{:S(2)}, u32[]{:S(2)}) collective-permute-start(bf16[128,1536]{1,0:T(8,128)(2,1)S(1)} %collective-permute-done.10), channel_id=1, source_target_pairs={{0,1},{1,2},{2,3},{4,5},{5,6},{6,7},{8,9},{9,10},{10,11},{12,13},{... | collective-permute-start | bytes 1179656 | tf_op jit(solution)/shard_map/attn_in_gather/ppermute | solution.py:73
  123.8 2.8 %collective-permute-done.12 = bf16[128,1536]{1,0:T(8,128)(2,1)S(1)} collective-permute-done((bf16[128,1536]{1,0:T(8,128)(2,1)S(1)}, bf16[128,1536]{1,0:T(8,128)(2,1)S(1)}, u32[]{:S(2)}, u32[]{:S(2)}) %collective-permute-start.12) | collective-permute-done | bytes 393248 | tf_op jit(solution)/shard_map/attn_in_gather/ppermute | solution.py:73
  127.4 3.4 %collective-permute-done.13 = bf16[128,1536]{1,0:T(8,128)(2,1)S(1)} collective-permute-done((bf16[128,1536]{1,0:T(8,128)(2,1)S(1)}, bf16[128,1536]{1,0:T(8,128)(2,1)S(1)}, u32[]{:S(2)}, u32[]{:S(2)}) %collective-permute-start.13) | collective-permute-done | bytes 393248 | tf_op jit(solution)/shard_map/attn_in_gather/ppermute | solution.py:74
  134.6 8.6 %collective-permute-done.14 = bf16[2,512,256]{2,1,0:T(8,128)(2,1)S(1)} collective-permute-done((bf16[2,512,256]{2,1,0:T(8,128)(2,1)S(1)}, bf16[2,512,256]{2,1,0:T(8,128)(2,1)S(1)}, u32[]{:S(2)}, u32[]{:S(2)}) %collective-permute-start.14) | collective-permute-done | bytes 524320 | tf_op jit(solution)/shard_map/kv_ring/ppermute | solution.py:152
  143.7 8.2 %collective-permute-done.15 = bf16[2,512,256]{2,1,0:T(8,128)(2,1)S(1)} collective-permute-done((bf16[2,512,256]{2,1,0:T(8,128)(2,1)S(1)}, bf16[2,512,256]{2,1,0:T(8,128)(2,1)S(1)}, u32[]{:S(2)}, u32[]{:S(2)}) %collective-permute-start.15) | collective-permute-done | bytes 524320 | tf_op jit(solution)/shard_map/kv_ring/ppermute | solution.py:152
  152.7 7.7 %collective-permute-done.16 = bf16[2,512,256]{2,1,0:T(8,128)(2,1)S(1)} collective-permute-done((bf16[2,512,256]{2,1,0:T(8,128)(2,1)S(1)}, bf16[2,512,256]{2,1,0:T(8,128)(2,1)S(1)}, u32[]{:S(2)}, u32[]{:S(2)}) %collective-permute-start.16) | collective-permute-done | bytes 524320 | tf_op jit(solution)/shard_map/kv_ring/ppermute | solution.py:152
  167.5 2.2 collective-permute-start.17
  171.1 7.1 %collective-permute-done.17 = bf16[128,1536]{1,0:T(8,128)(2,1)S(1)} collective-permute-done((bf16[128,1536]{1,0:T(8,128)(2,1)S(1)}, bf16[128,1536]{1,0:T(8,128)(2,1)S(1)}, u32[]{:S(2)}, u32[]{:S(2)}) %collective-permute-start.17) | collective-permute-done | bytes 393248 | tf_op jit(solution)/shard_map/out_reduce/ppermute | solution.py:57
  178.2 4.4 %collective-permute-start.18 = (bf16[128,1536]{1,0:T(8,128)(2,1)S(1)}, bf16[128,1536]{1,0:T(8,128)(2,1)S(1)}, u32[]{:S(2)}, u32[]{:S(2)}) collective-permute-start(bf16[128,1536]{1,0:T(8,128)(2,1)S(1)} %fusion.58), channel_id=1, source_target_pairs={{0,1},{1,2},{2,3},{4,5},{5,6},{6,7},{8,9},{9,10},{10,11},{12,13},{... | collective-permute-start | bytes 1179656 | tf_op jit(solution)/shard_map/out_reduce/ppermute | solution.py:57
  182.7 7.3 %collective-permute-done.18 = bf16[128,1536]{1,0:T(8,128)(2,1)S(1)} collective-permute-done((bf16[128,1536]{1,0:T(8,128)(2,1)S(1)}, bf16[128,1536]{1,0:T(8,128)(2,1)S(1)}, u32[]{:S(2)}, u32[]{:S(2)}) %collective-permute-start.18) | collective-permute-done | bytes 393248 | tf_op jit(solution)/shard_map/out_reduce/ppermute | solution.py:57
  191.6 5.0 %collective-permute-start.19 = (bf16[128,1536]{1,0:T(8,128)(2,1)S(1)}, bf16[128,1536]{1,0:T(8,128)(2,1)S(1)}, u32[]{:S(2)}, u32[]{:S(2)}) collective-permute-start(bf16[128,1536]{1,0:T(8,128)(2,1)S(1)} %get-tuple-element.14), channel_id=1, source_target_pairs={{0,1},{1,2},{2,3},{4,5},{5,6},{6,7},{8,9},{9,10},{10,11},{12,13},{... | collective-permute-start | bytes 1179656 | tf_op jit(solution)/shard_map/out_reduce/ppermute | solution.py:57
  196.6 5.5 %collective-permute-done.21 = bf16[128,1536]{1,0:T(8,128)(2,1)S(1)} collective-permute-done((bf16[128,1536]{1,0:T(8,128)(2,1)S(1)}, bf16[128,1536]{1,0:T(8,128)(2,1)S(1)}, u32[]{:S(2)}, u32[]{:S(2)}) %collective-permute-start.21) | collective-permute-done | bytes 393248 | tf_op jit(solution)/shard_map/out_reduce/ppermute | solution.py:58
  203.7 8.4 %collective-permute-done.22 = bf16[128,1536]{1,0:T(8,128)(2,1)S(1)} collective-permute-done((bf16[128,1536]{1,0:T(8,128)(2,1)S(1)}, bf16[128,1536]{1,0:T(8,128)(2,1)S(1)}, u32[]{:S(2)}, u32[]{:S(2)}) %collective-permute-start.22) | collective-permute-done | bytes 393248 | tf_op jit(solution)/shard_map/out_reduce/ppermute | solution.py:58
  217.0 2.0 collective-permute-start.24
  219.0 2.6 %collective-permute-done.24 = bf16[16,256]{1,0:T(8,128)(2,1)S(1)} collective-permute-done((bf16[16,256]{1,0:T(8,128)(2,1)S(1)}, bf16[16,256]{1,0:T(8,128)(2,1)S(1)}, u32[]{:S(2)}, u32[]{:S(2)}) %collective-permute-start.24) | collective-permute-done | bytes 8224 | tf_op jit(solution)/shard_map/sides_gather/ppermute | solution.py:89
  222.9 3.9 %collective-permute-done.26 = bf16[64,256]{1,0:T(8,128)(2,1)S(1)} collective-permute-done((bf16[64,256]{1,0:T(8,128)(2,1)S(1)}, bf16[64,256]{1,0:T(8,128)(2,1)S(1)}, u32[]{:S(2)}, u32[]{:S(2)}) %collective-permute-start.26) | collective-permute-done | bytes 32800 | tf_op jit(solution)/shard_map/sides_gather/ppermute | solution.py:89
  (100 shorter events, 54.3 us)
Async XLA Ops:
  0.6 132.4 %copy-start = (bf16[1536,768]{1,0:T(8,128)(2,1)S(1)}, bf16[1536,768]{1,0:T(8,128)(2,1)}, u32[]{:S(2)}) copy-start(bf16[1536,768]{1,0:T(8,128)(2,1)} %param.14) | copy-start | bytes 7077892
  3.9 18.0 %all-to-all-start = ((bf16[128,4,384]{2,0,1:T(8,128)(2,1)}), bf16[128,4,384]{2,0,1:T(8,128)(2,1)S(1)}, u32[]{:S(2)}, u32[]{:S(2)}) async-start(bf16[128,4,384]{2,0,1:T(8,128)(2,1)} %bitcast.205), calls=%async_computation | async-start | bytes 786432 | tf_op jit(solution)/shard_map/all_to_all | solution.py:106
  21.9 5.3 %collective-permute-start = (bf16[8,384]{1,0:T(8,128)(2,1)S(1)}, bf16[8,384]{1,0:T(8,128)(2,1)S(1)}, u32[]{:S(2)}, u32[]{:S(2)}) collective-permute-start(bf16[8,384]{1,0:T(8,128)(2,1)S(1)} %get-tuple-element.22), channel_id=1, source_target_pairs={{0,4},{4,8},{8,12},{1,5},{5,9},{9,13},{2,6},{6,10},{10,14},{3,7},{... | collective-permute-start | bytes 18440 | tf_op jit(solution)/shard_map/ppermute | solution.py:25
  25.9 4.6 %collective-permute-start.1 = (bf16[8,384]{1,0:T(8,128)(2,1)S(1)}, bf16[8,384]{1,0:T(8,128)(2,1)S(1)}, u32[]{:S(2)}, u32[]{:S(2)}) collective-permute-start(bf16[8,384]{1,0:T(8,128)(2,1)S(1)} %get-tuple-element.23), channel_id=1, source_target_pairs={{4,0},{8,4},{12,8},{5,1},{9,5},{13,9},{6,2},{10,6},{14,10},{7,3},{... | collective-permute-start | bytes 18440 | tf_op jit(solution)/shard_map/ppermute | solution.py:26
  35.2 9.3 %collective-permute-start.2 = (bf16[128,1536]{1,0:T(8,128)(2,1)S(1)}, bf16[128,1536]{1,0:T(8,128)(2,1)}, u32[]{:S(2)}, u32[]{:S(2)}) collective-permute-start(bf16[128,1536]{1,0:T(8,128)(2,1)S(1)} %get-tuple-element.20), channel_id=1, source_target_pairs={{0,1},{1,2},{2,3},{4,5},{5,6},{6,7},{8,9},{9,10},{10,11},{12,13},{... | collective-permute-start | bytes 1179656 | tf_op jit(solution)/shard_map/conv_reduce/ppermute | solution.py:57
  37.4 13.7 %collective-permute-start.5 = (bf16[128,1536]{1,0:T(8,128)(2,1)S(1)}, bf16[128,1536]{1,0:T(8,128)(2,1)}, u32[]{:S(2)}, u32[]{:S(2)}) collective-permute-start(bf16[128,1536]{1,0:T(8,128)(2,1)S(1)} %get-tuple-element.21), channel_id=1, source_target_pairs={{1,0},{2,1},{3,2},{5,4},{6,5},{7,6},{9,8},{10,9},{11,10},{13,12},{... | collective-permute-start | bytes 1179656 | tf_op jit(solution)/shard_map/conv_reduce/ppermute | solution.py:58
  45.8 13.2 %collective-permute-start.3 = (bf16[128,1536]{1,0:T(8,128)(2,1)S(1)}, bf16[128,1536]{1,0:T(8,128)(2,1)}, u32[]{:S(2)}, u32[]{:S(2)}) collective-permute-start(bf16[128,1536]{1,0:T(8,128)(2,1)S(1)} %fusion.65), channel_id=1, source_target_pairs={{0,1},{1,2},{2,3},{4,5},{5,6},{6,7},{8,9},{9,10},{10,11},{12,13},{... | collective-permute-start | bytes 1179656 | tf_op jit(solution)/shard_map/conv_reduce/ppermute | solution.py:57
  51.1 39.0 %copy-start.3 = (bf16[128,1536]{1,0:T(8,128)(2,1)S(1)}, bf16[128,1536]{1,0:T(8,128)(2,1)}, u32[]{:S(2)}) copy-start(bf16[128,1536]{1,0:T(8,128)(2,1)} %param.10) | copy-start | bytes 1179652
  61.6 14.3 %collective-permute-start.6 = (bf16[128,1536]{1,0:T(8,128)(2,1)S(1)}, bf16[128,1536]{1,0:T(8,128)(2,1)S(1)}, u32[]{:S(2)}, u32[]{:S(2)}) collective-permute-start(bf16[128,1536]{1,0:T(8,128)(2,1)S(1)} %get-tuple-element.19), channel_id=1, source_target_pairs={{1,0},{2,1},{3,2},{5,4},{6,5},{7,6},{9,8},{10,9},{11,10},{13,12},{... | collective-permute-start | bytes 1179656 | tf_op jit(solution)/shard_map/conv_reduce/ppermute | solution.py:58
  62.9 15.6 %collective-permute-start.4 = (bf16[128,1536]{1,0:T(8,128)(2,1)}, bf16[128,1536]{1,0:T(8,128)(2,1)}, u32[]{:S(2)}, u32[]{:S(2)}) collective-permute-start(bf16[128,1536]{1,0:T(8,128)(2,1)} %get-tuple-element.18), channel_id=1, source_target_pairs={{0,1},{1,2},{2,3},{4,5},{5,6},{6,7},{8,9},{9,10},{10,11},{12,13},{... | collective-permute-start | bytes 1179656 | tf_op jit(solution)/shard_map/conv_reduce/ppermute | solution.py:57
  77.1 12.9 %collective-permute-start.7 = (bf16[128,1536]{1,0:T(8,128)(2,1)S(1)}, bf16[128,1536]{1,0:T(8,128)(2,1)S(1)}, u32[]{:S(2)}, u32[]{:S(2)}) collective-permute-start(bf16[128,1536]{1,0:T(8,128)(2,1)S(1)} %fusion.64), channel_id=1, source_target_pairs={{1,0},{2,1},{3,2},{5,4},{6,5},{7,6},{9,8},{10,9},{11,10},{13,12},{... | collective-permute-start | bytes 1179656 | tf_op jit(solution)/shard_map/conv_reduce/ppermute | solution.py:58
  94.1 11.4 %collective-permute-start.8 = (bf16[128,1536]{1,0:T(8,128)(2,1)}, bf16[128,1536]{1,0:T(8,128)(2,1)S(1)}, u32[]{:S(2)}, u32[]{:S(2)}) collective-permute-start(bf16[128,1536]{1,0:T(8,128)(2,1)} %get-tuple-element.11), channel_id=1, source_target_pairs={{0,1},{1,2},{2,3},{4,5},{5,6},{6,7},{8,9},{9,10},{10,11},{12,13},{... | collective-permute-start | bytes 1179656 | tf_op jit(solution)/shard_map/attn_in_gather/ppermute | solution.py:73
  97.7 12.2 %collective-permute-start.9 = (bf16[128,1536]{1,0:T(8,128)(2,1)}, bf16[128,1536]{1,0:T(8,128)(2,1)S(1)}, u32[]{:S(2)}, u32[]{:S(2)}) collective-permute-start(bf16[128,1536]{1,0:T(8,128)(2,1)} %get-tuple-element.11), channel_id=1, source_target_pairs={{1,0},{2,1},{3,2},{5,4},{6,5},{7,6},{9,8},{10,9},{11,10},{13,12},{... | collective-permute-start | bytes 1179656 | tf_op jit(solution)/shard_map/attn_in_gather/ppermute | solution.py:74
  105.5 10.9 %collective-permute-start.10 = (bf16[128,1536]{1,0:T(8,128)(2,1)S(1)}, bf16[128,1536]{1,0:T(8,128)(2,1)S(1)}, u32[]{:S(2)}, u32[]{:S(2)}) collective-permute-start(bf16[128,1536]{1,0:T(8,128)(2,1)S(1)} %collective-permute-done.8), channel_id=1, source_target_pairs={{0,1},{1,2},{2,3},{4,5},{5,6},{6,7},{8,9},{9,10},{10,11},{12,13},{... | collective-permute-start | bytes 1179656 | tf_op jit(solution)/shard_map/attn_in_gather/ppermute | solution.py:73
  109.9 11.0 %collective-permute-start.11 = (bf16[128,1536]{1,0:T(8,128)(2,1)S(1)}, bf16[128,1536]{1,0:T(8,128)(2,1)S(1)}, u32[]{:S(2)}, u32[]{:S(2)}) collective-permute-start(bf16[128,1536]{1,0:T(8,128)(2,1)S(1)} %collective-permute-done.9), channel_id=1, source_target_pairs={{1,0},{2,1},{3,2},{5,4},{6,5},{7,6},{9,8},{10,9},{11,10},{13,12},{... | collective-permute-start | bytes 1179656 | tf_op jit(solution)/shard_map/attn_in_gather/ppermute | solution.py:74
  116.5 10.1 %collective-permute-start.12 = (bf16[128,1536]{1,0:T(8,128)(2,1)S(1)}, bf16[128,1536]{1,0:T(8,128)(2,1)S(1)}, u32[]{:S(2)}, u32[]{:S(2)}) collective-permute-start(bf16[128,1536]{1,0:T(8,128)(2,1)S(1)} %collective-permute-done.10), channel_id=1, source_target_pairs={{0,1},{1,2},{2,3},{4,5},{5,6},{6,7},{8,9},{9,10},{10,11},{12,13},{... | collective-permute-start | bytes 1179656 | tf_op jit(solution)/shard_map/attn_in_gather/ppermute | solution.py:73
  120.9 9.8 %collective-permute-start.13 = (bf16[128,1536]{1,0:T(8,128)(2,1)S(1)}, bf16[128,1536]{1,0:T(8,128)(2,1)S(1)}, u32[]{:S(2)}, u32[]{:S(2)}) collective-permute-start(bf16[128,1536]{1,0:T(8,128)(2,1)S(1)} %collective-permute-done.11), channel_id=1, source_target_pairs={{1,0},{2,1},{3,2},{5,4},{6,5},{7,6},{9,8},{10,9},{11,10},{13,12},{... | collective-permute-start | bytes 1179656 | tf_op jit(solution)/shard_map/attn_in_gather/ppermute | solution.py:74
  134.6 8.7 %collective-permute-start.14 = (bf16[2,512,256]{2,1,0:T(8,128)(2,1)S(1)}, bf16[2,512,256]{2,1,0:T(8,128)(2,1)S(1)}, u32[]{:S(2)}, u32[]{:S(2)}) collective-permute-start(bf16[2,512,256]{2,1,0:T(8,128)(2,1)S(1)} %slice.92), channel_id=1, source_target_pairs={{0,4},{4,8},{8,12},{12,0},{1,5},{5,9},{9,13},{13,1},{2,6},{6,10},{... | collective-permute-start | bytes 1572872 | tf_op jit(solution)/shard_map/kv_ring/ppermute | solution.py:152
  143.2 8.6 %collective-permute-start.15 = (bf16[2,512,256]{2,1,0:T(8,128)(2,1)S(1)}, bf16[2,512,256]{2,1,0:T(8,128)(2,1)S(1)}, u32[]{:S(2)}, u32[]{:S(2)}) collective-permute-start(bf16[2,512,256]{2,1,0:T(8,128)(2,1)S(1)} %collective-permute-done.14), channel_id=1, source_target_pairs={{0,4},{4,8},{8,12},{12,0},{1,5},{5,9},{9,13},{13,1},{2,6},{6,10},{... | collective-permute-start | bytes 1572872 | tf_op jit(solution)/shard_map/kv_ring/ppermute | solution.py:152
  151.8 8.6 %collective-permute-start.16 = (bf16[2,512,256]{2,1,0:T(8,128)(2,1)S(1)}, bf16[2,512,256]{2,1,0:T(8,128)(2,1)S(1)}, u32[]{:S(2)}, u32[]{:S(2)}) collective-permute-start(bf16[2,512,256]{2,1,0:T(8,128)(2,1)S(1)} %collective-permute-done.15), channel_id=1, source_target_pairs={{0,4},{4,8},{8,12},{12,0},{1,5},{5,9},{9,13},{13,1},{2,6},{6,10},{... | collective-permute-start | bytes 1572872 | tf_op jit(solution)/shard_map/kv_ring/ppermute | solution.py:152
  167.5 10.6 %collective-permute-start.17 = (bf16[128,1536]{1,0:T(8,128)(2,1)S(1)}, bf16[128,1536]{1,0:T(8,128)(2,1)S(1)}, u32[]{:S(2)}, u32[]{:S(2)}) collective-permute-start(bf16[128,1536]{1,0:T(8,128)(2,1)S(1)} %get-tuple-element.16), channel_id=1, source_target_pairs={{0,1},{1,2},{2,3},{4,5},{5,6},{6,7},{8,9},{9,10},{10,11},{12,13},{... | collective-permute-start | bytes 1179656 | tf_op jit(solution)/shard_map/out_reduce/ppermute | solution.py:57
  169.8 12.9 %collective-permute-start.20 = (bf16[128,1536]{1,0:T(8,128)(2,1)S(1)}, bf16[128,1536]{1,0:T(8,128)(2,1)S(1)}, u32[]{:S(2)}, u32[]{:S(2)}) collective-permute-start(bf16[128,1536]{1,0:T(8,128)(2,1)S(1)} %get-tuple-element.17), channel_id=1, source_target_pairs={{1,0},{2,1},{3,2},{5,4},{6,5},{7,6},{9,8},{10,9},{11,10},{13,12},{... | collective-permute-start | bytes 1179656 | tf_op jit(solution)/shard_map/out_reduce/ppermute | solution.py:58
  178.2 11.7 %collective-permute-start.18 = (bf16[128,1536]{1,0:T(8,128)(2,1)S(1)}, bf16[128,1536]{1,0:T(8,128)(2,1)S(1)}, u32[]{:S(2)}, u32[]{:S(2)}) collective-permute-start(bf16[128,1536]{1,0:T(8,128)(2,1)S(1)} %fusion.58), channel_id=1, source_target_pairs={{0,1},{1,2},{2,3},{4,5},{5,6},{6,7},{8,9},{9,10},{10,11},{12,13},{... | collective-permute-start | bytes 1179656 | tf_op jit(solution)/shard_map/out_reduce/ppermute | solution.py:57
  190.1 12.0 %collective-permute-start.21 = (bf16[128,1536]{1,0:T(8,128)(2,1)S(1)}, bf16[128,1536]{1,0:T(8,128)(2,1)S(1)}, u32[]{:S(2)}, u32[]{:S(2)}) collective-permute-start(bf16[128,1536]{1,0:T(8,128)(2,1)S(1)} %get-tuple-element.15), channel_id=1, source_target_pairs={{1,0},{2,1},{3,2},{5,4},{6,5},{7,6},{9,8},{10,9},{11,10},{13,12},{... | collective-permute-start | bytes 1179656 | tf_op jit(solution)/shard_map/out_reduce/ppermute | solution.py:58
  191.6 12.1 %collective-permute-start.19 = (bf16[128,1536]{1,0:T(8,128)(2,1)S(1)}, bf16[128,1536]{1,0:T(8,128)(2,1)S(1)}, u32[]{:S(2)}, u32[]{:S(2)}) collective-permute-start(bf16[128,1536]{1,0:T(8,128)(2,1)S(1)} %get-tuple-element.14), channel_id=1, source_target_pairs={{0,1},{1,2},{2,3},{4,5},{5,6},{6,7},{8,9},{9,10},{10,11},{12,13},{... | collective-permute-start | bytes 1179656 | tf_op jit(solution)/shard_map/out_reduce/ppermute | solution.py:57
  202.2 24.6 %copy-start.7 = (bf16[256,128]{1,0:T(8,128)(2,1)S(1)}, bf16[256,128]{1,0:T(8,128)(2,1)}, u32[]{:S(2)}) copy-start(bf16[256,128]{1,0:T(8,128)(2,1)} %param.19) | copy-start | bytes 196612
  202.2 24.6 %copy-start.8 = (bf16[128,256]{1,0:T(8,128)(2,1)S(1)}, bf16[128,256]{1,0:T(8,128)(2,1)}, u32[]{:S(2)}) copy-start(bf16[128,256]{1,0:T(8,128)(2,1)} %param.18) | copy-start | bytes 196612
  202.2 9.8 %collective-permute-start.22 = (bf16[128,1536]{1,0:T(8,128)(2,1)S(1)}, bf16[128,1536]{1,0:T(8,128)(2,1)S(1)}, u32[]{:S(2)}, u32[]{:S(2)}) collective-permute-start(bf16[128,1536]{1,0:T(8,128)(2,1)S(1)} %fusion.57), channel_id=1, source_target_pairs={{1,0},{2,1},{3,2},{5,4},{6,5},{7,6},{9,8},{10,9},{11,10},{13,12},{... | collective-permute-start | bytes 1179656 | tf_op jit(solution)/shard_map/out_reduce/ppermute | solution.py:58
  213.4 3.6 %collective-permute-start.23 = (bf16[8,256]{1,0:T(8,128)(2,1)S(1)}, bf16[8,256]{1,0:T(8,128)(2,1)S(1)}, u32[]{:S(2)}, u32[]{:S(2)}) collective-permute-start(bf16[8,256]{1,0:T(8,128)(2,1)S(1)} %convolution_convert_fusion.1), channel_id=1, source_target_pairs={{0,1},{1,0},{2,3},{3,2},{4,5},{5,4},{6,7},{7,6},{8,9},{9,8},{10,11... | collective-permute-start | bytes 12296 | tf_op jit(solution)/shard_map/sides_gather/ppermute | solution.py:89
  217.0 4.5 %collective-permute-start.24 = (bf16[16,256]{1,0:T(8,128)(2,1)S(1)}, bf16[16,256]{1,0:T(8,128)(2,1)S(1)}, u32[]{:S(2)}, u32[]{:S(2)}) collective-permute-start(bf16[16,256]{1,0:T(8,128)(2,1)S(1)} %maximum_select_fusion.3), channel_id=1, source_target_pairs={{0,2},{1,3},{2,0},{3,1},{4,6},{5,7},{6,4},{7,5},{8,10},{9,11},{10,... | collective-permute-start | bytes 24584 | tf_op jit(solution)/shard_map/sides_gather/ppermute | solution.py:89
  221.6 1.2 collective-permute-start.25
  222.8 4.0 %collective-permute-start.26 = (bf16[64,256]{1,0:T(8,128)(2,1)S(1)}, bf16[64,256]{1,0:T(8,128)(2,1)S(1)}, u32[]{:S(2)}, u32[]{:S(2)}) collective-permute-start(bf16[64,256]{1,0:T(8,128)(2,1)S(1)} %maximum_select_fusion.1), channel_id=1, source_target_pairs={{0,8},{4,12},{8,0},{12,4},{1,9},{5,13},{9,1},{13,5},{2,10},{6,14},... | collective-permute-start | bytes 98312 | tf_op jit(solution)/shard_map/sides_gather/ppermute | solution.py:89
  (5 other events, 67.6 us)

commit v2 on v1

--- a/solution.py
+++ b/solution.py
@@ -40,24 +40,31 @@
     return summed
 
 
-def line_reduce_scatter(partial, axis):
+def direct_reduce_scatter(partial, axis):
     n = lax.axis_size(axis)
     me = lax.axis_index(axis)
     rows = partial.shape[0] // n
     blocks = partial.reshape(n, rows, partial.shape[1])
-    right = [(i, i + 1) for i in range(n - 1)]
-    left = [(i + 1, i) for i in range(n - 1)]
-    got_r = jnp.zeros((rows, partial.shape[1]), jnp.bfloat16)
-    got_l = jnp.zeros((rows, partial.shape[1]), jnp.bfloat16)
-    for step in range(1, n):
-        idx_r = jnp.clip(me + n - step, 0, n - 1)
-        idx_l = jnp.clip(me - (n - step), 0, n - 1)
-        send_r = (blocks[idx_r] + got_r.astype(jnp.float32)).astype(jnp.bfloat16)
-        send_l = (blocks[idx_l] + got_l.astype(jnp.float32)).astype(jnp.bfloat16)
-        got_r = lax.ppermute(send_r, axis, right)
-        got_l = lax.ppermute(send_l, axis, left)
-    own = blocks[me]
-    return own + got_r.astype(jnp.float32) + got_l.astype(jnp.float32)
+    total = blocks[me]
+    for shift in range(1, n):
+        outgoing = blocks[(me + shift) % n].astype(jnp.bfloat16)
+        incoming = lax.ppermute(outgoing, axis, [(i, (i + shift) % n) for i in range(n)])
+        total = total + incoming.astype(jnp.float32)
+    return total
+
+
+def permute_all_to_all(value, axis):
+    n = lax.axis_size(axis)
+    me = lax.axis_index(axis)
+    width = value.shape[1] // n
+    pieces = value.reshape(value.shape[0], n, width)
+    slots = jnp.zeros((n, value.shape[0], width), value.dtype)
+    slots = lax.dynamic_update_index_in_dim(slots, pieces[:, me], me, 0)
+    for shift in range(1, n):
+        outgoing = pieces[:, (me + shift) % n]
+        incoming = lax.ppermute(outgoing, axis, [(i, (i + shift) % n) for i in range(n)])
+        slots = lax.dynamic_update_index_in_dim(slots, incoming, (me + n - shift) % n, 0)
+    return slots.reshape(n * value.shape[0], width)
 
 
 def line_all_gather(value, axis):
@@ -103,10 +110,10 @@
     local_rows = row_count * pair_count
     inputs = sequence.astype(jnp.float32)
     normed = norm_rows(inputs, gain_conv).astype(jnp.bfloat16)
-    swapped = lax.all_to_all(normed, "pair", split_axis=1, concat_axis=0, tiled=True)
+    swapped = permute_all_to_all(normed, "pair")
     padded = padded_2(swapped, (("seq", 0),), DILATION * (conv_weight.shape[0] - 1) // 2)
     with jax.named_scope("conv_reduce"):
-        summed = line_reduce_scatter(conv_rows(padded, conv_weight, local_rows), "pair")
+        summed = direct_reduce_scatter(conv_rows(padded, conv_weight, local_rows), "pair")
     first_out = (inputs + summed).astype(jnp.bfloat16)
     attn_in = norm_rows(first_out.astype(jnp.float32), gain_attn).astype(jnp.bfloat16)
     with jax.named_scope("attn_in_gather"):
@@ -157,7 +164,7 @@
     attended = (weighted / running_sum[:, :, None]).astype(jnp.bfloat16)
     attended = attended.transpose(1, 0, 2).reshape(local_rows, head_count * VALUE_SIZE)
     with jax.named_scope("out_reduce"):
-        mixed = line_reduce_scatter(
+        mixed = direct_reduce_scatter(
             jnp.dot(attended, w_out, preferred_element_type=jnp.float32), "pair"
         )
     seq_out = (first_out.astype(jnp.float32) + mixed).astype(jnp.bfloat16)

time: 229 us -> 201 us (0.88)
  waiting for transfers between devices: 125 us -> 108 us
  starting transfers between devices: 62.1 us -> 54.9 us
  other arithmetic: 13.1 us -> 7.94 us
    ppermute x12 -> x9, starting transfers between devices: 33 us -> 17.5 us  [the longest x6 10.4 us: direct_reduce_scatter(): lax.ppermute(outgoing, axis, [(i, (i + shift) % n) for i in range(n)])]
    all_to_all x1 -> x0, waiting for transfers between devices: 11.7 us -> none  [shards(): lax.all_to_all(normed, 'pair', split_axis=1, concat_axis=0, tiled=True)]
    ppermute x4, starting transfers between devices: 3.83 us -> 11.2 us  [doubling_all_gather(): other = lax.ppermute(out, axis, [(i, i ^ k) for i in range(n)])]
    ppermute x12 -> x9, waiting for transfers between devices: 60.7 us -> 53.9 us  [the longest x6 48.7 us: direct_reduce_scatter(): lax.ppermute(outgoing, axis, [(i, (i + shift) % n) for i in range(n)])]
    ppermute x3, starting transfers between devices: 12.2 us -> 19 us  [line_all_gather(): flow_r = lax.ppermute(flow_r, axis, right)]
    all_to_all x1 -> x0, starting transfers between devices: 6.32 us -> none  [shards(): lax.all_to_all(normed, 'pair', split_axis=1, concat_axis=0, tiled=True)]
    convert_element_type x6 -> x0, other arithmetic: 5.42 us -> none  [the longest x4 4.13 us: line_reduce_scatter(): send_r = (blocks[idx_r] + got_r.astype(jnp.float32)).astype(jnp.bfloat16)]
    ppermute x3, waiting for transfers between devices: 13.1 us -> 16.5 us  [line_all_gather(): flow_r = lax.ppermute(flow_r, axis, right)]
  transfers between devices with their start and end apart: 28 -> 24, of which waited for: 21 -> 19; matrix products, arithmetic and copies ran while one was open for 5% -> 5% of each run, Pallas kernels for 0% -> 0%
where the time goes in v2:
time: 201 us; the launch traced here: 200 us
  waiting for transfers between devices  108 us (54%)
  starting transfers between devices  54.9 us (27%)
  matrix products  15.7 us (8%)
  local copies, waits for them, and re-layouts  12.9 us (6%)
  other arithmetic  7.94 us (4%)
    ppermute x6, waiting for transfers between devices, direct_reduce_scatter(): lax.ppermute(outgoing, axis, [(i, (i + shift) % n) for i in range(n)])  48.7 us
    ppermute x3, waiting for transfers between devices, shards(): arriving = lax.ppermute(current, 'seq', ring)  24.4 us
    ppermute x3, starting transfers between devices, line_all_gather(): flow_r = lax.ppermute(flow_r, axis, right)  19 us
    ppermute x3, waiting for transfers between devices, line_all_gather(): flow_r = lax.ppermute(flow_r, axis, right)  16.5 us
    ppermute x4, starting transfers between devices, doubling_all_gather(): other = lax.ppermute(out, axis, [(i, i ^ k) for i in range(n)])  11.2 us
    ppermute x6, starting transfers between devices, direct_reduce_scatter(): lax.ppermute(outgoing, axis, [(i, (i + shift) % n) for i in range(n)])  10.4 us
    ppermute x4, waiting for transfers between devices, doubling_all_gather(): other = lax.ppermute(out, axis, [(i, i ^ k) for i in range(n)])  8.6 us
    ppermute x3, starting transfers between devices, permute_all_to_all(): lax.ppermute(outgoing, axis, [(i, (i + shift) % n) for i in range(n)])  7.13 us
  transfers between devices with their start and end apart: 24, of which 19 were waited for; matrix products, arithmetic and copies ran while one was open for 5% of the time, Pallas kernels for 0%

profile of v2, /device:TPU:0, one launch (start us, length us, event | category | flops | bytes accessed | tf_op | source)
XLA Modules:
  0.0 200.2 jit_solution(1673300269778915591)
XLA Ops:
  4.1 3.1 %collective-permute-start = (bf16[128,384]{1,0:T(8,128)(2,1)S(1)}, bf16[128,384]{1,0:T(8,128)(2,1)S(1)}, u32[]{:S(2)}, u32[]{:S(2)}) collective-permute-start(bf16[128,384]{1,0:T(8,128)(2,1)S(1)} %bitcast.214), channel_id=1, source_target_pairs={{0,1},{1,2},{2,3},{3,0},{4,5},{5,6},{6,7},{7,4},{8,9},{9,10},{10,1... | collective-permute-start | bytes 294920 | tf_op jit(solution)/shard_map/ppermute | solution.py:65
  7.2 2.7 %collective-permute-start.1 = (bf16[128,384]{1,0:T(8,128)(2,1)S(1)}, bf16[128,384]{1,0:T(8,128)(2,1)S(1)}, u32[]{:S(2)}, u32[]{:S(2)}) collective-permute-start(bf16[128,384]{1,0:T(8,128)(2,1)S(1)} %bitcast.213), channel_id=1, source_target_pairs={{0,2},{1,3},{2,0},{3,1},{4,6},{5,7},{6,4},{7,5},{8,10},{9,11},{10,... | collective-permute-start | bytes 294920 | tf_op jit(solution)/shard_map/ppermute | solution.py:65
  12.9 3.5 %collective-permute-done.1 = bf16[128,384]{1,0:T(8,128)(2,1)S(1)} collective-permute-done((bf16[128,384]{1,0:T(8,128)(2,1)S(1)}, bf16[128,384]{1,0:T(8,128)(2,1)S(1)}, u32[]{:S(2)}, u32[]{:S(2)}) %collective-permute-start.1) | collective-permute-done | bytes 98336 | tf_op jit(solution)/shard_map/ppermute | solution.py:65
  16.6 1.7 collective-permute-start.3
  18.3 1.6 collective-permute-start.4
  19.9 2.4 %fusion.28 = f32[512,1536]{1,0:T(8,128)S(1)} fusion(bf16[512,384]{1,0:T(8,128)(2,1)S(1)} %bitcast.196, bf16[5,384,1536]{2,1,0:T(8,128)(2,1)} %param.12), kind=kOutput, calls=%fused_computation.49 | convolution fusion | flops 603979776 | bytes 4718592 | tf_op jit(solution)/shard_map/conv_reduce/dot_general | solution.py:39
  27.3 1.6 copy-done.1
  29.9 2.4 %collective-permute-start.5 = (bf16[128,1536]{1,0:T(8,128)(2,1)}, bf16[128,1536]{1,0:T(8,128)(2,1)S(1)}, u32[]{:S(2)}, u32[]{:S(2)}) collective-permute-start(bf16[128,1536]{1,0:T(8,128)(2,1)} %get-tuple-element.17), channel_id=1, source_target_pairs={{0,1},{1,2},{2,3},{3,0},{4,5},{5,6},{6,7},{7,4},{8,9},{9,10},{10,1... | collective-permute-start | bytes 1179656 | tf_op jit(solution)/shard_map/conv_reduce/ppermute | solution.py:51
  32.3 1.7 collective-permute-start.6
  34.7 8.1 %collective-permute-done.5 = bf16[128,1536]{1,0:T(8,128)(2,1)S(1)} collective-permute-done((bf16[128,1536]{1,0:T(8,128)(2,1)}, bf16[128,1536]{1,0:T(8,128)(2,1)S(1)}, u32[]{:S(2)}, u32[]{:S(2)}) %collective-permute-start.5) | collective-permute-done | bytes 393248 | tf_op jit(solution)/shard_map/conv_reduce/ppermute | solution.py:51
  42.8 17.9 %collective-permute-done.6 = bf16[128,1536]{1,0:T(8,128)(2,1)S(1)} collective-permute-done((bf16[128,1536]{1,0:T(8,128)(2,1)}, bf16[128,1536]{1,0:T(8,128)(2,1)S(1)}, u32[]{:S(2)}, u32[]{:S(2)}) %collective-permute-start.6) | collective-permute-done | bytes 393248 | tf_op jit(solution)/shard_map/conv_reduce/ppermute | solution.py:51
  61.5 1.7 fusion.54
  65.7 10.3 %collective-permute-start.8 = (bf16[128,1536]{1,0:T(8,128)(2,1)}, bf16[128,1536]{1,0:T(8,128)(2,1)S(1)}, u32[]{:S(2)}, u32[]{:S(2)}) collective-permute-start(bf16[128,1536]{1,0:T(8,128)(2,1)} %get-tuple-element.11), channel_id=1, source_target_pairs={{0,1},{1,2},{2,3},{4,5},{5,6},{6,7},{8,9},{9,10},{10,11},{12,13},{... | collective-permute-start | bytes 1179656 | tf_op jit(solution)/shard_map/attn_in_gather/ppermute | solution.py:80
  77.4 7.6 %collective-permute-done.8 = bf16[128,1536]{1,0:T(8,128)(2,1)S(1)} collective-permute-done((bf16[128,1536]{1,0:T(8,128)(2,1)}, bf16[128,1536]{1,0:T(8,128)(2,1)S(1)}, u32[]{:S(2)}, u32[]{:S(2)}) %collective-permute-start.8) | collective-permute-done | bytes 393248 | tf_op jit(solution)/shard_map/attn_in_gather/ppermute | solution.py:80
  84.9 4.3 %collective-permute-start.10 = (bf16[128,1536]{1,0:T(8,128)(2,1)S(1)}, bf16[128,1536]{1,0:T(8,128)(2,1)S(1)}, u32[]{:S(2)}, u32[]{:S(2)}) collective-permute-start(bf16[128,1536]{1,0:T(8,128)(2,1)S(1)} %collective-permute-done.8), channel_id=1, source_target_pairs={{0,1},{1,2},{2,3},{4,5},{5,6},{6,7},{8,9},{9,10},{10,11},{12,13},{... | collective-permute-start | bytes 1179656 | tf_op jit(solution)/shard_map/attn_in_gather/ppermute | solution.py:80
  92.1 4.9 %collective-permute-done.10 = bf16[128,1536]{1,0:T(8,128)(2,1)S(1)} collective-permute-done((bf16[128,1536]{1,0:T(8,128)(2,1)S(1)}, bf16[128,1536]{1,0:T(8,128)(2,1)S(1)}, u32[]{:S(2)}, u32[]{:S(2)}) %collective-permute-start.10) | collective-permute-done | bytes 393248 | tf_op jit(solution)/shard_map/attn_in_gather/ppermute | solution.py:80
  97.0 4.4 %collective-permute-start.12 = (bf16[128,1536]{1,0:T(8,128)(2,1)S(1)}, bf16[128,1536]{1,0:T(8,128)(2,1)S(1)}, u32[]{:S(2)}, u32[]{:S(2)}) collective-permute-start(bf16[128,1536]{1,0:T(8,128)(2,1)S(1)} %collective-permute-done.10), channel_id=1, source_target_pairs={{0,1},{1,2},{2,3},{4,5},{5,6},{6,7},{8,9},{9,10},{10,11},{12,13},{... | collective-permute-start | bytes 1179656 | tf_op jit(solution)/shard_map/attn_in_gather/ppermute | solution.py:80
  104.3 4.0 %collective-permute-done.12 = bf16[128,1536]{1,0:T(8,128)(2,1)S(1)} collective-permute-done((bf16[128,1536]{1,0:T(8,128)(2,1)S(1)}, bf16[128,1536]{1,0:T(8,128)(2,1)S(1)}, u32[]{:S(2)}, u32[]{:S(2)}) %collective-permute-start.12) | collective-permute-done | bytes 393248 | tf_op jit(solution)/shard_map/attn_in_gather/ppermute | solution.py:80
  109.1 3.4 %collective-permute-done.13 = bf16[128,1536]{1,0:T(8,128)(2,1)S(1)} collective-permute-done((bf16[128,1536]{1,0:T(8,128)(2,1)S(1)}, bf16[128,1536]{1,0:T(8,128)(2,1)S(1)}, u32[]{:S(2)}, u32[]{:S(2)}) %collective-permute-start.13) | collective-permute-done | bytes 393248 | tf_op jit(solution)/shard_map/attn_in_gather/ppermute | solution.py:81
  116.3 8.6 %collective-permute-done.14 = bf16[2,512,256]{2,1,0:T(8,128)(2,1)S(1)} collective-permute-done((bf16[2,512,256]{2,1,0:T(8,128)(2,1)S(1)}, bf16[2,512,256]{2,1,0:T(8,128)(2,1)S(1)}, u32[]{:S(2)}, u32[]{:S(2)}) %collective-permute-start.14) | collective-permute-done | bytes 524320 | tf_op jit(solution)/shard_map/kv_ring/ppermute | solution.py:159
  125.4 8.2 %collective-permute-done.15 = bf16[2,512,256]{2,1,0:T(8,128)(2,1)S(1)} collective-permute-done((bf16[2,512,256]{2,1,0:T(8,128)(2,1)S(1)}, bf16[2,512,256]{2,1,0:T(8,128)(2,1)S(1)}, u32[]{:S(2)}, u32[]{:S(2)}) %collective-permute-start.15) | collective-permute-done | bytes 524320 | tf_op jit(solution)/shard_map/kv_ring/ppermute | solution.py:159
  134.4 7.7 %collective-permute-done.16 = bf16[2,512,256]{2,1,0:T(8,128)(2,1)S(1)} collective-permute-done((bf16[2,512,256]{2,1,0:T(8,128)(2,1)S(1)}, bf16[2,512,256]{2,1,0:T(8,128)(2,1)S(1)}, u32[]{:S(2)}, u32[]{:S(2)}) %collective-permute-start.16) | collective-permute-done | bytes 524320 | tf_op jit(solution)/shard_map/kv_ring/ppermute | solution.py:159
  147.4 1.7 fusion.60
  149.3 1.5 collective-permute-start.17
  152.1 2.8 %collective-permute-start.19 = (bf16[128,1536]{1,0:T(8,128)(2,1)S(1)}, bf16[128,1536]{1,0:T(8,128)(2,1)S(1)}, u32[]{:S(2)}, u32[]{:S(2)}) collective-permute-start(bf16[128,1536]{1,0:T(8,128)(2,1)S(1)} %get-tuple-element.15), channel_id=1, source_target_pairs={{0,3},{1,0},{2,1},{3,2},{4,7},{5,4},{6,5},{7,6},{8,11},{9,8},{10,9... | collective-permute-start | bytes 1179656 | tf_op jit(solution)/shard_map/out_reduce/ppermute | solution.py:51
  154.9 8.4 %collective-permute-done.17 = bf16[128,1536]{1,0:T(8,128)(2,1)S(1)} collective-permute-done((bf16[128,1536]{1,0:T(8,128)(2,1)S(1)}, bf16[128,1536]{1,0:T(8,128)(2,1)S(1)}, u32[]{:S(2)}, u32[]{:S(2)}) %collective-permute-start.17) | collective-permute-done | bytes 393248 | tf_op jit(solution)/shard_map/out_reduce/ppermute | solution.py:51
  163.3 14.3 %collective-permute-done.18 = bf16[128,1536]{1,0:T(8,128)(2,1)S(1)} collective-permute-done((bf16[128,1536]{1,0:T(8,128)(2,1)S(1)}, bf16[128,1536]{1,0:T(8,128)(2,1)S(1)}, u32[]{:S(2)}, u32[]{:S(2)}) %collective-permute-start.18) | collective-permute-done | bytes 393248 | tf_op jit(solution)/shard_map/out_reduce/ppermute | solution.py:51
  179.0 8.5 %collective-permute-start.20 = (bf16[8,256]{1,0:T(8,128)(2,1)S(1)}, bf16[8,256]{1,0:T(8,128)(2,1)S(1)}, u32[]{:S(2)}, u32[]{:S(2)}) collective-permute-start(bf16[8,256]{1,0:T(8,128)(2,1)S(1)} %convolution_convert_fusion.1), channel_id=1, source_target_pairs={{0,1},{1,0},{2,3},{3,2},{4,5},{5,4},{6,7},{7,6},{8,9},{9,8},{10,11... | collective-permute-start | bytes 12296 | tf_op jit(solution)/shard_map/sides_gather/ppermute | solution.py:96
  187.6 1.6 collective-permute-done.20
  190.1 3.5 %collective-permute-done.21 = bf16[16,256]{1,0:T(8,128)(2,1)S(1)} collective-permute-done((bf16[16,256]{1,0:T(8,128)(2,1)S(1)}, bf16[16,256]{1,0:T(8,128)(2,1)S(1)}, u32[]{:S(2)}, u32[]{:S(2)}) %collective-permute-start.21) | collective-permute-done | bytes 8224 | tf_op jit(solution)/shard_map/sides_gather/ppermute | solution.py:96
  194.9 1.7 collective-permute-start.23
  196.6 2.3 %collective-permute-done.23 = bf16[64,256]{1,0:T(8,128)(2,1)S(1)} collective-permute-done((bf16[64,256]{1,0:T(8,128)(2,1)S(1)}, bf16[64,256]{1,0:T(8,128)(2,1)S(1)}, u32[]{:S(2)}, u32[]{:S(2)}) %collective-permute-start.23) | collective-permute-done | bytes 32800 | tf_op jit(solution)/shard_map/sides_gather/ppermute | solution.py:96
  (97 shorter events, 41.1 us)
Async XLA Ops:
  0.6 114.1 %copy-start = (bf16[1536,768]{1,0:T(8,128)(2,1)S(1)}, bf16[1536,768]{1,0:T(8,128)(2,1)}, u32[]{:S(2)}) copy-start(bf16[1536,768]{1,0:T(8,128)(2,1)} %param.14) | copy-start | bytes 7077892
  4.1 8.7 %collective-permute-start = (bf16[128,384]{1,0:T(8,128)(2,1)S(1)}, bf16[128,384]{1,0:T(8,128)(2,1)S(1)}, u32[]{:S(2)}, u32[]{:S(2)}) collective-permute-start(bf16[128,384]{1,0:T(8,128)(2,1)S(1)} %bitcast.214), channel_id=1, source_target_pairs={{0,1},{1,2},{2,3},{3,0},{4,5},{5,6},{6,7},{7,4},{8,9},{9,10},{10,1... | collective-permute-start | bytes 294920 | tf_op jit(solution)/shard_map/ppermute | solution.py:65
  7.2 9.2 %collective-permute-start.1 = (bf16[128,384]{1,0:T(8,128)(2,1)S(1)}, bf16[128,384]{1,0:T(8,128)(2,1)S(1)}, u32[]{:S(2)}, u32[]{:S(2)}) collective-permute-start(bf16[128,384]{1,0:T(8,128)(2,1)S(1)} %bitcast.213), channel_id=1, source_target_pairs={{0,2},{1,3},{2,0},{3,1},{4,6},{5,7},{6,4},{7,5},{8,10},{9,11},{10,... | collective-permute-start | bytes 294920 | tf_op jit(solution)/shard_map/ppermute | solution.py:65
  9.9 6.7 %collective-permute-start.2 = (bf16[128,384]{1,0:T(8,128)(2,1)S(1)}, bf16[128,384]{1,0:T(8,128)(2,1)S(1)}, u32[]{:S(2)}, u32[]{:S(2)}) collective-permute-start(bf16[128,384]{1,0:T(8,128)(2,1)S(1)} %bitcast.212), channel_id=1, source_target_pairs={{0,3},{1,0},{2,1},{3,2},{4,7},{5,4},{6,5},{7,6},{8,11},{9,8},{10,9... | collective-permute-start | bytes 294920 | tf_op jit(solution)/shard_map/ppermute | solution.py:65
  16.6 8.5 %collective-permute-start.3 = (bf16[8,384]{1,0:T(8,128)(2,1)S(1)}, bf16[8,384]{1,0:T(8,128)(2,1)S(1)}, u32[]{:S(2)}, u32[]{:S(2)}) collective-permute-start(bf16[8,384]{1,0:T(8,128)(2,1)S(1)} %get-tuple-element.20), channel_id=1, source_target_pairs={{0,4},{4,8},{8,12},{1,5},{5,9},{9,13},{2,6},{6,10},{10,14},{3,7},{... | collective-permute-start | bytes 18440 | tf_op jit(solution)/shard_map/ppermute | solution.py:25
  18.3 4.8 %copy-start.2 = (bf16[5,384,1536]{2,1,0:T(8,128)(2,1)S(1)}, bf16[5,384,1536]{2,1,0:T(8,128)(2,1)}, u32[]{:S(2)}) copy-start(bf16[5,384,1536]{2,1,0:T(8,128)(2,1)} %param.12) | copy-start | bytes 17694724
  18.3 4.8 %collective-permute-start.4 = (bf16[8,384]{1,0:T(8,128)(2,1)S(1)}, bf16[8,384]{1,0:T(8,128)(2,1)S(1)}, u32[]{:S(2)}, u32[]{:S(2)}) collective-permute-start(bf16[8,384]{1,0:T(8,128)(2,1)S(1)} %get-tuple-element.21), channel_id=1, source_target_pairs={{4,0},{8,4},{12,8},{5,1},{9,5},{13,9},{6,2},{10,6},{14,10},{7,3},{... | collective-permute-start | bytes 18440 | tf_op jit(solution)/shard_map/ppermute | solution.py:26
  27.2 34.2 %copy-start.3 = (bf16[128,1536]{1,0:T(8,128)(2,1)S(1)}, bf16[128,1536]{1,0:T(8,128)(2,1)}, u32[]{:S(2)}) copy-start(bf16[128,1536]{1,0:T(8,128)(2,1)} %param.10) | copy-start | bytes 1179652
  29.9 12.9 %collective-permute-start.5 = (bf16[128,1536]{1,0:T(8,128)(2,1)}, bf16[128,1536]{1,0:T(8,128)(2,1)S(1)}, u32[]{:S(2)}, u32[]{:S(2)}) collective-permute-start(bf16[128,1536]{1,0:T(8,128)(2,1)} %get-tuple-element.17), channel_id=1, source_target_pairs={{0,1},{1,2},{2,3},{3,0},{4,5},{5,6},{6,7},{7,4},{8,9},{9,10},{10,1... | collective-permute-start | bytes 1179656 | tf_op jit(solution)/shard_map/conv_reduce/ppermute | solution.py:51
  32.3 28.4 %collective-permute-start.6 = (bf16[128,1536]{1,0:T(8,128)(2,1)}, bf16[128,1536]{1,0:T(8,128)(2,1)S(1)}, u32[]{:S(2)}, u32[]{:S(2)}) collective-permute-start(bf16[128,1536]{1,0:T(8,128)(2,1)} %get-tuple-element.19), channel_id=1, source_target_pairs={{0,2},{1,3},{2,0},{3,1},{4,6},{5,7},{6,4},{7,5},{8,10},{9,11},{10,... | collective-permute-start | bytes 1179656 | tf_op jit(solution)/shard_map/conv_reduce/ppermute | solution.py:51
  34.0 27.5 %collective-permute-start.7 = (bf16[128,1536]{1,0:T(8,128)(2,1)}, bf16[128,1536]{1,0:T(8,128)(2,1)}, u32[]{:S(2)}, u32[]{:S(2)}) collective-permute-start(bf16[128,1536]{1,0:T(8,128)(2,1)} %get-tuple-element.18), channel_id=1, source_target_pairs={{0,3},{1,0},{2,1},{3,2},{4,7},{5,4},{6,5},{7,6},{8,11},{9,8},{10,9... | collective-permute-start | bytes 1179656 | tf_op jit(solution)/shard_map/conv_reduce/ppermute | solution.py:51
  34.7 30.0 %copy-start.6 = (f32[1536]{0:T(1024)S(1)}, f32[1536]{0:T(1024)}, u32[]{:S(2)}) copy-start(f32[1536]{0:T(1024)} %param.13) | copy-start | bytes 18436
  65.7 19.2 %collective-permute-start.8 = (bf16[128,1536]{1,0:T(8,128)(2,1)}, bf16[128,1536]{1,0:T(8,128)(2,1)S(1)}, u32[]{:S(2)}, u32[]{:S(2)}) collective-permute-start(bf16[128,1536]{1,0:T(8,128)(2,1)} %get-tuple-element.11), channel_id=1, source_target_pairs={{0,1},{1,2},{2,3},{4,5},{5,6},{6,7},{8,9},{9,10},{10,11},{12,13},{... | collective-permute-start | bytes 1179656 | tf_op jit(solution)/shard_map/attn_in_gather/ppermute | solution.py:80
  76.0 13.2 %collective-permute-start.9 = (bf16[128,1536]{1,0:T(8,128)(2,1)}, bf16[128,1536]{1,0:T(8,128)(2,1)S(1)}, u32[]{:S(2)}, u32[]{:S(2)}) collective-permute-start(bf16[128,1536]{1,0:T(8,128)(2,1)} %get-tuple-element.11), channel_id=1, source_target_pairs={{1,0},{2,1},{3,2},{5,4},{6,5},{7,6},{9,8},{10,9},{11,10},{13,12},{... | collective-permute-start | bytes 1179656 | tf_op jit(solution)/shard_map/attn_in_gather/ppermute | solution.py:81
  84.9 12.1 %collective-permute-start.10 = (bf16[128,1536]{1,0:T(8,128)(2,1)S(1)}, bf16[128,1536]{1,0:T(8,128)(2,1)S(1)}, u32[]{:S(2)}, u32[]{:S(2)}) collective-permute-start(bf16[128,1536]{1,0:T(8,128)(2,1)S(1)} %collective-permute-done.8), channel_id=1, source_target_pairs={{0,1},{1,2},{2,3},{4,5},{5,6},{6,7},{8,9},{9,10},{10,11},{12,13},{... | collective-permute-start | bytes 1179656 | tf_op jit(solution)/shard_map/attn_in_gather/ppermute | solution.py:80
  89.3 12.2 %collective-permute-start.11 = (bf16[128,1536]{1,0:T(8,128)(2,1)S(1)}, bf16[128,1536]{1,0:T(8,128)(2,1)S(1)}, u32[]{:S(2)}, u32[]{:S(2)}) collective-permute-start(bf16[128,1536]{1,0:T(8,128)(2,1)S(1)} %collective-permute-done.9), channel_id=1, source_target_pairs={{1,0},{2,1},{3,2},{5,4},{6,5},{7,6},{9,8},{10,9},{11,10},{13,12},{... | collective-permute-start | bytes 1179656 | tf_op jit(solution)/shard_map/attn_in_gather/ppermute | solution.py:81
  97.0 11.3 %collective-permute-start.12 = (bf16[128,1536]{1,0:T(8,128)(2,1)S(1)}, bf16[128,1536]{1,0:T(8,128)(2,1)S(1)}, u32[]{:S(2)}, u32[]{:S(2)}) collective-permute-start(bf16[128,1536]{1,0:T(8,128)(2,1)S(1)} %collective-permute-done.10), channel_id=1, source_target_pairs={{0,1},{1,2},{2,3},{4,5},{5,6},{6,7},{8,9},{9,10},{10,11},{12,13},{... | collective-permute-start | bytes 1179656 | tf_op jit(solution)/shard_map/attn_in_gather/ppermute | solution.py:80
  101.4 11.0 %collective-permute-start.13 = (bf16[128,1536]{1,0:T(8,128)(2,1)S(1)}, bf16[128,1536]{1,0:T(8,128)(2,1)S(1)}, u32[]{:S(2)}, u32[]{:S(2)}) collective-permute-start(bf16[128,1536]{1,0:T(8,128)(2,1)S(1)} %collective-permute-done.11), channel_id=1, source_target_pairs={{1,0},{2,1},{3,2},{5,4},{6,5},{7,6},{9,8},{10,9},{11,10},{13,12},{... | collective-permute-start | bytes 1179656 | tf_op jit(solution)/shard_map/attn_in_gather/ppermute | solution.py:81
  116.3 8.7 %collective-permute-start.14 = (bf16[2,512,256]{2,1,0:T(8,128)(2,1)S(1)}, bf16[2,512,256]{2,1,0:T(8,128)(2,1)S(1)}, u32[]{:S(2)}, u32[]{:S(2)}) collective-permute-start(bf16[2,512,256]{2,1,0:T(8,128)(2,1)S(1)} %slice.92), channel_id=1, source_target_pairs={{0,4},{4,8},{8,12},{12,0},{1,5},{5,9},{9,13},{13,1},{2,6},{6,10},{... | collective-permute-start | bytes 1572872 | tf_op jit(solution)/shard_map/kv_ring/ppermute | solution.py:159
  124.9 8.6 %collective-permute-start.15 = (bf16[2,512,256]{2,1,0:T(8,128)(2,1)S(1)}, bf16[2,512,256]{2,1,0:T(8,128)(2,1)S(1)}, u32[]{:S(2)}, u32[]{:S(2)}) collective-permute-start(bf16[2,512,256]{2,1,0:T(8,128)(2,1)S(1)} %collective-permute-done.14), channel_id=1, source_target_pairs={{0,4},{4,8},{8,12},{12,0},{1,5},{5,9},{9,13},{13,1},{2,6},{6,10},{... | collective-permute-start | bytes 1572872 | tf_op jit(solution)/shard_map/kv_ring/ppermute | solution.py:159
  133.5 8.6 %collective-permute-start.16 = (bf16[2,512,256]{2,1,0:T(8,128)(2,1)S(1)}, bf16[2,512,256]{2,1,0:T(8,128)(2,1)S(1)}, u32[]{:S(2)}, u32[]{:S(2)}) collective-permute-start(bf16[2,512,256]{2,1,0:T(8,128)(2,1)S(1)} %collective-permute-done.15), channel_id=1, source_target_pairs={{0,4},{4,8},{8,12},{12,0},{1,5},{5,9},{9,13},{13,1},{2,6},{6,10},{... | collective-permute-start | bytes 1572872 | tf_op jit(solution)/shard_map/kv_ring/ppermute | solution.py:159
  149.2 29.6 %copy-start.4 = (bf16[1536,256]{1,0:T(8,128)(2,1)S(1)}, bf16[1536,256]{1,0:T(8,128)(2,1)}, u32[]{:S(2)}) copy-start(bf16[1536,256]{1,0:T(8,128)(2,1)} %param.17) | copy-start | bytes 2359300
  149.2 29.6 %copy-start.7 = (f32[1536]{0:T(1024)S(1)}, f32[1536]{0:T(1024)}, u32[]{:S(2)}) copy-start(f32[1536]{0:T(1024)} %param.16) | copy-start | bytes 18436
  149.3 14.0 %collective-permute-start.17 = (bf16[128,1536]{1,0:T(8,128)(2,1)S(1)}, bf16[128,1536]{1,0:T(8,128)(2,1)S(1)}, u32[]{:S(2)}, u32[]{:S(2)}) collective-permute-start(bf16[128,1536]{1,0:T(8,128)(2,1)S(1)} %get-tuple-element.14), channel_id=1, source_target_pairs={{0,1},{1,2},{2,3},{3,0},{4,5},{5,6},{6,7},{7,4},{8,9},{9,10},{10,1... | collective-permute-start | bytes 1179656 | tf_op jit(solution)/shard_map/out_reduce/ppermute | solution.py:51
  150.8 26.7 %collective-permute-start.18 = (bf16[128,1536]{1,0:T(8,128)(2,1)S(1)}, bf16[128,1536]{1,0:T(8,128)(2,1)S(1)}, u32[]{:S(2)}, u32[]{:S(2)}) collective-permute-start(bf16[128,1536]{1,0:T(8,128)(2,1)S(1)} %get-tuple-element.16), channel_id=1, source_target_pairs={{0,2},{1,3},{2,0},{3,1},{4,6},{5,7},{6,4},{7,5},{8,10},{9,11},{10,... | collective-permute-start | bytes 1179656 | tf_op jit(solution)/shard_map/out_reduce/ppermute | solution.py:51
  152.1 46.9 %copy-start.8 = (bf16[256,128]{1,0:T(8,128)(2,1)S(1)}, bf16[256,128]{1,0:T(8,128)(2,1)}, u32[]{:S(2)}) copy-start(bf16[256,128]{1,0:T(8,128)(2,1)} %param.19) | copy-start | bytes 196612
  152.1 46.9 %copy-start.9 = (bf16[128,256]{1,0:T(8,128)(2,1)S(1)}, bf16[128,256]{1,0:T(8,128)(2,1)}, u32[]{:S(2)}) copy-start(bf16[128,256]{1,0:T(8,128)(2,1)} %param.18) | copy-start | bytes 196612
  152.1 25.5 %collective-permute-start.19 = (bf16[128,1536]{1,0:T(8,128)(2,1)S(1)}, bf16[128,1536]{1,0:T(8,128)(2,1)S(1)}, u32[]{:S(2)}, u32[]{:S(2)}) collective-permute-start(bf16[128,1536]{1,0:T(8,128)(2,1)S(1)} %get-tuple-element.15), channel_id=1, source_target_pairs={{0,3},{1,0},{2,1},{3,2},{4,7},{5,4},{6,5},{7,6},{8,11},{9,8},{10,9... | collective-permute-start | bytes 1179656 | tf_op jit(solution)/shard_map/out_reduce/ppermute | solution.py:51
  179.0 10.1 %collective-permute-start.20 = (bf16[8,256]{1,0:T(8,128)(2,1)S(1)}, bf16[8,256]{1,0:T(8,128)(2,1)S(1)}, u32[]{:S(2)}, u32[]{:S(2)}) collective-permute-start(bf16[8,256]{1,0:T(8,128)(2,1)S(1)} %convolution_convert_fusion.1), channel_id=1, source_target_pairs={{0,1},{1,0},{2,3},{3,2},{4,5},{5,4},{6,7},{7,6},{8,9},{9,8},{10,11... | collective-permute-start | bytes 12296 | tf_op jit(solution)/shard_map/sides_gather/ppermute | solution.py:96
  189.1 4.5 %collective-permute-start.21 = (bf16[16,256]{1,0:T(8,128)(2,1)S(1)}, bf16[16,256]{1,0:T(8,128)(2,1)S(1)}, u32[]{:S(2)}, u32[]{:S(2)}) collective-permute-start(bf16[16,256]{1,0:T(8,128)(2,1)S(1)} %maximum_select_fusion.3), channel_id=1, source_target_pairs={{0,2},{1,3},{2,0},{3,1},{4,6},{5,7},{6,4},{7,5},{8,10},{9,11},{10,... | collective-permute-start | bytes 24584 | tf_op jit(solution)/shard_map/sides_gather/ppermute | solution.py:96
  193.7 1.2 collective-permute-start.22
  194.9 4.0 %collective-permute-start.23 = (bf16[64,256]{1,0:T(8,128)(2,1)S(1)}, bf16[64,256]{1,0:T(8,128)(2,1)S(1)}, u32[]{:S(2)}, u32[]{:S(2)}) collective-permute-start(bf16[64,256]{1,0:T(8,128)(2,1)S(1)} %maximum_select_fusion.1), channel_id=1, source_target_pairs={{0,8},{4,12},{8,0},{12,4},{1,9},{5,13},{9,1},{13,5},{2,10},{6,14},... | collective-permute-start | bytes 98312 | tf_op jit(solution)/shard_map/sides_gather/ppermute | solution.py:96
  (2 other events, 2.4 us)

commit v3 on v2

--- a/solution.py
+++ b/solution.py
@@ -84,6 +84,36 @@
         slots = lax.dynamic_update_index_in_dim(slots, flow_r, at_r, 0)
         slots = lax.dynamic_update_index_in_dim(slots, flow_l, at_l, 0)
     return slots[:n].reshape((n * rows,) + value.shape[1:])
+
+
+def rows_to_heads(value, axis):
+    n = lax.axis_size(axis)
+    me = lax.axis_index(axis)
+    rows = value.shape[0] // n
+    pieces = value.reshape(n, rows, value.shape[1])
+    slots = jnp.zeros((n, rows, value.shape[1]), value.dtype)
+    slots = lax.dynamic_update_index_in_dim(slots, pieces[me], me, 0)
+    for shift in range(1, n):
+        outgoing = pieces[(me + shift) % n]
+        incoming = lax.ppermute(outgoing, axis, [(i, (i + shift) % n) for i in range(n)])
+        slots = lax.dynamic_update_index_in_dim(slots, incoming, (me + n - shift) % n, 0)
+    return slots.transpose(1, 0, 2).reshape(rows, n * value.shape[1])
+
+
+def gather_weight_rows(weight, axis, chip_axis):
+    peers = lax.axis_size(chip_axis)
+    if peers % 2:
+        return line_all_gather(weight, axis)
+    core = lax.axis_index(chip_axis) % 2
+    half = weight.shape[1] // 2
+    mine = lax.dynamic_slice_in_dim(weight, core * half, half, 1)
+    gathered = line_all_gather(mine, axis)
+    other = lax.ppermute(gathered, chip_axis, [(i, i ^ 1) for i in range(peers)])
+    return jnp.where(
+        core == 0,
+        jnp.concatenate([gathered, other], 1),
+        jnp.concatenate([other, gathered], 1),
+    )
 
 
 def doubling_all_gather(value, axis):
@@ -163,10 +193,11 @@
     running_max, running_sum, weighted = state
     attended = (weighted / running_sum[:, :, None]).astype(jnp.bfloat16)
     attended = attended.transpose(1, 0, 2).reshape(local_rows, head_count * VALUE_SIZE)
-    with jax.named_scope("out_reduce"):
-        mixed = direct_reduce_scatter(
-            jnp.dot(attended, w_out, preferred_element_type=jnp.float32), "pair"
-        )
+    with jax.named_scope("out_projection"):
+        late_w_out, unused = lax.optimization_barrier((w_out, kv))
+        full_w_out = gather_weight_rows(late_w_out, "pair", "seq")
+        own_heads = rows_to_heads(attended, "pair")
+        mixed = jnp.dot(own_heads, full_w_out, preferred_element_type=jnp.float32)
     seq_out = (first_out.astype(jnp.float32) + mixed).astype(jnp.bfloat16)
     bin_count = row_count // POOL
     pooled = jnp.mean(seq_out.astype(jnp.float32).reshape(bin_count, POOL, channels), axis=1)

time: 201 us -> 196 us (0.975)
  waiting for transfers between devices: 108 us -> 78.7 us
  local copies, waits for them, and re-layouts: 12.9 us -> 26 us
  starting transfers between devices: 54.9 us -> 63.5 us
  matrix products: 15.7 us -> 19 us
    ppermute x3, waiting for transfers between devices: 24.4 us -> 0.42 us  [shards(): arriving = lax.ppermute(current, 'seq', ring)]
    ppermute x6 -> x3, waiting for transfers between devices: 48.7 us -> 26 us  [direct_reduce_scatter(): lax.ppermute(outgoing, axis, [(i, (i + shift) % n) for i in range(n)])]
    ppermute x3 -> x6, starting transfers between devices: 19 us -> 31.9 us  [line_all_gather(): flow_r = lax.ppermute(flow_r, axis, right)]
    ppermute x3 -> x6, waiting for transfers between devices: 16.5 us -> 24.9 us  [line_all_gather(): flow_r = lax.ppermute(flow_r, axis, right)]
    ppermute x4, starting transfers between devices: 11.2 us -> 4.83 us  [doubling_all_gather(): other = lax.ppermute(out, axis, [(i, i ^ k) for i in range(n)])]
    ppermute x6 -> x3, starting transfers between devices: 10.4 us -> 4.75 us  [direct_reduce_scatter(): lax.ppermute(outgoing, axis, [(i, (i + shift) % n) for i in range(n)])]
    ppermute x0 -> x4, waiting for transfers between devices: none -> 4.77 us  [the longest x3 4.77 us: rows_to_heads(): lax.ppermute(outgoing, axis, [(i, (i + shift) % n) for i in range(n)])]
    ppermute x3 -> x6, waiting for transfers between devices: 3.38 us -> 7.41 us  [line_all_gather(): flow_l = lax.ppermute(flow_l, axis, left)]
  transfers between devices with their start and end apart: 24 -> 31, of which waited for: 19 -> 23; matrix products, arithmetic and copies ran while one was open for 5% -> 13% of each run, Pallas kernels for 0% -> 0%
where the time goes in v3:
time: 196 us; the launch traced here: 195 us
  waiting for transfers between devices  78.7 us (40%)
  starting transfers between devices  63.5 us (32%)
  local copies, waits for them, and re-layouts  26 us (13%)
  matrix products  19 us (10%)
  other arithmetic  6.94 us (4%)
    ppermute x6, starting transfers between devices, line_all_gather(): flow_r = lax.ppermute(flow_r, axis, right)  31.9 us
    ppermute x3, waiting for transfers between devices, direct_reduce_scatter(): lax.ppermute(outgoing, axis, [(i, (i + shift) % n) for i in range(n)])  26 us
    ppermute x6, waiting for transfers between devices, line_all_gather(): flow_r = lax.ppermute(flow_r, axis, right)  24.9 us
    ppermute x4, waiting for transfers between devices, doubling_all_gather(): other = lax.ppermute(out, axis, [(i, i ^ k) for i in range(n)])  9.04 us
    ppermute x6, starting transfers between devices, line_all_gather(): flow_l = lax.ppermute(flow_l, axis, left)  7.72 us
    ppermute x6, waiting for transfers between devices, line_all_gather(): flow_l = lax.ppermute(flow_l, axis, left)  7.41 us
    ppermute x3, starting transfers between devices, permute_all_to_all(): lax.ppermute(outgoing, axis, [(i, (i + shift) % n) for i in range(n)])  7.13 us
    dot_general x5, matrix products, conv_rows(): jnp.dot(shifted, conv_weight[offset], preferred_element_type=jnp.float32)  6.46 us
  transfers between devices with their start and end apart: 31, of which 23 were waited for; matrix products, arithmetic and copies ran while one was open for 13% of the time, Pallas kernels for 0%

profile of v3, /device:TPU:0, one launch (start us, length us, event | category | flops | bytes accessed | tf_op | source)
XLA Modules:
  0.0 195.4 jit_solution(8361595953119745472)
XLA Ops:
  4.1 3.1 %collective-permute-start = (bf16[128,384]{1,0:T(8,128)(2,1)S(1)}, bf16[128,384]{1,0:T(8,128)(2,1)S(1)}, u32[]{:S(2)}, u32[]{:S(2)}) collective-permute-start(bf16[128,384]{1,0:T(8,128)(2,1)S(1)} %bitcast.224), channel_id=1, source_target_pairs={{0,1},{1,2},{2,3},{3,0},{4,5},{5,6},{6,7},{7,4},{8,9},{9,10},{10,1... | collective-permute-start | bytes 294920 | tf_op jit(solution)/shard_map/ppermute | solution.py:65
  7.2 2.7 %collective-permute-start.1 = (bf16[128,384]{1,0:T(8,128)(2,1)S(1)}, bf16[128,384]{1,0:T(8,128)(2,1)S(1)}, u32[]{:S(2)}, u32[]{:S(2)}) collective-permute-start(bf16[128,384]{1,0:T(8,128)(2,1)S(1)} %bitcast.223), channel_id=1, source_target_pairs={{0,2},{1,3},{2,0},{3,1},{4,6},{5,7},{6,4},{7,5},{8,10},{9,11},{10,... | collective-permute-start | bytes 294920 | tf_op jit(solution)/shard_map/ppermute | solution.py:65
  12.9 3.5 %collective-permute-done.1 = bf16[128,384]{1,0:T(8,128)(2,1)S(1)} collective-permute-done((bf16[128,384]{1,0:T(8,128)(2,1)S(1)}, bf16[128,384]{1,0:T(8,128)(2,1)S(1)}, u32[]{:S(2)}, u32[]{:S(2)}) %collective-permute-start.1) | collective-permute-done | bytes 98336 | tf_op jit(solution)/shard_map/ppermute | solution.py:65
  19.9 2.4 %fusion.37 = f32[512,1536]{1,0:T(8,128)S(1)} fusion(bf16[512,384]{1,0:T(8,128)(2,1)S(1)} %bitcast.205, bf16[5,384,1536]{2,1,0:T(8,128)(2,1)} %param.12), kind=kOutput, calls=%fused_computation.58 | convolution fusion | flops 603979776 | bytes 4718592 | tf_op jit(solution)/shard_map/conv_reduce/dot_general | solution.py:39
  29.9 2.4 %collective-permute-start.5 = (bf16[128,1536]{1,0:T(8,128)(2,1)}, bf16[128,1536]{1,0:T(8,128)(2,1)S(1)}, u32[]{:S(2)}, u32[]{:S(2)}) collective-permute-start(bf16[128,1536]{1,0:T(8,128)(2,1)} %get-tuple-element.16), channel_id=1, source_target_pairs={{0,1},{1,2},{2,3},{3,0},{4,5},{5,6},{6,7},{7,4},{8,9},{9,10},{10,1... | collective-permute-start | bytes 1179656 | tf_op jit(solution)/shard_map/conv_reduce/ppermute | solution.py:51
  34.7 8.1 %collective-permute-done.5 = bf16[128,1536]{1,0:T(8,128)(2,1)S(1)} collective-permute-done((bf16[128,1536]{1,0:T(8,128)(2,1)}, bf16[128,1536]{1,0:T(8,128)(2,1)S(1)}, u32[]{:S(2)}, u32[]{:S(2)}) %collective-permute-start.5) | collective-permute-done | bytes 393248 | tf_op jit(solution)/shard_map/conv_reduce/ppermute | solution.py:51
  42.8 17.9 %collective-permute-done.6 = bf16[128,1536]{1,0:T(8,128)(2,1)S(1)} collective-permute-done((bf16[128,1536]{1,0:T(8,128)(2,1)}, bf16[128,1536]{1,0:T(8,128)(2,1)S(1)}, u32[]{:S(2)}, u32[]{:S(2)}) %collective-permute-start.6) | collective-permute-done | bytes 393248 | tf_op jit(solution)/shard_map/conv_reduce/ppermute | solution.py:51
  61.5 1.7 fusion.63
  65.7 10.3 %collective-permute-start.8 = (bf16[128,1536]{1,0:T(8,128)(2,1)}, bf16[128,1536]{1,0:T(8,128)(2,1)S(1)}, u32[]{:S(2)}, u32[]{:S(2)}) collective-permute-start(bf16[128,1536]{1,0:T(8,128)(2,1)} %get-tuple-element.13), channel_id=1, source_target_pairs={{0,1},{1,2},{2,3},{4,5},{5,6},{6,7},{8,9},{9,10},{10,11},{12,13},{... | collective-permute-start | bytes 1179656 | tf_op jit(solution)/shard_map/attn_in_gather/ppermute | solution.py:80
  77.4 7.6 %collective-permute-done.8 = bf16[128,1536]{1,0:T(8,128)(2,1)S(1)} collective-permute-done((bf16[128,1536]{1,0:T(8,128)(2,1)}, bf16[128,1536]{1,0:T(8,128)(2,1)S(1)}, u32[]{:S(2)}, u32[]{:S(2)}) %collective-permute-start.8) | collective-permute-done | bytes 393248 | tf_op jit(solution)/shard_map/attn_in_gather/ppermute | solution.py:80
  84.9 4.3 %collective-permute-start.10 = (bf16[128,1536]{1,0:T(8,128)(2,1)S(1)}, bf16[128,1536]{1,0:T(8,128)(2,1)S(1)}, u32[]{:S(2)}, u32[]{:S(2)}) collective-permute-start(bf16[128,1536]{1,0:T(8,128)(2,1)S(1)} %collective-permute-done.8), channel_id=1, source_target_pairs={{0,1},{1,2},{2,3},{4,5},{5,6},{6,7},{8,9},{9,10},{10,11},{12,13},{... | collective-permute-start | bytes 1179656 | tf_op jit(solution)/shard_map/attn_in_gather/ppermute | solution.py:80
  92.1 4.9 %collective-permute-done.10 = bf16[128,1536]{1,0:T(8,128)(2,1)S(1)} collective-permute-done((bf16[128,1536]{1,0:T(8,128)(2,1)S(1)}, bf16[128,1536]{1,0:T(8,128)(2,1)S(1)}, u32[]{:S(2)}, u32[]{:S(2)}) %collective-permute-start.10) | collective-permute-done | bytes 393248 | tf_op jit(solution)/shard_map/attn_in_gather/ppermute | solution.py:80
  97.0 4.4 %collective-permute-start.12 = (bf16[128,1536]{1,0:T(8,128)(2,1)S(1)}, bf16[128,1536]{1,0:T(8,128)(2,1)S(1)}, u32[]{:S(2)}, u32[]{:S(2)}) collective-permute-start(bf16[128,1536]{1,0:T(8,128)(2,1)S(1)} %collective-permute-done.10), channel_id=1, source_target_pairs={{0,1},{1,2},{2,3},{4,5},{5,6},{6,7},{8,9},{9,10},{10,11},{12,13},{... | collective-permute-start | bytes 1179656 | tf_op jit(solution)/shard_map/attn_in_gather/ppermute | solution.py:80
  104.3 3.9 %collective-permute-done.12 = bf16[128,1536]{1,0:T(8,128)(2,1)S(1)} collective-permute-done((bf16[128,1536]{1,0:T(8,128)(2,1)S(1)}, bf16[128,1536]{1,0:T(8,128)(2,1)S(1)}, u32[]{:S(2)}, u32[]{:S(2)}) %collective-permute-start.12) | collective-permute-done | bytes 393248 | tf_op jit(solution)/shard_map/attn_in_gather/ppermute | solution.py:80
  109.1 3.3 %collective-permute-done.13 = bf16[128,1536]{1,0:T(8,128)(2,1)S(1)} collective-permute-done((bf16[128,1536]{1,0:T(8,128)(2,1)S(1)}, bf16[128,1536]{1,0:T(8,128)(2,1)S(1)}, u32[]{:S(2)}, u32[]{:S(2)}) %collective-permute-start.13) | collective-permute-done | bytes 393248 | tf_op jit(solution)/shard_map/attn_in_gather/ppermute | solution.py:81
  119.4 4.2 %collective-permute-start.20 = (bf16[256,768]{1,0:T(8,128)(2,1)}, bf16[256,768]{1,0:T(8,128)(2,1)}, u32[]{:S(2)}, u32[]{:S(2)}) collective-permute-start(bf16[256,768]{1,0:T(8,128)(2,1)} %get-tuple-element.5), channel_id=1, source_target_pairs={{0,1},{1,2},{2,3},{4,5},{5,6},{6,7},{8,9},{9,10},{10,11},{12,13},{... | collective-permute-start | bytes 1179656 | tf_op jit(solution)/shard_map/out_projection/ppermute | solution.py:80
  125.3 4.3 %collective-permute-done.20 = bf16[256,768]{1,0:T(8,128)(2,1)} collective-permute-done((bf16[256,768]{1,0:T(8,128)(2,1)}, bf16[256,768]{1,0:T(8,128)(2,1)}, u32[]{:S(2)}, u32[]{:S(2)}) %collective-permute-start.20) | collective-permute-done | bytes 393248 | tf_op jit(solution)/shard_map/out_projection/ppermute | solution.py:80
  129.7 4.4 %collective-permute-start.22 = (bf16[256,768]{1,0:T(8,128)(2,1)}, bf16[256,768]{1,0:T(8,128)(2,1)S(1)}, u32[]{:S(2)}, u32[]{:S(2)}) collective-permute-start(bf16[256,768]{1,0:T(8,128)(2,1)} %collective-permute-done.20), channel_id=1, source_target_pairs={{0,1},{1,2},{2,3},{4,5},{5,6},{6,7},{8,9},{9,10},{10,11},{12,13},{... | collective-permute-start | bytes 1179656 | tf_op jit(solution)/shard_map/out_projection/ppermute | solution.py:80
  135.8 1.8 bitcast_dynamic-update-slice_fusion.5
  137.6 1.8 bitcast_dynamic-update-slice_fusion.4
  140.0 4.4 %collective-permute-start.24 = (bf16[256,768]{1,0:T(8,128)(2,1)S(1)}, bf16[256,768]{1,0:T(8,128)(2,1)S(1)}, u32[]{:S(2)}, u32[]{:S(2)}) collective-permute-start(bf16[256,768]{1,0:T(8,128)(2,1)S(1)} %collective-permute-done.22), channel_id=1, source_target_pairs={{0,1},{1,2},{2,3},{4,5},{5,6},{6,7},{8,9},{9,10},{10,11},{12,13},{... | collective-permute-start | bytes 1179656 | tf_op jit(solution)/shard_map/out_projection/ppermute | solution.py:80
  148.4 4.1 %collective-permute-done.24 = bf16[256,768]{1,0:T(8,128)(2,1)S(1)} collective-permute-done((bf16[256,768]{1,0:T(8,128)(2,1)S(1)}, bf16[256,768]{1,0:T(8,128)(2,1)S(1)}, u32[]{:S(2)}, u32[]{:S(2)}) %collective-permute-start.24) | collective-permute-done | bytes 393248 | tf_op jit(solution)/shard_map/out_projection/ppermute | solution.py:80
  153.3 3.3 %collective-permute-done.25 = bf16[256,768]{1,0:T(8,128)(2,1)S(1)} collective-permute-done((bf16[256,768]{1,0:T(8,128)(2,1)S(1)}, bf16[256,768]{1,0:T(8,128)(2,1)S(1)}, u32[]{:S(2)}, u32[]{:S(2)}) %collective-permute-start.25) | collective-permute-done | bytes 393248 | tf_op jit(solution)/shard_map/out_projection/ppermute | solution.py:81
  157.4 2.7 %slice.103 = bf16[4,256,768]{2,1,0:T(8,128)(2,1)} slice(bf16[5,256,768]{2,1,0:T(8,128)(2,1)} %bitcast_dynamic-update-slice_fusion), slice={[0:4], [0:256], [0:768]} | slice | bytes 3145728 | tf_op jit(solution)/shard_map/out_projection/slice | solution.py:86
  166.4 3.1 %collective-permute-start.19 = (bf16[128,256]{1,0:T(8,128)(2,1)S(1)}, bf16[128,256]{1,0:T(8,128)(2,1)S(1)}, u32[]{:S(2)}, u32[]{:S(2)}) collective-permute-start(bf16[128,256]{1,0:T(8,128)(2,1)S(1)} %get-tuple-element.25), channel_id=1, source_target_pairs={{0,3},{1,0},{2,1},{3,2},{4,7},{5,4},{6,5},{7,6},{8,11},{9,8},{10,9... | collective-permute-start | bytes 196616 | tf_op jit(solution)/shard_map/out_projection/ppermute | solution.py:98
  169.5 2.9 %collective-permute-done.17 = bf16[128,256]{1,0:T(8,128)(2,1)S(1)} collective-permute-done((bf16[128,256]{1,0:T(8,128)(2,1)S(1)}, bf16[128,256]{1,0:T(8,128)(2,1)S(1)}, u32[]{:S(2)}, u32[]{:S(2)}) %collective-permute-start.17) | collective-permute-done | bytes 65568 | tf_op jit(solution)/shard_map/out_projection/ppermute | solution.py:98
  172.5 1.9 collective-permute-done.18
  174.7 5.0 %convert_reduce_fusion = (f32[8,1536]{1,0:T(8,128)S(1)}, bf16[128,1536]{1,0:T(8,128)(2,1)}) fusion(bf16[128,1024]{0,1:T(8,128)(2,1)S(1)} %bitcast.221, bf16[1024,768]{1,0:T(8,128)(2,1)} %collective-permute-done.26, bf16[1024,768]{1,0:T(8,128)(2,1)} %bitcast.54, pred[]{:T(512)S(6)} %eq.32, bf16[128,1536]{1,0:T(8,128)(2,1)S(1)} %get-tuple-element.15), kind=kOutput, calls=%fused_computation.85 | convolution fusion | flops 417779712 | bytes 4243457 | tf_op jit(solution)/shard_map/out_projection/dot_general | solution.py:200
  181.5 2.2 %collective-permute-done.27 = bf16[8,256]{1,0:T(8,128)(2,1)S(1)} collective-permute-done((bf16[8,256]{1,0:T(8,128)(2,1)S(1)}, bf16[8,256]{1,0:T(8,128)(2,1)S(1)}, u32[]{:S(2)}, u32[]{:S(2)}) %collective-permute-start.27) | collective-permute-done | bytes 4128 | tf_op jit(solution)/shard_map/sides_gather/ppermute | solution.py:126
  184.6 3.7 %collective-permute-done.28 = bf16[16,256]{1,0:T(8,128)(2,1)S(1)} collective-permute-done((bf16[16,256]{1,0:T(8,128)(2,1)S(1)}, bf16[16,256]{1,0:T(8,128)(2,1)S(1)}, u32[]{:S(2)}, u32[]{:S(2)}) %collective-permute-start.28) | collective-permute-done | bytes 8224 | tf_op jit(solution)/shard_map/sides_gather/ppermute | solution.py:126
  189.5 2.6 %collective-permute-start.30 = (bf16[64,256]{1,0:T(8,128)(2,1)S(1)}, bf16[64,256]{1,0:T(8,128)(2,1)S(1)}, u32[]{:S(2)}, u32[]{:S(2)}) collective-permute-start(bf16[64,256]{1,0:T(8,128)(2,1)S(1)} %maximum_select_fusion.7), channel_id=1, source_target_pairs={{0,8},{4,12},{8,0},{12,4},{1,9},{5,13},{9,1},{13,5},{2,10},{6,14},... | collective-permute-start | bytes 98312 | tf_op jit(solution)/shard_map/sides_gather/ppermute | solution.py:126
  192.2 1.9 collective-permute-done.30
  (130 shorter events, 59.3 us)
Async XLA Ops:
  0.6 114.1 %copy-start = (bf16[1536,768]{1,0:T(8,128)(2,1)S(1)}, bf16[1536,768]{1,0:T(8,128)(2,1)}, u32[]{:S(2)}) copy-start(bf16[1536,768]{1,0:T(8,128)(2,1)} %param.14) | copy-start | bytes 7077892
  4.1 8.7 %collective-permute-start = (bf16[128,384]{1,0:T(8,128)(2,1)S(1)}, bf16[128,384]{1,0:T(8,128)(2,1)S(1)}, u32[]{:S(2)}, u32[]{:S(2)}) collective-permute-start(bf16[128,384]{1,0:T(8,128)(2,1)S(1)} %bitcast.224), channel_id=1, source_target_pairs={{0,1},{1,2},{2,3},{3,0},{4,5},{5,6},{6,7},{7,4},{8,9},{9,10},{10,1... | collective-permute-start | bytes 294920 | tf_op jit(solution)/shard_map/ppermute | solution.py:65
  7.2 9.2 %collective-permute-start.1 = (bf16[128,384]{1,0:T(8,128)(2,1)S(1)}, bf16[128,384]{1,0:T(8,128)(2,1)S(1)}, u32[]{:S(2)}, u32[]{:S(2)}) collective-permute-start(bf16[128,384]{1,0:T(8,128)(2,1)S(1)} %bitcast.223), channel_id=1, source_target_pairs={{0,2},{1,3},{2,0},{3,1},{4,6},{5,7},{6,4},{7,5},{8,10},{9,11},{10,... | collective-permute-start | bytes 294920 | tf_op jit(solution)/shard_map/ppermute | solution.py:65
  9.9 6.7 %collective-permute-start.2 = (bf16[128,384]{1,0:T(8,128)(2,1)S(1)}, bf16[128,384]{1,0:T(8,128)(2,1)S(1)}, u32[]{:S(2)}, u32[]{:S(2)}) collective-permute-start(bf16[128,384]{1,0:T(8,128)(2,1)S(1)} %bitcast.222), channel_id=1, source_target_pairs={{0,3},{1,0},{2,1},{3,2},{4,7},{5,4},{6,5},{7,6},{8,11},{9,8},{10,9... | collective-permute-start | bytes 294920 | tf_op jit(solution)/shard_map/ppermute | solution.py:65
  16.6 8.5 %collective-permute-start.3 = (bf16[8,384]{1,0:T(8,128)(2,1)S(1)}, bf16[8,384]{1,0:T(8,128)(2,1)S(1)}, u32[]{:S(2)}, u32[]{:S(2)}) collective-permute-start(bf16[8,384]{1,0:T(8,128)(2,1)S(1)} %get-tuple-element.19), channel_id=1, source_target_pairs={{0,4},{4,8},{8,12},{1,5},{5,9},{9,13},{2,6},{6,10},{10,14},{3,7},{... | collective-permute-start | bytes 18440 | tf_op jit(solution)/shard_map/ppermute | solution.py:25
  18.3 4.8 %collective-permute-start.4 = (bf16[8,384]{1,0:T(8,128)(2,1)S(1)}, bf16[8,384]{1,0:T(8,128)(2,1)S(1)}, u32[]{:S(2)}, u32[]{:S(2)}) collective-permute-start(bf16[8,384]{1,0:T(8,128)(2,1)S(1)} %get-tuple-element.20), channel_id=1, source_target_pairs={{4,0},{8,4},{12,8},{5,1},{9,5},{13,9},{6,2},{10,6},{14,10},{7,3},{... | collective-permute-start | bytes 18440 | tf_op jit(solution)/shard_map/ppermute | solution.py:26
  29.9 12.9 %collective-permute-start.5 = (bf16[128,1536]{1,0:T(8,128)(2,1)}, bf16[128,1536]{1,0:T(8,128)(2,1)S(1)}, u32[]{:S(2)}, u32[]{:S(2)}) collective-permute-start(bf16[128,1536]{1,0:T(8,128)(2,1)} %get-tuple-element.16), channel_id=1, source_target_pairs={{0,1},{1,2},{2,3},{3,0},{4,5},{5,6},{6,7},{7,4},{8,9},{9,10},{10,1... | collective-permute-start | bytes 1179656 | tf_op jit(solution)/shard_map/conv_reduce/ppermute | solution.py:51
  32.3 28.4 %collective-permute-start.6 = (bf16[128,1536]{1,0:T(8,128)(2,1)}, bf16[128,1536]{1,0:T(8,128)(2,1)S(1)}, u32[]{:S(2)}, u32[]{:S(2)}) collective-permute-start(bf16[128,1536]{1,0:T(8,128)(2,1)} %get-tuple-element.18), channel_id=1, source_target_pairs={{0,2},{1,3},{2,0},{3,1},{4,6},{5,7},{6,4},{7,5},{8,10},{9,11},{10,... | collective-permute-start | bytes 1179656 | tf_op jit(solution)/shard_map/conv_reduce/ppermute | solution.py:51
  34.0 27.5 %collective-permute-start.7 = (bf16[128,1536]{1,0:T(8,128)(2,1)}, bf16[128,1536]{1,0:T(8,128)(2,1)}, u32[]{:S(2)}, u32[]{:S(2)}) collective-permute-start(bf16[128,1536]{1,0:T(8,128)(2,1)} %get-tuple-element.17), channel_id=1, source_target_pairs={{0,3},{1,0},{2,1},{3,2},{4,7},{5,4},{6,5},{7,6},{8,11},{9,8},{10,9... | collective-permute-start | bytes 1179656 | tf_op jit(solution)/shard_map/conv_reduce/ppermute | solution.py:51
  65.7 19.2 %collective-permute-start.8 = (bf16[128,1536]{1,0:T(8,128)(2,1)}, bf16[128,1536]{1,0:T(8,128)(2,1)S(1)}, u32[]{:S(2)}, u32[]{:S(2)}) collective-permute-start(bf16[128,1536]{1,0:T(8,128)(2,1)} %get-tuple-element.13), channel_id=1, source_target_pairs={{0,1},{1,2},{2,3},{4,5},{5,6},{6,7},{8,9},{9,10},{10,11},{12,13},{... | collective-permute-start | bytes 1179656 | tf_op jit(solution)/shard_map/attn_in_gather/ppermute | solution.py:80
  76.0 13.2 %collective-permute-start.9 = (bf16[128,1536]{1,0:T(8,128)(2,1)}, bf16[128,1536]{1,0:T(8,128)(2,1)S(1)}, u32[]{:S(2)}, u32[]{:S(2)}) collective-permute-start(bf16[128,1536]{1,0:T(8,128)(2,1)} %get-tuple-element.13), channel_id=1, source_target_pairs={{1,0},{2,1},{3,2},{5,4},{6,5},{7,6},{9,8},{10,9},{11,10},{13,12},{... | collective-permute-start | bytes 1179656 | tf_op jit(solution)/shard_map/attn_in_gather/ppermute | solution.py:81
  84.9 12.1 %collective-permute-start.10 = (bf16[128,1536]{1,0:T(8,128)(2,1)S(1)}, bf16[128,1536]{1,0:T(8,128)(2,1)S(1)}, u32[]{:S(2)}, u32[]{:S(2)}) collective-permute-start(bf16[128,1536]{1,0:T(8,128)(2,1)S(1)} %collective-permute-done.8), channel_id=1, source_target_pairs={{0,1},{1,2},{2,3},{4,5},{5,6},{6,7},{8,9},{9,10},{10,11},{12,13},{... | collective-permute-start | bytes 1179656 | tf_op jit(solution)/shard_map/attn_in_gather/ppermute | solution.py:80
  89.2 12.2 %collective-permute-start.11 = (bf16[128,1536]{1,0:T(8,128)(2,1)S(1)}, bf16[128,1536]{1,0:T(8,128)(2,1)S(1)}, u32[]{:S(2)}, u32[]{:S(2)}) collective-permute-start(bf16[128,1536]{1,0:T(8,128)(2,1)S(1)} %collective-permute-done.9), channel_id=1, source_target_pairs={{1,0},{2,1},{3,2},{5,4},{6,5},{7,6},{9,8},{10,9},{11,10},{13,12},{... | collective-permute-start | bytes 1179656 | tf_op jit(solution)/shard_map/attn_in_gather/ppermute | solution.py:81
  97.0 11.3 %collective-permute-start.12 = (bf16[128,1536]{1,0:T(8,128)(2,1)S(1)}, bf16[128,1536]{1,0:T(8,128)(2,1)S(1)}, u32[]{:S(2)}, u32[]{:S(2)}) collective-permute-start(bf16[128,1536]{1,0:T(8,128)(2,1)S(1)} %collective-permute-done.10), channel_id=1, source_target_pairs={{0,1},{1,2},{2,3},{4,5},{5,6},{6,7},{8,9},{9,10},{10,11},{12,13},{... | collective-permute-start | bytes 1179656 | tf_op jit(solution)/shard_map/attn_in_gather/ppermute | solution.py:80
  101.4 11.0 %collective-permute-start.13 = (bf16[128,1536]{1,0:T(8,128)(2,1)S(1)}, bf16[128,1536]{1,0:T(8,128)(2,1)S(1)}, u32[]{:S(2)}, u32[]{:S(2)}) collective-permute-start(bf16[128,1536]{1,0:T(8,128)(2,1)S(1)} %collective-permute-done.11), channel_id=1, source_target_pairs={{1,0},{2,1},{3,2},{5,4},{6,5},{7,6},{9,8},{10,9},{11,10},{13,12},{... | collective-permute-start | bytes 1179656 | tf_op jit(solution)/shard_map/attn_in_gather/ppermute | solution.py:81
  119.4 10.3 %collective-permute-start.20 = (bf16[256,768]{1,0:T(8,128)(2,1)}, bf16[256,768]{1,0:T(8,128)(2,1)}, u32[]{:S(2)}, u32[]{:S(2)}) collective-permute-start(bf16[256,768]{1,0:T(8,128)(2,1)} %get-tuple-element.5), channel_id=1, source_target_pairs={{0,1},{1,2},{2,3},{4,5},{5,6},{6,7},{8,9},{9,10},{10,11},{12,13},{... | collective-permute-start | bytes 1179656 | tf_op jit(solution)/shard_map/out_projection/ppermute | solution.py:80
  123.5 11.0 %collective-permute-start.21 = (bf16[256,768]{1,0:T(8,128)(2,1)}, bf16[256,768]{1,0:T(8,128)(2,1)}, u32[]{:S(2)}, u32[]{:S(2)}) collective-permute-start(bf16[256,768]{1,0:T(8,128)(2,1)} %get-tuple-element.5), channel_id=1, source_target_pairs={{1,0},{2,1},{3,2},{5,4},{6,5},{7,6},{9,8},{10,9},{11,10},{13,12},{... | collective-permute-start | bytes 1179656 | tf_op jit(solution)/shard_map/out_projection/ppermute | solution.py:81
  124.8 14.5 %collective-permute-start.14 = (bf16[2,512,256]{2,1,0:T(8,128)(2,1)}, bf16[2,512,256]{2,1,0:T(8,128)(2,1)S(1)}, u32[]{:S(2)}, u32[]{:S(2)}) collective-permute-start(bf16[2,512,256]{2,1,0:T(8,128)(2,1)} %slice.96), channel_id=1, source_target_pairs={{0,4},{4,8},{8,12},{12,0},{1,5},{5,9},{9,13},{13,1},{2,6},{6,10},{... | collective-permute-start | bytes 1572872 | tf_op jit(solution)/shard_map/kv_ring/ppermute | solution.py:189
  129.7 10.3 %collective-permute-start.22 = (bf16[256,768]{1,0:T(8,128)(2,1)}, bf16[256,768]{1,0:T(8,128)(2,1)S(1)}, u32[]{:S(2)}, u32[]{:S(2)}) collective-permute-start(bf16[256,768]{1,0:T(8,128)(2,1)} %collective-permute-done.20), channel_id=1, source_target_pairs={{0,1},{1,2},{2,3},{4,5},{5,6},{6,7},{8,9},{9,10},{10,11},{12,13},{... | collective-permute-start | bytes 1179656 | tf_op jit(solution)/shard_map/out_projection/ppermute | solution.py:80
  134.5 10.2 %collective-permute-start.23 = (bf16[256,768]{1,0:T(8,128)(2,1)}, bf16[256,768]{1,0:T(8,128)(2,1)S(1)}, u32[]{:S(2)}, u32[]{:S(2)}) collective-permute-start(bf16[256,768]{1,0:T(8,128)(2,1)} %collective-permute-done.21), channel_id=1, source_target_pairs={{1,0},{2,1},{3,2},{5,4},{6,5},{7,6},{9,8},{10,9},{11,10},{13,12},{... | collective-permute-start | bytes 1179656 | tf_op jit(solution)/shard_map/out_projection/ppermute | solution.py:81
  139.4 8.6 %collective-permute-start.15 = (bf16[2,512,256]{2,1,0:T(8,128)(2,1)S(1)}, bf16[2,512,256]{2,1,0:T(8,128)(2,1)S(1)}, u32[]{:S(2)}, u32[]{:S(2)}) collective-permute-start(bf16[2,512,256]{2,1,0:T(8,128)(2,1)S(1)} %collective-permute-done.14), channel_id=1, source_target_pairs={{0,4},{4,8},{8,12},{12,0},{1,5},{5,9},{9,13},{13,1},{2,6},{6,10},{... | collective-permute-start | bytes 1572872 | tf_op jit(solution)/shard_map/kv_ring/ppermute | solution.py:189
  140.0 12.5 %collective-permute-start.24 = (bf16[256,768]{1,0:T(8,128)(2,1)S(1)}, bf16[256,768]{1,0:T(8,128)(2,1)S(1)}, u32[]{:S(2)}, u32[]{:S(2)}) collective-permute-start(bf16[256,768]{1,0:T(8,128)(2,1)S(1)} %collective-permute-done.22), channel_id=1, source_target_pairs={{0,1},{1,2},{2,3},{4,5},{5,6},{6,7},{8,9},{9,10},{10,11},{12,13},{... | collective-permute-start | bytes 1179656 | tf_op jit(solution)/shard_map/out_projection/ppermute | solution.py:80
  144.7 12.0 %collective-permute-start.25 = (bf16[256,768]{1,0:T(8,128)(2,1)S(1)}, bf16[256,768]{1,0:T(8,128)(2,1)S(1)}, u32[]{:S(2)}, u32[]{:S(2)}) collective-permute-start(bf16[256,768]{1,0:T(8,128)(2,1)S(1)} %collective-permute-done.23), channel_id=1, source_target_pairs={{1,0},{2,1},{3,2},{5,4},{6,5},{7,6},{9,8},{10,9},{11,10},{13,12},{... | collective-permute-start | bytes 1179656 | tf_op jit(solution)/shard_map/out_projection/ppermute | solution.py:81
  148.0 12.1 %collective-permute-start.16 = (bf16[2,512,256]{2,1,0:T(8,128)(2,1)S(1)}, bf16[2,512,256]{2,1,0:T(8,128)(2,1)S(1)}, u32[]{:S(2)}, u32[]{:S(2)}) collective-permute-start(bf16[2,512,256]{2,1,0:T(8,128)(2,1)S(1)} %collective-permute-done.15), channel_id=1, source_target_pairs={{0,4},{4,8},{8,12},{12,0},{1,5},{5,9},{9,13},{13,1},{2,6},{6,10},{... | collective-permute-start | bytes 1572872 | tf_op jit(solution)/shard_map/kv_ring/ppermute | solution.py:189
  160.1 14.6 %collective-permute-start.26 = (bf16[1024,768]{1,0:T(8,128)(2,1)}, bf16[1024,768]{1,0:T(8,128)(2,1)}, u32[]{:S(2)}, u32[]{:S(2)}) collective-permute-start(bf16[1024,768]{1,0:T(8,128)(2,1)} %bitcast.54), channel_id=1, source_target_pairs={{0,4},{4,0},{8,12},{12,8},{1,5},{5,1},{9,13},{13,9},{2,6},{6,2},{1... | collective-permute-start | bytes 4718600 | tf_op jit(solution)/shard_map/out_projection/ppermute | solution.py:111
  165.5 6.8 %collective-permute-start.17 = (bf16[128,256]{1,0:T(8,128)(2,1)S(1)}, bf16[128,256]{1,0:T(8,128)(2,1)S(1)}, u32[]{:S(2)}, u32[]{:S(2)}) collective-permute-start(bf16[128,256]{1,0:T(8,128)(2,1)S(1)} %get-tuple-element.27), channel_id=1, source_target_pairs={{0,1},{1,2},{2,3},{3,0},{4,5},{5,6},{6,7},{7,4},{8,9},{9,10},{10,1... | collective-permute-start | bytes 196616 | tf_op jit(solution)/shard_map/out_projection/ppermute | solution.py:98
  165.9 8.5 %collective-permute-start.18 = (bf16[128,256]{1,0:T(8,128)(2,1)S(1)}, bf16[128,256]{1,0:T(8,128)(2,1)S(1)}, u32[]{:S(2)}, u32[]{:S(2)}) collective-permute-start(bf16[128,256]{1,0:T(8,128)(2,1)S(1)} %get-tuple-element.26), channel_id=1, source_target_pairs={{0,2},{1,3},{2,0},{3,1},{4,6},{5,7},{6,4},{7,5},{8,10},{9,11},{10,... | collective-permute-start | bytes 196616 | tf_op jit(solution)/shard_map/out_projection/ppermute | solution.py:98
  166.4 8.1 %collective-permute-start.19 = (bf16[128,256]{1,0:T(8,128)(2,1)S(1)}, bf16[128,256]{1,0:T(8,128)(2,1)S(1)}, u32[]{:S(2)}, u32[]{:S(2)}) collective-permute-start(bf16[128,256]{1,0:T(8,128)(2,1)S(1)} %get-tuple-element.25), channel_id=1, source_target_pairs={{0,3},{1,0},{2,1},{3,2},{4,7},{5,4},{6,5},{7,6},{8,11},{9,8},{10,9... | collective-permute-start | bytes 196616 | tf_op jit(solution)/shard_map/out_projection/ppermute | solution.py:98
  180.2 3.6 %collective-permute-start.27 = (bf16[8,256]{1,0:T(8,128)(2,1)S(1)}, bf16[8,256]{1,0:T(8,128)(2,1)S(1)}, u32[]{:S(2)}, u32[]{:S(2)}) collective-permute-start(bf16[8,256]{1,0:T(8,128)(2,1)S(1)} %convolution_convert_fusion.1), channel_id=1, source_target_pairs={{0,1},{1,0},{2,3},{3,2},{4,5},{5,4},{6,7},{7,6},{8,9},{9,8},{10,11... | collective-permute-start | bytes 12296 | tf_op jit(solution)/shard_map/sides_gather/ppermute | solution.py:126
  183.8 4.5 %collective-permute-start.28 = (bf16[16,256]{1,0:T(8,128)(2,1)S(1)}, bf16[16,256]{1,0:T(8,128)(2,1)S(1)}, u32[]{:S(2)}, u32[]{:S(2)}) collective-permute-start(bf16[16,256]{1,0:T(8,128)(2,1)S(1)} %maximum_select_fusion.9), channel_id=1, source_target_pairs={{0,2},{1,3},{2,0},{3,1},{4,6},{5,7},{6,4},{7,5},{8,10},{9,11},{10,... | collective-permute-start | bytes 24584 | tf_op jit(solution)/shard_map/sides_gather/ppermute | solution.py:126
  188.3 1.2 collective-permute-start.29
  189.5 4.5 %collective-permute-start.30 = (bf16[64,256]{1,0:T(8,128)(2,1)S(1)}, bf16[64,256]{1,0:T(8,128)(2,1)S(1)}, u32[]{:S(2)}, u32[]{:S(2)}) collective-permute-start(bf16[64,256]{1,0:T(8,128)(2,1)S(1)} %maximum_select_fusion.7), channel_id=1, source_target_pairs={{0,8},{4,12},{8,0},{12,4},{1,9},{5,13},{9,1},{13,5},{2,10},{6,14},... | collective-permute-start | bytes 98312 | tf_op jit(solution)/shard_map/sides_gather/ppermute | solution.py:126
  (10 other events, 123.1 us)

commit v4 on v3

--- a/solution.py
+++ b/solution.py
@@ -114,6 +114,19 @@
         jnp.concatenate([gathered, other], 1),
         jnp.concatenate([other, gathered], 1),
     )
+
+
+def direct_all_gather(value, axis):
+    n = lax.axis_size(axis)
+    if n > 4:
+        return line_all_gather(value, axis)
+    me = lax.axis_index(axis)
+    slots = jnp.zeros((n,) + value.shape, value.dtype)
+    slots = lax.dynamic_update_index_in_dim(slots, value, me, 0)
+    for shift in range(1, n):
+        incoming = lax.ppermute(value, axis, [(i, (i + shift) % n) for i in range(n)])
+        slots = lax.dynamic_update_index_in_dim(slots, incoming, (me + n - shift) % n, 0)
+    return slots.reshape((n * value.shape[0],) + value.shape[1:])
 
 
 def doubling_all_gather(value, axis):
@@ -147,7 +160,7 @@
     first_out = (inputs + summed).astype(jnp.bfloat16)
     attn_in = norm_rows(first_out.astype(jnp.float32), gain_attn).astype(jnp.bfloat16)
     with jax.named_scope("attn_in_gather"):
-        block_in = line_all_gather(attn_in, "pair")
+        block_in = direct_all_gather(attn_in, "pair")
     projected = jnp.dot(block_in, w_qkv, preferred_element_type=jnp.float32).astype(jnp.bfloat16)
     head_count = projected.shape[1] // (2 * KEY_SIZE + VALUE_SIZE)
     grouped = projected.reshape(local_rows, head_count, 2 * KEY_SIZE + VALUE_SIZE).transpose(1, 0, 2)
@@ -204,7 +217,10 @@
     bin_norm = norm_rows(pooled, gain_pool).astype(jnp.bfloat16)
     sides = jnp.dot(bin_norm, w_pair, preferred_element_type=jnp.float32).astype(jnp.bfloat16)
     with jax.named_scope("sides_gather"):
-        all_sides = doubling_all_gather(doubling_all_gather(sides, "pair"), "seq")
+        if seq_count > 4:
+            all_sides = doubling_all_gather(doubling_all_gather(sides, "pair"), "seq")
+        else:
+            all_sides = direct_all_gather(direct_all_gather(sides, "pair"), "seq")
     tile_rows = bin_count * pair_count
     tile_cols = bin_count * seq_count
     row_side = lax.dynamic_slice_in_dim(

time: 196 us -> 189 us (0.964)
  waiting for transfers between devices: 78.7 us -> 86.5 us
  starting transfers between devices: 63.5 us -> 56 us
  local copies, waits for them, and re-layouts: 26 us -> 18.6 us
    ppermute x4 -> x9, waiting for transfers between devices: 9.04 us -> 28.2 us  [direct_all_gather(): lax.ppermute(value, axis, [(i, (i + shift) % n) for i in range(n)])]
    ppermute x6 -> x3, waiting for transfers between devices: 24.9 us -> 10.3 us  [line_all_gather(): flow_r = lax.ppermute(flow_r, axis, right)]
    ppermute x6 -> x3, starting transfers between devices: 31.9 us -> 18.8 us  [line_all_gather(): flow_r = lax.ppermute(flow_r, axis, right)]
    ppermute x3, waiting for transfers between devices: 26 us -> 34.6 us  [direct_reduce_scatter(): lax.ppermute(outgoing, axis, [(i, (i + shift) % n) for i in range(n)])]
    ppermute x4 -> x9, starting transfers between devices: 4.83 us -> 12.9 us  [direct_all_gather(): lax.ppermute(value, axis, [(i, (i + shift) % n) for i in range(n)])]
    ppermute x6 -> x3, starting transfers between devices: 7.72 us -> 3.84 us  [line_all_gather(): flow_l = lax.ppermute(flow_l, axis, left)]
    ppermute x6 -> x3, waiting for transfers between devices: 7.41 us -> 4 us  [line_all_gather(): flow_l = lax.ppermute(flow_l, axis, left)]
    dynamic_update_slice x6 -> x3, local copies, waits for them, and re-layouts: 5.81 us -> 3.38 us  [line_all_gather(): slots = lax.dynamic_update_index_in_dim(slots, flow_r, at_r, 0)]
  transfers between devices with their start and end apart: 31 -> 30, of which waited for: 23 -> 20; matrix products, arithmetic and copies ran while one was open for 13% -> 12% of each run, Pallas kernels for 0% -> 0%
where the time goes in v4:
time: 189 us; the launch traced here: 188 us
  waiting for transfers between devices  86.5 us (46%)
  starting transfers between devices  56 us (30%)
  matrix products  20.5 us (11%)
  local copies, waits for them, and re-layouts  18.6 us (10%)
  other arithmetic  5.42 us (3%)
    ppermute x3, waiting for transfers between devices, direct_reduce_scatter(): lax.ppermute(outgoing, axis, [(i, (i + shift) % n) for i in range(n)])  34.6 us
    ppermute x9, waiting for transfers between devices, direct_all_gather(): lax.ppermute(value, axis, [(i, (i + shift) % n) for i in range(n)])  28.2 us
    ppermute x3, starting transfers between devices, line_all_gather(): flow_r = lax.ppermute(flow_r, axis, right)  18.8 us
    ppermute x9, starting transfers between devices, direct_all_gather(): lax.ppermute(value, axis, [(i, (i + shift) % n) for i in range(n)])  12.9 us
    ppermute x3, waiting for transfers between devices, line_all_gather(): flow_r = lax.ppermute(flow_r, axis, right)  10.3 us
    ppermute x3, starting transfers between devices, permute_all_to_all(): lax.ppermute(outgoing, axis, [(i, (i + shift) % n) for i in range(n)])  7.13 us
    dot_general x5, matrix products, conv_rows(): jnp.dot(shifted, conv_weight[offset], preferred_element_type=jnp.float32)  6.46 us
    ppermute x3, waiting for transfers between devices, permute_all_to_all(): lax.ppermute(outgoing, axis, [(i, (i + shift) % n) for i in range(n)])  5.16 us
  transfers between devices with their start and end apart: 30, of which 20 were waited for; matrix products, arithmetic and copies ran while one was open for 12% of the time, Pallas kernels for 0%

profile of v4, /device:TPU:0, one launch (start us, length us, event | category | flops | bytes accessed | tf_op | source)
XLA Modules:
  0.0 188.2 jit_solution(16316762960699771129)
XLA Ops:
  4.1 3.1 %collective-permute-start = (bf16[128,384]{1,0:T(8,128)(2,1)S(1)}, bf16[128,384]{1,0:T(8,128)(2,1)S(1)}, u32[]{:S(2)}, u32[]{:S(2)}) collective-permute-start(bf16[128,384]{1,0:T(8,128)(2,1)S(1)} %bitcast.236), channel_id=1, source_target_pairs={{0,1},{1,2},{2,3},{3,0},{4,5},{5,6},{6,7},{7,4},{8,9},{9,10},{10,1... | collective-permute-start | bytes 294920 | tf_op jit(solution)/shard_map/ppermute | solution.py:65
  7.2 2.7 %collective-permute-start.1 = (bf16[128,384]{1,0:T(8,128)(2,1)S(1)}, bf16[128,384]{1,0:T(8,128)(2,1)S(1)}, u32[]{:S(2)}, u32[]{:S(2)}) collective-permute-start(bf16[128,384]{1,0:T(8,128)(2,1)S(1)} %bitcast.235), channel_id=1, source_target_pairs={{0,2},{1,3},{2,0},{3,1},{4,6},{5,7},{6,4},{7,5},{8,10},{9,11},{10,... | collective-permute-start | bytes 294920 | tf_op jit(solution)/shard_map/ppermute | solution.py:65
  11.4 1.5 collective-permute-done
  12.9 3.5 %collective-permute-done.1 = bf16[128,384]{1,0:T(8,128)(2,1)S(1)} collective-permute-done((bf16[128,384]{1,0:T(8,128)(2,1)S(1)}, bf16[128,384]{1,0:T(8,128)(2,1)S(1)}, u32[]{:S(2)}, u32[]{:S(2)}) %collective-permute-start.1) | collective-permute-done | bytes 98336 | tf_op jit(solution)/shard_map/ppermute | solution.py:65
  16.6 1.6 collective-permute-start.4
  18.2 2.4 %fusion.37 = f32[512,1536]{1,0:T(8,128)S(1)} fusion(bf16[512,384]{1,0:T(8,128)(2,1)S(1)} %bitcast.217, bf16[5,384,1536]{2,1,0:T(8,128)(2,1)} %param.12), kind=kOutput, calls=%fused_computation.58 | convolution fusion | flops 603979776 | bytes 4718592 | tf_op jit(solution)/shard_map/conv_reduce/dot_general | solution.py:39
  20.6 2.9 %collective-permute-start.3 = (bf16[8,384]{1,0:T(8,128)(2,1)S(1)}, bf16[8,384]{1,0:T(8,128)(2,1)S(1)}, u32[]{:S(2)}, u32[]{:S(2)}) collective-permute-start(bf16[8,384]{1,0:T(8,128)(2,1)S(1)} %get-tuple-element.19), channel_id=1, source_target_pairs={{0,4},{4,8},{8,12},{1,5},{5,9},{9,13},{2,6},{6,10},{10,14},{3,7},{... | collective-permute-start | bytes 18440 | tf_op jit(solution)/shard_map/ppermute | solution.py:25
  27.8 3.5 %collective-permute-start.7 = (bf16[128,1536]{1,0:T(8,128)(2,1)S(1)}, bf16[128,1536]{1,0:T(8,128)(2,1)S(1)}, u32[]{:S(2)}, u32[]{:S(2)}) collective-permute-start(bf16[128,1536]{1,0:T(8,128)(2,1)S(1)} %get-tuple-element.17), channel_id=1, source_target_pairs={{0,3},{1,0},{2,1},{3,2},{4,7},{5,4},{6,5},{7,6},{8,11},{9,8},{10,9... | collective-permute-start | bytes 1179656 | tf_op jit(solution)/shard_map/conv_reduce/ppermute | solution.py:51
  32.0 8.6 %collective-permute-done.7 = bf16[128,1536]{1,0:T(8,128)(2,1)S(1)} collective-permute-done((bf16[128,1536]{1,0:T(8,128)(2,1)S(1)}, bf16[128,1536]{1,0:T(8,128)(2,1)S(1)}, u32[]{:S(2)}, u32[]{:S(2)}) %collective-permute-start.7) | collective-permute-done | bytes 393248 | tf_op jit(solution)/shard_map/conv_reduce/ppermute | solution.py:51
  40.6 26.0 %collective-permute-done.6 = bf16[128,1536]{1,0:T(8,128)(2,1)S(1)} collective-permute-done((bf16[128,1536]{1,0:T(8,128)(2,1)S(1)}, bf16[128,1536]{1,0:T(8,128)(2,1)S(1)}, u32[]{:S(2)}, u32[]{:S(2)}) %collective-permute-start.6) | collective-permute-done | bytes 393248 | tf_op jit(solution)/shard_map/conv_reduce/ppermute | solution.py:51
  69.2 1.9 collective-permute-start.9
  71.0 2.9 %collective-permute-start.10 = (bf16[128,1536]{1,0:T(8,128)(2,1)S(1)}, bf16[128,1536]{1,0:T(8,128)(2,1)S(1)}, u32[]{:S(2)}, u32[]{:S(2)}) collective-permute-start(bf16[128,1536]{1,0:T(8,128)(2,1)S(1)} %get-tuple-element.13), channel_id=1, source_target_pairs={{0,3},{1,0},{2,1},{3,2},{4,7},{5,4},{6,5},{7,6},{8,11},{9,8},{10,9... | collective-permute-start | bytes 1179656 | tf_op jit(solution)/shard_map/attn_in_gather/ppermute | solution.py:127
  73.9 9.1 %collective-permute-done.8 = bf16[128,1536]{1,0:T(8,128)(2,1)S(1)} collective-permute-done((bf16[128,1536]{1,0:T(8,128)(2,1)S(1)}, bf16[128,1536]{1,0:T(8,128)(2,1)S(1)}, u32[]{:S(2)}, u32[]{:S(2)}) %collective-permute-start.8) | collective-permute-done | bytes 393248 | tf_op jit(solution)/shard_map/attn_in_gather/ppermute | solution.py:127
  83.8 15.1 %collective-permute-done.9 = bf16[128,1536]{1,0:T(8,128)(2,1)S(1)} collective-permute-done((bf16[128,1536]{1,0:T(8,128)(2,1)S(1)}, bf16[128,1536]{1,0:T(8,128)(2,1)S(1)}, u32[]{:S(2)}, u32[]{:S(2)}) %collective-permute-start.9) | collective-permute-done | bytes 393248 | tf_op jit(solution)/shard_map/attn_in_gather/ppermute | solution.py:127
  100.5 2.8 %convolution_convert_fusion = bf16[512,768]{1,0:T(8,128)(2,1)S(1)} fusion(bf16[512,1536]{1,0:T(8,128)(2,1)} %bitcast.22, bf16[1536,768]{1,0:T(8,128)(2,1)S(1)} %copy-done), kind=kOutput, calls=%fused_computation.30 | convolution fusion | flops 1208352768 | bytes 4718592 | tf_op jit(solution)/shard_map/dot_general | solution.py:164
  106.6 10.1 %collective-permute-start.17 = (bf16[256,768]{1,0:T(8,128)(2,1)}, bf16[256,768]{1,0:T(8,128)(2,1)}, u32[]{:S(2)}, u32[]{:S(2)}) collective-permute-start(bf16[256,768]{1,0:T(8,128)(2,1)} %get-tuple-element.5), channel_id=1, source_target_pairs={{0,1},{1,2},{2,3},{4,5},{5,6},{6,7},{8,9},{9,10},{10,11},{12,13},{... | collective-permute-start | bytes 1179656 | tf_op jit(solution)/shard_map/out_projection/ppermute | solution.py:80
  118.5 5.5 %collective-permute-done.17 = bf16[256,768]{1,0:T(8,128)(2,1)} collective-permute-done((bf16[256,768]{1,0:T(8,128)(2,1)}, bf16[256,768]{1,0:T(8,128)(2,1)}, u32[]{:S(2)}, u32[]{:S(2)}) %collective-permute-start.17) | collective-permute-done | bytes 393248 | tf_op jit(solution)/shard_map/out_projection/ppermute | solution.py:80
  124.1 4.4 %collective-permute-start.19 = (bf16[256,768]{1,0:T(8,128)(2,1)}, bf16[256,768]{1,0:T(8,128)(2,1)S(1)}, u32[]{:S(2)}, u32[]{:S(2)}) collective-permute-start(bf16[256,768]{1,0:T(8,128)(2,1)} %collective-permute-done.17), channel_id=1, source_target_pairs={{0,1},{1,2},{2,3},{4,5},{5,6},{6,7},{8,9},{9,10},{10,11},{12,13},{... | collective-permute-start | bytes 1179656 | tf_op jit(solution)/shard_map/out_projection/ppermute | solution.py:80
  130.2 1.8 bitcast_dynamic-update-slice_fusion.5
  132.0 1.8 bitcast_dynamic-update-slice_fusion.4
  135.7 4.3 %collective-permute-start.21 = (bf16[256,768]{1,0:T(8,128)(2,1)S(1)}, bf16[256,768]{1,0:T(8,128)(2,1)S(1)}, u32[]{:S(2)}, u32[]{:S(2)}) collective-permute-start(bf16[256,768]{1,0:T(8,128)(2,1)S(1)} %collective-permute-done.19), channel_id=1, source_target_pairs={{0,1},{1,2},{2,3},{4,5},{5,6},{6,7},{8,9},{9,10},{10,11},{12,13},{... | collective-permute-start | bytes 1179656 | tf_op jit(solution)/shard_map/out_projection/ppermute | solution.py:80
  143.5 3.3 %collective-permute-done.21 = bf16[256,768]{1,0:T(8,128)(2,1)S(1)} collective-permute-done((bf16[256,768]{1,0:T(8,128)(2,1)S(1)}, bf16[256,768]{1,0:T(8,128)(2,1)S(1)}, u32[]{:S(2)}, u32[]{:S(2)}) %collective-permute-start.21) | collective-permute-done | bytes 393248 | tf_op jit(solution)/shard_map/out_projection/ppermute | solution.py:80
  147.6 3.4 %collective-permute-done.22 = bf16[256,768]{1,0:T(8,128)(2,1)S(1)} collective-permute-done((bf16[256,768]{1,0:T(8,128)(2,1)S(1)}, bf16[256,768]{1,0:T(8,128)(2,1)S(1)}, u32[]{:S(2)}, u32[]{:S(2)}) %collective-permute-start.22) | collective-permute-done | bytes 393248 | tf_op jit(solution)/shard_map/out_projection/ppermute | solution.py:81
  151.7 2.7 %slice.98 = bf16[4,256,768]{2,1,0:T(8,128)(2,1)} slice(bf16[5,256,768]{2,1,0:T(8,128)(2,1)} %bitcast_dynamic-update-slice_fusion), slice={[0:4], [0:256], [0:768]} | slice | bytes 3145728 | tf_op jit(solution)/shard_map/out_projection/slice | solution.py:86
  160.3 1.7 collective-permute-start.15
  162.1 2.4 %collective-permute-start.16 = (bf16[128,256]{1,0:T(8,128)(2,1)S(1)}, bf16[128,256]{1,0:T(8,128)(2,1)S(1)}, u32[]{:S(2)}, u32[]{:S(2)}) collective-permute-start(bf16[128,256]{1,0:T(8,128)(2,1)S(1)} %get-tuple-element.25), channel_id=1, source_target_pairs={{0,3},{1,0},{2,1},{3,2},{4,7},{5,4},{6,5},{7,6},{8,11},{9,8},{10,9... | collective-permute-start | bytes 196616 | tf_op jit(solution)/shard_map/out_projection/ppermute | solution.py:98
  164.5 2.2 %collective-permute-done.14 = bf16[128,256]{1,0:T(8,128)(2,1)S(1)} collective-permute-done((bf16[128,256]{1,0:T(8,128)(2,1)S(1)}, bf16[128,256]{1,0:T(8,128)(2,1)S(1)}, u32[]{:S(2)}, u32[]{:S(2)}) %collective-permute-start.14) | collective-permute-done | bytes 65568 | tf_op jit(solution)/shard_map/out_projection/ppermute | solution.py:98
  166.8 2.1 %collective-permute-done.15 = bf16[128,256]{1,0:T(8,128)(2,1)S(1)} collective-permute-done((bf16[128,256]{1,0:T(8,128)(2,1)S(1)}, bf16[128,256]{1,0:T(8,128)(2,1)S(1)}, u32[]{:S(2)}, u32[]{:S(2)}) %collective-permute-start.15) | collective-permute-done | bytes 65568 | tf_op jit(solution)/shard_map/out_projection/ppermute | solution.py:98
  169.3 5.0 %convert_reduce_fusion = (f32[8,1536]{1,0:T(8,128)S(1)}, bf16[128,1536]{1,0:T(8,128)(2,1)}) fusion(bf16[128,1024]{0,1:T(8,128)(2,1)S(1)} %bitcast.232, bf16[1024,768]{1,0:T(8,128)(2,1)} %collective-permute-done.23, bf16[1024,768]{1,0:T(8,128)(2,1)} %bitcast.51, pred[]{:T(512)S(6)} %eq.29, bf16[128,1536]{1,0:T(8,128)(2,1)S(1)} %get-tuple-element.15), kind=kOutput, calls=%fused_computation.85 | convolution fusion | flops 417779712 | bytes 4243457 | tf_op jit(solution)/shard_map/out_projection/dot_general | solution.py:213
  176.0 1.5 collective-permute-start.25
  178.6 1.6 collective-permute-done.24
  181.1 2.9 %collective-permute-start.28 = (bf16[32,256]{1,0:T(8,128)(2,1)S(1)}, bf16[32,256]{1,0:T(8,128)(2,1)S(1)}, u32[]{:S(2)}, u32[]{:S(2)}) collective-permute-start(bf16[32,256]{1,0:T(8,128)(2,1)S(1)} %bitcast.241), channel_id=1, source_target_pairs={{0,8},{4,12},{8,0},{12,4},{1,9},{5,13},{9,1},{13,5},{2,10},{6,14},... | collective-permute-start | bytes 49160 | tf_op jit(solution)/shard_map/sides_gather/ppermute | solution.py:127
  (125 shorter events, 42.9 us)
Async XLA Ops:
  0.6 99.9 %copy-start = (bf16[1536,768]{1,0:T(8,128)(2,1)S(1)}, bf16[1536,768]{1,0:T(8,128)(2,1)}, u32[]{:S(2)}) copy-start(bf16[1536,768]{1,0:T(8,128)(2,1)} %param.14) | copy-start | bytes 7077892
  4.1 8.7 %collective-permute-start = (bf16[128,384]{1,0:T(8,128)(2,1)S(1)}, bf16[128,384]{1,0:T(8,128)(2,1)S(1)}, u32[]{:S(2)}, u32[]{:S(2)}) collective-permute-start(bf16[128,384]{1,0:T(8,128)(2,1)S(1)} %bitcast.236), channel_id=1, source_target_pairs={{0,1},{1,2},{2,3},{3,0},{4,5},{5,6},{6,7},{7,4},{8,9},{9,10},{10,1... | collective-permute-start | bytes 294920 | tf_op jit(solution)/shard_map/ppermute | solution.py:65
  7.2 9.2 %collective-permute-start.1 = (bf16[128,384]{1,0:T(8,128)(2,1)S(1)}, bf16[128,384]{1,0:T(8,128)(2,1)S(1)}, u32[]{:S(2)}, u32[]{:S(2)}) collective-permute-start(bf16[128,384]{1,0:T(8,128)(2,1)S(1)} %bitcast.235), channel_id=1, source_target_pairs={{0,2},{1,3},{2,0},{3,1},{4,6},{5,7},{6,4},{7,5},{8,10},{9,11},{10,... | collective-permute-start | bytes 294920 | tf_op jit(solution)/shard_map/ppermute | solution.py:65
  9.9 6.7 %collective-permute-start.2 = (bf16[128,384]{1,0:T(8,128)(2,1)S(1)}, bf16[128,384]{1,0:T(8,128)(2,1)S(1)}, u32[]{:S(2)}, u32[]{:S(2)}) collective-permute-start(bf16[128,384]{1,0:T(8,128)(2,1)S(1)} %bitcast.234), channel_id=1, source_target_pairs={{0,3},{1,0},{2,1},{3,2},{4,7},{5,4},{6,5},{7,6},{8,11},{9,8},{10,9... | collective-permute-start | bytes 294920 | tf_op jit(solution)/shard_map/ppermute | solution.py:65
  16.6 6.9 %collective-permute-start.4 = (bf16[8,384]{1,0:T(8,128)(2,1)S(1)}, bf16[8,384]{1,0:T(8,128)(2,1)S(1)}, u32[]{:S(2)}, u32[]{:S(2)}) collective-permute-start(bf16[8,384]{1,0:T(8,128)(2,1)S(1)} %get-tuple-element.20), channel_id=1, source_target_pairs={{4,0},{8,4},{12,8},{5,1},{9,5},{13,9},{6,2},{10,6},{14,10},{7,3},{... | collective-permute-start | bytes 18440 | tf_op jit(solution)/shard_map/ppermute | solution.py:26
  20.6 4.9 %collective-permute-start.3 = (bf16[8,384]{1,0:T(8,128)(2,1)S(1)}, bf16[8,384]{1,0:T(8,128)(2,1)S(1)}, u32[]{:S(2)}, u32[]{:S(2)}) collective-permute-start(bf16[8,384]{1,0:T(8,128)(2,1)S(1)} %get-tuple-element.19), channel_id=1, source_target_pairs={{0,4},{4,8},{8,12},{1,5},{5,9},{9,13},{2,6},{6,10},{10,14},{3,7},{... | collective-permute-start | bytes 18440 | tf_op jit(solution)/shard_map/ppermute | solution.py:25
  27.6 39.0 %copy-start.2 = (bf16[128,1536]{1,0:T(8,128)(2,1)S(1)}, bf16[128,1536]{1,0:T(8,128)(2,1)}, u32[]{:S(2)}) copy-start(bf16[128,1536]{1,0:T(8,128)(2,1)} %param.10) | copy-start | bytes 1179652
  27.8 12.8 %collective-permute-start.7 = (bf16[128,1536]{1,0:T(8,128)(2,1)S(1)}, bf16[128,1536]{1,0:T(8,128)(2,1)S(1)}, u32[]{:S(2)}, u32[]{:S(2)}) collective-permute-start(bf16[128,1536]{1,0:T(8,128)(2,1)S(1)} %get-tuple-element.17), channel_id=1, source_target_pairs={{0,3},{1,0},{2,1},{3,2},{4,7},{5,4},{6,5},{7,6},{8,11},{9,8},{10,9... | collective-permute-start | bytes 1179656 | tf_op jit(solution)/shard_map/conv_reduce/ppermute | solution.py:51
  31.3 35.2 %collective-permute-start.6 = (bf16[128,1536]{1,0:T(8,128)(2,1)S(1)}, bf16[128,1536]{1,0:T(8,128)(2,1)S(1)}, u32[]{:S(2)}, u32[]{:S(2)}) collective-permute-start(bf16[128,1536]{1,0:T(8,128)(2,1)S(1)} %get-tuple-element.18), channel_id=1, source_target_pairs={{0,2},{1,3},{2,0},{3,1},{4,6},{5,7},{6,4},{7,5},{8,10},{9,11},{10,... | collective-permute-start | bytes 1179656 | tf_op jit(solution)/shard_map/conv_reduce/ppermute | solution.py:51
  31.7 34.9 %collective-permute-start.5 = (bf16[128,1536]{1,0:T(8,128)(2,1)S(1)}, bf16[128,1536]{1,0:T(8,128)(2,1)S(1)}, u32[]{:S(2)}, u32[]{:S(2)}) collective-permute-start(bf16[128,1536]{1,0:T(8,128)(2,1)S(1)} %get-tuple-element.16), channel_id=1, source_target_pairs={{0,1},{1,2},{2,3},{3,0},{4,5},{5,6},{6,7},{7,4},{8,9},{9,10},{10,1... | collective-permute-start | bytes 1179656 | tf_op jit(solution)/shard_map/conv_reduce/ppermute | solution.py:51
  69.2 13.9 %collective-permute-start.8 = (bf16[128,1536]{1,0:T(8,128)(2,1)S(1)}, bf16[128,1536]{1,0:T(8,128)(2,1)S(1)}, u32[]{:S(2)}, u32[]{:S(2)}) collective-permute-start(bf16[128,1536]{1,0:T(8,128)(2,1)S(1)} %get-tuple-element.13), channel_id=1, source_target_pairs={{0,1},{1,2},{2,3},{3,0},{4,5},{5,6},{6,7},{7,4},{8,9},{9,10},{10,1... | collective-permute-start | bytes 1179656 | tf_op jit(solution)/shard_map/attn_in_gather/ppermute | solution.py:127
  69.2 29.8 %collective-permute-start.9 = (bf16[128,1536]{1,0:T(8,128)(2,1)S(1)}, bf16[128,1536]{1,0:T(8,128)(2,1)S(1)}, u32[]{:S(2)}, u32[]{:S(2)}) collective-permute-start(bf16[128,1536]{1,0:T(8,128)(2,1)S(1)} %get-tuple-element.13), channel_id=1, source_target_pairs={{0,2},{1,3},{2,0},{3,1},{4,6},{5,7},{6,4},{7,5},{8,10},{9,11},{10,... | collective-permute-start | bytes 1179656 | tf_op jit(solution)/shard_map/attn_in_gather/ppermute | solution.py:127
  71.0 28.7 %collective-permute-start.10 = (bf16[128,1536]{1,0:T(8,128)(2,1)S(1)}, bf16[128,1536]{1,0:T(8,128)(2,1)S(1)}, u32[]{:S(2)}, u32[]{:S(2)}) collective-permute-start(bf16[128,1536]{1,0:T(8,128)(2,1)S(1)} %get-tuple-element.13), channel_id=1, source_target_pairs={{0,3},{1,0},{2,1},{3,2},{4,7},{5,4},{6,5},{7,6},{8,11},{9,8},{10,9... | collective-permute-start | bytes 1179656 | tf_op jit(solution)/shard_map/attn_in_gather/ppermute | solution.py:127
  106.6 17.5 %collective-permute-start.17 = (bf16[256,768]{1,0:T(8,128)(2,1)}, bf16[256,768]{1,0:T(8,128)(2,1)}, u32[]{:S(2)}, u32[]{:S(2)}) collective-permute-start(bf16[256,768]{1,0:T(8,128)(2,1)} %get-tuple-element.5), channel_id=1, source_target_pairs={{0,1},{1,2},{2,3},{4,5},{5,6},{6,7},{8,9},{9,10},{10,11},{12,13},{... | collective-permute-start | bytes 1179656 | tf_op jit(solution)/shard_map/out_projection/ppermute | solution.py:80
  116.7 12.3 %collective-permute-start.18 = (bf16[256,768]{1,0:T(8,128)(2,1)}, bf16[256,768]{1,0:T(8,128)(2,1)}, u32[]{:S(2)}, u32[]{:S(2)}) collective-permute-start(bf16[256,768]{1,0:T(8,128)(2,1)} %get-tuple-element.5), channel_id=1, source_target_pairs={{1,0},{2,1},{3,2},{5,4},{6,5},{7,6},{9,8},{10,9},{11,10},{13,12},{... | collective-permute-start | bytes 1179656 | tf_op jit(solution)/shard_map/out_projection/ppermute | solution.py:81
  118.0 15.8 %collective-permute-start.11 = (bf16[2,512,256]{2,1,0:T(8,128)(2,1)}, bf16[2,512,256]{2,1,0:T(8,128)(2,1)S(1)}, u32[]{:S(2)}, u32[]{:S(2)}) collective-permute-start(bf16[2,512,256]{2,1,0:T(8,128)(2,1)} %slice.91), channel_id=1, source_target_pairs={{0,4},{4,8},{8,12},{12,0},{1,5},{5,9},{9,13},{13,1},{2,6},{6,10},{... | collective-permute-start | bytes 1572872 | tf_op jit(solution)/shard_map/kv_ring/ppermute | solution.py:202
  124.1 11.6 %collective-permute-start.19 = (bf16[256,768]{1,0:T(8,128)(2,1)}, bf16[256,768]{1,0:T(8,128)(2,1)S(1)}, u32[]{:S(2)}, u32[]{:S(2)}) collective-permute-start(bf16[256,768]{1,0:T(8,128)(2,1)} %collective-permute-done.17), channel_id=1, source_target_pairs={{0,1},{1,2},{2,3},{4,5},{5,6},{6,7},{8,9},{9,10},{10,11},{12,13},{... | collective-permute-start | bytes 1179656 | tf_op jit(solution)/shard_map/out_projection/ppermute | solution.py:80
  128.9 11.2 %collective-permute-start.20 = (bf16[256,768]{1,0:T(8,128)(2,1)}, bf16[256,768]{1,0:T(8,128)(2,1)S(1)}, u32[]{:S(2)}, u32[]{:S(2)}) collective-permute-start(bf16[256,768]{1,0:T(8,128)(2,1)} %collective-permute-done.18), channel_id=1, source_target_pairs={{1,0},{2,1},{3,2},{5,4},{6,5},{7,6},{9,8},{10,9},{11,10},{13,12},{... | collective-permute-start | bytes 1179656 | tf_op jit(solution)/shard_map/out_projection/ppermute | solution.py:81
  133.8 9.3 %collective-permute-start.12 = (bf16[2,512,256]{2,1,0:T(8,128)(2,1)S(1)}, bf16[2,512,256]{2,1,0:T(8,128)(2,1)S(1)}, u32[]{:S(2)}, u32[]{:S(2)}) collective-permute-start(bf16[2,512,256]{2,1,0:T(8,128)(2,1)S(1)} %collective-permute-done.11), channel_id=1, source_target_pairs={{0,4},{4,8},{8,12},{12,0},{1,5},{5,9},{9,13},{13,1},{2,6},{6,10},{... | collective-permute-start | bytes 1572872 | tf_op jit(solution)/shard_map/kv_ring/ppermute | solution.py:202
  135.7 11.1 %collective-permute-start.21 = (bf16[256,768]{1,0:T(8,128)(2,1)S(1)}, bf16[256,768]{1,0:T(8,128)(2,1)S(1)}, u32[]{:S(2)}, u32[]{:S(2)}) collective-permute-start(bf16[256,768]{1,0:T(8,128)(2,1)S(1)} %collective-permute-done.19), channel_id=1, source_target_pairs={{0,1},{1,2},{2,3},{4,5},{5,6},{6,7},{8,9},{9,10},{10,11},{12,13},{... | collective-permute-start | bytes 1179656 | tf_op jit(solution)/shard_map/out_projection/ppermute | solution.py:80
  140.2 10.8 %collective-permute-start.22 = (bf16[256,768]{1,0:T(8,128)(2,1)S(1)}, bf16[256,768]{1,0:T(8,128)(2,1)S(1)}, u32[]{:S(2)}, u32[]{:S(2)}) collective-permute-start(bf16[256,768]{1,0:T(8,128)(2,1)S(1)} %collective-permute-done.20), channel_id=1, source_target_pairs={{1,0},{2,1},{3,2},{5,4},{6,5},{7,6},{9,8},{10,9},{11,10},{13,12},{... | collective-permute-start | bytes 1179656 | tf_op jit(solution)/shard_map/out_projection/ppermute | solution.py:81
  143.1 11.3 %collective-permute-start.13 = (bf16[2,512,256]{2,1,0:T(8,128)(2,1)S(1)}, bf16[2,512,256]{2,1,0:T(8,128)(2,1)S(1)}, u32[]{:S(2)}, u32[]{:S(2)}) collective-permute-start(bf16[2,512,256]{2,1,0:T(8,128)(2,1)S(1)} %collective-permute-done.12), channel_id=1, source_target_pairs={{0,4},{4,8},{8,12},{12,0},{1,5},{5,9},{9,13},{13,1},{2,6},{6,10},{... | collective-permute-start | bytes 1572872 | tf_op jit(solution)/shard_map/kv_ring/ppermute | solution.py:202
  154.4 14.8 %collective-permute-start.23 = (bf16[1024,768]{1,0:T(8,128)(2,1)}, bf16[1024,768]{1,0:T(8,128)(2,1)}, u32[]{:S(2)}, u32[]{:S(2)}) collective-permute-start(bf16[1024,768]{1,0:T(8,128)(2,1)} %bitcast.51), channel_id=1, source_target_pairs={{0,4},{4,0},{8,12},{12,8},{1,5},{5,1},{9,13},{13,9},{2,6},{6,2},{1... | collective-permute-start | bytes 4718600 | tf_op jit(solution)/shard_map/out_projection/ppermute | solution.py:111
  159.9 6.8 %collective-permute-start.14 = (bf16[128,256]{1,0:T(8,128)(2,1)S(1)}, bf16[128,256]{1,0:T(8,128)(2,1)S(1)}, u32[]{:S(2)}, u32[]{:S(2)}) collective-permute-start(bf16[128,256]{1,0:T(8,128)(2,1)S(1)} %get-tuple-element.27), channel_id=1, source_target_pairs={{0,1},{1,2},{2,3},{3,0},{4,5},{5,6},{6,7},{7,4},{8,9},{9,10},{10,1... | collective-permute-start | bytes 196616 | tf_op jit(solution)/shard_map/out_projection/ppermute | solution.py:98
  160.3 8.6 %collective-permute-start.15 = (bf16[128,256]{1,0:T(8,128)(2,1)S(1)}, bf16[128,256]{1,0:T(8,128)(2,1)S(1)}, u32[]{:S(2)}, u32[]{:S(2)}) collective-permute-start(bf16[128,256]{1,0:T(8,128)(2,1)S(1)} %get-tuple-element.26), channel_id=1, source_target_pairs={{0,2},{1,3},{2,0},{3,1},{4,6},{5,7},{6,4},{7,5},{8,10},{9,11},{10,... | collective-permute-start | bytes 196616 | tf_op jit(solution)/shard_map/out_projection/ppermute | solution.py:98
  162.1 6.9 %collective-permute-start.16 = (bf16[128,256]{1,0:T(8,128)(2,1)S(1)}, bf16[128,256]{1,0:T(8,128)(2,1)S(1)}, u32[]{:S(2)}, u32[]{:S(2)}) collective-permute-start(bf16[128,256]{1,0:T(8,128)(2,1)S(1)} %get-tuple-element.25), channel_id=1, source_target_pairs={{0,3},{1,0},{2,1},{3,2},{4,7},{5,4},{6,5},{7,6},{8,11},{9,8},{10,9... | collective-permute-start | bytes 196616 | tf_op jit(solution)/shard_map/out_projection/ppermute | solution.py:98
  174.7 5.4 %collective-permute-start.24 = (bf16[8,256]{1,0:T(8,128)(2,1)S(1)}, bf16[8,256]{1,0:T(8,128)(2,1)S(1)}, u32[]{:S(2)}, u32[]{:S(2)}) collective-permute-start(bf16[8,256]{1,0:T(8,128)(2,1)S(1)} %get-tuple-element.45), channel_id=1, source_target_pairs={{0,1},{1,2},{2,3},{3,0},{4,5},{5,6},{6,7},{7,4},{8,9},{9,10},{10,1... | collective-permute-start | bytes 12296 | tf_op jit(solution)/shard_map/sides_gather/ppermute | solution.py:127
  176.0 4.5 %collective-permute-start.25 = (bf16[8,256]{1,0:T(8,128)(2,1)S(1)}, bf16[8,256]{1,0:T(8,128)(2,1)S(1)}, u32[]{:S(2)}, u32[]{:S(2)}) collective-permute-start(bf16[8,256]{1,0:T(8,128)(2,1)S(1)} %get-tuple-element.45), channel_id=1, source_target_pairs={{0,2},{1,3},{2,0},{3,1},{4,6},{5,7},{6,4},{7,5},{8,10},{9,11},{10,... | collective-permute-start | bytes 12296 | tf_op jit(solution)/shard_map/sides_gather/ppermute | solution.py:127
  177.5 3.6 %collective-permute-start.26 = (bf16[8,256]{1,0:T(8,128)(2,1)S(1)}, bf16[8,256]{1,0:T(8,128)(2,1)S(1)}, u32[]{:S(2)}, u32[]{:S(2)}) collective-permute-start(bf16[8,256]{1,0:T(8,128)(2,1)S(1)} %get-tuple-element.45), channel_id=1, source_target_pairs={{0,3},{1,0},{2,1},{3,2},{4,7},{5,4},{6,5},{7,6},{8,11},{9,8},{10,9... | collective-permute-start | bytes 12296 | tf_op jit(solution)/shard_map/sides_gather/ppermute | solution.py:127
  181.1 4.3 %collective-permute-start.27 = (bf16[32,256]{1,0:T(8,128)(2,1)S(1)}, bf16[32,256]{1,0:T(8,128)(2,1)S(1)}, u32[]{:S(2)}, u32[]{:S(2)}) collective-permute-start(bf16[32,256]{1,0:T(8,128)(2,1)S(1)} %bitcast.240), channel_id=1, source_target_pairs={{0,4},{4,8},{8,12},{12,0},{1,5},{5,9},{9,13},{13,1},{2,6},{6,10},{... | collective-permute-start | bytes 49160 | tf_op jit(solution)/shard_map/sides_gather/ppermute | solution.py:127
  181.1 4.6 %collective-permute-start.28 = (bf16[32,256]{1,0:T(8,128)(2,1)S(1)}, bf16[32,256]{1,0:T(8,128)(2,1)S(1)}, u32[]{:S(2)}, u32[]{:S(2)}) collective-permute-start(bf16[32,256]{1,0:T(8,128)(2,1)S(1)} %bitcast.241), channel_id=1, source_target_pairs={{0,8},{4,12},{8,0},{12,4},{1,9},{5,13},{9,1},{13,5},{2,10},{6,14},... | collective-permute-start | bytes 49160 | tf_op jit(solution)/shard_map/sides_gather/ppermute | solution.py:127
  184.0 2.9 %collective-permute-start.29 = (bf16[32,256]{1,0:T(8,128)(2,1)S(1)}, bf16[32,256]{1,0:T(8,128)(2,1)S(1)}, u32[]{:S(2)}, u32[]{:S(2)}) collective-permute-start(bf16[32,256]{1,0:T(8,128)(2,1)S(1)} %bitcast.242), channel_id=1, source_target_pairs={{0,12},{4,0},{8,4},{12,8},{1,13},{5,1},{9,5},{13,9},{2,14},{6,2},{... | collective-permute-start | bytes 49160 | tf_op jit(solution)/shard_map/sides_gather/ppermute | solution.py:127
  (7 other events, 91.7 us)

commit v5 on v4

--- a/solution.py
+++ b/solution.py
@@ -107,7 +107,7 @@
     core = lax.axis_index(chip_axis) % 2
     half = weight.shape[1] // 2
     mine = lax.dynamic_slice_in_dim(weight, core * half, half, 1)
-    gathered = line_all_gather(mine, axis)
+    gathered = direct_all_gather(mine, axis)
     other = lax.ppermute(gathered, chip_axis, [(i, i ^ 1) for i in range(peers)])
     return jnp.where(
         core == 0,
@@ -155,8 +155,13 @@
     normed = norm_rows(inputs, gain_conv).astype(jnp.bfloat16)
     swapped = permute_all_to_all(normed, "pair")
     padded = padded_2(swapped, (("seq", 0),), DILATION * (conv_weight.shape[0] - 1) // 2)
+    early_w_out = pair_count <= 4
     with jax.named_scope("conv_reduce"):
-        summed = direct_reduce_scatter(conv_rows(padded, conv_weight, local_rows), "pair")
+        conv_partial = conv_rows(padded, conv_weight, local_rows)
+        if early_w_out:
+            full_w_out = gather_weight_rows(w_out, "pair", "seq")
+            conv_partial, full_w_out = lax.optimization_barrier((conv_partial, full_w_out))
+        summed = direct_reduce_scatter(conv_partial, "pair")
     first_out = (inputs + summed).astype(jnp.bfloat16)
     attn_in = norm_rows(first_out.astype(jnp.float32), gain_attn).astype(jnp.bfloat16)
     with jax.named_scope("attn_in_gather"):
@@ -207,8 +212,9 @@
     attended = (weighted / running_sum[:, :, None]).astype(jnp.bfloat16)
     attended = attended.transpose(1, 0, 2).reshape(local_rows, head_count * VALUE_SIZE)
     with jax.named_scope("out_projection"):
-        late_w_out, unused = lax.optimization_barrier((w_out, kv))
-        full_w_out = gather_weight_rows(late_w_out, "pair", "seq")
+        if not early_w_out:
+            late_w_out, unused = lax.optimization_barrier((w_out, kv))
+            full_w_out = gather_weight_rows(late_w_out, "pair", "seq")
         own_heads = rows_to_heads(attended, "pair")
         mixed = jnp.dot(own_heads, full_w_out, preferred_element_type=jnp.float32)
     seq_out = (first_out.astype(jnp.float32) + mixed).astype(jnp.bfloat16)

time: 189 us -> 208 us (1.10)
  waiting for transfers between devices: 86.5 us -> 128 us
  starting transfers between devices: 56 us -> 40.8 us
  local copies, waits for them, and re-layouts: 18.6 us -> 12.7 us
    ppermute x3, waiting for transfers between devices: 5.16 us -> 37.8 us  [permute_all_to_all(): lax.ppermute(outgoing, axis, [(i, (i + shift) % n) for i in range(n)])]
    ppermute x3, waiting for transfers between devices: 0.01 us -> 24.4 us  [shards(): arriving = lax.ppermute(current, 'seq', ring)]
    ppermute x6 -> x0, starting transfers between devices: 22.6 us -> none  [the longest x3 18.8 us: line_all_gather(): flow_r = lax.ppermute(flow_r, axis, right)]
    ppermute x6 -> x0, waiting for transfers between devices: 14.3 us -> none  [the longest x3 10.3 us: line_all_gather(): flow_r = lax.ppermute(flow_r, axis, right)]
    dynamic_update_slice x7 -> x0, local copies, waits for them, and re-layouts: 7.62 us -> none  [the longest x3 3.38 us: line_all_gather(): slots = lax.dynamic_update_index_in_dim(slots, flow_r, at_r, 0)]
    ppermute x3, starting transfers between devices: 7.13 us -> 1.03 us  [permute_all_to_all(): lax.ppermute(outgoing, axis, [(i, (i + shift) % n) for i in range(n)])]
    ppermute x3, starting transfers between devices: 4.58 us -> 10.4 us  [rows_to_heads(): lax.ppermute(outgoing, axis, [(i, (i + shift) % n) for i in range(n)])]
    ppermute x9 -> x12, starting transfers between devices: 12.9 us -> 17.8 us  [direct_all_gather(): lax.ppermute(value, axis, [(i, (i + shift) % n) for i in range(n)])]
  transfers between devices with their start and end apart: 30 -> 27, of which waited for: 20 -> 17; matrix products, arithmetic and copies ran while one was open for 12% -> 8% of each run, Pallas kernels for 0% -> 0%
where the time goes in v5:
time: 208 us; the launch traced here: 207 us
  waiting for transfers between devices  128 us (62%)
  starting transfers between devices  40.8 us (20%)
  matrix products  18.7 us (9%)
  local copies, waits for them, and re-layouts  12.7 us (6%)
  other arithmetic  6.36 us (3%)
    ppermute x3, waiting for transfers between devices, permute_all_to_all(): lax.ppermute(outgoing, axis, [(i, (i + shift) % n) for i in range(n)])  37.8 us
    ppermute x3, waiting for transfers between devices, direct_reduce_scatter(): lax.ppermute(outgoing, axis, [(i, (i + shift) % n) for i in range(n)])  32.5 us
    ppermute x12, waiting for transfers between devices, direct_all_gather(): lax.ppermute(value, axis, [(i, (i + shift) % n) for i in range(n)])  28.6 us
    ppermute x3, waiting for transfers between devices, shards(): arriving = lax.ppermute(current, 'seq', ring)  24.4 us
    ppermute x12, starting transfers between devices, direct_all_gather(): lax.ppermute(value, axis, [(i, (i + shift) % n) for i in range(n)])  17.8 us
    ppermute x3, starting transfers between devices, rows_to_heads(): lax.ppermute(outgoing, axis, [(i, (i + shift) % n) for i in range(n)])  10.4 us
    dot_general x5, matrix products, conv_rows(): jnp.dot(shifted, conv_weight[offset], preferred_element_type=jnp.float32)  7.74 us
    ppermute x3, starting transfers between devices, direct_reduce_scatter(): lax.ppermute(outgoing, axis, [(i, (i + shift) % n) for i in range(n)])  5.92 us
  transfers between devices with their start and end apart: 27, of which 17 were waited for; matrix products, arithmetic and copies ran while one was open for 8% of the time, Pallas kernels for 0%

profile of v5, /device:TPU:0, one launch (start us, length us, event | category | flops | bytes accessed | tf_op | source)
XLA Modules:
  0.0 207.2 jit_solution(1486017764207693956)
XLA Ops:
  1.9 2.0 bitcast_dynamic-update-slice_fusion.7
  4.0 3.0 %collective-permute-start.5 = (bf16[256,768]{1,0:T(8,128)(2,1)}, bf16[256,768]{1,0:T(8,128)(2,1)}, u32[]{:S(2)}, u32[]{:S(2)}) collective-permute-start(bf16[256,768]{1,0:T(8,128)(2,1)} %get-tuple-element.17), channel_id=1, source_target_pairs={{0,1},{1,2},{2,3},{3,0},{4,5},{5,6},{6,7},{7,4},{8,9},{9,10},{10,1... | collective-permute-start | bytes 1179656 | tf_op jit(solution)/shard_map/conv_reduce/ppermute | solution.py:127
  7.0 2.6 %collective-permute-start.6 = (bf16[256,768]{1,0:T(8,128)(2,1)}, bf16[256,768]{1,0:T(8,128)(2,1)}, u32[]{:S(2)}, u32[]{:S(2)}) collective-permute-start(bf16[256,768]{1,0:T(8,128)(2,1)} %get-tuple-element.17), channel_id=1, source_target_pairs={{0,2},{1,3},{2,0},{3,1},{4,6},{5,7},{6,4},{7,5},{8,10},{9,11},{10,... | collective-permute-start | bytes 1179656 | tf_op jit(solution)/shard_map/conv_reduce/ppermute | solution.py:127
  14.7 23.7 %collective-permute-done = bf16[128,384]{1,0:T(8,128)(2,1)S(1)} collective-permute-done((bf16[128,384]{1,0:T(8,128)(2,1)}, bf16[128,384]{1,0:T(8,128)(2,1)S(1)}, u32[]{:S(2)}, u32[]{:S(2)}) %collective-permute-start) | collective-permute-done | bytes 98336 | tf_op jit(solution)/shard_map/ppermute | solution.py:65
  38.3 11.7 %collective-permute-done.1 = bf16[128,384]{1,0:T(8,128)(2,1)S(1)} collective-permute-done((bf16[128,384]{1,0:T(8,128)(2,1)}, bf16[128,384]{1,0:T(8,128)(2,1)S(1)}, u32[]{:S(2)}, u32[]{:S(2)}) %collective-permute-start.1) | collective-permute-done | bytes 98336 | tf_op jit(solution)/shard_map/ppermute | solution.py:65
  50.1 2.4 %collective-permute-done.2 = bf16[128,384]{1,0:T(8,128)(2,1)S(1)} collective-permute-done((bf16[128,384]{1,0:T(8,128)(2,1)S(1)}, bf16[128,384]{1,0:T(8,128)(2,1)S(1)}, u32[]{:S(2)}, u32[]{:S(2)}) %collective-permute-start.2) | collective-permute-done | bytes 98336 | tf_op jit(solution)/shard_map/ppermute | solution.py:65
  53.8 2.4 %fusion.29 = f32[512,1536]{1,0:T(8,128)S(1)} fusion(bf16[512,384]{1,0:T(8,128)(2,1)S(1)} %bitcast.212, bf16[5,384,1536]{2,1,0:T(8,128)(2,1)} %param.12), kind=kOutput, calls=%fused_computation.51 | convolution fusion | flops 603979776 | bytes 4718592 | tf_op jit(solution)/shard_map/conv_reduce/dot_general | solution.py:39
  56.2 3.0 %collective-permute-start.3 = (bf16[8,384]{1,0:T(8,128)(2,1)S(1)}, bf16[8,384]{1,0:T(8,128)(2,1)S(1)}, u32[]{:S(2)}, u32[]{:S(2)}) collective-permute-start(bf16[8,384]{1,0:T(8,128)(2,1)S(1)} %get-tuple-element.21), channel_id=1, source_target_pairs={{0,4},{4,8},{8,12},{1,5},{5,9},{9,13},{2,6},{6,10},{10,14},{3,7},{... | collective-permute-start | bytes 18440 | tf_op jit(solution)/shard_map/ppermute | solution.py:25
  59.3 1.8 bitcast_dynamic-update-slice_fusion.6
  61.1 1.9 bitcast_dynamic-update-slice_fusion.5
  63.0 1.8 bitcast_dynamic-update-slice_fusion.4
  65.9 2.2 %fusion.25 = f32[512,1536]{1,0:T(8,128)S(1)} fusion(bf16[5,384,1536]{2,1,0:T(8,128)(2,1)} %param.12, bf16[8,384]{1,0:T(8,128)(2,1)S(1)} %collective-permute-done.4, bf16[512,384]{1,0:T(8,128)(2,1)S(1)} %bitcast.213), kind=kOutput, calls=%fused_computation.47 | convolution fusion | flops 604766208 | bytes 4724736 | tf_op jit(solution)/shard_map/conv_reduce/dot_general | solution.py:39
  71.3 3.8 %maximum_select_fusion = bf16[1024,1536]{1,0:T(8,128)(2,1)} fusion(bf16[1024,768]{1,0:T(8,128)(2,1)S(1)} %collective-permute-done.8, bf16[1024,768]{1,0:T(8,128)(2,1)} %bitcast.17, pred[]{:T(512)S(6)} %eq.32), kind=kLoop, calls=%fused_computation.4 | loop fusion | flops 14155776 | bytes 6291457 | tf_op jit(solution)/shard_map/conv_reduce/jit(_where)/select_n | solution.py:112
  75.3 2.9 %collective-permute-start.11 = (bf16[128,1536]{1,0:T(8,128)(2,1)S(1)}, bf16[128,1536]{1,0:T(8,128)(2,1)S(1)}, u32[]{:S(2)}, u32[]{:S(2)}) collective-permute-start(bf16[128,1536]{1,0:T(8,128)(2,1)S(1)} %get-tuple-element.19), channel_id=1, source_target_pairs={{0,3},{1,0},{2,1},{3,2},{4,7},{5,4},{6,5},{7,6},{8,11},{9,8},{10,9... | collective-permute-start | bytes 1179656 | tf_op jit(solution)/shard_map/conv_reduce/ppermute | solution.py:51
  79.3 1.9 collective-permute-start.9
  81.2 6.6 %collective-permute-done.11 = bf16[128,1536]{1,0:T(8,128)(2,1)S(1)} collective-permute-done((bf16[128,1536]{1,0:T(8,128)(2,1)S(1)}, bf16[128,1536]{1,0:T(8,128)(2,1)S(1)}, u32[]{:S(2)}, u32[]{:S(2)}) %collective-permute-start.11) | collective-permute-done | bytes 393248 | tf_op jit(solution)/shard_map/conv_reduce/ppermute | solution.py:51
  87.8 25.9 %collective-permute-done.10 = bf16[128,1536]{1,0:T(8,128)(2,1)S(1)} collective-permute-done((bf16[128,1536]{1,0:T(8,128)(2,1)S(1)}, bf16[128,1536]{1,0:T(8,128)(2,1)S(1)}, u32[]{:S(2)}, u32[]{:S(2)}) %collective-permute-start.10) | collective-permute-done | bytes 393248 | tf_op jit(solution)/shard_map/conv_reduce/ppermute | solution.py:51
  114.5 1.8 collective-permute-start.13
  116.3 2.8 %collective-permute-start.14 = (bf16[128,1536]{1,0:T(8,128)(2,1)S(1)}, bf16[128,1536]{1,0:T(8,128)(2,1)S(1)}, u32[]{:S(2)}, u32[]{:S(2)}) collective-permute-start(bf16[128,1536]{1,0:T(8,128)(2,1)S(1)} %get-tuple-element.13), channel_id=1, source_target_pairs={{0,3},{1,0},{2,1},{3,2},{4,7},{5,4},{6,5},{7,6},{8,11},{9,8},{10,9... | collective-permute-start | bytes 1179656 | tf_op jit(solution)/shard_map/attn_in_gather/ppermute | solution.py:127
  119.1 9.3 %collective-permute-done.12 = bf16[128,1536]{1,0:T(8,128)(2,1)S(1)} collective-permute-done((bf16[128,1536]{1,0:T(8,128)(2,1)S(1)}, bf16[128,1536]{1,0:T(8,128)(2,1)S(1)}, u32[]{:S(2)}, u32[]{:S(2)}) %collective-permute-start.12) | collective-permute-done | bytes 393248 | tf_op jit(solution)/shard_map/attn_in_gather/ppermute | solution.py:127
  128.5 15.4 %collective-permute-done.13 = bf16[128,1536]{1,0:T(8,128)(2,1)S(1)} collective-permute-done((bf16[128,1536]{1,0:T(8,128)(2,1)S(1)}, bf16[128,1536]{1,0:T(8,128)(2,1)S(1)}, u32[]{:S(2)}, u32[]{:S(2)}) %collective-permute-start.13) | collective-permute-done | bytes 393248 | tf_op jit(solution)/shard_map/attn_in_gather/ppermute | solution.py:127
  145.5 8.6 %collective-permute-done.15 = bf16[2,512,256]{2,1,0:T(8,128)(2,1)S(1)} collective-permute-done((bf16[2,512,256]{2,1,0:T(8,128)(2,1)S(1)}, bf16[2,512,256]{2,1,0:T(8,128)(2,1)S(1)}, u32[]{:S(2)}, u32[]{:S(2)}) %collective-permute-start.15) | collective-permute-done | bytes 524320 | tf_op jit(solution)/shard_map/kv_ring/ppermute | solution.py:207
  154.6 8.2 %collective-permute-done.16 = bf16[2,512,256]{2,1,0:T(8,128)(2,1)S(1)} collective-permute-done((bf16[2,512,256]{2,1,0:T(8,128)(2,1)S(1)}, bf16[2,512,256]{2,1,0:T(8,128)(2,1)S(1)}, u32[]{:S(2)}, u32[]{:S(2)}) %collective-permute-start.16) | collective-permute-done | bytes 524320 | tf_op jit(solution)/shard_map/kv_ring/ppermute | solution.py:207
  163.6 7.7 %collective-permute-done.17 = bf16[2,512,256]{2,1,0:T(8,128)(2,1)S(1)} collective-permute-done((bf16[2,512,256]{2,1,0:T(8,128)(2,1)S(1)}, bf16[2,512,256]{2,1,0:T(8,128)(2,1)S(1)}, u32[]{:S(2)}, u32[]{:S(2)}) %collective-permute-start.17) | collective-permute-done | bytes 524320 | tf_op jit(solution)/shard_map/kv_ring/ppermute | solution.py:207
  176.8 8.0 %collective-permute-start.18 = (bf16[128,256]{1,0:T(8,128)(2,1)S(1)}, bf16[128,256]{1,0:T(8,128)(2,1)S(1)}, u32[]{:S(2)}, u32[]{:S(2)}) collective-permute-start(bf16[128,256]{1,0:T(8,128)(2,1)S(1)} %get-tuple-element.29), channel_id=1, source_target_pairs={{0,1},{1,2},{2,3},{3,0},{4,5},{5,6},{6,7},{7,4},{8,9},{9,10},{10,1... | collective-permute-start | bytes 196616 | tf_op jit(solution)/shard_map/out_projection/ppermute | solution.py:98
  184.8 2.2 %collective-permute-start.19 = (bf16[128,256]{1,0:T(8,128)(2,1)S(1)}, bf16[128,256]{1,0:T(8,128)(2,1)S(1)}, u32[]{:S(2)}, u32[]{:S(2)}) collective-permute-start(bf16[128,256]{1,0:T(8,128)(2,1)S(1)} %get-tuple-element.28), channel_id=1, source_target_pairs={{0,2},{1,3},{2,0},{3,1},{4,6},{5,7},{6,4},{7,5},{8,10},{9,11},{10,... | collective-permute-start | bytes 196616 | tf_op jit(solution)/shard_map/out_projection/ppermute | solution.py:98
  187.3 1.9 collective-permute-done.18
  189.3 1.8 collective-permute-done.19
  191.9 3.4 %convert_reduce_fusion = (f32[8,1536]{1,0:T(8,128)S(1)}, bf16[128,1536]{1,0:T(8,128)(2,1)}) fusion(bf16[128,1024]{0,1:T(8,128)(2,1)S(1)} %bitcast.228, bf16[1024,1536]{1,0:T(8,128)(2,1)} %maximum_select_fusion, bf16[128,1536]{1,0:T(8,128)(2,1)S(1)} %get-tuple-element.15), kind=kOutput, calls=%fused_computation.78 | convolution fusion | flops 403623936 | bytes 4243456 | tf_op jit(solution)/shard_map/out_projection/dot_general | solution.py:219
  196.3 2.1 %collective-permute-start.22 = (bf16[8,256]{1,0:T(8,128)(2,1)S(1)}, bf16[8,256]{1,0:T(8,128)(2,1)S(1)}, u32[]{:S(2)}, u32[]{:S(2)}) collective-permute-start(bf16[8,256]{1,0:T(8,128)(2,1)S(1)} %get-tuple-element.47), channel_id=1, source_target_pairs={{0,2},{1,3},{2,0},{3,1},{4,6},{5,7},{6,4},{7,5},{8,10},{9,11},{10,... | collective-permute-start | bytes 12296 | tf_op jit(solution)/shard_map/sides_gather/ppermute | solution.py:127
  199.5 1.6 collective-permute-done.21
  202.9 1.4 collective-permute-start.26
  (119 shorter events, 30.1 us)
Async XLA Ops:
  0.6 143.3 %copy-start = (bf16[1536,768]{1,0:T(8,128)(2,1)S(1)}, bf16[1536,768]{1,0:T(8,128)(2,1)}, u32[]{:S(2)}) copy-start(bf16[1536,768]{1,0:T(8,128)(2,1)} %param.14) | copy-start | bytes 7077892
  4.0 55.3 %collective-permute-start.5 = (bf16[256,768]{1,0:T(8,128)(2,1)}, bf16[256,768]{1,0:T(8,128)(2,1)}, u32[]{:S(2)}, u32[]{:S(2)}) collective-permute-start(bf16[256,768]{1,0:T(8,128)(2,1)} %get-tuple-element.17), channel_id=1, source_target_pairs={{0,1},{1,2},{2,3},{3,0},{4,5},{5,6},{6,7},{7,4},{8,9},{9,10},{10,1... | collective-permute-start | bytes 1179656 | tf_op jit(solution)/shard_map/conv_reduce/ppermute | solution.py:127
  7.0 54.1 %collective-permute-start.6 = (bf16[256,768]{1,0:T(8,128)(2,1)}, bf16[256,768]{1,0:T(8,128)(2,1)}, u32[]{:S(2)}, u32[]{:S(2)}) collective-permute-start(bf16[256,768]{1,0:T(8,128)(2,1)} %get-tuple-element.17), channel_id=1, source_target_pairs={{0,2},{1,3},{2,0},{3,1},{4,6},{5,7},{6,4},{7,5},{8,10},{9,11},{10,... | collective-permute-start | bytes 1179656 | tf_op jit(solution)/shard_map/conv_reduce/ppermute | solution.py:127
  9.6 53.4 %collective-permute-start.7 = (bf16[256,768]{1,0:T(8,128)(2,1)}, bf16[256,768]{1,0:T(8,128)(2,1)}, u32[]{:S(2)}, u32[]{:S(2)}) collective-permute-start(bf16[256,768]{1,0:T(8,128)(2,1)} %get-tuple-element.17), channel_id=1, source_target_pairs={{0,3},{1,0},{2,1},{3,2},{4,7},{5,4},{6,5},{7,6},{8,11},{9,8},{10,9... | collective-permute-start | bytes 1179656 | tf_op jit(solution)/shard_map/conv_reduce/ppermute | solution.py:127
  12.9 25.5 %collective-permute-start = (bf16[128,384]{1,0:T(8,128)(2,1)}, bf16[128,384]{1,0:T(8,128)(2,1)S(1)}, u32[]{:S(2)}, u32[]{:S(2)}) collective-permute-start(bf16[128,384]{1,0:T(8,128)(2,1)} %bitcast.210), channel_id=1, source_target_pairs={{0,1},{1,2},{2,3},{3,0},{4,5},{5,6},{6,7},{7,4},{8,9},{9,10},{10,1... | collective-permute-start | bytes 294920 | tf_op jit(solution)/shard_map/ppermute | solution.py:65
  14.2 35.9 %collective-permute-start.1 = (bf16[128,384]{1,0:T(8,128)(2,1)}, bf16[128,384]{1,0:T(8,128)(2,1)S(1)}, u32[]{:S(2)}, u32[]{:S(2)}) collective-permute-start(bf16[128,384]{1,0:T(8,128)(2,1)} %bitcast.209), channel_id=1, source_target_pairs={{0,2},{1,3},{2,0},{3,1},{4,6},{5,7},{6,4},{7,5},{8,10},{9,11},{10,... | collective-permute-start | bytes 294920 | tf_op jit(solution)/shard_map/ppermute | solution.py:65
  38.3 14.2 %collective-permute-start.2 = (bf16[128,384]{1,0:T(8,128)(2,1)S(1)}, bf16[128,384]{1,0:T(8,128)(2,1)S(1)}, u32[]{:S(2)}, u32[]{:S(2)}) collective-permute-start(bf16[128,384]{1,0:T(8,128)(2,1)S(1)} %bitcast.232), channel_id=1, source_target_pairs={{0,3},{1,0},{2,1},{3,2},{4,7},{5,4},{6,5},{7,6},{8,11},{9,8},{10,9... | collective-permute-start | bytes 294920 | tf_op jit(solution)/shard_map/ppermute | solution.py:65
  52.5 13.4 %collective-permute-start.4 = (bf16[8,384]{1,0:T(8,128)(2,1)S(1)}, bf16[8,384]{1,0:T(8,128)(2,1)S(1)}, u32[]{:S(2)}, u32[]{:S(2)}) collective-permute-start(bf16[8,384]{1,0:T(8,128)(2,1)S(1)} %get-tuple-element.22), channel_id=1, source_target_pairs={{4,0},{8,4},{12,8},{5,1},{9,5},{13,9},{6,2},{10,6},{14,10},{7,3},{... | collective-permute-start | bytes 18440 | tf_op jit(solution)/shard_map/ppermute | solution.py:26
  53.8 14.3 %slice-start = ((s8[5898240]{0:T(1024)(128)(4,1)}), s8[4194304]{0:T(1024)(128)(4,1)S(1)}, s32[]{:S(2)}) async-start(s8[5898240]{0:T(1024)(128)(4,1)} %bitcast.225), calls=%async_computation | async-start | bytes 8388608
  56.2 12.9 %collective-permute-start.3 = (bf16[8,384]{1,0:T(8,128)(2,1)S(1)}, bf16[8,384]{1,0:T(8,128)(2,1)S(1)}, u32[]{:S(2)}, u32[]{:S(2)}) collective-permute-start(bf16[8,384]{1,0:T(8,128)(2,1)S(1)} %get-tuple-element.21), channel_id=1, source_target_pairs={{0,4},{4,8},{8,12},{1,5},{5,9},{9,13},{2,6},{6,10},{10,14},{3,7},{... | collective-permute-start | bytes 18440 | tf_op jit(solution)/shard_map/ppermute | solution.py:25
  64.7 6.6 %collective-permute-start.8 = (bf16[1024,768]{1,0:T(8,128)(2,1)}, bf16[1024,768]{1,0:T(8,128)(2,1)S(1)}, u32[]{:S(2)}, u32[]{:S(2)}) collective-permute-start(bf16[1024,768]{1,0:T(8,128)(2,1)} %bitcast.17), channel_id=1, source_target_pairs={{0,4},{4,0},{8,12},{12,8},{1,5},{5,1},{9,13},{13,9},{2,6},{6,2},{1... | collective-permute-start | bytes 4718600 | tf_op jit(solution)/shard_map/conv_reduce/ppermute | solution.py:111
  75.3 12.5 %collective-permute-start.11 = (bf16[128,1536]{1,0:T(8,128)(2,1)S(1)}, bf16[128,1536]{1,0:T(8,128)(2,1)S(1)}, u32[]{:S(2)}, u32[]{:S(2)}) collective-permute-start(bf16[128,1536]{1,0:T(8,128)(2,1)S(1)} %get-tuple-element.19), channel_id=1, source_target_pairs={{0,3},{1,0},{2,1},{3,2},{4,7},{5,4},{6,5},{7,6},{8,11},{9,8},{10,9... | collective-permute-start | bytes 1179656 | tf_op jit(solution)/shard_map/conv_reduce/ppermute | solution.py:51
  78.2 35.5 %collective-permute-start.10 = (bf16[128,1536]{1,0:T(8,128)(2,1)S(1)}, bf16[128,1536]{1,0:T(8,128)(2,1)S(1)}, u32[]{:S(2)}, u32[]{:S(2)}) collective-permute-start(bf16[128,1536]{1,0:T(8,128)(2,1)S(1)} %get-tuple-element.20), channel_id=1, source_target_pairs={{0,2},{1,3},{2,0},{3,1},{4,6},{5,7},{6,4},{7,5},{8,10},{9,11},{10,... | collective-permute-start | bytes 1179656 | tf_op jit(solution)/shard_map/conv_reduce/ppermute | solution.py:51
  79.2 35.0 %copy-start.4 = (f32[1536]{0:T(1024)S(1)}, f32[1536]{0:T(1024)}, u32[]{:S(2)}) copy-start(f32[1536]{0:T(1024)} %param.13) | copy-start | bytes 18436
  79.3 34.5 %collective-permute-start.9 = (bf16[128,1536]{1,0:T(8,128)(2,1)S(1)}, bf16[128,1536]{1,0:T(8,128)(2,1)S(1)}, u32[]{:S(2)}, u32[]{:S(2)}) collective-permute-start(bf16[128,1536]{1,0:T(8,128)(2,1)S(1)} %get-tuple-element.18), channel_id=1, source_target_pairs={{0,1},{1,2},{2,3},{3,0},{4,5},{5,6},{6,7},{7,4},{8,9},{9,10},{10,1... | collective-permute-start | bytes 1179656 | tf_op jit(solution)/shard_map/conv_reduce/ppermute | solution.py:51
  114.4 14.0 %collective-permute-start.12 = (bf16[128,1536]{1,0:T(8,128)(2,1)S(1)}, bf16[128,1536]{1,0:T(8,128)(2,1)S(1)}, u32[]{:S(2)}, u32[]{:S(2)}) collective-permute-start(bf16[128,1536]{1,0:T(8,128)(2,1)S(1)} %get-tuple-element.13), channel_id=1, source_target_pairs={{0,1},{1,2},{2,3},{3,0},{4,5},{5,6},{6,7},{7,4},{8,9},{9,10},{10,1... | collective-permute-start | bytes 1179656 | tf_op jit(solution)/shard_map/attn_in_gather/ppermute | solution.py:127
  114.5 29.3 %collective-permute-start.13 = (bf16[128,1536]{1,0:T(8,128)(2,1)S(1)}, bf16[128,1536]{1,0:T(8,128)(2,1)S(1)}, u32[]{:S(2)}, u32[]{:S(2)}) collective-permute-start(bf16[128,1536]{1,0:T(8,128)(2,1)S(1)} %get-tuple-element.13), channel_id=1, source_target_pairs={{0,2},{1,3},{2,0},{3,1},{4,6},{5,7},{6,4},{7,5},{8,10},{9,11},{10,... | collective-permute-start | bytes 1179656 | tf_op jit(solution)/shard_map/attn_in_gather/ppermute | solution.py:127
  116.3 27.6 %collective-permute-start.14 = (bf16[128,1536]{1,0:T(8,128)(2,1)S(1)}, bf16[128,1536]{1,0:T(8,128)(2,1)S(1)}, u32[]{:S(2)}, u32[]{:S(2)}) collective-permute-start(bf16[128,1536]{1,0:T(8,128)(2,1)S(1)} %get-tuple-element.13), channel_id=1, source_target_pairs={{0,3},{1,0},{2,1},{3,2},{4,7},{5,4},{6,5},{7,6},{8,11},{9,8},{10,9... | collective-permute-start | bytes 1179656 | tf_op jit(solution)/shard_map/attn_in_gather/ppermute | solution.py:127
  145.4 8.7 %collective-permute-start.15 = (bf16[2,512,256]{2,1,0:T(8,128)(2,1)S(1)}, bf16[2,512,256]{2,1,0:T(8,128)(2,1)S(1)}, u32[]{:S(2)}, u32[]{:S(2)}) collective-permute-start(bf16[2,512,256]{2,1,0:T(8,128)(2,1)S(1)} %slice.87), channel_id=1, source_target_pairs={{0,4},{4,8},{8,12},{12,0},{1,5},{5,9},{9,13},{13,1},{2,6},{6,10},{... | collective-permute-start | bytes 1572872 | tf_op jit(solution)/shard_map/kv_ring/ppermute | solution.py:207
  154.1 8.6 %collective-permute-start.16 = (bf16[2,512,256]{2,1,0:T(8,128)(2,1)S(1)}, bf16[2,512,256]{2,1,0:T(8,128)(2,1)S(1)}, u32[]{:S(2)}, u32[]{:S(2)}) collective-permute-start(bf16[2,512,256]{2,1,0:T(8,128)(2,1)S(1)} %collective-permute-done.15), channel_id=1, source_target_pairs={{0,4},{4,8},{8,12},{12,0},{1,5},{5,9},{9,13},{13,1},{2,6},{6,10},{... | collective-permute-start | bytes 1572872 | tf_op jit(solution)/shard_map/kv_ring/ppermute | solution.py:207
  162.7 8.6 %collective-permute-start.17 = (bf16[2,512,256]{2,1,0:T(8,128)(2,1)S(1)}, bf16[2,512,256]{2,1,0:T(8,128)(2,1)S(1)}, u32[]{:S(2)}, u32[]{:S(2)}) collective-permute-start(bf16[2,512,256]{2,1,0:T(8,128)(2,1)S(1)} %collective-permute-done.16), channel_id=1, source_target_pairs={{0,4},{4,8},{8,12},{12,0},{1,5},{5,9},{9,13},{13,1},{2,6},{6,10},{... | collective-permute-start | bytes 1572872 | tf_op jit(solution)/shard_map/kv_ring/ppermute | solution.py:207
  176.8 12.4 %collective-permute-start.18 = (bf16[128,256]{1,0:T(8,128)(2,1)S(1)}, bf16[128,256]{1,0:T(8,128)(2,1)S(1)}, u32[]{:S(2)}, u32[]{:S(2)}) collective-permute-start(bf16[128,256]{1,0:T(8,128)(2,1)S(1)} %get-tuple-element.29), channel_id=1, source_target_pairs={{0,1},{1,2},{2,3},{3,0},{4,5},{5,6},{6,7},{7,4},{8,9},{9,10},{10,1... | collective-permute-start | bytes 196616 | tf_op jit(solution)/shard_map/out_projection/ppermute | solution.py:98
  184.8 6.3 %collective-permute-start.19 = (bf16[128,256]{1,0:T(8,128)(2,1)S(1)}, bf16[128,256]{1,0:T(8,128)(2,1)S(1)}, u32[]{:S(2)}, u32[]{:S(2)}) collective-permute-start(bf16[128,256]{1,0:T(8,128)(2,1)S(1)} %get-tuple-element.28), channel_id=1, source_target_pairs={{0,2},{1,3},{2,0},{3,1},{4,6},{5,7},{6,4},{7,5},{8,10},{9,11},{10,... | collective-permute-start | bytes 196616 | tf_op jit(solution)/shard_map/out_projection/ppermute | solution.py:98
  187.0 4.7 %collective-permute-start.20 = (bf16[128,256]{1,0:T(8,128)(2,1)S(1)}, bf16[128,256]{1,0:T(8,128)(2,1)S(1)}, u32[]{:S(2)}, u32[]{:S(2)}) collective-permute-start(bf16[128,256]{1,0:T(8,128)(2,1)S(1)} %get-tuple-element.27), channel_id=1, source_target_pairs={{0,3},{1,0},{2,1},{3,2},{4,7},{5,4},{6,5},{7,6},{8,11},{9,8},{10,9... | collective-permute-start | bytes 196616 | tf_op jit(solution)/shard_map/out_projection/ppermute | solution.py:98
  191.9 14.1 %copy-start.6 = (bf16[256,128]{1,0:T(8,128)(2,1)S(1)}, bf16[256,128]{1,0:T(8,128)(2,1)}, u32[]{:S(2)}) copy-start(bf16[256,128]{1,0:T(8,128)(2,1)} %param.19) | copy-start | bytes 196612
  191.9 14.1 %copy-start.7 = (bf16[128,256]{1,0:T(8,128)(2,1)S(1)}, bf16[128,256]{1,0:T(8,128)(2,1)}, u32[]{:S(2)}) copy-start(bf16[128,256]{1,0:T(8,128)(2,1)} %param.18) | copy-start | bytes 196612
  195.7 5.4 %collective-permute-start.21 = (bf16[8,256]{1,0:T(8,128)(2,1)S(1)}, bf16[8,256]{1,0:T(8,128)(2,1)S(1)}, u32[]{:S(2)}, u32[]{:S(2)}) collective-permute-start(bf16[8,256]{1,0:T(8,128)(2,1)S(1)} %get-tuple-element.47), channel_id=1, source_target_pairs={{0,1},{1,2},{2,3},{3,0},{4,5},{5,6},{6,7},{7,4},{8,9},{9,10},{10,1... | collective-permute-start | bytes 12296 | tf_op jit(solution)/shard_map/sides_gather/ppermute | solution.py:127
  196.3 4.8 %collective-permute-start.22 = (bf16[8,256]{1,0:T(8,128)(2,1)S(1)}, bf16[8,256]{1,0:T(8,128)(2,1)S(1)}, u32[]{:S(2)}, u32[]{:S(2)}) collective-permute-start(bf16[8,256]{1,0:T(8,128)(2,1)S(1)} %get-tuple-element.47), channel_id=1, source_target_pairs={{0,2},{1,3},{2,0},{3,1},{4,6},{5,7},{6,4},{7,5},{8,10},{9,11},{10,... | collective-permute-start | bytes 12296 | tf_op jit(solution)/shard_map/sides_gather/ppermute | solution.py:127
  198.4 3.6 %collective-permute-start.23 = (bf16[8,256]{1,0:T(8,128)(2,1)S(1)}, bf16[8,256]{1,0:T(8,128)(2,1)S(1)}, u32[]{:S(2)}, u32[]{:S(2)}) collective-permute-start(bf16[8,256]{1,0:T(8,128)(2,1)S(1)} %get-tuple-element.47), channel_id=1, source_target_pairs={{0,3},{1,0},{2,1},{3,2},{4,7},{5,4},{6,5},{7,6},{8,11},{9,8},{10,9... | collective-permute-start | bytes 12296 | tf_op jit(solution)/shard_map/sides_gather/ppermute | solution.py:127
  202.0 3.2 %collective-permute-start.24 = (bf16[32,256]{1,0:T(8,128)(2,1)S(1)}, bf16[32,256]{1,0:T(8,128)(2,1)S(1)}, u32[]{:S(2)}, u32[]{:S(2)}) collective-permute-start(bf16[32,256]{1,0:T(8,128)(2,1)S(1)} %bitcast.236), channel_id=1, source_target_pairs={{0,4},{4,8},{8,12},{12,0},{1,5},{5,9},{9,13},{13,1},{2,6},{6,10},{... | collective-permute-start | bytes 49160 | tf_op jit(solution)/shard_map/sides_gather/ppermute | solution.py:127
  202.0 3.9 %collective-permute-start.25 = (bf16[32,256]{1,0:T(8,128)(2,1)S(1)}, bf16[32,256]{1,0:T(8,128)(2,1)S(1)}, u32[]{:S(2)}, u32[]{:S(2)}) collective-permute-start(bf16[32,256]{1,0:T(8,128)(2,1)S(1)} %bitcast.237), channel_id=1, source_target_pairs={{0,8},{4,12},{8,0},{12,4},{1,9},{5,13},{9,1},{13,5},{2,10},{6,14},... | collective-permute-start | bytes 49160 | tf_op jit(solution)/shard_map/sides_gather/ppermute | solution.py:127
  202.9 3.0 %collective-permute-start.26 = (bf16[32,256]{1,0:T(8,128)(2,1)S(1)}, bf16[32,256]{1,0:T(8,128)(2,1)S(1)}, u32[]{:S(2)}, u32[]{:S(2)}) collective-permute-start(bf16[32,256]{1,0:T(8,128)(2,1)S(1)} %bitcast.238), channel_id=1, source_target_pairs={{0,12},{4,0},{8,4},{12,8},{1,13},{5,1},{9,5},{13,9},{2,14},{6,2},{... | collective-permute-start | bytes 49160 | tf_op jit(solution)/shard_map/sides_gather/ppermute | solution.py:127
  (5 other events, 35.0 us)

commit v6 on v4

--- a/solution.py
+++ b/solution.py
@@ -167,7 +167,6 @@
     queries = grouped[:, :, :KEY_SIZE]
     kv = grouped[:, :, KEY_SIZE:]
     scale = 1.0 / math.sqrt(KEY_SIZE)
-    ring = [(i, (i + 1) % seq_count) for i in range(seq_count)]
 
     def attend(state, kv_block):
         running_max, running_sum, weighted = state
@@ -196,13 +195,19 @@
         jnp.zeros((head_count, local_rows, VALUE_SIZE), jnp.float32),
     )
     with jax.named_scope("kv_ring"):
-        current = kv
+        forward = [(i, (i + 1) % seq_count) for i in range(seq_count)]
+        backward = [((i + 1) % seq_count, i) for i in range(seq_count)]
+        half = local_rows // 2
+        going = kv[:, :half]
+        coming = kv[:, half:]
         for step in range(seq_count):
             if step + 1 < seq_count:
-                arriving = lax.ppermute(current, "seq", ring)
-            state = attend(state, current)
+                next_going = lax.ppermute(going, "seq", forward)
+                next_coming = lax.ppermute(coming, "seq", backward)
+            state = attend(state, going)
+            state = attend(state, coming)
             if step + 1 < seq_count:
-                current = arriving
+                going, coming = next_going, next_coming
     running_max, running_sum, weighted = state
     attended = (weighted / running_sum[:, :, None]).astype(jnp.bfloat16)
     attended = attended.transpose(1, 0, 2).reshape(local_rows, head_count * VALUE_SIZE)

time: 189 us -> 181 us (0.958)
  waiting for transfers between devices: 86.5 us -> 82.4 us
  other arithmetic: 5.42 us -> 2.39 us
  local copies, waits for them, and re-layouts: 18.6 us -> 16 us
    ppermute x3 -> x6, waiting for transfers between devices: 0.01 us -> 14.2 us  [the longest x3 9.47 us: shards(): next_going = lax.ppermute(going, 'seq', forward)]
    ppermute x3, waiting for transfers between devices: 10.3 us -> 0.01 us  [line_all_gather(): flow_r = lax.ppermute(flow_r, axis, right)]
    ppermute x3, waiting for transfers between devices: 34.6 us -> 27.4 us  [direct_reduce_scatter(): lax.ppermute(outgoing, axis, [(i, (i + shift) % n) for i in range(n)])]
    ppermute x3, starting transfers between devices: 4.58 us -> 11.4 us  [rows_to_heads(): lax.ppermute(outgoing, axis, [(i, (i + shift) % n) for i in range(n)])]
    ppermute x3, starting transfers between devices: 18.8 us -> 12.9 us  [line_all_gather(): flow_r = lax.ppermute(flow_r, axis, right)]
    ppermute x3, waiting for transfers between devices: 5.16 us -> 10.3 us  [permute_all_to_all(): lax.ppermute(outgoing, axis, [(i, (i + shift) % n) for i in range(n)])]
    ppermute x3, waiting for transfers between devices: 4 us -> 0.01 us  [line_all_gather(): flow_l = lax.ppermute(flow_l, axis, left)]
    ppermute x3 -> x6, starting transfers between devices: 0.06 us -> 3.56 us  [the longest x3 2.26 us: shards(): next_coming = lax.ppermute(coming, 'seq', backward)]
  transfers between devices with their start and end apart: 30 -> 33, of which waited for: 20 -> 18; matrix products, arithmetic and copies ran while one was open for 12% -> 17% of each run, Pallas kernels for 0% -> 0%
where the time goes in v6:
time: 181 us; the launch traced here: 180 us
  waiting for transfers between devices  82.4 us (46%)
  starting transfers between devices  56.8 us (31%)
  matrix products  21 us (12%)
  local copies, waits for them, and re-layouts  16 us (9%)
  other arithmetic  2.39 us (1%)
    ppermute x3, waiting for transfers between devices, direct_reduce_scatter(): lax.ppermute(outgoing, axis, [(i, (i + shift) % n) for i in range(n)])  27.4 us
    ppermute x9, waiting for transfers between devices, direct_all_gather(): lax.ppermute(value, axis, [(i, (i + shift) % n) for i in range(n)])  26.7 us
    ppermute x3, starting transfers between devices, line_all_gather(): flow_r = lax.ppermute(flow_r, axis, right)  12.9 us
    ppermute x3, starting transfers between devices, rows_to_heads(): lax.ppermute(outgoing, axis, [(i, (i + shift) % n) for i in range(n)])  11.4 us
    ppermute x3, waiting for transfers between devices, permute_all_to_all(): lax.ppermute(outgoing, axis, [(i, (i + shift) % n) for i in range(n)])  10.3 us
    ppermute x9, starting transfers between devices, direct_all_gather(): lax.ppermute(value, axis, [(i, (i + shift) % n) for i in range(n)])  9.85 us
    ppermute x3, waiting for transfers between devices, shards(): next_going = lax.ppermute(going, 'seq', forward)  9.47 us
    dot_general x5, matrix products, conv_rows(): jnp.dot(shifted, conv_weight[offset], preferred_element_type=jnp.float32)  6.46 us
  transfers between devices with their start and end apart: 33, of which 18 were waited for; matrix products, arithmetic and copies ran while one was open for 17% of the time, Pallas kernels for 0%

profile of v6, /device:TPU:0, one launch (start us, length us, event | category | flops | bytes accessed | tf_op | source)
XLA Modules:
  0.0 180.1 jit_solution(5574718515630001955)
XLA Ops:
  0.7 1.4 broadcast_in_dim.154
  3.5 5.7 %collective-permute-start.20 = (bf16[256,768]{1,0:T(8,128)(2,1)}, bf16[256,768]{1,0:T(8,128)(2,1)}, u32[]{:S(2)}, u32[]{:S(2)}) collective-permute-start(bf16[256,768]{1,0:T(8,128)(2,1)} %get-tuple-element.3), channel_id=1, source_target_pairs={{0,1},{1,2},{2,3},{4,5},{5,6},{6,7},{8,9},{9,10},{10,11},{12,13},{... | collective-permute-start | bytes 1179656 | tf_op jit(solution)/shard_map/out_projection/ppermute | solution.py:80
  12.4 2.6 %collective-permute-start = (bf16[128,384]{1,0:T(8,128)(2,1)}, bf16[128,384]{1,0:T(8,128)(2,1)S(1)}, u32[]{:S(2)}, u32[]{:S(2)}) collective-permute-start(bf16[128,384]{1,0:T(8,128)(2,1)} %bitcast.289), channel_id=1, source_target_pairs={{0,1},{1,2},{2,3},{3,0},{4,5},{5,6},{6,7},{7,4},{8,9},{9,10},{10,1... | collective-permute-start | bytes 294920 | tf_op jit(solution)/shard_map/ppermute | solution.py:65
  15.7 2.6 %collective-permute-start.1 = (bf16[128,384]{1,0:T(8,128)(2,1)}, bf16[128,384]{1,0:T(8,128)(2,1)S(1)}, u32[]{:S(2)}, u32[]{:S(2)}) collective-permute-start(bf16[128,384]{1,0:T(8,128)(2,1)} %bitcast.288), channel_id=1, source_target_pairs={{0,2},{1,3},{2,0},{3,1},{4,6},{5,7},{6,4},{7,5},{8,10},{9,11},{10,... | collective-permute-start | bytes 294920 | tf_op jit(solution)/shard_map/ppermute | solution.py:65
  19.1 7.6 %collective-permute-done = bf16[128,384]{1,0:T(8,128)(2,1)S(1)} collective-permute-done((bf16[128,384]{1,0:T(8,128)(2,1)}, bf16[128,384]{1,0:T(8,128)(2,1)S(1)}, u32[]{:S(2)}, u32[]{:S(2)}) %collective-permute-start) | collective-permute-done | bytes 98336 | tf_op jit(solution)/shard_map/ppermute | solution.py:65
  26.8 2.7 %collective-permute-done.1 = bf16[128,384]{1,0:T(8,128)(2,1)S(1)} collective-permute-done((bf16[128,384]{1,0:T(8,128)(2,1)}, bf16[128,384]{1,0:T(8,128)(2,1)S(1)}, u32[]{:S(2)}, u32[]{:S(2)}) %collective-permute-start.1) | collective-permute-done | bytes 98336 | tf_op jit(solution)/shard_map/ppermute | solution.py:65
  29.6 1.6 collective-permute-start.4
  31.1 2.4 %fusion.37 = f32[512,1536]{1,0:T(8,128)S(1)} fusion(bf16[512,384]{1,0:T(8,128)(2,1)S(1)} %bitcast.302, bf16[5,384,1536]{2,1,0:T(8,128)(2,1)} %param.12), kind=kOutput, calls=%fused_computation.62 | convolution fusion | flops 603979776 | bytes 4718592 | tf_op jit(solution)/shard_map/conv_reduce/dot_general | solution.py:39
  33.5 2.9 %collective-permute-start.3 = (bf16[8,384]{1,0:T(8,128)(2,1)S(1)}, bf16[8,384]{1,0:T(8,128)(2,1)S(1)}, u32[]{:S(2)}, u32[]{:S(2)}) collective-permute-start(bf16[8,384]{1,0:T(8,128)(2,1)S(1)} %get-tuple-element.29), channel_id=1, source_target_pairs={{0,4},{4,8},{8,12},{1,5},{5,9},{9,13},{2,6},{6,10},{10,14},{3,7},{... | collective-permute-start | bytes 18440 | tf_op jit(solution)/shard_map/ppermute | solution.py:25
  41.0 2.7 %collective-permute-start.6 = (bf16[128,1536]{1,0:T(8,128)(2,1)S(1)}, bf16[128,1536]{1,0:T(8,128)(2,1)S(1)}, u32[]{:S(2)}, u32[]{:S(2)}) collective-permute-start(bf16[128,1536]{1,0:T(8,128)(2,1)S(1)} %get-tuple-element.26), channel_id=1, source_target_pairs={{0,2},{1,3},{2,0},{3,1},{4,6},{5,7},{6,4},{7,5},{8,10},{9,11},{10,... | collective-permute-start | bytes 1179656 | tf_op jit(solution)/shard_map/conv_reduce/ppermute | solution.py:51
  43.8 2.7 %collective-permute-start.22 = (bf16[256,768]{1,0:T(8,128)(2,1)}, bf16[256,768]{1,0:T(8,128)(2,1)S(1)}, u32[]{:S(2)}, u32[]{:S(2)}) collective-permute-start(bf16[256,768]{1,0:T(8,128)(2,1)} %collective-permute-done.20), channel_id=1, source_target_pairs={{0,1},{1,2},{2,3},{4,5},{5,6},{6,7},{8,9},{9,10},{10,11},{12,13},{... | collective-permute-start | bytes 1179656 | tf_op jit(solution)/shard_map/out_projection/ppermute | solution.py:80
  47.8 1.8 bitcast_dynamic-update-slice_fusion.5
  49.5 1.8 bitcast_dynamic-update-slice_fusion.4
  52.4 26.3 %collective-permute-done.6 = bf16[128,1536]{1,0:T(8,128)(2,1)S(1)} collective-permute-done((bf16[128,1536]{1,0:T(8,128)(2,1)S(1)}, bf16[128,1536]{1,0:T(8,128)(2,1)S(1)}, u32[]{:S(2)}, u32[]{:S(2)}) %collective-permute-start.6) | collective-permute-done | bytes 393248 | tf_op jit(solution)/shard_map/conv_reduce/ppermute | solution.py:51
  80.1 3.2 %collective-permute-start.10 = (bf16[128,1536]{1,0:T(8,128)(2,1)S(1)}, bf16[128,1536]{1,0:T(8,128)(2,1)S(1)}, u32[]{:S(2)}, u32[]{:S(2)}) collective-permute-start(bf16[128,1536]{1,0:T(8,128)(2,1)S(1)} %get-tuple-element.21), channel_id=1, source_target_pairs={{0,3},{1,0},{2,1},{3,2},{4,7},{5,4},{6,5},{7,6},{8,11},{9,8},{10,9... | collective-permute-start | bytes 1179656 | tf_op jit(solution)/shard_map/attn_in_gather/ppermute | solution.py:127
  83.3 4.5 %collective-permute-start.24 = (bf16[256,768]{1,0:T(8,128)(2,1)S(1)}, bf16[256,768]{1,0:T(8,128)(2,1)S(1)}, u32[]{:S(2)}, u32[]{:S(2)}) collective-permute-start(bf16[256,768]{1,0:T(8,128)(2,1)S(1)} %collective-permute-done.22), channel_id=1, source_target_pairs={{0,1},{1,2},{2,3},{4,5},{5,6},{6,7},{8,9},{9,10},{10,11},{12,13},{... | collective-permute-start | bytes 1179656 | tf_op jit(solution)/shard_map/out_projection/ppermute | solution.py:80
  90.7 2.6 %collective-permute-done.8 = bf16[128,1536]{1,0:T(8,128)(2,1)S(1)} collective-permute-done((bf16[128,1536]{1,0:T(8,128)(2,1)S(1)}, bf16[128,1536]{1,0:T(8,128)(2,1)S(1)}, u32[]{:S(2)}, u32[]{:S(2)}) %collective-permute-start.8) | collective-permute-done | bytes 393248 | tf_op jit(solution)/shard_map/attn_in_gather/ppermute | solution.py:127
  93.4 19.2 %collective-permute-done.9 = bf16[128,1536]{1,0:T(8,128)(2,1)S(1)} collective-permute-done((bf16[128,1536]{1,0:T(8,128)(2,1)S(1)}, bf16[128,1536]{1,0:T(8,128)(2,1)S(1)}, u32[]{:S(2)}, u32[]{:S(2)}) %collective-permute-start.9) | collective-permute-done | bytes 393248 | tf_op jit(solution)/shard_map/attn_in_gather/ppermute | solution.py:127
  112.6 1.4 convolution_convert_fusion
  115.3 3.5 %collective-permute-done.12 = bf16[2,256,256]{2,1,0:T(8,128)(2,1)S(1)} collective-permute-done((bf16[2,256,256]{2,1,0:T(8,128)(2,1)S(1)}, bf16[2,256,256]{2,1,0:T(8,128)(2,1)S(1)}, u32[]{:S(2)}, u32[]{:S(2)}) %collective-permute-start.12) | collective-permute-done | bytes 262176 | tf_op jit(solution)/shard_map/kv_ring/ppermute | solution.py:206
  118.8 2.2 %collective-permute-start.14 = (bf16[2,256,256]{2,1,0:T(8,128)(2,1)S(1)}, bf16[2,256,256]{2,1,0:T(8,128)(2,1)S(1)}, u32[]{:S(2)}, u32[]{:S(2)}) collective-permute-start(bf16[2,256,256]{2,1,0:T(8,128)(2,1)S(1)} %collective-permute-done.12), channel_id=1, source_target_pairs={{4,0},{8,4},{12,8},{0,12},{5,1},{9,5},{13,9},{1,13},{6,2},{10,6},{... | collective-permute-start | bytes 786440 | tf_op jit(solution)/shard_map/kv_ring/ppermute | solution.py:206
  121.0 2.5 %collective-permute-done.11 = bf16[2,256,256]{2,1,0:T(8,128)(2,1)S(1)} collective-permute-done((bf16[2,256,256]{2,1,0:T(8,128)(2,1)S(1)}, bf16[2,256,256]{2,1,0:T(8,128)(2,1)S(1)}, u32[]{:S(2)}, u32[]{:S(2)}) %collective-permute-start.11) | collective-permute-done | bytes 262176 | tf_op jit(solution)/shard_map/kv_ring/ppermute | solution.py:205
  125.9 2.6 %slice.148 = bf16[4,256,768]{2,1,0:T(8,128)(2,1)} slice(bf16[5,256,768]{2,1,0:T(8,128)(2,1)} %bitcast_dynamic-update-slice_fusion), slice={[0:4], [0:256], [0:768]} | slice | bytes 3145728 | tf_op jit(solution)/shard_map/out_projection/slice | solution.py:86
  128.5 1.7 collective-permute-start.26
  134.5 5.7 %collective-permute-done.15 = bf16[2,256,256]{2,1,0:T(8,128)(2,1)S(1)} collective-permute-done((bf16[2,256,256]{2,1,0:T(8,128)(2,1)S(1)}, bf16[2,256,256]{2,1,0:T(8,128)(2,1)S(1)}, u32[]{:S(2)}, u32[]{:S(2)}) %collective-permute-start.15) | collective-permute-done | bytes 262176 | tf_op jit(solution)/shard_map/kv_ring/ppermute | solution.py:205
  146.7 9.0 %collective-permute-start.17 = (bf16[128,256]{1,0:T(8,128)(2,1)S(1)}, bf16[128,256]{1,0:T(8,128)(2,1)S(1)}, u32[]{:S(2)}, u32[]{:S(2)}) collective-permute-start(bf16[128,256]{1,0:T(8,128)(2,1)S(1)} %get-tuple-element.37), channel_id=1, source_target_pairs={{0,1},{1,2},{2,3},{3,0},{4,5},{5,6},{6,7},{7,4},{8,9},{9,10},{10,1... | collective-permute-start | bytes 196616 | tf_op jit(solution)/shard_map/out_projection/ppermute | solution.py:98
  156.2 1.9 %collective-permute-start.19 = (bf16[128,256]{1,0:T(8,128)(2,1)S(1)}, bf16[128,256]{1,0:T(8,128)(2,1)S(1)}, u32[]{:S(2)}, u32[]{:S(2)}) collective-permute-start(bf16[128,256]{1,0:T(8,128)(2,1)S(1)} %get-tuple-element.35), channel_id=1, source_target_pairs={{0,3},{1,0},{2,1},{3,2},{4,7},{5,4},{6,5},{7,6},{8,11},{9,8},{10,9... | collective-permute-start | bytes 196616 | tf_op jit(solution)/shard_map/out_projection/ppermute | solution.py:98
  158.5 3.5 %collective-permute-done.18 = bf16[128,256]{1,0:T(8,128)(2,1)S(1)} collective-permute-done((bf16[128,256]{1,0:T(8,128)(2,1)S(1)}, bf16[128,256]{1,0:T(8,128)(2,1)S(1)}, u32[]{:S(2)}, u32[]{:S(2)}) %collective-permute-start.18) | collective-permute-done | bytes 65568 | tf_op jit(solution)/shard_map/out_projection/ppermute | solution.py:98
  162.4 5.0 %convert_reduce_fusion = (f32[8,1536]{1,0:T(8,128)S(1)}, bf16[128,1536]{1,0:T(8,128)(2,1)}) fusion(bf16[128,1024]{0,1:T(8,128)(2,1)S(1)} %bitcast.312, bf16[1024,768]{1,0:T(8,128)(2,1)} %collective-permute-done.26, bf16[1024,768]{1,0:T(8,128)(2,1)} %bitcast.63, pred[]{:T(512)S(6)} %eq.29, bf16[128,1536]{1,0:T(8,128)(2,1)S(1)} %get-tuple-element.23), kind=kOutput, calls=%fused_computation.105 | convolution fusion | flops 417779712 | bytes 4243457 | tf_op jit(solution)/shard_map/out_projection/dot_general | solution.py:218
  167.8 1.8 collective-permute-start.27
  169.6 1.7 collective-permute-start.28
  175.0 1.8 collective-permute-start.32
  (144 shorter events, 40.0 us)
Async XLA Ops:
  3.5 40.3 %collective-permute-start.20 = (bf16[256,768]{1,0:T(8,128)(2,1)}, bf16[256,768]{1,0:T(8,128)(2,1)}, u32[]{:S(2)}, u32[]{:S(2)}) collective-permute-start(bf16[256,768]{1,0:T(8,128)(2,1)} %get-tuple-element.3), channel_id=1, source_target_pairs={{0,1},{1,2},{2,3},{4,5},{5,6},{6,7},{8,9},{9,10},{10,11},{12,13},{... | collective-permute-start | bytes 1179656 | tf_op jit(solution)/shard_map/out_projection/ppermute | solution.py:80
  9.1 37.3 %collective-permute-start.21 = (bf16[256,768]{1,0:T(8,128)(2,1)}, bf16[256,768]{1,0:T(8,128)(2,1)}, u32[]{:S(2)}, u32[]{:S(2)}) collective-permute-start(bf16[256,768]{1,0:T(8,128)(2,1)} %get-tuple-element.3), channel_id=1, source_target_pairs={{1,0},{2,1},{3,2},{5,4},{6,5},{7,6},{9,8},{10,9},{11,10},{13,12},{... | collective-permute-start | bytes 1179656 | tf_op jit(solution)/shard_map/out_projection/ppermute | solution.py:81
  12.4 14.3 %collective-permute-start = (bf16[128,384]{1,0:T(8,128)(2,1)}, bf16[128,384]{1,0:T(8,128)(2,1)S(1)}, u32[]{:S(2)}, u32[]{:S(2)}) collective-permute-start(bf16[128,384]{1,0:T(8,128)(2,1)} %bitcast.289), channel_id=1, source_target_pairs={{0,1},{1,2},{2,3},{3,0},{4,5},{5,6},{6,7},{7,4},{8,9},{9,10},{10,1... | collective-permute-start | bytes 294920 | tf_op jit(solution)/shard_map/ppermute | solution.py:65
  15.7 13.8 %collective-permute-start.1 = (bf16[128,384]{1,0:T(8,128)(2,1)}, bf16[128,384]{1,0:T(8,128)(2,1)S(1)}, u32[]{:S(2)}, u32[]{:S(2)}) collective-permute-start(bf16[128,384]{1,0:T(8,128)(2,1)} %bitcast.288), channel_id=1, source_target_pairs={{0,2},{1,3},{2,0},{3,1},{4,6},{5,7},{6,4},{7,5},{8,10},{9,11},{10,... | collective-permute-start | bytes 294920 | tf_op jit(solution)/shard_map/ppermute | solution.py:65
  18.3 11.2 %collective-permute-start.2 = (bf16[128,384]{1,0:T(8,128)(2,1)S(1)}, bf16[128,384]{1,0:T(8,128)(2,1)S(1)}, u32[]{:S(2)}, u32[]{:S(2)}) collective-permute-start(bf16[128,384]{1,0:T(8,128)(2,1)S(1)} %bitcast.314), channel_id=1, source_target_pairs={{0,3},{1,0},{2,1},{3,2},{4,7},{5,4},{6,5},{7,6},{8,11},{9,8},{10,9... | collective-permute-start | bytes 294920 | tf_op jit(solution)/shard_map/ppermute | solution.py:65
  29.6 6.9 %collective-permute-start.4 = (bf16[8,384]{1,0:T(8,128)(2,1)S(1)}, bf16[8,384]{1,0:T(8,128)(2,1)S(1)}, u32[]{:S(2)}, u32[]{:S(2)}) collective-permute-start(bf16[8,384]{1,0:T(8,128)(2,1)S(1)} %get-tuple-element.30), channel_id=1, source_target_pairs={{4,0},{8,4},{12,8},{5,1},{9,5},{13,9},{6,2},{10,6},{14,10},{7,3},{... | collective-permute-start | bytes 18440 | tf_op jit(solution)/shard_map/ppermute | solution.py:26
  33.5 4.9 %collective-permute-start.3 = (bf16[8,384]{1,0:T(8,128)(2,1)S(1)}, bf16[8,384]{1,0:T(8,128)(2,1)S(1)}, u32[]{:S(2)}, u32[]{:S(2)}) collective-permute-start(bf16[8,384]{1,0:T(8,128)(2,1)S(1)} %get-tuple-element.29), channel_id=1, source_target_pairs={{0,4},{4,8},{8,12},{1,5},{5,9},{9,13},{2,6},{6,10},{10,14},{3,7},{... | collective-permute-start | bytes 18440 | tf_op jit(solution)/shard_map/ppermute | solution.py:25
  40.7 11.7 %collective-permute-start.7 = (bf16[128,1536]{1,0:T(8,128)(2,1)S(1)}, bf16[128,1536]{1,0:T(8,128)(2,1)S(1)}, u32[]{:S(2)}, u32[]{:S(2)}) collective-permute-start(bf16[128,1536]{1,0:T(8,128)(2,1)S(1)} %get-tuple-element.25), channel_id=1, source_target_pairs={{0,3},{1,0},{2,1},{3,2},{4,7},{5,4},{6,5},{7,6},{8,11},{9,8},{10,9... | collective-permute-start | bytes 1179656 | tf_op jit(solution)/shard_map/conv_reduce/ppermute | solution.py:51
  41.0 37.7 %collective-permute-start.6 = (bf16[128,1536]{1,0:T(8,128)(2,1)S(1)}, bf16[128,1536]{1,0:T(8,128)(2,1)S(1)}, u32[]{:S(2)}, u32[]{:S(2)}) collective-permute-start(bf16[128,1536]{1,0:T(8,128)(2,1)S(1)} %get-tuple-element.26), channel_id=1, source_target_pairs={{0,2},{1,3},{2,0},{3,1},{4,6},{5,7},{6,4},{7,5},{8,10},{9,11},{10,... | collective-permute-start | bytes 1179656 | tf_op jit(solution)/shard_map/conv_reduce/ppermute | solution.py:51
  43.8 34.9 %collective-permute-start.5 = (bf16[128,1536]{1,0:T(8,128)(2,1)S(1)}, bf16[128,1536]{1,0:T(8,128)(2,1)S(1)}, u32[]{:S(2)}, u32[]{:S(2)}) collective-permute-start(bf16[128,1536]{1,0:T(8,128)(2,1)S(1)} %get-tuple-element.24), channel_id=1, source_target_pairs={{0,1},{1,2},{2,3},{3,0},{4,5},{5,6},{6,7},{7,4},{8,9},{9,10},{10,1... | collective-permute-start | bytes 1179656 | tf_op jit(solution)/shard_map/conv_reduce/ppermute | solution.py:51
  43.8 39.5 %collective-permute-start.22 = (bf16[256,768]{1,0:T(8,128)(2,1)}, bf16[256,768]{1,0:T(8,128)(2,1)S(1)}, u32[]{:S(2)}, u32[]{:S(2)}) collective-permute-start(bf16[256,768]{1,0:T(8,128)(2,1)} %collective-permute-done.20), channel_id=1, source_target_pairs={{0,1},{1,2},{2,3},{4,5},{5,6},{6,7},{8,9},{9,10},{10,11},{12,13},{... | collective-permute-start | bytes 1179656 | tf_op jit(solution)/shard_map/out_projection/ppermute | solution.py:80
  46.5 41.4 %collective-permute-start.23 = (bf16[256,768]{1,0:T(8,128)(2,1)}, bf16[256,768]{1,0:T(8,128)(2,1)S(1)}, u32[]{:S(2)}, u32[]{:S(2)}) collective-permute-start(bf16[256,768]{1,0:T(8,128)(2,1)} %collective-permute-done.21), channel_id=1, source_target_pairs={{1,0},{2,1},{3,2},{5,4},{6,5},{7,6},{9,8},{10,9},{11,10},{13,12},{... | collective-permute-start | bytes 1179656 | tf_op jit(solution)/shard_map/out_projection/ppermute | solution.py:81
  79.4 13.9 %collective-permute-start.8 = (bf16[128,1536]{1,0:T(8,128)(2,1)S(1)}, bf16[128,1536]{1,0:T(8,128)(2,1)S(1)}, u32[]{:S(2)}, u32[]{:S(2)}) collective-permute-start(bf16[128,1536]{1,0:T(8,128)(2,1)S(1)} %get-tuple-element.21), channel_id=1, source_target_pairs={{0,1},{1,2},{2,3},{3,0},{4,5},{5,6},{6,7},{7,4},{8,9},{9,10},{10,1... | collective-permute-start | bytes 1179656 | tf_op jit(solution)/shard_map/attn_in_gather/ppermute | solution.py:127
  79.5 33.0 %collective-permute-start.9 = (bf16[128,1536]{1,0:T(8,128)(2,1)S(1)}, bf16[128,1536]{1,0:T(8,128)(2,1)S(1)}, u32[]{:S(2)}, u32[]{:S(2)}) collective-permute-start(bf16[128,1536]{1,0:T(8,128)(2,1)S(1)} %get-tuple-element.21), channel_id=1, source_target_pairs={{0,2},{1,3},{2,0},{3,1},{4,6},{5,7},{6,4},{7,5},{8,10},{9,11},{10,... | collective-permute-start | bytes 1179656 | tf_op jit(solution)/shard_map/attn_in_gather/ppermute | solution.py:127
  80.1 32.4 %collective-permute-start.10 = (bf16[128,1536]{1,0:T(8,128)(2,1)S(1)}, bf16[128,1536]{1,0:T(8,128)(2,1)S(1)}, u32[]{:S(2)}, u32[]{:S(2)}) collective-permute-start(bf16[128,1536]{1,0:T(8,128)(2,1)S(1)} %get-tuple-element.21), channel_id=1, source_target_pairs={{0,3},{1,0},{2,1},{3,2},{4,7},{5,4},{6,5},{7,6},{8,11},{9,8},{10,9... | collective-permute-start | bytes 1179656 | tf_op jit(solution)/shard_map/attn_in_gather/ppermute | solution.py:127
  83.3 41.0 %collective-permute-start.24 = (bf16[256,768]{1,0:T(8,128)(2,1)S(1)}, bf16[256,768]{1,0:T(8,128)(2,1)S(1)}, u32[]{:S(2)}, u32[]{:S(2)}) collective-permute-start(bf16[256,768]{1,0:T(8,128)(2,1)S(1)} %collective-permute-done.22), channel_id=1, source_target_pairs={{0,1},{1,2},{2,3},{4,5},{5,6},{6,7},{8,9},{9,10},{10,11},{12,13},{... | collective-permute-start | bytes 1179656 | tf_op jit(solution)/shard_map/out_projection/ppermute | solution.py:80
  87.8 37.2 %collective-permute-start.25 = (bf16[256,768]{1,0:T(8,128)(2,1)S(1)}, bf16[256,768]{1,0:T(8,128)(2,1)S(1)}, u32[]{:S(2)}, u32[]{:S(2)}) collective-permute-start(bf16[256,768]{1,0:T(8,128)(2,1)S(1)} %collective-permute-done.23), channel_id=1, source_target_pairs={{1,0},{2,1},{3,2},{5,4},{6,5},{7,6},{9,8},{10,9},{11,10},{13,12},{... | collective-permute-start | bytes 1179656 | tf_op jit(solution)/shard_map/out_projection/ppermute | solution.py:81
  114.1 4.7 %collective-permute-start.12 = (bf16[2,256,256]{2,1,0:T(8,128)(2,1)S(1)}, bf16[2,256,256]{2,1,0:T(8,128)(2,1)S(1)}, u32[]{:S(2)}, u32[]{:S(2)}) collective-permute-start(bf16[2,256,256]{2,1,0:T(8,128)(2,1)S(1)} %get-tuple-element.28), channel_id=1, source_target_pairs={{4,0},{8,4},{12,8},{0,12},{5,1},{9,5},{13,9},{1,13},{6,2},{10,6},{... | collective-permute-start | bytes 786440 | tf_op jit(solution)/shard_map/kv_ring/ppermute | solution.py:206
  114.2 9.3 %collective-permute-start.11 = (bf16[2,256,256]{2,1,0:T(8,128)(2,1)S(1)}, bf16[2,256,256]{2,1,0:T(8,128)(2,1)S(1)}, u32[]{:S(2)}, u32[]{:S(2)}) collective-permute-start(bf16[2,256,256]{2,1,0:T(8,128)(2,1)S(1)} %get-tuple-element.27), channel_id=1, source_target_pairs={{0,4},{4,8},{8,12},{12,0},{1,5},{5,9},{9,13},{13,1},{2,6},{6,10},{... | collective-permute-start | bytes 786440 | tf_op jit(solution)/shard_map/kv_ring/ppermute | solution.py:205
  118.8 11.5 %collective-permute-start.14 = (bf16[2,256,256]{2,1,0:T(8,128)(2,1)S(1)}, bf16[2,256,256]{2,1,0:T(8,128)(2,1)S(1)}, u32[]{:S(2)}, u32[]{:S(2)}) collective-permute-start(bf16[2,256,256]{2,1,0:T(8,128)(2,1)S(1)} %collective-permute-done.12), channel_id=1, source_target_pairs={{4,0},{8,4},{12,8},{0,12},{5,1},{9,5},{13,9},{1,13},{6,2},{10,6},{... | collective-permute-start | bytes 786440 | tf_op jit(solution)/shard_map/kv_ring/ppermute | solution.py:206
  123.5 8.3 %collective-permute-start.13 = (bf16[2,256,256]{2,1,0:T(8,128)(2,1)S(1)}, bf16[2,256,256]{2,1,0:T(8,128)(2,1)S(1)}, u32[]{:S(2)}, u32[]{:S(2)}) collective-permute-start(bf16[2,256,256]{2,1,0:T(8,128)(2,1)S(1)} %collective-permute-done.11), channel_id=1, source_target_pairs={{0,4},{4,8},{8,12},{12,0},{1,5},{5,9},{9,13},{13,1},{2,6},{6,10},{... | collective-permute-start | bytes 786440 | tf_op jit(solution)/shard_map/kv_ring/ppermute | solution.py:205
  128.5 33.8 %collective-permute-start.26 = (bf16[1024,768]{1,0:T(8,128)(2,1)}, bf16[1024,768]{1,0:T(8,128)(2,1)}, u32[]{:S(2)}, u32[]{:S(2)}) collective-permute-start(bf16[1024,768]{1,0:T(8,128)(2,1)} %bitcast.63), channel_id=1, source_target_pairs={{0,4},{4,0},{8,12},{12,8},{1,5},{5,1},{9,13},{13,9},{2,6},{6,2},{1... | collective-permute-start | bytes 4718600 | tf_op jit(solution)/shard_map/out_projection/ppermute | solution.py:111
  130.3 3.9 %collective-permute-start.16 = (bf16[2,256,256]{2,1,0:T(8,128)(2,1)S(1)}, bf16[2,256,256]{2,1,0:T(8,128)(2,1)S(1)}, u32[]{:S(2)}, u32[]{:S(2)}) collective-permute-start(bf16[2,256,256]{2,1,0:T(8,128)(2,1)S(1)} %collective-permute-done.14), channel_id=1, source_target_pairs={{4,0},{8,4},{12,8},{0,12},{5,1},{9,5},{13,9},{1,13},{6,2},{10,6},{... | collective-permute-start | bytes 786440 | tf_op jit(solution)/shard_map/kv_ring/ppermute | solution.py:206
  131.8 8.3 %collective-permute-start.15 = (bf16[2,256,256]{2,1,0:T(8,128)(2,1)S(1)}, bf16[2,256,256]{2,1,0:T(8,128)(2,1)S(1)}, u32[]{:S(2)}, u32[]{:S(2)}) collective-permute-start(bf16[2,256,256]{2,1,0:T(8,128)(2,1)S(1)} %collective-permute-done.13), channel_id=1, source_target_pairs={{0,4},{4,8},{8,12},{12,0},{1,5},{5,9},{9,13},{13,1},{2,6},{6,10},{... | collective-permute-start | bytes 786440 | tf_op jit(solution)/shard_map/kv_ring/ppermute | solution.py:205
  146.7 11.7 %collective-permute-start.17 = (bf16[128,256]{1,0:T(8,128)(2,1)S(1)}, bf16[128,256]{1,0:T(8,128)(2,1)S(1)}, u32[]{:S(2)}, u32[]{:S(2)}) collective-permute-start(bf16[128,256]{1,0:T(8,128)(2,1)S(1)} %get-tuple-element.37), channel_id=1, source_target_pairs={{0,1},{1,2},{2,3},{3,0},{4,5},{5,6},{6,7},{7,4},{8,9},{9,10},{10,1... | collective-permute-start | bytes 196616 | tf_op jit(solution)/shard_map/out_projection/ppermute | solution.py:98
  155.7 6.3 %collective-permute-start.18 = (bf16[128,256]{1,0:T(8,128)(2,1)S(1)}, bf16[128,256]{1,0:T(8,128)(2,1)S(1)}, u32[]{:S(2)}, u32[]{:S(2)}) collective-permute-start(bf16[128,256]{1,0:T(8,128)(2,1)S(1)} %get-tuple-element.36), channel_id=1, source_target_pairs={{0,2},{1,3},{2,0},{3,1},{4,6},{5,7},{6,4},{7,5},{8,10},{9,11},{10,... | collective-permute-start | bytes 196616 | tf_op jit(solution)/shard_map/out_projection/ppermute | solution.py:98
  156.2 5.9 %collective-permute-start.19 = (bf16[128,256]{1,0:T(8,128)(2,1)S(1)}, bf16[128,256]{1,0:T(8,128)(2,1)S(1)}, u32[]{:S(2)}, u32[]{:S(2)}) collective-permute-start(bf16[128,256]{1,0:T(8,128)(2,1)S(1)} %get-tuple-element.35), channel_id=1, source_target_pairs={{0,3},{1,0},{2,1},{3,2},{4,7},{5,4},{6,5},{7,6},{8,11},{9,8},{10,9... | collective-permute-start | bytes 196616 | tf_op jit(solution)/shard_map/out_projection/ppermute | solution.py:98
  167.8 5.4 %collective-permute-start.27 = (bf16[8,256]{1,0:T(8,128)(2,1)S(1)}, bf16[8,256]{1,0:T(8,128)(2,1)S(1)}, u32[]{:S(2)}, u32[]{:S(2)}) collective-permute-start(bf16[8,256]{1,0:T(8,128)(2,1)S(1)} %get-tuple-element.63), channel_id=1, source_target_pairs={{0,1},{1,2},{2,3},{3,0},{4,5},{5,6},{6,7},{7,4},{8,9},{9,10},{10,1... | collective-permute-start | bytes 12296 | tf_op jit(solution)/shard_map/sides_gather/ppermute | solution.py:127
  169.6 4.5 %collective-permute-start.28 = (bf16[8,256]{1,0:T(8,128)(2,1)S(1)}, bf16[8,256]{1,0:T(8,128)(2,1)S(1)}, u32[]{:S(2)}, u32[]{:S(2)}) collective-permute-start(bf16[8,256]{1,0:T(8,128)(2,1)S(1)} %get-tuple-element.63), channel_id=1, source_target_pairs={{0,2},{1,3},{2,0},{3,1},{4,6},{5,7},{6,4},{7,5},{8,10},{9,11},{10,... | collective-permute-start | bytes 12296 | tf_op jit(solution)/shard_map/sides_gather/ppermute | solution.py:127
  171.3 3.6 %collective-permute-start.29 = (bf16[8,256]{1,0:T(8,128)(2,1)S(1)}, bf16[8,256]{1,0:T(8,128)(2,1)S(1)}, u32[]{:S(2)}, u32[]{:S(2)}) collective-permute-start(bf16[8,256]{1,0:T(8,128)(2,1)S(1)} %get-tuple-element.63), channel_id=1, source_target_pairs={{0,3},{1,0},{2,1},{3,2},{4,7},{5,4},{6,5},{7,6},{8,11},{9,8},{10,9... | collective-permute-start | bytes 12296 | tf_op jit(solution)/shard_map/sides_gather/ppermute | solution.py:127
  174.9 3.8 %collective-permute-start.31 = (bf16[32,256]{1,0:T(8,128)(2,1)S(1)}, bf16[32,256]{1,0:T(8,128)(2,1)S(1)}, u32[]{:S(2)}, u32[]{:S(2)}) collective-permute-start(bf16[32,256]{1,0:T(8,128)(2,1)S(1)} %bitcast.319), channel_id=1, source_target_pairs={{0,8},{4,12},{8,0},{12,4},{1,9},{5,13},{9,1},{13,5},{2,10},{6,14},... | collective-permute-start | bytes 49160 | tf_op jit(solution)/shard_map/sides_gather/ppermute | solution.py:127
  175.0 3.8 %collective-permute-start.32 = (bf16[32,256]{1,0:T(8,128)(2,1)S(1)}, bf16[32,256]{1,0:T(8,128)(2,1)S(1)}, u32[]{:S(2)}, u32[]{:S(2)}) collective-permute-start(bf16[32,256]{1,0:T(8,128)(2,1)S(1)} %bitcast.320), channel_id=1, source_target_pairs={{0,12},{4,0},{8,4},{12,8},{1,13},{5,1},{9,5},{13,9},{2,14},{6,2},{... | collective-permute-start | bytes 49160 | tf_op jit(solution)/shard_map/sides_gather/ppermute | solution.py:127
  (11 other events, 214.9 us)

commit v7 on v6

--- a/solution.py
+++ b/solution.py
@@ -166,6 +166,7 @@
     grouped = projected.reshape(local_rows, head_count, 2 * KEY_SIZE + VALUE_SIZE).transpose(1, 0, 2)
     queries = grouped[:, :, :KEY_SIZE]
     kv = grouped[:, :, KEY_SIZE:]
+    late_w_out, kv = lax.optimization_barrier((w_out, kv))
     scale = 1.0 / math.sqrt(KEY_SIZE)
 
     def attend(state, kv_block):
@@ -212,7 +213,6 @@
     attended = (weighted / running_sum[:, :, None]).astype(jnp.bfloat16)
     attended = attended.transpose(1, 0, 2).reshape(local_rows, head_count * VALUE_SIZE)
     with jax.named_scope("out_projection"):
-        late_w_out, unused = lax.optimization_barrier((w_out, kv))
         full_w_out = gather_weight_rows(late_w_out, "pair", "seq")
         own_heads = rows_to_heads(attended, "pair")
         mixed = jnp.dot(own_heads, full_w_out, preferred_element_type=jnp.float32)

time: 181 us -> 190 us (1.050)
  waiting for transfers between devices: 82.4 us -> 94.3 us
  local copies, waits for them, and re-layouts: 16 us -> 7.87 us
  other arithmetic: 2.39 us -> 5.24 us
    ppermute x3, waiting for transfers between devices: 0.01 us -> 11.1 us  [line_all_gather(): flow_r = lax.ppermute(flow_r, axis, right)]
    ppermute x3, waiting for transfers between devices: 9.47 us -> 1.09 us  [shards(): next_going = lax.ppermute(going, 'seq', forward)]
    ppermute x3, waiting for transfers between devices: 27.4 us -> 34.6 us  [direct_reduce_scatter(): lax.ppermute(outgoing, axis, [(i, (i + shift) % n) for i in range(n)])]
    ppermute x3, starting transfers between devices: 11.4 us -> 5.44 us  [rows_to_heads(): lax.ppermute(outgoing, axis, [(i, (i + shift) % n) for i in range(n)])]
    ppermute x3, starting transfers between devices: 12.9 us -> 18.1 us  [line_all_gather(): flow_r = lax.ppermute(flow_r, axis, right)]
    ppermute x3, waiting for transfers between devices: 10.3 us -> 5.16 us  [permute_all_to_all(): lax.ppermute(outgoing, axis, [(i, (i + shift) % n) for i in range(n)])]
    ppermute x3, waiting for transfers between devices: 0.01 us -> 4.96 us  [line_all_gather(): flow_l = lax.ppermute(flow_l, axis, left)]
    dynamic_update_slice x3, local copies, waits for them, and re-layouts: 3.34 us -> 0.1 us  [line_all_gather(): slots = lax.dynamic_update_index_in_dim(slots, flow_l, at_l, 0)]
  transfers between devices with their start and end apart: 33 -> 33, of which waited for: 18 -> 19; matrix products, arithmetic and copies ran while one was open for 17% -> 8% of each run, Pallas kernels for 0% -> 0%
where the time goes in v7:
time: 190 us
  waiting for transfers between devices  94.3 us (50%)
  starting transfers between devices  58.4 us (31%)
  matrix products  22.4 us (12%)
  local copies, waits for them, and re-layouts  7.87 us (4%)
  other arithmetic  5.24 us (3%)
    ppermute x3, waiting for transfers between devices, direct_reduce_scatter(): lax.ppermute(outgoing, axis, [(i, (i + shift) % n) for i in range(n)])  34.6 us
    ppermute x9, waiting for transfers between devices, direct_all_gather(): lax.ppermute(value, axis, [(i, (i + shift) % n) for i in range(n)])  28.5 us
    ppermute x3, starting transfers between devices, line_all_gather(): flow_r = lax.ppermute(flow_r, axis, right)  18.1 us
    ppermute x9, starting transfers between devices, direct_all_gather(): lax.ppermute(value, axis, [(i, (i + shift) % n) for i in range(n)])  12.8 us
    ppermute x3, waiting for transfers between devices, line_all_gather(): flow_r = lax.ppermute(flow_r, axis, right)  11.1 us
    ppermute x3, starting transfers between devices, permute_all_to_all(): lax.ppermute(outgoing, axis, [(i, (i + shift) % n) for i in range(n)])  7.13 us
    dot_general x5, matrix products, conv_rows(): jnp.dot(shifted, conv_weight[offset], preferred_element_type=jnp.float32)  6.46 us
    ppermute x3, starting transfers between devices, rows_to_heads(): lax.ppermute(outgoing, axis, [(i, (i + shift) % n) for i in range(n)])  5.44 us
  transfers between devices with their start and end apart: 33, of which 19 were waited for; matrix products, arithmetic and copies ran while one was open for 8% of the time, Pallas kernels for 0%

profile of v7, /device:TPU:0, one launch (start us, length us, event | category | flops | bytes accessed | tf_op | source)
XLA Modules:
  0.0 189.5 jit_solution(13217262968358840756)
XLA Ops:
  0.7 1.3 fusion.63
  4.1 3.1 %collective-permute-start = (bf16[128,384]{1,0:T(8,128)(2,1)S(1)}, bf16[128,384]{1,0:T(8,128)(2,1)S(1)}, u32[]{:S(2)}, u32[]{:S(2)}) collective-permute-start(bf16[128,384]{1,0:T(8,128)(2,1)S(1)} %bitcast.313), channel_id=1, source_target_pairs={{0,1},{1,2},{2,3},{3,0},{4,5},{5,6},{6,7},{7,4},{8,9},{9,10},{10,1... | collective-permute-start | bytes 294920 | tf_op jit(solution)/shard_map/ppermute | solution.py:65
  7.2 2.7 %collective-permute-start.1 = (bf16[128,384]{1,0:T(8,128)(2,1)S(1)}, bf16[128,384]{1,0:T(8,128)(2,1)S(1)}, u32[]{:S(2)}, u32[]{:S(2)}) collective-permute-start(bf16[128,384]{1,0:T(8,128)(2,1)S(1)} %bitcast.312), channel_id=1, source_target_pairs={{0,2},{1,3},{2,0},{3,1},{4,6},{5,7},{6,4},{7,5},{8,10},{9,11},{10,... | collective-permute-start | bytes 294920 | tf_op jit(solution)/shard_map/ppermute | solution.py:65
  9.9 1.4 collective-permute-start.2
  11.4 1.5 collective-permute-done
  12.9 3.5 %collective-permute-done.1 = bf16[128,384]{1,0:T(8,128)(2,1)S(1)} collective-permute-done((bf16[128,384]{1,0:T(8,128)(2,1)S(1)}, bf16[128,384]{1,0:T(8,128)(2,1)S(1)}, u32[]{:S(2)}, u32[]{:S(2)}) %collective-permute-start.1) | collective-permute-done | bytes 98336 | tf_op jit(solution)/shard_map/ppermute | solution.py:65
  16.6 1.6 collective-permute-start.4
  18.2 2.4 %fusion.37 = f32[512,1536]{1,0:T(8,128)S(1)} fusion(bf16[512,384]{1,0:T(8,128)(2,1)S(1)} %bitcast.291, bf16[5,384,1536]{2,1,0:T(8,128)(2,1)} %param.12), kind=kOutput, calls=%fused_computation.62 | convolution fusion | flops 603979776 | bytes 4718592 | tf_op jit(solution)/shard_map/conv_reduce/dot_general | solution.py:39
  20.6 2.9 %collective-permute-start.3 = (bf16[8,384]{1,0:T(8,128)(2,1)S(1)}, bf16[8,384]{1,0:T(8,128)(2,1)S(1)}, u32[]{:S(2)}, u32[]{:S(2)}) collective-permute-start(bf16[8,384]{1,0:T(8,128)(2,1)S(1)} %get-tuple-element.33), channel_id=1, source_target_pairs={{0,4},{4,8},{8,12},{1,5},{5,9},{9,13},{2,6},{6,10},{10,14},{3,7},{... | collective-permute-start | bytes 18440 | tf_op jit(solution)/shard_map/ppermute | solution.py:25
  27.8 3.5 %collective-permute-start.7 = (bf16[128,1536]{1,0:T(8,128)(2,1)S(1)}, bf16[128,1536]{1,0:T(8,128)(2,1)S(1)}, u32[]{:S(2)}, u32[]{:S(2)}) collective-permute-start(bf16[128,1536]{1,0:T(8,128)(2,1)S(1)} %get-tuple-element.29), channel_id=1, source_target_pairs={{0,3},{1,0},{2,1},{3,2},{4,7},{5,4},{6,5},{7,6},{8,11},{9,8},{10,9... | collective-permute-start | bytes 1179656 | tf_op jit(solution)/shard_map/conv_reduce/ppermute | solution.py:51
  32.0 8.6 %collective-permute-done.7 = bf16[128,1536]{1,0:T(8,128)(2,1)S(1)} collective-permute-done((bf16[128,1536]{1,0:T(8,128)(2,1)S(1)}, bf16[128,1536]{1,0:T(8,128)(2,1)S(1)}, u32[]{:S(2)}, u32[]{:S(2)}) %collective-permute-start.7) | collective-permute-done | bytes 393248 | tf_op jit(solution)/shard_map/conv_reduce/ppermute | solution.py:51
  40.6 26.0 %collective-permute-done.6 = bf16[128,1536]{1,0:T(8,128)(2,1)S(1)} collective-permute-done((bf16[128,1536]{1,0:T(8,128)(2,1)S(1)}, bf16[128,1536]{1,0:T(8,128)(2,1)S(1)}, u32[]{:S(2)}, u32[]{:S(2)}) %collective-permute-start.6) | collective-permute-done | bytes 393248 | tf_op jit(solution)/shard_map/conv_reduce/ppermute | solution.py:51
  69.1 1.9 collective-permute-start.9
  71.0 2.9 %collective-permute-start.10 = (bf16[128,1536]{1,0:T(8,128)(2,1)S(1)}, bf16[128,1536]{1,0:T(8,128)(2,1)S(1)}, u32[]{:S(2)}, u32[]{:S(2)}) collective-permute-start(bf16[128,1536]{1,0:T(8,128)(2,1)S(1)} %get-tuple-element.25), channel_id=1, source_target_pairs={{0,3},{1,0},{2,1},{3,2},{4,7},{5,4},{6,5},{7,6},{8,11},{9,8},{10,9... | collective-permute-start | bytes 1179656 | tf_op jit(solution)/shard_map/attn_in_gather/ppermute | solution.py:127
  73.9 9.1 %collective-permute-done.8 = bf16[128,1536]{1,0:T(8,128)(2,1)S(1)} collective-permute-done((bf16[128,1536]{1,0:T(8,128)(2,1)S(1)}, bf16[128,1536]{1,0:T(8,128)(2,1)S(1)}, u32[]{:S(2)}, u32[]{:S(2)}) %collective-permute-start.8) | collective-permute-done | bytes 393248 | tf_op jit(solution)/shard_map/attn_in_gather/ppermute | solution.py:127
  83.8 15.1 %collective-permute-done.9 = bf16[128,1536]{1,0:T(8,128)(2,1)S(1)} collective-permute-done((bf16[128,1536]{1,0:T(8,128)(2,1)S(1)}, bf16[128,1536]{1,0:T(8,128)(2,1)S(1)}, u32[]{:S(2)}, u32[]{:S(2)}) %collective-permute-start.9) | collective-permute-done | bytes 393248 | tf_op jit(solution)/shard_map/attn_in_gather/ppermute | solution.py:127
  100.4 2.8 %convolution_convert_fusion = bf16[512,768]{1,0:T(8,128)(2,1)S(1)} fusion(bf16[512,1536]{1,0:T(8,128)(2,1)} %bitcast.22, bf16[1536,768]{1,0:T(8,128)(2,1)S(1)} %copy-done), kind=kOutput, calls=%fused_computation.14 | convolution fusion | flops 1208352768 | bytes 4718592 | tf_op jit(solution)/shard_map/dot_general | solution.py:164
  104.6 9.4 %collective-permute-start.20 = (bf16[256,768]{1,0:T(8,128)(2,1)S(1)}, bf16[256,768]{1,0:T(8,128)(2,1)S(1)}, u32[]{:S(2)}, u32[]{:S(2)}) collective-permute-start(bf16[256,768]{1,0:T(8,128)(2,1)S(1)} %get-tuple-element.7), channel_id=1, source_target_pairs={{0,1},{1,2},{2,3},{4,5},{5,6},{6,7},{8,9},{9,10},{10,11},{12,13},{... | collective-permute-start | bytes 1179656 | tf_op jit(solution)/shard_map/out_projection/ppermute | solution.py:80
  117.2 5.7 %collective-permute-done.20 = bf16[256,768]{1,0:T(8,128)(2,1)S(1)} collective-permute-done((bf16[256,768]{1,0:T(8,128)(2,1)S(1)}, bf16[256,768]{1,0:T(8,128)(2,1)S(1)}, u32[]{:S(2)}, u32[]{:S(2)}) %collective-permute-start.20) | collective-permute-done | bytes 393248 | tf_op jit(solution)/shard_map/out_projection/ppermute | solution.py:80
  123.0 4.4 %collective-permute-start.22 = (bf16[256,768]{1,0:T(8,128)(2,1)S(1)}, bf16[256,768]{1,0:T(8,128)(2,1)S(1)}, u32[]{:S(2)}, u32[]{:S(2)}) collective-permute-start(bf16[256,768]{1,0:T(8,128)(2,1)S(1)} %collective-permute-done.20), channel_id=1, source_target_pairs={{0,1},{1,2},{2,3},{4,5},{5,6},{6,7},{8,9},{9,10},{10,11},{12,13},{... | collective-permute-start | bytes 1179656 | tf_op jit(solution)/shard_map/out_projection/ppermute | solution.py:80
  130.3 5.4 %collective-permute-done.16 = bf16[2,256,256]{2,1,0:T(8,128)(2,1)S(1)} collective-permute-done((bf16[2,256,256]{2,1,0:T(8,128)(2,1)S(1)}, bf16[2,256,256]{2,1,0:T(8,128)(2,1)S(1)}, u32[]{:S(2)}, u32[]{:S(2)}) %collective-permute-start.16) | collective-permute-done | bytes 262176 | tf_op jit(solution)/shard_map/kv_ring/ppermute | solution.py:207
  139.8 4.4 %collective-permute-start.24 = (bf16[256,768]{1,0:T(8,128)(2,1)S(1)}, bf16[256,768]{1,0:T(8,128)(2,1)S(1)}, u32[]{:S(2)}, u32[]{:S(2)}) collective-permute-start(bf16[256,768]{1,0:T(8,128)(2,1)S(1)} %collective-permute-done.22), channel_id=1, source_target_pairs={{0,1},{1,2},{2,3},{4,5},{5,6},{6,7},{8,9},{9,10},{10,11},{12,13},{... | collective-permute-start | bytes 1179656 | tf_op jit(solution)/shard_map/out_projection/ppermute | solution.py:80
  146.4 5.3 %collective-permute-done.24 = bf16[256,768]{1,0:T(8,128)(2,1)S(1)} collective-permute-done((bf16[256,768]{1,0:T(8,128)(2,1)S(1)}, bf16[256,768]{1,0:T(8,128)(2,1)S(1)}, u32[]{:S(2)}, u32[]{:S(2)}) %collective-permute-start.24) | collective-permute-done | bytes 393248 | tf_op jit(solution)/shard_map/out_projection/ppermute | solution.py:80
  151.8 5.0 %collective-permute-done.25 = bf16[256,768]{1,0:T(8,128)(2,1)S(1)} collective-permute-done((bf16[256,768]{1,0:T(8,128)(2,1)S(1)}, bf16[256,768]{1,0:T(8,128)(2,1)S(1)}, u32[]{:S(2)}, u32[]{:S(2)}) %collective-permute-start.25) | collective-permute-done | bytes 393248 | tf_op jit(solution)/shard_map/out_projection/ppermute | solution.py:81
  160.9 1.3 collective-permute-start.17
  163.5 2.8 %collective-permute-start.19 = (bf16[128,256]{1,0:T(8,128)(2,1)S(1)}, bf16[128,256]{1,0:T(8,128)(2,1)S(1)}, u32[]{:S(2)}, u32[]{:S(2)}) collective-permute-start(bf16[128,256]{1,0:T(8,128)(2,1)S(1)} %get-tuple-element.39), channel_id=1, source_target_pairs={{0,3},{1,0},{2,1},{3,2},{4,7},{5,4},{6,5},{7,6},{8,11},{9,8},{10,9... | collective-permute-start | bytes 196616 | tf_op jit(solution)/shard_map/out_projection/ppermute | solution.py:98
  167.6 2.5 %collective-permute-done.18 = bf16[128,256]{1,0:T(8,128)(2,1)S(1)} collective-permute-done((bf16[128,256]{1,0:T(8,128)(2,1)S(1)}, bf16[128,256]{1,0:T(8,128)(2,1)S(1)}, u32[]{:S(2)}, u32[]{:S(2)}) %collective-permute-start.18) | collective-permute-done | bytes 65568 | tf_op jit(solution)/shard_map/out_projection/ppermute | solution.py:98
  170.5 5.0 %convert_reduce_fusion = (f32[8,1536]{1,0:T(8,128)S(1)}, bf16[128,1536]{1,0:T(8,128)(2,1)}) fusion(bf16[128,1024]{0,1:T(8,128)(2,1)S(1)} %bitcast.309, bf16[1024,768]{1,0:T(8,128)(2,1)} %collective-permute-done.26, bf16[1024,768]{1,0:T(8,128)(2,1)} %bitcast.63, pred[]{:T(512)S(6)} %eq.29, bf16[128,1536]{1,0:T(8,128)(2,1)S(1)} %get-tuple-element.27), kind=kOutput, calls=%fused_computation.105 | convolution fusion | flops 417779712 | bytes 4243457 | tf_op jit(solution)/shard_map/out_projection/dot_general | solution.py:218
  175.9 1.8 collective-permute-start.27
  177.7 1.7 collective-permute-start.28
  183.0 2.3 %collective-permute-start.31 = (bf16[32,256]{1,0:T(8,128)(2,1)S(1)}, bf16[32,256]{1,0:T(8,128)(2,1)S(1)}, u32[]{:S(2)}, u32[]{:S(2)}) collective-permute-start(bf16[32,256]{1,0:T(8,128)(2,1)S(1)} %bitcast.318), channel_id=1, source_target_pairs={{0,8},{4,12},{8,0},{12,4},{1,9},{5,13},{9,1},{13,5},{2,10},{6,14},... | collective-permute-start | bytes 49160 | tf_op jit(solution)/shard_map/sides_gather/ppermute | solution.py:127
  185.4 1.4 collective-permute-start.32
  (143 shorter events, 39.6 us)
Async XLA Ops:
  4.1 8.7 %collective-permute-start = (bf16[128,384]{1,0:T(8,128)(2,1)S(1)}, bf16[128,384]{1,0:T(8,128)(2,1)S(1)}, u32[]{:S(2)}, u32[]{:S(2)}) collective-permute-start(bf16[128,384]{1,0:T(8,128)(2,1)S(1)} %bitcast.313), channel_id=1, source_target_pairs={{0,1},{1,2},{2,3},{3,0},{4,5},{5,6},{6,7},{7,4},{8,9},{9,10},{10,1... | collective-permute-start | bytes 294920 | tf_op jit(solution)/shard_map/ppermute | solution.py:65
  7.2 9.2 %collective-permute-start.1 = (bf16[128,384]{1,0:T(8,128)(2,1)S(1)}, bf16[128,384]{1,0:T(8,128)(2,1)S(1)}, u32[]{:S(2)}, u32[]{:S(2)}) collective-permute-start(bf16[128,384]{1,0:T(8,128)(2,1)S(1)} %bitcast.312), channel_id=1, source_target_pairs={{0,2},{1,3},{2,0},{3,1},{4,6},{5,7},{6,4},{7,5},{8,10},{9,11},{10,... | collective-permute-start | bytes 294920 | tf_op jit(solution)/shard_map/ppermute | solution.py:65
  9.9 6.7 %collective-permute-start.2 = (bf16[128,384]{1,0:T(8,128)(2,1)S(1)}, bf16[128,384]{1,0:T(8,128)(2,1)S(1)}, u32[]{:S(2)}, u32[]{:S(2)}) collective-permute-start(bf16[128,384]{1,0:T(8,128)(2,1)S(1)} %bitcast.311), channel_id=1, source_target_pairs={{0,3},{1,0},{2,1},{3,2},{4,7},{5,4},{6,5},{7,6},{8,11},{9,8},{10,9... | collective-permute-start | bytes 294920 | tf_op jit(solution)/shard_map/ppermute | solution.py:65
  16.6 6.9 %collective-permute-start.4 = (bf16[8,384]{1,0:T(8,128)(2,1)S(1)}, bf16[8,384]{1,0:T(8,128)(2,1)S(1)}, u32[]{:S(2)}, u32[]{:S(2)}) collective-permute-start(bf16[8,384]{1,0:T(8,128)(2,1)S(1)} %get-tuple-element.34), channel_id=1, source_target_pairs={{4,0},{8,4},{12,8},{5,1},{9,5},{13,9},{6,2},{10,6},{14,10},{7,3},{... | collective-permute-start | bytes 18440 | tf_op jit(solution)/shard_map/ppermute | solution.py:26
  20.6 4.9 %collective-permute-start.3 = (bf16[8,384]{1,0:T(8,128)(2,1)S(1)}, bf16[8,384]{1,0:T(8,128)(2,1)S(1)}, u32[]{:S(2)}, u32[]{:S(2)}) collective-permute-start(bf16[8,384]{1,0:T(8,128)(2,1)S(1)} %get-tuple-element.33), channel_id=1, source_target_pairs={{0,4},{4,8},{8,12},{1,5},{5,9},{9,13},{2,6},{6,10},{10,14},{3,7},{... | collective-permute-start | bytes 18440 | tf_op jit(solution)/shard_map/ppermute | solution.py:25
  27.8 12.8 %collective-permute-start.7 = (bf16[128,1536]{1,0:T(8,128)(2,1)S(1)}, bf16[128,1536]{1,0:T(8,128)(2,1)S(1)}, u32[]{:S(2)}, u32[]{:S(2)}) collective-permute-start(bf16[128,1536]{1,0:T(8,128)(2,1)S(1)} %get-tuple-element.29), channel_id=1, source_target_pairs={{0,3},{1,0},{2,1},{3,2},{4,7},{5,4},{6,5},{7,6},{8,11},{9,8},{10,9... | collective-permute-start | bytes 1179656 | tf_op jit(solution)/shard_map/conv_reduce/ppermute | solution.py:51
  31.3 35.2 %collective-permute-start.6 = (bf16[128,1536]{1,0:T(8,128)(2,1)S(1)}, bf16[128,1536]{1,0:T(8,128)(2,1)S(1)}, u32[]{:S(2)}, u32[]{:S(2)}) collective-permute-start(bf16[128,1536]{1,0:T(8,128)(2,1)S(1)} %get-tuple-element.30), channel_id=1, source_target_pairs={{0,2},{1,3},{2,0},{3,1},{4,6},{5,7},{6,4},{7,5},{8,10},{9,11},{10,... | collective-permute-start | bytes 1179656 | tf_op jit(solution)/shard_map/conv_reduce/ppermute | solution.py:51
  31.7 34.9 %collective-permute-start.5 = (bf16[128,1536]{1,0:T(8,128)(2,1)S(1)}, bf16[128,1536]{1,0:T(8,128)(2,1)S(1)}, u32[]{:S(2)}, u32[]{:S(2)}) collective-permute-start(bf16[128,1536]{1,0:T(8,128)(2,1)S(1)} %get-tuple-element.28), channel_id=1, source_target_pairs={{0,1},{1,2},{2,3},{3,0},{4,5},{5,6},{6,7},{7,4},{8,9},{9,10},{10,1... | collective-permute-start | bytes 1179656 | tf_op jit(solution)/shard_map/conv_reduce/ppermute | solution.py:51
  69.1 13.9 %collective-permute-start.8 = (bf16[128,1536]{1,0:T(8,128)(2,1)S(1)}, bf16[128,1536]{1,0:T(8,128)(2,1)S(1)}, u32[]{:S(2)}, u32[]{:S(2)}) collective-permute-start(bf16[128,1536]{1,0:T(8,128)(2,1)S(1)} %get-tuple-element.25), channel_id=1, source_target_pairs={{0,1},{1,2},{2,3},{3,0},{4,5},{5,6},{6,7},{7,4},{8,9},{9,10},{10,1... | collective-permute-start | bytes 1179656 | tf_op jit(solution)/shard_map/attn_in_gather/ppermute | solution.py:127
  69.1 29.8 %collective-permute-start.9 = (bf16[128,1536]{1,0:T(8,128)(2,1)S(1)}, bf16[128,1536]{1,0:T(8,128)(2,1)S(1)}, u32[]{:S(2)}, u32[]{:S(2)}) collective-permute-start(bf16[128,1536]{1,0:T(8,128)(2,1)S(1)} %get-tuple-element.25), channel_id=1, source_target_pairs={{0,2},{1,3},{2,0},{3,1},{4,6},{5,7},{6,4},{7,5},{8,10},{9,11},{10,... | collective-permute-start | bytes 1179656 | tf_op jit(solution)/shard_map/attn_in_gather/ppermute | solution.py:127
  71.0 28.7 %collective-permute-start.10 = (bf16[128,1536]{1,0:T(8,128)(2,1)S(1)}, bf16[128,1536]{1,0:T(8,128)(2,1)S(1)}, u32[]{:S(2)}, u32[]{:S(2)}) collective-permute-start(bf16[128,1536]{1,0:T(8,128)(2,1)S(1)} %get-tuple-element.25), channel_id=1, source_target_pairs={{0,3},{1,0},{2,1},{3,2},{4,7},{5,4},{6,5},{7,6},{8,11},{9,8},{10,9... | collective-permute-start | bytes 1179656 | tf_op jit(solution)/shard_map/attn_in_gather/ppermute | solution.py:127
  103.7 11.8 %collective-permute-start.12 = (bf16[2,256,256]{2,1,0:T(8,128)(2,1)S(1)}, bf16[2,256,256]{2,1,0:T(8,128)(2,1)S(1)}, u32[]{:S(2)}, u32[]{:S(2)}) collective-permute-start(bf16[2,256,256]{2,1,0:T(8,128)(2,1)S(1)} %get-tuple-element.32), channel_id=1, source_target_pairs={{4,0},{8,4},{12,8},{0,12},{5,1},{9,5},{13,9},{1,13},{6,2},{10,6},{... | collective-permute-start | bytes 786440 | tf_op jit(solution)/shard_map/kv_ring/ppermute | solution.py:207
  103.8 12.8 %collective-permute-start.11 = (bf16[2,256,256]{2,1,0:T(8,128)(2,1)S(1)}, bf16[2,256,256]{2,1,0:T(8,128)(2,1)S(1)}, u32[]{:S(2)}, u32[]{:S(2)}) collective-permute-start(bf16[2,256,256]{2,1,0:T(8,128)(2,1)S(1)} %get-tuple-element.31), channel_id=1, source_target_pairs={{0,4},{4,8},{8,12},{12,0},{1,5},{5,9},{9,13},{13,1},{2,6},{6,10},{... | collective-permute-start | bytes 786440 | tf_op jit(solution)/shard_map/kv_ring/ppermute | solution.py:206
  104.6 18.3 %collective-permute-start.20 = (bf16[256,768]{1,0:T(8,128)(2,1)S(1)}, bf16[256,768]{1,0:T(8,128)(2,1)S(1)}, u32[]{:S(2)}, u32[]{:S(2)}) collective-permute-start(bf16[256,768]{1,0:T(8,128)(2,1)S(1)} %get-tuple-element.7), channel_id=1, source_target_pairs={{0,1},{1,2},{2,3},{4,5},{5,6},{6,7},{8,9},{9,10},{10,11},{12,13},{... | collective-permute-start | bytes 1179656 | tf_op jit(solution)/shard_map/out_projection/ppermute | solution.py:80
  114.0 13.4 %collective-permute-start.21 = (bf16[256,768]{1,0:T(8,128)(2,1)S(1)}, bf16[256,768]{1,0:T(8,128)(2,1)S(1)}, u32[]{:S(2)}, u32[]{:S(2)}) collective-permute-start(bf16[256,768]{1,0:T(8,128)(2,1)S(1)} %get-tuple-element.7), channel_id=1, source_target_pairs={{1,0},{2,1},{3,2},{5,4},{6,5},{7,6},{9,8},{10,9},{11,10},{13,12},{... | collective-permute-start | bytes 1179656 | tf_op jit(solution)/shard_map/out_projection/ppermute | solution.py:81
  115.6 13.2 %collective-permute-start.14 = (bf16[2,256,256]{2,1,0:T(8,128)(2,1)S(1)}, bf16[2,256,256]{2,1,0:T(8,128)(2,1)S(1)}, u32[]{:S(2)}, u32[]{:S(2)}) collective-permute-start(bf16[2,256,256]{2,1,0:T(8,128)(2,1)S(1)} %collective-permute-done.12), channel_id=1, source_target_pairs={{4,0},{8,4},{12,8},{0,12},{5,1},{9,5},{13,9},{1,13},{6,2},{10,6},{... | collective-permute-start | bytes 786440 | tf_op jit(solution)/shard_map/kv_ring/ppermute | solution.py:207
  116.6 13.1 %collective-permute-start.13 = (bf16[2,256,256]{2,1,0:T(8,128)(2,1)S(1)}, bf16[2,256,256]{2,1,0:T(8,128)(2,1)S(1)}, u32[]{:S(2)}, u32[]{:S(2)}) collective-permute-start(bf16[2,256,256]{2,1,0:T(8,128)(2,1)S(1)} %collective-permute-done.11), channel_id=1, source_target_pairs={{0,4},{4,8},{8,12},{12,0},{1,5},{5,9},{9,13},{13,1},{2,6},{6,10},{... | collective-permute-start | bytes 786440 | tf_op jit(solution)/shard_map/kv_ring/ppermute | solution.py:206
  123.0 16.8 %collective-permute-start.22 = (bf16[256,768]{1,0:T(8,128)(2,1)S(1)}, bf16[256,768]{1,0:T(8,128)(2,1)S(1)}, u32[]{:S(2)}, u32[]{:S(2)}) collective-permute-start(bf16[256,768]{1,0:T(8,128)(2,1)S(1)} %collective-permute-done.20), channel_id=1, source_target_pairs={{0,1},{1,2},{2,3},{4,5},{5,6},{6,7},{8,9},{9,10},{10,11},{12,13},{... | collective-permute-start | bytes 1179656 | tf_op jit(solution)/shard_map/out_projection/ppermute | solution.py:80
  127.4 17.6 %collective-permute-start.23 = (bf16[256,768]{1,0:T(8,128)(2,1)S(1)}, bf16[256,768]{1,0:T(8,128)(2,1)S(1)}, u32[]{:S(2)}, u32[]{:S(2)}) collective-permute-start(bf16[256,768]{1,0:T(8,128)(2,1)S(1)} %collective-permute-done.21), channel_id=1, source_target_pairs={{1,0},{2,1},{3,2},{5,4},{6,5},{7,6},{9,8},{10,9},{11,10},{13,12},{... | collective-permute-start | bytes 1179656 | tf_op jit(solution)/shard_map/out_projection/ppermute | solution.py:81
  128.8 6.9 %collective-permute-start.16 = (bf16[2,256,256]{2,1,0:T(8,128)(2,1)S(1)}, bf16[2,256,256]{2,1,0:T(8,128)(2,1)S(1)}, u32[]{:S(2)}, u32[]{:S(2)}) collective-permute-start(bf16[2,256,256]{2,1,0:T(8,128)(2,1)S(1)} %collective-permute-done.14), channel_id=1, source_target_pairs={{4,0},{8,4},{12,8},{0,12},{5,1},{9,5},{13,9},{1,13},{6,2},{10,6},{... | collective-permute-start | bytes 786440 | tf_op jit(solution)/shard_map/kv_ring/ppermute | solution.py:207
  129.7 7.3 %collective-permute-start.15 = (bf16[2,256,256]{2,1,0:T(8,128)(2,1)S(1)}, bf16[2,256,256]{2,1,0:T(8,128)(2,1)S(1)}, u32[]{:S(2)}, u32[]{:S(2)}) collective-permute-start(bf16[2,256,256]{2,1,0:T(8,128)(2,1)S(1)} %collective-permute-done.13), channel_id=1, source_target_pairs={{0,4},{4,8},{8,12},{12,0},{1,5},{5,9},{9,13},{13,1},{2,6},{6,10},{... | collective-permute-start | bytes 786440 | tf_op jit(solution)/shard_map/kv_ring/ppermute | solution.py:206
  139.8 11.9 %collective-permute-start.24 = (bf16[256,768]{1,0:T(8,128)(2,1)S(1)}, bf16[256,768]{1,0:T(8,128)(2,1)S(1)}, u32[]{:S(2)}, u32[]{:S(2)}) collective-permute-start(bf16[256,768]{1,0:T(8,128)(2,1)S(1)} %collective-permute-done.22), channel_id=1, source_target_pairs={{0,1},{1,2},{2,3},{4,5},{5,6},{6,7},{8,9},{9,10},{10,11},{12,13},{... | collective-permute-start | bytes 1179656 | tf_op jit(solution)/shard_map/out_projection/ppermute | solution.py:80
  145.0 11.7 %collective-permute-start.25 = (bf16[256,768]{1,0:T(8,128)(2,1)S(1)}, bf16[256,768]{1,0:T(8,128)(2,1)S(1)}, u32[]{:S(2)}, u32[]{:S(2)}) collective-permute-start(bf16[256,768]{1,0:T(8,128)(2,1)S(1)} %collective-permute-done.23), channel_id=1, source_target_pairs={{1,0},{2,1},{3,2},{5,4},{6,5},{7,6},{9,8},{10,9},{11,10},{13,12},{... | collective-permute-start | bytes 1179656 | tf_op jit(solution)/shard_map/out_projection/ppermute | solution.py:81
  158.0 12.5 %collective-permute-start.26 = (bf16[1024,768]{1,0:T(8,128)(2,1)}, bf16[1024,768]{1,0:T(8,128)(2,1)}, u32[]{:S(2)}, u32[]{:S(2)}) collective-permute-start(bf16[1024,768]{1,0:T(8,128)(2,1)} %bitcast.63), channel_id=1, source_target_pairs={{0,4},{4,0},{8,12},{12,8},{1,5},{5,1},{9,13},{13,9},{2,6},{6,2},{1... | collective-permute-start | bytes 4718600 | tf_op jit(solution)/shard_map/out_projection/ppermute | solution.py:111
  160.9 6.6 %collective-permute-start.17 = (bf16[128,256]{1,0:T(8,128)(2,1)S(1)}, bf16[128,256]{1,0:T(8,128)(2,1)S(1)}, u32[]{:S(2)}, u32[]{:S(2)}) collective-permute-start(bf16[128,256]{1,0:T(8,128)(2,1)S(1)} %get-tuple-element.41), channel_id=1, source_target_pairs={{0,1},{1,2},{2,3},{3,0},{4,5},{5,6},{6,7},{7,4},{8,9},{9,10},{10,1... | collective-permute-start | bytes 196616 | tf_op jit(solution)/shard_map/out_projection/ppermute | solution.py:98
  162.3 7.9 %collective-permute-start.18 = (bf16[128,256]{1,0:T(8,128)(2,1)S(1)}, bf16[128,256]{1,0:T(8,128)(2,1)S(1)}, u32[]{:S(2)}, u32[]{:S(2)}) collective-permute-start(bf16[128,256]{1,0:T(8,128)(2,1)S(1)} %get-tuple-element.40), channel_id=1, source_target_pairs={{0,2},{1,3},{2,0},{3,1},{4,6},{5,7},{6,4},{7,5},{8,10},{9,11},{10,... | collective-permute-start | bytes 196616 | tf_op jit(solution)/shard_map/out_projection/ppermute | solution.py:98
  163.5 6.7 %collective-permute-start.19 = (bf16[128,256]{1,0:T(8,128)(2,1)S(1)}, bf16[128,256]{1,0:T(8,128)(2,1)S(1)}, u32[]{:S(2)}, u32[]{:S(2)}) collective-permute-start(bf16[128,256]{1,0:T(8,128)(2,1)S(1)} %get-tuple-element.39), channel_id=1, source_target_pairs={{0,3},{1,0},{2,1},{3,2},{4,7},{5,4},{6,5},{7,6},{8,11},{9,8},{10,9... | collective-permute-start | bytes 196616 | tf_op jit(solution)/shard_map/out_projection/ppermute | solution.py:98
  175.9 5.4 %collective-permute-start.27 = (bf16[8,256]{1,0:T(8,128)(2,1)S(1)}, bf16[8,256]{1,0:T(8,128)(2,1)S(1)}, u32[]{:S(2)}, u32[]{:S(2)}) collective-permute-start(bf16[8,256]{1,0:T(8,128)(2,1)S(1)} %get-tuple-element.67), channel_id=1, source_target_pairs={{0,1},{1,2},{2,3},{3,0},{4,5},{5,6},{6,7},{7,4},{8,9},{9,10},{10,1... | collective-permute-start | bytes 12296 | tf_op jit(solution)/shard_map/sides_gather/ppermute | solution.py:127
  177.7 4.5 %collective-permute-start.28 = (bf16[8,256]{1,0:T(8,128)(2,1)S(1)}, bf16[8,256]{1,0:T(8,128)(2,1)S(1)}, u32[]{:S(2)}, u32[]{:S(2)}) collective-permute-start(bf16[8,256]{1,0:T(8,128)(2,1)S(1)} %get-tuple-element.67), channel_id=1, source_target_pairs={{0,2},{1,3},{2,0},{3,1},{4,6},{5,7},{6,4},{7,5},{8,10},{9,11},{10,... | collective-permute-start | bytes 12296 | tf_op jit(solution)/shard_map/sides_gather/ppermute | solution.py:127
  179.4 3.6 %collective-permute-start.29 = (bf16[8,256]{1,0:T(8,128)(2,1)S(1)}, bf16[8,256]{1,0:T(8,128)(2,1)S(1)}, u32[]{:S(2)}, u32[]{:S(2)}) collective-permute-start(bf16[8,256]{1,0:T(8,128)(2,1)S(1)} %get-tuple-element.67), channel_id=1, source_target_pairs={{0,3},{1,0},{2,1},{3,2},{4,7},{5,4},{6,5},{7,6},{8,11},{9,8},{10,9... | collective-permute-start | bytes 12296 | tf_op jit(solution)/shard_map/sides_gather/ppermute | solution.py:127
  183.0 3.8 %collective-permute-start.30 = (bf16[32,256]{1,0:T(8,128)(2,1)S(1)}, bf16[32,256]{1,0:T(8,128)(2,1)S(1)}, u32[]{:S(2)}, u32[]{:S(2)}) collective-permute-start(bf16[32,256]{1,0:T(8,128)(2,1)S(1)} %bitcast.317), channel_id=1, source_target_pairs={{0,4},{4,8},{8,12},{12,0},{1,5},{5,9},{9,13},{13,1},{2,6},{6,10},{... | collective-permute-start | bytes 49160 | tf_op jit(solution)/shard_map/sides_gather/ppermute | solution.py:127
  183.0 4.0 %collective-permute-start.31 = (bf16[32,256]{1,0:T(8,128)(2,1)S(1)}, bf16[32,256]{1,0:T(8,128)(2,1)S(1)}, u32[]{:S(2)}, u32[]{:S(2)}) collective-permute-start(bf16[32,256]{1,0:T(8,128)(2,1)S(1)} %bitcast.318), channel_id=1, source_target_pairs={{0,8},{4,12},{8,0},{12,4},{1,9},{5,13},{9,1},{13,5},{2,10},{6,14},... | collective-permute-start | bytes 49160 | tf_op jit(solution)/shard_map/sides_gather/ppermute | solution.py:127
  (10 other events, 232.1 us)

commit v8 on v7

--- a/solution.py
+++ b/solution.py
@@ -166,7 +166,6 @@
     grouped = projected.reshape(local_rows, head_count, 2 * KEY_SIZE + VALUE_SIZE).transpose(1, 0, 2)
     queries = grouped[:, :, :KEY_SIZE]
     kv = grouped[:, :, KEY_SIZE:]
-    late_w_out, kv = lax.optimization_barrier((w_out, kv))
     scale = 1.0 / math.sqrt(KEY_SIZE)
 
     def attend(state, kv_block):
@@ -212,10 +211,10 @@
     running_max, running_sum, weighted = state
     attended = (weighted / running_sum[:, :, None]).astype(jnp.bfloat16)
     attended = attended.transpose(1, 0, 2).reshape(local_rows, head_count * VALUE_SIZE)
-    with jax.named_scope("out_projection"):
-        full_w_out = gather_weight_rows(late_w_out, "pair", "seq")
-        own_heads = rows_to_heads(attended, "pair")
-        mixed = jnp.dot(own_heads, full_w_out, preferred_element_type=jnp.float32)
+    with jax.named_scope("out_reduce"):
+        mixed = direct_reduce_scatter(
+            jnp.dot(attended, w_out, preferred_element_type=jnp.float32), "pair"
+        )
     seq_out = (first_out.astype(jnp.float32) + mixed).astype(jnp.bfloat16)
     bin_count = row_count // POOL
     pooled = jnp.mean(seq_out.astype(jnp.float32).reshape(bin_count, POOL, channels), axis=1)

time: 190 us -> 184 us (0.968)
  local copies, waits for them, and re-layouts: 7.87 us -> 2.22 us
  matrix products: 22.4 us -> 17.7 us
  waiting for transfers between devices: 94.3 us -> 98 us
    ppermute x10 -> x0, starting transfers between devices: 27.4 us -> none  [the longest x3 18.1 us: line_all_gather(): flow_r = lax.ppermute(flow_r, axis, right)]
    ppermute x10 -> x0, waiting for transfers between devices: 19.7 us -> none  [the longest x3 11.1 us: line_all_gather(): flow_r = lax.ppermute(flow_r, axis, right)]
    ppermute x3 -> x6, waiting for transfers between devices: 34.6 us -> 50.8 us  [direct_reduce_scatter(): lax.ppermute(outgoing, axis, [(i, (i + shift) % n) for i in range(n)])]
    ppermute x3 -> x6, starting transfers between devices: 4.19 us -> 17.1 us  [direct_reduce_scatter(): lax.ppermute(outgoing, axis, [(i, (i + shift) % n) for i in range(n)])]
    ppermute x9, starting transfers between devices: 12.8 us -> 25.2 us  [direct_all_gather(): lax.ppermute(value, axis, [(i, (i + shift) % n) for i in range(n)])]
    ppermute x3, waiting for transfers between devices: 1.09 us -> 13.5 us  [shards(): next_going = lax.ppermute(going, 'seq', forward)]
    ppermute x3, waiting for transfers between devices: 5.36 us -> 0.01 us  [shards(): next_coming = lax.ppermute(coming, 'seq', backward)]
    ppermute x3, starting transfers between devices: 1.63 us -> 5.55 us  [shards(): next_coming = lax.ppermute(coming, 'seq', backward)]
  transfers between devices with their start and end apart: 33 -> 26, of which waited for: 19 -> 18; matrix products, arithmetic and copies ran while one was open for 8% -> 4% of each run, Pallas kernels for 0% -> 0%
where the time goes in v8:
time: 184 us; the launch traced here: 183 us
  waiting for transfers between devices  98 us (53%)
  starting transfers between devices  58.4 us (32%)
  matrix products  17.7 us (10%)
  other arithmetic  5.54 us (3%)
  local copies, waits for them, and re-layouts  2.22 us (1%)
    ppermute x6, waiting for transfers between devices, direct_reduce_scatter(): lax.ppermute(outgoing, axis, [(i, (i + shift) % n) for i in range(n)])  50.8 us
    ppermute x9, waiting for transfers between devices, direct_all_gather(): lax.ppermute(value, axis, [(i, (i + shift) % n) for i in range(n)])  27.7 us
    ppermute x9, starting transfers between devices, direct_all_gather(): lax.ppermute(value, axis, [(i, (i + shift) % n) for i in range(n)])  25.2 us
    ppermute x6, starting transfers between devices, direct_reduce_scatter(): lax.ppermute(outgoing, axis, [(i, (i + shift) % n) for i in range(n)])  17.1 us
    ppermute x3, waiting for transfers between devices, shards(): next_going = lax.ppermute(going, 'seq', forward)  13.5 us
    ppermute x3, starting transfers between devices, permute_all_to_all(): lax.ppermute(outgoing, axis, [(i, (i + shift) % n) for i in range(n)])  7.13 us
    dot_general x5, matrix products, conv_rows(): jnp.dot(shifted, conv_weight[offset], preferred_element_type=jnp.float32)  6.46 us
    ppermute x3, starting transfers between devices, shards(): next_coming = lax.ppermute(coming, 'seq', backward)  5.55 us
  transfers between devices with their start and end apart: 26, of which 18 were waited for; matrix products, arithmetic and copies ran while one was open for 4% of the time, Pallas kernels for 0%

profile of v8, /device:TPU:0, one launch (start us, length us, event | category | flops | bytes accessed | tf_op | source)
XLA Modules:
  0.0 183.0 jit_solution(17273195864649826857)
XLA Ops:
  4.1 3.1 %collective-permute-start = (bf16[128,384]{1,0:T(8,128)(2,1)S(1)}, bf16[128,384]{1,0:T(8,128)(2,1)S(1)}, u32[]{:S(2)}, u32[]{:S(2)}) collective-permute-start(bf16[128,384]{1,0:T(8,128)(2,1)S(1)} %bitcast.306), channel_id=1, source_target_pairs={{0,1},{1,2},{2,3},{3,0},{4,5},{5,6},{6,7},{7,4},{8,9},{9,10},{10,1... | collective-permute-start | bytes 294920 | tf_op jit(solution)/shard_map/ppermute | solution.py:65
  7.2 2.7 %collective-permute-start.1 = (bf16[128,384]{1,0:T(8,128)(2,1)S(1)}, bf16[128,384]{1,0:T(8,128)(2,1)S(1)}, u32[]{:S(2)}, u32[]{:S(2)}) collective-permute-start(bf16[128,384]{1,0:T(8,128)(2,1)S(1)} %bitcast.305), channel_id=1, source_target_pairs={{0,2},{1,3},{2,0},{3,1},{4,6},{5,7},{6,4},{7,5},{8,10},{9,11},{10,... | collective-permute-start | bytes 294920 | tf_op jit(solution)/shard_map/ppermute | solution.py:65
  9.9 1.4 collective-permute-start.2
  11.4 1.5 collective-permute-done
  12.9 3.5 %collective-permute-done.1 = bf16[128,384]{1,0:T(8,128)(2,1)S(1)} collective-permute-done((bf16[128,384]{1,0:T(8,128)(2,1)S(1)}, bf16[128,384]{1,0:T(8,128)(2,1)S(1)}, u32[]{:S(2)}, u32[]{:S(2)}) %collective-permute-start.1) | collective-permute-done | bytes 98336 | tf_op jit(solution)/shard_map/ppermute | solution.py:65
  16.6 1.7 collective-permute-start.3
  18.3 1.6 collective-permute-start.4
  19.9 2.4 %fusion.28 = f32[512,1536]{1,0:T(8,128)S(1)} fusion(bf16[512,384]{1,0:T(8,128)(2,1)S(1)} %bitcast.293, bf16[5,384,1536]{2,1,0:T(8,128)(2,1)} %param.12), kind=kOutput, calls=%fused_computation.53 | convolution fusion | flops 603979776 | bytes 4718592 | tf_op jit(solution)/shard_map/conv_reduce/dot_general | solution.py:39
  27.4 2.4 %collective-permute-start.5 = (bf16[128,1536]{1,0:T(8,128)(2,1)S(1)}, bf16[128,1536]{1,0:T(8,128)(2,1)S(1)}, u32[]{:S(2)}, u32[]{:S(2)}) collective-permute-start(bf16[128,1536]{1,0:T(8,128)(2,1)S(1)} %get-tuple-element.27), channel_id=1, source_target_pairs={{0,1},{1,2},{2,3},{3,0},{4,5},{5,6},{6,7},{7,4},{8,9},{9,10},{10,1... | collective-permute-start | bytes 1179656 | tf_op jit(solution)/shard_map/conv_reduce/ppermute | solution.py:51
  29.8 1.7 collective-permute-start.6
  32.3 7.8 %collective-permute-done.5 = bf16[128,1536]{1,0:T(8,128)(2,1)S(1)} collective-permute-done((bf16[128,1536]{1,0:T(8,128)(2,1)S(1)}, bf16[128,1536]{1,0:T(8,128)(2,1)S(1)}, u32[]{:S(2)}, u32[]{:S(2)}) %collective-permute-start.5) | collective-permute-done | bytes 393248 | tf_op jit(solution)/shard_map/conv_reduce/ppermute | solution.py:51
  40.1 17.9 %collective-permute-done.6 = bf16[128,1536]{1,0:T(8,128)(2,1)S(1)} collective-permute-done((bf16[128,1536]{1,0:T(8,128)(2,1)S(1)}, bf16[128,1536]{1,0:T(8,128)(2,1)S(1)}, u32[]{:S(2)}, u32[]{:S(2)}) %collective-permute-start.6) | collective-permute-done | bytes 393248 | tf_op jit(solution)/shard_map/conv_reduce/ppermute | solution.py:51
  58.8 9.0 %collective-permute-start.8 = (bf16[128,1536]{1,0:T(8,128)(2,1)S(1)}, bf16[128,1536]{1,0:T(8,128)(2,1)S(1)}, u32[]{:S(2)}, u32[]{:S(2)}) collective-permute-start(bf16[128,1536]{1,0:T(8,128)(2,1)S(1)} %get-tuple-element.21), channel_id=1, source_target_pairs={{0,1},{1,2},{2,3},{3,0},{4,5},{5,6},{6,7},{7,4},{8,9},{9,10},{10,1... | collective-permute-start | bytes 1179656 | tf_op jit(solution)/shard_map/attn_in_gather/ppermute | solution.py:127
  67.8 2.4 %collective-permute-start.10 = (bf16[128,1536]{1,0:T(8,128)(2,1)S(1)}, bf16[128,1536]{1,0:T(8,128)(2,1)S(1)}, u32[]{:S(2)}, u32[]{:S(2)}) collective-permute-start(bf16[128,1536]{1,0:T(8,128)(2,1)S(1)} %get-tuple-element.21), channel_id=1, source_target_pairs={{0,3},{1,0},{2,1},{3,2},{4,7},{5,4},{6,5},{7,6},{8,11},{9,8},{10,9... | collective-permute-start | bytes 1179656 | tf_op jit(solution)/shard_map/attn_in_gather/ppermute | solution.py:127
  70.2 7.0 %collective-permute-done.8 = bf16[128,1536]{1,0:T(8,128)(2,1)S(1)} collective-permute-done((bf16[128,1536]{1,0:T(8,128)(2,1)S(1)}, bf16[128,1536]{1,0:T(8,128)(2,1)S(1)}, u32[]{:S(2)}, u32[]{:S(2)}) %collective-permute-start.8) | collective-permute-done | bytes 393248 | tf_op jit(solution)/shard_map/attn_in_gather/ppermute | solution.py:127
  77.3 16.2 %collective-permute-done.9 = bf16[128,1536]{1,0:T(8,128)(2,1)S(1)} collective-permute-done((bf16[128,1536]{1,0:T(8,128)(2,1)S(1)}, bf16[128,1536]{1,0:T(8,128)(2,1)S(1)}, u32[]{:S(2)}, u32[]{:S(2)}) %collective-permute-start.9) | collective-permute-done | bytes 393248 | tf_op jit(solution)/shard_map/attn_in_gather/ppermute | solution.py:127
  93.6 1.4 convolution_convert_fusion
  95.5 1.8 collective-permute-start.12
  97.6 4.8 %collective-permute-done.11 = bf16[2,256,256]{2,1,0:T(8,128)(2,1)S(1)} collective-permute-done((bf16[2,256,256]{2,1,0:T(8,128)(2,1)S(1)}, bf16[2,256,256]{2,1,0:T(8,128)(2,1)S(1)}, u32[]{:S(2)}, u32[]{:S(2)}) %collective-permute-start.11) | collective-permute-done | bytes 262176 | tf_op jit(solution)/shard_map/kv_ring/ppermute | solution.py:205
  102.8 1.8 collective-permute-start.14
  104.9 4.7 %collective-permute-done.13 = bf16[2,256,256]{2,1,0:T(8,128)(2,1)S(1)} collective-permute-done((bf16[2,256,256]{2,1,0:T(8,128)(2,1)S(1)}, bf16[2,256,256]{2,1,0:T(8,128)(2,1)S(1)}, u32[]{:S(2)}, u32[]{:S(2)}) %collective-permute-start.13) | collective-permute-done | bytes 262176 | tf_op jit(solution)/shard_map/kv_ring/ppermute | solution.py:205
  110.3 2.0 %collective-permute-start.16 = (bf16[2,256,256]{2,1,0:T(8,128)(2,1)S(1)}, bf16[2,256,256]{2,1,0:T(8,128)(2,1)S(1)}, u32[]{:S(2)}, u32[]{:S(2)}) collective-permute-start(bf16[2,256,256]{2,1,0:T(8,128)(2,1)S(1)} %collective-permute-done.14), channel_id=1, source_target_pairs={{4,0},{8,4},{12,8},{0,12},{5,1},{9,5},{13,9},{1,13},{6,2},{10,6},{... | collective-permute-start | bytes 786440 | tf_op jit(solution)/shard_map/kv_ring/ppermute | solution.py:206
  112.3 3.9 %collective-permute-done.15 = bf16[2,256,256]{2,1,0:T(8,128)(2,1)S(1)} collective-permute-done((bf16[2,256,256]{2,1,0:T(8,128)(2,1)S(1)}, bf16[2,256,256]{2,1,0:T(8,128)(2,1)S(1)}, u32[]{:S(2)}, u32[]{:S(2)}) %collective-permute-start.15) | collective-permute-done | bytes 262176 | tf_op jit(solution)/shard_map/kv_ring/ppermute | solution.py:205
  122.9 1.7 fusion.64
  124.8 9.4 %collective-permute-start.17 = (bf16[128,1536]{1,0:T(8,128)(2,1)S(1)}, bf16[128,1536]{1,0:T(8,128)(2,1)S(1)}, u32[]{:S(2)}, u32[]{:S(2)}) collective-permute-start(bf16[128,1536]{1,0:T(8,128)(2,1)S(1)} %get-tuple-element.24), channel_id=1, source_target_pairs={{0,1},{1,2},{2,3},{3,0},{4,5},{5,6},{6,7},{7,4},{8,9},{9,10},{10,1... | collective-permute-start | bytes 1179656 | tf_op jit(solution)/shard_map/out_reduce/ppermute | solution.py:51
  134.1 1.7 collective-permute-start.18
  137.0 7.2 %collective-permute-done.17 = bf16[128,1536]{1,0:T(8,128)(2,1)S(1)} collective-permute-done((bf16[128,1536]{1,0:T(8,128)(2,1)S(1)}, bf16[128,1536]{1,0:T(8,128)(2,1)S(1)}, u32[]{:S(2)}, u32[]{:S(2)}) %collective-permute-start.17) | collective-permute-done | bytes 393248 | tf_op jit(solution)/shard_map/out_reduce/ppermute | solution.py:51
  144.3 17.8 %collective-permute-done.18 = bf16[128,1536]{1,0:T(8,128)(2,1)S(1)} collective-permute-done((bf16[128,1536]{1,0:T(8,128)(2,1)S(1)}, bf16[128,1536]{1,0:T(8,128)(2,1)S(1)}, u32[]{:S(2)}, u32[]{:S(2)}) %collective-permute-start.18) | collective-permute-done | bytes 393248 | tf_op jit(solution)/shard_map/out_reduce/ppermute | solution.py:51
  163.5 9.0 %collective-permute-start.20 = (bf16[8,256]{1,0:T(8,128)(2,1)S(1)}, bf16[8,256]{1,0:T(8,128)(2,1)S(1)}, u32[]{:S(2)}, u32[]{:S(2)}) collective-permute-start(bf16[8,256]{1,0:T(8,128)(2,1)S(1)} %get-tuple-element.60), channel_id=1, source_target_pairs={{0,1},{1,2},{2,3},{3,0},{4,5},{5,6},{6,7},{7,4},{8,9},{9,10},{10,1... | collective-permute-start | bytes 12296 | tf_op jit(solution)/shard_map/sides_gather/ppermute | solution.py:127
  172.5 1.6 collective-permute-start.21
  175.2 1.9 %collective-permute-done.21 = bf16[8,256]{1,0:T(8,128)(2,1)S(1)} collective-permute-done((bf16[8,256]{1,0:T(8,128)(2,1)S(1)}, bf16[8,256]{1,0:T(8,128)(2,1)S(1)}, u32[]{:S(2)}, u32[]{:S(2)}) %collective-permute-start.21) | collective-permute-done | bytes 4128 | tf_op jit(solution)/shard_map/sides_gather/ppermute | solution.py:127
  178.7 1.4 collective-permute-start.25
  (109 shorter events, 27.4 us)
Async XLA Ops:
  0.6 93.0 %copy-start = (bf16[1536,768]{1,0:T(8,128)(2,1)S(1)}, bf16[1536,768]{1,0:T(8,128)(2,1)}, u32[]{:S(2)}) copy-start(bf16[1536,768]{1,0:T(8,128)(2,1)} %param.14) | copy-start | bytes 7077892
  4.1 8.7 %collective-permute-start = (bf16[128,384]{1,0:T(8,128)(2,1)S(1)}, bf16[128,384]{1,0:T(8,128)(2,1)S(1)}, u32[]{:S(2)}, u32[]{:S(2)}) collective-permute-start(bf16[128,384]{1,0:T(8,128)(2,1)S(1)} %bitcast.306), channel_id=1, source_target_pairs={{0,1},{1,2},{2,3},{3,0},{4,5},{5,6},{6,7},{7,4},{8,9},{9,10},{10,1... | collective-permute-start | bytes 294920 | tf_op jit(solution)/shard_map/ppermute | solution.py:65
  7.2 9.2 %collective-permute-start.1 = (bf16[128,384]{1,0:T(8,128)(2,1)S(1)}, bf16[128,384]{1,0:T(8,128)(2,1)S(1)}, u32[]{:S(2)}, u32[]{:S(2)}) collective-permute-start(bf16[128,384]{1,0:T(8,128)(2,1)S(1)} %bitcast.305), channel_id=1, source_target_pairs={{0,2},{1,3},{2,0},{3,1},{4,6},{5,7},{6,4},{7,5},{8,10},{9,11},{10,... | collective-permute-start | bytes 294920 | tf_op jit(solution)/shard_map/ppermute | solution.py:65
  9.9 6.7 %collective-permute-start.2 = (bf16[128,384]{1,0:T(8,128)(2,1)S(1)}, bf16[128,384]{1,0:T(8,128)(2,1)S(1)}, u32[]{:S(2)}, u32[]{:S(2)}) collective-permute-start(bf16[128,384]{1,0:T(8,128)(2,1)S(1)} %bitcast.304), channel_id=1, source_target_pairs={{0,3},{1,0},{2,1},{3,2},{4,7},{5,4},{6,5},{7,6},{8,11},{9,8},{10,9... | collective-permute-start | bytes 294920 | tf_op jit(solution)/shard_map/ppermute | solution.py:65
  16.6 8.5 %collective-permute-start.3 = (bf16[8,384]{1,0:T(8,128)(2,1)S(1)}, bf16[8,384]{1,0:T(8,128)(2,1)S(1)}, u32[]{:S(2)}, u32[]{:S(2)}) collective-permute-start(bf16[8,384]{1,0:T(8,128)(2,1)S(1)} %get-tuple-element.32), channel_id=1, source_target_pairs={{0,4},{4,8},{8,12},{1,5},{5,9},{9,13},{2,6},{6,10},{10,14},{3,7},{... | collective-permute-start | bytes 18440 | tf_op jit(solution)/shard_map/ppermute | solution.py:25
  18.3 4.8 %collective-permute-start.4 = (bf16[8,384]{1,0:T(8,128)(2,1)S(1)}, bf16[8,384]{1,0:T(8,128)(2,1)S(1)}, u32[]{:S(2)}, u32[]{:S(2)}) collective-permute-start(bf16[8,384]{1,0:T(8,128)(2,1)S(1)} %get-tuple-element.33), channel_id=1, source_target_pairs={{4,0},{8,4},{12,8},{5,1},{9,5},{13,9},{6,2},{10,6},{14,10},{7,3},{... | collective-permute-start | bytes 18440 | tf_op jit(solution)/shard_map/ppermute | solution.py:26
  26.1 32.0 %copy-start.2 = (bf16[128,1536]{1,0:T(8,128)(2,1)S(1)}, bf16[128,1536]{1,0:T(8,128)(2,1)}, u32[]{:S(2)}) copy-start(bf16[128,1536]{1,0:T(8,128)(2,1)} %param.10) | copy-start | bytes 1179652
  27.4 12.7 %collective-permute-start.5 = (bf16[128,1536]{1,0:T(8,128)(2,1)S(1)}, bf16[128,1536]{1,0:T(8,128)(2,1)S(1)}, u32[]{:S(2)}, u32[]{:S(2)}) collective-permute-start(bf16[128,1536]{1,0:T(8,128)(2,1)S(1)} %get-tuple-element.27), channel_id=1, source_target_pairs={{0,1},{1,2},{2,3},{3,0},{4,5},{5,6},{6,7},{7,4},{8,9},{9,10},{10,1... | collective-permute-start | bytes 1179656 | tf_op jit(solution)/shard_map/conv_reduce/ppermute | solution.py:51
  29.8 28.2 %collective-permute-start.6 = (bf16[128,1536]{1,0:T(8,128)(2,1)S(1)}, bf16[128,1536]{1,0:T(8,128)(2,1)S(1)}, u32[]{:S(2)}, u32[]{:S(2)}) collective-permute-start(bf16[128,1536]{1,0:T(8,128)(2,1)S(1)} %get-tuple-element.29), channel_id=1, source_target_pairs={{0,2},{1,3},{2,0},{3,1},{4,6},{5,7},{6,4},{7,5},{8,10},{9,11},{10,... | collective-permute-start | bytes 1179656 | tf_op jit(solution)/shard_map/conv_reduce/ppermute | solution.py:51
  31.5 26.5 %collective-permute-start.7 = (bf16[128,1536]{1,0:T(8,128)(2,1)S(1)}, bf16[128,1536]{1,0:T(8,128)(2,1)S(1)}, u32[]{:S(2)}, u32[]{:S(2)}) collective-permute-start(bf16[128,1536]{1,0:T(8,128)(2,1)S(1)} %get-tuple-element.28), channel_id=1, source_target_pairs={{0,3},{1,0},{2,1},{3,2},{4,7},{5,4},{6,5},{7,6},{8,11},{9,8},{10,9... | collective-permute-start | bytes 1179656 | tf_op jit(solution)/shard_map/conv_reduce/ppermute | solution.py:51
  58.8 18.5 %collective-permute-start.8 = (bf16[128,1536]{1,0:T(8,128)(2,1)S(1)}, bf16[128,1536]{1,0:T(8,128)(2,1)S(1)}, u32[]{:S(2)}, u32[]{:S(2)}) collective-permute-start(bf16[128,1536]{1,0:T(8,128)(2,1)S(1)} %get-tuple-element.21), channel_id=1, source_target_pairs={{0,1},{1,2},{2,3},{3,0},{4,5},{5,6},{6,7},{7,4},{8,9},{9,10},{10,1... | collective-permute-start | bytes 1179656 | tf_op jit(solution)/shard_map/attn_in_gather/ppermute | solution.py:127
  67.8 25.8 %collective-permute-start.9 = (bf16[128,1536]{1,0:T(8,128)(2,1)S(1)}, bf16[128,1536]{1,0:T(8,128)(2,1)S(1)}, u32[]{:S(2)}, u32[]{:S(2)}) collective-permute-start(bf16[128,1536]{1,0:T(8,128)(2,1)S(1)} %get-tuple-element.21), channel_id=1, source_target_pairs={{0,2},{1,3},{2,0},{3,1},{4,6},{5,7},{6,4},{7,5},{8,10},{9,11},{10,... | collective-permute-start | bytes 1179656 | tf_op jit(solution)/shard_map/attn_in_gather/ppermute | solution.py:127
  67.8 25.8 %collective-permute-start.10 = (bf16[128,1536]{1,0:T(8,128)(2,1)S(1)}, bf16[128,1536]{1,0:T(8,128)(2,1)S(1)}, u32[]{:S(2)}, u32[]{:S(2)}) collective-permute-start(bf16[128,1536]{1,0:T(8,128)(2,1)S(1)} %get-tuple-element.21), channel_id=1, source_target_pairs={{0,3},{1,0},{2,1},{3,2},{4,7},{5,4},{6,5},{7,6},{8,11},{9,8},{10,9... | collective-permute-start | bytes 1179656 | tf_op jit(solution)/shard_map/attn_in_gather/ppermute | solution.py:127
  95.2 7.3 %collective-permute-start.11 = (bf16[2,256,256]{2,1,0:T(8,128)(2,1)S(1)}, bf16[2,256,256]{2,1,0:T(8,128)(2,1)S(1)}, u32[]{:S(2)}, u32[]{:S(2)}) collective-permute-start(bf16[2,256,256]{2,1,0:T(8,128)(2,1)S(1)} %get-tuple-element.30), channel_id=1, source_target_pairs={{0,4},{4,8},{8,12},{12,0},{1,5},{5,9},{9,13},{13,1},{2,6},{6,10},{... | collective-permute-start | bytes 786440 | tf_op jit(solution)/shard_map/kv_ring/ppermute | solution.py:205
  95.5 7.2 %collective-permute-start.12 = (bf16[2,256,256]{2,1,0:T(8,128)(2,1)S(1)}, bf16[2,256,256]{2,1,0:T(8,128)(2,1)S(1)}, u32[]{:S(2)}, u32[]{:S(2)}) collective-permute-start(bf16[2,256,256]{2,1,0:T(8,128)(2,1)S(1)} %get-tuple-element.31), channel_id=1, source_target_pairs={{4,0},{8,4},{12,8},{0,12},{5,1},{9,5},{13,9},{1,13},{6,2},{10,6},{... | collective-permute-start | bytes 786440 | tf_op jit(solution)/shard_map/kv_ring/ppermute | solution.py:206
  102.5 7.2 %collective-permute-start.13 = (bf16[2,256,256]{2,1,0:T(8,128)(2,1)S(1)}, bf16[2,256,256]{2,1,0:T(8,128)(2,1)S(1)}, u32[]{:S(2)}, u32[]{:S(2)}) collective-permute-start(bf16[2,256,256]{2,1,0:T(8,128)(2,1)S(1)} %collective-permute-done.11), channel_id=1, source_target_pairs={{0,4},{4,8},{8,12},{12,0},{1,5},{5,9},{9,13},{13,1},{2,6},{6,10},{... | collective-permute-start | bytes 786440 | tf_op jit(solution)/shard_map/kv_ring/ppermute | solution.py:205
  102.8 7.2 %collective-permute-start.14 = (bf16[2,256,256]{2,1,0:T(8,128)(2,1)S(1)}, bf16[2,256,256]{2,1,0:T(8,128)(2,1)S(1)}, u32[]{:S(2)}, u32[]{:S(2)}) collective-permute-start(bf16[2,256,256]{2,1,0:T(8,128)(2,1)S(1)} %collective-permute-done.12), channel_id=1, source_target_pairs={{4,0},{8,4},{12,8},{0,12},{5,1},{9,5},{13,9},{1,13},{6,2},{10,6},{... | collective-permute-start | bytes 786440 | tf_op jit(solution)/shard_map/kv_ring/ppermute | solution.py:206
  109.6 6.6 %collective-permute-start.15 = (bf16[2,256,256]{2,1,0:T(8,128)(2,1)S(1)}, bf16[2,256,256]{2,1,0:T(8,128)(2,1)S(1)}, u32[]{:S(2)}, u32[]{:S(2)}) collective-permute-start(bf16[2,256,256]{2,1,0:T(8,128)(2,1)S(1)} %collective-permute-done.13), channel_id=1, source_target_pairs={{0,4},{4,8},{8,12},{12,0},{1,5},{5,9},{9,13},{13,1},{2,6},{6,10},{... | collective-permute-start | bytes 786440 | tf_op jit(solution)/shard_map/kv_ring/ppermute | solution.py:205
  110.3 6.2 %collective-permute-start.16 = (bf16[2,256,256]{2,1,0:T(8,128)(2,1)S(1)}, bf16[2,256,256]{2,1,0:T(8,128)(2,1)S(1)}, u32[]{:S(2)}, u32[]{:S(2)}) collective-permute-start(bf16[2,256,256]{2,1,0:T(8,128)(2,1)S(1)} %collective-permute-done.14), channel_id=1, source_target_pairs={{4,0},{8,4},{12,8},{0,12},{5,1},{9,5},{13,9},{1,13},{6,2},{10,6},{... | collective-permute-start | bytes 786440 | tf_op jit(solution)/shard_map/kv_ring/ppermute | solution.py:206
  124.6 38.7 %copy-start.3 = (bf16[1536,256]{1,0:T(8,128)(2,1)S(1)}, bf16[1536,256]{1,0:T(8,128)(2,1)}, u32[]{:S(2)}) copy-start(bf16[1536,256]{1,0:T(8,128)(2,1)} %param.17) | copy-start | bytes 2359300
  124.6 38.7 %copy-start.5 = (f32[1536]{0:T(1024)S(1)}, f32[1536]{0:T(1024)}, u32[]{:S(2)}) copy-start(f32[1536]{0:T(1024)} %param.16) | copy-start | bytes 18436
  124.6 57.2 %copy-start.6 = (bf16[256,128]{1,0:T(8,128)(2,1)S(1)}, bf16[256,128]{1,0:T(8,128)(2,1)}, u32[]{:S(2)}) copy-start(bf16[256,128]{1,0:T(8,128)(2,1)} %param.19) | copy-start | bytes 196612
  124.6 57.2 %copy-start.7 = (bf16[128,256]{1,0:T(8,128)(2,1)S(1)}, bf16[128,256]{1,0:T(8,128)(2,1)}, u32[]{:S(2)}) copy-start(bf16[128,256]{1,0:T(8,128)(2,1)} %param.18) | copy-start | bytes 196612
  124.8 19.5 %collective-permute-start.17 = (bf16[128,1536]{1,0:T(8,128)(2,1)S(1)}, bf16[128,1536]{1,0:T(8,128)(2,1)S(1)}, u32[]{:S(2)}, u32[]{:S(2)}) collective-permute-start(bf16[128,1536]{1,0:T(8,128)(2,1)S(1)} %get-tuple-element.24), channel_id=1, source_target_pairs={{0,1},{1,2},{2,3},{3,0},{4,5},{5,6},{6,7},{7,4},{8,9},{9,10},{10,1... | collective-permute-start | bytes 1179656 | tf_op jit(solution)/shard_map/out_reduce/ppermute | solution.py:51
  134.1 28.0 %collective-permute-start.18 = (bf16[128,1536]{1,0:T(8,128)(2,1)S(1)}, bf16[128,1536]{1,0:T(8,128)(2,1)S(1)}, u32[]{:S(2)}, u32[]{:S(2)}) collective-permute-start(bf16[128,1536]{1,0:T(8,128)(2,1)S(1)} %get-tuple-element.26), channel_id=1, source_target_pairs={{0,2},{1,3},{2,0},{3,1},{4,6},{5,7},{6,4},{7,5},{8,10},{9,11},{10,... | collective-permute-start | bytes 1179656 | tf_op jit(solution)/shard_map/out_reduce/ppermute | solution.py:51
  135.8 26.3 %collective-permute-start.19 = (bf16[128,1536]{1,0:T(8,128)(2,1)S(1)}, bf16[128,1536]{1,0:T(8,128)(2,1)S(1)}, u32[]{:S(2)}, u32[]{:S(2)}) collective-permute-start(bf16[128,1536]{1,0:T(8,128)(2,1)S(1)} %get-tuple-element.25), channel_id=1, source_target_pairs={{0,3},{1,0},{2,1},{3,2},{4,7},{5,4},{6,5},{7,6},{8,11},{9,8},{10,9... | collective-permute-start | bytes 1179656 | tf_op jit(solution)/shard_map/out_reduce/ppermute | solution.py:51
  163.5 11.6 %collective-permute-start.20 = (bf16[8,256]{1,0:T(8,128)(2,1)S(1)}, bf16[8,256]{1,0:T(8,128)(2,1)S(1)}, u32[]{:S(2)}, u32[]{:S(2)}) collective-permute-start(bf16[8,256]{1,0:T(8,128)(2,1)S(1)} %get-tuple-element.60), channel_id=1, source_target_pairs={{0,1},{1,2},{2,3},{3,0},{4,5},{5,6},{6,7},{7,4},{8,9},{9,10},{10,1... | collective-permute-start | bytes 12296 | tf_op jit(solution)/shard_map/sides_gather/ppermute | solution.py:127
  172.5 4.5 %collective-permute-start.21 = (bf16[8,256]{1,0:T(8,128)(2,1)S(1)}, bf16[8,256]{1,0:T(8,128)(2,1)S(1)}, u32[]{:S(2)}, u32[]{:S(2)}) collective-permute-start(bf16[8,256]{1,0:T(8,128)(2,1)S(1)} %get-tuple-element.60), channel_id=1, source_target_pairs={{0,2},{1,3},{2,0},{3,1},{4,6},{5,7},{6,4},{7,5},{8,10},{9,11},{10,... | collective-permute-start | bytes 12296 | tf_op jit(solution)/shard_map/sides_gather/ppermute | solution.py:127
  174.2 3.6 %collective-permute-start.22 = (bf16[8,256]{1,0:T(8,128)(2,1)S(1)}, bf16[8,256]{1,0:T(8,128)(2,1)S(1)}, u32[]{:S(2)}, u32[]{:S(2)}) collective-permute-start(bf16[8,256]{1,0:T(8,128)(2,1)S(1)} %get-tuple-element.60), channel_id=1, source_target_pairs={{0,3},{1,0},{2,1},{3,2},{4,7},{5,4},{6,5},{7,6},{8,11},{9,8},{10,9... | collective-permute-start | bytes 12296 | tf_op jit(solution)/shard_map/sides_gather/ppermute | solution.py:127
  177.8 3.2 %collective-permute-start.23 = (bf16[32,256]{1,0:T(8,128)(2,1)S(1)}, bf16[32,256]{1,0:T(8,128)(2,1)S(1)}, u32[]{:S(2)}, u32[]{:S(2)}) collective-permute-start(bf16[32,256]{1,0:T(8,128)(2,1)S(1)} %bitcast.307), channel_id=1, source_target_pairs={{0,4},{4,8},{8,12},{12,0},{1,5},{5,9},{9,13},{13,1},{2,6},{6,10},{... | collective-permute-start | bytes 49160 | tf_op jit(solution)/shard_map/sides_gather/ppermute | solution.py:127
  177.8 3.9 %collective-permute-start.24 = (bf16[32,256]{1,0:T(8,128)(2,1)S(1)}, bf16[32,256]{1,0:T(8,128)(2,1)S(1)}, u32[]{:S(2)}, u32[]{:S(2)}) collective-permute-start(bf16[32,256]{1,0:T(8,128)(2,1)S(1)} %bitcast.308), channel_id=1, source_target_pairs={{0,8},{4,12},{8,0},{12,4},{1,9},{5,13},{9,1},{13,5},{2,10},{6,14},... | collective-permute-start | bytes 49160 | tf_op jit(solution)/shard_map/sides_gather/ppermute | solution.py:127
  178.7 3.0 %collective-permute-start.25 = (bf16[32,256]{1,0:T(8,128)(2,1)S(1)}, bf16[32,256]{1,0:T(8,128)(2,1)S(1)}, u32[]{:S(2)}, u32[]{:S(2)}) collective-permute-start(bf16[32,256]{1,0:T(8,128)(2,1)S(1)} %bitcast.309), channel_id=1, source_target_pairs={{0,12},{4,0},{8,4},{12,8},{1,13},{5,1},{9,5},{13,9},{2,14},{6,2},{... | collective-permute-start | bytes 49160 | tf_op jit(solution)/shard_map/sides_gather/ppermute | solution.py:127
  (2 other events, 36.2 us)

commit v9 on v6

--- a/solution.py
+++ b/solution.py
@@ -36,6 +36,28 @@
     summed = jnp.zeros((row_total, conv_weight.shape[2]), jnp.float32)
     for offset in range(conv_weight.shape[0]):
         shifted = lax.dynamic_slice_in_dim(padded, offset * DILATION, row_total, 0)
+        summed = summed + jnp.dot(shifted, conv_weight[offset], preferred_element_type=jnp.float32)
+    return summed
+
+
+def direct_reduce_scatter_of(block_of, axis):
+    n = lax.axis_size(axis)
+    me = lax.axis_index(axis)
+    incoming = []
+    for shift in range(1, n):
+        outgoing = block_of((me + shift) % n).astype(jnp.bfloat16)
+        incoming.append(lax.ppermute(outgoing, axis, [(i, (i + shift) % n) for i in range(n)]))
+    total = block_of(me)
+    for piece in incoming:
+        total = total + piece.astype(jnp.float32)
+    return total
+
+
+def conv_block(padded, conv_weight, block, rows):
+    start = block * rows
+    summed = jnp.zeros((rows, conv_weight.shape[2]), jnp.float32)
+    for offset in range(conv_weight.shape[0]):
+        shifted = lax.dynamic_slice_in_dim(padded, start + offset * DILATION, rows, 0)
         summed = summed + jnp.dot(shifted, conv_weight[offset], preferred_element_type=jnp.float32)
     return summed
 
@@ -116,6 +138,24 @@
     )
 
 
+def projected_all_gather(value, weight, axis):
+    n = lax.axis_size(axis)
+    if n > 4:
+        gathered = line_all_gather(value, axis)
+        return jnp.dot(gathered, weight, preferred_element_type=jnp.float32).astype(jnp.bfloat16)
+    me = lax.axis_index(axis)
+
+    def project(rows):
+        return jnp.dot(rows, weight, preferred_element_type=jnp.float32).astype(jnp.bfloat16)
+
+    slots = jnp.zeros((n, value.shape[0], weight.shape[1]), jnp.bfloat16)
+    for shift in range(1, n):
+        incoming = lax.ppermute(value, axis, [(i, (i + shift) % n) for i in range(n)])
+        slots = lax.dynamic_update_index_in_dim(slots, project(incoming), (me + n - shift) % n, 0)
+    slots = lax.dynamic_update_index_in_dim(slots, project(value), me, 0)
+    return slots.reshape(n * value.shape[0], weight.shape[1])
+
+
 def direct_all_gather(value, axis):
     n = lax.axis_size(axis)
     if n > 4:
@@ -156,12 +196,13 @@
     swapped = permute_all_to_all(normed, "pair")
     padded = padded_2(swapped, (("seq", 0),), DILATION * (conv_weight.shape[0] - 1) // 2)
     with jax.named_scope("conv_reduce"):
-        summed = direct_reduce_scatter(conv_rows(padded, conv_weight, local_rows), "pair")
+        summed = direct_reduce_scatter_of(
+            lambda block: conv_block(padded, conv_weight, block, row_count), "pair"
+        )
     first_out = (inputs + summed).astype(jnp.bfloat16)
     attn_in = norm_rows(first_out.astype(jnp.float32), gain_attn).astype(jnp.bfloat16)
     with jax.named_scope("attn_in_gather"):
-        block_in = direct_all_gather(attn_in, "pair")
-    projected = jnp.dot(block_in, w_qkv, preferred_element_type=jnp.float32).astype(jnp.bfloat16)
+        projected = projected_all_gather(attn_in, w_qkv, "pair")
     head_count = projected.shape[1] // (2 * KEY_SIZE + VALUE_SIZE)
     grouped = projected.reshape(local_rows, head_count, 2 * KEY_SIZE + VALUE_SIZE).transpose(1, 0, 2)
     queries = grouped[:, :, :KEY_SIZE]

time: 181 us -> 193 us (1.066)
  waiting for transfers between devices: 82.4 us -> 59.7 us
  starting transfers between devices: 56.8 us -> 71.5 us
  local copies, waits for them, and re-layouts: 16 us -> 29.3 us
  matrix products: 21 us -> 28.1 us
    ppermute x9 -> x6, waiting for transfers between devices: 26.7 us -> 5.61 us  [direct_all_gather(): lax.ppermute(value, axis, [(i, (i + shift) % n) for i in range(n)])]
    ppermute x3, starting transfers between devices: 12.9 us -> 32.2 us  [line_all_gather(): flow_r = lax.ppermute(flow_r, axis, right)]
    ppermute x3, starting transfers between devices: 11.4 us -> 2.07 us  [rows_to_heads(): lax.ppermute(outgoing, axis, [(i, (i + shift) % n) for i in range(n)])]
    ppermute x3, waiting for transfers between devices: 9.47 us -> 2.82 us  [shards(): next_going = lax.ppermute(going, 'seq', forward)]
    dot_general x6 -> x24, matrix products: 7.84 us -> 14 us  [the longest x20 12.1 us: conv_block(): jnp.dot(shifted, conv_weight[offset], preferred_element_type=jnp.float32)]
    ppermute x3, starting transfers between devices: 1.3 us -> 6.49 us  [shards(): next_going = lax.ppermute(going, 'seq', forward)]
    ppermute x3 -> x6, starting transfers between devices: 3.1 us -> 6.8 us  [the longest x3 3.57 us: projected_all_gather(): lax.ppermute(value, axis, [(i, (i + shift) % n) for i in range(n)])]
    ppermute x1, waiting for transfers between devices: 0.01 us -> 3.37 us  [padded_2(): after = lax.ppermute(first, axis, down)]
  transfers between devices with their start and end apart: 33 -> 33, of which waited for: 18 -> 14; matrix products, arithmetic and copies ran while one was open for 17% -> 25% of each run, Pallas kernels for 0% -> 0%
where the time goes in v9:
time: 193 us; the launch traced here: 192 us
  starting transfers between devices  71.5 us (37%)
  waiting for transfers between devices  59.7 us (31%)
  local copies, waits for them, and re-layouts  29.3 us (15%)
  matrix products  28.1 us (15%)
  other arithmetic  2.02 us (1%)
    ppermute x3, starting transfers between devices, line_all_gather(): flow_r = lax.ppermute(flow_r, axis, right)  32.2 us
    ppermute x3, waiting for transfers between devices, direct_reduce_scatter_of(): lax.ppermute(outgoing, axis, [(i, (i + shift) % n) for i in range(n)])  20.2 us
    dot_general x20, matrix products, conv_block(): jnp.dot(shifted, conv_weight[offset], preferred_element_type=jnp.float32)  12.1 us
    ppermute x3, waiting for transfers between devices, permute_all_to_all(): lax.ppermute(outgoing, axis, [(i, (i + shift) % n) for i in range(n)])  10.4 us
    ppermute x3, waiting for transfers between devices, projected_all_gather(): lax.ppermute(value, axis, [(i, (i + shift) % n) for i in range(n)])  9.13 us
    ppermute x6, starting transfers between devices, direct_all_gather(): lax.ppermute(value, axis, [(i, (i + shift) % n) for i in range(n)])  7.38 us
    ppermute x3, starting transfers between devices, shards(): next_going = lax.ppermute(going, 'seq', forward)  6.49 us
    ppermute x3, starting transfers between devices, permute_all_to_all(): lax.ppermute(outgoing, axis, [(i, (i + shift) % n) for i in range(n)])  5.92 us
  transfers between devices with their start and end apart: 33, of which 14 were waited for; matrix products, arithmetic and copies ran while one was open for 25% of the time, Pallas kernels for 0%

profile of v9, /device:TPU:0, one launch (start us, length us, event | category | flops | bytes accessed | tf_op | source)
XLA Modules:
  0.0 192.3 jit_solution(3180385144415282834)
XLA Ops:
  3.3 5.7 %collective-permute-start.20 = (bf16[256,768]{1,0:T(8,128)(2,1)}, bf16[256,768]{1,0:T(8,128)(2,1)}, u32[]{:S(2)}, u32[]{:S(2)}) collective-permute-start(bf16[256,768]{1,0:T(8,128)(2,1)} %get-tuple-element.3), channel_id=1, source_target_pairs={{0,1},{1,2},{2,3},{4,5},{5,6},{6,7},{8,9},{9,10},{10,11},{12,13},{... | collective-permute-start | bytes 1179656 | tf_op jit(solution)/shard_map/out_projection/ppermute | solution.py:102
  12.3 2.6 %collective-permute-start = (bf16[128,384]{1,0:T(8,128)(2,1)}, bf16[128,384]{1,0:T(8,128)(2,1)S(1)}, u32[]{:S(2)}, u32[]{:S(2)}) collective-permute-start(bf16[128,384]{1,0:T(8,128)(2,1)} %bitcast.313), channel_id=1, source_target_pairs={{0,1},{1,2},{2,3},{3,0},{4,5},{5,6},{6,7},{7,4},{8,9},{9,10},{10,1... | collective-permute-start | bytes 294920 | tf_op jit(solution)/shard_map/ppermute | solution.py:87
  15.6 2.6 %collective-permute-start.1 = (bf16[128,384]{1,0:T(8,128)(2,1)}, bf16[128,384]{1,0:T(8,128)(2,1)S(1)}, u32[]{:S(2)}, u32[]{:S(2)}) collective-permute-start(bf16[128,384]{1,0:T(8,128)(2,1)} %bitcast.312), channel_id=1, source_target_pairs={{0,2},{1,3},{2,0},{3,1},{4,6},{5,7},{6,4},{7,5},{8,10},{9,11},{10,... | collective-permute-start | bytes 294920 | tf_op jit(solution)/shard_map/ppermute | solution.py:87
  19.0 7.6 %collective-permute-done = bf16[128,384]{1,0:T(8,128)(2,1)S(1)} collective-permute-done((bf16[128,384]{1,0:T(8,128)(2,1)}, bf16[128,384]{1,0:T(8,128)(2,1)S(1)}, u32[]{:S(2)}, u32[]{:S(2)}) %collective-permute-start) | collective-permute-done | bytes 98336 | tf_op jit(solution)/shard_map/ppermute | solution.py:87
  26.6 2.7 %collective-permute-done.1 = bf16[128,384]{1,0:T(8,128)(2,1)S(1)} collective-permute-done((bf16[128,384]{1,0:T(8,128)(2,1)}, bf16[128,384]{1,0:T(8,128)(2,1)S(1)}, u32[]{:S(2)}, u32[]{:S(2)}) %collective-permute-start.1) | collective-permute-done | bytes 98336 | tf_op jit(solution)/shard_map/ppermute | solution.py:87
  32.2 3.4 %collective-permute-done.4 = bf16[8,384]{1,0:T(8,128)(2,1)S(1)} collective-permute-done((bf16[8,384]{1,0:T(8,128)(2,1)S(1)}, bf16[8,384]{1,0:T(8,128)(2,1)S(1)}, u32[]{:S(2)}, u32[]{:S(2)}) %collective-permute-start.4) | collective-permute-done | bytes 6176 | tf_op jit(solution)/shard_map/ppermute | solution.py:26
  35.6 1.8 fusion.51
  37.4 1.9 fusion.59
  44.1 2.8 %collective-permute-start.6 = (bf16[128,1536]{1,0:T(8,128)(2,1)S(1)}, bf16[128,1536]{1,0:T(8,128)(2,1)S(1)}, u32[]{:S(2)}, u32[]{:S(2)}) collective-permute-start(bf16[128,1536]{1,0:T(8,128)(2,1)S(1)} %fusion.26), channel_id=1, source_target_pairs={{0,2},{1,3},{2,0},{3,1},{4,6},{5,7},{6,4},{7,5},{8,10},{9,11},{10,... | collective-permute-start | bytes 1179656 | tf_op jit(solution)/shard_map/conv_reduce/ppermute | solution.py:49
  50.4 3.3 %collective-permute-start.22 = (bf16[256,768]{1,0:T(8,128)(2,1)}, bf16[256,768]{1,0:T(8,128)(2,1)}, u32[]{:S(2)}, u32[]{:S(2)}) collective-permute-start(bf16[256,768]{1,0:T(8,128)(2,1)} %collective-permute-done.20), channel_id=1, source_target_pairs={{0,1},{1,2},{2,3},{4,5},{5,6},{6,7},{8,9},{9,10},{10,11},{12,13},{... | collective-permute-start | bytes 1179656 | tf_op jit(solution)/shard_map/out_projection/ppermute | solution.py:102
  55.0 1.8 bitcast_dynamic-update-slice_fusion.5
  56.8 1.8 bitcast_dynamic-update-slice_fusion.4
  58.6 20.2 %collective-permute-done.6 = bf16[128,1536]{1,0:T(8,128)(2,1)S(1)} collective-permute-done((bf16[128,1536]{1,0:T(8,128)(2,1)S(1)}, bf16[128,1536]{1,0:T(8,128)(2,1)S(1)}, u32[]{:S(2)}, u32[]{:S(2)}) %collective-permute-start.6) | collective-permute-done | bytes 393248 | tf_op jit(solution)/shard_map/conv_reduce/ppermute | solution.py:49
  81.3 1.9 %collective-permute-start.8 = (bf16[128,1536]{1,0:T(8,128)(2,1)S(1)}, bf16[128,1536]{1,0:T(8,128)(2,1)S(1)}, u32[]{:S(2)}, u32[]{:S(2)}) collective-permute-start(bf16[128,1536]{1,0:T(8,128)(2,1)S(1)} %multiply_convert_fusion), channel_id=1, source_target_pairs={{0,1},{1,2},{2,3},{3,0},{4,5},{5,6},{6,7},{7,4},{8,9},{9,10},{10,1... | collective-permute-start | bytes 1179656 | tf_op jit(solution)/shard_map/attn_in_gather/ppermute | solution.py:153
  83.2 23.2 %collective-permute-start.24 = (bf16[256,768]{1,0:T(8,128)(2,1)}, bf16[256,768]{1,0:T(8,128)(2,1)}, u32[]{:S(2)}, u32[]{:S(2)}) collective-permute-start(bf16[256,768]{1,0:T(8,128)(2,1)} %collective-permute-done.22), channel_id=1, source_target_pairs={{0,1},{1,2},{2,3},{4,5},{5,6},{6,7},{8,9},{9,10},{10,11},{12,13},{... | collective-permute-start | bytes 1179656 | tf_op jit(solution)/shard_map/out_projection/ppermute | solution.py:102
  107.7 1.8 bitcast_dynamic-update-slice_fusion.3
  109.4 1.8 bitcast_dynamic-update-slice_fusion.2
  111.8 9.1 %collective-permute-done.9 = bf16[128,1536]{1,0:T(8,128)(2,1)S(1)} collective-permute-done((bf16[128,1536]{1,0:T(8,128)(2,1)S(1)}, bf16[128,1536]{1,0:T(8,128)(2,1)S(1)}, u32[]{:S(2)}, u32[]{:S(2)}) %collective-permute-start.9) | collective-permute-done | bytes 393248 | tf_op jit(solution)/shard_map/attn_in_gather/ppermute | solution.py:153
  124.8 2.7 %collective-permute-start.11 = (bf16[2,256,256]{2,1,0:T(8,128)(2,1)S(1)}, bf16[2,256,256]{2,1,0:T(8,128)(2,1)S(1)}, u32[]{:S(2)}, u32[]{:S(2)}) collective-permute-start(bf16[2,256,256]{2,1,0:T(8,128)(2,1)S(1)} %get-tuple-element.20), channel_id=1, source_target_pairs={{0,4},{4,8},{8,12},{12,0},{1,5},{5,9},{9,13},{13,1},{2,6},{6,10},{... | collective-permute-start | bytes 786440 | tf_op jit(solution)/shard_map/kv_ring/ppermute | solution.py:246
  128.1 2.5 %collective-permute-done.11 = bf16[2,256,256]{2,1,0:T(8,128)(2,1)S(1)} collective-permute-done((bf16[2,256,256]{2,1,0:T(8,128)(2,1)S(1)}, bf16[2,256,256]{2,1,0:T(8,128)(2,1)S(1)}, u32[]{:S(2)}, u32[]{:S(2)}) %collective-permute-start.11) | collective-permute-done | bytes 262176 | tf_op jit(solution)/shard_map/kv_ring/ppermute | solution.py:246
  130.6 3.7 %collective-permute-start.13 = (bf16[2,256,256]{2,1,0:T(8,128)(2,1)S(1)}, bf16[2,256,256]{2,1,0:T(8,128)(2,1)S(1)}, u32[]{:S(2)}, u32[]{:S(2)}) collective-permute-start(bf16[2,256,256]{2,1,0:T(8,128)(2,1)S(1)} %collective-permute-done.11), channel_id=1, source_target_pairs={{0,4},{4,8},{8,12},{12,0},{1,5},{5,9},{9,13},{13,1},{2,6},{6,10},{... | collective-permute-start | bytes 786440 | tf_op jit(solution)/shard_map/kv_ring/ppermute | solution.py:246
  136.6 1.8 bitcast_dynamic-update-slice_fusion.1
  138.4 1.8 bitcast_dynamic-update-slice_fusion
  140.2 2.6 %slice.159 = bf16[4,256,768]{2,1,0:T(8,128)(2,1)} slice(bf16[5,256,768]{2,1,0:T(8,128)(2,1)} %bitcast_dynamic-update-slice_fusion), slice={[0:4], [0:256], [0:768]} | slice | bytes 3145728 | tf_op jit(solution)/shard_map/out_projection/slice | solution.py:108
  146.1 5.7 %collective-permute-done.16 = bf16[2,256,256]{2,1,0:T(8,128)(2,1)S(1)} collective-permute-done((bf16[2,256,256]{2,1,0:T(8,128)(2,1)S(1)}, bf16[2,256,256]{2,1,0:T(8,128)(2,1)S(1)}, u32[]{:S(2)}, u32[]{:S(2)}) %collective-permute-start.16) | collective-permute-done | bytes 262176 | tf_op jit(solution)/shard_map/kv_ring/ppermute | solution.py:247
  161.4 1.9 %collective-permute-start.17 = (bf16[128,256]{1,0:T(8,128)(2,1)}, bf16[128,256]{1,0:T(8,128)(2,1)}, u32[]{:S(2)}, u32[]{:S(2)}) collective-permute-start(bf16[128,256]{1,0:T(8,128)(2,1)} %get-tuple-element.30), channel_id=1, source_target_pairs={{0,1},{1,2},{2,3},{3,0},{4,5},{5,6},{6,7},{7,4},{8,9},{9,10},{10,1... | collective-permute-start | bytes 196616 | tf_op jit(solution)/shard_map/out_projection/ppermute | solution.py:120
  163.4 2.4 %collective-permute-done.19 = bf16[128,256]{1,0:T(8,128)(2,1)S(1)} collective-permute-done((bf16[128,256]{1,0:T(8,128)(2,1)}, bf16[128,256]{1,0:T(8,128)(2,1)S(1)}, u32[]{:S(2)}, u32[]{:S(2)}) %collective-permute-start.19) | collective-permute-done | bytes 65568 | tf_op jit(solution)/shard_map/out_projection/ppermute | solution.py:120
  171.6 5.0 %convert_reduce_fusion = (f32[8,1536]{1,0:T(8,128)S(1)}, bf16[128,1536]{1,0:T(8,128)(2,1)}) fusion(f32[128,1536]{1,0:T(8,128)S(1)} %copy-done.4, bf16[128,1024]{0,1:T(8,128)(2,1)S(1)} %bitcast.328, bf16[1024,768]{1,0:T(8,128)(2,1)} %collective-permute-done.26, bf16[1024,768]{1,0:T(8,128)(2,1)} %bitcast.57, pred[]{:T(512)S(6)} %eq.29), kind=kOutput, calls=%fused_computation.151 | convolution fusion | flops 417583104 | bytes 4636673 | tf_op jit(solution)/shard_map/out_projection/dot_general | solution.py:259
  178.3 1.9 collective-permute-start.28
  184.1 2.7 %collective-permute-start.31 = (bf16[32,256]{1,0:T(8,128)(2,1)S(1)}, bf16[32,256]{1,0:T(8,128)(2,1)S(1)}, u32[]{:S(2)}, u32[]{:S(2)}) collective-permute-start(bf16[32,256]{1,0:T(8,128)(2,1)S(1)} %bitcast.334), channel_id=1, source_target_pairs={{0,8},{4,12},{8,0},{12,4},{1,9},{5,13},{9,1},{13,5},{2,10},{6,14},... | collective-permute-start | bytes 49160 | tf_op jit(solution)/shard_map/sides_gather/ppermute | solution.py:167
  187.1 2.9 %collective-permute-done.30 = bf16[32,256]{1,0:T(8,128)(2,1)S(1)} collective-permute-done((bf16[32,256]{1,0:T(8,128)(2,1)S(1)}, bf16[32,256]{1,0:T(8,128)(2,1)S(1)}, u32[]{:S(2)}, u32[]{:S(2)}) %collective-permute-start.30) | collective-permute-done | bytes 16416 | tf_op jit(solution)/shard_map/sides_gather/ppermute | solution.py:167
  190.2 2.1 %fusion.49 = bf16[1024,128]{1,0:T(8,128)(2,1)} fusion(bf16[256,128]{1,0:T(8,128)(2,1)} %param.19, bf16[1024,128]{1,0:T(8,128)(2,1)S(1)} %bitcast.327, bf16[128,256]{1,0:T(8,128)(2,1)} %param.18), kind=kOutput, calls=%fused_computation.71 | convolution fusion | flops 135135232 | bytes 655360 | tf_op jit(solution)/shard_map/dot_general | solution.py:285
  (163 shorter events, 54.9 us)
Async XLA Ops:
  3.3 47.1 %collective-permute-start.20 = (bf16[256,768]{1,0:T(8,128)(2,1)}, bf16[256,768]{1,0:T(8,128)(2,1)}, u32[]{:S(2)}, u32[]{:S(2)}) collective-permute-start(bf16[256,768]{1,0:T(8,128)(2,1)} %get-tuple-element.3), channel_id=1, source_target_pairs={{0,1},{1,2},{2,3},{4,5},{5,6},{6,7},{8,9},{9,10},{10,11},{12,13},{... | collective-permute-start | bytes 1179656 | tf_op jit(solution)/shard_map/out_projection/ppermute | solution.py:102
  9.0 44.7 %collective-permute-start.21 = (bf16[256,768]{1,0:T(8,128)(2,1)}, bf16[256,768]{1,0:T(8,128)(2,1)}, u32[]{:S(2)}, u32[]{:S(2)}) collective-permute-start(bf16[256,768]{1,0:T(8,128)(2,1)} %get-tuple-element.3), channel_id=1, source_target_pairs={{1,0},{2,1},{3,2},{5,4},{6,5},{7,6},{9,8},{10,9},{11,10},{13,12},{... | collective-permute-start | bytes 1179656 | tf_op jit(solution)/shard_map/out_projection/ppermute | solution.py:103
  12.3 14.3 %collective-permute-start = (bf16[128,384]{1,0:T(8,128)(2,1)}, bf16[128,384]{1,0:T(8,128)(2,1)S(1)}, u32[]{:S(2)}, u32[]{:S(2)}) collective-permute-start(bf16[128,384]{1,0:T(8,128)(2,1)} %bitcast.313), channel_id=1, source_target_pairs={{0,1},{1,2},{2,3},{3,0},{4,5},{5,6},{6,7},{7,4},{8,9},{9,10},{10,1... | collective-permute-start | bytes 294920 | tf_op jit(solution)/shard_map/ppermute | solution.py:87
  15.6 13.8 %collective-permute-start.1 = (bf16[128,384]{1,0:T(8,128)(2,1)}, bf16[128,384]{1,0:T(8,128)(2,1)S(1)}, u32[]{:S(2)}, u32[]{:S(2)}) collective-permute-start(bf16[128,384]{1,0:T(8,128)(2,1)} %bitcast.312), channel_id=1, source_target_pairs={{0,2},{1,3},{2,0},{3,1},{4,6},{5,7},{6,4},{7,5},{8,10},{9,11},{10,... | collective-permute-start | bytes 294920 | tf_op jit(solution)/shard_map/ppermute | solution.py:87
  18.2 11.2 %collective-permute-start.2 = (bf16[128,384]{1,0:T(8,128)(2,1)S(1)}, bf16[128,384]{1,0:T(8,128)(2,1)S(1)}, u32[]{:S(2)}, u32[]{:S(2)}) collective-permute-start(bf16[128,384]{1,0:T(8,128)(2,1)S(1)} %bitcast.330), channel_id=1, source_target_pairs={{0,3},{1,0},{2,1},{3,2},{4,7},{5,4},{6,5},{7,6},{8,11},{9,8},{10,9... | collective-permute-start | bytes 294920 | tf_op jit(solution)/shard_map/ppermute | solution.py:87
  30.7 4.8 %collective-permute-start.4 = (bf16[8,384]{1,0:T(8,128)(2,1)S(1)}, bf16[8,384]{1,0:T(8,128)(2,1)S(1)}, u32[]{:S(2)}, u32[]{:S(2)}) collective-permute-start(bf16[8,384]{1,0:T(8,128)(2,1)S(1)} %get-tuple-element.23), channel_id=1, source_target_pairs={{4,0},{8,4},{12,8},{5,1},{9,5},{13,9},{6,2},{10,6},{14,10},{7,3},{... | collective-permute-start | bytes 18440 | tf_op jit(solution)/shard_map/ppermute | solution.py:26
  41.8 16.8 %collective-permute-start.7 = (bf16[128,1536]{1,0:T(8,128)(2,1)S(1)}, bf16[128,1536]{1,0:T(8,128)(2,1)S(1)}, u32[]{:S(2)}, u32[]{:S(2)}) collective-permute-start(bf16[128,1536]{1,0:T(8,128)(2,1)S(1)} %fusion.27), channel_id=1, source_target_pairs={{0,3},{1,0},{2,1},{3,2},{4,7},{5,4},{6,5},{7,6},{8,11},{9,8},{10,9... | collective-permute-start | bytes 1179656 | tf_op jit(solution)/shard_map/conv_reduce/ppermute | solution.py:49
  44.1 34.7 %collective-permute-start.6 = (bf16[128,1536]{1,0:T(8,128)(2,1)S(1)}, bf16[128,1536]{1,0:T(8,128)(2,1)S(1)}, u32[]{:S(2)}, u32[]{:S(2)}) collective-permute-start(bf16[128,1536]{1,0:T(8,128)(2,1)S(1)} %fusion.26), channel_id=1, source_target_pairs={{0,2},{1,3},{2,0},{3,1},{4,6},{5,7},{6,4},{7,5},{8,10},{9,11},{10,... | collective-permute-start | bytes 1179656 | tf_op jit(solution)/shard_map/conv_reduce/ppermute | solution.py:49
  48.8 29.9 %collective-permute-start.5 = (bf16[128,1536]{1,0:T(8,128)(2,1)S(1)}, bf16[128,1536]{1,0:T(8,128)(2,1)S(1)}, u32[]{:S(2)}, u32[]{:S(2)}) collective-permute-start(bf16[128,1536]{1,0:T(8,128)(2,1)S(1)} %fusion.25), channel_id=1, source_target_pairs={{0,1},{1,2},{2,3},{3,0},{4,5},{5,6},{6,7},{7,4},{8,9},{9,10},{10,1... | collective-permute-start | bytes 1179656 | tf_op jit(solution)/shard_map/conv_reduce/ppermute | solution.py:49
  50.4 32.8 %collective-permute-start.22 = (bf16[256,768]{1,0:T(8,128)(2,1)}, bf16[256,768]{1,0:T(8,128)(2,1)}, u32[]{:S(2)}, u32[]{:S(2)}) collective-permute-start(bf16[256,768]{1,0:T(8,128)(2,1)} %collective-permute-done.20), channel_id=1, source_target_pairs={{0,1},{1,2},{2,3},{4,5},{5,6},{6,7},{8,9},{9,10},{10,11},{12,13},{... | collective-permute-start | bytes 1179656 | tf_op jit(solution)/shard_map/out_projection/ppermute | solution.py:102
  53.7 52.6 %collective-permute-start.23 = (bf16[256,768]{1,0:T(8,128)(2,1)}, bf16[256,768]{1,0:T(8,128)(2,1)}, u32[]{:S(2)}, u32[]{:S(2)}) collective-permute-start(bf16[256,768]{1,0:T(8,128)(2,1)} %collective-permute-done.21), channel_id=1, source_target_pairs={{1,0},{2,1},{3,2},{5,4},{6,5},{7,6},{9,8},{10,9},{11,10},{13,12},{... | collective-permute-start | bytes 1179656 | tf_op jit(solution)/shard_map/out_projection/ppermute | solution.py:103
  79.6 41.8 %collective-permute-start.10 = (bf16[128,1536]{1,0:T(8,128)(2,1)S(1)}, bf16[128,1536]{1,0:T(8,128)(2,1)S(1)}, u32[]{:S(2)}, u32[]{:S(2)}) collective-permute-start(bf16[128,1536]{1,0:T(8,128)(2,1)S(1)} %multiply_convert_fusion), channel_id=1, source_target_pairs={{0,3},{1,0},{2,1},{3,2},{4,7},{5,4},{6,5},{7,6},{8,11},{9,8},{10,9... | collective-permute-start | bytes 1179656 | tf_op jit(solution)/shard_map/attn_in_gather/ppermute | solution.py:153
  79.7 41.2 %collective-permute-start.9 = (bf16[128,1536]{1,0:T(8,128)(2,1)S(1)}, bf16[128,1536]{1,0:T(8,128)(2,1)S(1)}, u32[]{:S(2)}, u32[]{:S(2)}) collective-permute-start(bf16[128,1536]{1,0:T(8,128)(2,1)S(1)} %multiply_convert_fusion), channel_id=1, source_target_pairs={{0,2},{1,3},{2,0},{3,1},{4,6},{5,7},{6,4},{7,5},{8,10},{9,11},{10,... | collective-permute-start | bytes 1179656 | tf_op jit(solution)/shard_map/attn_in_gather/ppermute | solution.py:153
  81.3 30.0 %collective-permute-start.8 = (bf16[128,1536]{1,0:T(8,128)(2,1)S(1)}, bf16[128,1536]{1,0:T(8,128)(2,1)S(1)}, u32[]{:S(2)}, u32[]{:S(2)}) collective-permute-start(bf16[128,1536]{1,0:T(8,128)(2,1)S(1)} %multiply_convert_fusion), channel_id=1, source_target_pairs={{0,1},{1,2},{2,3},{3,0},{4,5},{5,6},{6,7},{7,4},{8,9},{9,10},{10,1... | collective-permute-start | bytes 1179656 | tf_op jit(solution)/shard_map/attn_in_gather/ppermute | solution.py:153
  83.2 53.4 %collective-permute-start.24 = (bf16[256,768]{1,0:T(8,128)(2,1)}, bf16[256,768]{1,0:T(8,128)(2,1)}, u32[]{:S(2)}, u32[]{:S(2)}) collective-permute-start(bf16[256,768]{1,0:T(8,128)(2,1)} %collective-permute-done.22), channel_id=1, source_target_pairs={{0,1},{1,2},{2,3},{4,5},{5,6},{6,7},{8,9},{9,10},{10,11},{12,13},{... | collective-permute-start | bytes 1179656 | tf_op jit(solution)/shard_map/out_projection/ppermute | solution.py:102
  106.4 32.0 %collective-permute-start.25 = (bf16[256,768]{1,0:T(8,128)(2,1)}, bf16[256,768]{1,0:T(8,128)(2,1)}, u32[]{:S(2)}, u32[]{:S(2)}) collective-permute-start(bf16[256,768]{1,0:T(8,128)(2,1)} %collective-permute-done.23), channel_id=1, source_target_pairs={{1,0},{2,1},{3,2},{5,4},{6,5},{7,6},{9,8},{10,9},{11,10},{13,12},{... | collective-permute-start | bytes 1179656 | tf_op jit(solution)/shard_map/out_projection/ppermute | solution.py:103
  124.8 5.8 %collective-permute-start.11 = (bf16[2,256,256]{2,1,0:T(8,128)(2,1)S(1)}, bf16[2,256,256]{2,1,0:T(8,128)(2,1)S(1)}, u32[]{:S(2)}, u32[]{:S(2)}) collective-permute-start(bf16[2,256,256]{2,1,0:T(8,128)(2,1)S(1)} %get-tuple-element.20), channel_id=1, source_target_pairs={{0,4},{4,8},{8,12},{12,0},{1,5},{5,9},{9,13},{13,1},{2,6},{6,10},{... | collective-permute-start | bytes 786440 | tf_op jit(solution)/shard_map/kv_ring/ppermute | solution.py:246
  127.5 6.8 %collective-permute-start.12 = (bf16[2,256,256]{2,1,0:T(8,128)(2,1)S(1)}, bf16[2,256,256]{2,1,0:T(8,128)(2,1)S(1)}, u32[]{:S(2)}, u32[]{:S(2)}) collective-permute-start(bf16[2,256,256]{2,1,0:T(8,128)(2,1)S(1)} %get-tuple-element.21), channel_id=1, source_target_pairs={{4,0},{8,4},{12,8},{0,12},{5,1},{9,5},{13,9},{1,13},{6,2},{10,6},{... | collective-permute-start | bytes 786440 | tf_op jit(solution)/shard_map/kv_ring/ppermute | solution.py:247
  130.6 15.1 %collective-permute-start.13 = (bf16[2,256,256]{2,1,0:T(8,128)(2,1)S(1)}, bf16[2,256,256]{2,1,0:T(8,128)(2,1)S(1)}, u32[]{:S(2)}, u32[]{:S(2)}) collective-permute-start(bf16[2,256,256]{2,1,0:T(8,128)(2,1)S(1)} %collective-permute-done.11), channel_id=1, source_target_pairs={{0,4},{4,8},{8,12},{12,0},{1,5},{5,9},{9,13},{13,1},{2,6},{6,10},{... | collective-permute-start | bytes 786440 | tf_op jit(solution)/shard_map/kv_ring/ppermute | solution.py:246
  134.3 9.3 %collective-permute-start.14 = (bf16[2,256,256]{2,1,0:T(8,128)(2,1)S(1)}, bf16[2,256,256]{2,1,0:T(8,128)(2,1)S(1)}, u32[]{:S(2)}, u32[]{:S(2)}) collective-permute-start(bf16[2,256,256]{2,1,0:T(8,128)(2,1)S(1)} %collective-permute-done.12), channel_id=1, source_target_pairs={{4,0},{8,4},{12,8},{0,12},{5,1},{9,5},{13,9},{1,13},{6,2},{10,6},{... | collective-permute-start | bytes 786440 | tf_op jit(solution)/shard_map/kv_ring/ppermute | solution.py:247
  142.8 28.8 %collective-permute-start.26 = (bf16[1024,768]{1,0:T(8,128)(2,1)}, bf16[1024,768]{1,0:T(8,128)(2,1)}, u32[]{:S(2)}, u32[]{:S(2)}) collective-permute-start(bf16[1024,768]{1,0:T(8,128)(2,1)} %bitcast.57), channel_id=1, source_target_pairs={{0,4},{4,0},{8,12},{12,8},{1,5},{5,1},{9,13},{13,9},{2,6},{6,2},{1... | collective-permute-start | bytes 4718600 | tf_op jit(solution)/shard_map/out_projection/ppermute | solution.py:133
  143.7 8.1 %collective-permute-start.16 = (bf16[2,256,256]{2,1,0:T(8,128)(2,1)S(1)}, bf16[2,256,256]{2,1,0:T(8,128)(2,1)S(1)}, u32[]{:S(2)}, u32[]{:S(2)}) collective-permute-start(bf16[2,256,256]{2,1,0:T(8,128)(2,1)S(1)} %collective-permute-done.14), channel_id=1, source_target_pairs={{4,0},{8,4},{12,8},{0,12},{5,1},{9,5},{13,9},{1,13},{6,2},{10,6},{... | collective-permute-start | bytes 786440 | tf_op jit(solution)/shard_map/kv_ring/ppermute | solution.py:247
  145.7 6.7 %collective-permute-start.15 = (bf16[2,256,256]{2,1,0:T(8,128)(2,1)S(1)}, bf16[2,256,256]{2,1,0:T(8,128)(2,1)S(1)}, u32[]{:S(2)}, u32[]{:S(2)}) collective-permute-start(bf16[2,256,256]{2,1,0:T(8,128)(2,1)S(1)} %collective-permute-done.13), channel_id=1, source_target_pairs={{0,4},{4,8},{8,12},{12,0},{1,5},{5,9},{9,13},{13,1},{2,6},{6,10},{... | collective-permute-start | bytes 786440 | tf_op jit(solution)/shard_map/kv_ring/ppermute | solution.py:246
  161.3 4.5 %collective-permute-start.19 = (bf16[128,256]{1,0:T(8,128)(2,1)}, bf16[128,256]{1,0:T(8,128)(2,1)S(1)}, u32[]{:S(2)}, u32[]{:S(2)}) collective-permute-start(bf16[128,256]{1,0:T(8,128)(2,1)} %get-tuple-element.28), channel_id=1, source_target_pairs={{0,3},{1,0},{2,1},{3,2},{4,7},{5,4},{6,5},{7,6},{8,11},{9,8},{10,9... | collective-permute-start | bytes 196616 | tf_op jit(solution)/shard_map/out_projection/ppermute | solution.py:120
  161.3 6.2 %collective-permute-start.18 = (bf16[128,256]{1,0:T(8,128)(2,1)}, bf16[128,256]{1,0:T(8,128)(2,1)S(1)}, u32[]{:S(2)}, u32[]{:S(2)}) collective-permute-start(bf16[128,256]{1,0:T(8,128)(2,1)} %get-tuple-element.29), channel_id=1, source_target_pairs={{0,2},{1,3},{2,0},{3,1},{4,6},{5,7},{6,4},{7,5},{8,10},{9,11},{10,... | collective-permute-start | bytes 196616 | tf_op jit(solution)/shard_map/out_projection/ppermute | solution.py:120
  161.4 7.7 %collective-permute-start.17 = (bf16[128,256]{1,0:T(8,128)(2,1)}, bf16[128,256]{1,0:T(8,128)(2,1)}, u32[]{:S(2)}, u32[]{:S(2)}) collective-permute-start(bf16[128,256]{1,0:T(8,128)(2,1)} %get-tuple-element.30), channel_id=1, source_target_pairs={{0,1},{1,2},{2,3},{3,0},{4,5},{5,6},{6,7},{7,4},{8,9},{9,10},{10,1... | collective-permute-start | bytes 196616 | tf_op jit(solution)/shard_map/out_projection/ppermute | solution.py:120
  177.0 5.4 %collective-permute-start.27 = (bf16[8,256]{1,0:T(8,128)(2,1)S(1)}, bf16[8,256]{1,0:T(8,128)(2,1)S(1)}, u32[]{:S(2)}, u32[]{:S(2)}) collective-permute-start(bf16[8,256]{1,0:T(8,128)(2,1)S(1)} %get-tuple-element.58), channel_id=1, source_target_pairs={{0,1},{1,2},{2,3},{3,0},{4,5},{5,6},{6,7},{7,4},{8,9},{9,10},{10,1... | collective-permute-start | bytes 12296 | tf_op jit(solution)/shard_map/sides_gather/ppermute | solution.py:167
  178.3 4.5 %collective-permute-start.28 = (bf16[8,256]{1,0:T(8,128)(2,1)S(1)}, bf16[8,256]{1,0:T(8,128)(2,1)S(1)}, u32[]{:S(2)}, u32[]{:S(2)}) collective-permute-start(bf16[8,256]{1,0:T(8,128)(2,1)S(1)} %get-tuple-element.58), channel_id=1, source_target_pairs={{0,2},{1,3},{2,0},{3,1},{4,6},{5,7},{6,4},{7,5},{8,10},{9,11},{10,... | collective-permute-start | bytes 12296 | tf_op jit(solution)/shard_map/sides_gather/ppermute | solution.py:167
  180.2 3.6 %collective-permute-start.29 = (bf16[8,256]{1,0:T(8,128)(2,1)S(1)}, bf16[8,256]{1,0:T(8,128)(2,1)S(1)}, u32[]{:S(2)}, u32[]{:S(2)}) collective-permute-start(bf16[8,256]{1,0:T(8,128)(2,1)S(1)} %get-tuple-element.58), channel_id=1, source_target_pairs={{0,3},{1,0},{2,1},{3,2},{4,7},{5,4},{6,5},{7,6},{8,11},{9,8},{10,9... | collective-permute-start | bytes 12296 | tf_op jit(solution)/shard_map/sides_gather/ppermute | solution.py:167
  183.8 6.3 %collective-permute-start.32 = (bf16[32,256]{1,0:T(8,128)(2,1)S(1)}, bf16[32,256]{1,0:T(8,128)(2,1)S(1)}, u32[]{:S(2)}, u32[]{:S(2)}) collective-permute-start(bf16[32,256]{1,0:T(8,128)(2,1)S(1)} %bitcast.333), channel_id=1, source_target_pairs={{0,12},{4,0},{8,4},{12,8},{1,13},{5,1},{9,5},{13,9},{2,14},{6,2},{... | collective-permute-start | bytes 49160 | tf_op jit(solution)/shard_map/sides_gather/ppermute | solution.py:167
  184.1 5.9 %collective-permute-start.31 = (bf16[32,256]{1,0:T(8,128)(2,1)S(1)}, bf16[32,256]{1,0:T(8,128)(2,1)S(1)}, u32[]{:S(2)}, u32[]{:S(2)}) collective-permute-start(bf16[32,256]{1,0:T(8,128)(2,1)S(1)} %bitcast.334), channel_id=1, source_target_pairs={{0,8},{4,12},{8,0},{12,4},{1,9},{5,13},{9,1},{13,5},{2,10},{6,14},... | collective-permute-start | bytes 49160 | tf_op jit(solution)/shard_map/sides_gather/ppermute | solution.py:167
  186.9 3.2 %collective-permute-start.30 = (bf16[32,256]{1,0:T(8,128)(2,1)S(1)}, bf16[32,256]{1,0:T(8,128)(2,1)S(1)}, u32[]{:S(2)}, u32[]{:S(2)}) collective-permute-start(bf16[32,256]{1,0:T(8,128)(2,1)S(1)} %bitcast.335), channel_id=1, source_target_pairs={{0,4},{4,8},{8,12},{12,0},{1,5},{5,9},{9,13},{13,1},{2,6},{6,10},{... | collective-permute-start | bytes 49160 | tf_op jit(solution)/shard_map/sides_gather/ppermute | solution.py:167
  (13 other events, 218.2 us)

commit v10 on v6

--- a/solution.py
+++ b/solution.py
@@ -107,7 +107,7 @@
     core = lax.axis_index(chip_axis) % 2
     half = weight.shape[1] // 2
     mine = lax.dynamic_slice_in_dim(weight, core * half, half, 1)
-    gathered = line_all_gather(mine, axis)
+    gathered = lax.all_gather(mine, axis, axis=0, tiled=True)
     other = lax.ppermute(gathered, chip_axis, [(i, i ^ 1) for i in range(peers)])
     return jnp.where(
         core == 0,

time: 181 us -> 207 us (1.14)
  between operations: 1.44 us -> 14.7 us
  waiting for transfers between devices: 82.4 us -> 93.4 us
  local copies, waits for them, and re-layouts: 16 us -> 9.07 us
  matrix products: 21 us -> 27 us
  other arithmetic: 2.39 us -> 5.26 us
    ppermute x6 -> x0, starting transfers between devices: 16.7 us -> none  [the longest x3 12.9 us: line_all_gather(): flow_r = lax.ppermute(flow_r, axis, right)]
    ppermute x9, waiting for transfers between devices: 26.7 us -> 42.5 us  [direct_all_gather(): lax.ppermute(value, axis, [(i, (i + shift) % n) for i in range(n)])]
    dynamic_update_slice x7 -> x0, local copies, waits for them, and re-layouts: 7.59 us -> none  [the longest x3 3.34 us: line_all_gather(): slots = lax.dynamic_update_index_in_dim(slots, flow_l, at_l, 0)]
    ppermute x9, starting transfers between devices: 9.85 us -> 17.4 us  [direct_all_gather(): lax.ppermute(value, axis, [(i, (i + shift) % n) for i in range(n)])]
    ppermute x3, starting transfers between devices: 11.4 us -> 18.1 us  [rows_to_heads(): lax.ppermute(outgoing, axis, [(i, (i + shift) % n) for i in range(n)])]
    ppermute x3, waiting for transfers between devices: 9.47 us -> 15.4 us  [shards(): next_going = lax.ppermute(going, 'seq', forward)]
    ppermute x3, waiting for transfers between devices: 10.3 us -> 5.16 us  [permute_all_to_all(): lax.ppermute(outgoing, axis, [(i, (i + shift) % n) for i in range(n)])]
    ppermute x3, waiting for transfers between devices: 4.77 us -> 0.01 us  [shards(): next_coming = lax.ppermute(coming, 'seq', backward)]
  transfers between devices with their start and end apart: 33 -> 28, of which waited for: 18 -> 17; matrix products, arithmetic and copies ran while one was open for 17% -> 12% of each run, Pallas kernels for 0% -> 0%
where the time goes in v10:
time: 207 us; the launch traced here: 206 us
  waiting for transfers between devices  93.4 us (45%)
  starting transfers between devices  56.8 us (27%)
  matrix products  27 us (13%)
  between operations  14.7 us (7%)
  local copies, waits for them, and re-layouts  9.07 us (4%)
  other arithmetic  5.26 us (3%)
    ppermute x9, waiting for transfers between devices, direct_all_gather(): lax.ppermute(value, axis, [(i, (i + shift) % n) for i in range(n)])  42.5 us
    ppermute x3, waiting for transfers between devices, direct_reduce_scatter(): lax.ppermute(outgoing, axis, [(i, (i + shift) % n) for i in range(n)])  25.8 us
    ppermute x3, starting transfers between devices, rows_to_heads(): lax.ppermute(outgoing, axis, [(i, (i + shift) % n) for i in range(n)])  18.1 us
    ppermute x9, starting transfers between devices, direct_all_gather(): lax.ppermute(value, axis, [(i, (i + shift) % n) for i in range(n)])  17.4 us
    ppermute x3, waiting for transfers between devices, shards(): next_going = lax.ppermute(going, 'seq', forward)  15.4 us
    dot_general x8, matrix products, attend(): jnp.einsum('hqk,hkd->hqd', weights.astype(jnp.bfloat16), value_block, pre...  8.84 us
    ppermute x3, starting transfers between devices, permute_all_to_all(): lax.ppermute(outgoing, axis, [(i, (i + shift) % n) for i in range(n)])  7.13 us
    dot_general x5, matrix products, conv_rows(): jnp.dot(shifted, conv_weight[offset], preferred_element_type=jnp.float32)  6.46 us
  transfers between devices with their start and end apart: 28, of which 17 were waited for; matrix products, arithmetic and copies ran while one was open for 12% of the time, Pallas kernels for 0%

profile of v10, /device:TPU:0, one launch (start us, length us, event | category | flops | bytes accessed | tf_op | source)
XLA Modules:
  0.0 206.2 jit_solution(11423683162625415730)
XLA Ops:
  10.7 3.1 %collective-permute-start = (bf16[128,384]{1,0:T(8,128)(2,1)S(1)}, bf16[128,384]{1,0:T(8,128)(2,1)S(1)}, u32[]{:S(2)}, u32[]{:S(2)}) collective-permute-start(bf16[128,384]{1,0:T(8,128)(2,1)S(1)} %bitcast.300), channel_id=1, source_target_pairs={{0,1},{1,2},{2,3},{3,0},{4,5},{5,6},{6,7},{7,4},{8,9},{9,10},{10,1... | collective-permute-start | bytes 294920 | tf_op jit(solution)/shard_map/ppermute | solution.py:65
  13.8 2.7 %collective-permute-start.1 = (bf16[128,384]{1,0:T(8,128)(2,1)S(1)}, bf16[128,384]{1,0:T(8,128)(2,1)S(1)}, u32[]{:S(2)}, u32[]{:S(2)}) collective-permute-start(bf16[128,384]{1,0:T(8,128)(2,1)S(1)} %bitcast.299), channel_id=1, source_target_pairs={{0,2},{1,3},{2,0},{3,1},{4,6},{5,7},{6,4},{7,5},{8,10},{9,11},{10,... | collective-permute-start | bytes 294920 | tf_op jit(solution)/shard_map/ppermute | solution.py:65
  18.0 1.5 collective-permute-done
  19.5 3.5 %collective-permute-done.1 = bf16[128,384]{1,0:T(8,128)(2,1)S(1)} collective-permute-done((bf16[128,384]{1,0:T(8,128)(2,1)S(1)}, bf16[128,384]{1,0:T(8,128)(2,1)S(1)}, u32[]{:S(2)}, u32[]{:S(2)}) %collective-permute-start.1) | collective-permute-done | bytes 98336 | tf_op jit(solution)/shard_map/ppermute | solution.py:65
  23.2 1.7 collective-permute-start.3
  24.9 1.6 collective-permute-start.4
  26.4 2.4 %fusion.37 = f32[512,1536]{1,0:T(8,128)S(1)} fusion(bf16[512,384]{1,0:T(8,128)(2,1)S(1)} %bitcast.287, bf16[5,384,1536]{2,1,0:T(8,128)(2,1)} %param.12), kind=kOutput, calls=%fused_computation.62 | convolution fusion | flops 603979776 | bytes 4718592 | tf_op jit(solution)/shard_map/conv_reduce/dot_general | solution.py:39
  34.0 2.4 %collective-permute-start.5 = (bf16[128,1536]{1,0:T(8,128)(2,1)S(1)}, bf16[128,1536]{1,0:T(8,128)(2,1)S(1)}, u32[]{:S(2)}, u32[]{:S(2)}) collective-permute-start(bf16[128,1536]{1,0:T(8,128)(2,1)S(1)} %get-tuple-element.22), channel_id=1, source_target_pairs={{0,1},{1,2},{2,3},{3,0},{4,5},{5,6},{6,7},{7,4},{8,9},{9,10},{10,1... | collective-permute-start | bytes 1179656 | tf_op jit(solution)/shard_map/conv_reduce/ppermute | solution.py:51
  36.4 1.7 collective-permute-start.6
  38.9 7.8 %collective-permute-done.5 = bf16[128,1536]{1,0:T(8,128)(2,1)S(1)} collective-permute-done((bf16[128,1536]{1,0:T(8,128)(2,1)S(1)}, bf16[128,1536]{1,0:T(8,128)(2,1)S(1)}, u32[]{:S(2)}, u32[]{:S(2)}) %collective-permute-start.5) | collective-permute-done | bytes 393248 | tf_op jit(solution)/shard_map/conv_reduce/ppermute | solution.py:51
  46.7 17.9 %collective-permute-done.6 = bf16[128,1536]{1,0:T(8,128)(2,1)S(1)} collective-permute-done((bf16[128,1536]{1,0:T(8,128)(2,1)S(1)}, bf16[128,1536]{1,0:T(8,128)(2,1)S(1)}, u32[]{:S(2)}, u32[]{:S(2)}) %collective-permute-start.6) | collective-permute-done | bytes 393248 | tf_op jit(solution)/shard_map/conv_reduce/ppermute | solution.py:51
  67.2 9.0 %collective-permute-start.8 = (bf16[128,1536]{1,0:T(8,128)(2,1)S(1)}, bf16[128,1536]{1,0:T(8,128)(2,1)S(1)}, u32[]{:S(2)}, u32[]{:S(2)}) collective-permute-start(bf16[128,1536]{1,0:T(8,128)(2,1)S(1)} %get-tuple-element.19), channel_id=1, source_target_pairs={{0,1},{1,2},{2,3},{3,0},{4,5},{5,6},{6,7},{7,4},{8,9},{9,10},{10,1... | collective-permute-start | bytes 1179656 | tf_op jit(solution)/shard_map/attn_in_gather/ppermute | solution.py:127
  76.2 1.8 constant_dynamic-slice_fusion.1
  78.1 2.4 %collective-permute-start.10 = (bf16[128,1536]{1,0:T(8,128)(2,1)S(1)}, bf16[128,1536]{1,0:T(8,128)(2,1)S(1)}, u32[]{:S(2)}, u32[]{:S(2)}) collective-permute-start(bf16[128,1536]{1,0:T(8,128)(2,1)S(1)} %get-tuple-element.19), channel_id=1, source_target_pairs={{0,3},{1,0},{2,1},{3,2},{4,7},{5,4},{6,5},{7,6},{8,11},{9,8},{10,9... | collective-permute-start | bytes 1179656 | tf_op jit(solution)/shard_map/attn_in_gather/ppermute | solution.py:127
  80.5 6.2 %collective-permute-done.8 = bf16[128,1536]{1,0:T(8,128)(2,1)S(1)} collective-permute-done((bf16[128,1536]{1,0:T(8,128)(2,1)S(1)}, bf16[128,1536]{1,0:T(8,128)(2,1)S(1)}, u32[]{:S(2)}, u32[]{:S(2)}) %collective-permute-start.8) | collective-permute-done | bytes 393248 | tf_op jit(solution)/shard_map/attn_in_gather/ppermute | solution.py:127
  87.4 31.4 %collective-permute-done.9 = bf16[128,1536]{1,0:T(8,128)(2,1)S(1)} collective-permute-done((bf16[128,1536]{1,0:T(8,128)(2,1)S(1)}, bf16[128,1536]{1,0:T(8,128)(2,1)S(1)}, u32[]{:S(2)}, u32[]{:S(2)}) %collective-permute-start.9) | collective-permute-done | bytes 393248 | tf_op jit(solution)/shard_map/attn_in_gather/ppermute | solution.py:127
  120.4 2.8 %convolution_convert_fusion = bf16[512,768]{1,0:T(8,128)(2,1)S(1)} fusion(bf16[512,1536]{1,0:T(8,128)(2,1)} %bitcast.22, bf16[1536,768]{1,0:T(8,128)(2,1)S(1)} %copy-done), kind=kOutput, calls=%fused_computation.14 | convolution fusion | flops 1208352768 | bytes 4718592 | tf_op jit(solution)/shard_map/dot_general | solution.py:164
  123.7 1.8 collective-permute-start.12
  125.8 5.4 %collective-permute-done.11 = bf16[2,256,256]{2,1,0:T(8,128)(2,1)S(1)} collective-permute-done((bf16[2,256,256]{2,1,0:T(8,128)(2,1)S(1)}, bf16[2,256,256]{2,1,0:T(8,128)(2,1)S(1)}, u32[]{:S(2)}, u32[]{:S(2)}) %collective-permute-start.11) | collective-permute-done | bytes 262176 | tf_op jit(solution)/shard_map/kv_ring/ppermute | solution.py:205
  131.6 1.8 collective-permute-start.14
  133.7 5.4 %collective-permute-done.13 = bf16[2,256,256]{2,1,0:T(8,128)(2,1)S(1)} collective-permute-done((bf16[2,256,256]{2,1,0:T(8,128)(2,1)S(1)}, bf16[2,256,256]{2,1,0:T(8,128)(2,1)S(1)}, u32[]{:S(2)}, u32[]{:S(2)}) %collective-permute-start.13) | collective-permute-done | bytes 262176 | tf_op jit(solution)/shard_map/kv_ring/ppermute | solution.py:205
  139.7 2.0 collective-permute-start.16
  141.7 4.6 %collective-permute-done.15 = bf16[2,256,256]{2,1,0:T(8,128)(2,1)S(1)} collective-permute-done((bf16[2,256,256]{2,1,0:T(8,128)(2,1)S(1)}, bf16[2,256,256]{2,1,0:T(8,128)(2,1)S(1)}, u32[]{:S(2)}, u32[]{:S(2)}) %collective-permute-start.15) | collective-permute-done | bytes 262176 | tf_op jit(solution)/shard_map/kv_ring/ppermute | solution.py:205
  154.1 1.7 convolution_bitcast_fusion
  155.8 1.9 fusion.22
  159.6 15.6 %collective-permute-start.17 = (bf16[128,256]{1,0:T(8,128)(2,1)S(1)}, bf16[128,256]{1,0:T(8,128)(2,1)S(1)}, u32[]{:S(2)}, u32[]{:S(2)}) collective-permute-start(bf16[128,256]{1,0:T(8,128)(2,1)S(1)} %get-tuple-element.35), channel_id=1, source_target_pairs={{0,1},{1,2},{2,3},{3,0},{4,5},{5,6},{6,7},{7,4},{8,9},{9,10},{10,1... | collective-permute-start | bytes 196616 | tf_op jit(solution)/shard_map/out_projection/ppermute | solution.py:98
  175.2 2.4 %collective-permute-start.19 = (bf16[128,256]{1,0:T(8,128)(2,1)S(1)}, bf16[128,256]{1,0:T(8,128)(2,1)S(1)}, u32[]{:S(2)}, u32[]{:S(2)}) collective-permute-start(bf16[128,256]{1,0:T(8,128)(2,1)S(1)} %get-tuple-element.33), channel_id=1, source_target_pairs={{0,3},{1,0},{2,1},{3,2},{4,7},{5,4},{6,5},{7,6},{8,11},{9,8},{10,9... | collective-permute-start | bytes 196616 | tf_op jit(solution)/shard_map/out_projection/ppermute | solution.py:98
  177.8 3.6 %collective-permute-done.18 = bf16[128,256]{1,0:T(8,128)(2,1)S(1)} collective-permute-done((bf16[128,256]{1,0:T(8,128)(2,1)S(1)}, bf16[128,256]{1,0:T(8,128)(2,1)S(1)}, u32[]{:S(2)}, u32[]{:S(2)}) %collective-permute-start.18) | collective-permute-done | bytes 65568 | tf_op jit(solution)/shard_map/out_projection/ppermute | solution.py:98
  181.8 4.9 %convert_reduce_fusion = (f32[8,1536]{1,0:T(8,128)S(1)}, bf16[128,1536]{1,0:T(8,128)(2,1)}) fusion(bf16[128,1024]{0,1:T(8,128)(2,1)S(1)} %bitcast.296, bf16[1024,768]{1,0:T(8,128)(2,1)} %collective-permute-done.20, bf16[1024,768]{1,0:T(8,128)(2,1)} %all-gather.2.cloned.1.call-done, pred[]{:T(512)S(6)} %eq.29, bf16[128,1536]{1,0:T(8,128)(2,1)S(1)} %copy-done.10), kind=kOutput, calls=%fused_computation.105 | convolution fusion | flops 417779712 | bytes 4243457 | tf_op jit(solution)/shard_map/out_projection/dot_general | solution.py:218
  187.2 1.8 collective-permute-start.21
  188.9 1.7 collective-permute-start.22
  194.5 1.6 collective-permute-start.26
  (151 shorter events, 35.6 us)
Async XLA Ops:
  7.2 113.3 %copy-start = (bf16[1536,768]{1,0:T(8,128)(2,1)S(1)}, bf16[1536,768]{1,0:T(8,128)(2,1)}, u32[]{:S(2)}) copy-start(bf16[1536,768]{1,0:T(8,128)(2,1)} %param.14) | copy-start | bytes 7077892
  7.2 146.5 %all-gather.2.cloned.1.call-start = ((), (), s32[]{:S(2)}) async-start(), calls=%async_computation | async-start | bytes 1966080 | tf_op jit(solution)/shard_map/out_projection/all_gather | solution.py:110
  10.7 8.7 %collective-permute-start = (bf16[128,384]{1,0:T(8,128)(2,1)S(1)}, bf16[128,384]{1,0:T(8,128)(2,1)S(1)}, u32[]{:S(2)}, u32[]{:S(2)}) collective-permute-start(bf16[128,384]{1,0:T(8,128)(2,1)S(1)} %bitcast.300), channel_id=1, source_target_pairs={{0,1},{1,2},{2,3},{3,0},{4,5},{5,6},{6,7},{7,4},{8,9},{9,10},{10,1... | collective-permute-start | bytes 294920 | tf_op jit(solution)/shard_map/ppermute | solution.py:65
  13.8 9.2 %collective-permute-start.1 = (bf16[128,384]{1,0:T(8,128)(2,1)S(1)}, bf16[128,384]{1,0:T(8,128)(2,1)S(1)}, u32[]{:S(2)}, u32[]{:S(2)}) collective-permute-start(bf16[128,384]{1,0:T(8,128)(2,1)S(1)} %bitcast.299), channel_id=1, source_target_pairs={{0,2},{1,3},{2,0},{3,1},{4,6},{5,7},{6,4},{7,5},{8,10},{9,11},{10,... | collective-permute-start | bytes 294920 | tf_op jit(solution)/shard_map/ppermute | solution.py:65
  16.5 6.7 %collective-permute-start.2 = (bf16[128,384]{1,0:T(8,128)(2,1)S(1)}, bf16[128,384]{1,0:T(8,128)(2,1)S(1)}, u32[]{:S(2)}, u32[]{:S(2)}) collective-permute-start(bf16[128,384]{1,0:T(8,128)(2,1)S(1)} %bitcast.298), channel_id=1, source_target_pairs={{0,3},{1,0},{2,1},{3,2},{4,7},{5,4},{6,5},{7,6},{8,11},{9,8},{10,9... | collective-permute-start | bytes 294920 | tf_op jit(solution)/shard_map/ppermute | solution.py:65
  23.2 8.5 %collective-permute-start.3 = (bf16[8,384]{1,0:T(8,128)(2,1)S(1)}, bf16[8,384]{1,0:T(8,128)(2,1)S(1)}, u32[]{:S(2)}, u32[]{:S(2)}) collective-permute-start(bf16[8,384]{1,0:T(8,128)(2,1)S(1)} %get-tuple-element.27), channel_id=1, source_target_pairs={{0,4},{4,8},{8,12},{1,5},{5,9},{9,13},{2,6},{6,10},{10,14},{3,7},{... | collective-permute-start | bytes 18440 | tf_op jit(solution)/shard_map/ppermute | solution.py:25
  24.9 4.8 %collective-permute-start.4 = (bf16[8,384]{1,0:T(8,128)(2,1)S(1)}, bf16[8,384]{1,0:T(8,128)(2,1)S(1)}, u32[]{:S(2)}, u32[]{:S(2)}) collective-permute-start(bf16[8,384]{1,0:T(8,128)(2,1)S(1)} %get-tuple-element.28), channel_id=1, source_target_pairs={{4,0},{8,4},{12,8},{5,1},{9,5},{13,9},{6,2},{10,6},{14,10},{7,3},{... | collective-permute-start | bytes 18440 | tf_op jit(solution)/shard_map/ppermute | solution.py:26
  32.7 32.0 %copy-start.7 = (bf16[128,1536]{1,0:T(8,128)(2,1)S(1)}, bf16[128,1536]{1,0:T(8,128)(2,1)}, u32[]{:S(2)}) copy-start(bf16[128,1536]{1,0:T(8,128)(2,1)} %param.10) | copy-start | bytes 1179652
  33.8 32.5 %copy-start.18 = (f32[1536]{0:T(1024)S(1)}, f32[1536]{0:T(1024)}, u32[]{:S(2)}) copy-start(f32[1536]{0:T(1024)} %param.13) | copy-start | bytes 18436
  34.0 12.7 %collective-permute-start.5 = (bf16[128,1536]{1,0:T(8,128)(2,1)S(1)}, bf16[128,1536]{1,0:T(8,128)(2,1)S(1)}, u32[]{:S(2)}, u32[]{:S(2)}) collective-permute-start(bf16[128,1536]{1,0:T(8,128)(2,1)S(1)} %get-tuple-element.22), channel_id=1, source_target_pairs={{0,1},{1,2},{2,3},{3,0},{4,5},{5,6},{6,7},{7,4},{8,9},{9,10},{10,1... | collective-permute-start | bytes 1179656 | tf_op jit(solution)/shard_map/conv_reduce/ppermute | solution.py:51
  36.4 28.2 %collective-permute-start.6 = (bf16[128,1536]{1,0:T(8,128)(2,1)S(1)}, bf16[128,1536]{1,0:T(8,128)(2,1)S(1)}, u32[]{:S(2)}, u32[]{:S(2)}) collective-permute-start(bf16[128,1536]{1,0:T(8,128)(2,1)S(1)} %get-tuple-element.24), channel_id=1, source_target_pairs={{0,2},{1,3},{2,0},{3,1},{4,6},{5,7},{6,4},{7,5},{8,10},{9,11},{10,... | collective-permute-start | bytes 1179656 | tf_op jit(solution)/shard_map/conv_reduce/ppermute | solution.py:51
  38.1 26.5 %collective-permute-start.7 = (bf16[128,1536]{1,0:T(8,128)(2,1)S(1)}, bf16[128,1536]{1,0:T(8,128)(2,1)S(1)}, u32[]{:S(2)}, u32[]{:S(2)}) collective-permute-start(bf16[128,1536]{1,0:T(8,128)(2,1)S(1)} %get-tuple-element.23), channel_id=1, source_target_pairs={{0,3},{1,0},{2,1},{3,2},{4,7},{5,4},{6,5},{7,6},{8,11},{9,8},{10,9... | collective-permute-start | bytes 1179656 | tf_op jit(solution)/shard_map/conv_reduce/ppermute | solution.py:51
  67.2 19.4 %collective-permute-start.8 = (bf16[128,1536]{1,0:T(8,128)(2,1)S(1)}, bf16[128,1536]{1,0:T(8,128)(2,1)S(1)}, u32[]{:S(2)}, u32[]{:S(2)}) collective-permute-start(bf16[128,1536]{1,0:T(8,128)(2,1)S(1)} %get-tuple-element.19), channel_id=1, source_target_pairs={{0,1},{1,2},{2,3},{3,0},{4,5},{5,6},{6,7},{7,4},{8,9},{9,10},{10,1... | collective-permute-start | bytes 1179656 | tf_op jit(solution)/shard_map/attn_in_gather/ppermute | solution.py:127
  78.0 40.8 %collective-permute-start.9 = (bf16[128,1536]{1,0:T(8,128)(2,1)S(1)}, bf16[128,1536]{1,0:T(8,128)(2,1)S(1)}, u32[]{:S(2)}, u32[]{:S(2)}) collective-permute-start(bf16[128,1536]{1,0:T(8,128)(2,1)S(1)} %get-tuple-element.19), channel_id=1, source_target_pairs={{0,2},{1,3},{2,0},{3,1},{4,6},{5,7},{6,4},{7,5},{8,10},{9,11},{10,... | collective-permute-start | bytes 1179656 | tf_op jit(solution)/shard_map/attn_in_gather/ppermute | solution.py:127
  78.1 41.5 %collective-permute-start.10 = (bf16[128,1536]{1,0:T(8,128)(2,1)S(1)}, bf16[128,1536]{1,0:T(8,128)(2,1)S(1)}, u32[]{:S(2)}, u32[]{:S(2)}) collective-permute-start(bf16[128,1536]{1,0:T(8,128)(2,1)S(1)} %get-tuple-element.19), channel_id=1, source_target_pairs={{0,3},{1,0},{2,1},{3,2},{4,7},{5,4},{6,5},{7,6},{8,11},{9,8},{10,9... | collective-permute-start | bytes 1179656 | tf_op jit(solution)/shard_map/attn_in_gather/ppermute | solution.py:127
  123.4 7.9 %collective-permute-start.11 = (bf16[2,256,256]{2,1,0:T(8,128)(2,1)S(1)}, bf16[2,256,256]{2,1,0:T(8,128)(2,1)S(1)}, u32[]{:S(2)}, u32[]{:S(2)}) collective-permute-start(bf16[2,256,256]{2,1,0:T(8,128)(2,1)S(1)} %get-tuple-element.25), channel_id=1, source_target_pairs={{0,4},{4,8},{8,12},{12,0},{1,5},{5,9},{9,13},{13,1},{2,6},{6,10},{... | collective-permute-start | bytes 786440 | tf_op jit(solution)/shard_map/kv_ring/ppermute | solution.py:205
  123.7 7.8 %collective-permute-start.12 = (bf16[2,256,256]{2,1,0:T(8,128)(2,1)S(1)}, bf16[2,256,256]{2,1,0:T(8,128)(2,1)S(1)}, u32[]{:S(2)}, u32[]{:S(2)}) collective-permute-start(bf16[2,256,256]{2,1,0:T(8,128)(2,1)S(1)} %get-tuple-element.26), channel_id=1, source_target_pairs={{4,0},{8,4},{12,8},{0,12},{5,1},{9,5},{13,9},{1,13},{6,2},{10,6},{... | collective-permute-start | bytes 786440 | tf_op jit(solution)/shard_map/kv_ring/ppermute | solution.py:206
  131.2 7.8 %collective-permute-start.13 = (bf16[2,256,256]{2,1,0:T(8,128)(2,1)S(1)}, bf16[2,256,256]{2,1,0:T(8,128)(2,1)S(1)}, u32[]{:S(2)}, u32[]{:S(2)}) collective-permute-start(bf16[2,256,256]{2,1,0:T(8,128)(2,1)S(1)} %collective-permute-done.11), channel_id=1, source_target_pairs={{0,4},{4,8},{8,12},{12,0},{1,5},{5,9},{9,13},{13,1},{2,6},{6,10},{... | collective-permute-start | bytes 786440 | tf_op jit(solution)/shard_map/kv_ring/ppermute | solution.py:205
  131.6 7.9 %collective-permute-start.14 = (bf16[2,256,256]{2,1,0:T(8,128)(2,1)S(1)}, bf16[2,256,256]{2,1,0:T(8,128)(2,1)S(1)}, u32[]{:S(2)}, u32[]{:S(2)}) collective-permute-start(bf16[2,256,256]{2,1,0:T(8,128)(2,1)S(1)} %collective-permute-done.12), channel_id=1, source_target_pairs={{4,0},{8,4},{12,8},{0,12},{5,1},{9,5},{13,9},{1,13},{6,2},{10,6},{... | collective-permute-start | bytes 786440 | tf_op jit(solution)/shard_map/kv_ring/ppermute | solution.py:206
  139.1 7.3 %collective-permute-start.15 = (bf16[2,256,256]{2,1,0:T(8,128)(2,1)S(1)}, bf16[2,256,256]{2,1,0:T(8,128)(2,1)S(1)}, u32[]{:S(2)}, u32[]{:S(2)}) collective-permute-start(bf16[2,256,256]{2,1,0:T(8,128)(2,1)S(1)} %collective-permute-done.13), channel_id=1, source_target_pairs={{0,4},{4,8},{8,12},{12,0},{1,5},{5,9},{9,13},{13,1},{2,6},{6,10},{... | collective-permute-start | bytes 786440 | tf_op jit(solution)/shard_map/kv_ring/ppermute | solution.py:205
  139.7 7.3 %collective-permute-start.16 = (bf16[2,256,256]{2,1,0:T(8,128)(2,1)S(1)}, bf16[2,256,256]{2,1,0:T(8,128)(2,1)S(1)}, u32[]{:S(2)}, u32[]{:S(2)}) collective-permute-start(bf16[2,256,256]{2,1,0:T(8,128)(2,1)S(1)} %collective-permute-done.14), channel_id=1, source_target_pairs={{4,0},{8,4},{12,8},{0,12},{5,1},{9,5},{13,9},{1,13},{6,2},{10,6},{... | collective-permute-start | bytes 786440 | tf_op jit(solution)/shard_map/kv_ring/ppermute | solution.py:206
  153.7 28.1 %collective-permute-start.20 = (bf16[1024,768]{1,0:T(8,128)(2,1)}, bf16[1024,768]{1,0:T(8,128)(2,1)}, u32[]{:S(2)}, u32[]{:S(2)}) collective-permute-start(bf16[1024,768]{1,0:T(8,128)(2,1)} %all-gather.2.cloned.1.call-done), channel_id=1, source_target_pairs={{0,4},{4,0},{8,12},{12,8},{1,5},{5,1},{9,13},{13,9},{2,6},{6,2},{1... | collective-permute-start | bytes 4718600 | tf_op jit(solution)/shard_map/out_projection/ppermute | solution.py:111
  158.4 23.4 %copy-start.10 = (bf16[128,1536]{1,0:T(8,128)(2,1)S(1)}, bf16[128,1536]{1,0:T(8,128)(2,1)}, u32[]{:S(2)}) copy-start(bf16[128,1536]{1,0:T(8,128)(2,1)} %copy-done.9) | copy-start | bytes 1179652
  159.6 18.1 %collective-permute-start.17 = (bf16[128,256]{1,0:T(8,128)(2,1)S(1)}, bf16[128,256]{1,0:T(8,128)(2,1)S(1)}, u32[]{:S(2)}, u32[]{:S(2)}) collective-permute-start(bf16[128,256]{1,0:T(8,128)(2,1)S(1)} %get-tuple-element.35), channel_id=1, source_target_pairs={{0,1},{1,2},{2,3},{3,0},{4,5},{5,6},{6,7},{7,4},{8,9},{9,10},{10,1... | collective-permute-start | bytes 196616 | tf_op jit(solution)/shard_map/out_projection/ppermute | solution.py:98
  175.2 6.3 %collective-permute-start.18 = (bf16[128,256]{1,0:T(8,128)(2,1)S(1)}, bf16[128,256]{1,0:T(8,128)(2,1)S(1)}, u32[]{:S(2)}, u32[]{:S(2)}) collective-permute-start(bf16[128,256]{1,0:T(8,128)(2,1)S(1)} %get-tuple-element.34), channel_id=1, source_target_pairs={{0,2},{1,3},{2,0},{3,1},{4,6},{5,7},{6,4},{7,5},{8,10},{9,11},{10,... | collective-permute-start | bytes 196616 | tf_op jit(solution)/shard_map/out_projection/ppermute | solution.py:98
  175.2 6.4 %collective-permute-start.19 = (bf16[128,256]{1,0:T(8,128)(2,1)S(1)}, bf16[128,256]{1,0:T(8,128)(2,1)S(1)}, u32[]{:S(2)}, u32[]{:S(2)}) collective-permute-start(bf16[128,256]{1,0:T(8,128)(2,1)S(1)} %get-tuple-element.33), channel_id=1, source_target_pairs={{0,3},{1,0},{2,1},{3,2},{4,7},{5,4},{6,5},{7,6},{8,11},{9,8},{10,9... | collective-permute-start | bytes 196616 | tf_op jit(solution)/shard_map/out_projection/ppermute | solution.py:98
  187.2 5.4 %collective-permute-start.21 = (bf16[8,256]{1,0:T(8,128)(2,1)S(1)}, bf16[8,256]{1,0:T(8,128)(2,1)S(1)}, u32[]{:S(2)}, u32[]{:S(2)}) collective-permute-start(bf16[8,256]{1,0:T(8,128)(2,1)S(1)} %get-tuple-element.61), channel_id=1, source_target_pairs={{0,1},{1,2},{2,3},{3,0},{4,5},{5,6},{6,7},{7,4},{8,9},{9,10},{10,1... | collective-permute-start | bytes 12296 | tf_op jit(solution)/shard_map/sides_gather/ppermute | solution.py:127
  188.9 4.5 %collective-permute-start.22 = (bf16[8,256]{1,0:T(8,128)(2,1)S(1)}, bf16[8,256]{1,0:T(8,128)(2,1)S(1)}, u32[]{:S(2)}, u32[]{:S(2)}) collective-permute-start(bf16[8,256]{1,0:T(8,128)(2,1)S(1)} %get-tuple-element.61), channel_id=1, source_target_pairs={{0,2},{1,3},{2,0},{3,1},{4,6},{5,7},{6,4},{7,5},{8,10},{9,11},{10,... | collective-permute-start | bytes 12296 | tf_op jit(solution)/shard_map/sides_gather/ppermute | solution.py:127
  190.7 3.6 %collective-permute-start.23 = (bf16[8,256]{1,0:T(8,128)(2,1)S(1)}, bf16[8,256]{1,0:T(8,128)(2,1)S(1)}, u32[]{:S(2)}, u32[]{:S(2)}) collective-permute-start(bf16[8,256]{1,0:T(8,128)(2,1)S(1)} %get-tuple-element.61), channel_id=1, source_target_pairs={{0,3},{1,0},{2,1},{3,2},{4,7},{5,4},{6,5},{7,6},{8,11},{9,8},{10,9... | collective-permute-start | bytes 12296 | tf_op jit(solution)/shard_map/sides_gather/ppermute | solution.py:127
  194.3 3.2 %collective-permute-start.24 = (bf16[32,256]{1,0:T(8,128)(2,1)S(1)}, bf16[32,256]{1,0:T(8,128)(2,1)S(1)}, u32[]{:S(2)}, u32[]{:S(2)}) collective-permute-start(bf16[32,256]{1,0:T(8,128)(2,1)S(1)} %bitcast.304), channel_id=1, source_target_pairs={{0,4},{4,8},{8,12},{12,0},{1,5},{5,9},{9,13},{13,1},{2,6},{6,10},{... | collective-permute-start | bytes 49160 | tf_op jit(solution)/shard_map/sides_gather/ppermute | solution.py:127
  194.3 3.8 %collective-permute-start.25 = (bf16[32,256]{1,0:T(8,128)(2,1)S(1)}, bf16[32,256]{1,0:T(8,128)(2,1)S(1)}, u32[]{:S(2)}, u32[]{:S(2)}) collective-permute-start(bf16[32,256]{1,0:T(8,128)(2,1)S(1)} %bitcast.305), channel_id=1, source_target_pairs={{0,8},{4,12},{8,0},{12,4},{1,9},{5,13},{9,1},{13,5},{2,10},{6,14},... | collective-permute-start | bytes 49160 | tf_op jit(solution)/shard_map/sides_gather/ppermute | solution.py:127
  194.5 3.6 %collective-permute-start.26 = (bf16[32,256]{1,0:T(8,128)(2,1)S(1)}, bf16[32,256]{1,0:T(8,128)(2,1)S(1)}, u32[]{:S(2)}, u32[]{:S(2)}) collective-permute-start(bf16[32,256]{1,0:T(8,128)(2,1)S(1)} %bitcast.306), channel_id=1, source_target_pairs={{0,12},{4,0},{8,4},{12,8},{1,13},{5,1},{9,5},{13,9},{2,14},{6,2},{... | collective-permute-start | bytes 49160 | tf_op jit(solution)/shard_map/sides_gather/ppermute | solution.py:127
  (18 other events, 104.8 us)
Sparse Core Ops, SparseCore 0:
  78.1 51.1 all-gather.1

commit v11 on v6

--- a/solution.py
+++ b/solution.py
@@ -114,6 +114,14 @@
         jnp.concatenate([gathered, other], 1),
         jnp.concatenate([other, gathered], 1),
     )
+
+
+def rotated_all_gather(value, axis):
+    n = lax.axis_size(axis)
+    pieces = [value]
+    for shift in range(1, n):
+        pieces.append(lax.ppermute(value, axis, [(i, (i + shift) % n) for i in range(n)]))
+    return jnp.concatenate(pieces, 0)
 
 
 def direct_all_gather(value, axis):
@@ -160,7 +168,11 @@
     first_out = (inputs + summed).astype(jnp.bfloat16)
     attn_in = norm_rows(first_out.astype(jnp.float32), gain_attn).astype(jnp.bfloat16)
     with jax.named_scope("attn_in_gather"):
-        block_in = direct_all_gather(attn_in, "pair")
+        rotated = pair_count <= 4
+        if rotated:
+            block_in = rotated_all_gather(attn_in, "pair")
+        else:
+            block_in = direct_all_gather(attn_in, "pair")
     projected = jnp.dot(block_in, w_qkv, preferred_element_type=jnp.float32).astype(jnp.bfloat16)
     head_count = projected.shape[1] // (2 * KEY_SIZE + VALUE_SIZE)
     grouped = projected.reshape(local_rows, head_count, 2 * KEY_SIZE + VALUE_SIZE).transpose(1, 0, 2)
@@ -214,8 +226,30 @@
     with jax.named_scope("out_projection"):
         late_w_out, unused = lax.optimization_barrier((w_out, kv))
         full_w_out = gather_weight_rows(late_w_out, "pair", "seq")
-        own_heads = rows_to_heads(attended, "pair")
-        mixed = jnp.dot(own_heads, full_w_out, preferred_element_type=jnp.float32)
+        if rotated:
+            me = lax.axis_index("pair")
+            pieces = attended.reshape(pair_count, row_count, attended.shape[1])
+            head_rows = attended.shape[1]
+            mixed = jnp.dot(
+                pieces[0],
+                lax.dynamic_slice_in_dim(full_w_out, me * head_rows, head_rows, 0),
+                preferred_element_type=jnp.float32,
+            )
+            for shift in range(1, pair_count):
+                incoming = lax.ppermute(
+                    pieces[pair_count - shift],
+                    "pair",
+                    [(i, (i + shift) % pair_count) for i in range(pair_count)],
+                )
+                source = (me + pair_count - shift) % pair_count
+                mixed = mixed + jnp.dot(
+                    incoming,
+                    lax.dynamic_slice_in_dim(full_w_out, source * head_rows, head_rows, 0),
+                    preferred_element_type=jnp.float32,
+                )
+        else:
+            own_heads = rows_to_heads(attended, "pair")
+            mixed = jnp.dot(own_heads, full_w_out, preferred_element_type=jnp.float32)
     seq_out = (first_out.astype(jnp.float32) + mixed).astype(jnp.bfloat16)
     bin_count = row_count // POOL
     pooled = jnp.mean(seq_out.astype(jnp.float32).reshape(bin_count, POOL, channels), axis=1)

time: 181 us -> 176 us (0.972)
  starting transfers between devices: 56.8 us -> 64.4 us
  waiting for transfers between devices: 82.4 us -> 75.3 us
  matrix products: 21 us -> 16.5 us
    ppermute x9 -> x6, waiting for transfers between devices: 26.7 us -> 3.75 us  [direct_all_gather(): lax.ppermute(value, axis, [(i, (i + shift) % n) for i in range(n)])]
    ppermute x3, starting transfers between devices: 12.9 us -> 31.1 us  [line_all_gather(): flow_r = lax.ppermute(flow_r, axis, right)]
    ppermute x3 -> x6, waiting for transfers between devices: 3.71 us -> 18.6 us  [the longest x3 13.4 us: rotated_all_gather(): lax.ppermute(value, axis, [(i, (i + shift) % n) for i in range(n)])]
    ppermute x3 -> x6, starting transfers between devices: 11.4 us -> 4.72 us  [the longest x3 2.65 us: rotated_all_gather(): lax.ppermute(value, axis, [(i, (i + shift) % n) for i in range(n)])]
    ppermute x9 -> x6, starting transfers between devices: 9.85 us -> 5.98 us  [direct_all_gather(): lax.ppermute(value, axis, [(i, (i + shift) % n) for i in range(n)])]
    dot_general x1 -> x4, matrix products: 5.01 us -> 2.07 us  [the longest x1 1.22 us: shards(): jnp.dot(pieces[0], lax.dynamic_slice_in_dim(full_w_out, me * head_rows, h...]
    ppermute x3, waiting for transfers between devices: 9.47 us -> 11.6 us  [shards(): next_going = lax.ppermute(going, 'seq', forward)]
  transfers between devices with their start and end apart: 33 -> 33, of which waited for: 18 -> 16; matrix products, arithmetic and copies ran while one was open for 17% -> 16% of each run, Pallas kernels for 0% -> 0%
where the time goes in v11:
time: 176 us; the launch traced here: 175 us
  waiting for transfers between devices  75.3 us (43%)
  starting transfers between devices  64.4 us (37%)
  matrix products  16.5 us (9%)
  local copies, waits for them, and re-layouts  14.4 us (8%)
  other arithmetic  3.17 us (2%)
    ppermute x3, starting transfers between devices, line_all_gather(): flow_r = lax.ppermute(flow_r, axis, right)  31.1 us
    ppermute x3, waiting for transfers between devices, direct_reduce_scatter(): lax.ppermute(outgoing, axis, [(i, (i + shift) % n) for i in range(n)])  27.4 us
    ppermute x3, waiting for transfers between devices, rotated_all_gather(): lax.ppermute(value, axis, [(i, (i + shift) % n) for i in range(n)])  13.4 us
    ppermute x3, waiting for transfers between devices, shards(): next_going = lax.ppermute(going, 'seq', forward)  11.6 us
    ppermute x3, waiting for transfers between devices, permute_all_to_all(): lax.ppermute(outgoing, axis, [(i, (i + shift) % n) for i in range(n)])  10.3 us
    dot_general x5, matrix products, conv_rows(): jnp.dot(shifted, conv_weight[offset], preferred_element_type=jnp.float32)  6.46 us
    ppermute x6, starting transfers between devices, direct_all_gather(): lax.ppermute(value, axis, [(i, (i + shift) % n) for i in range(n)])  5.98 us
    ppermute x3, starting transfers between devices, permute_all_to_all(): lax.ppermute(outgoing, axis, [(i, (i + shift) % n) for i in range(n)])  5.89 us
  transfers between devices with their start and end apart: 33, of which 16 were waited for; matrix products, arithmetic and copies ran while one was open for 16% of the time, Pallas kernels for 0%

profile of v11, /device:TPU:0, one launch (start us, length us, event | category | flops | bytes accessed | tf_op | source)
XLA Modules:
  0.0 175.2 jit_solution(16974063950366334031)
XLA Ops:
  0.7 1.4 broadcast_in_dim.115
  2.1 2.0 %bitcast_dynamic-update-slice_fusion.6 = (bf16[5,256,768]{2,1,0:T(8,128)(2,1)}, bf16[256,768]{1,0:T(8,128)(2,1)}) fusion(bf16[5,256,768]{2,1,0:T(8,128)(2,1)} %broadcast_in_dim.115, s32[]{:T(128)S(6)} %select_n.174, bf16[256,1536]{1,0:T(8,128)(2,1)} %param.15, s32[]{:T(128)S(6)} %select_n.173), kind=kLoop, calls=%fused_computation.152 | loop fusion | bytes 1179656 | tf_op jit(solution)/shard_map/out_projection/jit(dynamic_update_index_in_dim)/dynamic_update_slice | solution.py:77
  4.1 5.7 %collective-permute-start.17 = (bf16[256,768]{1,0:T(8,128)(2,1)}, bf16[256,768]{1,0:T(8,128)(2,1)}, u32[]{:S(2)}, u32[]{:S(2)}) collective-permute-start(bf16[256,768]{1,0:T(8,128)(2,1)} %get-tuple-element.3), channel_id=1, source_target_pairs={{0,1},{1,2},{2,3},{4,5},{5,6},{6,7},{8,9},{9,10},{10,11},{12,13},{... | collective-permute-start | bytes 1179656 | tf_op jit(solution)/shard_map/out_projection/ppermute | solution.py:80
  13.1 2.6 %collective-permute-start = (bf16[128,384]{1,0:T(8,128)(2,1)}, bf16[128,384]{1,0:T(8,128)(2,1)S(1)}, u32[]{:S(2)}, u32[]{:S(2)}) collective-permute-start(bf16[128,384]{1,0:T(8,128)(2,1)} %bitcast.274), channel_id=1, source_target_pairs={{0,1},{1,2},{2,3},{3,0},{4,5},{5,6},{6,7},{7,4},{8,9},{9,10},{10,1... | collective-permute-start | bytes 294920 | tf_op jit(solution)/shard_map/ppermute | solution.py:65
  16.4 2.5 %collective-permute-start.1 = (bf16[128,384]{1,0:T(8,128)(2,1)}, bf16[128,384]{1,0:T(8,128)(2,1)S(1)}, u32[]{:S(2)}, u32[]{:S(2)}) collective-permute-start(bf16[128,384]{1,0:T(8,128)(2,1)} %bitcast.273), channel_id=1, source_target_pairs={{0,2},{1,3},{2,0},{3,1},{4,6},{5,7},{6,4},{7,5},{8,10},{9,11},{10,... | collective-permute-start | bytes 294920 | tf_op jit(solution)/shard_map/ppermute | solution.py:65
  19.8 7.6 %collective-permute-done = bf16[128,384]{1,0:T(8,128)(2,1)S(1)} collective-permute-done((bf16[128,384]{1,0:T(8,128)(2,1)}, bf16[128,384]{1,0:T(8,128)(2,1)S(1)}, u32[]{:S(2)}, u32[]{:S(2)}) %collective-permute-start) | collective-permute-done | bytes 98336 | tf_op jit(solution)/shard_map/ppermute | solution.py:65
  27.4 2.7 %collective-permute-done.1 = bf16[128,384]{1,0:T(8,128)(2,1)S(1)} collective-permute-done((bf16[128,384]{1,0:T(8,128)(2,1)}, bf16[128,384]{1,0:T(8,128)(2,1)S(1)}, u32[]{:S(2)}, u32[]{:S(2)}) %collective-permute-start.1) | collective-permute-done | bytes 98336 | tf_op jit(solution)/shard_map/ppermute | solution.py:65
  30.2 1.6 collective-permute-start.4
  31.8 2.4 %fusion.43 = f32[512,1536]{1,0:T(8,128)S(1)} fusion(bf16[512,384]{1,0:T(8,128)(2,1)S(1)} %bitcast.287, bf16[5,384,1536]{2,1,0:T(8,128)(2,1)} %param.12), kind=kOutput, calls=%fused_computation.66 | convolution fusion | flops 603979776 | bytes 4718592 | tf_op jit(solution)/shard_map/conv_reduce/dot_general | solution.py:39
  34.2 2.9 %collective-permute-start.3 = (bf16[8,384]{1,0:T(8,128)(2,1)S(1)}, bf16[8,384]{1,0:T(8,128)(2,1)S(1)}, u32[]{:S(2)}, u32[]{:S(2)}) collective-permute-start(bf16[8,384]{1,0:T(8,128)(2,1)S(1)} %get-tuple-element.27), channel_id=1, source_target_pairs={{0,4},{4,8},{8,12},{1,5},{5,9},{9,13},{2,6},{6,10},{10,14},{3,7},{... | collective-permute-start | bytes 18440 | tf_op jit(solution)/shard_map/ppermute | solution.py:25
  41.7 2.7 %collective-permute-start.6 = (bf16[128,1536]{1,0:T(8,128)(2,1)S(1)}, bf16[128,1536]{1,0:T(8,128)(2,1)S(1)}, u32[]{:S(2)}, u32[]{:S(2)}) collective-permute-start(bf16[128,1536]{1,0:T(8,128)(2,1)S(1)} %get-tuple-element.24), channel_id=1, source_target_pairs={{0,2},{1,3},{2,0},{3,1},{4,6},{5,7},{6,4},{7,5},{8,10},{9,11},{10,... | collective-permute-start | bytes 1179656 | tf_op jit(solution)/shard_map/conv_reduce/ppermute | solution.py:51
  44.4 2.7 %collective-permute-start.19 = (bf16[256,768]{1,0:T(8,128)(2,1)}, bf16[256,768]{1,0:T(8,128)(2,1)S(1)}, u32[]{:S(2)}, u32[]{:S(2)}) collective-permute-start(bf16[256,768]{1,0:T(8,128)(2,1)} %collective-permute-done.17), channel_id=1, source_target_pairs={{0,1},{1,2},{2,3},{4,5},{5,6},{6,7},{8,9},{9,10},{10,11},{12,13},{... | collective-permute-start | bytes 1179656 | tf_op jit(solution)/shard_map/out_projection/ppermute | solution.py:80
  48.4 1.8 %bitcast_dynamic-update-slice_fusion.5 = bf16[5,256,768]{2,1,0:T(8,128)(2,1)} fusion(bf16[5,256,768]{2,1,0:T(8,128)(2,1)} %get-tuple-element.2, s32[]{:T(128)S(6)} %select_n.176, bf16[256,768]{1,0:T(8,128)(2,1)} %collective-permute-done.17), kind=kLoop, calls=%fused_computation.151 | loop fusion | bytes 786436 | tf_op jit(solution)/shard_map/out_projection/jit(dynamic_update_index_in_dim)/dynamic_update_slice | solution.py:84
  50.2 1.8 %bitcast_dynamic-update-slice_fusion.4 = bf16[5,256,768]{2,1,0:T(8,128)(2,1)} fusion(bf16[5,256,768]{2,1,0:T(8,128)(2,1)} %bitcast_dynamic-update-slice_fusion.5, s32[]{:T(128)S(6)} %select_n.178, bf16[256,768]{1,0:T(8,128)(2,1)} %collective-permute-done.18), kind=kLoop, calls=%fused_computation.150 | loop fusion | bytes 786436 | tf_op jit(solution)/shard_map/out_projection/jit(dynamic_update_index_in_dim)/dynamic_update_slice | solution.py:85
  53.1 26.3 %collective-permute-done.6 = bf16[128,1536]{1,0:T(8,128)(2,1)S(1)} collective-permute-done((bf16[128,1536]{1,0:T(8,128)(2,1)S(1)}, bf16[128,1536]{1,0:T(8,128)(2,1)S(1)}, u32[]{:S(2)}, u32[]{:S(2)}) %collective-permute-start.6) | collective-permute-done | bytes 393248 | tf_op jit(solution)/shard_map/conv_reduce/ppermute | solution.py:51
  80.7 1.9 %collective-permute-start.8 = (bf16[128,1536]{1,0:T(8,128)(2,1)S(1)}, bf16[128,1536]{1,0:T(8,128)(2,1)S(1)}, u32[]{:S(2)}, u32[]{:S(2)}) collective-permute-start(bf16[128,1536]{1,0:T(8,128)(2,1)S(1)} %fusion.75), channel_id=1, source_target_pairs={{0,1},{1,2},{2,3},{3,0},{4,5},{5,6},{6,7},{7,4},{8,9},{9,10},{10,1... | collective-permute-start | bytes 1179656 | tf_op jit(solution)/shard_map/attn_in_gather/ppermute | solution.py:123
  82.6 22.7 %collective-permute-start.21 = (bf16[256,768]{1,0:T(8,128)(2,1)S(1)}, bf16[256,768]{1,0:T(8,128)(2,1)S(1)}, u32[]{:S(2)}, u32[]{:S(2)}) collective-permute-start(bf16[256,768]{1,0:T(8,128)(2,1)S(1)} %collective-permute-done.19), channel_id=1, source_target_pairs={{0,1},{1,2},{2,3},{4,5},{5,6},{6,7},{8,9},{9,10},{10,11},{12,13},{... | collective-permute-start | bytes 1179656 | tf_op jit(solution)/shard_map/out_projection/ppermute | solution.py:80
  108.2 13.4 %collective-permute-done.9 = bf16[128,1536]{1,0:T(8,128)(2,1)S(1)} collective-permute-done((bf16[128,1536]{1,0:T(8,128)(2,1)S(1)}, bf16[128,1536]{1,0:T(8,128)(2,1)S(1)}, u32[]{:S(2)}, u32[]{:S(2)}) %collective-permute-start.9) | collective-permute-done | bytes 393248 | tf_op jit(solution)/shard_map/attn_in_gather/ppermute | solution.py:123
  121.6 1.4 fusion.15
  124.3 3.5 %collective-permute-done.12 = bf16[2,256,256]{2,1,0:T(8,128)(2,1)S(1)} collective-permute-done((bf16[2,256,256]{2,1,0:T(8,128)(2,1)S(1)}, bf16[2,256,256]{2,1,0:T(8,128)(2,1)S(1)}, u32[]{:S(2)}, u32[]{:S(2)}) %collective-permute-start.12) | collective-permute-done | bytes 262176 | tf_op jit(solution)/shard_map/kv_ring/ppermute | solution.py:218
  127.8 2.2 %collective-permute-start.14 = (bf16[2,256,256]{2,1,0:T(8,128)(2,1)S(1)}, bf16[2,256,256]{2,1,0:T(8,128)(2,1)S(1)}, u32[]{:S(2)}, u32[]{:S(2)}) collective-permute-start(bf16[2,256,256]{2,1,0:T(8,128)(2,1)S(1)} %collective-permute-done.12), channel_id=1, source_target_pairs={{4,0},{8,4},{12,8},{0,12},{5,1},{9,5},{13,9},{1,13},{6,2},{10,6},{... | collective-permute-start | bytes 786440 | tf_op jit(solution)/shard_map/kv_ring/ppermute | solution.py:218
  130.0 2.5 %collective-permute-done.11 = bf16[2,256,256]{2,1,0:T(8,128)(2,1)S(1)} collective-permute-done((bf16[2,256,256]{2,1,0:T(8,128)(2,1)S(1)}, bf16[2,256,256]{2,1,0:T(8,128)(2,1)S(1)}, u32[]{:S(2)}, u32[]{:S(2)}) %collective-permute-start.11) | collective-permute-done | bytes 262176 | tf_op jit(solution)/shard_map/kv_ring/ppermute | solution.py:217
  134.9 1.5 slice.169
  136.4 1.8 %collective-permute-start.23 = (bf16[1024,768]{1,0:T(8,128)(2,1)S(1)}, bf16[1024,768]{1,0:T(8,128)(2,1)S(1)}, u32[]{:S(2)}, u32[]{:S(2)}) collective-permute-start(bf16[1024,768]{1,0:T(8,128)(2,1)S(1)} %bitcast.294), channel_id=1, source_target_pairs={{0,4},{4,0},{8,12},{12,8},{1,5},{5,1},{9,13},{13,9},{2,6},{6,2},{1... | collective-permute-start | bytes 4718600 | tf_op jit(solution)/shard_map/out_projection/ppermute | solution.py:111
  138.5 2.3 %collective-permute-done.13 = bf16[2,256,256]{2,1,0:T(8,128)(2,1)S(1)} collective-permute-done((bf16[2,256,256]{2,1,0:T(8,128)(2,1)S(1)}, bf16[2,256,256]{2,1,0:T(8,128)(2,1)S(1)}, u32[]{:S(2)}, u32[]{:S(2)}) %collective-permute-start.13) | collective-permute-done | bytes 262176 | tf_op jit(solution)/shard_map/kv_ring/ppermute | solution.py:217
  142.4 6.8 %collective-permute-done.15 = bf16[2,256,256]{2,1,0:T(8,128)(2,1)S(1)} collective-permute-done((bf16[2,256,256]{2,1,0:T(8,128)(2,1)S(1)}, bf16[2,256,256]{2,1,0:T(8,128)(2,1)S(1)}, u32[]{:S(2)}, u32[]{:S(2)}) %collective-permute-start.15) | collective-permute-done | bytes 262176 | tf_op jit(solution)/shard_map/kv_ring/ppermute | solution.py:217
  153.6 1.9 %collective-permute-start.24 = (bf16[128,256]{0,1:T(8,128)(2,1)S(1)}, bf16[128,256]{0,1:T(8,128)(2,1)S(1)}, u32[]{:S(2)}, u32[]{:S(2)}) collective-permute-start(bf16[128,256]{0,1:T(8,128)(2,1)S(1)} %bitcast.304), channel_id=1, source_target_pairs={{0,1},{1,2},{2,3},{3,0},{4,5},{5,6},{6,7},{7,4},{8,9},{9,10},{10,1... | collective-permute-start | bytes 196616 | tf_op jit(solution)/shard_map/out_projection/ppermute | solution.py:239
  156.3 2.8 %collective-permute-done.26 = bf16[128,256]{0,1:T(8,128)(2,1)S(1)} collective-permute-done((bf16[128,256]{0,1:T(8,128)(2,1)S(1)}, bf16[128,256]{0,1:T(8,128)(2,1)S(1)}, u32[]{:S(2)}, u32[]{:S(2)}) %collective-permute-start.26) | collective-permute-done | bytes 65568 | tf_op jit(solution)/shard_map/out_projection/ppermute | solution.py:239
  159.4 2.4 %collective-permute-done.25 = bf16[128,256]{0,1:T(8,128)(2,1)S(1)} collective-permute-done((bf16[128,256]{0,1:T(8,128)(2,1)S(1)}, bf16[128,256]{0,1:T(8,128)(2,1)S(1)}, u32[]{:S(2)}, u32[]{:S(2)}) %collective-permute-start.25) | collective-permute-done | bytes 65568 | tf_op jit(solution)/shard_map/out_projection/ppermute | solution.py:239
  164.1 1.9 %collective-permute-start.28 = (bf16[8,256]{1,0:T(8,128)(2,1)S(1)}, bf16[8,256]{1,0:T(8,128)(2,1)S(1)}, u32[]{:S(2)}, u32[]{:S(2)}) collective-permute-start(bf16[8,256]{1,0:T(8,128)(2,1)S(1)} %get-tuple-element.61), channel_id=1, source_target_pairs={{0,2},{1,3},{2,0},{3,1},{4,6},{5,7},{6,4},{7,5},{8,10},{9,11},{10,... | collective-permute-start | bytes 12296 | tf_op jit(solution)/shard_map/sides_gather/ppermute | solution.py:135
  166.0 2.3 %collective-permute-start.29 = (bf16[8,256]{1,0:T(8,128)(2,1)S(1)}, bf16[8,256]{1,0:T(8,128)(2,1)S(1)}, u32[]{:S(2)}, u32[]{:S(2)}) collective-permute-start(bf16[8,256]{1,0:T(8,128)(2,1)S(1)} %get-tuple-element.61), channel_id=1, source_target_pairs={{0,3},{1,0},{2,1},{3,2},{4,7},{5,4},{6,5},{7,6},{8,11},{9,8},{10,9... | collective-permute-start | bytes 12296 | tf_op jit(solution)/shard_map/sides_gather/ppermute | solution.py:135
  170.1 1.8 %collective-permute-start.32 = (bf16[32,256]{1,0:T(8,128)(2,1)S(1)}, bf16[32,256]{1,0:T(8,128)(2,1)S(1)}, u32[]{:S(2)}, u32[]{:S(2)}) collective-permute-start(bf16[32,256]{1,0:T(8,128)(2,1)S(1)} %bitcast.303), channel_id=1, source_target_pairs={{0,12},{4,0},{8,4},{12,8},{1,13},{5,1},{9,5},{13,9},{2,14},{6,2},{... | collective-permute-start | bytes 49160 | tf_op jit(solution)/shard_map/sides_gather/ppermute | solution.py:135
  (131 shorter events, 34.0 us)
Async XLA Ops:
  4.1 40.3 %collective-permute-start.17 = (bf16[256,768]{1,0:T(8,128)(2,1)}, bf16[256,768]{1,0:T(8,128)(2,1)}, u32[]{:S(2)}, u32[]{:S(2)}) collective-permute-start(bf16[256,768]{1,0:T(8,128)(2,1)} %get-tuple-element.3), channel_id=1, source_target_pairs={{0,1},{1,2},{2,3},{4,5},{5,6},{6,7},{8,9},{9,10},{10,11},{12,13},{... | collective-permute-start | bytes 1179656 | tf_op jit(solution)/shard_map/out_projection/ppermute | solution.py:80
  9.8 37.3 %collective-permute-start.18 = (bf16[256,768]{1,0:T(8,128)(2,1)}, bf16[256,768]{1,0:T(8,128)(2,1)}, u32[]{:S(2)}, u32[]{:S(2)}) collective-permute-start(bf16[256,768]{1,0:T(8,128)(2,1)} %get-tuple-element.3), channel_id=1, source_target_pairs={{1,0},{2,1},{3,2},{5,4},{6,5},{7,6},{9,8},{10,9},{11,10},{13,12},{... | collective-permute-start | bytes 1179656 | tf_op jit(solution)/shard_map/out_projection/ppermute | solution.py:81
  13.1 14.3 %collective-permute-start = (bf16[128,384]{1,0:T(8,128)(2,1)}, bf16[128,384]{1,0:T(8,128)(2,1)S(1)}, u32[]{:S(2)}, u32[]{:S(2)}) collective-permute-start(bf16[128,384]{1,0:T(8,128)(2,1)} %bitcast.274), channel_id=1, source_target_pairs={{0,1},{1,2},{2,3},{3,0},{4,5},{5,6},{6,7},{7,4},{8,9},{9,10},{10,1... | collective-permute-start | bytes 294920 | tf_op jit(solution)/shard_map/ppermute | solution.py:65
  16.4 13.7 %collective-permute-start.1 = (bf16[128,384]{1,0:T(8,128)(2,1)}, bf16[128,384]{1,0:T(8,128)(2,1)S(1)}, u32[]{:S(2)}, u32[]{:S(2)}) collective-permute-start(bf16[128,384]{1,0:T(8,128)(2,1)} %bitcast.273), channel_id=1, source_target_pairs={{0,2},{1,3},{2,0},{3,1},{4,6},{5,7},{6,4},{7,5},{8,10},{9,11},{10,... | collective-permute-start | bytes 294920 | tf_op jit(solution)/shard_map/ppermute | solution.py:65
  18.9 11.2 %collective-permute-start.2 = (bf16[128,384]{1,0:T(8,128)(2,1)S(1)}, bf16[128,384]{1,0:T(8,128)(2,1)S(1)}, u32[]{:S(2)}, u32[]{:S(2)}) collective-permute-start(bf16[128,384]{1,0:T(8,128)(2,1)S(1)} %bitcast.300), channel_id=1, source_target_pairs={{0,3},{1,0},{2,1},{3,2},{4,7},{5,4},{6,5},{7,6},{8,11},{9,8},{10,9... | collective-permute-start | bytes 294920 | tf_op jit(solution)/shard_map/ppermute | solution.py:65
  30.2 6.9 %collective-permute-start.4 = (bf16[8,384]{1,0:T(8,128)(2,1)S(1)}, bf16[8,384]{1,0:T(8,128)(2,1)S(1)}, u32[]{:S(2)}, u32[]{:S(2)}) collective-permute-start(bf16[8,384]{1,0:T(8,128)(2,1)S(1)} %get-tuple-element.28), channel_id=1, source_target_pairs={{4,0},{8,4},{12,8},{5,1},{9,5},{13,9},{6,2},{10,6},{14,10},{7,3},{... | collective-permute-start | bytes 18440 | tf_op jit(solution)/shard_map/ppermute | solution.py:26
  34.2 4.9 %collective-permute-start.3 = (bf16[8,384]{1,0:T(8,128)(2,1)S(1)}, bf16[8,384]{1,0:T(8,128)(2,1)S(1)}, u32[]{:S(2)}, u32[]{:S(2)}) collective-permute-start(bf16[8,384]{1,0:T(8,128)(2,1)S(1)} %get-tuple-element.27), channel_id=1, source_target_pairs={{0,4},{4,8},{8,12},{1,5},{5,9},{9,13},{2,6},{6,10},{10,14},{3,7},{... | collective-permute-start | bytes 18440 | tf_op jit(solution)/shard_map/ppermute | solution.py:25
  41.3 11.7 %collective-permute-start.7 = (bf16[128,1536]{1,0:T(8,128)(2,1)S(1)}, bf16[128,1536]{1,0:T(8,128)(2,1)S(1)}, u32[]{:S(2)}, u32[]{:S(2)}) collective-permute-start(bf16[128,1536]{1,0:T(8,128)(2,1)S(1)} %get-tuple-element.23), channel_id=1, source_target_pairs={{0,3},{1,0},{2,1},{3,2},{4,7},{5,4},{6,5},{7,6},{8,11},{9,8},{10,9... | collective-permute-start | bytes 1179656 | tf_op jit(solution)/shard_map/conv_reduce/ppermute | solution.py:51
  41.7 37.7 %collective-permute-start.6 = (bf16[128,1536]{1,0:T(8,128)(2,1)S(1)}, bf16[128,1536]{1,0:T(8,128)(2,1)S(1)}, u32[]{:S(2)}, u32[]{:S(2)}) collective-permute-start(bf16[128,1536]{1,0:T(8,128)(2,1)S(1)} %get-tuple-element.24), channel_id=1, source_target_pairs={{0,2},{1,3},{2,0},{3,1},{4,6},{5,7},{6,4},{7,5},{8,10},{9,11},{10,... | collective-permute-start | bytes 1179656 | tf_op jit(solution)/shard_map/conv_reduce/ppermute | solution.py:51
  44.4 34.9 %collective-permute-start.5 = (bf16[128,1536]{1,0:T(8,128)(2,1)S(1)}, bf16[128,1536]{1,0:T(8,128)(2,1)S(1)}, u32[]{:S(2)}, u32[]{:S(2)}) collective-permute-start(bf16[128,1536]{1,0:T(8,128)(2,1)S(1)} %get-tuple-element.22), channel_id=1, source_target_pairs={{0,1},{1,2},{2,3},{3,0},{4,5},{5,6},{6,7},{7,4},{8,9},{9,10},{10,1... | collective-permute-start | bytes 1179656 | tf_op jit(solution)/shard_map/conv_reduce/ppermute | solution.py:51
  44.4 38.2 %collective-permute-start.19 = (bf16[256,768]{1,0:T(8,128)(2,1)}, bf16[256,768]{1,0:T(8,128)(2,1)S(1)}, u32[]{:S(2)}, u32[]{:S(2)}) collective-permute-start(bf16[256,768]{1,0:T(8,128)(2,1)} %collective-permute-done.17), channel_id=1, source_target_pairs={{0,1},{1,2},{2,3},{4,5},{5,6},{6,7},{8,9},{9,10},{10,11},{12,13},{... | collective-permute-start | bytes 1179656 | tf_op jit(solution)/shard_map/out_projection/ppermute | solution.py:80
  47.1 58.2 %collective-permute-start.20 = (bf16[256,768]{1,0:T(8,128)(2,1)}, bf16[256,768]{1,0:T(8,128)(2,1)S(1)}, u32[]{:S(2)}, u32[]{:S(2)}) collective-permute-start(bf16[256,768]{1,0:T(8,128)(2,1)} %collective-permute-done.18), channel_id=1, source_target_pairs={{1,0},{2,1},{3,2},{5,4},{6,5},{7,6},{9,8},{10,9},{11,10},{13,12},{... | collective-permute-start | bytes 1179656 | tf_op jit(solution)/shard_map/out_projection/ppermute | solution.py:81
  80.0 28.3 %collective-permute-start.10 = (bf16[128,1536]{1,0:T(8,128)(2,1)S(1)}, bf16[128,1536]{1,0:T(8,128)(2,1)S(1)}, u32[]{:S(2)}, u32[]{:S(2)}) collective-permute-start(bf16[128,1536]{1,0:T(8,128)(2,1)S(1)} %fusion.75), channel_id=1, source_target_pairs={{0,3},{1,0},{2,1},{3,2},{4,7},{5,4},{6,5},{7,6},{8,11},{9,8},{10,9... | collective-permute-start | bytes 1179656 | tf_op jit(solution)/shard_map/attn_in_gather/ppermute | solution.py:123
  80.0 41.6 %collective-permute-start.9 = (bf16[128,1536]{1,0:T(8,128)(2,1)S(1)}, bf16[128,1536]{1,0:T(8,128)(2,1)S(1)}, u32[]{:S(2)}, u32[]{:S(2)}) collective-permute-start(bf16[128,1536]{1,0:T(8,128)(2,1)S(1)} %fusion.75), channel_id=1, source_target_pairs={{0,2},{1,3},{2,0},{3,1},{4,6},{5,7},{6,4},{7,5},{8,10},{9,11},{10,... | collective-permute-start | bytes 1179656 | tf_op jit(solution)/shard_map/attn_in_gather/ppermute | solution.py:123
  80.7 40.9 %collective-permute-start.8 = (bf16[128,1536]{1,0:T(8,128)(2,1)S(1)}, bf16[128,1536]{1,0:T(8,128)(2,1)S(1)}, u32[]{:S(2)}, u32[]{:S(2)}) collective-permute-start(bf16[128,1536]{1,0:T(8,128)(2,1)S(1)} %fusion.75), channel_id=1, source_target_pairs={{0,1},{1,2},{2,3},{3,0},{4,5},{5,6},{6,7},{7,4},{8,9},{9,10},{10,1... | collective-permute-start | bytes 1179656 | tf_op jit(solution)/shard_map/attn_in_gather/ppermute | solution.py:123
  82.6 50.7 %collective-permute-start.21 = (bf16[256,768]{1,0:T(8,128)(2,1)S(1)}, bf16[256,768]{1,0:T(8,128)(2,1)S(1)}, u32[]{:S(2)}, u32[]{:S(2)}) collective-permute-start(bf16[256,768]{1,0:T(8,128)(2,1)S(1)} %collective-permute-done.19), channel_id=1, source_target_pairs={{0,1},{1,2},{2,3},{4,5},{5,6},{6,7},{8,9},{9,10},{10,11},{12,13},{... | collective-permute-start | bytes 1179656 | tf_op jit(solution)/shard_map/out_projection/ppermute | solution.py:80
  105.4 28.7 %collective-permute-start.22 = (bf16[256,768]{1,0:T(8,128)(2,1)S(1)}, bf16[256,768]{1,0:T(8,128)(2,1)S(1)}, u32[]{:S(2)}, u32[]{:S(2)}) collective-permute-start(bf16[256,768]{1,0:T(8,128)(2,1)S(1)} %collective-permute-done.20), channel_id=1, source_target_pairs={{1,0},{2,1},{3,2},{5,4},{6,5},{7,6},{9,8},{10,9},{11,10},{13,12},{... | collective-permute-start | bytes 1179656 | tf_op jit(solution)/shard_map/out_projection/ppermute | solution.py:81
  123.1 4.7 %collective-permute-start.12 = (bf16[2,256,256]{2,1,0:T(8,128)(2,1)S(1)}, bf16[2,256,256]{2,1,0:T(8,128)(2,1)S(1)}, u32[]{:S(2)}, u32[]{:S(2)}) collective-permute-start(bf16[2,256,256]{2,1,0:T(8,128)(2,1)S(1)} %get-tuple-element.26), channel_id=1, source_target_pairs={{4,0},{8,4},{12,8},{0,12},{5,1},{9,5},{13,9},{1,13},{6,2},{10,6},{... | collective-permute-start | bytes 786440 | tf_op jit(solution)/shard_map/kv_ring/ppermute | solution.py:218
  123.2 9.3 %collective-permute-start.11 = (bf16[2,256,256]{2,1,0:T(8,128)(2,1)S(1)}, bf16[2,256,256]{2,1,0:T(8,128)(2,1)S(1)}, u32[]{:S(2)}, u32[]{:S(2)}) collective-permute-start(bf16[2,256,256]{2,1,0:T(8,128)(2,1)S(1)} %get-tuple-element.25), channel_id=1, source_target_pairs={{0,4},{4,8},{8,12},{12,0},{1,5},{5,9},{9,13},{13,1},{2,6},{6,10},{... | collective-permute-start | bytes 786440 | tf_op jit(solution)/shard_map/kv_ring/ppermute | solution.py:217
  127.8 10.4 %collective-permute-start.14 = (bf16[2,256,256]{2,1,0:T(8,128)(2,1)S(1)}, bf16[2,256,256]{2,1,0:T(8,128)(2,1)S(1)}, u32[]{:S(2)}, u32[]{:S(2)}) collective-permute-start(bf16[2,256,256]{2,1,0:T(8,128)(2,1)S(1)} %collective-permute-done.12), channel_id=1, source_target_pairs={{4,0},{8,4},{12,8},{0,12},{5,1},{9,5},{13,9},{1,13},{6,2},{10,6},{... | collective-permute-start | bytes 786440 | tf_op jit(solution)/shard_map/kv_ring/ppermute | solution.py:218
  132.5 8.3 %collective-permute-start.13 = (bf16[2,256,256]{2,1,0:T(8,128)(2,1)S(1)}, bf16[2,256,256]{2,1,0:T(8,128)(2,1)S(1)}, u32[]{:S(2)}, u32[]{:S(2)}) collective-permute-start(bf16[2,256,256]{2,1,0:T(8,128)(2,1)S(1)} %collective-permute-done.11), channel_id=1, source_target_pairs={{0,4},{4,8},{8,12},{12,0},{1,5},{5,9},{9,13},{13,1},{2,6},{6,10},{... | collective-permute-start | bytes 786440 | tf_op jit(solution)/shard_map/kv_ring/ppermute | solution.py:217
  136.4 19.2 %collective-permute-start.23 = (bf16[1024,768]{1,0:T(8,128)(2,1)S(1)}, bf16[1024,768]{1,0:T(8,128)(2,1)S(1)}, u32[]{:S(2)}, u32[]{:S(2)}) collective-permute-start(bf16[1024,768]{1,0:T(8,128)(2,1)S(1)} %bitcast.294), channel_id=1, source_target_pairs={{0,4},{4,0},{8,12},{12,8},{1,5},{5,1},{9,13},{13,9},{2,6},{6,2},{1... | collective-permute-start | bytes 4718600 | tf_op jit(solution)/shard_map/out_projection/ppermute | solution.py:111
  138.2 3.9 %collective-permute-start.16 = (bf16[2,256,256]{2,1,0:T(8,128)(2,1)S(1)}, bf16[2,256,256]{2,1,0:T(8,128)(2,1)S(1)}, u32[]{:S(2)}, u32[]{:S(2)}) collective-permute-start(bf16[2,256,256]{2,1,0:T(8,128)(2,1)S(1)} %collective-permute-done.14), channel_id=1, source_target_pairs={{4,0},{8,4},{12,8},{0,12},{5,1},{9,5},{13,9},{1,13},{6,2},{10,6},{... | collective-permute-start | bytes 786440 | tf_op jit(solution)/shard_map/kv_ring/ppermute | solution.py:218
  140.8 8.3 %collective-permute-start.15 = (bf16[2,256,256]{2,1,0:T(8,128)(2,1)S(1)}, bf16[2,256,256]{2,1,0:T(8,128)(2,1)S(1)}, u32[]{:S(2)}, u32[]{:S(2)}) collective-permute-start(bf16[2,256,256]{2,1,0:T(8,128)(2,1)S(1)} %collective-permute-done.13), channel_id=1, source_target_pairs={{0,4},{4,8},{8,12},{12,0},{1,5},{5,9},{9,13},{13,1},{2,6},{6,10},{... | collective-permute-start | bytes 786440 | tf_op jit(solution)/shard_map/kv_ring/ppermute | solution.py:217
  153.5 5.7 %collective-permute-start.26 = (bf16[128,256]{0,1:T(8,128)(2,1)S(1)}, bf16[128,256]{0,1:T(8,128)(2,1)S(1)}, u32[]{:S(2)}, u32[]{:S(2)}) collective-permute-start(bf16[128,256]{0,1:T(8,128)(2,1)S(1)} %bitcast.306), channel_id=1, source_target_pairs={{0,3},{1,0},{2,1},{3,2},{4,7},{5,4},{6,5},{7,6},{8,11},{9,8},{10,9... | collective-permute-start | bytes 196616 | tf_op jit(solution)/shard_map/out_projection/ppermute | solution.py:239
  153.6 8.3 %collective-permute-start.25 = (bf16[128,256]{0,1:T(8,128)(2,1)S(1)}, bf16[128,256]{0,1:T(8,128)(2,1)S(1)}, u32[]{:S(2)}, u32[]{:S(2)}) collective-permute-start(bf16[128,256]{0,1:T(8,128)(2,1)S(1)} %bitcast.305), channel_id=1, source_target_pairs={{0,2},{1,3},{2,0},{3,1},{4,6},{5,7},{6,4},{7,5},{8,10},{9,11},{10,... | collective-permute-start | bytes 196616 | tf_op jit(solution)/shard_map/out_projection/ppermute | solution.py:239
  153.6 8.5 %collective-permute-start.24 = (bf16[128,256]{0,1:T(8,128)(2,1)S(1)}, bf16[128,256]{0,1:T(8,128)(2,1)S(1)}, u32[]{:S(2)}, u32[]{:S(2)}) collective-permute-start(bf16[128,256]{0,1:T(8,128)(2,1)S(1)} %bitcast.304), channel_id=1, source_target_pairs={{0,1},{1,2},{2,3},{3,0},{4,5},{5,6},{6,7},{7,4},{8,9},{9,10},{10,1... | collective-permute-start | bytes 196616 | tf_op jit(solution)/shard_map/out_projection/ppermute | solution.py:239
  164.1 5.4 %collective-permute-start.27 = (bf16[8,256]{1,0:T(8,128)(2,1)S(1)}, bf16[8,256]{1,0:T(8,128)(2,1)S(1)}, u32[]{:S(2)}, u32[]{:S(2)}) collective-permute-start(bf16[8,256]{1,0:T(8,128)(2,1)S(1)} %get-tuple-element.61), channel_id=1, source_target_pairs={{0,1},{1,2},{2,3},{3,0},{4,5},{5,6},{6,7},{7,4},{8,9},{9,10},{10,1... | collective-permute-start | bytes 12296 | tf_op jit(solution)/shard_map/sides_gather/ppermute | solution.py:135
  164.1 5.4 %collective-permute-start.28 = (bf16[8,256]{1,0:T(8,128)(2,1)S(1)}, bf16[8,256]{1,0:T(8,128)(2,1)S(1)}, u32[]{:S(2)}, u32[]{:S(2)}) collective-permute-start(bf16[8,256]{1,0:T(8,128)(2,1)S(1)} %get-tuple-element.61), channel_id=1, source_target_pairs={{0,2},{1,3},{2,0},{3,1},{4,6},{5,7},{6,4},{7,5},{8,10},{9,11},{10,... | collective-permute-start | bytes 12296 | tf_op jit(solution)/shard_map/sides_gather/ppermute | solution.py:135
  166.0 4.1 %collective-permute-start.29 = (bf16[8,256]{1,0:T(8,128)(2,1)S(1)}, bf16[8,256]{1,0:T(8,128)(2,1)S(1)}, u32[]{:S(2)}, u32[]{:S(2)}) collective-permute-start(bf16[8,256]{1,0:T(8,128)(2,1)S(1)} %get-tuple-element.61), channel_id=1, source_target_pairs={{0,3},{1,0},{2,1},{3,2},{4,7},{5,4},{6,5},{7,6},{8,11},{9,8},{10,9... | collective-permute-start | bytes 12296 | tf_op jit(solution)/shard_map/sides_gather/ppermute | solution.py:135
  170.1 3.8 %collective-permute-start.31 = (bf16[32,256]{1,0:T(8,128)(2,1)S(1)}, bf16[32,256]{1,0:T(8,128)(2,1)S(1)}, u32[]{:S(2)}, u32[]{:S(2)}) collective-permute-start(bf16[32,256]{1,0:T(8,128)(2,1)S(1)} %bitcast.302), channel_id=1, source_target_pairs={{0,8},{4,12},{8,0},{12,4},{1,9},{5,13},{9,1},{13,5},{2,10},{6,14},... | collective-permute-start | bytes 49160 | tf_op jit(solution)/shard_map/sides_gather/ppermute | solution.py:135
  170.1 3.8 %collective-permute-start.32 = (bf16[32,256]{1,0:T(8,128)(2,1)S(1)}, bf16[32,256]{1,0:T(8,128)(2,1)S(1)}, u32[]{:S(2)}, u32[]{:S(2)}) collective-permute-start(bf16[32,256]{1,0:T(8,128)(2,1)S(1)} %bitcast.303), channel_id=1, source_target_pairs={{0,12},{4,0},{8,4},{12,8},{1,13},{5,1},{9,5},{13,9},{2,14},{6,2},{... | collective-permute-start | bytes 49160 | tf_op jit(solution)/shard_map/sides_gather/ppermute | solution.py:135
  (10 other events, 217.2 us)

commit v12 on v11

--- a/solution.py
+++ b/solution.py
@@ -178,6 +178,8 @@
     grouped = projected.reshape(local_rows, head_count, 2 * KEY_SIZE + VALUE_SIZE).transpose(1, 0, 2)
     queries = grouped[:, :, :KEY_SIZE]
     kv = grouped[:, :, KEY_SIZE:]
+    if rotated and seq_count % 2 == 0:
+        late_w_out, kv = lax.optimization_barrier((w_out, kv))
     scale = 1.0 / math.sqrt(KEY_SIZE)
 
     def attend(state, kv_block):
@@ -224,30 +226,45 @@
     attended = (weighted / running_sum[:, :, None]).astype(jnp.bfloat16)
     attended = attended.transpose(1, 0, 2).reshape(local_rows, head_count * VALUE_SIZE)
     with jax.named_scope("out_projection"):
-        late_w_out, unused = lax.optimization_barrier((w_out, kv))
-        full_w_out = gather_weight_rows(late_w_out, "pair", "seq")
-        if rotated:
+        if rotated and seq_count % 2 == 0:
             me = lax.axis_index("pair")
+            core = lax.axis_index("seq") % 2
+            half = w_out.shape[1] // 2
+            mine_w = lax.dynamic_slice_in_dim(late_w_out, core * half, half, 1)
+            other_w = lax.dynamic_slice_in_dim(late_w_out, (1 - core) * half, half, 1)
             pieces = attended.reshape(pair_count, row_count, attended.shape[1])
-            head_rows = attended.shape[1]
-            mixed = jnp.dot(
-                pieces[0],
-                lax.dynamic_slice_in_dim(full_w_out, me * head_rows, head_rows, 0),
-                preferred_element_type=jnp.float32,
+            fetched = []
+            for shift in range(1, pair_count):
+                fetched.append(
+                    lax.ppermute(
+                        mine_w, "pair", [(i, (i + shift) % pair_count) for i in range(pair_count)]
+                    )
+                )
+            swapped_w = lax.ppermute(
+                jnp.stack(fetched), "seq", [(i, i ^ 1) for i in range(seq_count)]
             )
+            mixed_mine = jnp.dot(pieces[0], mine_w, preferred_element_type=jnp.float32)
+            mixed_other = jnp.dot(pieces[0], other_w, preferred_element_type=jnp.float32)
             for shift in range(1, pair_count):
                 incoming = lax.ppermute(
                     pieces[pair_count - shift],
                     "pair",
                     [(i, (i + shift) % pair_count) for i in range(pair_count)],
                 )
-                source = (me + pair_count - shift) % pair_count
-                mixed = mixed + jnp.dot(
-                    incoming,
-                    lax.dynamic_slice_in_dim(full_w_out, source * head_rows, head_rows, 0),
-                    preferred_element_type=jnp.float32,
+                mixed_mine = mixed_mine + jnp.dot(
+                    incoming, fetched[shift - 1], preferred_element_type=jnp.float32
                 )
+                mixed_other = mixed_other + jnp.dot(
+                    incoming, swapped_w[shift - 1], preferred_element_type=jnp.float32
+                )
+            mixed = jnp.where(
+                core == 0,
+                jnp.concatenate([mixed_mine, mixed_other], 1),
+                jnp.concatenate([mixed_other, mixed_mine], 1),
+            )
         else:
+            late_w_out, unused = lax.optimization_barrier((w_out, kv))
+            full_w_out = gather_weight_rows(late_w_out, "pair", "seq")
             own_heads = rows_to_heads(attended, "pair")
             mixed = jnp.dot(own_heads, full_w_out, preferred_element_type=jnp.float32)
     seq_out = (first_out.astype(jnp.float32) + mixed).astype(jnp.bfloat16)

time: 176 us -> 181 us (1.028)
  waiting for transfers between devices: 75.3 us -> 103 us
  starting transfers between devices: 64.4 us -> 51.1 us
  local copies, waits for them, and re-layouts: 14.4 us -> 1.55 us
  other arithmetic: 3.17 us -> 5.53 us
    ppermute x7 -> x4, starting transfers between devices: 36.8 us -> 3.94 us  [the longest x3 3.87 us: shards(): lax.ppermute(mine_w, 'pair', [(i, (i + shift) % pair_count) for i in rang...]
    ppermute x7 -> x4, waiting for transfers between devices: 0.02 us -> 21.5 us  [the longest x3 21.5 us: shards(): lax.ppermute(mine_w, 'pair', [(i, (i + shift) % pair_count) for i in rang...]
    ppermute x3, waiting for transfers between devices: 13.4 us -> 34.5 us  [rotated_all_gather(): lax.ppermute(value, axis, [(i, (i + shift) % n) for i in range(n)])]
    dynamic_update_slice x7 -> x0, local copies, waits for them, and re-layouts: 8.68 us -> none  [the longest x3 3.36 us: line_all_gather(): slots = lax.dynamic_update_index_in_dim(slots, flow_r, at_r, 0)]
    ppermute x3, starting transfers between devices: 2.65 us -> 10.5 us  [rotated_all_gather(): lax.ppermute(value, axis, [(i, (i + shift) % n) for i in range(n)])]
    ppermute x3, starting transfers between devices: 2.07 us -> 9.58 us  [shards(): lax.ppermute(pieces[pair_count - shift], 'pair', [(i, (i + shift) % pair_...]
    ppermute x3, waiting for transfers between devices: 11.6 us -> 5 us  [shards(): next_going = lax.ppermute(going, 'seq', forward)]
    ppermute x3, waiting for transfers between devices: 10.3 us -> 5.16 us  [permute_all_to_all(): lax.ppermute(outgoing, axis, [(i, (i + shift) % n) for i in range(n)])]
  transfers between devices with their start and end apart: 33 -> 30, of which waited for: 16 -> 21; matrix products, arithmetic and copies ran while one was open for 16% -> 7% of each run, Pallas kernels for 0% -> 0%
where the time goes in v12:
time: 181 us; the launch traced here: 180 us
  waiting for transfers between devices  103 us (57%)
  starting transfers between devices  51.1 us (28%)
  matrix products  17.4 us (10%)
  other arithmetic  5.53 us (3%)
    ppermute x3, waiting for transfers between devices, rotated_all_gather(): lax.ppermute(value, axis, [(i, (i + shift) % n) for i in range(n)])  34.5 us
    ppermute x3, waiting for transfers between devices, direct_reduce_scatter(): lax.ppermute(outgoing, axis, [(i, (i + shift) % n) for i in range(n)])  25.8 us
    ppermute x3, waiting for transfers between devices, shards(): lax.ppermute(mine_w, 'pair', [(i, (i + shift) % pair_count) for i in rang...  21.5 us
    ppermute x3, starting transfers between devices, rotated_all_gather(): lax.ppermute(value, axis, [(i, (i + shift) % n) for i in range(n)])  10.5 us
    ppermute x3, starting transfers between devices, shards(): lax.ppermute(pieces[pair_count - shift], 'pair', [(i, (i + shift) % pair_...  9.58 us
    ppermute x3, starting transfers between devices, permute_all_to_all(): lax.ppermute(outgoing, axis, [(i, (i + shift) % n) for i in range(n)])  7.13 us
    dot_general x5, matrix products, conv_rows(): jnp.dot(shifted, conv_weight[offset], preferred_element_type=jnp.float32)  6.46 us
    ppermute x6, starting transfers between devices, direct_all_gather(): lax.ppermute(value, axis, [(i, (i + shift) % n) for i in range(n)])  6.2 us
  transfers between devices with their start and end apart: 30, of which 21 were waited for; matrix products, arithmetic and copies ran while one was open for 7% of the time, Pallas kernels for 0%

profile of v12, /device:TPU:0, one launch (start us, length us, event | category | flops | bytes accessed | tf_op | source)
XLA Modules:
  0.0 180.3 jit_solution(12872964633391396774)
XLA Ops:
  4.1 3.1 %collective-permute-start = (bf16[128,384]{1,0:T(8,128)(2,1)S(1)}, bf16[128,384]{1,0:T(8,128)(2,1)S(1)}, u32[]{:S(2)}, u32[]{:S(2)}) collective-permute-start(bf16[128,384]{1,0:T(8,128)(2,1)S(1)} %bitcast.307), channel_id=1, source_target_pairs={{0,1},{1,2},{2,3},{3,0},{4,5},{5,6},{6,7},{7,4},{8,9},{9,10},{10,1... | collective-permute-start | bytes 294920 | tf_op jit(solution)/shard_map/ppermute | solution.py:65
  7.2 2.7 %collective-permute-start.1 = (bf16[128,384]{1,0:T(8,128)(2,1)S(1)}, bf16[128,384]{1,0:T(8,128)(2,1)S(1)}, u32[]{:S(2)}, u32[]{:S(2)}) collective-permute-start(bf16[128,384]{1,0:T(8,128)(2,1)S(1)} %bitcast.306), channel_id=1, source_target_pairs={{0,2},{1,3},{2,0},{3,1},{4,6},{5,7},{6,4},{7,5},{8,10},{9,11},{10,... | collective-permute-start | bytes 294920 | tf_op jit(solution)/shard_map/ppermute | solution.py:65
  9.9 1.4 collective-permute-start.2
  11.4 1.5 collective-permute-done
  12.9 3.5 %collective-permute-done.1 = bf16[128,384]{1,0:T(8,128)(2,1)S(1)} collective-permute-done((bf16[128,384]{1,0:T(8,128)(2,1)S(1)}, bf16[128,384]{1,0:T(8,128)(2,1)S(1)}, u32[]{:S(2)}, u32[]{:S(2)}) %collective-permute-start.1) | collective-permute-done | bytes 98336 | tf_op jit(solution)/shard_map/ppermute | solution.py:65
  16.6 1.7 collective-permute-start.3
  18.3 1.6 collective-permute-start.4
  19.9 2.4 %fusion.41 = f32[512,1536]{1,0:T(8,128)S(1)} fusion(bf16[512,384]{1,0:T(8,128)(2,1)S(1)} %bitcast.281, bf16[5,384,1536]{2,1,0:T(8,128)(2,1)} %param.12), kind=kOutput, calls=%fused_computation.68 | convolution fusion | flops 603979776 | bytes 4718592 | tf_op jit(solution)/shard_map/conv_reduce/dot_general | solution.py:39
  27.4 2.4 %collective-permute-start.5 = (bf16[128,1536]{1,0:T(8,128)(2,1)S(1)}, bf16[128,1536]{1,0:T(8,128)(2,1)S(1)}, u32[]{:S(2)}, u32[]{:S(2)}) collective-permute-start(bf16[128,1536]{1,0:T(8,128)(2,1)S(1)} %get-tuple-element.26), channel_id=1, source_target_pairs={{0,1},{1,2},{2,3},{3,0},{4,5},{5,6},{6,7},{7,4},{8,9},{9,10},{10,1... | collective-permute-start | bytes 1179656 | tf_op jit(solution)/shard_map/conv_reduce/ppermute | solution.py:51
  29.8 1.7 collective-permute-start.6
  32.3 7.8 %collective-permute-done.5 = bf16[128,1536]{1,0:T(8,128)(2,1)S(1)} collective-permute-done((bf16[128,1536]{1,0:T(8,128)(2,1)S(1)}, bf16[128,1536]{1,0:T(8,128)(2,1)S(1)}, u32[]{:S(2)}, u32[]{:S(2)}) %collective-permute-start.5) | collective-permute-done | bytes 393248 | tf_op jit(solution)/shard_map/conv_reduce/ppermute | solution.py:51
  40.1 17.9 %collective-permute-done.6 = bf16[128,1536]{1,0:T(8,128)(2,1)S(1)} collective-permute-done((bf16[128,1536]{1,0:T(8,128)(2,1)S(1)}, bf16[128,1536]{1,0:T(8,128)(2,1)S(1)}, u32[]{:S(2)}, u32[]{:S(2)}) %collective-permute-start.6) | collective-permute-done | bytes 393248 | tf_op jit(solution)/shard_map/conv_reduce/ppermute | solution.py:51
  58.6 7.8 %collective-permute-start.10 = (bf16[128,1536]{1,0:T(8,128)(2,1)S(1)}, bf16[128,1536]{1,0:T(8,128)(2,1)S(1)}, u32[]{:S(2)}, u32[]{:S(2)}) collective-permute-start(bf16[128,1536]{1,0:T(8,128)(2,1)S(1)} %fusion.73), channel_id=1, source_target_pairs={{0,3},{1,0},{2,1},{3,2},{4,7},{5,4},{6,5},{7,6},{8,11},{9,8},{10,9... | collective-permute-start | bytes 1179656 | tf_op jit(solution)/shard_map/attn_in_gather/ppermute | solution.py:123
  67.7 1.4 collective-permute-start.9
  69.1 8.2 %collective-permute-done.10 = bf16[128,1536]{1,0:T(8,128)(2,1)S(1)} collective-permute-done((bf16[128,1536]{1,0:T(8,128)(2,1)S(1)}, bf16[128,1536]{1,0:T(8,128)(2,1)S(1)}, u32[]{:S(2)}, u32[]{:S(2)}) %collective-permute-start.10) | collective-permute-done | bytes 393248 | tf_op jit(solution)/shard_map/attn_in_gather/ppermute | solution.py:123
  77.3 9.3 %collective-permute-done.8 = bf16[128,1536]{1,0:T(8,128)(2,1)} collective-permute-done((bf16[128,1536]{1,0:T(8,128)(2,1)S(1)}, bf16[128,1536]{1,0:T(8,128)(2,1)}, u32[]{:S(2)}, u32[]{:S(2)}) %collective-permute-start.8) | collective-permute-done | bytes 393248 | tf_op jit(solution)/shard_map/attn_in_gather/ppermute | solution.py:123
  86.6 17.0 %collective-permute-done.9 = bf16[128,1536]{1,0:T(8,128)(2,1)} collective-permute-done((bf16[128,1536]{1,0:T(8,128)(2,1)S(1)}, bf16[128,1536]{1,0:T(8,128)(2,1)}, u32[]{:S(2)}, u32[]{:S(2)}) %collective-permute-start.9) | collective-permute-done | bytes 393248 | tf_op jit(solution)/shard_map/attn_in_gather/ppermute | solution.py:123
  103.6 2.5 %fusion.11 = bf16[512,768]{1,0:T(8,128)(2,1)S(1)} fusion(bf16[1536,768]{1,0:T(8,128)(2,1)S(1)} %copy-done, bf16[128,1536]{1,0:T(8,128)(2,1)S(1)} %collective-permute-done.10, bf16[128,1536]{1,0:T(8,128)(2,1)} %collective-permute-done.9, bf16[128,1536]{1,0:T(8,128)(2,1)} %collective-permute-done.8, bf16[128,1536]{1,0:T(8,128)(2,1)S(1)} %fusion.73), kind=kOutput, calls=%fused_computation.12 | convolution fusion | flops 1214644224 | bytes 4718592 | tf_op jit(solution)/shard_map/dot_general | solution.py:176
  106.7 1.7 collective-permute-start.12
  108.8 2.6 %collective-permute-start.20 = (bf16[256,768]{1,0:T(8,128)(2,1)S(1)}, bf16[256,768]{1,0:T(8,128)(2,1)S(1)}, u32[]{:S(2)}, u32[]{:S(2)}) collective-permute-start(bf16[256,768]{1,0:T(8,128)(2,1)S(1)} %constant_dynamic-slice_fusion), channel_id=1, source_target_pairs={{0,2},{1,3},{2,0},{3,1},{4,6},{5,7},{6,4},{7,5},{8,10},{9,11},{10,... | collective-permute-start | bytes 1179656 | tf_op jit(solution)/shard_map/out_projection/ppermute | solution.py:239
  114.7 1.8 collective-permute-start.14
  116.5 6.3 %collective-permute-done.18 = bf16[256,768]{1,0:T(8,128)(2,1)S(1)} collective-permute-done((bf16[256,768]{1,0:T(8,128)(2,1)S(1)}, bf16[256,768]{1,0:T(8,128)(2,1)S(1)}, u32[]{:S(2)}, u32[]{:S(2)}) %collective-permute-start.18) | collective-permute-done | bytes 393248 | tf_op jit(solution)/shard_map/out_projection/ppermute | solution.py:239
  122.8 15.2 %collective-permute-done.20 = bf16[256,768]{1,0:T(8,128)(2,1)S(1)} collective-permute-done((bf16[256,768]{1,0:T(8,128)(2,1)S(1)}, bf16[256,768]{1,0:T(8,128)(2,1)S(1)}, u32[]{:S(2)}, u32[]{:S(2)}) %collective-permute-start.20) | collective-permute-done | bytes 393248 | tf_op jit(solution)/shard_map/out_projection/ppermute | solution.py:239
  139.4 1.5 collective-permute-start.16
  140.9 3.6 %collective-permute-done.15 = bf16[2,256,256]{2,1,0:T(8,128)(2,1)S(1)} collective-permute-done((bf16[2,256,256]{2,1,0:T(8,128)(2,1)S(1)}, bf16[2,256,256]{2,1,0:T(8,128)(2,1)S(1)}, u32[]{:S(2)}, u32[]{:S(2)}) %collective-permute-start.15) | collective-permute-done | bytes 262176 | tf_op jit(solution)/shard_map/kv_ring/ppermute | solution.py:219
  149.8 8.1 %collective-permute-start.17 = (bf16[128,256]{0,1:T(8,128)(2,1)S(1)}, bf16[128,256]{0,1:T(8,128)(2,1)S(1)}, u32[]{:S(2)}, u32[]{:S(2)}) collective-permute-start(bf16[128,256]{0,1:T(8,128)(2,1)S(1)} %bitcast.313), channel_id=1, source_target_pairs={{0,1},{1,2},{2,3},{3,0},{4,5},{5,6},{6,7},{7,4},{8,9},{9,10},{10,1... | collective-permute-start | bytes 196616 | tf_op jit(solution)/shard_map/out_projection/ppermute | solution.py:249
  158.4 1.5 collective-permute-start.19
  160.4 4.1 %collective-permute-done.21 = bf16[128,256]{0,1:T(8,128)(2,1)S(1)} collective-permute-done((bf16[128,256]{0,1:T(8,128)(2,1)S(1)}, bf16[128,256]{0,1:T(8,128)(2,1)S(1)}, u32[]{:S(2)}, u32[]{:S(2)}) %collective-permute-start.21) | collective-permute-done | bytes 65568 | tf_op jit(solution)/shard_map/out_projection/ppermute | solution.py:249
  168.4 3.0 %collective-permute-start.25 = (bf16[8,256]{1,0:T(8,128)(2,1)S(1)}, bf16[8,256]{1,0:T(8,128)(2,1)S(1)}, u32[]{:S(2)}, u32[]{:S(2)}) collective-permute-start(bf16[8,256]{1,0:T(8,128)(2,1)S(1)} %get-tuple-element.63), channel_id=1, source_target_pairs={{0,2},{1,3},{2,0},{3,1},{4,6},{5,7},{6,4},{7,5},{8,10},{9,11},{10,... | collective-permute-start | bytes 12296 | tf_op jit(solution)/shard_map/sides_gather/ppermute | solution.py:135
  171.9 1.6 collective-permute-done.24
  173.5 1.5 collective-permute-done.26
  175.9 1.4 collective-permute-start.29
  (123 shorter events, 31.3 us)
Async XLA Ops:
  0.6 103.0 %copy-start = (bf16[1536,768]{1,0:T(8,128)(2,1)S(1)}, bf16[1536,768]{1,0:T(8,128)(2,1)}, u32[]{:S(2)}) copy-start(bf16[1536,768]{1,0:T(8,128)(2,1)} %param.14) | copy-start | bytes 7077892
  4.1 8.7 %collective-permute-start = (bf16[128,384]{1,0:T(8,128)(2,1)S(1)}, bf16[128,384]{1,0:T(8,128)(2,1)S(1)}, u32[]{:S(2)}, u32[]{:S(2)}) collective-permute-start(bf16[128,384]{1,0:T(8,128)(2,1)S(1)} %bitcast.307), channel_id=1, source_target_pairs={{0,1},{1,2},{2,3},{3,0},{4,5},{5,6},{6,7},{7,4},{8,9},{9,10},{10,1... | collective-permute-start | bytes 294920 | tf_op jit(solution)/shard_map/ppermute | solution.py:65
  7.2 9.2 %collective-permute-start.1 = (bf16[128,384]{1,0:T(8,128)(2,1)S(1)}, bf16[128,384]{1,0:T(8,128)(2,1)S(1)}, u32[]{:S(2)}, u32[]{:S(2)}) collective-permute-start(bf16[128,384]{1,0:T(8,128)(2,1)S(1)} %bitcast.306), channel_id=1, source_target_pairs={{0,2},{1,3},{2,0},{3,1},{4,6},{5,7},{6,4},{7,5},{8,10},{9,11},{10,... | collective-permute-start | bytes 294920 | tf_op jit(solution)/shard_map/ppermute | solution.py:65
  9.9 6.7 %collective-permute-start.2 = (bf16[128,384]{1,0:T(8,128)(2,1)S(1)}, bf16[128,384]{1,0:T(8,128)(2,1)S(1)}, u32[]{:S(2)}, u32[]{:S(2)}) collective-permute-start(bf16[128,384]{1,0:T(8,128)(2,1)S(1)} %bitcast.305), channel_id=1, source_target_pairs={{0,3},{1,0},{2,1},{3,2},{4,7},{5,4},{6,5},{7,6},{8,11},{9,8},{10,9... | collective-permute-start | bytes 294920 | tf_op jit(solution)/shard_map/ppermute | solution.py:65
  16.6 8.5 %collective-permute-start.3 = (bf16[8,384]{1,0:T(8,128)(2,1)S(1)}, bf16[8,384]{1,0:T(8,128)(2,1)S(1)}, u32[]{:S(2)}, u32[]{:S(2)}) collective-permute-start(bf16[8,384]{1,0:T(8,128)(2,1)S(1)} %get-tuple-element.31), channel_id=1, source_target_pairs={{0,4},{4,8},{8,12},{1,5},{5,9},{9,13},{2,6},{6,10},{10,14},{3,7},{... | collective-permute-start | bytes 18440 | tf_op jit(solution)/shard_map/ppermute | solution.py:25
  18.3 4.8 %collective-permute-start.4 = (bf16[8,384]{1,0:T(8,128)(2,1)S(1)}, bf16[8,384]{1,0:T(8,128)(2,1)S(1)}, u32[]{:S(2)}, u32[]{:S(2)}) collective-permute-start(bf16[8,384]{1,0:T(8,128)(2,1)S(1)} %get-tuple-element.32), channel_id=1, source_target_pairs={{4,0},{8,4},{12,8},{5,1},{9,5},{13,9},{6,2},{10,6},{14,10},{7,3},{... | collective-permute-start | bytes 18440 | tf_op jit(solution)/shard_map/ppermute | solution.py:26
  26.1 32.0 %copy-start.2 = (bf16[128,1536]{1,0:T(8,128)(2,1)S(1)}, bf16[128,1536]{1,0:T(8,128)(2,1)}, u32[]{:S(2)}) copy-start(bf16[128,1536]{1,0:T(8,128)(2,1)} %param.10) | copy-start | bytes 1179652
  27.4 12.7 %collective-permute-start.5 = (bf16[128,1536]{1,0:T(8,128)(2,1)S(1)}, bf16[128,1536]{1,0:T(8,128)(2,1)S(1)}, u32[]{:S(2)}, u32[]{:S(2)}) collective-permute-start(bf16[128,1536]{1,0:T(8,128)(2,1)S(1)} %get-tuple-element.26), channel_id=1, source_target_pairs={{0,1},{1,2},{2,3},{3,0},{4,5},{5,6},{6,7},{7,4},{8,9},{9,10},{10,1... | collective-permute-start | bytes 1179656 | tf_op jit(solution)/shard_map/conv_reduce/ppermute | solution.py:51
  29.8 28.2 %collective-permute-start.6 = (bf16[128,1536]{1,0:T(8,128)(2,1)S(1)}, bf16[128,1536]{1,0:T(8,128)(2,1)S(1)}, u32[]{:S(2)}, u32[]{:S(2)}) collective-permute-start(bf16[128,1536]{1,0:T(8,128)(2,1)S(1)} %get-tuple-element.28), channel_id=1, source_target_pairs={{0,2},{1,3},{2,0},{3,1},{4,6},{5,7},{6,4},{7,5},{8,10},{9,11},{10,... | collective-permute-start | bytes 1179656 | tf_op jit(solution)/shard_map/conv_reduce/ppermute | solution.py:51
  31.5 26.5 %collective-permute-start.7 = (bf16[128,1536]{1,0:T(8,128)(2,1)S(1)}, bf16[128,1536]{1,0:T(8,128)(2,1)S(1)}, u32[]{:S(2)}, u32[]{:S(2)}) collective-permute-start(bf16[128,1536]{1,0:T(8,128)(2,1)S(1)} %get-tuple-element.27), channel_id=1, source_target_pairs={{0,3},{1,0},{2,1},{3,2},{4,7},{5,4},{6,5},{7,6},{8,11},{9,8},{10,9... | collective-permute-start | bytes 1179656 | tf_op jit(solution)/shard_map/conv_reduce/ppermute | solution.py:51
  58.6 18.7 %collective-permute-start.10 = (bf16[128,1536]{1,0:T(8,128)(2,1)S(1)}, bf16[128,1536]{1,0:T(8,128)(2,1)S(1)}, u32[]{:S(2)}, u32[]{:S(2)}) collective-permute-start(bf16[128,1536]{1,0:T(8,128)(2,1)S(1)} %fusion.73), channel_id=1, source_target_pairs={{0,3},{1,0},{2,1},{3,2},{4,7},{5,4},{6,5},{7,6},{8,11},{9,8},{10,9... | collective-permute-start | bytes 1179656 | tf_op jit(solution)/shard_map/attn_in_gather/ppermute | solution.py:123
  66.4 20.2 %collective-permute-start.8 = (bf16[128,1536]{1,0:T(8,128)(2,1)S(1)}, bf16[128,1536]{1,0:T(8,128)(2,1)}, u32[]{:S(2)}, u32[]{:S(2)}) collective-permute-start(bf16[128,1536]{1,0:T(8,128)(2,1)S(1)} %fusion.73), channel_id=1, source_target_pairs={{0,1},{1,2},{2,3},{3,0},{4,5},{5,6},{6,7},{7,4},{8,9},{9,10},{10,1... | collective-permute-start | bytes 1179656 | tf_op jit(solution)/shard_map/attn_in_gather/ppermute | solution.py:123
  67.7 35.9 %collective-permute-start.9 = (bf16[128,1536]{1,0:T(8,128)(2,1)S(1)}, bf16[128,1536]{1,0:T(8,128)(2,1)}, u32[]{:S(2)}, u32[]{:S(2)}) collective-permute-start(bf16[128,1536]{1,0:T(8,128)(2,1)S(1)} %fusion.73), channel_id=1, source_target_pairs={{0,2},{1,3},{2,0},{3,1},{4,6},{5,7},{6,4},{7,5},{8,10},{9,11},{10,... | collective-permute-start | bytes 1179656 | tf_op jit(solution)/shard_map/attn_in_gather/ppermute | solution.py:123
  106.6 7.4 %collective-permute-start.11 = (bf16[2,256,256]{2,1,0:T(8,128)(2,1)S(1)}, bf16[2,256,256]{2,1,0:T(8,128)(2,1)S(1)}, u32[]{:S(2)}, u32[]{:S(2)}) collective-permute-start(bf16[2,256,256]{2,1,0:T(8,128)(2,1)S(1)} %get-tuple-element.29), channel_id=1, source_target_pairs={{0,4},{4,8},{8,12},{12,0},{1,5},{5,9},{9,13},{13,1},{2,6},{6,10},{... | collective-permute-start | bytes 786440 | tf_op jit(solution)/shard_map/kv_ring/ppermute | solution.py:219
  106.7 7.7 %collective-permute-start.12 = (bf16[2,256,256]{2,1,0:T(8,128)(2,1)S(1)}, bf16[2,256,256]{2,1,0:T(8,128)(2,1)S(1)}, u32[]{:S(2)}, u32[]{:S(2)}) collective-permute-start(bf16[2,256,256]{2,1,0:T(8,128)(2,1)S(1)} %get-tuple-element.30), channel_id=1, source_target_pairs={{4,0},{8,4},{12,8},{0,12},{5,1},{9,5},{13,9},{1,13},{6,2},{10,6},{... | collective-permute-start | bytes 786440 | tf_op jit(solution)/shard_map/kv_ring/ppermute | solution.py:220
  108.8 14.0 %collective-permute-start.18 = (bf16[256,768]{1,0:T(8,128)(2,1)S(1)}, bf16[256,768]{1,0:T(8,128)(2,1)S(1)}, u32[]{:S(2)}, u32[]{:S(2)}) collective-permute-start(bf16[256,768]{1,0:T(8,128)(2,1)S(1)} %constant_dynamic-slice_fusion), channel_id=1, source_target_pairs={{0,1},{1,2},{2,3},{3,0},{4,5},{5,6},{6,7},{7,4},{8,9},{9,10},{10,1... | collective-permute-start | bytes 1179656 | tf_op jit(solution)/shard_map/out_projection/ppermute | solution.py:239
  108.8 29.2 %collective-permute-start.20 = (bf16[256,768]{1,0:T(8,128)(2,1)S(1)}, bf16[256,768]{1,0:T(8,128)(2,1)S(1)}, u32[]{:S(2)}, u32[]{:S(2)}) collective-permute-start(bf16[256,768]{1,0:T(8,128)(2,1)S(1)} %constant_dynamic-slice_fusion), channel_id=1, source_target_pairs={{0,2},{1,3},{2,0},{3,1},{4,6},{5,7},{6,4},{7,5},{8,10},{9,11},{10,... | collective-permute-start | bytes 1179656 | tf_op jit(solution)/shard_map/out_projection/ppermute | solution.py:239
  111.4 26.6 %collective-permute-start.22 = (bf16[256,768]{1,0:T(8,128)(2,1)S(1)}, bf16[256,768]{1,0:T(8,128)(2,1)S(1)}, u32[]{:S(2)}, u32[]{:S(2)}) collective-permute-start(bf16[256,768]{1,0:T(8,128)(2,1)S(1)} %constant_dynamic-slice_fusion), channel_id=1, source_target_pairs={{0,3},{1,0},{2,1},{3,2},{4,7},{5,4},{6,5},{7,6},{8,11},{9,8},{10,9... | collective-permute-start | bytes 1179656 | tf_op jit(solution)/shard_map/out_projection/ppermute | solution.py:239
  114.0 24.2 %collective-permute-start.13 = (bf16[2,256,256]{2,1,0:T(8,128)(2,1)S(1)}, bf16[2,256,256]{2,1,0:T(8,128)(2,1)S(1)}, u32[]{:S(2)}, u32[]{:S(2)}) collective-permute-start(bf16[2,256,256]{2,1,0:T(8,128)(2,1)S(1)} %collective-permute-done.11), channel_id=1, source_target_pairs={{0,4},{4,8},{8,12},{12,0},{1,5},{5,9},{9,13},{13,1},{2,6},{6,10},{... | collective-permute-start | bytes 786440 | tf_op jit(solution)/shard_map/kv_ring/ppermute | solution.py:219
  114.7 24.4 %collective-permute-start.14 = (bf16[2,256,256]{2,1,0:T(8,128)(2,1)S(1)}, bf16[2,256,256]{2,1,0:T(8,128)(2,1)S(1)}, u32[]{:S(2)}, u32[]{:S(2)}) collective-permute-start(bf16[2,256,256]{2,1,0:T(8,128)(2,1)S(1)} %collective-permute-done.12), channel_id=1, source_target_pairs={{4,0},{8,4},{12,8},{0,12},{5,1},{9,5},{13,9},{1,13},{6,2},{10,6},{... | collective-permute-start | bytes 786440 | tf_op jit(solution)/shard_map/kv_ring/ppermute | solution.py:220
  138.1 27.9 %collective-permute-start.23 = (bf16[3,256,768]{2,1,0:T(8,128)(2,1)S(1)}, bf16[3,256,768]{2,1,0:T(8,128)(2,1)S(1)}, u32[]{:S(2)}, u32[]{:S(2)}) collective-permute-start(bf16[3,256,768]{2,1,0:T(8,128)(2,1)S(1)} %pad_maximum_fusion), channel_id=1, source_target_pairs={{0,4},{4,0},{8,12},{12,8},{1,5},{5,1},{9,13},{13,9},{2,6},{6,2},{1... | collective-permute-start | bytes 3538952 | tf_op jit(solution)/shard_map/out_projection/ppermute | solution.py:243
  138.2 6.3 %collective-permute-start.15 = (bf16[2,256,256]{2,1,0:T(8,128)(2,1)S(1)}, bf16[2,256,256]{2,1,0:T(8,128)(2,1)S(1)}, u32[]{:S(2)}, u32[]{:S(2)}) collective-permute-start(bf16[2,256,256]{2,1,0:T(8,128)(2,1)S(1)} %collective-permute-done.13), channel_id=1, source_target_pairs={{0,4},{4,8},{8,12},{12,0},{1,5},{5,9},{9,13},{13,1},{2,6},{6,10},{... | collective-permute-start | bytes 786440 | tf_op jit(solution)/shard_map/kv_ring/ppermute | solution.py:219
  139.4 6.2 %collective-permute-start.16 = (bf16[2,256,256]{2,1,0:T(8,128)(2,1)S(1)}, bf16[2,256,256]{2,1,0:T(8,128)(2,1)S(1)}, u32[]{:S(2)}, u32[]{:S(2)}) collective-permute-start(bf16[2,256,256]{2,1,0:T(8,128)(2,1)S(1)} %collective-permute-done.14), channel_id=1, source_target_pairs={{4,0},{8,4},{12,8},{0,12},{5,1},{9,5},{13,9},{1,13},{6,2},{10,6},{... | collective-permute-start | bytes 786440 | tf_op jit(solution)/shard_map/kv_ring/ppermute | solution.py:220
  149.8 10.3 %collective-permute-start.17 = (bf16[128,256]{0,1:T(8,128)(2,1)S(1)}, bf16[128,256]{0,1:T(8,128)(2,1)S(1)}, u32[]{:S(2)}, u32[]{:S(2)}) collective-permute-start(bf16[128,256]{0,1:T(8,128)(2,1)S(1)} %bitcast.313), channel_id=1, source_target_pairs={{0,1},{1,2},{2,3},{3,0},{4,5},{5,6},{6,7},{7,4},{8,9},{9,10},{10,1... | collective-permute-start | bytes 196616 | tf_op jit(solution)/shard_map/out_projection/ppermute | solution.py:249
  158.4 6.1 %collective-permute-start.21 = (bf16[128,256]{0,1:T(8,128)(2,1)S(1)}, bf16[128,256]{0,1:T(8,128)(2,1)S(1)}, u32[]{:S(2)}, u32[]{:S(2)}) collective-permute-start(bf16[128,256]{0,1:T(8,128)(2,1)S(1)} %bitcast.312), channel_id=1, source_target_pairs={{0,3},{1,0},{2,1},{3,2},{4,7},{5,4},{6,5},{7,6},{8,11},{9,8},{10,9... | collective-permute-start | bytes 196616 | tf_op jit(solution)/shard_map/out_projection/ppermute | solution.py:249
  158.4 7.3 %collective-permute-start.19 = (bf16[128,256]{0,1:T(8,128)(2,1)S(1)}, bf16[128,256]{0,1:T(8,128)(2,1)S(1)}, u32[]{:S(2)}, u32[]{:S(2)}) collective-permute-start(bf16[128,256]{0,1:T(8,128)(2,1)S(1)} %bitcast.311), channel_id=1, source_target_pairs={{0,2},{1,3},{2,0},{3,1},{4,6},{5,7},{6,4},{7,5},{8,10},{9,11},{10,... | collective-permute-start | bytes 196616 | tf_op jit(solution)/shard_map/out_projection/ppermute | solution.py:249
  168.1 5.4 %collective-permute-start.24 = (bf16[8,256]{1,0:T(8,128)(2,1)S(1)}, bf16[8,256]{1,0:T(8,128)(2,1)S(1)}, u32[]{:S(2)}, u32[]{:S(2)}) collective-permute-start(bf16[8,256]{1,0:T(8,128)(2,1)S(1)} %get-tuple-element.63), channel_id=1, source_target_pairs={{0,1},{1,2},{2,3},{3,0},{4,5},{5,6},{6,7},{7,4},{8,9},{9,10},{10,1... | collective-permute-start | bytes 12296 | tf_op jit(solution)/shard_map/sides_gather/ppermute | solution.py:135
  168.4 5.1 %collective-permute-start.25 = (bf16[8,256]{1,0:T(8,128)(2,1)S(1)}, bf16[8,256]{1,0:T(8,128)(2,1)S(1)}, u32[]{:S(2)}, u32[]{:S(2)}) collective-permute-start(bf16[8,256]{1,0:T(8,128)(2,1)S(1)} %get-tuple-element.63), channel_id=1, source_target_pairs={{0,2},{1,3},{2,0},{3,1},{4,6},{5,7},{6,4},{7,5},{8,10},{9,11},{10,... | collective-permute-start | bytes 12296 | tf_op jit(solution)/shard_map/sides_gather/ppermute | solution.py:135
  171.4 3.6 %collective-permute-start.26 = (bf16[8,256]{1,0:T(8,128)(2,1)S(1)}, bf16[8,256]{1,0:T(8,128)(2,1)S(1)}, u32[]{:S(2)}, u32[]{:S(2)}) collective-permute-start(bf16[8,256]{1,0:T(8,128)(2,1)S(1)} %get-tuple-element.63), channel_id=1, source_target_pairs={{0,3},{1,0},{2,1},{3,2},{4,7},{5,4},{6,5},{7,6},{8,11},{9,8},{10,9... | collective-permute-start | bytes 12296 | tf_op jit(solution)/shard_map/sides_gather/ppermute | solution.py:135
  175.0 3.2 %collective-permute-start.27 = (bf16[32,256]{1,0:T(8,128)(2,1)S(1)}, bf16[32,256]{1,0:T(8,128)(2,1)S(1)}, u32[]{:S(2)}, u32[]{:S(2)}) collective-permute-start(bf16[32,256]{1,0:T(8,128)(2,1)S(1)} %bitcast.308), channel_id=1, source_target_pairs={{0,4},{4,8},{8,12},{12,0},{1,5},{5,9},{9,13},{13,1},{2,6},{6,10},{... | collective-permute-start | bytes 49160 | tf_op jit(solution)/shard_map/sides_gather/ppermute | solution.py:135
  175.0 3.9 %collective-permute-start.28 = (bf16[32,256]{1,0:T(8,128)(2,1)S(1)}, bf16[32,256]{1,0:T(8,128)(2,1)S(1)}, u32[]{:S(2)}, u32[]{:S(2)}) collective-permute-start(bf16[32,256]{1,0:T(8,128)(2,1)S(1)} %bitcast.309), channel_id=1, source_target_pairs={{0,8},{4,12},{8,0},{12,4},{1,9},{5,13},{9,1},{13,5},{2,10},{6,14},... | collective-permute-start | bytes 49160 | tf_op jit(solution)/shard_map/sides_gather/ppermute | solution.py:135
  175.9 3.0 %collective-permute-start.29 = (bf16[32,256]{1,0:T(8,128)(2,1)S(1)}, bf16[32,256]{1,0:T(8,128)(2,1)S(1)}, u32[]{:S(2)}, u32[]{:S(2)}) collective-permute-start(bf16[32,256]{1,0:T(8,128)(2,1)S(1)} %bitcast.310), channel_id=1, source_target_pairs={{0,12},{4,0},{8,4},{12,8},{1,13},{5,1},{9,5},{13,9},{2,14},{6,2},{... | collective-permute-start | bytes 49160 | tf_op jit(solution)/shard_map/sides_gather/ppermute | solution.py:135
  (7 other events, 70.4 us)

commit v13 on v12

--- a/solution.py
+++ b/solution.py
@@ -179,7 +179,7 @@
     queries = grouped[:, :, :KEY_SIZE]
     kv = grouped[:, :, KEY_SIZE:]
     if rotated and seq_count % 2 == 0:
-        late_w_out, kv = lax.optimization_barrier((w_out, kv))
+        late_w_out = w_out
     scale = 1.0 / math.sqrt(KEY_SIZE)
 
     def attend(state, kv_block):

time: 181 us -> 195 us (1.077)
  starting transfers between devices: 51.1 us -> 81.5 us
  waiting for transfers between devices: 103 us -> 78 us
  local copies, waits for them, and re-layouts: 1.55 us -> 4.77 us
  matrix products: 17.4 us -> 20.5 us
  other arithmetic: 5.53 us -> 8.12 us
    ppermute x3, starting transfers between devices: 10.5 us -> 32.9 us  [rotated_all_gather(): lax.ppermute(value, axis, [(i, (i + shift) % n) for i in range(n)])]
    ppermute x3, waiting for transfers between devices: 21.5 us -> 0.01 us  [shards(): lax.ppermute(mine_w, 'pair', [(i, (i + shift) % pair_count) for i in rang...]
    ppermute x1, starting transfers between devices: 0.07 us -> 10.4 us  [shards(): lax.ppermute(jnp.stack(fetched), 'seq', [(i, i ^ 1) for i in range(seq_co...]
    ppermute x3, waiting for transfers between devices: 5 us -> 12 us  [shards(): next_going = lax.ppermute(going, 'seq', forward)]
    ppermute x3, waiting for transfers between devices: 34.5 us -> 28 us  [rotated_all_gather(): lax.ppermute(value, axis, [(i, (i + shift) % n) for i in range(n)])]
    ppermute x3, starting transfers between devices: 9.58 us -> 5.04 us  [shards(): lax.ppermute(pieces[pair_count - shift], 'pair', [(i, (i + shift) % pair_...]
    ppermute x3, waiting for transfers between devices: 25.8 us -> 21.7 us  [direct_reduce_scatter(): lax.ppermute(outgoing, axis, [(i, (i + shift) % n) for i in range(n)])]
    dot_general x3, matrix products: 0.7 us -> 2.76 us  [shards(): jnp.dot(incoming, fetched[shift - 1], preferred_element_type=jnp.float32)]
  transfers between devices with their start and end apart: 30 -> 30, of which waited for: 21 -> 19; matrix products, arithmetic and copies ran while one was open for 7% -> 11% of each run, Pallas kernels for 0% -> 0%
where the time goes in v13:
time: 195 us; the launch traced here: 194 us
  starting transfers between devices  81.5 us (42%)
  waiting for transfers between devices  78 us (40%)
  matrix products  20.5 us (11%)
  other arithmetic  8.12 us (4%)
  local copies, waits for them, and re-layouts  4.77 us (2%)
    ppermute x3, starting transfers between devices, rotated_all_gather(): lax.ppermute(value, axis, [(i, (i + shift) % n) for i in range(n)])  32.9 us
    ppermute x3, waiting for transfers between devices, rotated_all_gather(): lax.ppermute(value, axis, [(i, (i + shift) % n) for i in range(n)])  28 us
    ppermute x3, waiting for transfers between devices, direct_reduce_scatter(): lax.ppermute(outgoing, axis, [(i, (i + shift) % n) for i in range(n)])  21.7 us
    ppermute x3, waiting for transfers between devices, shards(): next_going = lax.ppermute(going, 'seq', forward)  12 us
    ppermute x1, starting transfers between devices, shards(): lax.ppermute(jnp.stack(fetched), 'seq', [(i, i ^ 1) for i in range(seq_co...  10.4 us
    ppermute x3, starting transfers between devices, permute_all_to_all(): lax.ppermute(outgoing, axis, [(i, (i + shift) % n) for i in range(n)])  7.13 us
    ppermute x6, starting transfers between devices, direct_all_gather(): lax.ppermute(value, axis, [(i, (i + shift) % n) for i in range(n)])  7.08 us
    dot_general x5, matrix products, conv_rows(): jnp.dot(shifted, conv_weight[offset], preferred_element_type=jnp.float32)  6.46 us
  transfers between devices with their start and end apart: 30, of which 19 were waited for; matrix products, arithmetic and copies ran while one was open for 11% of the time, Pallas kernels for 0%

profile of v13, /device:TPU:0, one launch (start us, length us, event | category | flops | bytes accessed | tf_op | source)
XLA Modules:
  0.0 194.2 jit_solution(13014688246337037862)
XLA Ops:
  4.1 3.1 %collective-permute-start = (bf16[128,384]{1,0:T(8,128)(2,1)S(1)}, bf16[128,384]{1,0:T(8,128)(2,1)S(1)}, u32[]{:S(2)}, u32[]{:S(2)}) collective-permute-start(bf16[128,384]{1,0:T(8,128)(2,1)S(1)} %bitcast.307), channel_id=1, source_target_pairs={{0,1},{1,2},{2,3},{3,0},{4,5},{5,6},{6,7},{7,4},{8,9},{9,10},{10,1... | collective-permute-start | bytes 294920 | tf_op jit(solution)/shard_map/ppermute | solution.py:65
  7.2 2.7 %collective-permute-start.1 = (bf16[128,384]{1,0:T(8,128)(2,1)S(1)}, bf16[128,384]{1,0:T(8,128)(2,1)S(1)}, u32[]{:S(2)}, u32[]{:S(2)}) collective-permute-start(bf16[128,384]{1,0:T(8,128)(2,1)S(1)} %bitcast.306), channel_id=1, source_target_pairs={{0,2},{1,3},{2,0},{3,1},{4,6},{5,7},{6,4},{7,5},{8,10},{9,11},{10,... | collective-permute-start | bytes 294920 | tf_op jit(solution)/shard_map/ppermute | solution.py:65
  11.4 1.5 collective-permute-done
  12.9 3.5 %collective-permute-done.1 = bf16[128,384]{1,0:T(8,128)(2,1)S(1)} collective-permute-done((bf16[128,384]{1,0:T(8,128)(2,1)S(1)}, bf16[128,384]{1,0:T(8,128)(2,1)S(1)}, u32[]{:S(2)}, u32[]{:S(2)}) %collective-permute-start.1) | collective-permute-done | bytes 98336 | tf_op jit(solution)/shard_map/ppermute | solution.py:65
  16.6 1.7 collective-permute-start.3
  18.3 1.6 collective-permute-start.4
  19.9 2.4 %fusion.41 = f32[512,1536]{1,0:T(8,128)S(1)} fusion(bf16[512,384]{1,0:T(8,128)(2,1)S(1)} %bitcast.292, bf16[5,384,1536]{2,1,0:T(8,128)(2,1)} %param.12), kind=kOutput, calls=%fused_computation.68 | convolution fusion | flops 603979776 | bytes 4718592 | tf_op jit(solution)/shard_map/conv_reduce/dot_general | solution.py:39
  27.3 1.6 copy-done.1
  29.9 2.4 %collective-permute-start.5 = (bf16[128,1536]{1,0:T(8,128)(2,1)}, bf16[128,1536]{1,0:T(8,128)(2,1)}, u32[]{:S(2)}, u32[]{:S(2)}) collective-permute-start(bf16[128,1536]{1,0:T(8,128)(2,1)} %get-tuple-element.22), channel_id=1, source_target_pairs={{0,1},{1,2},{2,3},{3,0},{4,5},{5,6},{6,7},{7,4},{8,9},{9,10},{10,1... | collective-permute-start | bytes 1179656 | tf_op jit(solution)/shard_map/conv_reduce/ppermute | solution.py:51
  32.3 1.7 collective-permute-start.6
  38.0 4.9 %collective-permute-done.5 = bf16[128,1536]{1,0:T(8,128)(2,1)} collective-permute-done((bf16[128,1536]{1,0:T(8,128)(2,1)}, bf16[128,1536]{1,0:T(8,128)(2,1)}, u32[]{:S(2)}, u32[]{:S(2)}) %collective-permute-start.5) | collective-permute-done | bytes 393248 | tf_op jit(solution)/shard_map/conv_reduce/ppermute | solution.py:51
  42.9 2.5 %collective-permute-start.22 = (bf16[256,768]{1,0:T(8,128)(2,1)}, bf16[256,768]{1,0:T(8,128)(2,1)}, u32[]{:S(2)}, u32[]{:S(2)}) collective-permute-start(bf16[256,768]{1,0:T(8,128)(2,1)} %constant_dynamic-slice_fusion), channel_id=1, source_target_pairs={{0,3},{1,0},{2,1},{3,2},{4,7},{5,4},{6,5},{7,6},{8,11},{9,8},{10,9... | collective-permute-start | bytes 1179656 | tf_op jit(solution)/shard_map/out_projection/ppermute | solution.py:239
  45.4 16.8 %collective-permute-done.6 = bf16[128,1536]{1,0:T(8,128)(2,1)} collective-permute-done((bf16[128,1536]{1,0:T(8,128)(2,1)}, bf16[128,1536]{1,0:T(8,128)(2,1)}, u32[]{:S(2)}, u32[]{:S(2)}) %collective-permute-start.6) | collective-permute-done | bytes 393248 | tf_op jit(solution)/shard_map/conv_reduce/ppermute | solution.py:51
  62.2 1.8 fusion.71
  64.2 6.6 %collective-permute-start.10 = (bf16[128,1536]{1,0:T(8,128)(2,1)S(1)}, bf16[128,1536]{1,0:T(8,128)(2,1)}, u32[]{:S(2)}, u32[]{:S(2)}) collective-permute-start(bf16[128,1536]{1,0:T(8,128)(2,1)S(1)} %fusion.73), channel_id=1, source_target_pairs={{0,3},{1,0},{2,1},{3,2},{4,7},{5,4},{6,5},{7,6},{8,11},{9,8},{10,9... | collective-permute-start | bytes 1179656 | tf_op jit(solution)/shard_map/attn_in_gather/ppermute | solution.py:123
  70.8 18.1 %collective-permute-start.8 = (bf16[128,1536]{1,0:T(8,128)(2,1)S(1)}, bf16[128,1536]{1,0:T(8,128)(2,1)}, u32[]{:S(2)}, u32[]{:S(2)}) collective-permute-start(bf16[128,1536]{1,0:T(8,128)(2,1)S(1)} %fusion.73), channel_id=1, source_target_pairs={{0,1},{1,2},{2,3},{3,0},{4,5},{5,6},{6,7},{7,4},{8,9},{9,10},{10,1... | collective-permute-start | bytes 1179656 | tf_op jit(solution)/shard_map/attn_in_gather/ppermute | solution.py:123
  88.9 8.3 %collective-permute-start.9 = (bf16[128,1536]{1,0:T(8,128)(2,1)S(1)}, bf16[128,1536]{1,0:T(8,128)(2,1)}, u32[]{:S(2)}, u32[]{:S(2)}) collective-permute-start(bf16[128,1536]{1,0:T(8,128)(2,1)S(1)} %fusion.73), channel_id=1, source_target_pairs={{0,2},{1,3},{2,0},{3,1},{4,6},{5,7},{6,4},{7,5},{8,10},{9,11},{10,... | collective-permute-start | bytes 1179656 | tf_op jit(solution)/shard_map/attn_in_gather/ppermute | solution.py:123
  98.4 10.4 %collective-permute-start.23 = (bf16[3,256,768]{2,1,0:T(8,128)(2,1)S(1)}, bf16[3,256,768]{2,1,0:T(8,128)(2,1)S(1)}, u32[]{:S(2)}, u32[]{:S(2)}) collective-permute-start(bf16[3,256,768]{2,1,0:T(8,128)(2,1)S(1)} %pad_maximum_fusion), channel_id=1, source_target_pairs={{0,4},{4,0},{8,12},{12,8},{1,5},{5,1},{9,13},{13,9},{2,6},{6,2},{1... | collective-permute-start | bytes 3538952 | tf_op jit(solution)/shard_map/out_projection/ppermute | solution.py:243
  110.0 26.8 %collective-permute-done.9 = bf16[128,1536]{1,0:T(8,128)(2,1)} collective-permute-done((bf16[128,1536]{1,0:T(8,128)(2,1)S(1)}, bf16[128,1536]{1,0:T(8,128)(2,1)}, u32[]{:S(2)}, u32[]{:S(2)}) %collective-permute-start.9) | collective-permute-done | bytes 393248 | tf_op jit(solution)/shard_map/attn_in_gather/ppermute | solution.py:123
  136.8 2.6 %fusion.11 = bf16[512,768]{1,0:T(8,128)(2,1)S(1)} fusion(bf16[1536,768]{1,0:T(8,128)(2,1)S(1)} %copy-done, bf16[128,1536]{1,0:T(8,128)(2,1)} %collective-permute-done.10, bf16[128,1536]{1,0:T(8,128)(2,1)} %collective-permute-done.9, bf16[128,1536]{1,0:T(8,128)(2,1)} %collective-permute-done.8, bf16[128,1536]{1,0:T(8,128)(2,1)S(1)} %fusion.73), kind=kOutput, calls=%fused_computation.12 | convolution fusion | flops 1214644224 | bytes 4718592 | tf_op jit(solution)/shard_map/dot_general | solution.py:176
  140.0 1.7 collective-permute-start.12
  142.0 4.4 %collective-permute-done.11 = bf16[2,256,256]{2,1,0:T(8,128)(2,1)S(1)} collective-permute-done((bf16[2,256,256]{2,1,0:T(8,128)(2,1)S(1)}, bf16[2,256,256]{2,1,0:T(8,128)(2,1)S(1)}, u32[]{:S(2)}, u32[]{:S(2)}) %collective-permute-start.11) | collective-permute-done | bytes 262176 | tf_op jit(solution)/shard_map/kv_ring/ppermute | solution.py:219
  146.8 1.9 collective-permute-start.14
  148.9 4.3 %collective-permute-done.13 = bf16[2,256,256]{2,1,0:T(8,128)(2,1)S(1)} collective-permute-done((bf16[2,256,256]{2,1,0:T(8,128)(2,1)S(1)}, bf16[2,256,256]{2,1,0:T(8,128)(2,1)S(1)}, u32[]{:S(2)}, u32[]{:S(2)}) %collective-permute-start.13) | collective-permute-done | bytes 262176 | tf_op jit(solution)/shard_map/kv_ring/ppermute | solution.py:219
  153.9 2.1 %collective-permute-start.16 = (bf16[2,256,256]{2,1,0:T(8,128)(2,1)S(1)}, bf16[2,256,256]{2,1,0:T(8,128)(2,1)S(1)}, u32[]{:S(2)}, u32[]{:S(2)}) collective-permute-start(bf16[2,256,256]{2,1,0:T(8,128)(2,1)S(1)} %collective-permute-done.14), channel_id=1, source_target_pairs={{4,0},{8,4},{12,8},{0,12},{5,1},{9,5},{13,9},{1,13},{6,2},{10,6},{... | collective-permute-start | bytes 786440 | tf_op jit(solution)/shard_map/kv_ring/ppermute | solution.py:220
  156.1 3.3 %collective-permute-done.15 = bf16[2,256,256]{2,1,0:T(8,128)(2,1)S(1)} collective-permute-done((bf16[2,256,256]{2,1,0:T(8,128)(2,1)S(1)}, bf16[2,256,256]{2,1,0:T(8,128)(2,1)S(1)}, u32[]{:S(2)}, u32[]{:S(2)}) %collective-permute-start.15) | collective-permute-done | bytes 262176 | tf_op jit(solution)/shard_map/kv_ring/ppermute | solution.py:219
  164.7 4.4 %collective-permute-start.21 = (bf16[128,256]{0,1:T(8,128)(2,1)S(1)}, bf16[128,256]{0,1:T(8,128)(2,1)S(1)}, u32[]{:S(2)}, u32[]{:S(2)}) collective-permute-start(bf16[128,256]{0,1:T(8,128)(2,1)S(1)} %bitcast.313), channel_id=1, source_target_pairs={{0,3},{1,0},{2,1},{3,2},{4,7},{5,4},{6,5},{7,6},{8,11},{9,8},{10,9... | collective-permute-start | bytes 196616 | tf_op jit(solution)/shard_map/out_projection/ppermute | solution.py:249
  171.9 5.7 %collective-permute-done.17 = bf16[128,256]{0,1:T(8,128)(2,1)S(1)} collective-permute-done((bf16[128,256]{0,1:T(8,128)(2,1)S(1)}, bf16[128,256]{0,1:T(8,128)(2,1)S(1)}, u32[]{:S(2)}, u32[]{:S(2)}) %collective-permute-start.17) | collective-permute-done | bytes 65568 | tf_op jit(solution)/shard_map/out_projection/ppermute | solution.py:249
  183.6 2.4 %collective-permute-start.26 = (bf16[8,256]{1,0:T(8,128)(2,1)S(1)}, bf16[8,256]{1,0:T(8,128)(2,1)S(1)}, u32[]{:S(2)}, u32[]{:S(2)}) collective-permute-start(bf16[8,256]{1,0:T(8,128)(2,1)S(1)} %get-tuple-element.59), channel_id=1, source_target_pairs={{0,3},{1,0},{2,1},{3,2},{4,7},{5,4},{6,5},{7,6},{8,11},{9,8},{10,9... | collective-permute-start | bytes 12296 | tf_op jit(solution)/shard_map/sides_gather/ppermute | solution.py:135
  186.0 1.6 collective-permute-done.24
  188.2 1.8 collective-permute-start.28
  190.0 1.4 collective-permute-start.29
  (126 shorter events, 37.2 us)
Async XLA Ops:
  0.6 136.1 %copy-start = (bf16[1536,768]{1,0:T(8,128)(2,1)S(1)}, bf16[1536,768]{1,0:T(8,128)(2,1)}, u32[]{:S(2)}) copy-start(bf16[1536,768]{1,0:T(8,128)(2,1)} %param.14) | copy-start | bytes 7077892
  4.1 8.7 %collective-permute-start = (bf16[128,384]{1,0:T(8,128)(2,1)S(1)}, bf16[128,384]{1,0:T(8,128)(2,1)S(1)}, u32[]{:S(2)}, u32[]{:S(2)}) collective-permute-start(bf16[128,384]{1,0:T(8,128)(2,1)S(1)} %bitcast.307), channel_id=1, source_target_pairs={{0,1},{1,2},{2,3},{3,0},{4,5},{5,6},{6,7},{7,4},{8,9},{9,10},{10,1... | collective-permute-start | bytes 294920 | tf_op jit(solution)/shard_map/ppermute | solution.py:65
  7.2 9.2 %collective-permute-start.1 = (bf16[128,384]{1,0:T(8,128)(2,1)S(1)}, bf16[128,384]{1,0:T(8,128)(2,1)S(1)}, u32[]{:S(2)}, u32[]{:S(2)}) collective-permute-start(bf16[128,384]{1,0:T(8,128)(2,1)S(1)} %bitcast.306), channel_id=1, source_target_pairs={{0,2},{1,3},{2,0},{3,1},{4,6},{5,7},{6,4},{7,5},{8,10},{9,11},{10,... | collective-permute-start | bytes 294920 | tf_op jit(solution)/shard_map/ppermute | solution.py:65
  9.9 6.7 %collective-permute-start.2 = (bf16[128,384]{1,0:T(8,128)(2,1)S(1)}, bf16[128,384]{1,0:T(8,128)(2,1)S(1)}, u32[]{:S(2)}, u32[]{:S(2)}) collective-permute-start(bf16[128,384]{1,0:T(8,128)(2,1)S(1)} %bitcast.305), channel_id=1, source_target_pairs={{0,3},{1,0},{2,1},{3,2},{4,7},{5,4},{6,5},{7,6},{8,11},{9,8},{10,9... | collective-permute-start | bytes 294920 | tf_op jit(solution)/shard_map/ppermute | solution.py:65
  16.6 8.5 %collective-permute-start.3 = (bf16[8,384]{1,0:T(8,128)(2,1)S(1)}, bf16[8,384]{1,0:T(8,128)(2,1)S(1)}, u32[]{:S(2)}, u32[]{:S(2)}) collective-permute-start(bf16[8,384]{1,0:T(8,128)(2,1)S(1)} %get-tuple-element.27), channel_id=1, source_target_pairs={{0,4},{4,8},{8,12},{1,5},{5,9},{9,13},{2,6},{6,10},{10,14},{3,7},{... | collective-permute-start | bytes 18440 | tf_op jit(solution)/shard_map/ppermute | solution.py:25
  18.3 4.8 %collective-permute-start.4 = (bf16[8,384]{1,0:T(8,128)(2,1)S(1)}, bf16[8,384]{1,0:T(8,128)(2,1)S(1)}, u32[]{:S(2)}, u32[]{:S(2)}) collective-permute-start(bf16[8,384]{1,0:T(8,128)(2,1)S(1)} %get-tuple-element.28), channel_id=1, source_target_pairs={{4,0},{8,4},{12,8},{5,1},{9,5},{13,9},{6,2},{10,6},{14,10},{7,3},{... | collective-permute-start | bytes 18440 | tf_op jit(solution)/shard_map/ppermute | solution.py:26
  27.3 36.8 %copy-start.7 = (f32[1536]{0:T(1024)S(1)}, f32[1536]{0:T(1024)}, u32[]{:S(2)}) copy-start(f32[1536]{0:T(1024)} %param.13) | copy-start | bytes 18436
  29.9 13.0 %collective-permute-start.5 = (bf16[128,1536]{1,0:T(8,128)(2,1)}, bf16[128,1536]{1,0:T(8,128)(2,1)}, u32[]{:S(2)}, u32[]{:S(2)}) collective-permute-start(bf16[128,1536]{1,0:T(8,128)(2,1)} %get-tuple-element.22), channel_id=1, source_target_pairs={{0,1},{1,2},{2,3},{3,0},{4,5},{5,6},{6,7},{7,4},{8,9},{9,10},{10,1... | collective-permute-start | bytes 1179656 | tf_op jit(solution)/shard_map/conv_reduce/ppermute | solution.py:51
  32.3 29.8 %collective-permute-start.6 = (bf16[128,1536]{1,0:T(8,128)(2,1)}, bf16[128,1536]{1,0:T(8,128)(2,1)}, u32[]{:S(2)}, u32[]{:S(2)}) collective-permute-start(bf16[128,1536]{1,0:T(8,128)(2,1)} %get-tuple-element.24), channel_id=1, source_target_pairs={{0,2},{1,3},{2,0},{3,1},{4,6},{5,7},{6,4},{7,5},{8,10},{9,11},{10,... | collective-permute-start | bytes 1179656 | tf_op jit(solution)/shard_map/conv_reduce/ppermute | solution.py:51
  34.0 28.2 %collective-permute-start.7 = (bf16[128,1536]{1,0:T(8,128)(2,1)}, bf16[128,1536]{1,0:T(8,128)(2,1)}, u32[]{:S(2)}, u32[]{:S(2)}) collective-permute-start(bf16[128,1536]{1,0:T(8,128)(2,1)} %get-tuple-element.23), channel_id=1, source_target_pairs={{0,3},{1,0},{2,1},{3,2},{4,7},{5,4},{6,5},{7,6},{8,11},{9,8},{10,9... | collective-permute-start | bytes 1179656 | tf_op jit(solution)/shard_map/conv_reduce/ppermute | solution.py:51
  35.5 53.4 %collective-permute-start.18 = (bf16[256,768]{1,0:T(8,128)(2,1)}, bf16[256,768]{1,0:T(8,128)(2,1)S(1)}, u32[]{:S(2)}, u32[]{:S(2)}) collective-permute-start(bf16[256,768]{1,0:T(8,128)(2,1)} %constant_dynamic-slice_fusion), channel_id=1, source_target_pairs={{0,1},{1,2},{2,3},{3,0},{4,5},{5,6},{6,7},{7,4},{8,9},{9,10},{10,1... | collective-permute-start | bytes 1179656 | tf_op jit(solution)/shard_map/out_projection/ppermute | solution.py:239
  36.8 60.4 %collective-permute-start.20 = (bf16[256,768]{1,0:T(8,128)(2,1)}, bf16[256,768]{1,0:T(8,128)(2,1)}, u32[]{:S(2)}, u32[]{:S(2)}) collective-permute-start(bf16[256,768]{1,0:T(8,128)(2,1)} %constant_dynamic-slice_fusion), channel_id=1, source_target_pairs={{0,2},{1,3},{2,0},{3,1},{4,6},{5,7},{6,4},{7,5},{8,10},{9,11},{10,... | collective-permute-start | bytes 1179656 | tf_op jit(solution)/shard_map/out_projection/ppermute | solution.py:239
  42.9 54.2 %collective-permute-start.22 = (bf16[256,768]{1,0:T(8,128)(2,1)}, bf16[256,768]{1,0:T(8,128)(2,1)}, u32[]{:S(2)}, u32[]{:S(2)}) collective-permute-start(bf16[256,768]{1,0:T(8,128)(2,1)} %constant_dynamic-slice_fusion), channel_id=1, source_target_pairs={{0,3},{1,0},{2,1},{3,2},{4,7},{5,4},{6,5},{7,6},{8,11},{9,8},{10,9... | collective-permute-start | bytes 1179656 | tf_op jit(solution)/shard_map/out_projection/ppermute | solution.py:239
  64.2 45.8 %collective-permute-start.10 = (bf16[128,1536]{1,0:T(8,128)(2,1)S(1)}, bf16[128,1536]{1,0:T(8,128)(2,1)}, u32[]{:S(2)}, u32[]{:S(2)}) collective-permute-start(bf16[128,1536]{1,0:T(8,128)(2,1)S(1)} %fusion.73), channel_id=1, source_target_pairs={{0,3},{1,0},{2,1},{3,2},{4,7},{5,4},{6,5},{7,6},{8,11},{9,8},{10,9... | collective-permute-start | bytes 1179656 | tf_op jit(solution)/shard_map/attn_in_gather/ppermute | solution.py:123
  70.8 39.2 %collective-permute-start.8 = (bf16[128,1536]{1,0:T(8,128)(2,1)S(1)}, bf16[128,1536]{1,0:T(8,128)(2,1)}, u32[]{:S(2)}, u32[]{:S(2)}) collective-permute-start(bf16[128,1536]{1,0:T(8,128)(2,1)S(1)} %fusion.73), channel_id=1, source_target_pairs={{0,1},{1,2},{2,3},{3,0},{4,5},{5,6},{6,7},{7,4},{8,9},{9,10},{10,1... | collective-permute-start | bytes 1179656 | tf_op jit(solution)/shard_map/attn_in_gather/ppermute | solution.py:123
  88.9 47.9 %collective-permute-start.9 = (bf16[128,1536]{1,0:T(8,128)(2,1)S(1)}, bf16[128,1536]{1,0:T(8,128)(2,1)}, u32[]{:S(2)}, u32[]{:S(2)}) collective-permute-start(bf16[128,1536]{1,0:T(8,128)(2,1)S(1)} %fusion.73), channel_id=1, source_target_pairs={{0,2},{1,3},{2,0},{3,1},{4,6},{5,7},{6,4},{7,5},{8,10},{9,11},{10,... | collective-permute-start | bytes 1179656 | tf_op jit(solution)/shard_map/attn_in_gather/ppermute | solution.py:123
  98.4 72.9 %collective-permute-start.23 = (bf16[3,256,768]{2,1,0:T(8,128)(2,1)S(1)}, bf16[3,256,768]{2,1,0:T(8,128)(2,1)S(1)}, u32[]{:S(2)}, u32[]{:S(2)}) collective-permute-start(bf16[3,256,768]{2,1,0:T(8,128)(2,1)S(1)} %pad_maximum_fusion), channel_id=1, source_target_pairs={{0,4},{4,0},{8,12},{12,8},{1,5},{5,1},{9,13},{13,9},{2,6},{6,2},{1... | collective-permute-start | bytes 3538952 | tf_op jit(solution)/shard_map/out_projection/ppermute | solution.py:243
  139.5 6.9 %collective-permute-start.11 = (bf16[2,256,256]{2,1,0:T(8,128)(2,1)S(1)}, bf16[2,256,256]{2,1,0:T(8,128)(2,1)S(1)}, u32[]{:S(2)}, u32[]{:S(2)}) collective-permute-start(bf16[2,256,256]{2,1,0:T(8,128)(2,1)S(1)} %get-tuple-element.25), channel_id=1, source_target_pairs={{0,4},{4,8},{8,12},{12,0},{1,5},{5,9},{9,13},{13,1},{2,6},{6,10},{... | collective-permute-start | bytes 786440 | tf_op jit(solution)/shard_map/kv_ring/ppermute | solution.py:219
  140.0 6.7 %collective-permute-start.12 = (bf16[2,256,256]{2,1,0:T(8,128)(2,1)S(1)}, bf16[2,256,256]{2,1,0:T(8,128)(2,1)S(1)}, u32[]{:S(2)}, u32[]{:S(2)}) collective-permute-start(bf16[2,256,256]{2,1,0:T(8,128)(2,1)S(1)} %get-tuple-element.26), channel_id=1, source_target_pairs={{4,0},{8,4},{12,8},{0,12},{5,1},{9,5},{13,9},{1,13},{6,2},{10,6},{... | collective-permute-start | bytes 786440 | tf_op jit(solution)/shard_map/kv_ring/ppermute | solution.py:220
  146.4 6.8 %collective-permute-start.13 = (bf16[2,256,256]{2,1,0:T(8,128)(2,1)S(1)}, bf16[2,256,256]{2,1,0:T(8,128)(2,1)S(1)}, u32[]{:S(2)}, u32[]{:S(2)}) collective-permute-start(bf16[2,256,256]{2,1,0:T(8,128)(2,1)S(1)} %collective-permute-done.11), channel_id=1, source_target_pairs={{0,4},{4,8},{8,12},{12,0},{1,5},{5,9},{9,13},{13,1},{2,6},{6,10},{... | collective-permute-start | bytes 786440 | tf_op jit(solution)/shard_map/kv_ring/ppermute | solution.py:219
  146.8 6.8 %collective-permute-start.14 = (bf16[2,256,256]{2,1,0:T(8,128)(2,1)S(1)}, bf16[2,256,256]{2,1,0:T(8,128)(2,1)S(1)}, u32[]{:S(2)}, u32[]{:S(2)}) collective-permute-start(bf16[2,256,256]{2,1,0:T(8,128)(2,1)S(1)} %collective-permute-done.12), channel_id=1, source_target_pairs={{4,0},{8,4},{12,8},{0,12},{5,1},{9,5},{13,9},{1,13},{6,2},{10,6},{... | collective-permute-start | bytes 786440 | tf_op jit(solution)/shard_map/kv_ring/ppermute | solution.py:220
  153.2 6.2 %collective-permute-start.15 = (bf16[2,256,256]{2,1,0:T(8,128)(2,1)S(1)}, bf16[2,256,256]{2,1,0:T(8,128)(2,1)S(1)}, u32[]{:S(2)}, u32[]{:S(2)}) collective-permute-start(bf16[2,256,256]{2,1,0:T(8,128)(2,1)S(1)} %collective-permute-done.13), channel_id=1, source_target_pairs={{0,4},{4,8},{8,12},{12,0},{1,5},{5,9},{9,13},{13,1},{2,6},{6,10},{... | collective-permute-start | bytes 786440 | tf_op jit(solution)/shard_map/kv_ring/ppermute | solution.py:219
  153.9 6.5 %collective-permute-start.16 = (bf16[2,256,256]{2,1,0:T(8,128)(2,1)S(1)}, bf16[2,256,256]{2,1,0:T(8,128)(2,1)S(1)}, u32[]{:S(2)}, u32[]{:S(2)}) collective-permute-start(bf16[2,256,256]{2,1,0:T(8,128)(2,1)S(1)} %collective-permute-done.14), channel_id=1, source_target_pairs={{4,0},{8,4},{12,8},{0,12},{5,1},{9,5},{13,9},{1,13},{6,2},{10,6},{... | collective-permute-start | bytes 786440 | tf_op jit(solution)/shard_map/kv_ring/ppermute | solution.py:220
  164.7 6.9 %collective-permute-start.21 = (bf16[128,256]{0,1:T(8,128)(2,1)S(1)}, bf16[128,256]{0,1:T(8,128)(2,1)S(1)}, u32[]{:S(2)}, u32[]{:S(2)}) collective-permute-start(bf16[128,256]{0,1:T(8,128)(2,1)S(1)} %bitcast.313), channel_id=1, source_target_pairs={{0,3},{1,0},{2,1},{3,2},{4,7},{5,4},{6,5},{7,6},{8,11},{9,8},{10,9... | collective-permute-start | bytes 196616 | tf_op jit(solution)/shard_map/out_projection/ppermute | solution.py:249
  170.6 6.9 %collective-permute-start.17 = (bf16[128,256]{0,1:T(8,128)(2,1)S(1)}, bf16[128,256]{0,1:T(8,128)(2,1)S(1)}, u32[]{:S(2)}, u32[]{:S(2)}) collective-permute-start(bf16[128,256]{0,1:T(8,128)(2,1)S(1)} %bitcast.312), channel_id=1, source_target_pairs={{0,1},{1,2},{2,3},{3,0},{4,5},{5,6},{6,7},{7,4},{8,9},{9,10},{10,1... | collective-permute-start | bytes 196616 | tf_op jit(solution)/shard_map/out_projection/ppermute | solution.py:249
  170.7 8.7 %collective-permute-start.19 = (bf16[128,256]{0,1:T(8,128)(2,1)S(1)}, bf16[128,256]{0,1:T(8,128)(2,1)S(1)}, u32[]{:S(2)}, u32[]{:S(2)}) collective-permute-start(bf16[128,256]{0,1:T(8,128)(2,1)S(1)} %bitcast.311), channel_id=1, source_target_pairs={{0,2},{1,3},{2,0},{3,1},{4,6},{5,7},{6,4},{7,5},{8,10},{9,11},{10,... | collective-permute-start | bytes 196616 | tf_op jit(solution)/shard_map/out_projection/ppermute | solution.py:249
  182.2 5.4 %collective-permute-start.24 = (bf16[8,256]{1,0:T(8,128)(2,1)S(1)}, bf16[8,256]{1,0:T(8,128)(2,1)S(1)}, u32[]{:S(2)}, u32[]{:S(2)}) collective-permute-start(bf16[8,256]{1,0:T(8,128)(2,1)S(1)} %get-tuple-element.59), channel_id=1, source_target_pairs={{0,1},{1,2},{2,3},{3,0},{4,5},{5,6},{6,7},{7,4},{8,9},{9,10},{10,1... | collective-permute-start | bytes 12296 | tf_op jit(solution)/shard_map/sides_gather/ppermute | solution.py:135
  182.2 5.4 %collective-permute-start.25 = (bf16[8,256]{1,0:T(8,128)(2,1)S(1)}, bf16[8,256]{1,0:T(8,128)(2,1)S(1)}, u32[]{:S(2)}, u32[]{:S(2)}) collective-permute-start(bf16[8,256]{1,0:T(8,128)(2,1)S(1)} %get-tuple-element.59), channel_id=1, source_target_pairs={{0,2},{1,3},{2,0},{3,1},{4,6},{5,7},{6,4},{7,5},{8,10},{9,11},{10,... | collective-permute-start | bytes 12296 | tf_op jit(solution)/shard_map/sides_gather/ppermute | solution.py:135
  183.6 4.5 %collective-permute-start.26 = (bf16[8,256]{1,0:T(8,128)(2,1)S(1)}, bf16[8,256]{1,0:T(8,128)(2,1)S(1)}, u32[]{:S(2)}, u32[]{:S(2)}) collective-permute-start(bf16[8,256]{1,0:T(8,128)(2,1)S(1)} %get-tuple-element.59), channel_id=1, source_target_pairs={{0,3},{1,0},{2,1},{3,2},{4,7},{5,4},{6,5},{7,6},{8,11},{9,8},{10,9... | collective-permute-start | bytes 12296 | tf_op jit(solution)/shard_map/sides_gather/ppermute | solution.py:135
  188.2 3.3 %collective-permute-start.27 = (bf16[32,256]{1,0:T(8,128)(2,1)S(1)}, bf16[32,256]{1,0:T(8,128)(2,1)S(1)}, u32[]{:S(2)}, u32[]{:S(2)}) collective-permute-start(bf16[32,256]{1,0:T(8,128)(2,1)S(1)} %bitcast.308), channel_id=1, source_target_pairs={{0,4},{4,8},{8,12},{12,0},{1,5},{5,9},{9,13},{13,1},{2,6},{6,10},{... | collective-permute-start | bytes 49160 | tf_op jit(solution)/shard_map/sides_gather/ppermute | solution.py:135
  188.2 3.8 %collective-permute-start.28 = (bf16[32,256]{1,0:T(8,128)(2,1)S(1)}, bf16[32,256]{1,0:T(8,128)(2,1)S(1)}, u32[]{:S(2)}, u32[]{:S(2)}) collective-permute-start(bf16[32,256]{1,0:T(8,128)(2,1)S(1)} %bitcast.309), channel_id=1, source_target_pairs={{0,8},{4,12},{8,0},{12,4},{1,9},{5,13},{9,1},{13,5},{2,10},{6,14},... | collective-permute-start | bytes 49160 | tf_op jit(solution)/shard_map/sides_gather/ppermute | solution.py:135
  190.0 2.9 %collective-permute-start.29 = (bf16[32,256]{1,0:T(8,128)(2,1)S(1)}, bf16[32,256]{1,0:T(8,128)(2,1)S(1)}, u32[]{:S(2)}, u32[]{:S(2)}) collective-permute-start(bf16[32,256]{1,0:T(8,128)(2,1)S(1)} %bitcast.310), channel_id=1, source_target_pairs={{0,12},{4,0},{8,4},{12,8},{1,13},{5,1},{9,5},{13,9},{2,14},{6,2},{... | collective-permute-start | bytes 49160 | tf_op jit(solution)/shard_map/sides_gather/ppermute | solution.py:135
  (9 other events, 91.3 us)

commit v14 on v13

--- a/solution.py
+++ b/solution.py
@@ -65,6 +65,24 @@
         incoming = lax.ppermute(outgoing, axis, [(i, (i + shift) % n) for i in range(n)])
         slots = lax.dynamic_update_index_in_dim(slots, incoming, (me + n - shift) % n, 0)
     return slots.reshape(n * value.shape[0], width)
+
+
+def line_flows(value, axis):
+    n = lax.axis_size(axis)
+    me = lax.axis_index(axis)
+    right = [(i, i + 1) for i in range(n - 1)]
+    left = [(i + 1, i) for i in range(n - 1)]
+    flow_r, flow_l = value, value
+    from_left, from_right = [], []
+    for step in range(1, n):
+        flow_r = lax.ppermute(flow_r, axis, right)
+        flow_l = lax.ppermute(flow_l, axis, left)
+        from_left.append(flow_r)
+        from_right.append(flow_l)
+    return [
+        jnp.where(me >= shift, from_left[shift - 1], from_right[n - shift - 1])
+        for shift in range(1, n)
+    ]
 
 
 def line_all_gather(value, axis):
@@ -178,8 +196,6 @@
     grouped = projected.reshape(local_rows, head_count, 2 * KEY_SIZE + VALUE_SIZE).transpose(1, 0, 2)
     queries = grouped[:, :, :KEY_SIZE]
     kv = grouped[:, :, KEY_SIZE:]
-    if rotated and seq_count % 2 == 0:
-        late_w_out = w_out
     scale = 1.0 / math.sqrt(KEY_SIZE)
 
     def attend(state, kv_block):
@@ -226,23 +242,18 @@
     attended = (weighted / running_sum[:, :, None]).astype(jnp.bfloat16)
     attended = attended.transpose(1, 0, 2).reshape(local_rows, head_count * VALUE_SIZE)
     with jax.named_scope("out_projection"):
+        late_w_out, unused = lax.optimization_barrier((w_out, kv))
         if rotated and seq_count % 2 == 0:
             me = lax.axis_index("pair")
             core = lax.axis_index("seq") % 2
             half = w_out.shape[1] // 2
             mine_w = lax.dynamic_slice_in_dim(late_w_out, core * half, half, 1)
             other_w = lax.dynamic_slice_in_dim(late_w_out, (1 - core) * half, half, 1)
-            pieces = attended.reshape(pair_count, row_count, attended.shape[1])
-            fetched = []
-            for shift in range(1, pair_count):
-                fetched.append(
-                    lax.ppermute(
-                        mine_w, "pair", [(i, (i + shift) % pair_count) for i in range(pair_count)]
-                    )
-                )
+            fetched = line_flows(mine_w, "pair")
             swapped_w = lax.ppermute(
                 jnp.stack(fetched), "seq", [(i, i ^ 1) for i in range(seq_count)]
             )
+            pieces = attended.reshape(pair_count, row_count, attended.shape[1])
             mixed_mine = jnp.dot(pieces[0], mine_w, preferred_element_type=jnp.float32)
             mixed_other = jnp.dot(pieces[0], other_w, preferred_element_type=jnp.float32)
             for shift in range(1, pair_count):
@@ -263,7 +274,6 @@
                 jnp.concatenate([mixed_other, mixed_mine], 1),
             )
         else:
-            late_w_out, unused = lax.optimization_barrier((w_out, kv))
             full_w_out = gather_weight_rows(late_w_out, "pair", "seq")
             own_heads = rows_to_heads(attended, "pair")
             mixed = jnp.dot(own_heads, full_w_out, preferred_element_type=jnp.float32)

time: 195 us -> 174 us (0.89)
  starting transfers between devices: 81.5 us -> 70.1 us
  waiting for transfers between devices: 78 us -> 73.6 us
    ppermute x3, starting transfers between devices: 32.9 us -> 10.4 us  [rotated_all_gather(): lax.ppermute(value, axis, [(i, (i + shift) % n) for i in range(n)])]
    ppermute x3 -> x6, starting transfers between devices: 5.04 us -> 25.5 us  [the longest x3 21.6 us: line_flows(): flow_r = lax.ppermute(flow_r, axis, right)]
    ppermute x1, starting transfers between devices: 10.4 us -> 0.07 us  [shards(): lax.ppermute(jnp.stack(fetched), 'seq', [(i, i ^ 1) for i in range(seq_co...]
    ppermute x3, waiting for transfers between devices: 12 us -> 6.7 us  [shards(): next_going = lax.ppermute(going, 'seq', forward)]
    ppermute x3, waiting for transfers between devices: 0.73 us -> 5.2 us  [shards(): next_coming = lax.ppermute(coming, 'seq', backward)]
    ppermute x3, starting transfers between devices: 4.75 us -> 6.86 us  [direct_reduce_scatter(): lax.ppermute(outgoing, axis, [(i, (i + shift) % n) for i in range(n)])]
  transfers between devices with their start and end apart: 30 -> 33, of which waited for: 19 -> 19; matrix products, arithmetic and copies ran while one was open for 11% -> 14% of each run, Pallas kernels for 0% -> 0%
where the time goes in v14:
time: 174 us
  waiting for transfers between devices  73.6 us (42%)
  starting transfers between devices  70.1 us (40%)
  matrix products  18.6 us (11%)
  other arithmetic  7.3 us (4%)
  local copies, waits for them, and re-layouts  2.86 us (2%)
    ppermute x3, waiting for transfers between devices, rotated_all_gather(): lax.ppermute(value, axis, [(i, (i + shift) % n) for i in range(n)])  26.8 us
    ppermute x3, starting transfers between devices, line_flows(): flow_r = lax.ppermute(flow_r, axis, right)  21.6 us
    ppermute x3, waiting for transfers between devices, direct_reduce_scatter(): lax.ppermute(outgoing, axis, [(i, (i + shift) % n) for i in range(n)])  20 us
    ppermute x3, starting transfers between devices, rotated_all_gather(): lax.ppermute(value, axis, [(i, (i + shift) % n) for i in range(n)])  10.4 us
    ppermute x6, starting transfers between devices, direct_all_gather(): lax.ppermute(value, axis, [(i, (i + shift) % n) for i in range(n)])  7.08 us
    ppermute x3, starting transfers between devices, direct_reduce_scatter(): lax.ppermute(outgoing, axis, [(i, (i + shift) % n) for i in range(n)])  6.86 us
    ppermute x3, waiting for transfers between devices, shards(): next_going = lax.ppermute(going, 'seq', forward)  6.7 us
    dot_general x5, matrix products, conv_rows(): jnp.dot(shifted, conv_weight[offset], preferred_element_type=jnp.float32)  6.47 us
  transfers between devices with their start and end apart: 33, of which 19 were waited for; matrix products, arithmetic and copies ran while one was open for 14% of the time, Pallas kernels for 0%

profile of v14, /device:TPU:0, one launch (start us, length us, event | category | flops | bytes accessed | tf_op | source)
XLA Modules:
  0.0 173.8 jit_solution(2477490158347014507)
XLA Ops:
  3.2 6.3 %collective-permute-start.18 = (bf16[256,768]{1,0:T(8,128)(2,1)S(1)}, bf16[256,768]{1,0:T(8,128)(2,1)}, u32[]{:S(2)}, u32[]{:S(2)}) collective-permute-start(bf16[256,768]{1,0:T(8,128)(2,1)S(1)} %constant_dynamic-slice_fusion), channel_id=1, source_target_pairs={{0,1},{1,2},{2,3},{4,5},{5,6},{6,7},{8,9},{9,10},{10,11},{12,13},{... | collective-permute-start | bytes 1179656 | tf_op jit(solution)/shard_map/out_projection/ppermute | solution.py:78
  14.2 1.8 %collective-permute-start.1 = (bf16[128,384]{1,0:T(8,128)(2,1)S(1)}, bf16[128,384]{1,0:T(8,128)(2,1)S(1)}, u32[]{:S(2)}, u32[]{:S(2)}) collective-permute-start(bf16[128,384]{1,0:T(8,128)(2,1)S(1)} %bitcast.305), channel_id=1, source_target_pairs={{0,2},{1,3},{2,0},{3,1},{4,6},{5,7},{6,4},{7,5},{8,10},{9,11},{10,... | collective-permute-start | bytes 294920 | tf_op jit(solution)/shard_map/ppermute | solution.py:65
  16.0 3.0 %collective-permute-start.2 = (bf16[128,384]{1,0:T(8,128)(2,1)S(1)}, bf16[128,384]{1,0:T(8,128)(2,1)S(1)}, u32[]{:S(2)}, u32[]{:S(2)}) collective-permute-start(bf16[128,384]{1,0:T(8,128)(2,1)S(1)} %bitcast.304), channel_id=1, source_target_pairs={{0,3},{1,0},{2,1},{3,2},{4,7},{5,4},{6,5},{7,6},{8,11},{9,8},{10,9... | collective-permute-start | bytes 294920 | tf_op jit(solution)/shard_map/ppermute | solution.py:65
  19.0 2.3 %collective-permute-done = bf16[128,384]{1,0:T(8,128)(2,1)S(1)} collective-permute-done((bf16[128,384]{1,0:T(8,128)(2,1)S(1)}, bf16[128,384]{1,0:T(8,128)(2,1)S(1)}, u32[]{:S(2)}, u32[]{:S(2)}) %collective-permute-start) | collective-permute-done | bytes 98336 | tf_op jit(solution)/shard_map/ppermute | solution.py:65
  21.4 2.8 %collective-permute-done.1 = bf16[128,384]{1,0:T(8,128)(2,1)S(1)} collective-permute-done((bf16[128,384]{1,0:T(8,128)(2,1)S(1)}, bf16[128,384]{1,0:T(8,128)(2,1)S(1)}, u32[]{:S(2)}, u32[]{:S(2)}) %collective-permute-start.1) | collective-permute-done | bytes 98336 | tf_op jit(solution)/shard_map/ppermute | solution.py:65
  25.6 1.6 collective-permute-start.4
  27.2 2.4 %fusion.41 = f32[512,1536]{1,0:T(8,128)S(1)} fusion(bf16[512,384]{1,0:T(8,128)(2,1)S(1)} %bitcast.292, bf16[5,384,1536]{2,1,0:T(8,128)(2,1)} %param.12), kind=kOutput, calls=%fused_computation.68 | convolution fusion | flops 603979776 | bytes 4718592 | tf_op jit(solution)/shard_map/conv_reduce/dot_general | solution.py:39
  35.1 3.0 %collective-permute-start.5 = (bf16[128,1536]{1,0:T(8,128)(2,1)S(1)}, bf16[128,1536]{1,0:T(8,128)(2,1)S(1)}, u32[]{:S(2)}, u32[]{:S(2)}) collective-permute-start(bf16[128,1536]{1,0:T(8,128)(2,1)S(1)} %get-tuple-element.22), channel_id=1, source_target_pairs={{0,1},{1,2},{2,3},{3,0},{4,5},{5,6},{6,7},{7,4},{8,9},{9,10},{10,1... | collective-permute-start | bytes 1179656 | tf_op jit(solution)/shard_map/conv_reduce/ppermute | solution.py:51
  38.2 3.4 %collective-permute-start.6 = (bf16[128,1536]{1,0:T(8,128)(2,1)S(1)}, bf16[128,1536]{1,0:T(8,128)(2,1)S(1)}, u32[]{:S(2)}, u32[]{:S(2)}) collective-permute-start(bf16[128,1536]{1,0:T(8,128)(2,1)S(1)} %get-tuple-element.24), channel_id=1, source_target_pairs={{0,2},{1,3},{2,0},{3,1},{4,6},{5,7},{6,4},{7,5},{8,10},{9,11},{10,... | collective-permute-start | bytes 1179656 | tf_op jit(solution)/shard_map/conv_reduce/ppermute | solution.py:51
  43.3 4.6 %collective-permute-start.23 = (bf16[256,768]{1,0:T(8,128)(2,1)}, bf16[256,768]{1,0:T(8,128)(2,1)S(1)}, u32[]{:S(2)}, u32[]{:S(2)}) collective-permute-start(bf16[256,768]{1,0:T(8,128)(2,1)} %collective-permute-done.18), channel_id=1, source_target_pairs={{0,1},{1,2},{2,3},{4,5},{5,6},{6,7},{8,9},{9,10},{10,11},{12,13},{... | collective-permute-start | bytes 1179656 | tf_op jit(solution)/shard_map/out_projection/ppermute | solution.py:78
  47.9 1.6 collective-permute-done.5
  49.5 18.3 %collective-permute-done.6 = bf16[128,1536]{1,0:T(8,128)(2,1)S(1)} collective-permute-done((bf16[128,1536]{1,0:T(8,128)(2,1)S(1)}, bf16[128,1536]{1,0:T(8,128)(2,1)S(1)}, u32[]{:S(2)}, u32[]{:S(2)}) %collective-permute-start.6) | collective-permute-done | bytes 393248 | tf_op jit(solution)/shard_map/conv_reduce/ppermute | solution.py:51
  69.2 8.2 %collective-permute-start.10 = (bf16[128,1536]{1,0:T(8,128)(2,1)}, bf16[128,1536]{1,0:T(8,128)(2,1)}, u32[]{:S(2)}, u32[]{:S(2)}) collective-permute-start(bf16[128,1536]{1,0:T(8,128)(2,1)} %fusion.73), channel_id=1, source_target_pairs={{0,3},{1,0},{2,1},{3,2},{4,7},{5,4},{6,5},{7,6},{8,11},{9,8},{10,9... | collective-permute-start | bytes 1179656 | tf_op jit(solution)/shard_map/attn_in_gather/ppermute | solution.py:141
  78.1 1.5 collective-permute-start.9
  80.9 10.7 %collective-permute-start.25 = (bf16[256,768]{1,0:T(8,128)(2,1)S(1)}, bf16[256,768]{1,0:T(8,128)(2,1)S(1)}, u32[]{:S(2)}, u32[]{:S(2)}) collective-permute-start(bf16[256,768]{1,0:T(8,128)(2,1)S(1)} %collective-permute-done.23), channel_id=1, source_target_pairs={{0,1},{1,2},{2,3},{4,5},{5,6},{6,7},{8,9},{9,10},{10,11},{12,13},{... | collective-permute-start | bytes 1179656 | tf_op jit(solution)/shard_map/out_projection/ppermute | solution.py:78
  91.6 5.3 %collective-permute-done.8 = bf16[128,1536]{1,0:T(8,128)(2,1)} collective-permute-done((bf16[128,1536]{1,0:T(8,128)(2,1)}, bf16[128,1536]{1,0:T(8,128)(2,1)}, u32[]{:S(2)}, u32[]{:S(2)}) %collective-permute-start.8) | collective-permute-done | bytes 393248 | tf_op jit(solution)/shard_map/attn_in_gather/ppermute | solution.py:141
  97.0 21.5 %collective-permute-done.9 = bf16[128,1536]{1,0:T(8,128)(2,1)} collective-permute-done((bf16[128,1536]{1,0:T(8,128)(2,1)}, bf16[128,1536]{1,0:T(8,128)(2,1)}, u32[]{:S(2)}, u32[]{:S(2)}) %collective-permute-start.9) | collective-permute-done | bytes 393248 | tf_op jit(solution)/shard_map/attn_in_gather/ppermute | solution.py:141
  118.5 2.7 %fusion.11 = bf16[512,768]{1,0:T(8,128)(2,1)S(1)} fusion(bf16[1536,768]{1,0:T(8,128)(2,1)S(1)} %copy-done, bf16[128,1536]{1,0:T(8,128)(2,1)} %collective-permute-done.10, bf16[128,1536]{1,0:T(8,128)(2,1)} %collective-permute-done.9, bf16[128,1536]{1,0:T(8,128)(2,1)} %collective-permute-done.8, bf16[128,1536]{1,0:T(8,128)(2,1)} %fusion.73), kind=kOutput, calls=%fused_computation.12 | convolution fusion | flops 1214644224 | bytes 4718592 | tf_op jit(solution)/shard_map/dot_general | solution.py:194
  121.5 1.6 collective-permute-start.12
  123.8 4.5 %collective-permute-done.11 = bf16[2,256,256]{2,1,0:T(8,128)(2,1)S(1)} collective-permute-done((bf16[2,256,256]{2,1,0:T(8,128)(2,1)S(1)}, bf16[2,256,256]{2,1,0:T(8,128)(2,1)S(1)}, u32[]{:S(2)}, u32[]{:S(2)}) %collective-permute-start.11) | collective-permute-done | bytes 262176 | tf_op jit(solution)/shard_map/kv_ring/ppermute | solution.py:235
  128.9 1.9 %collective-permute-start.14 = (bf16[2,256,256]{2,1,0:T(8,128)(2,1)S(1)}, bf16[2,256,256]{2,1,0:T(8,128)(2,1)S(1)}, u32[]{:S(2)}, u32[]{:S(2)}) collective-permute-start(bf16[2,256,256]{2,1,0:T(8,128)(2,1)S(1)} %collective-permute-done.12), channel_id=1, source_target_pairs={{4,0},{8,4},{12,8},{0,12},{5,1},{9,5},{13,9},{1,13},{6,2},{10,6},{... | collective-permute-start | bytes 786440 | tf_op jit(solution)/shard_map/kv_ring/ppermute | solution.py:236
  132.8 1.4 collective-permute-done.13
  134.2 1.7 collective-permute-start.15
  136.9 2.1 %collective-permute-start.16 = (bf16[2,256,256]{2,1,0:T(8,128)(2,1)S(1)}, bf16[2,256,256]{2,1,0:T(8,128)(2,1)S(1)}, u32[]{:S(2)}, u32[]{:S(2)}) collective-permute-start(bf16[2,256,256]{2,1,0:T(8,128)(2,1)S(1)} %collective-permute-done.14), channel_id=1, source_target_pairs={{4,0},{8,4},{12,8},{0,12},{5,1},{9,5},{13,9},{1,13},{6,2},{10,6},{... | collective-permute-start | bytes 786440 | tf_op jit(solution)/shard_map/kv_ring/ppermute | solution.py:236
  140.3 4.0 %collective-permute-done.16 = bf16[2,256,256]{2,1,0:T(8,128)(2,1)S(1)} collective-permute-done((bf16[2,256,256]{2,1,0:T(8,128)(2,1)S(1)}, bf16[2,256,256]{2,1,0:T(8,128)(2,1)S(1)}, u32[]{:S(2)}, u32[]{:S(2)}) %collective-permute-start.16) | collective-permute-done | bytes 262176 | tf_op jit(solution)/shard_map/kv_ring/ppermute | solution.py:236
  149.4 3.7 %collective-permute-start.24 = (bf16[128,256]{0,1:T(8,128)(2,1)S(1)}, bf16[128,256]{0,1:T(8,128)(2,1)S(1)}, u32[]{:S(2)}, u32[]{:S(2)}) collective-permute-start(bf16[128,256]{0,1:T(8,128)(2,1)S(1)} %bitcast.311), channel_id=1, source_target_pairs={{0,3},{1,0},{2,1},{3,2},{4,7},{5,4},{6,5},{7,6},{8,11},{9,8},{10,9... | collective-permute-start | bytes 196616 | tf_op jit(solution)/shard_map/out_projection/ppermute | solution.py:260
  153.1 2.4 %collective-permute-done.17 = bf16[128,256]{0,1:T(8,128)(2,1)S(1)} collective-permute-done((bf16[128,256]{0,1:T(8,128)(2,1)S(1)}, bf16[128,256]{0,1:T(8,128)(2,1)S(1)}, u32[]{:S(2)}, u32[]{:S(2)}) %collective-permute-start.17) | collective-permute-done | bytes 65568 | tf_op jit(solution)/shard_map/out_projection/ppermute | solution.py:260
  157.0 2.3 %collective-permute-done.22 = bf16[128,256]{0,1:T(8,128)(2,1)S(1)} collective-permute-done((bf16[128,256]{0,1:T(8,128)(2,1)S(1)}, bf16[128,256]{0,1:T(8,128)(2,1)S(1)}, u32[]{:S(2)}, u32[]{:S(2)}) %collective-permute-start.22) | collective-permute-done | bytes 65568 | tf_op jit(solution)/shard_map/out_projection/ppermute | solution.py:260
  161.7 2.5 %collective-permute-start.28 = (bf16[8,256]{1,0:T(8,128)(2,1)S(1)}, bf16[8,256]{1,0:T(8,128)(2,1)S(1)}, u32[]{:S(2)}, u32[]{:S(2)}) collective-permute-start(bf16[8,256]{1,0:T(8,128)(2,1)S(1)} %get-tuple-element.59), channel_id=1, source_target_pairs={{0,2},{1,3},{2,0},{3,1},{4,6},{5,7},{6,4},{7,5},{8,10},{9,11},{10,... | collective-permute-start | bytes 12296 | tf_op jit(solution)/shard_map/sides_gather/ppermute | solution.py:153
  165.5 1.6 collective-permute-done.27
  167.8 1.8 %collective-permute-start.31 = (bf16[32,256]{1,0:T(8,128)(2,1)S(1)}, bf16[32,256]{1,0:T(8,128)(2,1)S(1)}, u32[]{:S(2)}, u32[]{:S(2)}) collective-permute-start(bf16[32,256]{1,0:T(8,128)(2,1)S(1)} %bitcast.308), channel_id=1, source_target_pairs={{0,8},{4,12},{8,0},{12,4},{1,9},{5,13},{9,1},{13,5},{2,10},{6,14},... | collective-permute-start | bytes 49160 | tf_op jit(solution)/shard_map/sides_gather/ppermute | solution.py:153
  169.6 1.4 collective-permute-start.32
  (135 shorter events, 38.5 us)
Async XLA Ops:
  1.9 40.1 %collective-permute-start.19 = (bf16[256,768]{1,0:T(8,128)(2,1)S(1)}, bf16[256,768]{1,0:T(8,128)(2,1)}, u32[]{:S(2)}, u32[]{:S(2)}) collective-permute-start(bf16[256,768]{1,0:T(8,128)(2,1)S(1)} %constant_dynamic-slice_fusion), channel_id=1, source_target_pairs={{1,0},{2,1},{3,2},{5,4},{6,5},{7,6},{9,8},{10,9},{11,10},{13,12},{... | collective-permute-start | bytes 1179656 | tf_op jit(solution)/shard_map/out_projection/ppermute | solution.py:79
  3.2 40.1 %collective-permute-start.18 = (bf16[256,768]{1,0:T(8,128)(2,1)S(1)}, bf16[256,768]{1,0:T(8,128)(2,1)}, u32[]{:S(2)}, u32[]{:S(2)}) collective-permute-start(bf16[256,768]{1,0:T(8,128)(2,1)S(1)} %constant_dynamic-slice_fusion), channel_id=1, source_target_pairs={{0,1},{1,2},{2,3},{4,5},{5,6},{6,7},{8,9},{9,10},{10,11},{12,13},{... | collective-permute-start | bytes 1179656 | tf_op jit(solution)/shard_map/out_projection/ppermute | solution.py:78
  12.8 8.6 %collective-permute-start = (bf16[128,384]{1,0:T(8,128)(2,1)S(1)}, bf16[128,384]{1,0:T(8,128)(2,1)S(1)}, u32[]{:S(2)}, u32[]{:S(2)}) collective-permute-start(bf16[128,384]{1,0:T(8,128)(2,1)S(1)} %bitcast.306), channel_id=1, source_target_pairs={{0,1},{1,2},{2,3},{3,0},{4,5},{5,6},{6,7},{7,4},{8,9},{9,10},{10,1... | collective-permute-start | bytes 294920 | tf_op jit(solution)/shard_map/ppermute | solution.py:65
  14.2 10.1 %collective-permute-start.1 = (bf16[128,384]{1,0:T(8,128)(2,1)S(1)}, bf16[128,384]{1,0:T(8,128)(2,1)S(1)}, u32[]{:S(2)}, u32[]{:S(2)}) collective-permute-start(bf16[128,384]{1,0:T(8,128)(2,1)S(1)} %bitcast.305), channel_id=1, source_target_pairs={{0,2},{1,3},{2,0},{3,1},{4,6},{5,7},{6,4},{7,5},{8,10},{9,11},{10,... | collective-permute-start | bytes 294920 | tf_op jit(solution)/shard_map/ppermute | solution.py:65
  16.0 8.2 %collective-permute-start.2 = (bf16[128,384]{1,0:T(8,128)(2,1)S(1)}, bf16[128,384]{1,0:T(8,128)(2,1)S(1)}, u32[]{:S(2)}, u32[]{:S(2)}) collective-permute-start(bf16[128,384]{1,0:T(8,128)(2,1)S(1)} %bitcast.304), channel_id=1, source_target_pairs={{0,3},{1,0},{2,1},{3,2},{4,7},{5,4},{6,5},{7,6},{8,11},{9,8},{10,9... | collective-permute-start | bytes 294920 | tf_op jit(solution)/shard_map/ppermute | solution.py:65
  24.3 8.5 %collective-permute-start.3 = (bf16[8,384]{1,0:T(8,128)(2,1)S(1)}, bf16[8,384]{1,0:T(8,128)(2,1)S(1)}, u32[]{:S(2)}, u32[]{:S(2)}) collective-permute-start(bf16[8,384]{1,0:T(8,128)(2,1)S(1)} %get-tuple-element.27), channel_id=1, source_target_pairs={{0,4},{4,8},{8,12},{1,5},{5,9},{9,13},{2,6},{6,10},{10,14},{3,7},{... | collective-permute-start | bytes 18440 | tf_op jit(solution)/shard_map/ppermute | solution.py:25
  25.6 5.3 %collective-permute-start.4 = (bf16[8,384]{1,0:T(8,128)(2,1)S(1)}, bf16[8,384]{1,0:T(8,128)(2,1)S(1)}, u32[]{:S(2)}, u32[]{:S(2)}) collective-permute-start(bf16[8,384]{1,0:T(8,128)(2,1)S(1)} %get-tuple-element.28), channel_id=1, source_target_pairs={{4,0},{8,4},{12,8},{5,1},{9,5},{13,9},{6,2},{10,6},{14,10},{7,3},{... | collective-permute-start | bytes 18440 | tf_op jit(solution)/shard_map/ppermute | solution.py:26
  35.1 14.4 %collective-permute-start.5 = (bf16[128,1536]{1,0:T(8,128)(2,1)S(1)}, bf16[128,1536]{1,0:T(8,128)(2,1)S(1)}, u32[]{:S(2)}, u32[]{:S(2)}) collective-permute-start(bf16[128,1536]{1,0:T(8,128)(2,1)S(1)} %get-tuple-element.22), channel_id=1, source_target_pairs={{0,1},{1,2},{2,3},{3,0},{4,5},{5,6},{6,7},{7,4},{8,9},{9,10},{10,1... | collective-permute-start | bytes 1179656 | tf_op jit(solution)/shard_map/conv_reduce/ppermute | solution.py:51
  38.2 29.7 %collective-permute-start.6 = (bf16[128,1536]{1,0:T(8,128)(2,1)S(1)}, bf16[128,1536]{1,0:T(8,128)(2,1)S(1)}, u32[]{:S(2)}, u32[]{:S(2)}) collective-permute-start(bf16[128,1536]{1,0:T(8,128)(2,1)S(1)} %get-tuple-element.24), channel_id=1, source_target_pairs={{0,2},{1,3},{2,0},{3,1},{4,6},{5,7},{6,4},{7,5},{8,10},{9,11},{10,... | collective-permute-start | bytes 1179656 | tf_op jit(solution)/shard_map/conv_reduce/ppermute | solution.py:51
  41.5 26.3 %collective-permute-start.7 = (bf16[128,1536]{1,0:T(8,128)(2,1)S(1)}, bf16[128,1536]{1,0:T(8,128)(2,1)S(1)}, u32[]{:S(2)}, u32[]{:S(2)}) collective-permute-start(bf16[128,1536]{1,0:T(8,128)(2,1)S(1)} %get-tuple-element.23), channel_id=1, source_target_pairs={{0,3},{1,0},{2,1},{3,2},{4,7},{5,4},{6,5},{7,6},{8,11},{9,8},{10,9... | collective-permute-start | bytes 1179656 | tf_op jit(solution)/shard_map/conv_reduce/ppermute | solution.py:51
  42.0 37.6 %collective-permute-start.20 = (bf16[256,768]{1,0:T(8,128)(2,1)}, bf16[256,768]{1,0:T(8,128)(2,1)S(1)}, u32[]{:S(2)}, u32[]{:S(2)}) collective-permute-start(bf16[256,768]{1,0:T(8,128)(2,1)} %collective-permute-done.19), channel_id=1, source_target_pairs={{1,0},{2,1},{3,2},{5,4},{6,5},{7,6},{9,8},{10,9},{11,10},{13,12},{... | collective-permute-start | bytes 1179656 | tf_op jit(solution)/shard_map/out_projection/ppermute | solution.py:79
  43.3 37.5 %collective-permute-start.23 = (bf16[256,768]{1,0:T(8,128)(2,1)}, bf16[256,768]{1,0:T(8,128)(2,1)S(1)}, u32[]{:S(2)}, u32[]{:S(2)}) collective-permute-start(bf16[256,768]{1,0:T(8,128)(2,1)} %collective-permute-done.18), channel_id=1, source_target_pairs={{0,1},{1,2},{2,3},{4,5},{5,6},{6,7},{8,9},{9,10},{10,11},{12,13},{... | collective-permute-start | bytes 1179656 | tf_op jit(solution)/shard_map/out_projection/ppermute | solution.py:78
  69.2 22.5 %collective-permute-start.10 = (bf16[128,1536]{1,0:T(8,128)(2,1)}, bf16[128,1536]{1,0:T(8,128)(2,1)}, u32[]{:S(2)}, u32[]{:S(2)}) collective-permute-start(bf16[128,1536]{1,0:T(8,128)(2,1)} %fusion.73), channel_id=1, source_target_pairs={{0,3},{1,0},{2,1},{3,2},{4,7},{5,4},{6,5},{7,6},{8,11},{9,8},{10,9... | collective-permute-start | bytes 1179656 | tf_op jit(solution)/shard_map/attn_in_gather/ppermute | solution.py:141
  77.3 19.6 %collective-permute-start.8 = (bf16[128,1536]{1,0:T(8,128)(2,1)}, bf16[128,1536]{1,0:T(8,128)(2,1)}, u32[]{:S(2)}, u32[]{:S(2)}) collective-permute-start(bf16[128,1536]{1,0:T(8,128)(2,1)} %fusion.73), channel_id=1, source_target_pairs={{0,1},{1,2},{2,3},{3,0},{4,5},{5,6},{6,7},{7,4},{8,9},{9,10},{10,1... | collective-permute-start | bytes 1179656 | tf_op jit(solution)/shard_map/attn_in_gather/ppermute | solution.py:141
  78.1 40.4 %collective-permute-start.9 = (bf16[128,1536]{1,0:T(8,128)(2,1)}, bf16[128,1536]{1,0:T(8,128)(2,1)}, u32[]{:S(2)}, u32[]{:S(2)}) collective-permute-start(bf16[128,1536]{1,0:T(8,128)(2,1)} %fusion.73), channel_id=1, source_target_pairs={{0,2},{1,3},{2,0},{3,1},{4,6},{5,7},{6,4},{7,5},{8,10},{9,11},{10,... | collective-permute-start | bytes 1179656 | tf_op jit(solution)/shard_map/attn_in_gather/ppermute | solution.py:141
  79.6 51.9 %collective-permute-start.21 = (bf16[256,768]{1,0:T(8,128)(2,1)S(1)}, bf16[256,768]{1,0:T(8,128)(2,1)S(1)}, u32[]{:S(2)}, u32[]{:S(2)}) collective-permute-start(bf16[256,768]{1,0:T(8,128)(2,1)S(1)} %collective-permute-done.20), channel_id=1, source_target_pairs={{1,0},{2,1},{3,2},{5,4},{6,5},{7,6},{9,8},{10,9},{11,10},{13,12},{... | collective-permute-start | bytes 1179656 | tf_op jit(solution)/shard_map/out_projection/ppermute | solution.py:79
  80.9 50.7 %collective-permute-start.25 = (bf16[256,768]{1,0:T(8,128)(2,1)S(1)}, bf16[256,768]{1,0:T(8,128)(2,1)S(1)}, u32[]{:S(2)}, u32[]{:S(2)}) collective-permute-start(bf16[256,768]{1,0:T(8,128)(2,1)S(1)} %collective-permute-done.23), channel_id=1, source_target_pairs={{0,1},{1,2},{2,3},{4,5},{5,6},{6,7},{8,9},{9,10},{10,11},{12,13},{... | collective-permute-start | bytes 1179656 | tf_op jit(solution)/shard_map/out_projection/ppermute | solution.py:78
  121.3 6.9 %collective-permute-start.11 = (bf16[2,256,256]{2,1,0:T(8,128)(2,1)S(1)}, bf16[2,256,256]{2,1,0:T(8,128)(2,1)S(1)}, u32[]{:S(2)}, u32[]{:S(2)}) collective-permute-start(bf16[2,256,256]{2,1,0:T(8,128)(2,1)S(1)} %get-tuple-element.25), channel_id=1, source_target_pairs={{0,4},{4,8},{8,12},{12,0},{1,5},{5,9},{9,13},{13,1},{2,6},{6,10},{... | collective-permute-start | bytes 786440 | tf_op jit(solution)/shard_map/kv_ring/ppermute | solution.py:235
  121.5 7.4 %collective-permute-start.12 = (bf16[2,256,256]{2,1,0:T(8,128)(2,1)S(1)}, bf16[2,256,256]{2,1,0:T(8,128)(2,1)S(1)}, u32[]{:S(2)}, u32[]{:S(2)}) collective-permute-start(bf16[2,256,256]{2,1,0:T(8,128)(2,1)S(1)} %get-tuple-element.26), channel_id=1, source_target_pairs={{4,0},{8,4},{12,8},{0,12},{5,1},{9,5},{13,9},{1,13},{6,2},{10,6},{... | collective-permute-start | bytes 786440 | tf_op jit(solution)/shard_map/kv_ring/ppermute | solution.py:236
  128.2 6.0 %collective-permute-start.13 = (bf16[2,256,256]{2,1,0:T(8,128)(2,1)S(1)}, bf16[2,256,256]{2,1,0:T(8,128)(2,1)S(1)}, u32[]{:S(2)}, u32[]{:S(2)}) collective-permute-start(bf16[2,256,256]{2,1,0:T(8,128)(2,1)S(1)} %collective-permute-done.11), channel_id=1, source_target_pairs={{0,4},{4,8},{8,12},{12,0},{1,5},{5,9},{9,13},{13,1},{2,6},{6,10},{... | collective-permute-start | bytes 786440 | tf_op jit(solution)/shard_map/kv_ring/ppermute | solution.py:235
  128.9 7.7 %collective-permute-start.14 = (bf16[2,256,256]{2,1,0:T(8,128)(2,1)S(1)}, bf16[2,256,256]{2,1,0:T(8,128)(2,1)S(1)}, u32[]{:S(2)}, u32[]{:S(2)}) collective-permute-start(bf16[2,256,256]{2,1,0:T(8,128)(2,1)S(1)} %collective-permute-done.12), channel_id=1, source_target_pairs={{4,0},{8,4},{12,8},{0,12},{5,1},{9,5},{13,9},{1,13},{6,2},{10,6},{... | collective-permute-start | bytes 786440 | tf_op jit(solution)/shard_map/kv_ring/ppermute | solution.py:236
  132.7 26.9 %collective-permute-start.26 = (bf16[3,256,768]{2,1,0:T(8,128)(2,1)S(1)}, bf16[3,256,768]{2,1,0:T(8,128)(2,1)S(1)}, u32[]{:S(2)}, u32[]{:S(2)}) collective-permute-start(bf16[3,256,768]{2,1,0:T(8,128)(2,1)S(1)} %pad_maximum_fusion), channel_id=1, source_target_pairs={{0,4},{4,0},{8,12},{12,8},{1,5},{5,1},{9,13},{13,9},{2,6},{6,2},{1... | collective-permute-start | bytes 3538952 | tf_op jit(solution)/shard_map/out_projection/ppermute | solution.py:253
  134.2 5.8 %collective-permute-start.15 = (bf16[2,256,256]{2,1,0:T(8,128)(2,1)S(1)}, bf16[2,256,256]{2,1,0:T(8,128)(2,1)S(1)}, u32[]{:S(2)}, u32[]{:S(2)}) collective-permute-start(bf16[2,256,256]{2,1,0:T(8,128)(2,1)S(1)} %collective-permute-done.13), channel_id=1, source_target_pairs={{0,4},{4,8},{8,12},{12,0},{1,5},{5,9},{9,13},{13,1},{2,6},{6,10},{... | collective-permute-start | bytes 786440 | tf_op jit(solution)/shard_map/kv_ring/ppermute | solution.py:235
  136.9 7.4 %collective-permute-start.16 = (bf16[2,256,256]{2,1,0:T(8,128)(2,1)S(1)}, bf16[2,256,256]{2,1,0:T(8,128)(2,1)S(1)}, u32[]{:S(2)}, u32[]{:S(2)}) collective-permute-start(bf16[2,256,256]{2,1,0:T(8,128)(2,1)S(1)} %collective-permute-done.14), channel_id=1, source_target_pairs={{4,0},{8,4},{12,8},{0,12},{5,1},{9,5},{13,9},{1,13},{6,2},{10,6},{... | collective-permute-start | bytes 786440 | tf_op jit(solution)/shard_map/kv_ring/ppermute | solution.py:236
  148.7 6.8 %collective-permute-start.17 = (bf16[128,256]{0,1:T(8,128)(2,1)S(1)}, bf16[128,256]{0,1:T(8,128)(2,1)S(1)}, u32[]{:S(2)}, u32[]{:S(2)}) collective-permute-start(bf16[128,256]{0,1:T(8,128)(2,1)S(1)} %bitcast.312), channel_id=1, source_target_pairs={{0,1},{1,2},{2,3},{3,0},{4,5},{5,6},{6,7},{7,4},{8,9},{9,10},{10,1... | collective-permute-start | bytes 196616 | tf_op jit(solution)/shard_map/out_projection/ppermute | solution.py:260
  149.4 6.4 %collective-permute-start.24 = (bf16[128,256]{0,1:T(8,128)(2,1)S(1)}, bf16[128,256]{0,1:T(8,128)(2,1)S(1)}, u32[]{:S(2)}, u32[]{:S(2)}) collective-permute-start(bf16[128,256]{0,1:T(8,128)(2,1)S(1)} %bitcast.311), channel_id=1, source_target_pairs={{0,3},{1,0},{2,1},{3,2},{4,7},{5,4},{6,5},{7,6},{8,11},{9,8},{10,9... | collective-permute-start | bytes 196616 | tf_op jit(solution)/shard_map/out_projection/ppermute | solution.py:260
  153.1 6.2 %collective-permute-start.22 = (bf16[128,256]{0,1:T(8,128)(2,1)S(1)}, bf16[128,256]{0,1:T(8,128)(2,1)S(1)}, u32[]{:S(2)}, u32[]{:S(2)}) collective-permute-start(bf16[128,256]{0,1:T(8,128)(2,1)S(1)} %bitcast.310), channel_id=1, source_target_pairs={{0,2},{1,3},{2,0},{3,1},{4,6},{5,7},{6,4},{7,5},{8,10},{9,11},{10,... | collective-permute-start | bytes 196616 | tf_op jit(solution)/shard_map/out_projection/ppermute | solution.py:260
  161.7 5.4 %collective-permute-start.27 = (bf16[8,256]{1,0:T(8,128)(2,1)S(1)}, bf16[8,256]{1,0:T(8,128)(2,1)S(1)}, u32[]{:S(2)}, u32[]{:S(2)}) collective-permute-start(bf16[8,256]{1,0:T(8,128)(2,1)S(1)} %get-tuple-element.59), channel_id=1, source_target_pairs={{0,1},{1,2},{2,3},{3,0},{4,5},{5,6},{6,7},{7,4},{8,9},{9,10},{10,1... | collective-permute-start | bytes 12296 | tf_op jit(solution)/shard_map/sides_gather/ppermute | solution.py:153
  161.7 5.4 %collective-permute-start.28 = (bf16[8,256]{1,0:T(8,128)(2,1)S(1)}, bf16[8,256]{1,0:T(8,128)(2,1)S(1)}, u32[]{:S(2)}, u32[]{:S(2)}) collective-permute-start(bf16[8,256]{1,0:T(8,128)(2,1)S(1)} %get-tuple-element.59), channel_id=1, source_target_pairs={{0,2},{1,3},{2,0},{3,1},{4,6},{5,7},{6,4},{7,5},{8,10},{9,11},{10,... | collective-permute-start | bytes 12296 | tf_op jit(solution)/shard_map/sides_gather/ppermute | solution.py:153
  164.2 3.6 %collective-permute-start.29 = (bf16[8,256]{1,0:T(8,128)(2,1)S(1)}, bf16[8,256]{1,0:T(8,128)(2,1)S(1)}, u32[]{:S(2)}, u32[]{:S(2)}) collective-permute-start(bf16[8,256]{1,0:T(8,128)(2,1)S(1)} %get-tuple-element.59), channel_id=1, source_target_pairs={{0,3},{1,0},{2,1},{3,2},{4,7},{5,4},{6,5},{7,6},{8,11},{9,8},{10,9... | collective-permute-start | bytes 12296 | tf_op jit(solution)/shard_map/sides_gather/ppermute | solution.py:153
  167.8 3.3 %collective-permute-start.30 = (bf16[32,256]{1,0:T(8,128)(2,1)S(1)}, bf16[32,256]{1,0:T(8,128)(2,1)S(1)}, u32[]{:S(2)}, u32[]{:S(2)}) collective-permute-start(bf16[32,256]{1,0:T(8,128)(2,1)S(1)} %bitcast.307), channel_id=1, source_target_pairs={{0,4},{4,8},{8,12},{12,0},{1,5},{5,9},{9,13},{13,1},{2,6},{6,10},{... | collective-permute-start | bytes 49160 | tf_op jit(solution)/shard_map/sides_gather/ppermute | solution.py:153
  167.8 3.8 %collective-permute-start.31 = (bf16[32,256]{1,0:T(8,128)(2,1)S(1)}, bf16[32,256]{1,0:T(8,128)(2,1)S(1)}, u32[]{:S(2)}, u32[]{:S(2)}) collective-permute-start(bf16[32,256]{1,0:T(8,128)(2,1)S(1)} %bitcast.308), channel_id=1, source_target_pairs={{0,8},{4,12},{8,0},{12,4},{1,9},{5,13},{9,1},{13,5},{2,10},{6,14},... | collective-permute-start | bytes 49160 | tf_op jit(solution)/shard_map/sides_gather/ppermute | solution.py:153
  (12 other events, 252.3 us)

commit v15 on v14

--- a/solution.py
+++ b/solution.py
@@ -38,6 +38,26 @@
         shifted = lax.dynamic_slice_in_dim(padded, offset * DILATION, row_total, 0)
         summed = summed + jnp.dot(shifted, conv_weight[offset], preferred_element_type=jnp.float32)
     return summed
+
+
+def line4_reduce_scatter(partial, axis):
+    me = lax.axis_index(axis)
+    rows = partial.shape[0] // 4
+    blocks = partial.reshape(4, rows, partial.shape[1])
+
+    def send(index, pairs):
+        return lax.ppermute(blocks[index].astype(jnp.bfloat16), axis, pairs)
+
+    near_r = send(jnp.clip(me + 1, 0, 3), [(0, 1), (1, 2), (2, 3)])
+    near_l = send(jnp.clip(me - 1, 0, 3), [(1, 0), (2, 1), (3, 2)])
+    far_seed = send(jnp.where(me == 0, 3, 0), [(0, 1), (3, 2)])
+    two_hop = send(jnp.where(me == 0, 2, 1), [(0, 2), (3, 1)])
+    far_sum = (blocks[jnp.where(me == 1, 3, 0)] + far_seed.astype(jnp.float32)).astype(jnp.bfloat16)
+    far = lax.ppermute(far_sum, axis, [(1, 3), (2, 0)])
+    total = blocks[me]
+    for piece in (near_r, near_l, two_hop, far):
+        total = total + piece.astype(jnp.float32)
+    return total
 
 
 def direct_reduce_scatter(partial, axis):
@@ -182,7 +202,11 @@
     swapped = permute_all_to_all(normed, "pair")
     padded = padded_2(swapped, (("seq", 0),), DILATION * (conv_weight.shape[0] - 1) // 2)
     with jax.named_scope("conv_reduce"):
-        summed = direct_reduce_scatter(conv_rows(padded, conv_weight, local_rows), "pair")
+        conv_partial = conv_rows(padded, conv_weight, local_rows)
+        if pair_count == 4:
+            summed = line4_reduce_scatter(conv_partial, "pair")
+        else:
+            summed = direct_reduce_scatter(conv_partial, "pair")
     first_out = (inputs + summed).astype(jnp.bfloat16)
     attn_in = norm_rows(first_out.astype(jnp.float32), gain_attn).astype(jnp.bfloat16)
     with jax.named_scope("attn_in_gather"):

time: 174 us -> 189 us (1.086)
  starting transfers between devices: 70.1 us -> 80.3 us
  local copies, waits for them, and re-layouts: 2.86 us -> 5.91 us
  other arithmetic: 7.3 us -> 10.3 us
  waiting for transfers between devices: 73.6 us -> 71.4 us
    ppermute x3, waiting for transfers between devices: 0.01 us -> 17.2 us  [line_flows(): flow_l = lax.ppermute(flow_l, axis, left)]
    ppermute x3 -> x5, waiting for transfers between devices: 20 us -> 4.88 us  [the longest x1 4.87 us: line4_reduce_scatter(): far = lax.ppermute(far_sum, axis, [(1, 3), (2, 0)])]
    ppermute x3, waiting for transfers between devices: 26.8 us -> 14.9 us  [rotated_all_gather(): lax.ppermute(value, axis, [(i, (i + shift) % n) for i in range(n)])]
    ppermute x3 -> x5, starting transfers between devices: 6.86 us -> 16.6 us  [the longest x4 15.4 us: send(): return lax.ppermute(blocks[index].astype(jnp.bfloat16), axis, pairs)]
    ppermute x3, waiting for transfers between devices: 0.01 us -> 7.99 us  [line_flows(): flow_r = lax.ppermute(flow_r, axis, right)]
    ppermute x3, starting transfers between devices: 1.84 us -> 9.23 us  [shards(): next_going = lax.ppermute(going, 'seq', forward)]
    ppermute x3, starting transfers between devices: 10.4 us -> 3.87 us  [rotated_all_gather(): lax.ppermute(value, axis, [(i, (i + shift) % n) for i in range(n)])]
    ppermute x3, starting transfers between devices: 3.77 us -> 8.55 us  [shards(): lax.ppermute(pieces[pair_count - shift], 'pair', [(i, (i + shift) % pair_...]
  transfers between devices with their start and end apart: 33 -> 35, of which waited for: 19 -> 19; matrix products, arithmetic and copies ran while one was open for 14% -> 15% of each run, Pallas kernels for 0% -> 0%
where the time goes in v15:
time: 189 us; the launch traced here: 187 us
  starting transfers between devices  80.3 us (42%)
  waiting for transfers between devices  71.4 us (38%)
  matrix products  18.3 us (10%)
  other arithmetic  10.3 us (5%)
  local copies, waits for them, and re-layouts  5.91 us (3%)
    ppermute x3, starting transfers between devices, line_flows(): flow_r = lax.ppermute(flow_r, axis, right)  18.9 us
    ppermute x3, waiting for transfers between devices, line_flows(): flow_l = lax.ppermute(flow_l, axis, left)  17.2 us
    ppermute x4, starting transfers between devices, send(): return lax.ppermute(blocks[index].astype(jnp.bfloat16), axis, pairs)  15.4 us
    ppermute x3, waiting for transfers between devices, rotated_all_gather(): lax.ppermute(value, axis, [(i, (i + shift) % n) for i in range(n)])  14.9 us
    ppermute x3, starting transfers between devices, shards(): next_going = lax.ppermute(going, 'seq', forward)  9.23 us
    ppermute x3, starting transfers between devices, shards(): lax.ppermute(pieces[pair_count - shift], 'pair', [(i, (i + shift) % pair_...  8.55 us
    ppermute x3, waiting for transfers between devices, line_flows(): flow_r = lax.ppermute(flow_r, axis, right)  7.99 us
    dot_general x5, matrix products, conv_rows(): jnp.dot(shifted, conv_weight[offset], preferred_element_type=jnp.float32)  6.46 us
  transfers between devices with their start and end apart: 35, of which 19 were waited for; matrix products, arithmetic and copies ran while one was open for 15% of the time, Pallas kernels for 0%

profile of v15, /device:TPU:0, one launch (start us, length us, event | category | flops | bytes accessed | tf_op | source)
XLA Modules:
  0.0 187.5 jit_solution(17914796286738247075)
XLA Ops:
  0.7 1.9 %constant_dynamic-slice_fusion = bf16[256,768]{1,0:T(8,128)(2,1)} fusion(bf16[256,1536]{1,0:T(8,128)(2,1)} %param.15, s32[]{:T(128)S(6)} %select_n.146), kind=kLoop, calls=%fused_computation.208 | loop fusion | bytes 786436 | tf_op jit(solution)/shard_map/out_projection/dynamic_slice | solution.py:274
  3.9 6.3 %collective-permute-start.20 = (bf16[256,768]{1,0:T(8,128)(2,1)}, bf16[256,768]{1,0:T(8,128)(2,1)}, u32[]{:S(2)}, u32[]{:S(2)}) collective-permute-start(bf16[256,768]{1,0:T(8,128)(2,1)} %constant_dynamic-slice_fusion), channel_id=1, source_target_pairs={{0,1},{1,2},{2,3},{4,5},{5,6},{6,7},{8,9},{9,10},{10,11},{12,13},{... | collective-permute-start | bytes 1179656 | tf_op jit(solution)/shard_map/out_projection/ppermute | solution.py:98
  14.9 1.8 collective-permute-start.1
  16.7 3.0 %collective-permute-start.2 = (bf16[128,384]{1,0:T(8,128)(2,1)S(1)}, bf16[128,384]{1,0:T(8,128)(2,1)S(1)}, u32[]{:S(2)}, u32[]{:S(2)}) collective-permute-start(bf16[128,384]{1,0:T(8,128)(2,1)S(1)} %bitcast.313), channel_id=1, source_target_pairs={{0,3},{1,0},{2,1},{3,2},{4,7},{5,4},{6,5},{7,6},{8,11},{9,8},{10,9... | collective-permute-start | bytes 294920 | tf_op jit(solution)/shard_map/ppermute | solution.py:85
  19.8 2.6 %collective-permute-done = bf16[128,384]{1,0:T(8,128)(2,1)S(1)} collective-permute-done((bf16[128,384]{1,0:T(8,128)(2,1)S(1)}, bf16[128,384]{1,0:T(8,128)(2,1)S(1)}, u32[]{:S(2)}, u32[]{:S(2)}) %collective-permute-start) | collective-permute-done | bytes 98336 | tf_op jit(solution)/shard_map/ppermute | solution.py:85
  22.3 2.7 %collective-permute-done.1 = bf16[128,384]{1,0:T(8,128)(2,1)S(1)} collective-permute-done((bf16[128,384]{1,0:T(8,128)(2,1)S(1)}, bf16[128,384]{1,0:T(8,128)(2,1)S(1)}, u32[]{:S(2)}, u32[]{:S(2)}) %collective-permute-start.1) | collective-permute-done | bytes 98336 | tf_op jit(solution)/shard_map/ppermute | solution.py:85
  26.4 1.6 collective-permute-start.4
  28.0 2.4 %fusion.41 = f32[512,1536]{1,0:T(8,128)S(1)} fusion(bf16[512,384]{1,0:T(8,128)(2,1)S(1)} %bitcast.300, bf16[5,384,1536]{2,1,0:T(8,128)(2,1)} %param.12), kind=kOutput, calls=%fused_computation.68 | convolution fusion | flops 603979776 | bytes 4718592 | tf_op jit(solution)/shard_map/conv_reduce/dot_general | solution.py:39
  35.7 1.6 copy-done.1
  38.4 5.9 %collective-permute-start.8 = (bf16[128,1536]{1,0:T(8,128)(2,1)S(1)}, bf16[128,1536]{1,0:T(8,128)(2,1)}, u32[]{:S(2)}, u32[]{:S(2)}) collective-permute-start(bf16[128,1536]{1,0:T(8,128)(2,1)S(1)} %get-tuple-element.23), channel_id=1, source_target_pairs={{0,1},{3,2},{4,5},{7,6},{8,9},{11,10},{12,13},{15,14},{16,17},{19,... | collective-permute-start | bytes 1179656 | tf_op jit(solution)/shard_map/conv_reduce/ppermute | solution.py:49
  44.3 2.0 %collective-permute-start.5 = (bf16[128,1536]{1,0:T(8,128)(2,1)}, bf16[128,1536]{1,0:T(8,128)(2,1)}, u32[]{:S(2)}, u32[]{:S(2)}) collective-permute-start(bf16[128,1536]{1,0:T(8,128)(2,1)} %get-tuple-element.22), channel_id=1, source_target_pairs={{0,1},{1,2},{2,3},{4,5},{5,6},{6,7},{8,9},{9,10},{10,11},{12,13},{... | collective-permute-start | bytes 1179656 | tf_op jit(solution)/shard_map/conv_reduce/ppermute | solution.py:49
  47.7 6.1 %collective-permute-start.7 = (bf16[128,1536]{1,0:T(8,128)(2,1)}, bf16[128,1536]{1,0:T(8,128)(2,1)}, u32[]{:S(2)}, u32[]{:S(2)}) collective-permute-start(bf16[128,1536]{1,0:T(8,128)(2,1)} %get-tuple-element.24), channel_id=1, source_target_pairs={{0,2},{3,1},{4,6},{7,5},{8,10},{11,9},{12,14},{15,13},{16,18},{19,... | collective-permute-start | bytes 1179656 | tf_op jit(solution)/shard_map/conv_reduce/ppermute | solution.py:49
  55.1 4.6 %collective-permute-start.25 = (bf16[256,768]{1,0:T(8,128)(2,1)}, bf16[256,768]{1,0:T(8,128)(2,1)S(1)}, u32[]{:S(2)}, u32[]{:S(2)}) collective-permute-start(bf16[256,768]{1,0:T(8,128)(2,1)} %collective-permute-done.20), channel_id=1, source_target_pairs={{0,1},{1,2},{2,3},{4,5},{5,6},{6,7},{8,9},{9,10},{10,11},{12,13},{... | collective-permute-start | bytes 1179656 | tf_op jit(solution)/shard_map/out_projection/ppermute | solution.py:98
  59.7 2.1 %fusion.75 = bf16[128,1536]{1,0:T(8,128)(2,1)} fusion(bf16[128,1536]{1,0:T(8,128)(2,1)} %collective-permute-done.8, f32[4,128,1536]{2,1,0:T(8,128)} %bitcast.306, s32[]{:T(128)S(6)} %select_n.142), kind=kLoop, calls=%fused_computation.115 | loop fusion | flops 589824 | bytes 1572868 | tf_op jit(solution)/shard_map/conv_reduce/convert_element_type | solution.py:55
  61.7 6.1 %collective-permute-done.22 = bf16[256,768]{1,0:T(8,128)(2,1)S(1)} collective-permute-done((bf16[256,768]{1,0:T(8,128)(2,1)}, bf16[256,768]{1,0:T(8,128)(2,1)S(1)}, u32[]{:S(2)}, u32[]{:S(2)}) %collective-permute-start.22) | collective-permute-done | bytes 393248 | tf_op jit(solution)/shard_map/out_projection/ppermute | solution.py:99
  69.2 8.0 %collective-permute-done.25 = bf16[256,768]{1,0:T(8,128)(2,1)S(1)} collective-permute-done((bf16[256,768]{1,0:T(8,128)(2,1)}, bf16[256,768]{1,0:T(8,128)(2,1)S(1)}, u32[]{:S(2)}, u32[]{:S(2)}) %collective-permute-start.25) | collective-permute-done | bytes 393248 | tf_op jit(solution)/shard_map/out_projection/ppermute | solution.py:98
  78.5 8.0 %collective-permute-start.27 = (bf16[256,768]{1,0:T(8,128)(2,1)S(1)}, bf16[256,768]{1,0:T(8,128)(2,1)S(1)}, u32[]{:S(2)}, u32[]{:S(2)}) collective-permute-start(bf16[256,768]{1,0:T(8,128)(2,1)S(1)} %collective-permute-done.25), channel_id=1, source_target_pairs={{0,1},{1,2},{2,3},{4,5},{5,6},{6,7},{8,9},{9,10},{10,11},{12,13},{... | collective-permute-start | bytes 1179656 | tf_op jit(solution)/shard_map/out_projection/ppermute | solution.py:98
  86.5 4.9 %collective-permute-done.9 = bf16[128,1536]{1,0:T(8,128)(2,1)} collective-permute-done((bf16[128,1536]{1,0:T(8,128)(2,1)}, bf16[128,1536]{1,0:T(8,128)(2,1)}, u32[]{:S(2)}, u32[]{:S(2)}) %collective-permute-start.9) | collective-permute-done | bytes 393248 | tf_op jit(solution)/shard_map/conv_reduce/ppermute | solution.py:56
  91.4 2.0 %fusion.71 = (f32[128]{0:T(128)S(1)}, bf16[128,1536]{1,0:T(8,128)(2,1)S(1)}) fusion(bf16[128,1536]{1,0:T(8,128)(2,1)} %collective-permute-done.9, bf16[128,1536]{1,0:T(8,128)(2,1)} %collective-permute-done.7, bf16[128,1536]{1,0:T(8,128)(2,1)} %collective-permute-done.6, bf16[128,1536]{1,0:T(8,128)(2,1)} %collective-permute-done.5, ...), kind=kLoop, calls=%fused_computation.107 | loop fusion | flops 2752384 | bytes 3146244 | tf_op jit(solution)/shard_map/reduce_sum | solution.py:32
  93.7 3.2 %collective-permute-start.11 = (bf16[128,1536]{1,0:T(8,128)(2,1)S(1)}, bf16[128,1536]{1,0:T(8,128)(2,1)S(1)}, u32[]{:S(2)}, u32[]{:S(2)}) collective-permute-start(bf16[128,1536]{1,0:T(8,128)(2,1)S(1)} %fusion.73), channel_id=1, source_target_pairs={{0,2},{1,3},{2,0},{3,1},{4,6},{5,7},{6,4},{7,5},{8,10},{9,11},{10,... | collective-permute-start | bytes 1179656 | tf_op jit(solution)/shard_map/attn_in_gather/ppermute | solution.py:161
  97.5 11.0 %collective-permute-done.23 = bf16[256,768]{1,0:T(8,128)(2,1)S(1)} collective-permute-done((bf16[256,768]{1,0:T(8,128)(2,1)S(1)}, bf16[256,768]{1,0:T(8,128)(2,1)S(1)}, u32[]{:S(2)}, u32[]{:S(2)}) %collective-permute-start.23) | collective-permute-done | bytes 393248 | tf_op jit(solution)/shard_map/out_projection/ppermute | solution.py:99
  110.1 14.8 %collective-permute-done.11 = bf16[128,1536]{1,0:T(8,128)(2,1)S(1)} collective-permute-done((bf16[128,1536]{1,0:T(8,128)(2,1)S(1)}, bf16[128,1536]{1,0:T(8,128)(2,1)S(1)}, u32[]{:S(2)}, u32[]{:S(2)}) %collective-permute-start.11) | collective-permute-done | bytes 393248 | tf_op jit(solution)/shard_map/attn_in_gather/ppermute | solution.py:161
  129.0 3.4 %collective-permute-done.13 = bf16[2,256,256]{2,1,0:T(8,128)(2,1)S(1)} collective-permute-done((bf16[2,256,256]{2,1,0:T(8,128)(2,1)S(1)}, bf16[2,256,256]{2,1,0:T(8,128)(2,1)S(1)}, u32[]{:S(2)}, u32[]{:S(2)}) %collective-permute-start.13) | collective-permute-done | bytes 262176 | tf_op jit(solution)/shard_map/kv_ring/ppermute | solution.py:259
  132.3 3.1 %collective-permute-start.15 = (bf16[2,256,256]{2,1,0:T(8,128)(2,1)S(1)}, bf16[2,256,256]{2,1,0:T(8,128)(2,1)S(1)}, u32[]{:S(2)}, u32[]{:S(2)}) collective-permute-start(bf16[2,256,256]{2,1,0:T(8,128)(2,1)S(1)} %collective-permute-done.13), channel_id=1, source_target_pairs={{0,4},{4,8},{8,12},{12,0},{1,5},{5,9},{9,13},{13,1},{2,6},{6,10},{... | collective-permute-start | bytes 786440 | tf_op jit(solution)/shard_map/kv_ring/ppermute | solution.py:259
  138.9 5.2 %collective-permute-start.17 = (bf16[2,256,256]{2,1,0:T(8,128)(2,1)S(1)}, bf16[2,256,256]{2,1,0:T(8,128)(2,1)S(1)}, u32[]{:S(2)}, u32[]{:S(2)}) collective-permute-start(bf16[2,256,256]{2,1,0:T(8,128)(2,1)S(1)} %collective-permute-done.15), channel_id=1, source_target_pairs={{0,4},{4,8},{8,12},{12,0},{1,5},{5,9},{9,13},{13,1},{2,6},{6,10},{... | collective-permute-start | bytes 786440 | tf_op jit(solution)/shard_map/kv_ring/ppermute | solution.py:259
  144.7 1.9 %collective-permute-start.18 = (bf16[2,256,256]{2,1,0:T(8,128)(2,1)S(1)}, bf16[2,256,256]{2,1,0:T(8,128)(2,1)S(1)}, u32[]{:S(2)}, u32[]{:S(2)}) collective-permute-start(bf16[2,256,256]{2,1,0:T(8,128)(2,1)S(1)} %collective-permute-done.16), channel_id=1, source_target_pairs={{4,0},{8,4},{12,8},{0,12},{5,1},{9,5},{13,9},{1,13},{6,2},{10,6},{... | collective-permute-start | bytes 786440 | tf_op jit(solution)/shard_map/kv_ring/ppermute | solution.py:260
  147.4 5.1 %collective-permute-done.18 = bf16[2,256,256]{2,1,0:T(8,128)(2,1)S(1)} collective-permute-done((bf16[2,256,256]{2,1,0:T(8,128)(2,1)S(1)}, bf16[2,256,256]{2,1,0:T(8,128)(2,1)S(1)}, u32[]{:S(2)}, u32[]{:S(2)}) %collective-permute-start.18) | collective-permute-done | bytes 262176 | tf_op jit(solution)/shard_map/kv_ring/ppermute | solution.py:260
  156.9 5.6 %collective-permute-start.19 = (bf16[128,256]{0,1:T(8,128)(2,1)S(1)}, bf16[128,256]{0,1:T(8,128)(2,1)S(1)}, u32[]{:S(2)}, u32[]{:S(2)}) collective-permute-start(bf16[128,256]{0,1:T(8,128)(2,1)S(1)} %bitcast.321), channel_id=1, source_target_pairs={{0,1},{1,2},{2,3},{3,0},{4,5},{5,6},{6,7},{7,4},{8,9},{9,10},{10,1... | collective-permute-start | bytes 196616 | tf_op jit(solution)/shard_map/out_projection/ppermute | solution.py:284
  164.0 2.3 %collective-permute-start.26 = (bf16[128,256]{0,1:T(8,128)(2,1)S(1)}, bf16[128,256]{0,1:T(8,128)(2,1)S(1)}, u32[]{:S(2)}, u32[]{:S(2)}) collective-permute-start(bf16[128,256]{0,1:T(8,128)(2,1)S(1)} %bitcast.320), channel_id=1, source_target_pairs={{0,3},{1,0},{2,1},{3,2},{4,7},{5,4},{6,5},{7,6},{8,11},{9,8},{10,9... | collective-permute-start | bytes 196616 | tf_op jit(solution)/shard_map/out_projection/ppermute | solution.py:284
  170.3 3.0 %collective-permute-done.24 = bf16[128,256]{0,1:T(8,128)(2,1)S(1)} collective-permute-done((bf16[128,256]{0,1:T(8,128)(2,1)S(1)}, bf16[128,256]{0,1:T(8,128)(2,1)S(1)}, u32[]{:S(2)}, u32[]{:S(2)}) %collective-permute-start.24) | collective-permute-done | bytes 65568 | tf_op jit(solution)/shard_map/out_projection/ppermute | solution.py:284
  175.7 3.1 %collective-permute-start.30 = (bf16[8,256]{1,0:T(8,128)(2,1)S(1)}, bf16[8,256]{1,0:T(8,128)(2,1)S(1)}, u32[]{:S(2)}, u32[]{:S(2)}) collective-permute-start(bf16[8,256]{1,0:T(8,128)(2,1)S(1)} %get-tuple-element.60), channel_id=1, source_target_pairs={{0,2},{1,3},{2,0},{3,1},{4,6},{5,7},{6,4},{7,5},{8,10},{9,11},{10,... | collective-permute-start | bytes 12296 | tf_op jit(solution)/shard_map/sides_gather/ppermute | solution.py:173
  179.5 1.6 collective-permute-done.29
  (138 shorter events, 49.3 us)
Async XLA Ops:
  2.6 45.1 %collective-permute-start.21 = (bf16[256,768]{1,0:T(8,128)(2,1)}, bf16[256,768]{1,0:T(8,128)(2,1)}, u32[]{:S(2)}, u32[]{:S(2)}) collective-permute-start(bf16[256,768]{1,0:T(8,128)(2,1)} %constant_dynamic-slice_fusion), channel_id=1, source_target_pairs={{1,0},{2,1},{3,2},{5,4},{6,5},{7,6},{9,8},{10,9},{11,10},{13,12},{... | collective-permute-start | bytes 1179656 | tf_op jit(solution)/shard_map/out_projection/ppermute | solution.py:99
  3.9 49.9 %collective-permute-start.20 = (bf16[256,768]{1,0:T(8,128)(2,1)}, bf16[256,768]{1,0:T(8,128)(2,1)}, u32[]{:S(2)}, u32[]{:S(2)}) collective-permute-start(bf16[256,768]{1,0:T(8,128)(2,1)} %constant_dynamic-slice_fusion), channel_id=1, source_target_pairs={{0,1},{1,2},{2,3},{4,5},{5,6},{6,7},{8,9},{9,10},{10,11},{12,13},{... | collective-permute-start | bytes 1179656 | tf_op jit(solution)/shard_map/out_projection/ppermute | solution.py:98
  13.5 8.8 %collective-permute-start = (bf16[128,384]{1,0:T(8,128)(2,1)S(1)}, bf16[128,384]{1,0:T(8,128)(2,1)S(1)}, u32[]{:S(2)}, u32[]{:S(2)}) collective-permute-start(bf16[128,384]{1,0:T(8,128)(2,1)S(1)} %bitcast.315), channel_id=1, source_target_pairs={{0,1},{1,2},{2,3},{3,0},{4,5},{5,6},{6,7},{7,4},{8,9},{9,10},{10,1... | collective-permute-start | bytes 294920 | tf_op jit(solution)/shard_map/ppermute | solution.py:85
  14.9 10.1 %collective-permute-start.1 = (bf16[128,384]{1,0:T(8,128)(2,1)S(1)}, bf16[128,384]{1,0:T(8,128)(2,1)S(1)}, u32[]{:S(2)}, u32[]{:S(2)}) collective-permute-start(bf16[128,384]{1,0:T(8,128)(2,1)S(1)} %bitcast.314), channel_id=1, source_target_pairs={{0,2},{1,3},{2,0},{3,1},{4,6},{5,7},{6,4},{7,5},{8,10},{9,11},{10,... | collective-permute-start | bytes 294920 | tf_op jit(solution)/shard_map/ppermute | solution.py:85
  16.7 8.3 %collective-permute-start.2 = (bf16[128,384]{1,0:T(8,128)(2,1)S(1)}, bf16[128,384]{1,0:T(8,128)(2,1)S(1)}, u32[]{:S(2)}, u32[]{:S(2)}) collective-permute-start(bf16[128,384]{1,0:T(8,128)(2,1)S(1)} %bitcast.313), channel_id=1, source_target_pairs={{0,3},{1,0},{2,1},{3,2},{4,7},{5,4},{6,5},{7,6},{8,11},{9,8},{10,9... | collective-permute-start | bytes 294920 | tf_op jit(solution)/shard_map/ppermute | solution.py:85
  25.1 8.5 %collective-permute-start.3 = (bf16[8,384]{1,0:T(8,128)(2,1)S(1)}, bf16[8,384]{1,0:T(8,128)(2,1)S(1)}, u32[]{:S(2)}, u32[]{:S(2)}) collective-permute-start(bf16[8,384]{1,0:T(8,128)(2,1)S(1)} %get-tuple-element.28), channel_id=1, source_target_pairs={{0,4},{4,8},{8,12},{1,5},{5,9},{9,13},{2,6},{6,10},{10,14},{3,7},{... | collective-permute-start | bytes 18440 | tf_op jit(solution)/shard_map/ppermute | solution.py:25
  26.4 5.2 %collective-permute-start.4 = (bf16[8,384]{1,0:T(8,128)(2,1)S(1)}, bf16[8,384]{1,0:T(8,128)(2,1)S(1)}, u32[]{:S(2)}, u32[]{:S(2)}) collective-permute-start(bf16[8,384]{1,0:T(8,128)(2,1)S(1)} %get-tuple-element.29), channel_id=1, source_target_pairs={{4,0},{8,4},{12,8},{5,1},{9,5},{13,9},{6,2},{10,6},{14,10},{7,3},{... | collective-permute-start | bytes 18440 | tf_op jit(solution)/shard_map/ppermute | solution.py:26
  38.4 16.7 %collective-permute-start.8 = (bf16[128,1536]{1,0:T(8,128)(2,1)S(1)}, bf16[128,1536]{1,0:T(8,128)(2,1)}, u32[]{:S(2)}, u32[]{:S(2)}) collective-permute-start(bf16[128,1536]{1,0:T(8,128)(2,1)S(1)} %get-tuple-element.23), channel_id=1, source_target_pairs={{0,1},{3,2},{4,5},{7,6},{8,9},{11,10},{12,13},{15,14},{16,17},{19,... | collective-permute-start | bytes 1179656 | tf_op jit(solution)/shard_map/conv_reduce/ppermute | solution.py:49
  44.3 34.2 %collective-permute-start.5 = (bf16[128,1536]{1,0:T(8,128)(2,1)}, bf16[128,1536]{1,0:T(8,128)(2,1)}, u32[]{:S(2)}, u32[]{:S(2)}) collective-permute-start(bf16[128,1536]{1,0:T(8,128)(2,1)} %get-tuple-element.22), channel_id=1, source_target_pairs={{0,1},{1,2},{2,3},{4,5},{5,6},{6,7},{8,9},{9,10},{10,11},{12,13},{... | collective-permute-start | bytes 1179656 | tf_op jit(solution)/shard_map/conv_reduce/ppermute | solution.py:49
  46.4 40.2 %collective-permute-start.6 = (bf16[128,1536]{1,0:T(8,128)(2,1)}, bf16[128,1536]{1,0:T(8,128)(2,1)}, u32[]{:S(2)}, u32[]{:S(2)}) collective-permute-start(bf16[128,1536]{1,0:T(8,128)(2,1)} %get-tuple-element.25), channel_id=1, source_target_pairs={{1,0},{2,1},{3,2},{5,4},{6,5},{7,6},{9,8},{10,9},{11,10},{13,12},{... | collective-permute-start | bytes 1179656 | tf_op jit(solution)/shard_map/conv_reduce/ppermute | solution.py:49
  47.7 38.9 %collective-permute-start.7 = (bf16[128,1536]{1,0:T(8,128)(2,1)}, bf16[128,1536]{1,0:T(8,128)(2,1)}, u32[]{:S(2)}, u32[]{:S(2)}) collective-permute-start(bf16[128,1536]{1,0:T(8,128)(2,1)} %get-tuple-element.24), channel_id=1, source_target_pairs={{0,2},{3,1},{4,6},{7,5},{8,10},{11,9},{12,14},{15,13},{16,18},{19,... | collective-permute-start | bytes 1179656 | tf_op jit(solution)/shard_map/conv_reduce/ppermute | solution.py:49
  53.8 14.1 %collective-permute-start.22 = (bf16[256,768]{1,0:T(8,128)(2,1)}, bf16[256,768]{1,0:T(8,128)(2,1)S(1)}, u32[]{:S(2)}, u32[]{:S(2)}) collective-permute-start(bf16[256,768]{1,0:T(8,128)(2,1)} %collective-permute-done.21), channel_id=1, source_target_pairs={{1,0},{2,1},{3,2},{5,4},{6,5},{7,6},{9,8},{10,9},{11,10},{13,12},{... | collective-permute-start | bytes 1179656 | tf_op jit(solution)/shard_map/out_projection/ppermute | solution.py:99
  55.1 22.1 %collective-permute-start.25 = (bf16[256,768]{1,0:T(8,128)(2,1)}, bf16[256,768]{1,0:T(8,128)(2,1)S(1)}, u32[]{:S(2)}, u32[]{:S(2)}) collective-permute-start(bf16[256,768]{1,0:T(8,128)(2,1)} %collective-permute-done.20), channel_id=1, source_target_pairs={{0,1},{1,2},{2,3},{4,5},{5,6},{6,7},{8,9},{9,10},{10,11},{12,13},{... | collective-permute-start | bytes 1179656 | tf_op jit(solution)/shard_map/out_projection/ppermute | solution.py:98
  67.9 23.5 %collective-permute-start.9 = (bf16[128,1536]{1,0:T(8,128)(2,1)}, bf16[128,1536]{1,0:T(8,128)(2,1)}, u32[]{:S(2)}, u32[]{:S(2)}) collective-permute-start(bf16[128,1536]{1,0:T(8,128)(2,1)} %fusion.75), channel_id=1, source_target_pairs={{1,3},{2,0},{5,7},{6,4},{9,11},{10,8},{13,15},{14,12},{17,19},{18,... | collective-permute-start | bytes 1179656 | tf_op jit(solution)/shard_map/conv_reduce/ppermute | solution.py:56
  77.2 31.4 %collective-permute-start.23 = (bf16[256,768]{1,0:T(8,128)(2,1)S(1)}, bf16[256,768]{1,0:T(8,128)(2,1)S(1)}, u32[]{:S(2)}, u32[]{:S(2)}) collective-permute-start(bf16[256,768]{1,0:T(8,128)(2,1)S(1)} %collective-permute-done.22), channel_id=1, source_target_pairs={{1,0},{2,1},{3,2},{5,4},{6,5},{7,6},{9,8},{10,9},{11,10},{13,12},{... | collective-permute-start | bytes 1179656 | tf_op jit(solution)/shard_map/out_projection/ppermute | solution.py:99
  78.5 30.1 %collective-permute-start.27 = (bf16[256,768]{1,0:T(8,128)(2,1)S(1)}, bf16[256,768]{1,0:T(8,128)(2,1)S(1)}, u32[]{:S(2)}, u32[]{:S(2)}) collective-permute-start(bf16[256,768]{1,0:T(8,128)(2,1)S(1)} %collective-permute-done.25), channel_id=1, source_target_pairs={{0,1},{1,2},{2,3},{4,5},{5,6},{6,7},{8,9},{9,10},{10,11},{12,13},{... | collective-permute-start | bytes 1179656 | tf_op jit(solution)/shard_map/out_projection/ppermute | solution.py:98
  93.6 16.5 %collective-permute-start.10 = (bf16[128,1536]{1,0:T(8,128)(2,1)S(1)}, bf16[128,1536]{1,0:T(8,128)(2,1)S(1)}, u32[]{:S(2)}, u32[]{:S(2)}) collective-permute-start(bf16[128,1536]{1,0:T(8,128)(2,1)S(1)} %fusion.73), channel_id=1, source_target_pairs={{0,1},{1,2},{2,3},{3,0},{4,5},{5,6},{6,7},{7,4},{8,9},{9,10},{10,1... | collective-permute-start | bytes 1179656 | tf_op jit(solution)/shard_map/attn_in_gather/ppermute | solution.py:161
  93.7 31.3 %collective-permute-start.11 = (bf16[128,1536]{1,0:T(8,128)(2,1)S(1)}, bf16[128,1536]{1,0:T(8,128)(2,1)S(1)}, u32[]{:S(2)}, u32[]{:S(2)}) collective-permute-start(bf16[128,1536]{1,0:T(8,128)(2,1)S(1)} %fusion.73), channel_id=1, source_target_pairs={{0,2},{1,3},{2,0},{3,1},{4,6},{5,7},{6,4},{7,5},{8,10},{9,11},{10,... | collective-permute-start | bytes 1179656 | tf_op jit(solution)/shard_map/attn_in_gather/ppermute | solution.py:161
  96.8 28.1 %collective-permute-start.12 = (bf16[128,1536]{1,0:T(8,128)(2,1)S(1)}, bf16[128,1536]{1,0:T(8,128)(2,1)S(1)}, u32[]{:S(2)}, u32[]{:S(2)}) collective-permute-start(bf16[128,1536]{1,0:T(8,128)(2,1)S(1)} %fusion.73), channel_id=1, source_target_pairs={{0,3},{1,0},{2,1},{3,2},{4,7},{5,4},{6,5},{7,6},{8,11},{9,8},{10,9... | collective-permute-start | bytes 1179656 | tf_op jit(solution)/shard_map/attn_in_gather/ppermute | solution.py:161
  109.8 63.8 %collective-permute-start.28 = (bf16[3,256,768]{2,1,0:T(8,128)(2,1)S(1)}, bf16[3,256,768]{2,1,0:T(8,128)(2,1)S(1)}, u32[]{:S(2)}, u32[]{:S(2)}) collective-permute-start(bf16[3,256,768]{2,1,0:T(8,128)(2,1)S(1)} %pad_maximum_fusion), channel_id=1, source_target_pairs={{0,4},{4,0},{8,12},{12,8},{1,5},{5,1},{9,13},{13,9},{2,6},{6,2},{1... | collective-permute-start | bytes 3538952 | tf_op jit(solution)/shard_map/out_projection/ppermute | solution.py:277
  126.5 5.8 %collective-permute-start.13 = (bf16[2,256,256]{2,1,0:T(8,128)(2,1)S(1)}, bf16[2,256,256]{2,1,0:T(8,128)(2,1)S(1)}, u32[]{:S(2)}, u32[]{:S(2)}) collective-permute-start(bf16[2,256,256]{2,1,0:T(8,128)(2,1)S(1)} %get-tuple-element.26), channel_id=1, source_target_pairs={{0,4},{4,8},{8,12},{12,0},{1,5},{5,9},{9,13},{13,1},{2,6},{6,10},{... | collective-permute-start | bytes 786440 | tf_op jit(solution)/shard_map/kv_ring/ppermute | solution.py:259
  127.7 8.0 %collective-permute-start.14 = (bf16[2,256,256]{2,1,0:T(8,128)(2,1)S(1)}, bf16[2,256,256]{2,1,0:T(8,128)(2,1)S(1)}, u32[]{:S(2)}, u32[]{:S(2)}) collective-permute-start(bf16[2,256,256]{2,1,0:T(8,128)(2,1)S(1)} %get-tuple-element.27), channel_id=1, source_target_pairs={{4,0},{8,4},{12,8},{0,12},{5,1},{9,5},{13,9},{1,13},{6,2},{10,6},{... | collective-permute-start | bytes 786440 | tf_op jit(solution)/shard_map/kv_ring/ppermute | solution.py:260
  132.3 6.6 %collective-permute-start.15 = (bf16[2,256,256]{2,1,0:T(8,128)(2,1)S(1)}, bf16[2,256,256]{2,1,0:T(8,128)(2,1)S(1)}, u32[]{:S(2)}, u32[]{:S(2)}) collective-permute-start(bf16[2,256,256]{2,1,0:T(8,128)(2,1)S(1)} %collective-permute-done.13), channel_id=1, source_target_pairs={{0,4},{4,8},{8,12},{12,0},{1,5},{5,9},{9,13},{13,1},{2,6},{6,10},{... | collective-permute-start | bytes 786440 | tf_op jit(solution)/shard_map/kv_ring/ppermute | solution.py:259
  135.8 8.6 %collective-permute-start.16 = (bf16[2,256,256]{2,1,0:T(8,128)(2,1)S(1)}, bf16[2,256,256]{2,1,0:T(8,128)(2,1)S(1)}, u32[]{:S(2)}, u32[]{:S(2)}) collective-permute-start(bf16[2,256,256]{2,1,0:T(8,128)(2,1)S(1)} %collective-permute-done.14), channel_id=1, source_target_pairs={{4,0},{8,4},{12,8},{0,12},{5,1},{9,5},{13,9},{1,13},{6,2},{10,6},{... | collective-permute-start | bytes 786440 | tf_op jit(solution)/shard_map/kv_ring/ppermute | solution.py:260
  138.9 8.2 %collective-permute-start.17 = (bf16[2,256,256]{2,1,0:T(8,128)(2,1)S(1)}, bf16[2,256,256]{2,1,0:T(8,128)(2,1)S(1)}, u32[]{:S(2)}, u32[]{:S(2)}) collective-permute-start(bf16[2,256,256]{2,1,0:T(8,128)(2,1)S(1)} %collective-permute-done.15), channel_id=1, source_target_pairs={{0,4},{4,8},{8,12},{12,0},{1,5},{5,9},{9,13},{13,1},{2,6},{6,10},{... | collective-permute-start | bytes 786440 | tf_op jit(solution)/shard_map/kv_ring/ppermute | solution.py:259
  144.7 7.8 %collective-permute-start.18 = (bf16[2,256,256]{2,1,0:T(8,128)(2,1)S(1)}, bf16[2,256,256]{2,1,0:T(8,128)(2,1)S(1)}, u32[]{:S(2)}, u32[]{:S(2)}) collective-permute-start(bf16[2,256,256]{2,1,0:T(8,128)(2,1)S(1)} %collective-permute-done.16), channel_id=1, source_target_pairs={{4,0},{8,4},{12,8},{0,12},{5,1},{9,5},{13,9},{1,13},{6,2},{10,6},{... | collective-permute-start | bytes 786440 | tf_op jit(solution)/shard_map/kv_ring/ppermute | solution.py:260
  156.9 10.5 %collective-permute-start.19 = (bf16[128,256]{0,1:T(8,128)(2,1)S(1)}, bf16[128,256]{0,1:T(8,128)(2,1)S(1)}, u32[]{:S(2)}, u32[]{:S(2)}) collective-permute-start(bf16[128,256]{0,1:T(8,128)(2,1)S(1)} %bitcast.321), channel_id=1, source_target_pairs={{0,1},{1,2},{2,3},{3,0},{4,5},{5,6},{6,7},{7,4},{8,9},{9,10},{10,1... | collective-permute-start | bytes 196616 | tf_op jit(solution)/shard_map/out_projection/ppermute | solution.py:284
  164.0 5.1 %collective-permute-start.26 = (bf16[128,256]{0,1:T(8,128)(2,1)S(1)}, bf16[128,256]{0,1:T(8,128)(2,1)S(1)}, u32[]{:S(2)}, u32[]{:S(2)}) collective-permute-start(bf16[128,256]{0,1:T(8,128)(2,1)S(1)} %bitcast.320), channel_id=1, source_target_pairs={{0,3},{1,0},{2,1},{3,2},{4,7},{5,4},{6,5},{7,6},{8,11},{9,8},{10,9... | collective-permute-start | bytes 196616 | tf_op jit(solution)/shard_map/out_projection/ppermute | solution.py:284
  166.3 7.1 %collective-permute-start.24 = (bf16[128,256]{0,1:T(8,128)(2,1)S(1)}, bf16[128,256]{0,1:T(8,128)(2,1)S(1)}, u32[]{:S(2)}, u32[]{:S(2)}) collective-permute-start(bf16[128,256]{0,1:T(8,128)(2,1)S(1)} %bitcast.319), channel_id=1, source_target_pairs={{0,2},{1,3},{2,0},{3,1},{4,6},{5,7},{6,4},{7,5},{8,10},{9,11},{10,... | collective-permute-start | bytes 196616 | tf_op jit(solution)/shard_map/out_projection/ppermute | solution.py:284
  175.7 5.4 %collective-permute-start.29 = (bf16[8,256]{1,0:T(8,128)(2,1)S(1)}, bf16[8,256]{1,0:T(8,128)(2,1)S(1)}, u32[]{:S(2)}, u32[]{:S(2)}) collective-permute-start(bf16[8,256]{1,0:T(8,128)(2,1)S(1)} %get-tuple-element.60), channel_id=1, source_target_pairs={{0,1},{1,2},{2,3},{3,0},{4,5},{5,6},{6,7},{7,4},{8,9},{9,10},{10,1... | collective-permute-start | bytes 12296 | tf_op jit(solution)/shard_map/sides_gather/ppermute | solution.py:173
  175.7 5.4 %collective-permute-start.30 = (bf16[8,256]{1,0:T(8,128)(2,1)S(1)}, bf16[8,256]{1,0:T(8,128)(2,1)S(1)}, u32[]{:S(2)}, u32[]{:S(2)}) collective-permute-start(bf16[8,256]{1,0:T(8,128)(2,1)S(1)} %get-tuple-element.60), channel_id=1, source_target_pairs={{0,2},{1,3},{2,0},{3,1},{4,6},{5,7},{6,4},{7,5},{8,10},{9,11},{10,... | collective-permute-start | bytes 12296 | tf_op jit(solution)/shard_map/sides_gather/ppermute | solution.py:173
  182.4 3.8 %collective-permute-start.33 = (bf16[32,256]{1,0:T(8,128)(2,1)S(1)}, bf16[32,256]{1,0:T(8,128)(2,1)S(1)}, u32[]{:S(2)}, u32[]{:S(2)}) collective-permute-start(bf16[32,256]{1,0:T(8,128)(2,1)S(1)} %bitcast.317), channel_id=1, source_target_pairs={{0,8},{4,12},{8,0},{12,4},{1,9},{5,13},{9,1},{13,5},{2,10},{6,14},... | collective-permute-start | bytes 49160 | tf_op jit(solution)/shard_map/sides_gather/ppermute | solution.py:173
  (13 other events, 288.1 us)

commit v16 on v14

--- a/solution.py
+++ b/solution.py
@@ -188,10 +188,22 @@
     with jax.named_scope("attn_in_gather"):
         rotated = pair_count <= 4
         if rotated:
-            block_in = rotated_all_gather(attn_in, "pair")
+            pieces_in = [attn_in] + [
+                lax.ppermute(attn_in, "pair", [(i, (i + k) % pair_count) for i in range(pair_count)])
+                for k in range(1, pair_count)
+            ]
+            projected = jnp.concatenate(
+                [
+                    jnp.dot(piece, w_qkv, preferred_element_type=jnp.float32).astype(jnp.bfloat16)
+                    for piece in pieces_in
+                ],
+                0,
+            )
         else:
             block_in = direct_all_gather(attn_in, "pair")
-    projected = jnp.dot(block_in, w_qkv, preferred_element_type=jnp.float32).astype(jnp.bfloat16)
+            projected = jnp.dot(
+                block_in, w_qkv, preferred_element_type=jnp.float32
+            ).astype(jnp.bfloat16)
     head_count = projected.shape[1] // (2 * KEY_SIZE + VALUE_SIZE)
     grouped = projected.reshape(local_rows, head_count, 2 * KEY_SIZE + VALUE_SIZE).transpose(1, 0, 2)
     queries = grouped[:, :, :KEY_SIZE]

time: 174 us -> 177 us (1.017)
  starting transfers between devices: 70.1 us -> 76.5 us
  waiting for transfers between devices: 73.6 us -> 67.9 us
  local copies, waits for them, and re-layouts: 2.86 us -> 5.94 us
    ppermute x3, waiting for transfers between devices: 26.8 us -> 18.5 us  [shards(): lax.ppermute(attn_in, 'pair', [(i, (i + k) % pair_count) for i in range(p...]
    ppermute x3, starting transfers between devices: 21.6 us -> 28.1 us  [line_flows(): flow_r = lax.ppermute(flow_r, axis, right)]
where the time goes in v16:
time: 177 us; the launch traced here: 176 us
  starting transfers between devices  76.5 us (43%)
  waiting for transfers between devices  67.9 us (38%)
  matrix products  17.8 us (10%)
  other arithmetic  6.94 us (4%)
  local copies, waits for them, and re-layouts  5.94 us (3%)
    ppermute x3, starting transfers between devices, line_flows(): flow_r = lax.ppermute(flow_r, axis, right)  28.1 us
    ppermute x3, waiting for transfers between devices, direct_reduce_scatter(): lax.ppermute(outgoing, axis, [(i, (i + shift) % n) for i in range(n)])  20.3 us
    ppermute x3, waiting for transfers between devices, shards(): lax.ppermute(attn_in, 'pair', [(i, (i + k) % pair_count) for i in range(p...  18.5 us
    ppermute x3, starting transfers between devices, shards(): lax.ppermute(attn_in, 'pair', [(i, (i + k) % pair_count) for i in range(p...  10.4 us
    ppermute x3, waiting for transfers between devices, shards(): next_going = lax.ppermute(going, 'seq', forward)  7.85 us
    ppermute x6, starting transfers between devices, direct_all_gather(): lax.ppermute(value, axis, [(i, (i + shift) % n) for i in range(n)])  7.42 us
    ppermute x3, starting transfers between devices, direct_reduce_scatter(): lax.ppermute(outgoing, axis, [(i, (i + shift) % n) for i in range(n)])  6.98 us
    dot_general x5, matrix products, conv_rows(): jnp.dot(shifted, conv_weight[offset], preferred_element_type=jnp.float32)  6.46 us
  transfers between devices with their start and end apart: 33, of which 19 were waited for; matrix products, arithmetic and copies ran while one was open for 14% of the time, Pallas kernels for 0%

profile of v16, /device:TPU:0, one launch (start us, length us, event | category | flops | bytes accessed | tf_op | source)
XLA Modules:
  0.0 176.4 jit_solution(12803494059133105808)
XLA Ops:
  0.7 1.9 %constant_dynamic-slice_fusion = bf16[256,768]{1,0:T(8,128)(2,1)} fusion(bf16[256,1536]{1,0:T(8,128)(2,1)} %param.15, s32[]{:T(128)S(6)} %select_n.137), kind=kLoop, calls=%fused_computation.200 | loop fusion | bytes 786436 | tf_op jit(solution)/shard_map/out_projection/dynamic_slice | solution.py:262
  3.9 6.3 %collective-permute-start.18 = (bf16[256,768]{1,0:T(8,128)(2,1)}, bf16[256,768]{1,0:T(8,128)(2,1)}, u32[]{:S(2)}, u32[]{:S(2)}) collective-permute-start(bf16[256,768]{1,0:T(8,128)(2,1)} %constant_dynamic-slice_fusion), channel_id=1, source_target_pairs={{0,1},{1,2},{2,3},{4,5},{5,6},{6,7},{8,9},{9,10},{10,11},{12,13},{... | collective-permute-start | bytes 1179656 | tf_op jit(solution)/shard_map/out_projection/ppermute | solution.py:78
  13.5 1.4 collective-permute-start
  16.0 3.0 %collective-permute-start.2 = (bf16[128,384]{1,0:T(8,128)(2,1)S(1)}, bf16[128,384]{1,0:T(8,128)(2,1)S(1)}, u32[]{:S(2)}, u32[]{:S(2)}) collective-permute-start(bf16[128,384]{1,0:T(8,128)(2,1)S(1)} %bitcast.311), channel_id=1, source_target_pairs={{0,3},{1,0},{2,1},{3,2},{4,7},{5,4},{6,5},{7,6},{8,11},{9,8},{10,9... | collective-permute-start | bytes 294920 | tf_op jit(solution)/shard_map/ppermute | solution.py:65
  19.0 3.3 %collective-permute-done = bf16[128,384]{1,0:T(8,128)(2,1)S(1)} collective-permute-done((bf16[128,384]{1,0:T(8,128)(2,1)S(1)}, bf16[128,384]{1,0:T(8,128)(2,1)S(1)}, u32[]{:S(2)}, u32[]{:S(2)}) %collective-permute-start) | collective-permute-done | bytes 98336 | tf_op jit(solution)/shard_map/ppermute | solution.py:65
  22.3 2.7 %collective-permute-done.1 = bf16[128,384]{1,0:T(8,128)(2,1)S(1)} collective-permute-done((bf16[128,384]{1,0:T(8,128)(2,1)S(1)}, bf16[128,384]{1,0:T(8,128)(2,1)S(1)}, u32[]{:S(2)}, u32[]{:S(2)}) %collective-permute-start.1) | collective-permute-done | bytes 98336 | tf_op jit(solution)/shard_map/ppermute | solution.py:65
  26.4 1.6 collective-permute-start.4
  28.0 2.4 %fusion.30 = f32[512,1536]{1,0:T(8,128)S(1)} fusion(bf16[512,384]{1,0:T(8,128)(2,1)S(1)} %bitcast.299, bf16[5,384,1536]{2,1,0:T(8,128)(2,1)} %param.12), kind=kOutput, calls=%fused_computation.59 | convolution fusion | flops 603979776 | bytes 4718592 | tf_op jit(solution)/shard_map/conv_reduce/dot_general | solution.py:39
  35.7 1.6 copy-done.1
  38.4 3.2 %collective-permute-start.5 = (bf16[128,1536]{1,0:T(8,128)(2,1)}, bf16[128,1536]{1,0:T(8,128)(2,1)S(1)}, u32[]{:S(2)}, u32[]{:S(2)}) collective-permute-start(bf16[128,1536]{1,0:T(8,128)(2,1)} %get-tuple-element.22), channel_id=1, source_target_pairs={{0,1},{1,2},{2,3},{3,0},{4,5},{5,6},{6,7},{7,4},{8,9},{9,10},{10,1... | collective-permute-start | bytes 1179656 | tf_op jit(solution)/shard_map/conv_reduce/ppermute | solution.py:51
  41.6 3.4 %collective-permute-start.6 = (bf16[128,1536]{1,0:T(8,128)(2,1)}, bf16[128,1536]{1,0:T(8,128)(2,1)}, u32[]{:S(2)}, u32[]{:S(2)}) collective-permute-start(bf16[128,1536]{1,0:T(8,128)(2,1)} %get-tuple-element.24), channel_id=1, source_target_pairs={{0,2},{1,3},{2,0},{3,1},{4,6},{5,7},{6,4},{7,5},{8,10},{9,11},{10,... | collective-permute-start | bytes 1179656 | tf_op jit(solution)/shard_map/conv_reduce/ppermute | solution.py:51
  46.7 4.6 %collective-permute-start.23 = (bf16[256,768]{1,0:T(8,128)(2,1)}, bf16[256,768]{1,0:T(8,128)(2,1)S(1)}, u32[]{:S(2)}, u32[]{:S(2)}) collective-permute-start(bf16[256,768]{1,0:T(8,128)(2,1)} %collective-permute-done.18), channel_id=1, source_target_pairs={{0,1},{1,2},{2,3},{4,5},{5,6},{6,7},{8,9},{9,10},{10,11},{12,13},{... | collective-permute-start | bytes 1179656 | tf_op jit(solution)/shard_map/out_projection/ppermute | solution.py:78
  51.3 1.8 %collective-permute-done.5 = bf16[128,1536]{1,0:T(8,128)(2,1)S(1)} collective-permute-done((bf16[128,1536]{1,0:T(8,128)(2,1)}, bf16[128,1536]{1,0:T(8,128)(2,1)S(1)}, u32[]{:S(2)}, u32[]{:S(2)}) %collective-permute-start.5) | collective-permute-done | bytes 393248 | tf_op jit(solution)/shard_map/conv_reduce/ppermute | solution.py:51
  53.1 18.4 %collective-permute-done.6 = bf16[128,1536]{1,0:T(8,128)(2,1)} collective-permute-done((bf16[128,1536]{1,0:T(8,128)(2,1)}, bf16[128,1536]{1,0:T(8,128)(2,1)}, u32[]{:S(2)}, u32[]{:S(2)}) %collective-permute-start.6) | collective-permute-done | bytes 393248 | tf_op jit(solution)/shard_map/conv_reduce/ppermute | solution.py:51
  71.6 1.7 fusion.60
  73.5 8.2 %collective-permute-start.10 = (bf16[128,1536]{1,0:T(8,128)(2,1)S(1)}, bf16[128,1536]{1,0:T(8,128)(2,1)S(1)}, u32[]{:S(2)}, u32[]{:S(2)}) collective-permute-start(bf16[128,1536]{1,0:T(8,128)(2,1)S(1)} %fusion.62), channel_id=1, source_target_pairs={{0,3},{1,0},{2,1},{3,2},{4,7},{5,4},{6,5},{7,6},{8,11},{9,8},{10,9... | collective-permute-start | bytes 1179656 | tf_op jit(solution)/shard_map/attn_in_gather/ppermute | solution.py:192
  81.7 2.2 %collective-permute-start.9 = (bf16[128,1536]{1,0:T(8,128)(2,1)S(1)}, bf16[128,1536]{1,0:T(8,128)(2,1)S(1)}, u32[]{:S(2)}, u32[]{:S(2)}) collective-permute-start(bf16[128,1536]{1,0:T(8,128)(2,1)S(1)} %fusion.62), channel_id=1, source_target_pairs={{0,2},{1,3},{2,0},{3,1},{4,6},{5,7},{6,4},{7,5},{8,10},{9,11},{10,... | collective-permute-start | bytes 1179656 | tf_op jit(solution)/shard_map/attn_in_gather/ppermute | solution.py:192
  85.7 17.2 %collective-permute-start.25 = (bf16[256,768]{1,0:T(8,128)(2,1)S(1)}, bf16[256,768]{1,0:T(8,128)(2,1)S(1)}, u32[]{:S(2)}, u32[]{:S(2)}) collective-permute-start(bf16[256,768]{1,0:T(8,128)(2,1)S(1)} %collective-permute-done.23), channel_id=1, source_target_pairs={{0,1},{1,2},{2,3},{4,5},{5,6},{6,7},{8,9},{9,10},{10,11},{12,13},{... | collective-permute-start | bytes 1179656 | tf_op jit(solution)/shard_map/out_projection/ppermute | solution.py:78
  103.5 18.4 %collective-permute-done.9 = bf16[128,1536]{1,0:T(8,128)(2,1)S(1)} collective-permute-done((bf16[128,1536]{1,0:T(8,128)(2,1)S(1)}, bf16[128,1536]{1,0:T(8,128)(2,1)S(1)}, u32[]{:S(2)}, u32[]{:S(2)}) %collective-permute-start.9) | collective-permute-done | bytes 393248 | tf_op jit(solution)/shard_map/attn_in_gather/ppermute | solution.py:192
  123.3 1.6 collective-permute-start.12
  125.6 4.5 %collective-permute-done.11 = bf16[2,256,256]{2,1,0:T(8,128)(2,1)S(1)} collective-permute-done((bf16[2,256,256]{2,1,0:T(8,128)(2,1)S(1)}, bf16[2,256,256]{2,1,0:T(8,128)(2,1)S(1)}, u32[]{:S(2)}, u32[]{:S(2)}) %collective-permute-start.11) | collective-permute-done | bytes 262176 | tf_op jit(solution)/shard_map/kv_ring/ppermute | solution.py:247
  130.7 1.9 %collective-permute-start.14 = (bf16[2,256,256]{2,1,0:T(8,128)(2,1)S(1)}, bf16[2,256,256]{2,1,0:T(8,128)(2,1)S(1)}, u32[]{:S(2)}, u32[]{:S(2)}) collective-permute-start(bf16[2,256,256]{2,1,0:T(8,128)(2,1)S(1)} %collective-permute-done.12), channel_id=1, source_target_pairs={{4,0},{8,4},{12,8},{0,12},{5,1},{9,5},{13,9},{1,13},{6,2},{10,6},{... | collective-permute-start | bytes 786440 | tf_op jit(solution)/shard_map/kv_ring/ppermute | solution.py:248
  133.6 2.4 %collective-permute-done.13 = bf16[2,256,256]{2,1,0:T(8,128)(2,1)S(1)} collective-permute-done((bf16[2,256,256]{2,1,0:T(8,128)(2,1)S(1)}, bf16[2,256,256]{2,1,0:T(8,128)(2,1)S(1)}, u32[]{:S(2)}, u32[]{:S(2)}) %collective-permute-start.13) | collective-permute-done | bytes 262176 | tf_op jit(solution)/shard_map/kv_ring/ppermute | solution.py:247
  136.0 1.6 collective-permute-start.15
  138.7 2.1 %collective-permute-start.16 = (bf16[2,256,256]{2,1,0:T(8,128)(2,1)S(1)}, bf16[2,256,256]{2,1,0:T(8,128)(2,1)S(1)}, u32[]{:S(2)}, u32[]{:S(2)}) collective-permute-start(bf16[2,256,256]{2,1,0:T(8,128)(2,1)S(1)} %collective-permute-done.14), channel_id=1, source_target_pairs={{4,0},{8,4},{12,8},{0,12},{5,1},{9,5},{13,9},{1,13},{6,2},{10,6},{... | collective-permute-start | bytes 786440 | tf_op jit(solution)/shard_map/kv_ring/ppermute | solution.py:248
  142.1 4.0 %collective-permute-done.16 = bf16[2,256,256]{2,1,0:T(8,128)(2,1)S(1)} collective-permute-done((bf16[2,256,256]{2,1,0:T(8,128)(2,1)S(1)}, bf16[2,256,256]{2,1,0:T(8,128)(2,1)S(1)}, u32[]{:S(2)}, u32[]{:S(2)}) %collective-permute-start.16) | collective-permute-done | bytes 262176 | tf_op jit(solution)/shard_map/kv_ring/ppermute | solution.py:248
  152.0 3.9 %collective-permute-start.24 = (bf16[128,256]{0,1:T(8,128)(2,1)S(1)}, bf16[128,256]{0,1:T(8,128)(2,1)S(1)}, u32[]{:S(2)}, u32[]{:S(2)}) collective-permute-start(bf16[128,256]{0,1:T(8,128)(2,1)S(1)} %bitcast.318), channel_id=1, source_target_pairs={{0,3},{1,0},{2,1},{3,2},{4,7},{5,4},{6,5},{7,6},{8,11},{9,8},{10,9... | collective-permute-start | bytes 196616 | tf_op jit(solution)/shard_map/out_projection/ppermute | solution.py:272
  158.6 2.7 %collective-permute-done.22 = bf16[128,256]{0,1:T(8,128)(2,1)S(1)} collective-permute-done((bf16[128,256]{0,1:T(8,128)(2,1)S(1)}, bf16[128,256]{0,1:T(8,128)(2,1)S(1)}, u32[]{:S(2)}, u32[]{:S(2)}) %collective-permute-start.22) | collective-permute-done | bytes 65568 | tf_op jit(solution)/shard_map/out_projection/ppermute | solution.py:272
  163.6 3.3 %collective-permute-start.28 = (bf16[8,256]{1,0:T(8,128)(2,1)S(1)}, bf16[8,256]{1,0:T(8,128)(2,1)S(1)}, u32[]{:S(2)}, u32[]{:S(2)}) collective-permute-start(bf16[8,256]{1,0:T(8,128)(2,1)S(1)} %get-tuple-element.59), channel_id=1, source_target_pairs={{0,2},{1,3},{2,0},{3,1},{4,6},{5,7},{6,4},{7,5},{8,10},{9,11},{10,... | collective-permute-start | bytes 12296 | tf_op jit(solution)/shard_map/sides_gather/ppermute | solution.py:153
  169.1 1.5 collective-permute-done.29
  170.5 1.7 collective-permute-start.31
  172.3 1.4 collective-permute-start.32
  (137 shorter events, 39.2 us)
Async XLA Ops:
  2.6 42.8 %collective-permute-start.19 = (bf16[256,768]{1,0:T(8,128)(2,1)}, bf16[256,768]{1,0:T(8,128)(2,1)S(1)}, u32[]{:S(2)}, u32[]{:S(2)}) collective-permute-start(bf16[256,768]{1,0:T(8,128)(2,1)} %constant_dynamic-slice_fusion), channel_id=1, source_target_pairs={{1,0},{2,1},{3,2},{5,4},{6,5},{7,6},{9,8},{10,9},{11,10},{13,12},{... | collective-permute-start | bytes 1179656 | tf_op jit(solution)/shard_map/out_projection/ppermute | solution.py:79
  3.9 42.8 %collective-permute-start.18 = (bf16[256,768]{1,0:T(8,128)(2,1)}, bf16[256,768]{1,0:T(8,128)(2,1)}, u32[]{:S(2)}, u32[]{:S(2)}) collective-permute-start(bf16[256,768]{1,0:T(8,128)(2,1)} %constant_dynamic-slice_fusion), channel_id=1, source_target_pairs={{0,1},{1,2},{2,3},{4,5},{5,6},{6,7},{8,9},{9,10},{10,11},{12,13},{... | collective-permute-start | bytes 1179656 | tf_op jit(solution)/shard_map/out_projection/ppermute | solution.py:78
  13.5 8.8 %collective-permute-start = (bf16[128,384]{1,0:T(8,128)(2,1)S(1)}, bf16[128,384]{1,0:T(8,128)(2,1)S(1)}, u32[]{:S(2)}, u32[]{:S(2)}) collective-permute-start(bf16[128,384]{1,0:T(8,128)(2,1)S(1)} %bitcast.313), channel_id=1, source_target_pairs={{0,1},{1,2},{2,3},{3,0},{4,5},{5,6},{6,7},{7,4},{8,9},{9,10},{10,1... | collective-permute-start | bytes 294920 | tf_op jit(solution)/shard_map/ppermute | solution.py:65
  14.9 10.1 %collective-permute-start.1 = (bf16[128,384]{1,0:T(8,128)(2,1)S(1)}, bf16[128,384]{1,0:T(8,128)(2,1)S(1)}, u32[]{:S(2)}, u32[]{:S(2)}) collective-permute-start(bf16[128,384]{1,0:T(8,128)(2,1)S(1)} %bitcast.312), channel_id=1, source_target_pairs={{0,2},{1,3},{2,0},{3,1},{4,6},{5,7},{6,4},{7,5},{8,10},{9,11},{10,... | collective-permute-start | bytes 294920 | tf_op jit(solution)/shard_map/ppermute | solution.py:65
  16.0 9.0 %collective-permute-start.2 = (bf16[128,384]{1,0:T(8,128)(2,1)S(1)}, bf16[128,384]{1,0:T(8,128)(2,1)S(1)}, u32[]{:S(2)}, u32[]{:S(2)}) collective-permute-start(bf16[128,384]{1,0:T(8,128)(2,1)S(1)} %bitcast.311), channel_id=1, source_target_pairs={{0,3},{1,0},{2,1},{3,2},{4,7},{5,4},{6,5},{7,6},{8,11},{9,8},{10,9... | collective-permute-start | bytes 294920 | tf_op jit(solution)/shard_map/ppermute | solution.py:65
  25.1 8.5 %collective-permute-start.3 = (bf16[8,384]{1,0:T(8,128)(2,1)S(1)}, bf16[8,384]{1,0:T(8,128)(2,1)S(1)}, u32[]{:S(2)}, u32[]{:S(2)}) collective-permute-start(bf16[8,384]{1,0:T(8,128)(2,1)S(1)} %get-tuple-element.27), channel_id=1, source_target_pairs={{0,4},{4,8},{8,12},{1,5},{5,9},{9,13},{2,6},{6,10},{10,14},{3,7},{... | collective-permute-start | bytes 18440 | tf_op jit(solution)/shard_map/ppermute | solution.py:25
  26.4 5.2 %collective-permute-start.4 = (bf16[8,384]{1,0:T(8,128)(2,1)S(1)}, bf16[8,384]{1,0:T(8,128)(2,1)S(1)}, u32[]{:S(2)}, u32[]{:S(2)}) collective-permute-start(bf16[8,384]{1,0:T(8,128)(2,1)S(1)} %get-tuple-element.28), channel_id=1, source_target_pairs={{4,0},{8,4},{12,8},{5,1},{9,5},{13,9},{6,2},{10,6},{14,10},{7,3},{... | collective-permute-start | bytes 18440 | tf_op jit(solution)/shard_map/ppermute | solution.py:26
  38.4 14.7 %collective-permute-start.5 = (bf16[128,1536]{1,0:T(8,128)(2,1)}, bf16[128,1536]{1,0:T(8,128)(2,1)S(1)}, u32[]{:S(2)}, u32[]{:S(2)}) collective-permute-start(bf16[128,1536]{1,0:T(8,128)(2,1)} %get-tuple-element.22), channel_id=1, source_target_pairs={{0,1},{1,2},{2,3},{3,0},{4,5},{5,6},{6,7},{7,4},{8,9},{9,10},{10,1... | collective-permute-start | bytes 1179656 | tf_op jit(solution)/shard_map/conv_reduce/ppermute | solution.py:51
  41.6 30.0 %collective-permute-start.6 = (bf16[128,1536]{1,0:T(8,128)(2,1)}, bf16[128,1536]{1,0:T(8,128)(2,1)}, u32[]{:S(2)}, u32[]{:S(2)}) collective-permute-start(bf16[128,1536]{1,0:T(8,128)(2,1)} %get-tuple-element.24), channel_id=1, source_target_pairs={{0,2},{1,3},{2,0},{3,1},{4,6},{5,7},{6,4},{7,5},{8,10},{9,11},{10,... | collective-permute-start | bytes 1179656 | tf_op jit(solution)/shard_map/conv_reduce/ppermute | solution.py:51
  44.9 26.6 %collective-permute-start.7 = (bf16[128,1536]{1,0:T(8,128)(2,1)}, bf16[128,1536]{1,0:T(8,128)(2,1)}, u32[]{:S(2)}, u32[]{:S(2)}) collective-permute-start(bf16[128,1536]{1,0:T(8,128)(2,1)} %get-tuple-element.23), channel_id=1, source_target_pairs={{0,3},{1,0},{2,1},{3,2},{4,7},{5,4},{6,5},{7,6},{8,11},{9,8},{10,9... | collective-permute-start | bytes 1179656 | tf_op jit(solution)/shard_map/conv_reduce/ppermute | solution.py:51
  45.4 39.0 %collective-permute-start.20 = (bf16[256,768]{1,0:T(8,128)(2,1)S(1)}, bf16[256,768]{1,0:T(8,128)(2,1)S(1)}, u32[]{:S(2)}, u32[]{:S(2)}) collective-permute-start(bf16[256,768]{1,0:T(8,128)(2,1)S(1)} %collective-permute-done.19), channel_id=1, source_target_pairs={{1,0},{2,1},{3,2},{5,4},{6,5},{7,6},{9,8},{10,9},{11,10},{13,12},{... | collective-permute-start | bytes 1179656 | tf_op jit(solution)/shard_map/out_projection/ppermute | solution.py:79
  46.7 39.0 %collective-permute-start.23 = (bf16[256,768]{1,0:T(8,128)(2,1)}, bf16[256,768]{1,0:T(8,128)(2,1)S(1)}, u32[]{:S(2)}, u32[]{:S(2)}) collective-permute-start(bf16[256,768]{1,0:T(8,128)(2,1)} %collective-permute-done.18), channel_id=1, source_target_pairs={{0,1},{1,2},{2,3},{4,5},{5,6},{6,7},{8,9},{9,10},{10,11},{12,13},{... | collective-permute-start | bytes 1179656 | tf_op jit(solution)/shard_map/out_projection/ppermute | solution.py:78
  73.5 29.5 %collective-permute-start.10 = (bf16[128,1536]{1,0:T(8,128)(2,1)S(1)}, bf16[128,1536]{1,0:T(8,128)(2,1)S(1)}, u32[]{:S(2)}, u32[]{:S(2)}) collective-permute-start(bf16[128,1536]{1,0:T(8,128)(2,1)S(1)} %fusion.62), channel_id=1, source_target_pairs={{0,3},{1,0},{2,1},{3,2},{4,7},{5,4},{6,5},{7,6},{8,11},{9,8},{10,9... | collective-permute-start | bytes 1179656 | tf_op jit(solution)/shard_map/attn_in_gather/ppermute | solution.py:192
  81.7 40.3 %collective-permute-start.9 = (bf16[128,1536]{1,0:T(8,128)(2,1)S(1)}, bf16[128,1536]{1,0:T(8,128)(2,1)S(1)}, u32[]{:S(2)}, u32[]{:S(2)}) collective-permute-start(bf16[128,1536]{1,0:T(8,128)(2,1)S(1)} %fusion.62), channel_id=1, source_target_pairs={{0,2},{1,3},{2,0},{3,1},{4,6},{5,7},{6,4},{7,5},{8,10},{9,11},{10,... | collective-permute-start | bytes 1179656 | tf_op jit(solution)/shard_map/attn_in_gather/ppermute | solution.py:192
  83.9 38.5 %collective-permute-start.8 = (bf16[128,1536]{1,0:T(8,128)(2,1)S(1)}, bf16[128,1536]{1,0:T(8,128)(2,1)S(1)}, u32[]{:S(2)}, u32[]{:S(2)}) collective-permute-start(bf16[128,1536]{1,0:T(8,128)(2,1)S(1)} %fusion.62), channel_id=1, source_target_pairs={{0,1},{1,2},{2,3},{3,0},{4,5},{5,6},{6,7},{7,4},{8,9},{9,10},{10,1... | collective-permute-start | bytes 1179656 | tf_op jit(solution)/shard_map/attn_in_gather/ppermute | solution.py:192
  84.4 48.8 %collective-permute-start.21 = (bf16[256,768]{1,0:T(8,128)(2,1)S(1)}, bf16[256,768]{1,0:T(8,128)(2,1)S(1)}, u32[]{:S(2)}, u32[]{:S(2)}) collective-permute-start(bf16[256,768]{1,0:T(8,128)(2,1)S(1)} %collective-permute-done.20), channel_id=1, source_target_pairs={{1,0},{2,1},{3,2},{5,4},{6,5},{7,6},{9,8},{10,9},{11,10},{13,12},{... | collective-permute-start | bytes 1179656 | tf_op jit(solution)/shard_map/out_projection/ppermute | solution.py:79
  85.7 47.6 %collective-permute-start.25 = (bf16[256,768]{1,0:T(8,128)(2,1)S(1)}, bf16[256,768]{1,0:T(8,128)(2,1)S(1)}, u32[]{:S(2)}, u32[]{:S(2)}) collective-permute-start(bf16[256,768]{1,0:T(8,128)(2,1)S(1)} %collective-permute-done.23), channel_id=1, source_target_pairs={{0,1},{1,2},{2,3},{4,5},{5,6},{6,7},{8,9},{9,10},{10,11},{12,13},{... | collective-permute-start | bytes 1179656 | tf_op jit(solution)/shard_map/out_projection/ppermute | solution.py:78
  123.1 6.9 %collective-permute-start.11 = (bf16[2,256,256]{2,1,0:T(8,128)(2,1)S(1)}, bf16[2,256,256]{2,1,0:T(8,128)(2,1)S(1)}, u32[]{:S(2)}, u32[]{:S(2)}) collective-permute-start(bf16[2,256,256]{2,1,0:T(8,128)(2,1)S(1)} %get-tuple-element.25), channel_id=1, source_target_pairs={{0,4},{4,8},{8,12},{12,0},{1,5},{5,9},{9,13},{13,1},{2,6},{6,10},{... | collective-permute-start | bytes 786440 | tf_op jit(solution)/shard_map/kv_ring/ppermute | solution.py:247
  123.3 7.4 %collective-permute-start.12 = (bf16[2,256,256]{2,1,0:T(8,128)(2,1)S(1)}, bf16[2,256,256]{2,1,0:T(8,128)(2,1)S(1)}, u32[]{:S(2)}, u32[]{:S(2)}) collective-permute-start(bf16[2,256,256]{2,1,0:T(8,128)(2,1)S(1)} %get-tuple-element.26), channel_id=1, source_target_pairs={{4,0},{8,4},{12,8},{0,12},{5,1},{9,5},{13,9},{1,13},{6,2},{10,6},{... | collective-permute-start | bytes 786440 | tf_op jit(solution)/shard_map/kv_ring/ppermute | solution.py:248
  130.0 6.0 %collective-permute-start.13 = (bf16[2,256,256]{2,1,0:T(8,128)(2,1)S(1)}, bf16[2,256,256]{2,1,0:T(8,128)(2,1)S(1)}, u32[]{:S(2)}, u32[]{:S(2)}) collective-permute-start(bf16[2,256,256]{2,1,0:T(8,128)(2,1)S(1)} %collective-permute-done.11), channel_id=1, source_target_pairs={{0,4},{4,8},{8,12},{12,0},{1,5},{5,9},{9,13},{13,1},{2,6},{6,10},{... | collective-permute-start | bytes 786440 | tf_op jit(solution)/shard_map/kv_ring/ppermute | solution.py:247
  130.7 7.7 %collective-permute-start.14 = (bf16[2,256,256]{2,1,0:T(8,128)(2,1)S(1)}, bf16[2,256,256]{2,1,0:T(8,128)(2,1)S(1)}, u32[]{:S(2)}, u32[]{:S(2)}) collective-permute-start(bf16[2,256,256]{2,1,0:T(8,128)(2,1)S(1)} %collective-permute-done.12), channel_id=1, source_target_pairs={{4,0},{8,4},{12,8},{0,12},{5,1},{9,5},{13,9},{1,13},{6,2},{10,6},{... | collective-permute-start | bytes 786440 | tf_op jit(solution)/shard_map/kv_ring/ppermute | solution.py:248
  133.5 28.0 %collective-permute-start.26 = (bf16[3,256,768]{2,1,0:T(8,128)(2,1)S(1)}, bf16[3,256,768]{2,1,0:T(8,128)(2,1)S(1)}, u32[]{:S(2)}, u32[]{:S(2)}) collective-permute-start(bf16[3,256,768]{2,1,0:T(8,128)(2,1)S(1)} %pad_maximum_fusion), channel_id=1, source_target_pairs={{0,4},{4,0},{8,12},{12,8},{1,5},{5,1},{9,13},{13,9},{2,6},{6,2},{1... | collective-permute-start | bytes 3538952 | tf_op jit(solution)/shard_map/out_projection/ppermute | solution.py:265
  136.0 5.8 %collective-permute-start.15 = (bf16[2,256,256]{2,1,0:T(8,128)(2,1)S(1)}, bf16[2,256,256]{2,1,0:T(8,128)(2,1)S(1)}, u32[]{:S(2)}, u32[]{:S(2)}) collective-permute-start(bf16[2,256,256]{2,1,0:T(8,128)(2,1)S(1)} %collective-permute-done.13), channel_id=1, source_target_pairs={{0,4},{4,8},{8,12},{12,0},{1,5},{5,9},{9,13},{13,1},{2,6},{6,10},{... | collective-permute-start | bytes 786440 | tf_op jit(solution)/shard_map/kv_ring/ppermute | solution.py:247
  138.7 7.4 %collective-permute-start.16 = (bf16[2,256,256]{2,1,0:T(8,128)(2,1)S(1)}, bf16[2,256,256]{2,1,0:T(8,128)(2,1)S(1)}, u32[]{:S(2)}, u32[]{:S(2)}) collective-permute-start(bf16[2,256,256]{2,1,0:T(8,128)(2,1)S(1)} %collective-permute-done.14), channel_id=1, source_target_pairs={{4,0},{8,4},{12,8},{0,12},{5,1},{9,5},{13,9},{1,13},{6,2},{10,6},{... | collective-permute-start | bytes 786440 | tf_op jit(solution)/shard_map/kv_ring/ppermute | solution.py:248
  150.5 6.7 %collective-permute-start.17 = (bf16[128,256]{0,1:T(8,128)(2,1)S(1)}, bf16[128,256]{0,1:T(8,128)(2,1)S(1)}, u32[]{:S(2)}, u32[]{:S(2)}) collective-permute-start(bf16[128,256]{0,1:T(8,128)(2,1)S(1)} %bitcast.319), channel_id=1, source_target_pairs={{0,1},{1,2},{2,3},{3,0},{4,5},{5,6},{6,7},{7,4},{8,9},{9,10},{10,1... | collective-permute-start | bytes 196616 | tf_op jit(solution)/shard_map/out_projection/ppermute | solution.py:272
  152.0 6.4 %collective-permute-start.24 = (bf16[128,256]{0,1:T(8,128)(2,1)S(1)}, bf16[128,256]{0,1:T(8,128)(2,1)S(1)}, u32[]{:S(2)}, u32[]{:S(2)}) collective-permute-start(bf16[128,256]{0,1:T(8,128)(2,1)S(1)} %bitcast.318), channel_id=1, source_target_pairs={{0,3},{1,0},{2,1},{3,2},{4,7},{5,4},{6,5},{7,6},{8,11},{9,8},{10,9... | collective-permute-start | bytes 196616 | tf_op jit(solution)/shard_map/out_projection/ppermute | solution.py:272
  155.9 5.4 %collective-permute-start.22 = (bf16[128,256]{0,1:T(8,128)(2,1)S(1)}, bf16[128,256]{0,1:T(8,128)(2,1)S(1)}, u32[]{:S(2)}, u32[]{:S(2)}) collective-permute-start(bf16[128,256]{0,1:T(8,128)(2,1)S(1)} %bitcast.317), channel_id=1, source_target_pairs={{0,2},{1,3},{2,0},{3,1},{4,6},{5,7},{6,4},{7,5},{8,10},{9,11},{10,... | collective-permute-start | bytes 196616 | tf_op jit(solution)/shard_map/out_projection/ppermute | solution.py:272
  163.6 5.4 %collective-permute-start.27 = (bf16[8,256]{1,0:T(8,128)(2,1)S(1)}, bf16[8,256]{1,0:T(8,128)(2,1)S(1)}, u32[]{:S(2)}, u32[]{:S(2)}) collective-permute-start(bf16[8,256]{1,0:T(8,128)(2,1)S(1)} %get-tuple-element.59), channel_id=1, source_target_pairs={{0,1},{1,2},{2,3},{3,0},{4,5},{5,6},{6,7},{7,4},{8,9},{9,10},{10,1... | collective-permute-start | bytes 12296 | tf_op jit(solution)/shard_map/sides_gather/ppermute | solution.py:153
  163.6 5.4 %collective-permute-start.28 = (bf16[8,256]{1,0:T(8,128)(2,1)S(1)}, bf16[8,256]{1,0:T(8,128)(2,1)S(1)}, u32[]{:S(2)}, u32[]{:S(2)}) collective-permute-start(bf16[8,256]{1,0:T(8,128)(2,1)S(1)} %get-tuple-element.59), channel_id=1, source_target_pairs={{0,2},{1,3},{2,0},{3,1},{4,6},{5,7},{6,4},{7,5},{8,10},{9,11},{10,... | collective-permute-start | bytes 12296 | tf_op jit(solution)/shard_map/sides_gather/ppermute | solution.py:153
  166.9 3.6 %collective-permute-start.29 = (bf16[8,256]{1,0:T(8,128)(2,1)S(1)}, bf16[8,256]{1,0:T(8,128)(2,1)S(1)}, u32[]{:S(2)}, u32[]{:S(2)}) collective-permute-start(bf16[8,256]{1,0:T(8,128)(2,1)S(1)} %get-tuple-element.59), channel_id=1, source_target_pairs={{0,3},{1,0},{2,1},{3,2},{4,7},{5,4},{6,5},{7,6},{8,11},{9,8},{10,9... | collective-permute-start | bytes 12296 | tf_op jit(solution)/shard_map/sides_gather/ppermute | solution.py:153
  170.5 3.2 %collective-permute-start.30 = (bf16[32,256]{1,0:T(8,128)(2,1)S(1)}, bf16[32,256]{1,0:T(8,128)(2,1)S(1)}, u32[]{:S(2)}, u32[]{:S(2)}) collective-permute-start(bf16[32,256]{1,0:T(8,128)(2,1)S(1)} %bitcast.314), channel_id=1, source_target_pairs={{0,4},{4,8},{8,12},{12,0},{1,5},{5,9},{9,13},{13,1},{2,6},{6,10},{... | collective-permute-start | bytes 49160 | tf_op jit(solution)/shard_map/sides_gather/ppermute | solution.py:153
  170.5 3.8 %collective-permute-start.31 = (bf16[32,256]{1,0:T(8,128)(2,1)S(1)}, bf16[32,256]{1,0:T(8,128)(2,1)S(1)}, u32[]{:S(2)}, u32[]{:S(2)}) collective-permute-start(bf16[32,256]{1,0:T(8,128)(2,1)S(1)} %bitcast.315), channel_id=1, source_target_pairs={{0,8},{4,12},{8,0},{12,4},{1,9},{5,13},{9,1},{13,5},{2,10},{6,14},... | collective-permute-start | bytes 49160 | tf_op jit(solution)/shard_map/sides_gather/ppermute | solution.py:153
  (11 other events, 195.9 us)

commit v17 on v14

--- a/solution.py
+++ b/solution.py
@@ -246,33 +246,35 @@
         if rotated and seq_count % 2 == 0:
             me = lax.axis_index("pair")
             core = lax.axis_index("seq") % 2
-            half = w_out.shape[1] // 2
-            mine_w = lax.dynamic_slice_in_dim(late_w_out, core * half, half, 1)
-            other_w = lax.dynamic_slice_in_dim(late_w_out, (1 - core) * half, half, 1)
-            fetched = line_flows(mine_w, "pair")
-            swapped_w = lax.ppermute(
-                jnp.stack(fetched), "seq", [(i, i ^ 1) for i in range(seq_count)]
-            )
+            ways = []
+            for s_i in range(seq_count):
+                for p_i in range(pair_count):
+                    src = s_i * pair_count + p_i
+                    if s_i % 2 == 0 and p_i + 1 < pair_count:
+                        ways.append((src, src + 1))
+                    if s_i % 2 == 1 and p_i > 0:
+                        ways.append((src, src - 1))
+            flow = late_w_out
+            received = []
+            for step in range(1, pair_count):
+                flow = lax.ppermute(flow, ("seq", "pair"), ways)
+                received.append(flow)
+            received = jnp.stack(received)
+            swapped_w = lax.ppermute(received, "seq", [(i, i ^ 1) for i in range(seq_count)])
+            from_left = jnp.where(core == 0, received, swapped_w)
+            from_right = jnp.where(core == 0, swapped_w, received)
             pieces = attended.reshape(pair_count, row_count, attended.shape[1])
-            mixed_mine = jnp.dot(pieces[0], mine_w, preferred_element_type=jnp.float32)
-            mixed_other = jnp.dot(pieces[0], other_w, preferred_element_type=jnp.float32)
+            mixed = jnp.dot(pieces[0], late_w_out, preferred_element_type=jnp.float32)
             for shift in range(1, pair_count):
                 incoming = lax.ppermute(
                     pieces[pair_count - shift],
                     "pair",
                     [(i, (i + shift) % pair_count) for i in range(pair_count)],
                 )
-                mixed_mine = mixed_mine + jnp.dot(
-                    incoming, fetched[shift - 1], preferred_element_type=jnp.float32
+                block = jnp.where(
+                    me >= shift, from_left[shift - 1], from_right[pair_count - shift - 1]
                 )
-                mixed_other = mixed_other + jnp.dot(
-                    incoming, swapped_w[shift - 1], preferred_element_type=jnp.float32
-                )
-            mixed = jnp.where(
-                core == 0,
-                jnp.concatenate([mixed_mine, mixed_other], 1),
-                jnp.concatenate([mixed_other, mixed_mine], 1),
-            )
+                mixed = mixed + jnp.dot(incoming, block, preferred_element_type=jnp.float32)
         else:
             full_w_out = gather_weight_rows(late_w_out, "pair", "seq")
             own_heads = rows_to_heads(attended, "pair")

time: 174 us -> 167 us (0.960)
  waiting for transfers between devices: 73.6 us -> 70.7 us
  starting transfers between devices: 70.1 us -> 67.8 us
    ppermute x3, waiting for transfers between devices: 26.8 us -> 18.9 us  [rotated_all_gather(): lax.ppermute(value, axis, [(i, (i + shift) % n) for i in range(n)])]
    ppermute x3, waiting for transfers between devices: 5.2 us -> 0.32 us  [shards(): next_coming = lax.ppermute(coming, 'seq', backward)]
    ppermute x7 -> x4, waiting for transfers between devices: 0.02 us -> 4.6 us  [the longest x3 4.6 us: shards(): flow = lax.ppermute(flow, ('seq', 'pair'), ways)]
    ppermute x3, waiting for transfers between devices: 6.7 us -> 10.6 us  [shards(): next_going = lax.ppermute(going, 'seq', forward)]
    ppermute x3, waiting for transfers between devices: 20 us -> 22.6 us  [direct_reduce_scatter(): lax.ppermute(outgoing, axis, [(i, (i + shift) % n) for i in range(n)])]
    ppermute x7 -> x4, starting transfers between devices: 25.5 us -> 22.9 us  [the longest x3 22 us: shards(): flow = lax.ppermute(flow, ('seq', 'pair'), ways)]
    ppermute x3, starting transfers between devices: 6.86 us -> 4.88 us  [direct_reduce_scatter(): lax.ppermute(outgoing, axis, [(i, (i + shift) % n) for i in range(n)])]
  transfers between devices with their start and end apart: 33 -> 30, of which waited for: 19 -> 20; matrix products, arithmetic and copies ran while one was open for 14% -> 11% of each run, Pallas kernels for 0% -> 0%
where the time goes in v17:
time: 167 us; the launch traced here: 166 us
  waiting for transfers between devices  70.7 us (42%)
  starting transfers between devices  67.8 us (41%)
  matrix products  19 us (11%)
  other arithmetic  6 us (4%)
    ppermute x3, waiting for transfers between devices, direct_reduce_scatter(): lax.ppermute(outgoing, axis, [(i, (i + shift) % n) for i in range(n)])  22.6 us
    ppermute x3, starting transfers between devices, shards(): flow = lax.ppermute(flow, ('seq', 'pair'), ways)  22 us
    ppermute x3, waiting for transfers between devices, rotated_all_gather(): lax.ppermute(value, axis, [(i, (i + shift) % n) for i in range(n)])  18.9 us
    ppermute x3, waiting for transfers between devices, shards(): next_going = lax.ppermute(going, 'seq', forward)  10.6 us
    ppermute x3, starting transfers between devices, rotated_all_gather(): lax.ppermute(value, axis, [(i, (i + shift) % n) for i in range(n)])  10.4 us
    ppermute x3, starting transfers between devices, permute_all_to_all(): lax.ppermute(outgoing, axis, [(i, (i + shift) % n) for i in range(n)])  7.13 us
    dot_general x5, matrix products, conv_rows(): jnp.dot(shifted, conv_weight[offset], preferred_element_type=jnp.float32)  6.46 us
    ppermute x6, starting transfers between devices, direct_all_gather(): lax.ppermute(value, axis, [(i, (i + shift) % n) for i in range(n)])  6.45 us
  transfers between devices with their start and end apart: 30, of which 20 were waited for; matrix products, arithmetic and copies ran while one was open for 11% of the time, Pallas kernels for 0%

profile of v17, /device:TPU:0, one launch (start us, length us, event | category | flops | bytes accessed | tf_op | source)
XLA Modules:
  0.0 166.3 jit_solution(14587472225538642734)
XLA Ops:
  4.1 3.1 %collective-permute-start = (bf16[128,384]{1,0:T(8,128)(2,1)S(1)}, bf16[128,384]{1,0:T(8,128)(2,1)S(1)}, u32[]{:S(2)}, u32[]{:S(2)}) collective-permute-start(bf16[128,384]{1,0:T(8,128)(2,1)S(1)} %bitcast.306), channel_id=1, source_target_pairs={{0,1},{1,2},{2,3},{3,0},{4,5},{5,6},{6,7},{7,4},{8,9},{9,10},{10,1... | collective-permute-start | bytes 294920 | tf_op jit(solution)/shard_map/ppermute | solution.py:65
  7.2 2.7 %collective-permute-start.1 = (bf16[128,384]{1,0:T(8,128)(2,1)S(1)}, bf16[128,384]{1,0:T(8,128)(2,1)S(1)}, u32[]{:S(2)}, u32[]{:S(2)}) collective-permute-start(bf16[128,384]{1,0:T(8,128)(2,1)S(1)} %bitcast.305), channel_id=1, source_target_pairs={{0,2},{1,3},{2,0},{3,1},{4,6},{5,7},{6,4},{7,5},{8,10},{9,11},{10,... | collective-permute-start | bytes 294920 | tf_op jit(solution)/shard_map/ppermute | solution.py:65
  11.4 1.5 collective-permute-done
  12.9 3.5 %collective-permute-done.1 = bf16[128,384]{1,0:T(8,128)(2,1)S(1)} collective-permute-done((bf16[128,384]{1,0:T(8,128)(2,1)S(1)}, bf16[128,384]{1,0:T(8,128)(2,1)S(1)}, u32[]{:S(2)}, u32[]{:S(2)}) %collective-permute-start.1) | collective-permute-done | bytes 98336 | tf_op jit(solution)/shard_map/ppermute | solution.py:65
  16.6 1.7 %collective-permute-start.3 = (bf16[8,384]{1,0:T(8,128)(2,1)S(1)}, bf16[8,384]{1,0:T(8,128)(2,1)S(1)}, u32[]{:S(2)}, u32[]{:S(2)}) collective-permute-start(bf16[8,384]{1,0:T(8,128)(2,1)S(1)} %get-tuple-element.27), channel_id=1, source_target_pairs={{0,4},{4,8},{8,12},{1,5},{5,9},{9,13},{2,6},{6,10},{10,14},{3,7},{... | collective-permute-start | bytes 18440 | tf_op jit(solution)/shard_map/ppermute | solution.py:25
  18.3 1.6 collective-permute-start.4
  19.9 2.4 %fusion.42 = f32[512,1536]{1,0:T(8,128)S(1)} fusion(bf16[512,384]{1,0:T(8,128)(2,1)S(1)} %bitcast.287, bf16[5,384,1536]{2,1,0:T(8,128)(2,1)} %param.12), kind=kOutput, calls=%fused_computation.68 | convolution fusion | flops 603979776 | bytes 4718592 | tf_op jit(solution)/shard_map/conv_reduce/dot_general | solution.py:39
  27.4 2.4 %collective-permute-start.5 = (bf16[128,1536]{1,0:T(8,128)(2,1)S(1)}, bf16[128,1536]{1,0:T(8,128)(2,1)S(1)}, u32[]{:S(2)}, u32[]{:S(2)}) collective-permute-start(bf16[128,1536]{1,0:T(8,128)(2,1)S(1)} %get-tuple-element.22), channel_id=1, source_target_pairs={{0,1},{1,2},{2,3},{3,0},{4,5},{5,6},{6,7},{7,4},{8,9},{9,10},{10,1... | collective-permute-start | bytes 1179656 | tf_op jit(solution)/shard_map/conv_reduce/ppermute | solution.py:51
  29.8 1.7 %collective-permute-start.6 = (bf16[128,1536]{1,0:T(8,128)(2,1)S(1)}, bf16[128,1536]{1,0:T(8,128)(2,1)S(1)}, u32[]{:S(2)}, u32[]{:S(2)}) collective-permute-start(bf16[128,1536]{1,0:T(8,128)(2,1)S(1)} %get-tuple-element.24), channel_id=1, source_target_pairs={{0,2},{1,3},{2,0},{3,1},{4,6},{5,7},{6,4},{7,5},{8,10},{9,11},{10,... | collective-permute-start | bytes 1179656 | tf_op jit(solution)/shard_map/conv_reduce/ppermute | solution.py:51
  32.3 3.2 %collective-permute-start.18 = (bf16[256,1536]{1,0:T(8,128)(2,1)}, bf16[256,1536]{1,0:T(8,128)(2,1)S(1)}, u32[]{:S(2)}, u32[]{:S(2)}) collective-permute-start(bf16[256,1536]{1,0:T(8,128)(2,1)} %param.15), channel_id=1, source_target_pairs={{0,1},{1,2},{2,3},{5,4},{6,5},{7,6},{8,9},{9,10},{10,11},{13,12},{... | collective-permute-start | bytes 2359304 | tf_op jit(solution)/shard_map/out_projection/ppermute | solution.py:260
  35.5 4.6 %collective-permute-done.5 = bf16[128,1536]{1,0:T(8,128)(2,1)S(1)} collective-permute-done((bf16[128,1536]{1,0:T(8,128)(2,1)S(1)}, bf16[128,1536]{1,0:T(8,128)(2,1)S(1)}, u32[]{:S(2)}, u32[]{:S(2)}) %collective-permute-start.5) | collective-permute-done | bytes 393248 | tf_op jit(solution)/shard_map/conv_reduce/ppermute | solution.py:51
  40.1 18.0 %collective-permute-done.6 = bf16[128,1536]{1,0:T(8,128)(2,1)S(1)} collective-permute-done((bf16[128,1536]{1,0:T(8,128)(2,1)S(1)}, bf16[128,1536]{1,0:T(8,128)(2,1)S(1)}, u32[]{:S(2)}, u32[]{:S(2)}) %collective-permute-start.6) | collective-permute-done | bytes 393248 | tf_op jit(solution)/shard_map/conv_reduce/ppermute | solution.py:51
  59.4 7.8 %collective-permute-start.10 = (bf16[128,1536]{1,0:T(8,128)(2,1)}, bf16[128,1536]{1,0:T(8,128)(2,1)}, u32[]{:S(2)}, u32[]{:S(2)}) collective-permute-start(bf16[128,1536]{1,0:T(8,128)(2,1)} %fusion.74), channel_id=1, source_target_pairs={{0,3},{1,0},{2,1},{3,2},{4,7},{5,4},{6,5},{7,6},{8,11},{9,8},{10,9... | collective-permute-start | bytes 1179656 | tf_op jit(solution)/shard_map/attn_in_gather/ppermute | solution.py:141
  68.4 1.5 collective-permute-start.9
  69.8 16.7 %collective-permute-start.19 = (bf16[256,1536]{1,0:T(8,128)(2,1)S(1)}, bf16[256,1536]{1,0:T(8,128)(2,1)S(1)}, u32[]{:S(2)}, u32[]{:S(2)}) collective-permute-start(bf16[256,1536]{1,0:T(8,128)(2,1)S(1)} %collective-permute-done.18), channel_id=1, source_target_pairs={{0,1},{1,2},{2,3},{5,4},{6,5},{7,6},{8,9},{9,10},{10,11},{13,12},{... | collective-permute-start | bytes 2359304 | tf_op jit(solution)/shard_map/out_projection/ppermute | solution.py:260
  87.0 18.4 %collective-permute-done.9 = bf16[128,1536]{1,0:T(8,128)(2,1)} collective-permute-done((bf16[128,1536]{1,0:T(8,128)(2,1)}, bf16[128,1536]{1,0:T(8,128)(2,1)}, u32[]{:S(2)}, u32[]{:S(2)}) %collective-permute-start.9) | collective-permute-done | bytes 393248 | tf_op jit(solution)/shard_map/attn_in_gather/ppermute | solution.py:141
  105.5 2.7 %fusion.14 = bf16[512,768]{1,0:T(8,128)(2,1)S(1)} fusion(bf16[1536,768]{1,0:T(8,128)(2,1)S(1)} %copy-done, bf16[128,1536]{1,0:T(8,128)(2,1)} %collective-permute-done.10, bf16[128,1536]{1,0:T(8,128)(2,1)} %collective-permute-done.9, bf16[128,1536]{1,0:T(8,128)(2,1)} %collective-permute-done.8, bf16[128,1536]{1,0:T(8,128)(2,1)} %fusion.74), kind=kOutput, calls=%fused_computation.20 | convolution fusion | flops 1214644224 | bytes 4718592 | tf_op jit(solution)/shard_map/dot_general | solution.py:194
  108.3 3.3 %collective-permute-start.11 = (bf16[2,256,256]{2,1,0:T(8,128)(2,1)S(1)}, bf16[2,256,256]{2,1,0:T(8,128)(2,1)S(1)}, u32[]{:S(2)}, u32[]{:S(2)}) collective-permute-start(bf16[2,256,256]{2,1,0:T(8,128)(2,1)S(1)} %get-tuple-element.25), channel_id=1, source_target_pairs={{0,4},{4,8},{8,12},{12,0},{1,5},{5,9},{9,13},{13,1},{2,6},{6,10},{... | collective-permute-start | bytes 786440 | tf_op jit(solution)/shard_map/kv_ring/ppermute | solution.py:235
  112.9 4.4 %collective-permute-done.11 = bf16[2,256,256]{2,1,0:T(8,128)(2,1)S(1)} collective-permute-done((bf16[2,256,256]{2,1,0:T(8,128)(2,1)S(1)}, bf16[2,256,256]{2,1,0:T(8,128)(2,1)S(1)}, u32[]{:S(2)}, u32[]{:S(2)}) %collective-permute-start.11) | collective-permute-done | bytes 262176 | tf_op jit(solution)/shard_map/kv_ring/ppermute | solution.py:235
  117.7 1.8 %collective-permute-start.14 = (bf16[2,256,256]{2,1,0:T(8,128)(2,1)S(1)}, bf16[2,256,256]{2,1,0:T(8,128)(2,1)S(1)}, u32[]{:S(2)}, u32[]{:S(2)}) collective-permute-start(bf16[2,256,256]{2,1,0:T(8,128)(2,1)S(1)} %collective-permute-done.12), channel_id=1, source_target_pairs={{4,0},{8,4},{12,8},{0,12},{5,1},{9,5},{13,9},{1,13},{6,2},{10,6},{... | collective-permute-start | bytes 786440 | tf_op jit(solution)/shard_map/kv_ring/ppermute | solution.py:236
  119.8 4.4 %collective-permute-done.13 = bf16[2,256,256]{2,1,0:T(8,128)(2,1)S(1)} collective-permute-done((bf16[2,256,256]{2,1,0:T(8,128)(2,1)S(1)}, bf16[2,256,256]{2,1,0:T(8,128)(2,1)S(1)}, u32[]{:S(2)}, u32[]{:S(2)}) %collective-permute-start.13) | collective-permute-done | bytes 262176 | tf_op jit(solution)/shard_map/kv_ring/ppermute | solution.py:235
  124.8 1.9 %collective-permute-start.16 = (bf16[2,256,256]{2,1,0:T(8,128)(2,1)S(1)}, bf16[2,256,256]{2,1,0:T(8,128)(2,1)S(1)}, u32[]{:S(2)}, u32[]{:S(2)}) collective-permute-start(bf16[2,256,256]{2,1,0:T(8,128)(2,1)S(1)} %collective-permute-done.14), channel_id=1, source_target_pairs={{4,0},{8,4},{12,8},{0,12},{5,1},{9,5},{13,9},{1,13},{6,2},{10,6},{... | collective-permute-start | bytes 786440 | tf_op jit(solution)/shard_map/kv_ring/ppermute | solution.py:236
  126.7 2.0 %collective-permute-start.20 = (bf16[256,1536]{1,0:T(8,128)(2,1)S(1)}, bf16[256,1536]{1,0:T(8,128)(2,1)S(1)}, u32[]{:S(2)}, u32[]{:S(2)}) collective-permute-start(bf16[256,1536]{1,0:T(8,128)(2,1)S(1)} %collective-permute-done.19), channel_id=1, source_target_pairs={{0,1},{1,2},{2,3},{5,4},{6,5},{7,6},{8,9},{9,10},{10,11},{13,12},{... | collective-permute-start | bytes 2359304 | tf_op jit(solution)/shard_map/out_projection/ppermute | solution.py:260
  128.8 1.8 %collective-permute-done.15 = bf16[2,256,256]{2,1,0:T(8,128)(2,1)S(1)} collective-permute-done((bf16[2,256,256]{2,1,0:T(8,128)(2,1)S(1)}, bf16[2,256,256]{2,1,0:T(8,128)(2,1)S(1)}, u32[]{:S(2)}, u32[]{:S(2)}) %collective-permute-start.15) | collective-permute-done | bytes 262176 | tf_op jit(solution)/shard_map/kv_ring/ppermute | solution.py:235
  133.4 4.6 %collective-permute-done.20 = bf16[256,1536]{1,0:T(8,128)(2,1)S(1)} collective-permute-done((bf16[256,1536]{1,0:T(8,128)(2,1)S(1)}, bf16[256,1536]{1,0:T(8,128)(2,1)S(1)}, u32[]{:S(2)}, u32[]{:S(2)}) %collective-permute-start.20) | collective-permute-done | bytes 786464 | tf_op jit(solution)/shard_map/out_projection/ppermute | solution.py:260
  141.4 1.6 collective-permute-start.17
  143.0 3.0 %collective-permute-start.23 = (bf16[128,256]{0,1:T(8,128)(2,1)S(1)}, bf16[128,256]{0,1:T(8,128)(2,1)S(1)}, u32[]{:S(2)}, u32[]{:S(2)}) collective-permute-start(bf16[128,256]{0,1:T(8,128)(2,1)S(1)} %bitcast.311), channel_id=1, source_target_pairs={{0,3},{1,0},{2,1},{3,2},{4,7},{5,4},{6,5},{7,6},{8,11},{9,8},{10,9... | collective-permute-start | bytes 196616 | tf_op jit(solution)/shard_map/out_projection/ppermute | solution.py:269
  146.5 1.4 fusion.176
  149.6 3.4 %collective-permute-done.22 = bf16[128,256]{0,1:T(8,128)(2,1)S(1)} collective-permute-done((bf16[128,256]{0,1:T(8,128)(2,1)S(1)}, bf16[128,256]{0,1:T(8,128)(2,1)S(1)}, u32[]{:S(2)}, u32[]{:S(2)}) %collective-permute-start.22) | collective-permute-done | bytes 65568 | tf_op jit(solution)/shard_map/out_projection/ppermute | solution.py:269
  154.5 2.8 %collective-permute-start.25 = (bf16[8,256]{1,0:T(8,128)(2,1)S(1)}, bf16[8,256]{1,0:T(8,128)(2,1)S(1)}, u32[]{:S(2)}, u32[]{:S(2)}) collective-permute-start(bf16[8,256]{1,0:T(8,128)(2,1)S(1)} %get-tuple-element.61), channel_id=1, source_target_pairs={{0,2},{1,3},{2,0},{3,1},{4,6},{5,7},{6,4},{7,5},{8,10},{9,11},{10,... | collective-permute-start | bytes 12296 | tf_op jit(solution)/shard_map/sides_gather/ppermute | solution.py:153
  158.3 1.6 collective-permute-done.24
  162.1 1.4 collective-permute-start.29
  (115 shorter events, 32.3 us)
Async XLA Ops:
  0.6 104.8 %copy-start = (bf16[1536,768]{1,0:T(8,128)(2,1)S(1)}, bf16[1536,768]{1,0:T(8,128)(2,1)}, u32[]{:S(2)}) copy-start(bf16[1536,768]{1,0:T(8,128)(2,1)} %param.14) | copy-start | bytes 7077892
  4.1 8.7 %collective-permute-start = (bf16[128,384]{1,0:T(8,128)(2,1)S(1)}, bf16[128,384]{1,0:T(8,128)(2,1)S(1)}, u32[]{:S(2)}, u32[]{:S(2)}) collective-permute-start(bf16[128,384]{1,0:T(8,128)(2,1)S(1)} %bitcast.306), channel_id=1, source_target_pairs={{0,1},{1,2},{2,3},{3,0},{4,5},{5,6},{6,7},{7,4},{8,9},{9,10},{10,1... | collective-permute-start | bytes 294920 | tf_op jit(solution)/shard_map/ppermute | solution.py:65
  7.2 9.2 %collective-permute-start.1 = (bf16[128,384]{1,0:T(8,128)(2,1)S(1)}, bf16[128,384]{1,0:T(8,128)(2,1)S(1)}, u32[]{:S(2)}, u32[]{:S(2)}) collective-permute-start(bf16[128,384]{1,0:T(8,128)(2,1)S(1)} %bitcast.305), channel_id=1, source_target_pairs={{0,2},{1,3},{2,0},{3,1},{4,6},{5,7},{6,4},{7,5},{8,10},{9,11},{10,... | collective-permute-start | bytes 294920 | tf_op jit(solution)/shard_map/ppermute | solution.py:65
  9.9 6.7 %collective-permute-start.2 = (bf16[128,384]{1,0:T(8,128)(2,1)S(1)}, bf16[128,384]{1,0:T(8,128)(2,1)S(1)}, u32[]{:S(2)}, u32[]{:S(2)}) collective-permute-start(bf16[128,384]{1,0:T(8,128)(2,1)S(1)} %bitcast.304), channel_id=1, source_target_pairs={{0,3},{1,0},{2,1},{3,2},{4,7},{5,4},{6,5},{7,6},{8,11},{9,8},{10,9... | collective-permute-start | bytes 294920 | tf_op jit(solution)/shard_map/ppermute | solution.py:65
  16.6 8.5 %collective-permute-start.3 = (bf16[8,384]{1,0:T(8,128)(2,1)S(1)}, bf16[8,384]{1,0:T(8,128)(2,1)S(1)}, u32[]{:S(2)}, u32[]{:S(2)}) collective-permute-start(bf16[8,384]{1,0:T(8,128)(2,1)S(1)} %get-tuple-element.27), channel_id=1, source_target_pairs={{0,4},{4,8},{8,12},{1,5},{5,9},{9,13},{2,6},{6,10},{10,14},{3,7},{... | collective-permute-start | bytes 18440 | tf_op jit(solution)/shard_map/ppermute | solution.py:25
  18.3 4.8 %collective-permute-start.4 = (bf16[8,384]{1,0:T(8,128)(2,1)S(1)}, bf16[8,384]{1,0:T(8,128)(2,1)S(1)}, u32[]{:S(2)}, u32[]{:S(2)}) collective-permute-start(bf16[8,384]{1,0:T(8,128)(2,1)S(1)} %get-tuple-element.28), channel_id=1, source_target_pairs={{4,0},{8,4},{12,8},{5,1},{9,5},{13,9},{6,2},{10,6},{14,10},{7,3},{... | collective-permute-start | bytes 18440 | tf_op jit(solution)/shard_map/ppermute | solution.py:26
  27.2 31.3 %copy-start.4 = (f32[1536]{0:T(1024)S(1)}, f32[1536]{0:T(1024)}, u32[]{:S(2)}) copy-start(f32[1536]{0:T(1024)} %param.13) | copy-start | bytes 18436
  27.4 12.7 %collective-permute-start.5 = (bf16[128,1536]{1,0:T(8,128)(2,1)S(1)}, bf16[128,1536]{1,0:T(8,128)(2,1)S(1)}, u32[]{:S(2)}, u32[]{:S(2)}) collective-permute-start(bf16[128,1536]{1,0:T(8,128)(2,1)S(1)} %get-tuple-element.22), channel_id=1, source_target_pairs={{0,1},{1,2},{2,3},{3,0},{4,5},{5,6},{6,7},{7,4},{8,9},{9,10},{10,1... | collective-permute-start | bytes 1179656 | tf_op jit(solution)/shard_map/conv_reduce/ppermute | solution.py:51
  29.8 28.3 %collective-permute-start.6 = (bf16[128,1536]{1,0:T(8,128)(2,1)S(1)}, bf16[128,1536]{1,0:T(8,128)(2,1)S(1)}, u32[]{:S(2)}, u32[]{:S(2)}) collective-permute-start(bf16[128,1536]{1,0:T(8,128)(2,1)S(1)} %get-tuple-element.24), channel_id=1, source_target_pairs={{0,2},{1,3},{2,0},{3,1},{4,6},{5,7},{6,4},{7,5},{8,10},{9,11},{10,... | collective-permute-start | bytes 1179656 | tf_op jit(solution)/shard_map/conv_reduce/ppermute | solution.py:51
  31.5 26.6 %collective-permute-start.7 = (bf16[128,1536]{1,0:T(8,128)(2,1)S(1)}, bf16[128,1536]{1,0:T(8,128)(2,1)S(1)}, u32[]{:S(2)}, u32[]{:S(2)}) collective-permute-start(bf16[128,1536]{1,0:T(8,128)(2,1)S(1)} %get-tuple-element.23), channel_id=1, source_target_pairs={{0,3},{1,0},{2,1},{3,2},{4,7},{5,4},{6,5},{7,6},{8,11},{9,8},{10,9... | collective-permute-start | bytes 1179656 | tf_op jit(solution)/shard_map/conv_reduce/ppermute | solution.py:51
  32.3 37.6 %collective-permute-start.18 = (bf16[256,1536]{1,0:T(8,128)(2,1)}, bf16[256,1536]{1,0:T(8,128)(2,1)S(1)}, u32[]{:S(2)}, u32[]{:S(2)}) collective-permute-start(bf16[256,1536]{1,0:T(8,128)(2,1)} %param.15), channel_id=1, source_target_pairs={{0,1},{1,2},{2,3},{5,4},{6,5},{7,6},{8,9},{9,10},{10,11},{13,12},{... | collective-permute-start | bytes 2359304 | tf_op jit(solution)/shard_map/out_projection/ppermute | solution.py:260
  59.4 27.1 %collective-permute-start.10 = (bf16[128,1536]{1,0:T(8,128)(2,1)}, bf16[128,1536]{1,0:T(8,128)(2,1)}, u32[]{:S(2)}, u32[]{:S(2)}) collective-permute-start(bf16[128,1536]{1,0:T(8,128)(2,1)} %fusion.74), channel_id=1, source_target_pairs={{0,3},{1,0},{2,1},{3,2},{4,7},{5,4},{6,5},{7,6},{8,11},{9,8},{10,9... | collective-permute-start | bytes 1179656 | tf_op jit(solution)/shard_map/attn_in_gather/ppermute | solution.py:141
  67.2 19.8 %collective-permute-start.8 = (bf16[128,1536]{1,0:T(8,128)(2,1)}, bf16[128,1536]{1,0:T(8,128)(2,1)}, u32[]{:S(2)}, u32[]{:S(2)}) collective-permute-start(bf16[128,1536]{1,0:T(8,128)(2,1)} %fusion.74), channel_id=1, source_target_pairs={{0,1},{1,2},{2,3},{3,0},{4,5},{5,6},{6,7},{7,4},{8,9},{9,10},{10,1... | collective-permute-start | bytes 1179656 | tf_op jit(solution)/shard_map/attn_in_gather/ppermute | solution.py:141
  68.4 37.1 %collective-permute-start.9 = (bf16[128,1536]{1,0:T(8,128)(2,1)}, bf16[128,1536]{1,0:T(8,128)(2,1)}, u32[]{:S(2)}, u32[]{:S(2)}) collective-permute-start(bf16[128,1536]{1,0:T(8,128)(2,1)} %fusion.74), channel_id=1, source_target_pairs={{0,2},{1,3},{2,0},{3,1},{4,6},{5,7},{6,4},{7,5},{8,10},{9,11},{10,... | collective-permute-start | bytes 1179656 | tf_op jit(solution)/shard_map/attn_in_gather/ppermute | solution.py:141
  69.8 56.9 %collective-permute-start.19 = (bf16[256,1536]{1,0:T(8,128)(2,1)S(1)}, bf16[256,1536]{1,0:T(8,128)(2,1)S(1)}, u32[]{:S(2)}, u32[]{:S(2)}) collective-permute-start(bf16[256,1536]{1,0:T(8,128)(2,1)S(1)} %collective-permute-done.18), channel_id=1, source_target_pairs={{0,1},{1,2},{2,3},{5,4},{6,5},{7,6},{8,9},{9,10},{10,11},{13,12},{... | collective-permute-start | bytes 2359304 | tf_op jit(solution)/shard_map/out_projection/ppermute | solution.py:260
  108.3 9.0 %collective-permute-start.11 = (bf16[2,256,256]{2,1,0:T(8,128)(2,1)S(1)}, bf16[2,256,256]{2,1,0:T(8,128)(2,1)S(1)}, u32[]{:S(2)}, u32[]{:S(2)}) collective-permute-start(bf16[2,256,256]{2,1,0:T(8,128)(2,1)S(1)} %get-tuple-element.25), channel_id=1, source_target_pairs={{0,4},{4,8},{8,12},{12,0},{1,5},{5,9},{9,13},{13,1},{2,6},{6,10},{... | collective-permute-start | bytes 786440 | tf_op jit(solution)/shard_map/kv_ring/ppermute | solution.py:235
  111.9 5.8 %collective-permute-start.12 = (bf16[2,256,256]{2,1,0:T(8,128)(2,1)S(1)}, bf16[2,256,256]{2,1,0:T(8,128)(2,1)S(1)}, u32[]{:S(2)}, u32[]{:S(2)}) collective-permute-start(bf16[2,256,256]{2,1,0:T(8,128)(2,1)S(1)} %get-tuple-element.26), channel_id=1, source_target_pairs={{4,0},{8,4},{12,8},{0,12},{5,1},{9,5},{13,9},{1,13},{6,2},{10,6},{... | collective-permute-start | bytes 786440 | tf_op jit(solution)/shard_map/kv_ring/ppermute | solution.py:236
  117.4 6.8 %collective-permute-start.13 = (bf16[2,256,256]{2,1,0:T(8,128)(2,1)S(1)}, bf16[2,256,256]{2,1,0:T(8,128)(2,1)S(1)}, u32[]{:S(2)}, u32[]{:S(2)}) collective-permute-start(bf16[2,256,256]{2,1,0:T(8,128)(2,1)S(1)} %collective-permute-done.11), channel_id=1, source_target_pairs={{0,4},{4,8},{8,12},{12,0},{1,5},{5,9},{9,13},{13,1},{2,6},{6,10},{... | collective-permute-start | bytes 786440 | tf_op jit(solution)/shard_map/kv_ring/ppermute | solution.py:235
  117.7 6.8 %collective-permute-start.14 = (bf16[2,256,256]{2,1,0:T(8,128)(2,1)S(1)}, bf16[2,256,256]{2,1,0:T(8,128)(2,1)S(1)}, u32[]{:S(2)}, u32[]{:S(2)}) collective-permute-start(bf16[2,256,256]{2,1,0:T(8,128)(2,1)S(1)} %collective-permute-done.12), channel_id=1, source_target_pairs={{4,0},{8,4},{12,8},{0,12},{5,1},{9,5},{13,9},{1,13},{6,2},{10,6},{... | collective-permute-start | bytes 786440 | tf_op jit(solution)/shard_map/kv_ring/ppermute | solution.py:236
  124.2 6.4 %collective-permute-start.15 = (bf16[2,256,256]{2,1,0:T(8,128)(2,1)S(1)}, bf16[2,256,256]{2,1,0:T(8,128)(2,1)S(1)}, u32[]{:S(2)}, u32[]{:S(2)}) collective-permute-start(bf16[2,256,256]{2,1,0:T(8,128)(2,1)S(1)} %collective-permute-done.13), channel_id=1, source_target_pairs={{0,4},{4,8},{8,12},{12,0},{1,5},{5,9},{9,13},{13,1},{2,6},{6,10},{... | collective-permute-start | bytes 786440 | tf_op jit(solution)/shard_map/kv_ring/ppermute | solution.py:235
  124.8 6.4 %collective-permute-start.16 = (bf16[2,256,256]{2,1,0:T(8,128)(2,1)S(1)}, bf16[2,256,256]{2,1,0:T(8,128)(2,1)S(1)}, u32[]{:S(2)}, u32[]{:S(2)}) collective-permute-start(bf16[2,256,256]{2,1,0:T(8,128)(2,1)S(1)} %collective-permute-done.14), channel_id=1, source_target_pairs={{4,0},{8,4},{12,8},{0,12},{5,1},{9,5},{13,9},{1,13},{6,2},{10,6},{... | collective-permute-start | bytes 786440 | tf_op jit(solution)/shard_map/kv_ring/ppermute | solution.py:236
  126.7 11.3 %collective-permute-start.20 = (bf16[256,1536]{1,0:T(8,128)(2,1)S(1)}, bf16[256,1536]{1,0:T(8,128)(2,1)S(1)}, u32[]{:S(2)}, u32[]{:S(2)}) collective-permute-start(bf16[256,1536]{1,0:T(8,128)(2,1)S(1)} %collective-permute-done.19), channel_id=1, source_target_pairs={{0,1},{1,2},{2,3},{5,4},{6,5},{7,6},{8,9},{9,10},{10,11},{13,12},{... | collective-permute-start | bytes 2359304 | tf_op jit(solution)/shard_map/out_projection/ppermute | solution.py:260
  138.3 9.7 %collective-permute-start.21 = (bf16[3,256,1536]{2,1,0:T(8,128)(2,1)S(1)}, bf16[3,256,1536]{2,1,0:T(8,128)(2,1)S(1)}, u32[]{:S(2)}, u32[]{:S(2)}) collective-permute-start(bf16[3,256,1536]{2,1,0:T(8,128)(2,1)S(1)} %pad_maximum_fusion), channel_id=1, source_target_pairs={{0,4},{4,0},{8,12},{12,8},{1,5},{5,1},{9,13},{13,9},{2,6},{6,2},{1... | collective-permute-start | bytes 7077896 | tf_op jit(solution)/shard_map/out_projection/ppermute | solution.py:263
  141.4 7.4 %collective-permute-start.17 = (bf16[128,256]{0,1:T(8,128)(2,1)S(1)}, bf16[128,256]{0,1:T(8,128)(2,1)S(1)}, u32[]{:S(2)}, u32[]{:S(2)}) collective-permute-start(bf16[128,256]{0,1:T(8,128)(2,1)S(1)} %bitcast.312), channel_id=1, source_target_pairs={{0,1},{1,2},{2,3},{3,0},{4,5},{5,6},{6,7},{7,4},{8,9},{9,10},{10,1... | collective-permute-start | bytes 196616 | tf_op jit(solution)/shard_map/out_projection/ppermute | solution.py:269
  143.0 6.1 %collective-permute-start.23 = (bf16[128,256]{0,1:T(8,128)(2,1)S(1)}, bf16[128,256]{0,1:T(8,128)(2,1)S(1)}, u32[]{:S(2)}, u32[]{:S(2)}) collective-permute-start(bf16[128,256]{0,1:T(8,128)(2,1)S(1)} %bitcast.311), channel_id=1, source_target_pairs={{0,3},{1,0},{2,1},{3,2},{4,7},{5,4},{6,5},{7,6},{8,11},{9,8},{10,9... | collective-permute-start | bytes 196616 | tf_op jit(solution)/shard_map/out_projection/ppermute | solution.py:269
  146.0 6.9 %collective-permute-start.22 = (bf16[128,256]{0,1:T(8,128)(2,1)S(1)}, bf16[128,256]{0,1:T(8,128)(2,1)S(1)}, u32[]{:S(2)}, u32[]{:S(2)}) collective-permute-start(bf16[128,256]{0,1:T(8,128)(2,1)S(1)} %bitcast.310), channel_id=1, source_target_pairs={{0,2},{1,3},{2,0},{3,1},{4,6},{5,7},{6,4},{7,5},{8,10},{9,11},{10,... | collective-permute-start | bytes 196616 | tf_op jit(solution)/shard_map/out_projection/ppermute | solution.py:269
  154.5 5.4 %collective-permute-start.24 = (bf16[8,256]{1,0:T(8,128)(2,1)S(1)}, bf16[8,256]{1,0:T(8,128)(2,1)S(1)}, u32[]{:S(2)}, u32[]{:S(2)}) collective-permute-start(bf16[8,256]{1,0:T(8,128)(2,1)S(1)} %get-tuple-element.61), channel_id=1, source_target_pairs={{0,1},{1,2},{2,3},{3,0},{4,5},{5,6},{6,7},{7,4},{8,9},{9,10},{10,1... | collective-permute-start | bytes 12296 | tf_op jit(solution)/shard_map/sides_gather/ppermute | solution.py:153
  154.5 5.4 %collective-permute-start.25 = (bf16[8,256]{1,0:T(8,128)(2,1)S(1)}, bf16[8,256]{1,0:T(8,128)(2,1)S(1)}, u32[]{:S(2)}, u32[]{:S(2)}) collective-permute-start(bf16[8,256]{1,0:T(8,128)(2,1)S(1)} %get-tuple-element.61), channel_id=1, source_target_pairs={{0,2},{1,3},{2,0},{3,1},{4,6},{5,7},{6,4},{7,5},{8,10},{9,11},{10,... | collective-permute-start | bytes 12296 | tf_op jit(solution)/shard_map/sides_gather/ppermute | solution.py:153
  157.3 3.6 %collective-permute-start.26 = (bf16[8,256]{1,0:T(8,128)(2,1)S(1)}, bf16[8,256]{1,0:T(8,128)(2,1)S(1)}, u32[]{:S(2)}, u32[]{:S(2)}) collective-permute-start(bf16[8,256]{1,0:T(8,128)(2,1)S(1)} %get-tuple-element.61), channel_id=1, source_target_pairs={{0,3},{1,0},{2,1},{3,2},{4,7},{5,4},{6,5},{7,6},{8,11},{9,8},{10,9... | collective-permute-start | bytes 12296 | tf_op jit(solution)/shard_map/sides_gather/ppermute | solution.py:153
  160.9 3.2 %collective-permute-start.27 = (bf16[32,256]{1,0:T(8,128)(2,1)S(1)}, bf16[32,256]{1,0:T(8,128)(2,1)S(1)}, u32[]{:S(2)}, u32[]{:S(2)}) collective-permute-start(bf16[32,256]{1,0:T(8,128)(2,1)S(1)} %bitcast.307), channel_id=1, source_target_pairs={{0,4},{4,8},{8,12},{12,0},{1,5},{5,9},{9,13},{13,1},{2,6},{6,10},{... | collective-permute-start | bytes 49160 | tf_op jit(solution)/shard_map/sides_gather/ppermute | solution.py:153
  160.9 3.8 %collective-permute-start.28 = (bf16[32,256]{1,0:T(8,128)(2,1)S(1)}, bf16[32,256]{1,0:T(8,128)(2,1)S(1)}, u32[]{:S(2)}, u32[]{:S(2)}) collective-permute-start(bf16[32,256]{1,0:T(8,128)(2,1)S(1)} %bitcast.308), channel_id=1, source_target_pairs={{0,8},{4,12},{8,0},{12,4},{1,9},{5,13},{9,1},{13,5},{2,10},{6,14},... | collective-permute-start | bytes 49160 | tf_op jit(solution)/shard_map/sides_gather/ppermute | solution.py:153
  162.1 2.9 %collective-permute-start.29 = (bf16[32,256]{1,0:T(8,128)(2,1)S(1)}, bf16[32,256]{1,0:T(8,128)(2,1)S(1)}, u32[]{:S(2)}, u32[]{:S(2)}) collective-permute-start(bf16[32,256]{1,0:T(8,128)(2,1)S(1)} %bitcast.309), channel_id=1, source_target_pairs={{0,12},{4,0},{8,4},{12,8},{1,13},{5,1},{9,5},{13,9},{2,14},{6,2},{... | collective-permute-start | bytes 49160 | tf_op jit(solution)/shard_map/sides_gather/ppermute | solution.py:153
  (6 other events, 76.2 us)

commit v18 on v17

--- a/solution.py
+++ b/solution.py
@@ -227,17 +227,31 @@
     with jax.named_scope("kv_ring"):
         forward = [(i, (i + 1) % seq_count) for i in range(seq_count)]
         backward = [((i + 1) % seq_count, i) for i in range(seq_count)]
-        half = local_rows // 2
-        going = kv[:, :half]
-        coming = kv[:, half:]
-        for step in range(seq_count):
-            if step + 1 < seq_count:
-                next_going = lax.ppermute(going, "seq", forward)
-                next_coming = lax.ppermute(coming, "seq", backward)
-            state = attend(state, going)
-            state = attend(state, coming)
-            if step + 1 < seq_count:
-                going, coming = next_going, next_coming
+        forward_steps = seq_count // 2
+        backward_steps = seq_count - 1 - forward_steps
+        if seq_count <= 4:
+            going = kv
+            coming = kv
+            state = attend(state, kv)
+            for step in range(forward_steps):
+                going = lax.ppermute(going, "seq", forward)
+                if step < backward_steps:
+                    coming = lax.ppermute(coming, "seq", backward)
+                state = attend(state, going)
+                if step < backward_steps:
+                    state = attend(state, coming)
+        else:
+            half = local_rows // 2
+            going = kv[:, :half]
+            coming = kv[:, half:]
+            for step in range(seq_count):
+                if step + 1 < seq_count:
+                    next_going = lax.ppermute(going, "seq", forward)
+                    next_coming = lax.ppermute(coming, "seq", backward)
+                state = attend(state, going)
+                state = attend(state, coming)
+                if step + 1 < seq_count:
+                    going, coming = next_going, next_coming
     running_max, running_sum, weighted = state
     attended = (weighted / running_sum[:, :, None]).astype(jnp.bfloat16)
     attended = attended.transpose(1, 0, 2).reshape(local_rows, head_count * VALUE_SIZE)

time: 167 us -> 178 us (1.066)
  waiting for transfers between devices: 70.7 us -> 98 us
  starting transfers between devices: 67.8 us -> 49.8 us
  other arithmetic: 6 us -> 8.01 us
    ppermute x3, waiting for transfers between devices: 4.6 us -> 23.7 us  [shards(): flow = lax.ppermute(flow, ('seq', 'pair'), ways)]
    ppermute x3, waiting for transfers between devices: 18.9 us -> 34.4 us  [rotated_all_gather(): lax.ppermute(value, axis, [(i, (i + shift) % n) for i in range(n)])]
    ppermute x6 -> x3, waiting for transfers between devices: 10.9 us -> 0.01 us  [the longest x2 0.01 us: shards(): going = lax.ppermute(going, 'seq', forward)]
    ppermute x3, starting transfers between devices: 22 us -> 12.2 us  [shards(): flow = lax.ppermute(flow, ('seq', 'pair'), ways)]
    ppermute x6 -> x3, starting transfers between devices: 7.68 us -> 0.56 us  [the longest x2 0.56 us: shards(): going = lax.ppermute(going, 'seq', forward)]
    ppermute x3, waiting for transfers between devices: 22.6 us -> 25.8 us  [direct_reduce_scatter(): lax.ppermute(outgoing, axis, [(i, (i + shift) % n) for i in range(n)])]
  transfers between devices with their start and end apart: 30 -> 27, of which waited for: 20 -> 18; matrix products, arithmetic and copies ran while one was open for 11% -> 8% of each run, Pallas kernels for 0% -> 0%
where the time goes in v18:
time: 178 us; the launch traced here: 177 us
  waiting for transfers between devices  98 us (55%)
  starting transfers between devices  49.8 us (28%)
  matrix products  17.3 us (10%)
  other arithmetic  8.01 us (4%)
  local copies, waits for them, and re-layouts  2.67 us (2%)
    ppermute x3, waiting for transfers between devices, rotated_all_gather(): lax.ppermute(value, axis, [(i, (i + shift) % n) for i in range(n)])  34.4 us
    ppermute x3, waiting for transfers between devices, direct_reduce_scatter(): lax.ppermute(outgoing, axis, [(i, (i + shift) % n) for i in range(n)])  25.8 us
    ppermute x3, waiting for transfers between devices, shards(): flow = lax.ppermute(flow, ('seq', 'pair'), ways)  23.7 us
    ppermute x3, starting transfers between devices, shards(): flow = lax.ppermute(flow, ('seq', 'pair'), ways)  12.2 us
    ppermute x3, starting transfers between devices, rotated_all_gather(): lax.ppermute(value, axis, [(i, (i + shift) % n) for i in range(n)])  10.5 us
    ppermute x3, starting transfers between devices, permute_all_to_all(): lax.ppermute(outgoing, axis, [(i, (i + shift) % n) for i in range(n)])  7.13 us
    dot_general x5, matrix products, conv_rows(): jnp.dot(shifted, conv_weight[offset], preferred_element_type=jnp.float32)  6.48 us
    ppermute x3, starting transfers between devices, shards(): lax.ppermute(pieces[pair_count - shift], 'pair', [(i, (i + shift) % pair_...  5.62 us
  transfers between devices with their start and end apart: 27, of which 18 were waited for; matrix products, arithmetic and copies ran while one was open for 8% of the time, Pallas kernels for 0%

profile of v18, /device:TPU:0, one launch (start us, length us, event | category | flops | bytes accessed | tf_op | source)
XLA Modules:
  0.0 177.0 jit_solution(7901399672417882685)
XLA Ops:
  4.1 3.1 %collective-permute-start = (bf16[128,384]{1,0:T(8,128)(2,1)S(1)}, bf16[128,384]{1,0:T(8,128)(2,1)S(1)}, u32[]{:S(2)}, u32[]{:S(2)}) collective-permute-start(bf16[128,384]{1,0:T(8,128)(2,1)S(1)} %bitcast.223), channel_id=1, source_target_pairs={{0,1},{1,2},{2,3},{3,0},{4,5},{5,6},{6,7},{7,4},{8,9},{9,10},{10,1... | collective-permute-start | bytes 294920 | tf_op jit(solution)/shard_map/ppermute | solution.py:65
  7.2 2.7 %collective-permute-start.1 = (bf16[128,384]{1,0:T(8,128)(2,1)S(1)}, bf16[128,384]{1,0:T(8,128)(2,1)S(1)}, u32[]{:S(2)}, u32[]{:S(2)}) collective-permute-start(bf16[128,384]{1,0:T(8,128)(2,1)S(1)} %bitcast.222), channel_id=1, source_target_pairs={{0,2},{1,3},{2,0},{3,1},{4,6},{5,7},{6,4},{7,5},{8,10},{9,11},{10,... | collective-permute-start | bytes 294920 | tf_op jit(solution)/shard_map/ppermute | solution.py:65
  9.9 1.4 collective-permute-start.2
  11.4 1.5 collective-permute-done
  12.9 3.5 %collective-permute-done.1 = bf16[128,384]{1,0:T(8,128)(2,1)S(1)} collective-permute-done((bf16[128,384]{1,0:T(8,128)(2,1)S(1)}, bf16[128,384]{1,0:T(8,128)(2,1)S(1)}, u32[]{:S(2)}, u32[]{:S(2)}) %collective-permute-start.1) | collective-permute-done | bytes 98336 | tf_op jit(solution)/shard_map/ppermute | solution.py:65
  16.6 1.7 collective-permute-start.3
  18.3 1.6 collective-permute-start.4
  19.9 2.4 %fusion.42 = f32[512,1536]{1,0:T(8,128)S(1)} fusion(bf16[512,384]{1,0:T(8,128)(2,1)S(1)} %bitcast.202, bf16[5,384,1536]{2,1,0:T(8,128)(2,1)} %param.12), kind=kOutput, calls=%fused_computation.64 | convolution fusion | flops 603979776 | bytes 4718592 | tf_op jit(solution)/shard_map/conv_reduce/dot_general | solution.py:39
  27.4 2.4 %collective-permute-start.5 = (bf16[128,1536]{1,0:T(8,128)(2,1)S(1)}, bf16[128,1536]{1,0:T(8,128)(2,1)S(1)}, u32[]{:S(2)}, u32[]{:S(2)}) collective-permute-start(bf16[128,1536]{1,0:T(8,128)(2,1)S(1)} %get-tuple-element.14), channel_id=1, source_target_pairs={{0,1},{1,2},{2,3},{3,0},{4,5},{5,6},{6,7},{7,4},{8,9},{9,10},{10,1... | collective-permute-start | bytes 1179656 | tf_op jit(solution)/shard_map/conv_reduce/ppermute | solution.py:51
  29.9 1.7 collective-permute-start.6
  32.3 7.8 %collective-permute-done.5 = bf16[128,1536]{1,0:T(8,128)(2,1)S(1)} collective-permute-done((bf16[128,1536]{1,0:T(8,128)(2,1)S(1)}, bf16[128,1536]{1,0:T(8,128)(2,1)S(1)}, u32[]{:S(2)}, u32[]{:S(2)}) %collective-permute-start.5) | collective-permute-done | bytes 393248 | tf_op jit(solution)/shard_map/conv_reduce/ppermute | solution.py:51
  40.1 17.9 %collective-permute-done.6 = bf16[128,1536]{1,0:T(8,128)(2,1)S(1)} collective-permute-done((bf16[128,1536]{1,0:T(8,128)(2,1)S(1)}, bf16[128,1536]{1,0:T(8,128)(2,1)S(1)}, u32[]{:S(2)}, u32[]{:S(2)}) %collective-permute-start.6) | collective-permute-done | bytes 393248 | tf_op jit(solution)/shard_map/conv_reduce/ppermute | solution.py:51
  58.6 7.8 %collective-permute-start.10 = (bf16[128,1536]{1,0:T(8,128)(2,1)S(1)}, bf16[128,1536]{1,0:T(8,128)(2,1)S(1)}, u32[]{:S(2)}, u32[]{:S(2)}) collective-permute-start(bf16[128,1536]{1,0:T(8,128)(2,1)S(1)} %fusion.70), channel_id=1, source_target_pairs={{0,3},{1,0},{2,1},{3,2},{4,7},{5,4},{6,5},{7,6},{8,11},{9,8},{10,9... | collective-permute-start | bytes 1179656 | tf_op jit(solution)/shard_map/attn_in_gather/ppermute | solution.py:141
  67.7 1.4 collective-permute-start.9
  69.1 8.2 %collective-permute-done.10 = bf16[128,1536]{1,0:T(8,128)(2,1)S(1)} collective-permute-done((bf16[128,1536]{1,0:T(8,128)(2,1)S(1)}, bf16[128,1536]{1,0:T(8,128)(2,1)S(1)}, u32[]{:S(2)}, u32[]{:S(2)}) %collective-permute-start.10) | collective-permute-done | bytes 393248 | tf_op jit(solution)/shard_map/attn_in_gather/ppermute | solution.py:141
  77.3 9.2 %collective-permute-done.8 = bf16[128,1536]{1,0:T(8,128)(2,1)S(1)} collective-permute-done((bf16[128,1536]{1,0:T(8,128)(2,1)S(1)}, bf16[128,1536]{1,0:T(8,128)(2,1)S(1)}, u32[]{:S(2)}, u32[]{:S(2)}) %collective-permute-start.8) | collective-permute-done | bytes 393248 | tf_op jit(solution)/shard_map/attn_in_gather/ppermute | solution.py:141
  86.6 17.0 %collective-permute-done.9 = bf16[128,1536]{1,0:T(8,128)(2,1)S(1)} collective-permute-done((bf16[128,1536]{1,0:T(8,128)(2,1)S(1)}, bf16[128,1536]{1,0:T(8,128)(2,1)S(1)}, u32[]{:S(2)}, u32[]{:S(2)}) %collective-permute-start.9) | collective-permute-done | bytes 393248 | tf_op jit(solution)/shard_map/attn_in_gather/ppermute | solution.py:141
  106.2 2.2 %collective-permute-start.15 = (bf16[256,1536]{1,0:T(8,128)(2,1)S(1)}, bf16[256,1536]{1,0:T(8,128)(2,1)}, u32[]{:S(2)}, u32[]{:S(2)}) collective-permute-start(bf16[256,1536]{1,0:T(8,128)(2,1)S(1)} %copy-done.3), channel_id=1, source_target_pairs={{0,1},{1,2},{2,3},{5,4},{6,5},{7,6},{8,9},{9,10},{10,11},{13,12},{... | collective-permute-start | bytes 2359304 | tf_op jit(solution)/shard_map/out_projection/ppermute | solution.py:274
  108.4 8.6 %collective-permute-done.15 = bf16[256,1536]{1,0:T(8,128)(2,1)} collective-permute-done((bf16[256,1536]{1,0:T(8,128)(2,1)S(1)}, bf16[256,1536]{1,0:T(8,128)(2,1)}, u32[]{:S(2)}, u32[]{:S(2)}) %collective-permute-start.15) | collective-permute-done | bytes 786464 | tf_op jit(solution)/shard_map/out_projection/ppermute | solution.py:274
  117.0 5.4 %collective-permute-start.16 = (bf16[256,1536]{1,0:T(8,128)(2,1)}, bf16[256,1536]{1,0:T(8,128)(2,1)}, u32[]{:S(2)}, u32[]{:S(2)}) collective-permute-start(bf16[256,1536]{1,0:T(8,128)(2,1)} %collective-permute-done.15), channel_id=1, source_target_pairs={{0,1},{1,2},{2,3},{5,4},{6,5},{7,6},{8,9},{9,10},{10,11},{13,12},{... | collective-permute-start | bytes 2359304 | tf_op jit(solution)/shard_map/out_projection/ppermute | solution.py:274
  124.8 6.5 %collective-permute-done.16 = bf16[256,1536]{1,0:T(8,128)(2,1)} collective-permute-done((bf16[256,1536]{1,0:T(8,128)(2,1)}, bf16[256,1536]{1,0:T(8,128)(2,1)}, u32[]{:S(2)}, u32[]{:S(2)}) %collective-permute-start.16) | collective-permute-done | bytes 786464 | tf_op jit(solution)/shard_map/out_projection/ppermute | solution.py:274
  131.3 4.6 %collective-permute-start.17 = (bf16[256,1536]{1,0:T(8,128)(2,1)}, bf16[256,1536]{1,0:T(8,128)(2,1)S(1)}, u32[]{:S(2)}, u32[]{:S(2)}) collective-permute-start(bf16[256,1536]{1,0:T(8,128)(2,1)} %collective-permute-done.16), channel_id=1, source_target_pairs={{0,1},{1,2},{2,3},{5,4},{6,5},{7,6},{8,9},{9,10},{10,11},{13,12},{... | collective-permute-start | bytes 2359304 | tf_op jit(solution)/shard_map/out_projection/ppermute | solution.py:274
  136.9 8.6 %collective-permute-done.17 = bf16[256,1536]{1,0:T(8,128)(2,1)S(1)} collective-permute-done((bf16[256,1536]{1,0:T(8,128)(2,1)}, bf16[256,1536]{1,0:T(8,128)(2,1)S(1)}, u32[]{:S(2)}, u32[]{:S(2)}) %collective-permute-start.17) | collective-permute-done | bytes 786464 | tf_op jit(solution)/shard_map/out_projection/ppermute | solution.py:274
  145.5 1.6 pad_maximum_fusion
  149.7 1.5 fusion.35
  151.8 2.4 %collective-permute-start.14 = (bf16[128,256]{0,1:T(8,128)(2,1)S(1)}, bf16[128,256]{0,1:T(8,128)(2,1)S(1)}, u32[]{:S(2)}, u32[]{:S(2)}) collective-permute-start(bf16[128,256]{0,1:T(8,128)(2,1)S(1)} %bitcast.229), channel_id=1, source_target_pairs={{0,1},{1,2},{2,3},{3,0},{4,5},{5,6},{6,7},{7,4},{8,9},{9,10},{10,1... | collective-permute-start | bytes 196616 | tf_op jit(solution)/shard_map/out_projection/ppermute | solution.py:283
  154.3 2.7 %collective-permute-start.20 = (bf16[128,256]{0,1:T(8,128)(2,1)S(1)}, bf16[128,256]{0,1:T(8,128)(2,1)S(1)}, u32[]{:S(2)}, u32[]{:S(2)}) collective-permute-start(bf16[128,256]{0,1:T(8,128)(2,1)S(1)} %bitcast.228), channel_id=1, source_target_pairs={{0,3},{1,0},{2,1},{3,2},{4,7},{5,4},{6,5},{7,6},{8,11},{9,8},{10,9... | collective-permute-start | bytes 196616 | tf_op jit(solution)/shard_map/out_projection/ppermute | solution.py:283
  157.8 1.7 broadcast_select_fusion.1
  160.6 3.3 %collective-permute-done.19 = bf16[128,256]{0,1:T(8,128)(2,1)S(1)} collective-permute-done((bf16[128,256]{0,1:T(8,128)(2,1)S(1)}, bf16[128,256]{0,1:T(8,128)(2,1)S(1)}, u32[]{:S(2)}, u32[]{:S(2)}) %collective-permute-start.19) | collective-permute-done | bytes 65568 | tf_op jit(solution)/shard_map/out_projection/ppermute | solution.py:283
  165.5 2.8 %collective-permute-start.22 = (bf16[8,256]{1,0:T(8,128)(2,1)S(1)}, bf16[8,256]{1,0:T(8,128)(2,1)S(1)}, u32[]{:S(2)}, u32[]{:S(2)}) collective-permute-start(bf16[8,256]{1,0:T(8,128)(2,1)S(1)} %get-tuple-element.43), channel_id=1, source_target_pairs={{0,2},{1,3},{2,0},{3,1},{4,6},{5,7},{6,4},{7,5},{8,10},{9,11},{10,... | collective-permute-start | bytes 12296 | tf_op jit(solution)/shard_map/sides_gather/ppermute | solution.py:153
  169.3 1.6 collective-permute-done.21
  171.9 1.8 collective-permute-start.26
  (102 shorter events, 29.4 us)
Async XLA Ops:
  0.6 102.9 %copy-start = (bf16[1536,768]{1,0:T(8,128)(2,1)S(1)}, bf16[1536,768]{1,0:T(8,128)(2,1)}, u32[]{:S(2)}) copy-start(bf16[1536,768]{1,0:T(8,128)(2,1)} %param.14) | copy-start | bytes 7077892
  4.1 8.7 %collective-permute-start = (bf16[128,384]{1,0:T(8,128)(2,1)S(1)}, bf16[128,384]{1,0:T(8,128)(2,1)S(1)}, u32[]{:S(2)}, u32[]{:S(2)}) collective-permute-start(bf16[128,384]{1,0:T(8,128)(2,1)S(1)} %bitcast.223), channel_id=1, source_target_pairs={{0,1},{1,2},{2,3},{3,0},{4,5},{5,6},{6,7},{7,4},{8,9},{9,10},{10,1... | collective-permute-start | bytes 294920 | tf_op jit(solution)/shard_map/ppermute | solution.py:65
  7.2 9.2 %collective-permute-start.1 = (bf16[128,384]{1,0:T(8,128)(2,1)S(1)}, bf16[128,384]{1,0:T(8,128)(2,1)S(1)}, u32[]{:S(2)}, u32[]{:S(2)}) collective-permute-start(bf16[128,384]{1,0:T(8,128)(2,1)S(1)} %bitcast.222), channel_id=1, source_target_pairs={{0,2},{1,3},{2,0},{3,1},{4,6},{5,7},{6,4},{7,5},{8,10},{9,11},{10,... | collective-permute-start | bytes 294920 | tf_op jit(solution)/shard_map/ppermute | solution.py:65
  9.9 6.7 %collective-permute-start.2 = (bf16[128,384]{1,0:T(8,128)(2,1)S(1)}, bf16[128,384]{1,0:T(8,128)(2,1)S(1)}, u32[]{:S(2)}, u32[]{:S(2)}) collective-permute-start(bf16[128,384]{1,0:T(8,128)(2,1)S(1)} %bitcast.221), channel_id=1, source_target_pairs={{0,3},{1,0},{2,1},{3,2},{4,7},{5,4},{6,5},{7,6},{8,11},{9,8},{10,9... | collective-permute-start | bytes 294920 | tf_op jit(solution)/shard_map/ppermute | solution.py:65
  16.6 8.5 %collective-permute-start.3 = (bf16[8,384]{1,0:T(8,128)(2,1)S(1)}, bf16[8,384]{1,0:T(8,128)(2,1)S(1)}, u32[]{:S(2)}, u32[]{:S(2)}) collective-permute-start(bf16[8,384]{1,0:T(8,128)(2,1)S(1)} %get-tuple-element.17), channel_id=1, source_target_pairs={{0,4},{4,8},{8,12},{1,5},{5,9},{9,13},{2,6},{6,10},{10,14},{3,7},{... | collective-permute-start | bytes 18440 | tf_op jit(solution)/shard_map/ppermute | solution.py:25
  18.3 4.8 %collective-permute-start.4 = (bf16[8,384]{1,0:T(8,128)(2,1)S(1)}, bf16[8,384]{1,0:T(8,128)(2,1)S(1)}, u32[]{:S(2)}, u32[]{:S(2)}) collective-permute-start(bf16[8,384]{1,0:T(8,128)(2,1)S(1)} %get-tuple-element.18), channel_id=1, source_target_pairs={{4,0},{8,4},{12,8},{5,1},{9,5},{13,9},{6,2},{10,6},{14,10},{7,3},{... | collective-permute-start | bytes 18440 | tf_op jit(solution)/shard_map/ppermute | solution.py:26
  27.3 30.8 %copy-start.2 = (bf16[128,1536]{1,0:T(8,128)(2,1)S(1)}, bf16[128,1536]{1,0:T(8,128)(2,1)}, u32[]{:S(2)}) copy-start(bf16[128,1536]{1,0:T(8,128)(2,1)} %param.10) | copy-start | bytes 1179652
  27.3 31.2 %copy-start.6 = (f32[1536]{0:T(1024)S(1)}, f32[1536]{0:T(1024)}, u32[]{:S(2)}) copy-start(f32[1536]{0:T(1024)} %param.13) | copy-start | bytes 18436
  27.4 12.7 %collective-permute-start.5 = (bf16[128,1536]{1,0:T(8,128)(2,1)S(1)}, bf16[128,1536]{1,0:T(8,128)(2,1)S(1)}, u32[]{:S(2)}, u32[]{:S(2)}) collective-permute-start(bf16[128,1536]{1,0:T(8,128)(2,1)S(1)} %get-tuple-element.14), channel_id=1, source_target_pairs={{0,1},{1,2},{2,3},{3,0},{4,5},{5,6},{6,7},{7,4},{8,9},{9,10},{10,1... | collective-permute-start | bytes 1179656 | tf_op jit(solution)/shard_map/conv_reduce/ppermute | solution.py:51
  29.9 28.2 %collective-permute-start.6 = (bf16[128,1536]{1,0:T(8,128)(2,1)S(1)}, bf16[128,1536]{1,0:T(8,128)(2,1)S(1)}, u32[]{:S(2)}, u32[]{:S(2)}) collective-permute-start(bf16[128,1536]{1,0:T(8,128)(2,1)S(1)} %get-tuple-element.16), channel_id=1, source_target_pairs={{0,2},{1,3},{2,0},{3,1},{4,6},{5,7},{6,4},{7,5},{8,10},{9,11},{10,... | collective-permute-start | bytes 1179656 | tf_op jit(solution)/shard_map/conv_reduce/ppermute | solution.py:51
  31.6 26.5 %collective-permute-start.7 = (bf16[128,1536]{1,0:T(8,128)(2,1)S(1)}, bf16[128,1536]{1,0:T(8,128)(2,1)S(1)}, u32[]{:S(2)}, u32[]{:S(2)}) collective-permute-start(bf16[128,1536]{1,0:T(8,128)(2,1)S(1)} %get-tuple-element.15), channel_id=1, source_target_pairs={{0,3},{1,0},{2,1},{3,2},{4,7},{5,4},{6,5},{7,6},{8,11},{9,8},{10,9... | collective-permute-start | bytes 1179656 | tf_op jit(solution)/shard_map/conv_reduce/ppermute | solution.py:51
  58.6 18.7 %collective-permute-start.10 = (bf16[128,1536]{1,0:T(8,128)(2,1)S(1)}, bf16[128,1536]{1,0:T(8,128)(2,1)S(1)}, u32[]{:S(2)}, u32[]{:S(2)}) collective-permute-start(bf16[128,1536]{1,0:T(8,128)(2,1)S(1)} %fusion.70), channel_id=1, source_target_pairs={{0,3},{1,0},{2,1},{3,2},{4,7},{5,4},{6,5},{7,6},{8,11},{9,8},{10,9... | collective-permute-start | bytes 1179656 | tf_op jit(solution)/shard_map/attn_in_gather/ppermute | solution.py:141
  66.5 20.1 %collective-permute-start.8 = (bf16[128,1536]{1,0:T(8,128)(2,1)S(1)}, bf16[128,1536]{1,0:T(8,128)(2,1)S(1)}, u32[]{:S(2)}, u32[]{:S(2)}) collective-permute-start(bf16[128,1536]{1,0:T(8,128)(2,1)S(1)} %fusion.70), channel_id=1, source_target_pairs={{0,1},{1,2},{2,3},{3,0},{4,5},{5,6},{6,7},{7,4},{8,9},{9,10},{10,1... | collective-permute-start | bytes 1179656 | tf_op jit(solution)/shard_map/attn_in_gather/ppermute | solution.py:141
  67.7 35.8 %collective-permute-start.9 = (bf16[128,1536]{1,0:T(8,128)(2,1)S(1)}, bf16[128,1536]{1,0:T(8,128)(2,1)S(1)}, u32[]{:S(2)}, u32[]{:S(2)}) collective-permute-start(bf16[128,1536]{1,0:T(8,128)(2,1)S(1)} %fusion.70), channel_id=1, source_target_pairs={{0,2},{1,3},{2,0},{3,1},{4,6},{5,7},{6,4},{7,5},{8,10},{9,11},{10,... | collective-permute-start | bytes 1179656 | tf_op jit(solution)/shard_map/attn_in_gather/ppermute | solution.py:141
  106.2 10.8 %collective-permute-start.15 = (bf16[256,1536]{1,0:T(8,128)(2,1)S(1)}, bf16[256,1536]{1,0:T(8,128)(2,1)}, u32[]{:S(2)}, u32[]{:S(2)}) collective-permute-start(bf16[256,1536]{1,0:T(8,128)(2,1)S(1)} %copy-done.3), channel_id=1, source_target_pairs={{0,1},{1,2},{2,3},{5,4},{6,5},{7,6},{8,9},{9,10},{10,11},{13,12},{... | collective-permute-start | bytes 2359304 | tf_op jit(solution)/shard_map/out_projection/ppermute | solution.py:274
  108.4 14.5 %collective-permute-start.11 = (bf16[2,512,256]{2,1,0:T(8,128)(2,1)}, bf16[2,512,256]{2,1,0:T(8,128)(2,1)}, u32[]{:S(2)}, u32[]{:S(2)}) collective-permute-start(bf16[2,512,256]{2,1,0:T(8,128)(2,1)} %slice.131), channel_id=1, source_target_pairs={{0,4},{4,8},{8,12},{12,0},{1,5},{5,9},{9,13},{13,1},{2,6},{6,10},{... | collective-permute-start | bytes 1572872 | tf_op jit(solution)/shard_map/kv_ring/ppermute | solution.py:237
  117.0 14.3 %collective-permute-start.16 = (bf16[256,1536]{1,0:T(8,128)(2,1)}, bf16[256,1536]{1,0:T(8,128)(2,1)}, u32[]{:S(2)}, u32[]{:S(2)}) collective-permute-start(bf16[256,1536]{1,0:T(8,128)(2,1)} %collective-permute-done.15), channel_id=1, source_target_pairs={{0,1},{1,2},{2,3},{5,4},{6,5},{7,6},{8,9},{9,10},{10,11},{13,12},{... | collective-permute-start | bytes 2359304 | tf_op jit(solution)/shard_map/out_projection/ppermute | solution.py:274
  122.4 13.5 %collective-permute-start.12 = (bf16[2,512,256]{2,1,0:T(8,128)(2,1)}, bf16[2,512,256]{2,1,0:T(8,128)(2,1)S(1)}, u32[]{:S(2)}, u32[]{:S(2)}) collective-permute-start(bf16[2,512,256]{2,1,0:T(8,128)(2,1)} %slice.131), channel_id=1, source_target_pairs={{4,0},{8,4},{12,8},{0,12},{5,1},{9,5},{13,9},{1,13},{6,2},{10,6},{... | collective-permute-start | bytes 1572872 | tf_op jit(solution)/shard_map/kv_ring/ppermute | solution.py:239
  122.9 13.5 %collective-permute-start.13 = (bf16[2,512,256]{2,1,0:T(8,128)(2,1)}, bf16[2,512,256]{2,1,0:T(8,128)(2,1)S(1)}, u32[]{:S(2)}, u32[]{:S(2)}) collective-permute-start(bf16[2,512,256]{2,1,0:T(8,128)(2,1)} %collective-permute-done.11), channel_id=1, source_target_pairs={{0,4},{4,8},{8,12},{12,0},{1,5},{5,9},{9,13},{13,1},{2,6},{6,10},{... | collective-permute-start | bytes 1572872 | tf_op jit(solution)/shard_map/kv_ring/ppermute | solution.py:237
  131.3 14.2 %collective-permute-start.17 = (bf16[256,1536]{1,0:T(8,128)(2,1)}, bf16[256,1536]{1,0:T(8,128)(2,1)S(1)}, u32[]{:S(2)}, u32[]{:S(2)}) collective-permute-start(bf16[256,1536]{1,0:T(8,128)(2,1)} %collective-permute-done.16), channel_id=1, source_target_pairs={{0,1},{1,2},{2,3},{5,4},{6,5},{7,6},{8,9},{9,10},{10,11},{13,12},{... | collective-permute-start | bytes 2359304 | tf_op jit(solution)/shard_map/out_projection/ppermute | solution.py:274
  147.1 10.6 %collective-permute-start.18 = (bf16[3,256,1536]{2,1,0:T(8,128)(2,1)S(1)}, bf16[3,256,1536]{2,1,0:T(8,128)(2,1)S(1)}, u32[]{:S(2)}, u32[]{:S(2)}) collective-permute-start(bf16[3,256,1536]{2,1,0:T(8,128)(2,1)S(1)} %pad_maximum_fusion), channel_id=1, source_target_pairs={{0,4},{4,0},{8,12},{12,8},{1,5},{5,1},{9,13},{13,9},{2,6},{6,2},{1... | collective-permute-start | bytes 7077896 | tf_op jit(solution)/shard_map/out_projection/ppermute | solution.py:277
  151.8 8.0 %collective-permute-start.14 = (bf16[128,256]{0,1:T(8,128)(2,1)S(1)}, bf16[128,256]{0,1:T(8,128)(2,1)S(1)}, u32[]{:S(2)}, u32[]{:S(2)}) collective-permute-start(bf16[128,256]{0,1:T(8,128)(2,1)S(1)} %bitcast.229), channel_id=1, source_target_pairs={{0,1},{1,2},{2,3},{3,0},{4,5},{5,6},{6,7},{7,4},{8,9},{9,10},{10,1... | collective-permute-start | bytes 196616 | tf_op jit(solution)/shard_map/out_projection/ppermute | solution.py:283
  154.3 5.9 %collective-permute-start.20 = (bf16[128,256]{0,1:T(8,128)(2,1)S(1)}, bf16[128,256]{0,1:T(8,128)(2,1)S(1)}, u32[]{:S(2)}, u32[]{:S(2)}) collective-permute-start(bf16[128,256]{0,1:T(8,128)(2,1)S(1)} %bitcast.228), channel_id=1, source_target_pairs={{0,3},{1,0},{2,1},{3,2},{4,7},{5,4},{6,5},{7,6},{8,11},{9,8},{10,9... | collective-permute-start | bytes 196616 | tf_op jit(solution)/shard_map/out_projection/ppermute | solution.py:283
  157.0 6.9 %collective-permute-start.19 = (bf16[128,256]{0,1:T(8,128)(2,1)S(1)}, bf16[128,256]{0,1:T(8,128)(2,1)S(1)}, u32[]{:S(2)}, u32[]{:S(2)}) collective-permute-start(bf16[128,256]{0,1:T(8,128)(2,1)S(1)} %bitcast.227), channel_id=1, source_target_pairs={{0,2},{1,3},{2,0},{3,1},{4,6},{5,7},{6,4},{7,5},{8,10},{9,11},{10,... | collective-permute-start | bytes 196616 | tf_op jit(solution)/shard_map/out_projection/ppermute | solution.py:283
  160.5 15.2 %copy-start.8 = (bf16[256,128]{1,0:T(8,128)(2,1)S(1)}, bf16[256,128]{1,0:T(8,128)(2,1)}, u32[]{:S(2)}) copy-start(bf16[256,128]{1,0:T(8,128)(2,1)} %param.19) | copy-start | bytes 196612
  160.5 15.2 %copy-start.9 = (bf16[128,256]{1,0:T(8,128)(2,1)S(1)}, bf16[128,256]{1,0:T(8,128)(2,1)}, u32[]{:S(2)}) copy-start(bf16[128,256]{1,0:T(8,128)(2,1)} %param.18) | copy-start | bytes 196612
  165.5 5.4 %collective-permute-start.21 = (bf16[8,256]{1,0:T(8,128)(2,1)S(1)}, bf16[8,256]{1,0:T(8,128)(2,1)S(1)}, u32[]{:S(2)}, u32[]{:S(2)}) collective-permute-start(bf16[8,256]{1,0:T(8,128)(2,1)S(1)} %get-tuple-element.43), channel_id=1, source_target_pairs={{0,1},{1,2},{2,3},{3,0},{4,5},{5,6},{6,7},{7,4},{8,9},{9,10},{10,1... | collective-permute-start | bytes 12296 | tf_op jit(solution)/shard_map/sides_gather/ppermute | solution.py:153
  165.5 5.4 %collective-permute-start.22 = (bf16[8,256]{1,0:T(8,128)(2,1)S(1)}, bf16[8,256]{1,0:T(8,128)(2,1)S(1)}, u32[]{:S(2)}, u32[]{:S(2)}) collective-permute-start(bf16[8,256]{1,0:T(8,128)(2,1)S(1)} %get-tuple-element.43), channel_id=1, source_target_pairs={{0,2},{1,3},{2,0},{3,1},{4,6},{5,7},{6,4},{7,5},{8,10},{9,11},{10,... | collective-permute-start | bytes 12296 | tf_op jit(solution)/shard_map/sides_gather/ppermute | solution.py:153
  168.3 3.6 %collective-permute-start.23 = (bf16[8,256]{1,0:T(8,128)(2,1)S(1)}, bf16[8,256]{1,0:T(8,128)(2,1)S(1)}, u32[]{:S(2)}, u32[]{:S(2)}) collective-permute-start(bf16[8,256]{1,0:T(8,128)(2,1)S(1)} %get-tuple-element.43), channel_id=1, source_target_pairs={{0,3},{1,0},{2,1},{3,2},{4,7},{5,4},{6,5},{7,6},{8,11},{9,8},{10,9... | collective-permute-start | bytes 12296 | tf_op jit(solution)/shard_map/sides_gather/ppermute | solution.py:153
  171.9 3.2 %collective-permute-start.24 = (bf16[32,256]{1,0:T(8,128)(2,1)S(1)}, bf16[32,256]{1,0:T(8,128)(2,1)S(1)}, u32[]{:S(2)}, u32[]{:S(2)}) collective-permute-start(bf16[32,256]{1,0:T(8,128)(2,1)S(1)} %bitcast.224), channel_id=1, source_target_pairs={{0,4},{4,8},{8,12},{12,0},{1,5},{5,9},{9,13},{13,1},{2,6},{6,10},{... | collective-permute-start | bytes 49160 | tf_op jit(solution)/shard_map/sides_gather/ppermute | solution.py:153
  171.9 3.8 %collective-permute-start.25 = (bf16[32,256]{1,0:T(8,128)(2,1)S(1)}, bf16[32,256]{1,0:T(8,128)(2,1)S(1)}, u32[]{:S(2)}, u32[]{:S(2)}) collective-permute-start(bf16[32,256]{1,0:T(8,128)(2,1)S(1)} %bitcast.225), channel_id=1, source_target_pairs={{0,8},{4,12},{8,0},{12,4},{1,9},{5,13},{9,1},{13,5},{2,10},{6,14},... | collective-permute-start | bytes 49160 | tf_op jit(solution)/shard_map/sides_gather/ppermute | solution.py:153
  171.9 3.8 %collective-permute-start.26 = (bf16[32,256]{1,0:T(8,128)(2,1)S(1)}, bf16[32,256]{1,0:T(8,128)(2,1)S(1)}, u32[]{:S(2)}, u32[]{:S(2)}) collective-permute-start(bf16[32,256]{1,0:T(8,128)(2,1)S(1)} %bitcast.226), channel_id=1, source_target_pairs={{0,12},{4,0},{8,4},{12,8},{1,13},{5,1},{9,5},{13,9},{2,14},{6,2},{... | collective-permute-start | bytes 49160 | tf_op jit(solution)/shard_map/sides_gather/ppermute | solution.py:153
  (5 other events, 21.8 us)

commit v19 on v17

--- a/solution.py
+++ b/solution.py
@@ -196,6 +196,8 @@
     grouped = projected.reshape(local_rows, head_count, 2 * KEY_SIZE + VALUE_SIZE).transpose(1, 0, 2)
     queries = grouped[:, :, :KEY_SIZE]
     kv = grouped[:, :, KEY_SIZE:]
+    if rotated and seq_count % 2 == 0:
+        late_w_out, kv = lax.optimization_barrier((w_out, kv))
     scale = 1.0 / math.sqrt(KEY_SIZE)
 
     def attend(state, kv_block):
@@ -242,7 +244,6 @@
     attended = (weighted / running_sum[:, :, None]).astype(jnp.bfloat16)
     attended = attended.transpose(1, 0, 2).reshape(local_rows, head_count * VALUE_SIZE)
     with jax.named_scope("out_projection"):
-        late_w_out, unused = lax.optimization_barrier((w_out, kv))
         if rotated and seq_count % 2 == 0:
             me = lax.axis_index("pair")
             core = lax.axis_index("seq") % 2
@@ -276,6 +277,7 @@
                 )
                 mixed = mixed + jnp.dot(incoming, block, preferred_element_type=jnp.float32)
         else:
+            late_w_out, unused = lax.optimization_barrier((w_out, kv))
             full_w_out = gather_weight_rows(late_w_out, "pair", "seq")
             own_heads = rows_to_heads(attended, "pair")
             mixed = jnp.dot(own_heads, full_w_out, preferred_element_type=jnp.float32)

time: 167 us -> 178 us (1.066)
  waiting for transfers between devices: 70.7 us -> 99.4 us
  starting transfers between devices: 67.8 us -> 52.1 us
    ppermute x3, waiting for transfers between devices: 18.9 us -> 34.5 us  [rotated_all_gather(): lax.ppermute(value, axis, [(i, (i + shift) % n) for i in range(n)])]
    ppermute x3, starting transfers between devices: 22 us -> 8.88 us  [shards(): flow = lax.ppermute(flow, ('seq', 'pair'), ways)]
    ppermute x3, waiting for transfers between devices: 4.6 us -> 15.1 us  [shards(): flow = lax.ppermute(flow, ('seq', 'pair'), ways)]
    ppermute x3, starting transfers between devices: 3.27 us -> 0.06 us  [shards(): next_going = lax.ppermute(going, 'seq', forward)]
    ppermute x3, waiting for transfers between devices: 22.6 us -> 25.8 us  [direct_reduce_scatter(): lax.ppermute(outgoing, axis, [(i, (i + shift) % n) for i in range(n)])]
    ppermute x3, waiting for transfers between devices: 10.6 us -> 8.63 us  [shards(): next_going = lax.ppermute(going, 'seq', forward)]
  transfers between devices with their start and end apart: 30 -> 30, of which waited for: 20 -> 20; matrix products, arithmetic and copies ran while one was open for 11% -> 7% of each run, Pallas kernels for 0% -> 0%
where the time goes in v19:
time: 178 us; the launch traced here: 177 us
  waiting for transfers between devices  99.4 us (56%)
  starting transfers between devices  52.1 us (29%)
  matrix products  17.7 us (10%)
  other arithmetic  5.21 us (3%)
    ppermute x3, waiting for transfers between devices, rotated_all_gather(): lax.ppermute(value, axis, [(i, (i + shift) % n) for i in range(n)])  34.5 us
    ppermute x3, waiting for transfers between devices, direct_reduce_scatter(): lax.ppermute(outgoing, axis, [(i, (i + shift) % n) for i in range(n)])  25.8 us
    ppermute x3, waiting for transfers between devices, shards(): flow = lax.ppermute(flow, ('seq', 'pair'), ways)  15.1 us
    ppermute x3, starting transfers between devices, rotated_all_gather(): lax.ppermute(value, axis, [(i, (i + shift) % n) for i in range(n)])  10.5 us
    ppermute x3, starting transfers between devices, shards(): flow = lax.ppermute(flow, ('seq', 'pair'), ways)  8.88 us
    ppermute x3, waiting for transfers between devices, shards(): next_going = lax.ppermute(going, 'seq', forward)  8.63 us
    ppermute x3, starting transfers between devices, permute_all_to_all(): lax.ppermute(outgoing, axis, [(i, (i + shift) % n) for i in range(n)])  7.13 us
    dot_general x5, matrix products, conv_rows(): jnp.dot(shifted, conv_weight[offset], preferred_element_type=jnp.float32)  6.46 us
  transfers between devices with their start and end apart: 30, of which 20 were waited for; matrix products, arithmetic and copies ran while one was open for 7% of the time, Pallas kernels for 0%

profile of v19, /device:TPU:0, one launch (start us, length us, event | category | flops | bytes accessed | tf_op | source)
XLA Modules:
  0.0 177.2 jit_solution(17178857672617579172)
XLA Ops:
  4.1 3.1 %collective-permute-start = (bf16[128,384]{1,0:T(8,128)(2,1)S(1)}, bf16[128,384]{1,0:T(8,128)(2,1)S(1)}, u32[]{:S(2)}, u32[]{:S(2)}) collective-permute-start(bf16[128,384]{1,0:T(8,128)(2,1)S(1)} %bitcast.304), channel_id=1, source_target_pairs={{0,1},{1,2},{2,3},{3,0},{4,5},{5,6},{6,7},{7,4},{8,9},{9,10},{10,1... | collective-permute-start | bytes 294920 | tf_op jit(solution)/shard_map/ppermute | solution.py:65
  7.2 2.7 %collective-permute-start.1 = (bf16[128,384]{1,0:T(8,128)(2,1)S(1)}, bf16[128,384]{1,0:T(8,128)(2,1)S(1)}, u32[]{:S(2)}, u32[]{:S(2)}) collective-permute-start(bf16[128,384]{1,0:T(8,128)(2,1)S(1)} %bitcast.303), channel_id=1, source_target_pairs={{0,2},{1,3},{2,0},{3,1},{4,6},{5,7},{6,4},{7,5},{8,10},{9,11},{10,... | collective-permute-start | bytes 294920 | tf_op jit(solution)/shard_map/ppermute | solution.py:65
  11.4 1.5 collective-permute-done
  12.9 3.5 %collective-permute-done.1 = bf16[128,384]{1,0:T(8,128)(2,1)S(1)} collective-permute-done((bf16[128,384]{1,0:T(8,128)(2,1)S(1)}, bf16[128,384]{1,0:T(8,128)(2,1)S(1)}, u32[]{:S(2)}, u32[]{:S(2)}) %collective-permute-start.1) | collective-permute-done | bytes 98336 | tf_op jit(solution)/shard_map/ppermute | solution.py:65
  16.6 1.7 collective-permute-start.3
  18.3 1.6 collective-permute-start.4
  19.9 2.4 %fusion.42 = f32[512,1536]{1,0:T(8,128)S(1)} fusion(bf16[512,384]{1,0:T(8,128)(2,1)S(1)} %bitcast.276, bf16[5,384,1536]{2,1,0:T(8,128)(2,1)} %param.12), kind=kOutput, calls=%fused_computation.68 | convolution fusion | flops 603979776 | bytes 4718592 | tf_op jit(solution)/shard_map/conv_reduce/dot_general | solution.py:39
  27.4 2.4 %collective-permute-start.5 = (bf16[128,1536]{1,0:T(8,128)(2,1)S(1)}, bf16[128,1536]{1,0:T(8,128)(2,1)S(1)}, u32[]{:S(2)}, u32[]{:S(2)}) collective-permute-start(bf16[128,1536]{1,0:T(8,128)(2,1)S(1)} %get-tuple-element.26), channel_id=1, source_target_pairs={{0,1},{1,2},{2,3},{3,0},{4,5},{5,6},{6,7},{7,4},{8,9},{9,10},{10,1... | collective-permute-start | bytes 1179656 | tf_op jit(solution)/shard_map/conv_reduce/ppermute | solution.py:51
  29.8 1.7 collective-permute-start.6
  32.3 7.8 %collective-permute-done.5 = bf16[128,1536]{1,0:T(8,128)(2,1)S(1)} collective-permute-done((bf16[128,1536]{1,0:T(8,128)(2,1)S(1)}, bf16[128,1536]{1,0:T(8,128)(2,1)S(1)}, u32[]{:S(2)}, u32[]{:S(2)}) %collective-permute-start.5) | collective-permute-done | bytes 393248 | tf_op jit(solution)/shard_map/conv_reduce/ppermute | solution.py:51
  40.1 17.9 %collective-permute-done.6 = bf16[128,1536]{1,0:T(8,128)(2,1)S(1)} collective-permute-done((bf16[128,1536]{1,0:T(8,128)(2,1)S(1)}, bf16[128,1536]{1,0:T(8,128)(2,1)S(1)}, u32[]{:S(2)}, u32[]{:S(2)}) %collective-permute-start.6) | collective-permute-done | bytes 393248 | tf_op jit(solution)/shard_map/conv_reduce/ppermute | solution.py:51
  58.6 7.8 %collective-permute-start.10 = (bf16[128,1536]{1,0:T(8,128)(2,1)S(1)}, bf16[128,1536]{1,0:T(8,128)(2,1)S(1)}, u32[]{:S(2)}, u32[]{:S(2)}) collective-permute-start(bf16[128,1536]{1,0:T(8,128)(2,1)S(1)} %fusion.74), channel_id=1, source_target_pairs={{0,3},{1,0},{2,1},{3,2},{4,7},{5,4},{6,5},{7,6},{8,11},{9,8},{10,9... | collective-permute-start | bytes 1179656 | tf_op jit(solution)/shard_map/attn_in_gather/ppermute | solution.py:141
  69.1 8.2 %collective-permute-done.10 = bf16[128,1536]{1,0:T(8,128)(2,1)S(1)} collective-permute-done((bf16[128,1536]{1,0:T(8,128)(2,1)S(1)}, bf16[128,1536]{1,0:T(8,128)(2,1)S(1)}, u32[]{:S(2)}, u32[]{:S(2)}) %collective-permute-start.10) | collective-permute-done | bytes 393248 | tf_op jit(solution)/shard_map/attn_in_gather/ppermute | solution.py:141
  77.3 9.3 %collective-permute-done.8 = bf16[128,1536]{1,0:T(8,128)(2,1)} collective-permute-done((bf16[128,1536]{1,0:T(8,128)(2,1)S(1)}, bf16[128,1536]{1,0:T(8,128)(2,1)}, u32[]{:S(2)}, u32[]{:S(2)}) %collective-permute-start.8) | collective-permute-done | bytes 393248 | tf_op jit(solution)/shard_map/attn_in_gather/ppermute | solution.py:141
  86.6 17.0 %collective-permute-done.9 = bf16[128,1536]{1,0:T(8,128)(2,1)} collective-permute-done((bf16[128,1536]{1,0:T(8,128)(2,1)S(1)}, bf16[128,1536]{1,0:T(8,128)(2,1)}, u32[]{:S(2)}, u32[]{:S(2)}) %collective-permute-start.9) | collective-permute-done | bytes 393248 | tf_op jit(solution)/shard_map/attn_in_gather/ppermute | solution.py:141
  103.6 2.5 %fusion.14 = bf16[512,768]{1,0:T(8,128)(2,1)S(1)} fusion(bf16[1536,768]{1,0:T(8,128)(2,1)S(1)} %copy-done, bf16[128,1536]{1,0:T(8,128)(2,1)S(1)} %collective-permute-done.10, bf16[128,1536]{1,0:T(8,128)(2,1)} %collective-permute-done.9, bf16[128,1536]{1,0:T(8,128)(2,1)} %collective-permute-done.8, bf16[128,1536]{1,0:T(8,128)(2,1)S(1)} %fusion.74), kind=kOutput, calls=%fused_computation.20 | convolution fusion | flops 1214644224 | bytes 4718592 | tf_op jit(solution)/shard_map/dot_general | solution.py:194
  106.7 1.8 %collective-permute-start.12 = (bf16[2,256,256]{2,1,0:T(8,128)(2,1)S(1)}, bf16[2,256,256]{2,1,0:T(8,128)(2,1)S(1)}, u32[]{:S(2)}, u32[]{:S(2)}) collective-permute-start(bf16[2,256,256]{2,1,0:T(8,128)(2,1)S(1)} %get-tuple-element.30), channel_id=1, source_target_pairs={{4,0},{8,4},{12,8},{0,12},{5,1},{9,5},{13,9},{1,13},{6,2},{10,6},{... | collective-permute-start | bytes 786440 | tf_op jit(solution)/shard_map/kv_ring/ppermute | solution.py:238
  110.1 3.2 %collective-permute-done.11 = bf16[2,256,256]{2,1,0:T(8,128)(2,1)S(1)} collective-permute-done((bf16[2,256,256]{2,1,0:T(8,128)(2,1)S(1)}, bf16[2,256,256]{2,1,0:T(8,128)(2,1)S(1)}, u32[]{:S(2)}, u32[]{:S(2)}) %collective-permute-start.11) | collective-permute-done | bytes 262176 | tf_op jit(solution)/shard_map/kv_ring/ppermute | solution.py:237
  113.6 1.8 %collective-permute-start.14 = (bf16[2,256,256]{2,1,0:T(8,128)(2,1)S(1)}, bf16[2,256,256]{2,1,0:T(8,128)(2,1)S(1)}, u32[]{:S(2)}, u32[]{:S(2)}) collective-permute-start(bf16[2,256,256]{2,1,0:T(8,128)(2,1)S(1)} %collective-permute-done.12), channel_id=1, source_target_pairs={{4,0},{8,4},{12,8},{0,12},{5,1},{9,5},{13,9},{1,13},{6,2},{10,6},{... | collective-permute-start | bytes 786440 | tf_op jit(solution)/shard_map/kv_ring/ppermute | solution.py:238
  115.7 4.4 %collective-permute-done.13 = bf16[2,256,256]{2,1,0:T(8,128)(2,1)S(1)} collective-permute-done((bf16[2,256,256]{2,1,0:T(8,128)(2,1)S(1)}, bf16[2,256,256]{2,1,0:T(8,128)(2,1)S(1)}, u32[]{:S(2)}, u32[]{:S(2)}) %collective-permute-start.13) | collective-permute-done | bytes 262176 | tf_op jit(solution)/shard_map/kv_ring/ppermute | solution.py:237
  120.8 1.8 %collective-permute-start.16 = (bf16[2,256,256]{2,1,0:T(8,128)(2,1)S(1)}, bf16[2,256,256]{2,1,0:T(8,128)(2,1)S(1)}, u32[]{:S(2)}, u32[]{:S(2)}) collective-permute-start(bf16[2,256,256]{2,1,0:T(8,128)(2,1)S(1)} %collective-permute-done.14), channel_id=1, source_target_pairs={{4,0},{8,4},{12,8},{0,12},{5,1},{9,5},{13,9},{1,13},{6,2},{10,6},{... | collective-permute-start | bytes 786440 | tf_op jit(solution)/shard_map/kv_ring/ppermute | solution.py:238
  122.6 2.9 %collective-permute-start.19 = (bf16[256,1536]{1,0:T(8,128)(2,1)S(1)}, bf16[256,1536]{1,0:T(8,128)(2,1)S(1)}, u32[]{:S(2)}, u32[]{:S(2)}) collective-permute-start(bf16[256,1536]{1,0:T(8,128)(2,1)S(1)} %collective-permute-done.18), channel_id=1, source_target_pairs={{0,1},{1,2},{2,3},{5,4},{6,5},{7,6},{8,9},{9,10},{10,11},{13,12},{... | collective-permute-start | bytes 2359304 | tf_op jit(solution)/shard_map/out_projection/ppermute | solution.py:261
  127.9 7.1 %collective-permute-done.19 = bf16[256,1536]{1,0:T(8,128)(2,1)S(1)} collective-permute-done((bf16[256,1536]{1,0:T(8,128)(2,1)S(1)}, bf16[256,1536]{1,0:T(8,128)(2,1)S(1)}, u32[]{:S(2)}, u32[]{:S(2)}) %collective-permute-start.19) | collective-permute-done | bytes 786464 | tf_op jit(solution)/shard_map/out_projection/ppermute | solution.py:261
  135.0 4.6 %collective-permute-start.20 = (bf16[256,1536]{1,0:T(8,128)(2,1)S(1)}, bf16[256,1536]{1,0:T(8,128)(2,1)S(1)}, u32[]{:S(2)}, u32[]{:S(2)}) collective-permute-start(bf16[256,1536]{1,0:T(8,128)(2,1)S(1)} %collective-permute-done.19), channel_id=1, source_target_pairs={{0,1},{1,2},{2,3},{5,4},{6,5},{7,6},{8,9},{9,10},{10,11},{13,12},{... | collective-permute-start | bytes 2359304 | tf_op jit(solution)/shard_map/out_projection/ppermute | solution.py:261
  140.9 8.0 %collective-permute-done.20 = bf16[256,1536]{1,0:T(8,128)(2,1)S(1)} collective-permute-done((bf16[256,1536]{1,0:T(8,128)(2,1)S(1)}, bf16[256,1536]{1,0:T(8,128)(2,1)S(1)}, u32[]{:S(2)}, u32[]{:S(2)}) %collective-permute-start.20) | collective-permute-done | bytes 786464 | tf_op jit(solution)/shard_map/out_projection/ppermute | solution.py:261
  151.3 2.5 %collective-permute-start.17 = (bf16[128,256]{0,1:T(8,128)(2,1)S(1)}, bf16[128,256]{0,1:T(8,128)(2,1)S(1)}, u32[]{:S(2)}, u32[]{:S(2)}) collective-permute-start(bf16[128,256]{0,1:T(8,128)(2,1)S(1)} %bitcast.310), channel_id=1, source_target_pairs={{0,1},{1,2},{2,3},{3,0},{4,5},{5,6},{6,7},{7,4},{8,9},{9,10},{10,1... | collective-permute-start | bytes 196616 | tf_op jit(solution)/shard_map/out_projection/ppermute | solution.py:270
  153.9 3.3 %collective-permute-start.23 = (bf16[128,256]{0,1:T(8,128)(2,1)S(1)}, bf16[128,256]{0,1:T(8,128)(2,1)S(1)}, u32[]{:S(2)}, u32[]{:S(2)}) collective-permute-start(bf16[128,256]{0,1:T(8,128)(2,1)S(1)} %bitcast.309), channel_id=1, source_target_pairs={{0,3},{1,0},{2,1},{3,2},{4,7},{5,4},{6,5},{7,6},{8,11},{9,8},{10,9... | collective-permute-start | bytes 196616 | tf_op jit(solution)/shard_map/out_projection/ppermute | solution.py:270
  158.4 1.5 collective-permute-done.17
  160.7 3.4 %collective-permute-done.22 = bf16[128,256]{0,1:T(8,128)(2,1)S(1)} collective-permute-done((bf16[128,256]{0,1:T(8,128)(2,1)S(1)}, bf16[128,256]{0,1:T(8,128)(2,1)S(1)}, u32[]{:S(2)}, u32[]{:S(2)}) %collective-permute-start.22) | collective-permute-done | bytes 65568 | tf_op jit(solution)/shard_map/out_projection/ppermute | solution.py:270
  165.7 2.8 %collective-permute-start.25 = (bf16[8,256]{1,0:T(8,128)(2,1)S(1)}, bf16[8,256]{1,0:T(8,128)(2,1)S(1)}, u32[]{:S(2)}, u32[]{:S(2)}) collective-permute-start(bf16[8,256]{1,0:T(8,128)(2,1)S(1)} %get-tuple-element.65), channel_id=1, source_target_pairs={{0,2},{1,3},{2,0},{3,1},{4,6},{5,7},{6,4},{7,5},{8,10},{9,11},{10,... | collective-permute-start | bytes 12296 | tf_op jit(solution)/shard_map/sides_gather/ppermute | solution.py:153
  169.5 1.6 collective-permute-done.24
  172.0 1.8 collective-permute-start.29
  (118 shorter events, 32.4 us)
Async XLA Ops:
  0.6 103.0 %copy-start = (bf16[1536,768]{1,0:T(8,128)(2,1)S(1)}, bf16[1536,768]{1,0:T(8,128)(2,1)}, u32[]{:S(2)}) copy-start(bf16[1536,768]{1,0:T(8,128)(2,1)} %param.14) | copy-start | bytes 7077892
  4.1 8.7 %collective-permute-start = (bf16[128,384]{1,0:T(8,128)(2,1)S(1)}, bf16[128,384]{1,0:T(8,128)(2,1)S(1)}, u32[]{:S(2)}, u32[]{:S(2)}) collective-permute-start(bf16[128,384]{1,0:T(8,128)(2,1)S(1)} %bitcast.304), channel_id=1, source_target_pairs={{0,1},{1,2},{2,3},{3,0},{4,5},{5,6},{6,7},{7,4},{8,9},{9,10},{10,1... | collective-permute-start | bytes 294920 | tf_op jit(solution)/shard_map/ppermute | solution.py:65
  7.2 9.2 %collective-permute-start.1 = (bf16[128,384]{1,0:T(8,128)(2,1)S(1)}, bf16[128,384]{1,0:T(8,128)(2,1)S(1)}, u32[]{:S(2)}, u32[]{:S(2)}) collective-permute-start(bf16[128,384]{1,0:T(8,128)(2,1)S(1)} %bitcast.303), channel_id=1, source_target_pairs={{0,2},{1,3},{2,0},{3,1},{4,6},{5,7},{6,4},{7,5},{8,10},{9,11},{10,... | collective-permute-start | bytes 294920 | tf_op jit(solution)/shard_map/ppermute | solution.py:65
  9.9 6.7 %collective-permute-start.2 = (bf16[128,384]{1,0:T(8,128)(2,1)S(1)}, bf16[128,384]{1,0:T(8,128)(2,1)S(1)}, u32[]{:S(2)}, u32[]{:S(2)}) collective-permute-start(bf16[128,384]{1,0:T(8,128)(2,1)S(1)} %bitcast.302), channel_id=1, source_target_pairs={{0,3},{1,0},{2,1},{3,2},{4,7},{5,4},{6,5},{7,6},{8,11},{9,8},{10,9... | collective-permute-start | bytes 294920 | tf_op jit(solution)/shard_map/ppermute | solution.py:65
  16.6 8.5 %collective-permute-start.3 = (bf16[8,384]{1,0:T(8,128)(2,1)S(1)}, bf16[8,384]{1,0:T(8,128)(2,1)S(1)}, u32[]{:S(2)}, u32[]{:S(2)}) collective-permute-start(bf16[8,384]{1,0:T(8,128)(2,1)S(1)} %get-tuple-element.31), channel_id=1, source_target_pairs={{0,4},{4,8},{8,12},{1,5},{5,9},{9,13},{2,6},{6,10},{10,14},{3,7},{... | collective-permute-start | bytes 18440 | tf_op jit(solution)/shard_map/ppermute | solution.py:25
  18.3 4.8 %collective-permute-start.4 = (bf16[8,384]{1,0:T(8,128)(2,1)S(1)}, bf16[8,384]{1,0:T(8,128)(2,1)S(1)}, u32[]{:S(2)}, u32[]{:S(2)}) collective-permute-start(bf16[8,384]{1,0:T(8,128)(2,1)S(1)} %get-tuple-element.32), channel_id=1, source_target_pairs={{4,0},{8,4},{12,8},{5,1},{9,5},{13,9},{6,2},{10,6},{14,10},{7,3},{... | collective-permute-start | bytes 18440 | tf_op jit(solution)/shard_map/ppermute | solution.py:26
  27.2 31.2 %copy-start.5 = (f32[1536]{0:T(1024)S(1)}, f32[1536]{0:T(1024)}, u32[]{:S(2)}) copy-start(f32[1536]{0:T(1024)} %param.13) | copy-start | bytes 18436
  27.4 12.7 %collective-permute-start.5 = (bf16[128,1536]{1,0:T(8,128)(2,1)S(1)}, bf16[128,1536]{1,0:T(8,128)(2,1)S(1)}, u32[]{:S(2)}, u32[]{:S(2)}) collective-permute-start(bf16[128,1536]{1,0:T(8,128)(2,1)S(1)} %get-tuple-element.26), channel_id=1, source_target_pairs={{0,1},{1,2},{2,3},{3,0},{4,5},{5,6},{6,7},{7,4},{8,9},{9,10},{10,1... | collective-permute-start | bytes 1179656 | tf_op jit(solution)/shard_map/conv_reduce/ppermute | solution.py:51
  29.8 28.2 %collective-permute-start.6 = (bf16[128,1536]{1,0:T(8,128)(2,1)S(1)}, bf16[128,1536]{1,0:T(8,128)(2,1)S(1)}, u32[]{:S(2)}, u32[]{:S(2)}) collective-permute-start(bf16[128,1536]{1,0:T(8,128)(2,1)S(1)} %get-tuple-element.28), channel_id=1, source_target_pairs={{0,2},{1,3},{2,0},{3,1},{4,6},{5,7},{6,4},{7,5},{8,10},{9,11},{10,... | collective-permute-start | bytes 1179656 | tf_op jit(solution)/shard_map/conv_reduce/ppermute | solution.py:51
  31.5 26.5 %collective-permute-start.7 = (bf16[128,1536]{1,0:T(8,128)(2,1)S(1)}, bf16[128,1536]{1,0:T(8,128)(2,1)S(1)}, u32[]{:S(2)}, u32[]{:S(2)}) collective-permute-start(bf16[128,1536]{1,0:T(8,128)(2,1)S(1)} %get-tuple-element.27), channel_id=1, source_target_pairs={{0,3},{1,0},{2,1},{3,2},{4,7},{5,4},{6,5},{7,6},{8,11},{9,8},{10,9... | collective-permute-start | bytes 1179656 | tf_op jit(solution)/shard_map/conv_reduce/ppermute | solution.py:51
  58.6 18.7 %collective-permute-start.10 = (bf16[128,1536]{1,0:T(8,128)(2,1)S(1)}, bf16[128,1536]{1,0:T(8,128)(2,1)S(1)}, u32[]{:S(2)}, u32[]{:S(2)}) collective-permute-start(bf16[128,1536]{1,0:T(8,128)(2,1)S(1)} %fusion.74), channel_id=1, source_target_pairs={{0,3},{1,0},{2,1},{3,2},{4,7},{5,4},{6,5},{7,6},{8,11},{9,8},{10,9... | collective-permute-start | bytes 1179656 | tf_op jit(solution)/shard_map/attn_in_gather/ppermute | solution.py:141
  66.4 20.2 %collective-permute-start.8 = (bf16[128,1536]{1,0:T(8,128)(2,1)S(1)}, bf16[128,1536]{1,0:T(8,128)(2,1)}, u32[]{:S(2)}, u32[]{:S(2)}) collective-permute-start(bf16[128,1536]{1,0:T(8,128)(2,1)S(1)} %fusion.74), channel_id=1, source_target_pairs={{0,1},{1,2},{2,3},{3,0},{4,5},{5,6},{6,7},{7,4},{8,9},{9,10},{10,1... | collective-permute-start | bytes 1179656 | tf_op jit(solution)/shard_map/attn_in_gather/ppermute | solution.py:141
  67.7 35.9 %collective-permute-start.9 = (bf16[128,1536]{1,0:T(8,128)(2,1)S(1)}, bf16[128,1536]{1,0:T(8,128)(2,1)}, u32[]{:S(2)}, u32[]{:S(2)}) collective-permute-start(bf16[128,1536]{1,0:T(8,128)(2,1)S(1)} %fusion.74), channel_id=1, source_target_pairs={{0,2},{1,3},{2,0},{3,1},{4,6},{5,7},{6,4},{7,5},{8,10},{9,11},{10,... | collective-permute-start | bytes 1179656 | tf_op jit(solution)/shard_map/attn_in_gather/ppermute | solution.py:141
  106.3 7.0 %collective-permute-start.11 = (bf16[2,256,256]{2,1,0:T(8,128)(2,1)S(1)}, bf16[2,256,256]{2,1,0:T(8,128)(2,1)S(1)}, u32[]{:S(2)}, u32[]{:S(2)}) collective-permute-start(bf16[2,256,256]{2,1,0:T(8,128)(2,1)S(1)} %get-tuple-element.29), channel_id=1, source_target_pairs={{0,4},{4,8},{8,12},{12,0},{1,5},{5,9},{9,13},{13,1},{2,6},{6,10},{... | collective-permute-start | bytes 786440 | tf_op jit(solution)/shard_map/kv_ring/ppermute | solution.py:237
  106.7 6.9 %collective-permute-start.12 = (bf16[2,256,256]{2,1,0:T(8,128)(2,1)S(1)}, bf16[2,256,256]{2,1,0:T(8,128)(2,1)S(1)}, u32[]{:S(2)}, u32[]{:S(2)}) collective-permute-start(bf16[2,256,256]{2,1,0:T(8,128)(2,1)S(1)} %get-tuple-element.30), channel_id=1, source_target_pairs={{4,0},{8,4},{12,8},{0,12},{5,1},{9,5},{13,9},{1,13},{6,2},{10,6},{... | collective-permute-start | bytes 786440 | tf_op jit(solution)/shard_map/kv_ring/ppermute | solution.py:238
  108.8 13.8 %collective-permute-start.18 = (bf16[256,1536]{1,0:T(8,128)(2,1)S(1)}, bf16[256,1536]{1,0:T(8,128)(2,1)S(1)}, u32[]{:S(2)}, u32[]{:S(2)}) collective-permute-start(bf16[256,1536]{1,0:T(8,128)(2,1)S(1)} %copy-done.3), channel_id=1, source_target_pairs={{0,1},{1,2},{2,3},{5,4},{6,5},{7,6},{8,9},{9,10},{10,11},{13,12},{... | collective-permute-start | bytes 2359304 | tf_op jit(solution)/shard_map/out_projection/ppermute | solution.py:261
  113.3 6.9 %collective-permute-start.13 = (bf16[2,256,256]{2,1,0:T(8,128)(2,1)S(1)}, bf16[2,256,256]{2,1,0:T(8,128)(2,1)S(1)}, u32[]{:S(2)}, u32[]{:S(2)}) collective-permute-start(bf16[2,256,256]{2,1,0:T(8,128)(2,1)S(1)} %collective-permute-done.11), channel_id=1, source_target_pairs={{0,4},{4,8},{8,12},{12,0},{1,5},{5,9},{9,13},{13,1},{2,6},{6,10},{... | collective-permute-start | bytes 786440 | tf_op jit(solution)/shard_map/kv_ring/ppermute | solution.py:237
  113.6 6.9 %collective-permute-start.14 = (bf16[2,256,256]{2,1,0:T(8,128)(2,1)S(1)}, bf16[2,256,256]{2,1,0:T(8,128)(2,1)S(1)}, u32[]{:S(2)}, u32[]{:S(2)}) collective-permute-start(bf16[2,256,256]{2,1,0:T(8,128)(2,1)S(1)} %collective-permute-done.12), channel_id=1, source_target_pairs={{4,0},{8,4},{12,8},{0,12},{5,1},{9,5},{13,9},{1,13},{6,2},{10,6},{... | collective-permute-start | bytes 786440 | tf_op jit(solution)/shard_map/kv_ring/ppermute | solution.py:238
  120.2 6.4 %collective-permute-start.15 = (bf16[2,256,256]{2,1,0:T(8,128)(2,1)S(1)}, bf16[2,256,256]{2,1,0:T(8,128)(2,1)S(1)}, u32[]{:S(2)}, u32[]{:S(2)}) collective-permute-start(bf16[2,256,256]{2,1,0:T(8,128)(2,1)S(1)} %collective-permute-done.13), channel_id=1, source_target_pairs={{0,4},{4,8},{8,12},{12,0},{1,5},{5,9},{9,13},{13,1},{2,6},{6,10},{... | collective-permute-start | bytes 786440 | tf_op jit(solution)/shard_map/kv_ring/ppermute | solution.py:237
  120.8 6.1 %collective-permute-start.16 = (bf16[2,256,256]{2,1,0:T(8,128)(2,1)S(1)}, bf16[2,256,256]{2,1,0:T(8,128)(2,1)S(1)}, u32[]{:S(2)}, u32[]{:S(2)}) collective-permute-start(bf16[2,256,256]{2,1,0:T(8,128)(2,1)S(1)} %collective-permute-done.14), channel_id=1, source_target_pairs={{4,0},{8,4},{12,8},{0,12},{5,1},{9,5},{13,9},{1,13},{6,2},{10,6},{... | collective-permute-start | bytes 786440 | tf_op jit(solution)/shard_map/kv_ring/ppermute | solution.py:238
  122.6 12.4 %collective-permute-start.19 = (bf16[256,1536]{1,0:T(8,128)(2,1)S(1)}, bf16[256,1536]{1,0:T(8,128)(2,1)S(1)}, u32[]{:S(2)}, u32[]{:S(2)}) collective-permute-start(bf16[256,1536]{1,0:T(8,128)(2,1)S(1)} %collective-permute-done.18), channel_id=1, source_target_pairs={{0,1},{1,2},{2,3},{5,4},{6,5},{7,6},{8,9},{9,10},{10,11},{13,12},{... | collective-permute-start | bytes 2359304 | tf_op jit(solution)/shard_map/out_projection/ppermute | solution.py:261
  135.0 13.9 %collective-permute-start.20 = (bf16[256,1536]{1,0:T(8,128)(2,1)S(1)}, bf16[256,1536]{1,0:T(8,128)(2,1)S(1)}, u32[]{:S(2)}, u32[]{:S(2)}) collective-permute-start(bf16[256,1536]{1,0:T(8,128)(2,1)S(1)} %collective-permute-done.19), channel_id=1, source_target_pairs={{0,1},{1,2},{2,3},{5,4},{6,5},{7,6},{8,9},{9,10},{10,11},{13,12},{... | collective-permute-start | bytes 2359304 | tf_op jit(solution)/shard_map/out_projection/ppermute | solution.py:261
  149.1 8.8 %collective-permute-start.21 = (bf16[3,256,1536]{2,1,0:T(8,128)(2,1)S(1)}, bf16[3,256,1536]{2,1,0:T(8,128)(2,1)S(1)}, u32[]{:S(2)}, u32[]{:S(2)}) collective-permute-start(bf16[3,256,1536]{2,1,0:T(8,128)(2,1)S(1)} %pad_maximum_fusion), channel_id=1, source_target_pairs={{0,4},{4,0},{8,12},{12,8},{1,5},{5,1},{9,13},{13,9},{2,6},{6,2},{1... | collective-permute-start | bytes 7077896 | tf_op jit(solution)/shard_map/out_projection/ppermute | solution.py:264
  151.3 8.6 %collective-permute-start.17 = (bf16[128,256]{0,1:T(8,128)(2,1)S(1)}, bf16[128,256]{0,1:T(8,128)(2,1)S(1)}, u32[]{:S(2)}, u32[]{:S(2)}) collective-permute-start(bf16[128,256]{0,1:T(8,128)(2,1)S(1)} %bitcast.310), channel_id=1, source_target_pairs={{0,1},{1,2},{2,3},{3,0},{4,5},{5,6},{6,7},{7,4},{8,9},{9,10},{10,1... | collective-permute-start | bytes 196616 | tf_op jit(solution)/shard_map/out_projection/ppermute | solution.py:270
  153.9 6.4 %collective-permute-start.23 = (bf16[128,256]{0,1:T(8,128)(2,1)S(1)}, bf16[128,256]{0,1:T(8,128)(2,1)S(1)}, u32[]{:S(2)}, u32[]{:S(2)}) collective-permute-start(bf16[128,256]{0,1:T(8,128)(2,1)S(1)} %bitcast.309), channel_id=1, source_target_pairs={{0,3},{1,0},{2,1},{3,2},{4,7},{5,4},{6,5},{7,6},{8,11},{9,8},{10,9... | collective-permute-start | bytes 196616 | tf_op jit(solution)/shard_map/out_projection/ppermute | solution.py:270
  157.2 6.9 %collective-permute-start.22 = (bf16[128,256]{0,1:T(8,128)(2,1)S(1)}, bf16[128,256]{0,1:T(8,128)(2,1)S(1)}, u32[]{:S(2)}, u32[]{:S(2)}) collective-permute-start(bf16[128,256]{0,1:T(8,128)(2,1)S(1)} %bitcast.308), channel_id=1, source_target_pairs={{0,2},{1,3},{2,0},{3,1},{4,6},{5,7},{6,4},{7,5},{8,10},{9,11},{10,... | collective-permute-start | bytes 196616 | tf_op jit(solution)/shard_map/out_projection/ppermute | solution.py:270
  165.7 5.4 %collective-permute-start.24 = (bf16[8,256]{1,0:T(8,128)(2,1)S(1)}, bf16[8,256]{1,0:T(8,128)(2,1)S(1)}, u32[]{:S(2)}, u32[]{:S(2)}) collective-permute-start(bf16[8,256]{1,0:T(8,128)(2,1)S(1)} %get-tuple-element.65), channel_id=1, source_target_pairs={{0,1},{1,2},{2,3},{3,0},{4,5},{5,6},{6,7},{7,4},{8,9},{9,10},{10,1... | collective-permute-start | bytes 12296 | tf_op jit(solution)/shard_map/sides_gather/ppermute | solution.py:153
  165.7 5.4 %collective-permute-start.25 = (bf16[8,256]{1,0:T(8,128)(2,1)S(1)}, bf16[8,256]{1,0:T(8,128)(2,1)S(1)}, u32[]{:S(2)}, u32[]{:S(2)}) collective-permute-start(bf16[8,256]{1,0:T(8,128)(2,1)S(1)} %get-tuple-element.65), channel_id=1, source_target_pairs={{0,2},{1,3},{2,0},{3,1},{4,6},{5,7},{6,4},{7,5},{8,10},{9,11},{10,... | collective-permute-start | bytes 12296 | tf_op jit(solution)/shard_map/sides_gather/ppermute | solution.py:153
  168.4 3.6 %collective-permute-start.26 = (bf16[8,256]{1,0:T(8,128)(2,1)S(1)}, bf16[8,256]{1,0:T(8,128)(2,1)S(1)}, u32[]{:S(2)}, u32[]{:S(2)}) collective-permute-start(bf16[8,256]{1,0:T(8,128)(2,1)S(1)} %get-tuple-element.65), channel_id=1, source_target_pairs={{0,3},{1,0},{2,1},{3,2},{4,7},{5,4},{6,5},{7,6},{8,11},{9,8},{10,9... | collective-permute-start | bytes 12296 | tf_op jit(solution)/shard_map/sides_gather/ppermute | solution.py:153
  172.0 3.2 %collective-permute-start.27 = (bf16[32,256]{1,0:T(8,128)(2,1)S(1)}, bf16[32,256]{1,0:T(8,128)(2,1)S(1)}, u32[]{:S(2)}, u32[]{:S(2)}) collective-permute-start(bf16[32,256]{1,0:T(8,128)(2,1)S(1)} %bitcast.305), channel_id=1, source_target_pairs={{0,4},{4,8},{8,12},{12,0},{1,5},{5,9},{9,13},{13,1},{2,6},{6,10},{... | collective-permute-start | bytes 49160 | tf_op jit(solution)/shard_map/sides_gather/ppermute | solution.py:153
  172.0 3.8 %collective-permute-start.28 = (bf16[32,256]{1,0:T(8,128)(2,1)S(1)}, bf16[32,256]{1,0:T(8,128)(2,1)S(1)}, u32[]{:S(2)}, u32[]{:S(2)}) collective-permute-start(bf16[32,256]{1,0:T(8,128)(2,1)S(1)} %bitcast.306), channel_id=1, source_target_pairs={{0,8},{4,12},{8,0},{12,4},{1,9},{5,13},{9,1},{13,5},{2,10},{6,14},... | collective-permute-start | bytes 49160 | tf_op jit(solution)/shard_map/sides_gather/ppermute | solution.py:153
  172.0 3.8 %collective-permute-start.29 = (bf16[32,256]{1,0:T(8,128)(2,1)S(1)}, bf16[32,256]{1,0:T(8,128)(2,1)S(1)}, u32[]{:S(2)}, u32[]{:S(2)}) collective-permute-start(bf16[32,256]{1,0:T(8,128)(2,1)S(1)} %bitcast.307), channel_id=1, source_target_pairs={{0,12},{4,0},{8,4},{12,8},{1,13},{5,1},{9,5},{13,9},{2,14},{6,2},{... | collective-permute-start | bytes 49160 | tf_op jit(solution)/shard_map/sides_gather/ppermute | solution.py:153
  (7 other events, 78.1 us)

commit v20 on v17

--- a/solution.py
+++ b/solution.py
@@ -261,8 +261,6 @@
                 received.append(flow)
             received = jnp.stack(received)
             swapped_w = lax.ppermute(received, "seq", [(i, i ^ 1) for i in range(seq_count)])
-            from_left = jnp.where(core == 0, received, swapped_w)
-            from_right = jnp.where(core == 0, swapped_w, received)
             pieces = attended.reshape(pair_count, row_count, attended.shape[1])
             mixed = jnp.dot(pieces[0], late_w_out, preferred_element_type=jnp.float32)
             for shift in range(1, pair_count):
@@ -271,8 +269,12 @@
                     "pair",
                     [(i, (i + shift) % pair_count) for i in range(pair_count)],
                 )
+                near = shift - 1
+                far = pair_count - shift - 1
                 block = jnp.where(
-                    me >= shift, from_left[shift - 1], from_right[pair_count - shift - 1]
+                    me >= shift,
+                    jnp.where(core == 0, received[near], swapped_w[near]),
+                    jnp.where(core == 0, swapped_w[far], received[far]),
                 )
                 mixed = mixed + jnp.dot(incoming, block, preferred_element_type=jnp.float32)
         else:

time: 167 us -> 169 us (1.012)
  waiting for transfers between devices: 70.7 us -> 72.4 us
  transfers between devices with their start and end apart: 30 -> 30, of which waited for: 20 -> 21; matrix products, arithmetic and copies ran while one was open for 11% -> 10% of each run, Pallas kernels for 0% -> 0%
where the time goes in v20:
time: 169 us; the launch traced here: 168 us
  waiting for transfers between devices  72.4 us (43%)
  starting transfers between devices  68 us (40%)
  matrix products  19.2 us (11%)
  other arithmetic  5.5 us (3%)
    ppermute x3, waiting for transfers between devices, direct_reduce_scatter(): lax.ppermute(outgoing, axis, [(i, (i + shift) % n) for i in range(n)])  22.6 us
    ppermute x3, starting transfers between devices, shards(): flow = lax.ppermute(flow, ('seq', 'pair'), ways)  21.9 us
    ppermute x3, waiting for transfers between devices, rotated_all_gather(): lax.ppermute(value, axis, [(i, (i + shift) % n) for i in range(n)])  18.9 us
    ppermute x3, waiting for transfers between devices, shards(): next_going = lax.ppermute(going, 'seq', forward)  10.5 us
    ppermute x3, starting transfers between devices, rotated_all_gather(): lax.ppermute(value, axis, [(i, (i + shift) % n) for i in range(n)])  10.4 us
    ppermute x3, starting transfers between devices, permute_all_to_all(): lax.ppermute(outgoing, axis, [(i, (i + shift) % n) for i in range(n)])  7.13 us
    dot_general x5, matrix products, conv_rows(): jnp.dot(shifted, conv_weight[offset], preferred_element_type=jnp.float32)  6.46 us
    ppermute x6, starting transfers between devices, direct_all_gather(): lax.ppermute(value, axis, [(i, (i + shift) % n) for i in range(n)])  6.45 us
  transfers between devices with their start and end apart: 30, of which 21 were waited for; matrix products, arithmetic and copies ran while one was open for 10% of the time, Pallas kernels for 0%

profile of v20, /device:TPU:0, one launch (start us, length us, event | category | flops | bytes accessed | tf_op | source)
XLA Modules:
  0.0 167.7 jit_solution(9643259505363444368)
XLA Ops:
  4.1 3.1 %collective-permute-start = (bf16[128,384]{1,0:T(8,128)(2,1)S(1)}, bf16[128,384]{1,0:T(8,128)(2,1)S(1)}, u32[]{:S(2)}, u32[]{:S(2)}) collective-permute-start(bf16[128,384]{1,0:T(8,128)(2,1)S(1)} %bitcast.315), channel_id=1, source_target_pairs={{0,1},{1,2},{2,3},{3,0},{4,5},{5,6},{6,7},{7,4},{8,9},{9,10},{10,1... | collective-permute-start | bytes 294920 | tf_op jit(solution)/shard_map/ppermute | solution.py:65
  7.2 2.7 %collective-permute-start.1 = (bf16[128,384]{1,0:T(8,128)(2,1)S(1)}, bf16[128,384]{1,0:T(8,128)(2,1)S(1)}, u32[]{:S(2)}, u32[]{:S(2)}) collective-permute-start(bf16[128,384]{1,0:T(8,128)(2,1)S(1)} %bitcast.314), channel_id=1, source_target_pairs={{0,2},{1,3},{2,0},{3,1},{4,6},{5,7},{6,4},{7,5},{8,10},{9,11},{10,... | collective-permute-start | bytes 294920 | tf_op jit(solution)/shard_map/ppermute | solution.py:65
  11.4 1.5 collective-permute-done
  12.9 3.5 %collective-permute-done.1 = bf16[128,384]{1,0:T(8,128)(2,1)S(1)} collective-permute-done((bf16[128,384]{1,0:T(8,128)(2,1)S(1)}, bf16[128,384]{1,0:T(8,128)(2,1)S(1)}, u32[]{:S(2)}, u32[]{:S(2)}) %collective-permute-start.1) | collective-permute-done | bytes 98336 | tf_op jit(solution)/shard_map/ppermute | solution.py:65
  16.6 1.7 collective-permute-start.3
  18.3 1.6 collective-permute-start.4
  19.9 2.4 %fusion.42 = f32[512,1536]{1,0:T(8,128)S(1)} fusion(bf16[512,384]{1,0:T(8,128)(2,1)S(1)} %bitcast.299, bf16[5,384,1536]{2,1,0:T(8,128)(2,1)} %param.12), kind=kOutput, calls=%fused_computation.66 | convolution fusion | flops 603979776 | bytes 4718592 | tf_op jit(solution)/shard_map/conv_reduce/dot_general | solution.py:39
  27.4 2.4 %collective-permute-start.5 = (bf16[128,1536]{1,0:T(8,128)(2,1)S(1)}, bf16[128,1536]{1,0:T(8,128)(2,1)S(1)}, u32[]{:S(2)}, u32[]{:S(2)}) collective-permute-start(bf16[128,1536]{1,0:T(8,128)(2,1)S(1)} %get-tuple-element.20), channel_id=1, source_target_pairs={{0,1},{1,2},{2,3},{3,0},{4,5},{5,6},{6,7},{7,4},{8,9},{9,10},{10,1... | collective-permute-start | bytes 1179656 | tf_op jit(solution)/shard_map/conv_reduce/ppermute | solution.py:51
  29.8 1.7 %collective-permute-start.6 = (bf16[128,1536]{1,0:T(8,128)(2,1)S(1)}, bf16[128,1536]{1,0:T(8,128)(2,1)S(1)}, u32[]{:S(2)}, u32[]{:S(2)}) collective-permute-start(bf16[128,1536]{1,0:T(8,128)(2,1)S(1)} %get-tuple-element.22), channel_id=1, source_target_pairs={{0,2},{1,3},{2,0},{3,1},{4,6},{5,7},{6,4},{7,5},{8,10},{9,11},{10,... | collective-permute-start | bytes 1179656 | tf_op jit(solution)/shard_map/conv_reduce/ppermute | solution.py:51
  32.3 3.2 %collective-permute-start.18 = (bf16[256,1536]{1,0:T(8,128)(2,1)}, bf16[256,1536]{1,0:T(8,128)(2,1)S(1)}, u32[]{:S(2)}, u32[]{:S(2)}) collective-permute-start(bf16[256,1536]{1,0:T(8,128)(2,1)} %param.15), channel_id=1, source_target_pairs={{0,1},{1,2},{2,3},{5,4},{6,5},{7,6},{8,9},{9,10},{10,11},{13,12},{... | collective-permute-start | bytes 2359304 | tf_op jit(solution)/shard_map/out_projection/ppermute | solution.py:260
  35.5 4.6 %collective-permute-done.5 = bf16[128,1536]{1,0:T(8,128)(2,1)S(1)} collective-permute-done((bf16[128,1536]{1,0:T(8,128)(2,1)S(1)}, bf16[128,1536]{1,0:T(8,128)(2,1)S(1)}, u32[]{:S(2)}, u32[]{:S(2)}) %collective-permute-start.5) | collective-permute-done | bytes 393248 | tf_op jit(solution)/shard_map/conv_reduce/ppermute | solution.py:51
  40.1 18.0 %collective-permute-done.6 = bf16[128,1536]{1,0:T(8,128)(2,1)S(1)} collective-permute-done((bf16[128,1536]{1,0:T(8,128)(2,1)S(1)}, bf16[128,1536]{1,0:T(8,128)(2,1)S(1)}, u32[]{:S(2)}, u32[]{:S(2)}) %collective-permute-start.6) | collective-permute-done | bytes 393248 | tf_op jit(solution)/shard_map/conv_reduce/ppermute | solution.py:51
  59.4 7.8 %collective-permute-start.10 = (bf16[128,1536]{1,0:T(8,128)(2,1)}, bf16[128,1536]{1,0:T(8,128)(2,1)}, u32[]{:S(2)}, u32[]{:S(2)}) collective-permute-start(bf16[128,1536]{1,0:T(8,128)(2,1)} %fusion.74), channel_id=1, source_target_pairs={{0,3},{1,0},{2,1},{3,2},{4,7},{5,4},{6,5},{7,6},{8,11},{9,8},{10,9... | collective-permute-start | bytes 1179656 | tf_op jit(solution)/shard_map/attn_in_gather/ppermute | solution.py:141
  68.4 1.5 collective-permute-start.9
  69.8 16.7 %collective-permute-start.19 = (bf16[256,1536]{1,0:T(8,128)(2,1)S(1)}, bf16[256,1536]{1,0:T(8,128)(2,1)S(1)}, u32[]{:S(2)}, u32[]{:S(2)}) collective-permute-start(bf16[256,1536]{1,0:T(8,128)(2,1)S(1)} %collective-permute-done.18), channel_id=1, source_target_pairs={{0,1},{1,2},{2,3},{5,4},{6,5},{7,6},{8,9},{9,10},{10,11},{13,12},{... | collective-permute-start | bytes 2359304 | tf_op jit(solution)/shard_map/out_projection/ppermute | solution.py:260
  87.0 18.4 %collective-permute-done.9 = bf16[128,1536]{1,0:T(8,128)(2,1)} collective-permute-done((bf16[128,1536]{1,0:T(8,128)(2,1)}, bf16[128,1536]{1,0:T(8,128)(2,1)}, u32[]{:S(2)}, u32[]{:S(2)}) %collective-permute-start.9) | collective-permute-done | bytes 393248 | tf_op jit(solution)/shard_map/attn_in_gather/ppermute | solution.py:141
  105.5 2.7 %fusion.14 = bf16[512,768]{1,0:T(8,128)(2,1)S(1)} fusion(bf16[1536,768]{1,0:T(8,128)(2,1)S(1)} %copy-done, bf16[128,1536]{1,0:T(8,128)(2,1)} %collective-permute-done.10, bf16[128,1536]{1,0:T(8,128)(2,1)} %collective-permute-done.9, bf16[128,1536]{1,0:T(8,128)(2,1)} %collective-permute-done.8, bf16[128,1536]{1,0:T(8,128)(2,1)} %fusion.74), kind=kOutput, calls=%fused_computation.18 | convolution fusion | flops 1214644224 | bytes 4718592 | tf_op jit(solution)/shard_map/dot_general | solution.py:194
  108.3 3.3 %collective-permute-start.11 = (bf16[2,256,256]{2,1,0:T(8,128)(2,1)S(1)}, bf16[2,256,256]{2,1,0:T(8,128)(2,1)S(1)}, u32[]{:S(2)}, u32[]{:S(2)}) collective-permute-start(bf16[2,256,256]{2,1,0:T(8,128)(2,1)S(1)} %get-tuple-element.23), channel_id=1, source_target_pairs={{0,4},{4,8},{8,12},{12,0},{1,5},{5,9},{9,13},{13,1},{2,6},{6,10},{... | collective-permute-start | bytes 786440 | tf_op jit(solution)/shard_map/kv_ring/ppermute | solution.py:235
  112.9 4.4 %collective-permute-done.11 = bf16[2,256,256]{2,1,0:T(8,128)(2,1)S(1)} collective-permute-done((bf16[2,256,256]{2,1,0:T(8,128)(2,1)S(1)}, bf16[2,256,256]{2,1,0:T(8,128)(2,1)S(1)}, u32[]{:S(2)}, u32[]{:S(2)}) %collective-permute-start.11) | collective-permute-done | bytes 262176 | tf_op jit(solution)/shard_map/kv_ring/ppermute | solution.py:235
  117.7 1.8 %collective-permute-start.14 = (bf16[2,256,256]{2,1,0:T(8,128)(2,1)S(1)}, bf16[2,256,256]{2,1,0:T(8,128)(2,1)S(1)}, u32[]{:S(2)}, u32[]{:S(2)}) collective-permute-start(bf16[2,256,256]{2,1,0:T(8,128)(2,1)S(1)} %collective-permute-done.12), channel_id=1, source_target_pairs={{4,0},{8,4},{12,8},{0,12},{5,1},{9,5},{13,9},{1,13},{6,2},{10,6},{... | collective-permute-start | bytes 786440 | tf_op jit(solution)/shard_map/kv_ring/ppermute | solution.py:236
  119.8 4.3 %collective-permute-done.13 = bf16[2,256,256]{2,1,0:T(8,128)(2,1)S(1)} collective-permute-done((bf16[2,256,256]{2,1,0:T(8,128)(2,1)S(1)}, bf16[2,256,256]{2,1,0:T(8,128)(2,1)S(1)}, u32[]{:S(2)}, u32[]{:S(2)}) %collective-permute-start.13) | collective-permute-done | bytes 262176 | tf_op jit(solution)/shard_map/kv_ring/ppermute | solution.py:235
  124.8 1.9 %collective-permute-start.16 = (bf16[2,256,256]{2,1,0:T(8,128)(2,1)S(1)}, bf16[2,256,256]{2,1,0:T(8,128)(2,1)S(1)}, u32[]{:S(2)}, u32[]{:S(2)}) collective-permute-start(bf16[2,256,256]{2,1,0:T(8,128)(2,1)S(1)} %collective-permute-done.14), channel_id=1, source_target_pairs={{4,0},{8,4},{12,8},{0,12},{5,1},{9,5},{13,9},{1,13},{6,2},{10,6},{... | collective-permute-start | bytes 786440 | tf_op jit(solution)/shard_map/kv_ring/ppermute | solution.py:236
  126.8 2.0 %collective-permute-start.20 = (bf16[256,1536]{1,0:T(8,128)(2,1)S(1)}, bf16[256,1536]{1,0:T(8,128)(2,1)S(1)}, u32[]{:S(2)}, u32[]{:S(2)}) collective-permute-start(bf16[256,1536]{1,0:T(8,128)(2,1)S(1)} %collective-permute-done.19), channel_id=1, source_target_pairs={{0,1},{1,2},{2,3},{5,4},{6,5},{7,6},{8,9},{9,10},{10,11},{13,12},{... | collective-permute-start | bytes 2359304 | tf_op jit(solution)/shard_map/out_projection/ppermute | solution.py:260
  128.8 1.8 %collective-permute-done.15 = bf16[2,256,256]{2,1,0:T(8,128)(2,1)S(1)} collective-permute-done((bf16[2,256,256]{2,1,0:T(8,128)(2,1)S(1)}, bf16[2,256,256]{2,1,0:T(8,128)(2,1)S(1)}, u32[]{:S(2)}, u32[]{:S(2)}) %collective-permute-start.15) | collective-permute-done | bytes 262176 | tf_op jit(solution)/shard_map/kv_ring/ppermute | solution.py:235
  133.5 4.6 %collective-permute-done.20 = bf16[256,1536]{1,0:T(8,128)(2,1)S(1)} collective-permute-done((bf16[256,1536]{1,0:T(8,128)(2,1)S(1)}, bf16[256,1536]{1,0:T(8,128)(2,1)S(1)}, u32[]{:S(2)}, u32[]{:S(2)}) %collective-permute-start.20) | collective-permute-done | bytes 786464 | tf_op jit(solution)/shard_map/out_projection/ppermute | solution.py:260
  141.4 1.6 collective-permute-start.17
  144.5 3.0 %collective-permute-start.23 = (bf16[128,256]{0,1:T(8,128)(2,1)S(1)}, bf16[128,256]{0,1:T(8,128)(2,1)S(1)}, u32[]{:S(2)}, u32[]{:S(2)}) collective-permute-start(bf16[128,256]{0,1:T(8,128)(2,1)S(1)} %bitcast.320), channel_id=1, source_target_pairs={{0,3},{1,0},{2,1},{3,2},{4,7},{5,4},{6,5},{7,6},{8,11},{9,8},{10,9... | collective-permute-start | bytes 196616 | tf_op jit(solution)/shard_map/out_projection/ppermute | solution.py:267
  150.6 3.3 %collective-permute-done.22 = bf16[128,256]{0,1:T(8,128)(2,1)S(1)} collective-permute-done((bf16[128,256]{0,1:T(8,128)(2,1)S(1)}, bf16[128,256]{0,1:T(8,128)(2,1)S(1)}, u32[]{:S(2)}, u32[]{:S(2)}) %collective-permute-start.22) | collective-permute-done | bytes 65568 | tf_op jit(solution)/shard_map/out_projection/ppermute | solution.py:267
  155.5 3.3 %collective-permute-start.25 = (bf16[8,256]{1,0:T(8,128)(2,1)S(1)}, bf16[8,256]{1,0:T(8,128)(2,1)S(1)}, u32[]{:S(2)}, u32[]{:S(2)}) collective-permute-start(bf16[8,256]{1,0:T(8,128)(2,1)S(1)} %get-tuple-element.59), channel_id=1, source_target_pairs={{0,2},{1,3},{2,0},{3,1},{4,6},{5,7},{6,4},{7,5},{8,10},{9,11},{10,... | collective-permute-start | bytes 12296 | tf_op jit(solution)/shard_map/sides_gather/ppermute | solution.py:153
  159.3 1.6 collective-permute-done.24
  160.9 1.5 collective-permute-done.26
  163.5 1.4 collective-permute-start.29
  (114 shorter events, 33.3 us)
Async XLA Ops:
  0.6 104.8 %copy-start = (bf16[1536,768]{1,0:T(8,128)(2,1)S(1)}, bf16[1536,768]{1,0:T(8,128)(2,1)}, u32[]{:S(2)}) copy-start(bf16[1536,768]{1,0:T(8,128)(2,1)} %param.14) | copy-start | bytes 7077892
  4.1 8.7 %collective-permute-start = (bf16[128,384]{1,0:T(8,128)(2,1)S(1)}, bf16[128,384]{1,0:T(8,128)(2,1)S(1)}, u32[]{:S(2)}, u32[]{:S(2)}) collective-permute-start(bf16[128,384]{1,0:T(8,128)(2,1)S(1)} %bitcast.315), channel_id=1, source_target_pairs={{0,1},{1,2},{2,3},{3,0},{4,5},{5,6},{6,7},{7,4},{8,9},{9,10},{10,1... | collective-permute-start | bytes 294920 | tf_op jit(solution)/shard_map/ppermute | solution.py:65
  7.2 9.2 %collective-permute-start.1 = (bf16[128,384]{1,0:T(8,128)(2,1)S(1)}, bf16[128,384]{1,0:T(8,128)(2,1)S(1)}, u32[]{:S(2)}, u32[]{:S(2)}) collective-permute-start(bf16[128,384]{1,0:T(8,128)(2,1)S(1)} %bitcast.314), channel_id=1, source_target_pairs={{0,2},{1,3},{2,0},{3,1},{4,6},{5,7},{6,4},{7,5},{8,10},{9,11},{10,... | collective-permute-start | bytes 294920 | tf_op jit(solution)/shard_map/ppermute | solution.py:65
  9.9 6.7 %collective-permute-start.2 = (bf16[128,384]{1,0:T(8,128)(2,1)S(1)}, bf16[128,384]{1,0:T(8,128)(2,1)S(1)}, u32[]{:S(2)}, u32[]{:S(2)}) collective-permute-start(bf16[128,384]{1,0:T(8,128)(2,1)S(1)} %bitcast.313), channel_id=1, source_target_pairs={{0,3},{1,0},{2,1},{3,2},{4,7},{5,4},{6,5},{7,6},{8,11},{9,8},{10,9... | collective-permute-start | bytes 294920 | tf_op jit(solution)/shard_map/ppermute | solution.py:65
  16.6 8.5 %collective-permute-start.3 = (bf16[8,384]{1,0:T(8,128)(2,1)S(1)}, bf16[8,384]{1,0:T(8,128)(2,1)S(1)}, u32[]{:S(2)}, u32[]{:S(2)}) collective-permute-start(bf16[8,384]{1,0:T(8,128)(2,1)S(1)} %get-tuple-element.25), channel_id=1, source_target_pairs={{0,4},{4,8},{8,12},{1,5},{5,9},{9,13},{2,6},{6,10},{10,14},{3,7},{... | collective-permute-start | bytes 18440 | tf_op jit(solution)/shard_map/ppermute | solution.py:25
  18.3 4.8 %collective-permute-start.4 = (bf16[8,384]{1,0:T(8,128)(2,1)S(1)}, bf16[8,384]{1,0:T(8,128)(2,1)S(1)}, u32[]{:S(2)}, u32[]{:S(2)}) collective-permute-start(bf16[8,384]{1,0:T(8,128)(2,1)S(1)} %get-tuple-element.26), channel_id=1, source_target_pairs={{4,0},{8,4},{12,8},{5,1},{9,5},{13,9},{6,2},{10,6},{14,10},{7,3},{... | collective-permute-start | bytes 18440 | tf_op jit(solution)/shard_map/ppermute | solution.py:26
  26.1 32.1 %copy-start.2 = (bf16[128,1536]{1,0:T(8,128)(2,1)S(1)}, bf16[128,1536]{1,0:T(8,128)(2,1)}, u32[]{:S(2)}) copy-start(bf16[128,1536]{1,0:T(8,128)(2,1)} %param.10) | copy-start | bytes 1179652
  27.4 12.7 %collective-permute-start.5 = (bf16[128,1536]{1,0:T(8,128)(2,1)S(1)}, bf16[128,1536]{1,0:T(8,128)(2,1)S(1)}, u32[]{:S(2)}, u32[]{:S(2)}) collective-permute-start(bf16[128,1536]{1,0:T(8,128)(2,1)S(1)} %get-tuple-element.20), channel_id=1, source_target_pairs={{0,1},{1,2},{2,3},{3,0},{4,5},{5,6},{6,7},{7,4},{8,9},{9,10},{10,1... | collective-permute-start | bytes 1179656 | tf_op jit(solution)/shard_map/conv_reduce/ppermute | solution.py:51
  29.8 28.3 %collective-permute-start.6 = (bf16[128,1536]{1,0:T(8,128)(2,1)S(1)}, bf16[128,1536]{1,0:T(8,128)(2,1)S(1)}, u32[]{:S(2)}, u32[]{:S(2)}) collective-permute-start(bf16[128,1536]{1,0:T(8,128)(2,1)S(1)} %get-tuple-element.22), channel_id=1, source_target_pairs={{0,2},{1,3},{2,0},{3,1},{4,6},{5,7},{6,4},{7,5},{8,10},{9,11},{10,... | collective-permute-start | bytes 1179656 | tf_op jit(solution)/shard_map/conv_reduce/ppermute | solution.py:51
  31.5 26.6 %collective-permute-start.7 = (bf16[128,1536]{1,0:T(8,128)(2,1)S(1)}, bf16[128,1536]{1,0:T(8,128)(2,1)S(1)}, u32[]{:S(2)}, u32[]{:S(2)}) collective-permute-start(bf16[128,1536]{1,0:T(8,128)(2,1)S(1)} %get-tuple-element.21), channel_id=1, source_target_pairs={{0,3},{1,0},{2,1},{3,2},{4,7},{5,4},{6,5},{7,6},{8,11},{9,8},{10,9... | collective-permute-start | bytes 1179656 | tf_op jit(solution)/shard_map/conv_reduce/ppermute | solution.py:51
  32.3 37.6 %collective-permute-start.18 = (bf16[256,1536]{1,0:T(8,128)(2,1)}, bf16[256,1536]{1,0:T(8,128)(2,1)S(1)}, u32[]{:S(2)}, u32[]{:S(2)}) collective-permute-start(bf16[256,1536]{1,0:T(8,128)(2,1)} %param.15), channel_id=1, source_target_pairs={{0,1},{1,2},{2,3},{5,4},{6,5},{7,6},{8,9},{9,10},{10,11},{13,12},{... | collective-permute-start | bytes 2359304 | tf_op jit(solution)/shard_map/out_projection/ppermute | solution.py:260
  59.4 27.1 %collective-permute-start.10 = (bf16[128,1536]{1,0:T(8,128)(2,1)}, bf16[128,1536]{1,0:T(8,128)(2,1)}, u32[]{:S(2)}, u32[]{:S(2)}) collective-permute-start(bf16[128,1536]{1,0:T(8,128)(2,1)} %fusion.74), channel_id=1, source_target_pairs={{0,3},{1,0},{2,1},{3,2},{4,7},{5,4},{6,5},{7,6},{8,11},{9,8},{10,9... | collective-permute-start | bytes 1179656 | tf_op jit(solution)/shard_map/attn_in_gather/ppermute | solution.py:141
  67.2 19.8 %collective-permute-start.8 = (bf16[128,1536]{1,0:T(8,128)(2,1)}, bf16[128,1536]{1,0:T(8,128)(2,1)}, u32[]{:S(2)}, u32[]{:S(2)}) collective-permute-start(bf16[128,1536]{1,0:T(8,128)(2,1)} %fusion.74), channel_id=1, source_target_pairs={{0,1},{1,2},{2,3},{3,0},{4,5},{5,6},{6,7},{7,4},{8,9},{9,10},{10,1... | collective-permute-start | bytes 1179656 | tf_op jit(solution)/shard_map/attn_in_gather/ppermute | solution.py:141
  68.4 37.1 %collective-permute-start.9 = (bf16[128,1536]{1,0:T(8,128)(2,1)}, bf16[128,1536]{1,0:T(8,128)(2,1)}, u32[]{:S(2)}, u32[]{:S(2)}) collective-permute-start(bf16[128,1536]{1,0:T(8,128)(2,1)} %fusion.74), channel_id=1, source_target_pairs={{0,2},{1,3},{2,0},{3,1},{4,6},{5,7},{6,4},{7,5},{8,10},{9,11},{10,... | collective-permute-start | bytes 1179656 | tf_op jit(solution)/shard_map/attn_in_gather/ppermute | solution.py:141
  69.8 56.9 %collective-permute-start.19 = (bf16[256,1536]{1,0:T(8,128)(2,1)S(1)}, bf16[256,1536]{1,0:T(8,128)(2,1)S(1)}, u32[]{:S(2)}, u32[]{:S(2)}) collective-permute-start(bf16[256,1536]{1,0:T(8,128)(2,1)S(1)} %collective-permute-done.18), channel_id=1, source_target_pairs={{0,1},{1,2},{2,3},{5,4},{6,5},{7,6},{8,9},{9,10},{10,11},{13,12},{... | collective-permute-start | bytes 2359304 | tf_op jit(solution)/shard_map/out_projection/ppermute | solution.py:260
  108.3 9.0 %collective-permute-start.11 = (bf16[2,256,256]{2,1,0:T(8,128)(2,1)S(1)}, bf16[2,256,256]{2,1,0:T(8,128)(2,1)S(1)}, u32[]{:S(2)}, u32[]{:S(2)}) collective-permute-start(bf16[2,256,256]{2,1,0:T(8,128)(2,1)S(1)} %get-tuple-element.23), channel_id=1, source_target_pairs={{0,4},{4,8},{8,12},{12,0},{1,5},{5,9},{9,13},{13,1},{2,6},{6,10},{... | collective-permute-start | bytes 786440 | tf_op jit(solution)/shard_map/kv_ring/ppermute | solution.py:235
  111.9 5.8 %collective-permute-start.12 = (bf16[2,256,256]{2,1,0:T(8,128)(2,1)S(1)}, bf16[2,256,256]{2,1,0:T(8,128)(2,1)S(1)}, u32[]{:S(2)}, u32[]{:S(2)}) collective-permute-start(bf16[2,256,256]{2,1,0:T(8,128)(2,1)S(1)} %get-tuple-element.24), channel_id=1, source_target_pairs={{4,0},{8,4},{12,8},{0,12},{5,1},{9,5},{13,9},{1,13},{6,2},{10,6},{... | collective-permute-start | bytes 786440 | tf_op jit(solution)/shard_map/kv_ring/ppermute | solution.py:236
  117.4 6.8 %collective-permute-start.13 = (bf16[2,256,256]{2,1,0:T(8,128)(2,1)S(1)}, bf16[2,256,256]{2,1,0:T(8,128)(2,1)S(1)}, u32[]{:S(2)}, u32[]{:S(2)}) collective-permute-start(bf16[2,256,256]{2,1,0:T(8,128)(2,1)S(1)} %collective-permute-done.11), channel_id=1, source_target_pairs={{0,4},{4,8},{8,12},{12,0},{1,5},{5,9},{9,13},{13,1},{2,6},{6,10},{... | collective-permute-start | bytes 786440 | tf_op jit(solution)/shard_map/kv_ring/ppermute | solution.py:235
  117.7 6.8 %collective-permute-start.14 = (bf16[2,256,256]{2,1,0:T(8,128)(2,1)S(1)}, bf16[2,256,256]{2,1,0:T(8,128)(2,1)S(1)}, u32[]{:S(2)}, u32[]{:S(2)}) collective-permute-start(bf16[2,256,256]{2,1,0:T(8,128)(2,1)S(1)} %collective-permute-done.12), channel_id=1, source_target_pairs={{4,0},{8,4},{12,8},{0,12},{5,1},{9,5},{13,9},{1,13},{6,2},{10,6},{... | collective-permute-start | bytes 786440 | tf_op jit(solution)/shard_map/kv_ring/ppermute | solution.py:236
  124.2 6.4 %collective-permute-start.15 = (bf16[2,256,256]{2,1,0:T(8,128)(2,1)S(1)}, bf16[2,256,256]{2,1,0:T(8,128)(2,1)S(1)}, u32[]{:S(2)}, u32[]{:S(2)}) collective-permute-start(bf16[2,256,256]{2,1,0:T(8,128)(2,1)S(1)} %collective-permute-done.13), channel_id=1, source_target_pairs={{0,4},{4,8},{8,12},{12,0},{1,5},{5,9},{9,13},{13,1},{2,6},{6,10},{... | collective-permute-start | bytes 786440 | tf_op jit(solution)/shard_map/kv_ring/ppermute | solution.py:235
  124.8 6.4 %collective-permute-start.16 = (bf16[2,256,256]{2,1,0:T(8,128)(2,1)S(1)}, bf16[2,256,256]{2,1,0:T(8,128)(2,1)S(1)}, u32[]{:S(2)}, u32[]{:S(2)}) collective-permute-start(bf16[2,256,256]{2,1,0:T(8,128)(2,1)S(1)} %collective-permute-done.14), channel_id=1, source_target_pairs={{4,0},{8,4},{12,8},{0,12},{5,1},{9,5},{13,9},{1,13},{6,2},{10,6},{... | collective-permute-start | bytes 786440 | tf_op jit(solution)/shard_map/kv_ring/ppermute | solution.py:236
  126.8 11.3 %collective-permute-start.20 = (bf16[256,1536]{1,0:T(8,128)(2,1)S(1)}, bf16[256,1536]{1,0:T(8,128)(2,1)S(1)}, u32[]{:S(2)}, u32[]{:S(2)}) collective-permute-start(bf16[256,1536]{1,0:T(8,128)(2,1)S(1)} %collective-permute-done.19), channel_id=1, source_target_pairs={{0,1},{1,2},{2,3},{5,4},{6,5},{7,6},{8,9},{9,10},{10,11},{13,12},{... | collective-permute-start | bytes 2359304 | tf_op jit(solution)/shard_map/out_projection/ppermute | solution.py:260
  138.3 10.5 %collective-permute-start.21 = (bf16[3,256,1536]{2,1,0:T(8,128)(2,1)S(1)}, bf16[3,256,1536]{2,1,0:T(8,128)(2,1)S(1)}, u32[]{:S(2)}, u32[]{:S(2)}) collective-permute-start(bf16[3,256,1536]{2,1,0:T(8,128)(2,1)S(1)} %pad_maximum_fusion), channel_id=1, source_target_pairs={{0,4},{4,0},{8,12},{12,8},{1,5},{5,1},{9,13},{13,9},{2,6},{6,2},{1... | collective-permute-start | bytes 7077896 | tf_op jit(solution)/shard_map/out_projection/ppermute | solution.py:263
  141.4 7.4 %collective-permute-start.17 = (bf16[128,256]{0,1:T(8,128)(2,1)S(1)}, bf16[128,256]{0,1:T(8,128)(2,1)S(1)}, u32[]{:S(2)}, u32[]{:S(2)}) collective-permute-start(bf16[128,256]{0,1:T(8,128)(2,1)S(1)} %bitcast.321), channel_id=1, source_target_pairs={{0,1},{1,2},{2,3},{3,0},{4,5},{5,6},{6,7},{7,4},{8,9},{9,10},{10,1... | collective-permute-start | bytes 196616 | tf_op jit(solution)/shard_map/out_projection/ppermute | solution.py:267
  144.5 5.7 %collective-permute-start.23 = (bf16[128,256]{0,1:T(8,128)(2,1)S(1)}, bf16[128,256]{0,1:T(8,128)(2,1)S(1)}, u32[]{:S(2)}, u32[]{:S(2)}) collective-permute-start(bf16[128,256]{0,1:T(8,128)(2,1)S(1)} %bitcast.320), channel_id=1, source_target_pairs={{0,3},{1,0},{2,1},{3,2},{4,7},{5,4},{6,5},{7,6},{8,11},{9,8},{10,9... | collective-permute-start | bytes 196616 | tf_op jit(solution)/shard_map/out_projection/ppermute | solution.py:267
  147.5 6.4 %collective-permute-start.22 = (bf16[128,256]{0,1:T(8,128)(2,1)S(1)}, bf16[128,256]{0,1:T(8,128)(2,1)S(1)}, u32[]{:S(2)}, u32[]{:S(2)}) collective-permute-start(bf16[128,256]{0,1:T(8,128)(2,1)S(1)} %bitcast.319), channel_id=1, source_target_pairs={{0,2},{1,3},{2,0},{3,1},{4,6},{5,7},{6,4},{7,5},{8,10},{9,11},{10,... | collective-permute-start | bytes 196616 | tf_op jit(solution)/shard_map/out_projection/ppermute | solution.py:267
  155.5 5.4 %collective-permute-start.24 = (bf16[8,256]{1,0:T(8,128)(2,1)S(1)}, bf16[8,256]{1,0:T(8,128)(2,1)S(1)}, u32[]{:S(2)}, u32[]{:S(2)}) collective-permute-start(bf16[8,256]{1,0:T(8,128)(2,1)S(1)} %get-tuple-element.59), channel_id=1, source_target_pairs={{0,1},{1,2},{2,3},{3,0},{4,5},{5,6},{6,7},{7,4},{8,9},{9,10},{10,1... | collective-permute-start | bytes 12296 | tf_op jit(solution)/shard_map/sides_gather/ppermute | solution.py:153
  155.5 5.4 %collective-permute-start.25 = (bf16[8,256]{1,0:T(8,128)(2,1)S(1)}, bf16[8,256]{1,0:T(8,128)(2,1)S(1)}, u32[]{:S(2)}, u32[]{:S(2)}) collective-permute-start(bf16[8,256]{1,0:T(8,128)(2,1)S(1)} %get-tuple-element.59), channel_id=1, source_target_pairs={{0,2},{1,3},{2,0},{3,1},{4,6},{5,7},{6,4},{7,5},{8,10},{9,11},{10,... | collective-permute-start | bytes 12296 | tf_op jit(solution)/shard_map/sides_gather/ppermute | solution.py:153
  158.7 3.6 %collective-permute-start.26 = (bf16[8,256]{1,0:T(8,128)(2,1)S(1)}, bf16[8,256]{1,0:T(8,128)(2,1)S(1)}, u32[]{:S(2)}, u32[]{:S(2)}) collective-permute-start(bf16[8,256]{1,0:T(8,128)(2,1)S(1)} %get-tuple-element.59), channel_id=1, source_target_pairs={{0,3},{1,0},{2,1},{3,2},{4,7},{5,4},{6,5},{7,6},{8,11},{9,8},{10,9... | collective-permute-start | bytes 12296 | tf_op jit(solution)/shard_map/sides_gather/ppermute | solution.py:153
  162.3 3.2 %collective-permute-start.27 = (bf16[32,256]{1,0:T(8,128)(2,1)S(1)}, bf16[32,256]{1,0:T(8,128)(2,1)S(1)}, u32[]{:S(2)}, u32[]{:S(2)}) collective-permute-start(bf16[32,256]{1,0:T(8,128)(2,1)S(1)} %bitcast.316), channel_id=1, source_target_pairs={{0,4},{4,8},{8,12},{12,0},{1,5},{5,9},{9,13},{13,1},{2,6},{6,10},{... | collective-permute-start | bytes 49160 | tf_op jit(solution)/shard_map/sides_gather/ppermute | solution.py:153
  162.3 3.8 %collective-permute-start.28 = (bf16[32,256]{1,0:T(8,128)(2,1)S(1)}, bf16[32,256]{1,0:T(8,128)(2,1)S(1)}, u32[]{:S(2)}, u32[]{:S(2)}) collective-permute-start(bf16[32,256]{1,0:T(8,128)(2,1)S(1)} %bitcast.317), channel_id=1, source_target_pairs={{0,8},{4,12},{8,0},{12,4},{1,9},{5,13},{9,1},{13,5},{2,10},{6,14},... | collective-permute-start | bytes 49160 | tf_op jit(solution)/shard_map/sides_gather/ppermute | solution.py:153
  163.5 2.9 %collective-permute-start.29 = (bf16[32,256]{1,0:T(8,128)(2,1)S(1)}, bf16[32,256]{1,0:T(8,128)(2,1)S(1)}, u32[]{:S(2)}, u32[]{:S(2)}) collective-permute-start(bf16[32,256]{1,0:T(8,128)(2,1)S(1)} %bitcast.318), channel_id=1, source_target_pairs={{0,12},{4,0},{8,4},{12,8},{1,13},{5,1},{9,5},{13,9},{2,14},{6,2},{... | collective-permute-start | bytes 49160 | tf_op jit(solution)/shard_map/sides_gather/ppermute | solution.py:153
  (6 other events, 77.3 us)
